TPU v7x, 32 devices: a whole 2x2x4 slice. The times are simulated.
32 devices in a mesh: groups: 2 (over y), expert: 4 (over z), tensor: 4 (over x, core).
Axes of the slice: x: 2, y: 2, z: 4, core: 2. Of those that a mesh axis runs over, the one named last changes fastest.
Arguments:
- tokens: bfloat16 [1024, 2560], P(('groups', 'expert'), 'tensor'), parts along dimension 0, may hold values from -6 to 6
- route_scale: float32 [1024], P(('groups', 'expert')), parts along dimension 0, may hold values from 0.25 to 1
- expert_ids: int32 [1024, 1], P(('groups', 'expert')), parts along dimension 0, may hold values from 0 to 1; in each aligned block of 128 rows (0 to 127, 128 to 255, ...) at most 128 rows name the same one
- gate_weight: bfloat16 [4, 2560, 2048], P('expert', None, 'tensor'), may hold values from -0.125 to 0.125
- up_weight: bfloat16 [4, 2560, 2048], P('expert', None, 'tensor'), may hold values from -0.125 to 0.125
- down_weight: bfloat16 [4, 2048, 2560], P('expert', 'tensor'), may hold values from -0.09375 to 0.09375
Outputs:
- mixed: bfloat16 [1024, 2560], P(('groups', 'expert'), 'tensor'), parts along dimension 0
There are 2 independent parts, one for each index of `groups`. A program takes and returns all parts, laid end to end along the dimension named above; an argument that names none is the same for every part. Nothing has to cross between parts.
Inputs may be any that keep to these rules, and one draw needn't show every extreme that they name: `expert_ids`: within the rows of one index of the expert axis (aligned blocks of 128 tokens) no expert is named by more than 128 tokens, and in some block one expert is named by exactly 128 tokens.
All inputs are finite; a program needn't handle non-finite values.
Results may differ from a plain program's by a relative error of at most 0.019.
Values may be sent and summed in bfloat16 or wider, within the bound.
No kernel may reach another device: no remote copies, remote signals or barrier semaphores. Data moves between devices by JAX's collectives and lax.ppermute only.
A program may use at most 64 MiB of HBM per device.

v0:
```python
import jax
import jax.numpy as jnp
from jax import lax
from jax.sharding import PartitionSpec as P

SPAN = 2


def local(tokens, route_scale, expert_ids, gate_weight, up_weight, down_weight):
    tok_rows = tokens.shape[0]
    n_devices = lax.axis_size("expert")
    experts = n_devices // SPAN
    capacity = min(tok_rows, 2 * tok_rows * SPAN // n_devices)
    routed = expert_ids[:, 0]
    one_hot = (routed[:, None] == jnp.arange(experts, dtype=jnp.int32)[None, :]).astype(jnp.int32)
    slot_rank = jnp.sum((jnp.cumsum(one_hot, axis=0) - one_hot) * one_hot, axis=1)
    flat_slot = routed * capacity + slot_rank
    placing = (
        flat_slot[None, :] == jnp.arange(experts * capacity, dtype=jnp.int32)[:, None]
    ).astype(jnp.bfloat16)
    scaled = (tokens.astype(jnp.float32) * route_scale[:, None]).astype(jnp.bfloat16)
    gate_local = gate_weight[0]
    up_local = up_weight[0]
    down_local = down_weight[0]
    full_rows = lax.all_gather(scaled, "tensor", axis=1, tiled=True)
    width = full_rows.shape[1]
    packed = jnp.dot(placing, full_rows, preferred_element_type=jnp.float32).astype(jnp.bfloat16)
    outgoing = jnp.repeat(packed.reshape(experts, capacity, width), SPAN, axis=0)
    arrived = lax.all_to_all(outgoing, "expert", split_axis=0, concat_axis=0, tiled=True)
    slot_rows = arrived.reshape(n_devices * capacity, width)
    gate_act = jnp.dot(slot_rows, gate_local, preferred_element_type=jnp.float32)
    up_act = jnp.dot(slot_rows, up_local, preferred_element_type=jnp.float32)
    hidden = (jax.nn.silu(gate_act) * up_act).astype(jnp.bfloat16)
    partial_value = jnp.dot(hidden, down_local, preferred_element_type=jnp.float32)
    width = partial_value.shape[1]
    outgoing_back = partial_value.astype(jnp.bfloat16).reshape(n_devices, capacity, width)
    returned = lax.all_to_all(outgoing_back, "expert", split_axis=0, concat_axis=0, tiled=True)
    paired = jnp.sum(returned.astype(jnp.float32).reshape(experts, SPAN, capacity, width), axis=1)
    picked = jnp.take(paired.reshape(experts * capacity, width), flat_slot, axis=0)
    summed = lax.psum_scatter(
        picked.astype(jnp.bfloat16), "tensor", scatter_dimension=1, tiled=True
    )
    return summed


def solution(mesh):
    placed = (
        P(("groups", "expert"), "tensor"),
        P(("groups", "expert")),
        P(("groups", "expert"), None),
        P("expert", None, "tensor"),
        P("expert", None, "tensor"),
        P("expert", "tensor", None),
    )
    return jax.shard_map(
        local,
        mesh=mesh,
        in_specs=placed,
        out_specs=P(("groups", "expert"), "tensor"),
        check_vma=False,
    )
```

profile of v0, /device:TPU:0, one launch (start us, length us, event | category | flops | bytes accessed | tf_op | source)
XLA Modules:
  0.0 200.1 jit_solution(4771933198922784884)
XLA Ops:
  6.5 0.0 copy-start
  6.5 0.9 fusion.15
  7.4 0.2 reduce_window_sum.11
  7.6 0.8 select_reduce_fusion
  8.4 0.7 multiply_add_fusion
  9.1 1.0 multiply_convert_fusion
  10.1 9.3 %all_gather.3 = bf16[128,2560]{1,0:T(8,128)(2,1)S(1)} all-gather(bf16[128,640]{1,0:T(8,128)(2,1)S(1)} %multiply_convert_fusion), channel_id=1, replica_groups=mesh['groups'=2,'expert'=4,'tensor'=4] {'tensor'}, dimensions={1}, use_global_device_ids=true | all-gather | bytes 819200 | tf_op jit(solution)/shard_map/all_gather | solution.py:25
  19.4 0.5 convolution_convert_fusion.1
  19.9 0.2 broadcast_in_dim.18
  20.2 0.0 copy-start.3
  20.2 64.9 %all_to_all.10 = bf16[4,128,2560]{2,1,0:T(8,128)(2,1)S(1)} all-to-all(bf16[4,128,2560]{2,1,0:T(8,128)(2,1)S(1)} %bitcast.39), channel_id=1, replica_groups=mesh['groups'=2,'expert'=4,'tensor'=4] {'expert'}, dimensions={0} | all-to-all | bytes 5242880 | tf_op jit(solution)/shard_map/all_to_all | solution.py:29
  85.1 0.0 copy-start.1
  85.1 1.5 copy-done.1
  86.6 0.0 copy-done.3
  86.6 2.5 %fusion.3 = f32[512,512]{1,0:T(8,128)} fusion(bf16[512,2560]{1,0:T(8,128)(2,1)S(1)} %bitcast.42, bf16[1,2560,512]{2,1,0:T(8,128)(2,1)S(1)} %copy-done.3), kind=kOutput, calls=%fused_computation.7 | convolution fusion | flops 1342177280 | bytes 6291456 | tf_op jit(solution)/shard_map/dot_general | solution.py:31
  89.1 0.0 copy-done
  89.1 7.2 %convolution_convert_fusion = bf16[512,2560]{1,0:T(8,128)(2,1)} fusion(bf16[1,512,2560]{2,1,0:T(8,128)(2,1)S(1)} %copy-done, bf16[512,2560]{1,0:T(8,128)(2,1)} %bitcast.43, bf16[1,2560,512]{2,1,0:T(8,128)(2,1)} %param.10, f32[512,512]{1,0:T(8,128)} %fusion.3), kind=kOutput, calls=%fused_computation.2 | convolution fusion | flops 2687238144 | bytes 11534336 | tf_op jit(solution)/shard_map/dot_general | solution.py:34
  96.4 0.0 copy-start.2
  96.4 4.7 %all-to-all-start.1 = ((bf16[4,128,2560]{2,1,0:T(8,128)(2,1)}), bf16[4,128,2560]{2,1,0:T(8,128)(2,1)}, u32[]{:S(2)}, u32[]{:S(2)}) async-start(bf16[4,128,2560]{2,1,0:T(8,128)(2,1)} %bitcast.41), calls=%async_computation.1 | async-start | bytes 5242880 | tf_op jit(solution)/shard_map/all_to_all | solution.py:37
  101.1 0.0 reduce-scatter.4.cloned.1.call-start
  101.1 0.0 copy-done.2
  101.1 59.1 %all-to-all-done.1 = bf16[4,128,2560]{2,1,0:T(8,128)(2,1)} async-done(((bf16[4,128,2560]{2,1,0:T(8,128)(2,1)}), bf16[4,128,2560]{2,1,0:T(8,128)(2,1)}, u32[]{:S(2)}, u32[]{:S(2)}) %all-to-all-start.1) | async-done | bytes 2621472 | tf_op jit(solution)/shard_map/all_to_all | solution.py:37
  160.2 3.6 %convert_reduce_fusion = bf16[2,128,2560]{2,1,0:T(8,128)(2,1)} fusion(bf16[4,128,2560]{2,1,0:T(8,128)(2,1)} %all-to-all-done.1), kind=kLoop, calls=%fused_computation.1 | loop fusion | flops 1966080 | bytes 3932160 | tf_op jit(solution)/shard_map/reduce_sum | solution.py:38
  163.8 3.1 %gather_fusion = bf16[128,2560]{1,0:T(8,128)(2,1)S(1)} fusion(bf16[256,2560]{1,0:T(8,128)(2,1)} %bitcast.38, s32[1024]{0:T(1024)S(1)} %pad_clamp_fusion), kind=kCustom, calls=%fused_computation | custom fusion | bytes 1311232 | tf_op jit(solution)/shard_map/jit(_take)/gather | solution.py:39
  167.0 1.0 select_convert_fusion
  168.0 2.2 %copy.7 = bf16[128,2560]{0,1:T(8,128)(2,1)} copy(bf16[128,2560]{1,0:T(8,128)(2,1)} %select_convert_fusion) | data formatting | bytes 1310720
  170.2 0.0 reduce-scatter.4.cloned.1.call-update
  170.2 21.3 %reduce-scatter.4.cloned.1.call-done = bf16[640,128]{1,0:T(8,128)(2,1)} async-done(((bf16[2560,128]{1,0:T(8,128)(2,1)}), bf16[640,128]{1,0:T(8,128)(2,1)}) %reduce-scatter.4.cloned.1.call-update) | async-done | bytes 163856
  191.5 1.7 copy.8
  (2 shorter events, 0.0 us)
Async XLA Ops:
  6.5 82.6 %copy-start = (bf16[1,512,2560]{2,1,0:T(8,128)(2,1)S(1)}, bf16[1,512,2560]{2,1,0:T(8,128)(2,1)}, u32[]{:S(2)}) copy-start(bf16[1,512,2560]{2,1,0:T(8,128)(2,1)} %param.11) | copy-start | bytes 7864324
  20.2 66.4 %copy-start.3 = (bf16[1,2560,512]{2,1,0:T(8,128)(2,1)S(1)}, bf16[1,2560,512]{2,1,0:T(8,128)(2,1)}, u32[]{:S(2)}) copy-start(bf16[1,2560,512]{2,1,0:T(8,128)(2,1)} %param.9) | copy-start | bytes 7864324
  85.1 1.5 copy-start.1
  96.4 4.7 %copy-start.2 = (s32[128,1]{0,1:T(1,128)S(1)}, s32[128,1]{0,1:T(1,128)}, u32[]{:S(2)}) copy-start(s32[128,1]{0,1:T(1,128)} %param.8) | copy-start | bytes 1540
  96.4 63.9 %all-to-all-start.1 = ((bf16[4,128,2560]{2,1,0:T(8,128)(2,1)}), bf16[4,128,2560]{2,1,0:T(8,128)(2,1)}, u32[]{:S(2)}, u32[]{:S(2)}) async-start(bf16[4,128,2560]{2,1,0:T(8,128)(2,1)} %bitcast.41), calls=%async_computation.1 | async-start | bytes 5242880 | tf_op jit(solution)/shard_map/all_to_all | solution.py:37
  101.1 90.5 %reduce-scatter.4.cloned.1.call-start = ((), (), s32[]{:S(2)}) async-start(), calls=%async_computation.3 | async-start | bytes 819200
Sparse Core Ops, SparseCore 0:
  170.3 21.1 reduce-scatter.3
where the time goes:
time: 201 us; the launch traced here: 200 us
  waiting for transfers between devices  80.4 us (40%)
  blocking collectives  74.2 us (37%)
  between operations  13.5 us (7%)
  matrix products  10.3 us (5%)
  local copies, waits for them, and re-layouts  8.75 us (4%)
  other arithmetic  8.23 us (4%)
  starting transfers between devices  4.72 us (2%)
    all_to_all x1, blocking collectives, local(): lax.all_to_all(outgoing, 'expert', split_axis=0, concat_axis=0, tiled=True)  64.9 us
    all_to_all x1, waiting for transfers between devices, local(): lax.all_to_all(outgoing_back, 'expert', split_axis=0, concat_axis=0, tile...  59.1 us
    unnamed x2, waiting for transfers between devices  21.4 us
    all_gather x1, blocking collectives, local(): full_rows = lax.all_gather(scaled, 'tensor', axis=1, tiled=True)  9.33 us
    dot_general x1, matrix products, local(): jnp.dot(hidden, down_local, preferred_element_type=jnp.float32)  7.24 us
    unnamed x10, local copies, waits for them, and re-layouts  5.42 us
    all_to_all x1, starting transfers between devices, local(): lax.all_to_all(outgoing_back, 'expert', split_axis=0, concat_axis=0, tile...  4.68 us
  transfers between devices with their start and end apart: 2, of which 2 were waited for; matrix products, arithmetic and copies ran while one was open for 0% of the time, Pallas kernels for 0%

commit v1 on v0

--- a/solution.py
+++ b/solution.py
@@ -6,7 +6,7 @@
 SPAN = 2
 
 
-def local(tokens, route_scale, expert_ids, gate_weight, up_weight, down_weight):
+def dispatched(tokens, route_scale, expert_ids, gate_weight, up_weight, down_weight):
     tok_rows = tokens.shape[0]
     n_devices = lax.axis_size("expert")
     experts = n_devices // SPAN
@@ -43,6 +43,31 @@
     return summed
 
 
+def gathered(tokens, route_scale, expert_ids, gate_weight, up_weight, down_weight):
+    expert = lax.axis_index("expert") // SPAN
+    scaled = (tokens.astype(jnp.float32) * route_scale[:, None]).astype(jnp.bfloat16)
+    rows = lax.all_gather(scaled, "expert", axis=0, tiled=True)
+    routed = lax.all_gather(expert_ids[:, 0], "expert", axis=0, tiled=True)
+    full_rows = lax.all_gather(rows, "tensor", axis=1, tiled=True)
+    gate_act = jnp.dot(full_rows, gate_weight[0], preferred_element_type=jnp.float32)
+    up_act = jnp.dot(full_rows, up_weight[0], preferred_element_type=jnp.float32)
+    mine = (routed == expert)[:, None]
+    hidden = jnp.where(mine, jax.nn.silu(gate_act) * up_act, 0.0).astype(jnp.bfloat16)
+    partial_value = jnp.dot(hidden, down_weight[0], preferred_element_type=jnp.float32)
+    partial_value = partial_value.astype(jnp.bfloat16)
+    over_units = lax.psum_scatter(partial_value, "tensor", scatter_dimension=1, tiled=True)
+    return lax.psum_scatter(over_units, "expert", scatter_dimension=0, tiled=True)
+
+
+def local(tokens, route_scale, expert_ids, gate_weight, up_weight, down_weight):
+    tok_rows = tokens.shape[0]
+    n_devices = lax.axis_size("expert")
+    capacity = min(tok_rows, 2 * tok_rows * SPAN // n_devices)
+    if capacity == tok_rows:
+        return gathered(tokens, route_scale, expert_ids, gate_weight, up_weight, down_weight)
+    return dispatched(tokens, route_scale, expert_ids, gate_weight, up_weight, down_weight)
+
+
 def solution(mesh):
     placed = (
         P(("groups", "expert"), "tensor"),

time: 201 us -> 137 us (0.68)
  blocking collectives: 74.2 us -> 30.7 us
  waiting for transfers between devices: 80.4 us -> 72.8 us
  other arithmetic: 8.23 us -> 1.18 us
  starting transfers between devices: 4.72 us -> 0.09 us
  local copies, waits for them, and re-layouts: 8.75 us -> 6.56 us
    all_to_all x1 -> x0, blocking collectives: 64.9 us -> none  [local(): lax.all_to_all(outgoing, 'expert', split_axis=0, concat_axis=0, tiled=True)]
    all_to_all x1 -> x0, waiting for transfers between devices: 59.1 us -> none  [local(): lax.all_to_all(outgoing_back, 'expert', split_axis=0, concat_axis=0, tile...]
    reduce_scatter x0 -> x1, waiting for transfers between devices: none -> 22.4 us  [gathered(): lax.psum_scatter(over_units, 'expert', scatter_dimension=0, tiled=True)]
    all_gather x1 -> x2, blocking collectives: 9.33 us -> 30.7 us  [the longest x1 19.4 us: gathered(): rows = lax.all_gather(scaled, 'expert', axis=0, tiled=True)]
    all_gather x0 -> x1, waiting for transfers between devices: none -> 15.6 us  [gathered(): full_rows = lax.all_gather(rows, 'tensor', axis=1, tiled=True)]
    unnamed x2 -> x4, waiting for transfers between devices: 21.4 us -> 34.8 us
    all_to_all x1 -> x0, starting transfers between devices: 4.68 us -> none  [local(): lax.all_to_all(outgoing_back, 'expert', split_axis=0, concat_axis=0, tile...]
    reduce_sum x2 -> x0, other arithmetic: 4.44 us -> none  [the longest x1 3.62 us: local(): jnp.sum(returned.astype(jnp.float32).reshape(experts, SPAN, capacity, wid...]
  transfers between devices with their start and end apart: 2 -> 3, of which waited for: 2 -> 3; matrix products, arithmetic and copies ran while one was open for 0% -> 0% of each run, Pallas kernels for 0% -> 0%
where the time goes in v1:
time: 137 us
  waiting for transfers between devices  72.8 us (53%)
  blocking collectives  30.7 us (22%)
  between operations  13.1 us (10%)
  matrix products  12.3 us (9%)
  local copies, waits for them, and re-layouts  6.56 us (5%)
    unnamed x4, waiting for transfers between devices  34.8 us
    reduce_scatter x1, waiting for transfers between devices, gathered(): lax.psum_scatter(over_units, 'expert', scatter_dimension=0, tiled=True)  22.4 us
    all_gather x1, blocking collectives, gathered(): rows = lax.all_gather(scaled, 'expert', axis=0, tiled=True)  19.4 us
    all_gather x1, waiting for transfers between devices, gathered(): full_rows = lax.all_gather(rows, 'tensor', axis=1, tiled=True)  15.6 us
    all_gather x1, blocking collectives, gathered(): routed = lax.all_gather(expert_ids[:, 0], 'expert', axis=0, tiled=True)  11.3 us
    dot_general x1, matrix products, gathered(): jnp.dot(hidden, down_weight[0], preferred_element_type=jnp.float32)  7.27 us
    unnamed x4, local copies, waits for them, and re-layouts  6.56 us
    dot_general x1, matrix products, gathered(): jnp.dot(full_rows, gate_weight[0], preferred_element_type=jnp.float32)  5.05 us
  transfers between devices with their start and end apart: 3, of which 3 were waited for; matrix products, arithmetic and copies ran while one was open for 0% of the time, Pallas kernels for 0%

profile of v1, /device:TPU:0, one launch (start us, length us, event | category | flops | bytes accessed | tf_op | source)
XLA Modules:
  0.0 136.7 jit_solution(16961860777739095103)
XLA Ops:
  6.5 0.0 copy-start
  6.5 0.0 all-gather.3.cloned.1.call-start
  6.5 1.2 multiply_convert_fusion
  7.7 19.4 %all_gather.10 = bf16[512,640]{1,0:T(8,128)(2,1)} all-gather(bf16[128,640]{1,0:T(8,128)(2,1)S(1)} %multiply_convert_fusion), channel_id=1, replica_groups=mesh['groups'=2,'expert'=4,'tensor'=4] {'expert'}, dimensions={0}, use_global_device_ids=true | all-gather | bytes 819200 | tf_op jit(solution)/shard_map/all_gather | solution.py:49
  27.1 0.0 all-gather.3.cloned.1.call-update
  27.1 0.0 reduce-scatter.7.cloned.1.call-start
  27.2 11.3 %all-gather = s32[512,1]{0,1:T(1,128)S(1)} all-gather(s32[128,1]{0,1:T(1,128)} %param.8), channel_id=2, replica_groups=mesh['groups'=2,'expert'=4,'tensor'=4] {'expert'}, dimensions={0}, use_global_device_ids=true | all-gather | bytes 2560 | tf_op jit(solution)/shard_map/all_gather | solution.py:50
  38.5 15.6 %all-gather.3.cloned.1.call-done = bf16[512,2560]{1,0:T(8,128)(2,1)} async-done(((bf16[512,640]{1,0:T(8,128)(2,1)}), bf16[512,2560]{1,0:T(8,128)(2,1)}) %all-gather.3.cloned.1.call-update) | async-done | bytes 2621456 | tf_op jit(solution)/shard_map/all_gather | solution.py:51
  54.1 5.1 %fusion.3 = f32[512,512]{1,0:T(8,128)} fusion(bf16[512,2560]{1,0:T(8,128)(2,1)} %all-gather.3.cloned.1.call-done, bf16[1,2560,512]{2,1,0:T(8,128)(2,1)} %param.9), kind=kOutput, calls=%fused_computation.4 | convolution fusion | flops 1342177280 | bytes 6291456 | tf_op jit(solution)/shard_map/dot_general | solution.py:52
  59.1 0.0 copy-done
  59.1 7.3 %convolution_convert_fusion = bf16[512,2560]{1,0:T(8,128)(2,1)} fusion(bf16[1,512,2560]{2,1,0:T(8,128)(2,1)S(1)} %copy-done, bf16[512,2560]{1,0:T(8,128)(2,1)} %all-gather.3.cloned.1.call-done, bf16[1,2560,512]{2,1,0:T(8,128)(2,1)} %param.10, f32[512,512]{1,0:T(8,128)} %fusion.3, pred[512]{0:T(512)(128)(4,1)S(1)} %compare_reduce_fusion), kind=kOutput, calls=%fused_computation | convolution fusion | flops 2687500288 | bytes 11534848 | tf_op jit(solution)/shard_map/dot_general | solution.py:56
  66.4 4.4 %copy.7 = bf16[512,2560]{0,1:T(8,128)(2,1)} copy(bf16[512,2560]{1,0:T(8,128)(2,1)} %convolution_convert_fusion) | data formatting | bytes 5242880
  70.8 0.0 reduce-scatter.7.cloned.1.call-update
  70.8 0.0 reduce-scatter.5.cloned.1.call-start
  70.9 34.8 %reduce-scatter.7.cloned.1.call-done = bf16[640,512]{1,0:T(8,128)(2,1)} async-done(((bf16[2560,512]{1,0:T(8,128)(2,1)}), bf16[640,512]{1,0:T(8,128)(2,1)}) %reduce-scatter.7.cloned.1.call-update) | async-done | bytes 655376
  105.6 2.2 %copy.8 = bf16[512,640]{1,0:T(8,128)(2,1)} copy(bf16[512,640]{0,1:T(8,128)(2,1)} %bitcast.22) | data formatting | bytes 1310720
  107.8 0.0 reduce-scatter.5.cloned.1.call-update
  107.8 22.4 %reduce-scatter.5.cloned.1.call-done = bf16[128,640]{1,0:T(8,128)(2,1)} async-done(((bf16[512,640]{1,0:T(8,128)(2,1)}), bf16[128,640]{1,0:T(8,128)(2,1)}) %reduce-scatter.5.cloned.1.call-update) | async-done | bytes 163856 | tf_op jit(solution)/shard_map/reduce_scatter | solution.py:59
  (1 shorter events, 0.0 us)
Async XLA Ops:
  6.5 52.6 %copy-start = (bf16[1,512,2560]{2,1,0:T(8,128)(2,1)S(1)}, bf16[1,512,2560]{2,1,0:T(8,128)(2,1)}, u32[]{:S(2)}) copy-start(bf16[1,512,2560]{2,1,0:T(8,128)(2,1)} %param.11) | copy-start | bytes 7864324
  6.5 47.5 %all-gather.3.cloned.1.call-start = ((), (), s32[]{:S(2)}) async-start(), calls=%async_computation.2 | async-start | bytes 3276800 | tf_op jit(solution)/shard_map/all_gather | solution.py:51
  27.1 78.5 %reduce-scatter.7.cloned.1.call-start = ((), (), s32[]{:S(2)}) async-start(), calls=%async_computation.4 | async-start | bytes 3276800
  70.8 59.4 %reduce-scatter.5.cloned.1.call-start = ((), (), s32[]{:S(2)}) async-start(), calls=%async_computation.3 | async-start | bytes 819200 | tf_op jit(solution)/shard_map/reduce_scatter | solution.py:59
Sparse Core Ops, SparseCore 0:
  27.3 26.7 all-gather.2
  70.9 34.6 reduce-scatter.6
  108.0 22.1 reduce-scatter.4

commit v2 on v1

--- a/solution.py
+++ b/solution.py
@@ -44,19 +44,28 @@
 
 
 def gathered(tokens, route_scale, expert_ids, gate_weight, up_weight, down_weight):
+    tok_rows, width = tokens.shape
+    n_expert = lax.axis_size("expert")
+    n_tensor = lax.axis_size("tensor")
     expert = lax.axis_index("expert") // SPAN
     scaled = (tokens.astype(jnp.float32) * route_scale[:, None]).astype(jnp.bfloat16)
-    rows = lax.all_gather(scaled, "expert", axis=0, tiled=True)
-    routed = lax.all_gather(expert_ids[:, 0], "expert", axis=0, tiled=True)
-    full_rows = lax.all_gather(rows, "tensor", axis=1, tiled=True)
-    gate_act = jnp.dot(full_rows, gate_weight[0], preferred_element_type=jnp.float32)
-    up_act = jnp.dot(full_rows, up_weight[0], preferred_element_type=jnp.float32)
-    mine = (routed == expert)[:, None]
+    id_rows = jnp.zeros((16, width), jnp.bfloat16)
+    id_rows = id_rows.at[0, :tok_rows].set(expert_ids[:, 0].astype(jnp.bfloat16))
+    block = jnp.concatenate([scaled, id_rows], axis=0)
+    everything = lax.all_gather(block, ("expert", "tensor"), axis=0, tiled=False)
+    everything = everything.reshape(n_expert, n_tensor, tok_rows + 16, width)
+    routed = everything[:, 0, tok_rows, :tok_rows].reshape(n_expert * tok_rows)
+    rows = everything[:, :, :tok_rows, :]
+    gate_w = gate_weight[0].reshape(n_tensor, width, -1)
+    up_w = up_weight[0].reshape(n_tensor, width, -1)
+    gate_act = jnp.einsum("ztif,tfh->zih", rows, gate_w, preferred_element_type=jnp.float32)
+    up_act = jnp.einsum("ztif,tfh->zih", rows, up_w, preferred_element_type=jnp.float32)
+    mine = (routed == expert.astype(jnp.bfloat16)).reshape(n_expert, tok_rows, 1)
     hidden = jnp.where(mine, jax.nn.silu(gate_act) * up_act, 0.0).astype(jnp.bfloat16)
-    partial_value = jnp.dot(hidden, down_weight[0], preferred_element_type=jnp.float32)
-    partial_value = partial_value.astype(jnp.bfloat16)
-    over_units = lax.psum_scatter(partial_value, "tensor", scatter_dimension=1, tiled=True)
-    return lax.psum_scatter(over_units, "expert", scatter_dimension=0, tiled=True)
+    down_w = down_weight[0].reshape(-1, n_tensor, width)
+    partial_value = jnp.einsum("zih,htf->ztif", hidden, down_w, preferred_element_type=jnp.float32)
+    partial_value = partial_value.astype(jnp.bfloat16).reshape(n_expert * n_tensor, tok_rows, width)
+    return lax.psum_scatter(partial_value, ("expert", "tensor"), scatter_dimension=0, tiled=True).reshape(tok_rows, width)
 
 
 def local(tokens, route_scale, expert_ids, gate_weight, up_weight, down_weight):

time: 137 us -> 140 us (1.022)
  waiting for transfers between devices: 72.8 us -> 105 us
  blocking collectives: 30.7 us -> 0 us
  other arithmetic: 1.18 us -> 3.21 us
    reduce_scatter x1, waiting for transfers between devices: 22.4 us -> 62.3 us  [gathered(): lax.psum_scatter(partial_value, ('expert', 'tensor'), scatter_dimension=0...]
    unnamed x4 -> x2, waiting for transfers between devices: 34.8 us -> 0.03 us
    all_gather x2 -> x0, blocking collectives: 30.7 us -> none  [the longest x1 19.4 us: gathered(): rows = lax.all_gather(scaled, 'expert', axis=0, tiled=True)]
    all_gather x1, waiting for transfers between devices: 15.6 us -> 42.2 us  [gathered(): lax.all_gather(block, ('expert', 'tensor'), axis=0, tiled=False)]
    unnamed x4 -> x3, local copies, waits for them, and re-layouts: 6.56 us -> 0.01 us
    another operation x0 -> x1, local copies, waits for them, and re-layouts: none -> 5.73 us  [gathered(): down_w = down_weight[0].reshape(-1, n_tensor, width)]
  transfers between devices with their start and end apart: 3 -> 2, of which waited for: 3 -> 2; matrix products, arithmetic and copies ran while one was open for 0% -> 4% of each run, Pallas kernels for 0% -> 0%
where the time goes in v2:
time: 140 us; the launch traced here: 139 us
  waiting for transfers between devices  105 us (75%)
  between operations  13.4 us (10%)
  matrix products  12.4 us (9%)
  local copies, waits for them, and re-layouts  5.74 us (4%)
  other arithmetic  3.21 us (2%)
    reduce_scatter x1, waiting for transfers between devices, gathered(): lax.psum_scatter(partial_value, ('expert', 'tensor'), scatter_dimension=0...  62.3 us
    all_gather x1, waiting for transfers between devices, gathered(): lax.all_gather(block, ('expert', 'tensor'), axis=0, tiled=False)  42.2 us
    dot_general x1, matrix products, gathered(): jnp.einsum('zih,htf->ztif', hidden, down_w, preferred_element_type=jnp.fl...  7.32 us
    another operation x1, local copies, waits for them, and re-layouts, gathered(): down_w = down_weight[0].reshape(-1, n_tensor, width)  5.73 us
    dot_general x1, matrix products, gathered(): jnp.einsum('ztif,tfh->zih', rows, gate_w, preferred_element_type=jnp.floa...  5.1 us
  transfers between devices with their start and end apart: 2, of which 2 were waited for; matrix products, arithmetic and copies ran while one was open for 4% of the time, Pallas kernels for 0%

profile of v2, /device:TPU:0, one launch (start us, length us, event | category | flops | bytes accessed | tf_op | source)
XLA Modules:
  0.0 139.4 jit_solution(17947786663853540647)
XLA Ops:
  6.5 0.0 copy-start
  6.5 0.0 all-gather.3.cloned.1.call-start
  6.5 0.8 convert_bitcast_fusion
  7.3 1.0 multiply_convert_fusion
  8.4 0.7 fusion.34
  9.1 0.0 all-gather.3.cloned.1.call-update
  9.1 0.0 reduce-scatter.2.cloned.1.call-start
  9.2 5.7 %reshape_squeeze.12 = bf16[512,4,640]{2,1,0:T(4,128)(2,1)} reshape(bf16[1,512,2560]{2,1,0:T(8,128)(2,1)} %param.13) | data formatting | bytes 5242880 | tf_op jit(solution)/shard_map/reshape;squeeze | solution.py:65
  14.9 42.2 %all-gather.3.cloned.1.call-done = bf16[2304,640]{1,0:T(8,128)(2,1)} async-done(((bf16[144,640]{1,0:T(8,128)(2,1)}), bf16[2304,640]{1,0:T(8,128)(2,1)}) %all-gather.3.cloned.1.call-update) | async-done | bytes 2949136 | tf_op jit(solution)/shard_map/all_gather | solution.py:55
  57.1 0.7 slice_compare_fusion
  57.8 5.1 %fusion.10 = f32[4,128,512]{2,1,0:T(8,128)} fusion(bf16[4,640,512,1]{2,1,0,3:T(8,128)(2,1)} %bitcast.51, bf16[4,4,144,640]{3,2,1,0:T(8,128)(2,1)} %bitcast.49), kind=kOutput, calls=%fused_computation.8 | convolution fusion | flops 1342177280 | bytes 6291456 | tf_op jit(solution)/shard_map/ztif,tfh->zih/dot_general | solution.py:61
  62.9 0.0 copy-done
  62.9 7.3 %fusion.7 = bf16[4,128,4,640]{3,1,2,0:T(8,128)(2,1)} fusion(bf16[512,4,640]{2,1,0:T(4,128)(2,1)} %reshape_squeeze.12, bf16[4,640,512,1]{2,1,0,3:T(8,128)(2,1)S(1)} %bitcast.45, bf16[4,4,144,640]{3,2,1,0:T(8,128)(2,1)} %bitcast.50, f32[4,128,512]{2,1,0:T(8,128)} %fusion.10, pred[4,128]{1,0:T(4,128)(4,1)S(1)} %bitcast.47), kind=kOutput, calls=%fused_computation.7 | convolution fusion | flops 2687500288 | bytes 11534848 | tf_op jit(solution)/shard_map/zih,htf->ztif/dot_general | solution.py:66
  70.2 0.0 reduce-scatter.2.cloned.1.call-update
  70.2 62.3 %reduce-scatter.2.cloned.1.call-done = bf16[1,128,640]{2,1,0:T(8,128)(2,1)} async-done(((bf16[16,128,640]{2,1,0:T(8,128)(2,1)}), bf16[1,128,640]{2,1,0:T(8,128)(2,1)}) %reduce-scatter.2.cloned.1.call-update) | async-done | bytes 163856 | tf_op jit(solution)/shard_map/reduce_scatter | solution.py:68
  (1 shorter events, 0.0 us)
Async XLA Ops:
  6.5 56.4 %copy-start = (bf16[1,2560,512]{2,1,0:T(8,128)(2,1)S(1)}, bf16[1,2560,512]{2,1,0:T(8,128)(2,1)}, u32[]{:S(2)}) copy-start(bf16[1,2560,512]{2,1,0:T(8,128)(2,1)} %param.12) | copy-start | bytes 7864324
  6.5 50.5 %all-gather.3.cloned.1.call-start = ((), (), s32[]{:S(2)}) async-start(), calls=%async_computation.2 | async-start | bytes 3133440 | tf_op jit(solution)/shard_map/all_gather | solution.py:55
  9.1 123.5 %reduce-scatter.2.cloned.1.call-start = ((), (), s32[]{:S(2)}) async-start(), calls=%async_computation.1 | async-start | bytes 2785280 | tf_op jit(solution)/shard_map/reduce_scatter | solution.py:68
Sparse Core Ops, SparseCore 0:
  9.5 47.5 all-gather.2
  70.4 62.1 reduce-scatter.1

commit v3 on v2

--- a/solution.py
+++ b/solution.py
@@ -43,36 +43,70 @@
     return summed
 
 
+def _xor_pairs(size, k):
+    return [(i, i ^ k) for i in range(size)]
+
+
+def _full_rows(piece, x, c, n_tensor):
+    other_x = lax.ppermute(piece, "tensor", _xor_pairs(n_tensor, 2))
+    by_x = jnp.where(x == 0, jnp.stack([piece, other_x]), jnp.stack([other_x, piece]))
+    other_c = lax.ppermute(by_x, "tensor", _xor_pairs(n_tensor, 1))
+    return jnp.where(c == 0, jnp.stack([by_x, other_c]), jnp.stack([other_c, by_x]))
+
+
+def _unit_sum(partial_value, x, c, n_tensor):
+    mine_c = jnp.where(c == 0, partial_value[:, :, 0], partial_value[:, :, 1])
+    send_c = jnp.where(c == 0, partial_value[:, :, 1], partial_value[:, :, 0])
+    over_c = mine_c.astype(jnp.float32) + lax.ppermute(
+        send_c, "tensor", _xor_pairs(n_tensor, 1)).astype(jnp.float32)
+    mine_x = jnp.where(x == 0, over_c[:, 0], over_c[:, 1])
+    send_x = jnp.where(x == 0, over_c[:, 1], over_c[:, 0]).astype(jnp.bfloat16)
+    return mine_x + lax.ppermute(send_x, "tensor", _xor_pairs(n_tensor, 2)).astype(jnp.float32)
+
+
 def gathered(tokens, route_scale, expert_ids, gate_weight, up_weight, down_weight):
     tok_rows, width = tokens.shape
     n_expert = lax.axis_size("expert")
     n_tensor = lax.axis_size("tensor")
-    expert = lax.axis_index("expert") // SPAN
+    me = lax.axis_index("expert")
+    t = lax.axis_index("tensor")
+    x, c = t // 2, t % 2
+    expert = (me // SPAN).astype(jnp.bfloat16)
     scaled = (tokens.astype(jnp.float32) * route_scale[:, None]).astype(jnp.bfloat16)
     id_rows = jnp.zeros((16, width), jnp.bfloat16)
     id_rows = id_rows.at[0, :tok_rows].set(expert_ids[:, 0].astype(jnp.bfloat16))
     block = jnp.concatenate([scaled, id_rows], axis=0)
-    everything = lax.all_gather(block, ("expert", "tensor"), axis=0, tiled=False)
-    everything = everything.reshape(n_expert, n_tensor, tok_rows + 16, width)
-    routed = everything[:, 0, tok_rows, :tok_rows].reshape(n_expert * tok_rows)
-    rows = everything[:, :, :tok_rows, :]
-    gate_w = gate_weight[0].reshape(n_tensor, width, -1)
-    up_w = up_weight[0].reshape(n_tensor, width, -1)
-    gate_act = jnp.einsum("ztif,tfh->zih", rows, gate_w, preferred_element_type=jnp.float32)
-    up_act = jnp.einsum("ztif,tfh->zih", rows, up_w, preferred_element_type=jnp.float32)
-    mine = (routed == expert.astype(jnp.bfloat16)).reshape(n_expert, tok_rows, 1)
-    hidden = jnp.where(mine, jax.nn.silu(gate_act) * up_act, 0.0).astype(jnp.bfloat16)
-    down_w = down_weight[0].reshape(-1, n_tensor, width)
-    partial_value = jnp.einsum("zih,htf->ztif", hidden, down_w, preferred_element_type=jnp.float32)
-    partial_value = partial_value.astype(jnp.bfloat16).reshape(n_expert * n_tensor, tok_rows, width)
-    return lax.psum_scatter(partial_value, ("expert", "tensor"), scatter_dimension=0, tiled=True).reshape(tok_rows, width)
+    blocks = [block] + [
+        lax.ppermute(block, "expert", _xor_pairs(n_expert, k)) for k in range(1, n_expert)
+    ]
+    hid = gate_weight.shape[2]
+    gate_w = gate_weight[0].reshape(2, 2, width, hid)
+    up_w = up_weight[0].reshape(2, 2, width, hid)
+    down_w = down_weight[0].reshape(hid, 2, 2, width)
+    total = None
+    for k, blk in enumerate(blocks):
+        routed = blk[tok_rows, :tok_rows]
+        rows = _full_rows(blk[:tok_rows], x, c, n_tensor)
+        gate_act = jnp.einsum("cxrf,xcfh->rh", rows, gate_w, preferred_element_type=jnp.float32)
+        up_act = jnp.einsum("cxrf,xcfh->rh", rows, up_w, preferred_element_type=jnp.float32)
+        mine = (routed == expert)[:, None]
+        hidden = jnp.where(mine, jax.nn.silu(gate_act) * up_act, 0.0).astype(jnp.bfloat16)
+        partial_value = jnp.einsum("rh,hxcf->rxcf", hidden, down_w, preferred_element_type=jnp.float32)
+        summed = _unit_sum(partial_value.astype(jnp.bfloat16), x, c, n_tensor)
+        if k:
+            summed = lax.ppermute(
+                summed.astype(jnp.bfloat16), "expert", _xor_pairs(n_expert, k)).astype(jnp.float32)
+        total = summed if total is None else total + summed
+    return total.astype(jnp.bfloat16)
 
 
 def local(tokens, route_scale, expert_ids, gate_weight, up_weight, down_weight):
     tok_rows = tokens.shape[0]
     n_devices = lax.axis_size("expert")
     capacity = min(tok_rows, 2 * tok_rows * SPAN // n_devices)
-    if capacity == tok_rows:
+    n_tensor = lax.axis_size("tensor")
+    shaped = n_tensor == 4 and n_devices in (1, 2, 4) and tok_rows <= tokens.shape[1]
+    if capacity == tok_rows and shaped:
         return gathered(tokens, route_scale, expert_ids, gate_weight, up_weight, down_weight)
     return dispatched(tokens, route_scale, expert_ids, gate_weight, up_weight, down_weight)
 

time: 140 us -> 97.3 us (0.69)
  waiting for transfers between devices: 105 us -> 19 us
  starting transfers between devices: 0.04 us -> 22.5 us
  other arithmetic: 3.21 us -> 20.8 us
  between operations: 13.4 us -> 0.27 us
  matrix products: 12.4 us -> 24.4 us
  local copies, waits for them, and re-layouts: 5.74 us -> 9.68 us
    reduce_scatter x1 -> x0, waiting for transfers between devices: 62.3 us -> none  [gathered(): lax.psum_scatter(partial_value, ('expert', 'tensor'), scatter_dimension=0...]
    all_gather x1 -> x0, waiting for transfers between devices: 42.2 us -> none  [gathered(): lax.all_gather(block, ('expert', 'tensor'), axis=0, tiled=False)]
    ppermute x0 -> x22, starting transfers between devices: none -> 22.5 us  [the longest x3 6.96 us: gathered(): lax.ppermute(summed.astype(jnp.bfloat16), 'expert', _xor_pairs(n_expert, k))]
    ppermute x0 -> x22, waiting for transfers between devices: none -> 19 us  [the longest x3 8.76 us: gathered(): lax.ppermute(summed.astype(jnp.bfloat16), 'expert', _xor_pairs(n_expert, k))]
    dot_general x2 -> x8, matrix products: 12.4 us -> 24.4 us  [the longest x4 15.2 us: gathered(): jnp.einsum('rh,hxcf->rxcf', hidden, down_w, preferred_element_type=jnp.fl...]
    select_n x0 -> x12, other arithmetic: none -> 10.5 us  [the longest x4 5.67 us: _unit_sum(): send_c = jnp.where(c == 0, partial_value[:, :, 1], partial_value[:, :, 0])]
    another operation x1 -> x4, local copies, waits for them, and re-layouts: 5.73 us -> 9.64 us  [the longest x1 6.66 us: gathered(): down_w = down_weight[0].reshape(hid, 2, 2, width)]
    add x0 -> x4, other arithmetic: none -> 3.36 us  [_unit_sum(): mine_c.astype(jnp.float32)]
  transfers between devices with their start and end apart: 2 -> 22, of which waited for: 2 -> 7; matrix products, arithmetic and copies ran while one was open for 4% -> 54% of each run, Pallas kernels for 0% -> 0%
where the time goes in v3:
time: 97.3 us; the launch traced here: 96.6 us
  matrix products  24.4 us (25%)
  starting transfers between devices  22.5 us (23%)
  other arithmetic  20.8 us (21%)
  waiting for transfers between devices  19 us (20%)
  local copies, waits for them, and re-layouts  9.68 us (10%)
    dot_general x4, matrix products, gathered(): jnp.einsum('rh,hxcf->rxcf', hidden, down_w, preferred_element_type=jnp.fl...  15.2 us
    dot_general x4, matrix products, gathered(): jnp.einsum('cxrf,xcfh->rh', rows, gate_w, preferred_element_type=jnp.floa...  9.22 us
    ppermute x3, waiting for transfers between devices, gathered(): lax.ppermute(summed.astype(jnp.bfloat16), 'expert', _xor_pairs(n_expert, k))  8.76 us
    ppermute x3, starting transfers between devices, gathered(): lax.ppermute(summed.astype(jnp.bfloat16), 'expert', _xor_pairs(n_expert, k))  6.96 us
    another operation x1, local copies, waits for them, and re-layouts, gathered(): down_w = down_weight[0].reshape(hid, 2, 2, width)  6.66 us
    ppermute x3, starting transfers between devices, gathered(): lax.ppermute(block, 'expert', _xor_pairs(n_expert, k))  5.76 us
    select_n x4, other arithmetic, _unit_sum(): send_c = jnp.where(c == 0, partial_value[:, :, 1], partial_value[:, :, 0])  5.67 us
    select_n x8, other arithmetic, _full_rows(): jnp.where(x == 0, jnp.stack([piece, other_x]), jnp.stack([other_x, piece]))  4.83 us
  transfers between devices with their start and end apart: 22, of which 7 were waited for; matrix products, arithmetic and copies ran while one was open for 54% of the time, Pallas kernels for 0%

profile of v3, /device:TPU:0, one launch (start us, length us, event | category | flops | bytes accessed | tf_op | source)
XLA Modules:
  0.0 96.6 jit_solution(3897902540268058463)
XLA Ops:
  0.0 0.8 convert_bitcast_fusion
  0.8 1.0 %multiply_convert_fusion = bf16[128,640]{1,0:T(8,128)(2,1)S(1)} fusion(bf16[128,640]{1,0:T(8,128)(2,1)} %param.8, f32[128]{0:T(128)} %param.9), kind=kLoop, calls=%fused_computation.83 | loop fusion | flops 245760 | bytes 328192 | tf_op jit(solution)/shard_map/convert_element_type | solution.py:75
  1.9 5.1 %collective-permute-start.16 = (bf16[144,640]{1,0:T(8,128)(2,1)S(1)}, bf16[144,640]{1,0:T(8,128)(2,1)}, u32[]{:S(2)}, u32[]{:S(2)}) collective-permute-start(bf16[144,640]{1,0:T(8,128)(2,1)S(1)} %fusion.98), channel_id=1, source_target_pairs={{0,12},{4,8},{8,4},{12,0},{1,13},{5,9},{9,5},{13,1},{2,14},{6,10},... | collective-permute-start | bytes 552968 | tf_op jit(solution)/shard_map/ppermute | solution.py:80
  7.6 1.6 %collective-permute-start = (bf16[128,640]{1,0:T(8,128)(2,1)S(1)}, bf16[128,640]{1,0:T(8,128)(2,1)S(1)}, u32[]{:S(2)}, u32[]{:S(2)}) collective-permute-start(bf16[128,640]{1,0:T(8,128)(2,1)S(1)} %multiply_convert_fusion), channel_id=1, source_target_pairs={{0,2},{1,3},{2,0},{3,1},{4,6},{5,7},{6,4},{7,5},{8,10},{9,11},{10,... | collective-permute-start | bytes 491528 | tf_op jit(solution)/shard_map/ppermute | solution.py:51
  9.2 1.0 %fusion.154 = bf16[1,128,640]{2,1,0:T(8,128)(2,1)S(1)} fusion(f32[128]{0:T(128)} %param.9, bf16[128,640]{1,0:T(8,128)(2,1)} %param.8), kind=kLoop, calls=%fused_computation.140 | loop fusion | flops 245760 | bytes 328192 | tf_op jit(solution)/shard_map/stack | solution.py:52
  10.3 1.0 %fusion.153 = bf16[1,1,128,640]{3,2,1,0:T(8,128)(2,1)S(1)} fusion(f32[128]{0:T(128)} %param.9, bf16[128,640]{1,0:T(8,128)(2,1)} %param.8), kind=kLoop, calls=%fused_computation.139 | loop fusion | flops 245760 | bytes 328192 | tf_op jit(solution)/shard_map/stack | solution.py:52
  11.3 6.7 %reshape_squeeze.11 = bf16[512,2,2,640]{3,2,1,0:T(2,128)(2,1)} reshape(bf16[1,512,2560]{2,1,0:T(8,128)(2,1)} %param.13) | data formatting | bytes 5242880 | tf_op jit(solution)/shard_map/reshape;squeeze | solution.py:85
  18.2 1.1 %slice_bitcast_fusion.1 = (bf16[1,1,128,640]{3,2,1,0:T(8,128)(2,1)S(1)}, bf16[1,128,640]{2,1,0:T(8,128)(2,1)S(1)}, bf16[128,640]{1,0:T(8,128)(2,1)S(1)}) fusion(bf16[144,640]{1,0:T(8,128)(2,1)} %collective-permute-done.16), kind=kLoop, calls=%fused_computation.134 | loop fusion | bytes 655360 | tf_op jit(solution)/shard_map/stack | solution.py:52
  19.8 2.9 %collective-permute-done.10 = bf16[144,640]{1,0:T(8,128)(2,1)} collective-permute-done((bf16[144,640]{1,0:T(8,128)(2,1)S(1)}, bf16[144,640]{1,0:T(8,128)(2,1)}, u32[]{:S(2)}, u32[]{:S(2)}) %collective-permute-start.10) | collective-permute-done | bytes 184352 | tf_op jit(solution)/shard_map/ppermute | solution.py:80
  22.7 1.0 slice_bitcast_fusion.3
  23.7 1.6 %collective-permute-start.11 = (bf16[128,640]{1,0:T(8,128)(2,1)S(1)}, bf16[128,640]{1,0:T(8,128)(2,1)S(1)}, u32[]{:S(2)}, u32[]{:S(2)}) collective-permute-start(bf16[128,640]{1,0:T(8,128)(2,1)S(1)} %get-tuple-element.22), channel_id=1, source_target_pairs={{0,2},{1,3},{2,0},{3,1},{4,6},{5,7},{6,4},{7,5},{8,10},{9,11},{10,... | collective-permute-start | bytes 491528 | tf_op jit(solution)/shard_map/ppermute | solution.py:51
  25.2 1.0 slice_bitcast_fusion.5
  26.8 0.7 compare_bitcast_fusion
  27.5 0.7 compare_bitcast_fusion.1
  28.8 0.8 maximum_select_fusion.11
  29.6 1.3 %collective-permute-done.11 = bf16[128,640]{1,0:T(8,128)(2,1)S(1)} collective-permute-done((bf16[128,640]{1,0:T(8,128)(2,1)S(1)}, bf16[128,640]{1,0:T(8,128)(2,1)S(1)}, u32[]{:S(2)}, u32[]{:S(2)}) %collective-permute-start.11) | collective-permute-done | bytes 163872 | tf_op jit(solution)/shard_map/ppermute | solution.py:51
  30.9 0.8 maximum_select_fusion.9
  31.7 1.3 %collective-permute-done.5 = bf16[128,640]{1,0:T(8,128)(2,1)S(1)} collective-permute-done((bf16[128,640]{1,0:T(8,128)(2,1)S(1)}, bf16[128,640]{1,0:T(8,128)(2,1)S(1)}, u32[]{:S(2)}, u32[]{:S(2)}) %collective-permute-start.5) | collective-permute-done | bytes 163872 | tf_op jit(solution)/shard_map/ppermute | solution.py:51
  33.0 0.8 maximum_select_fusion.7
  33.8 0.8 maximum_select_fusion.10
  34.6 0.8 maximum_select_fusion.8
  35.4 0.8 maximum_select_fusion.6
  36.2 1.2 %fusion.36 = f32[128,512]{1,0:T(8,128)} fusion(bf16[2,2,640,512]{3,2,1,0:T(8,128)(2,1)S(1)} %bitcast.196, bf16[1,2,128,640]{3,2,1,0:T(8,128)(2,1)S(1)} %bitcast.197, bf16[1,2,128,640]{3,2,1,0:T(8,128)(2,1)S(1)} %maximum_select_fusion.4, pred[]{:T(512)S(6)} %eq.75), kind=kOutput, calls=%fused_computation.28 | convolution fusion | flops 336527360 | bytes 3538945 | tf_op jit(solution)/shard_map/cxrf,xcfh->rh/dot_general | solution.py:90
  37.4 3.2 %fusion.33 = bf16[128,2,2,640]{3,0,2,1:T(8,128)(2,1)S(1)} fusion(bf16[512,2,2,640]{3,2,1,0:T(2,128)(2,1)} %reshape_squeeze.11, bf16[2,2,640,512]{3,2,1,0:T(8,128)(2,1)S(1)} %bitcast.181, f32[128,512]{1,0:T(8,128)} %fusion.36, pred[128]{0:T(512)(128)(4,1)S(1)} %compare_bitcast_fusion.3, bf16[1,2,128,640]{3,2,1,0:T(8,128)(2,1)} %bitcast.198, ...), kind=kOutput, calls=%fused_computation.27 | convolution fusion | flops 672858112 | bytes 6815873 | tf_op jit(solution)/shard_map/rh,hxcf->rxcf/dot_general | solution.py:94
  40.6 0.8 fusion.84
  41.9 2.7 %fusion.45 = f32[128,512]{1,0:T(8,128)S(1)} fusion(bf16[2,2,640,512]{3,2,1,0:T(8,128)(2,1)} %bitcast.193, bf16[1,2,128,640]{3,2,1,0:T(8,128)(2,1)} %bitcast.60, bf16[1,2,128,640]{3,2,1,0:T(8,128)(2,1)} %maximum_select_fusion.10, pred[]{:T(512)S(6)} %eq.75), kind=kOutput, calls=%fused_computation.31 | convolution fusion | flops 336527360 | bytes 3538945 | tf_op jit(solution)/shard_map/cxrf,xcfh->rh/dot_general | solution.py:90
  44.6 4.0 %fusion.30 = bf16[128,2,2,640]{3,0,1,2:T(8,128)(2,1)} fusion(bf16[512,2,2,640]{3,2,1,0:T(2,128)(2,1)} %reshape_squeeze.11, bf16[2,2,640,512]{3,2,1,0:T(8,128)(2,1)S(1)} %bitcast.182, f32[128,512]{1,0:T(8,128)S(1)} %fusion.45, pred[128]{0:T(512)(128)(4,1)S(1)} %compare_bitcast_fusion, bf16[1,2,128,640]{3,2,1,0:T(8,128)(2,1)} %bitcast.60, ...), kind=kOutput, calls=%fused_computation.26 | convolution fusion | flops 672858112 | bytes 6815873 | tf_op jit(solution)/shard_map/rh,hxcf->rxcf/dot_general | solution.py:94
  48.6 1.9 %select_bitcast_fusion = bf16[128,2,640]{2,0,1:T(8,128)(2,1)} fusion(pred[]{:T(512)S(6)} %eq.75, bf16[128,2,2,640]{3,0,1,2:T(8,128)(2,1)} %fusion.30), kind=kLoop, calls=%fused_computation.77 | loop fusion | flops 163840 | bytes 983041 | tf_op jit(solution)/shard_map/jit(_where)/select_n | solution.py:59
  50.5 2.7 %fusion.42 = f32[128,512]{1,0:T(8,128)S(1)} fusion(bf16[2,2,640,512]{3,2,1,0:T(8,128)(2,1)} %bitcast.194, bf16[1,2,128,640]{3,2,1,0:T(8,128)(2,1)} %bitcast.44, bf16[1,2,128,640]{3,2,1,0:T(8,128)(2,1)} %maximum_select_fusion.8, pred[]{:T(512)S(6)} %eq.75), kind=kOutput, calls=%fused_computation.30 | convolution fusion | flops 336527360 | bytes 3538945 | tf_op jit(solution)/shard_map/cxrf,xcfh->rh/dot_general | solution.py:90
  53.1 4.0 %fusion.27 = bf16[128,2,2,640]{3,0,1,2:T(8,128)(2,1)} fusion(bf16[512,2,2,640]{3,2,1,0:T(2,128)(2,1)} %reshape_squeeze.11, bf16[2,2,640,512]{3,2,1,0:T(8,128)(2,1)S(1)} %bitcast.183, f32[128,512]{1,0:T(8,128)S(1)} %fusion.42, pred[128]{0:T(512)(128)(4,1)S(1)} %compare_bitcast_fusion.1, bf16[1,2,128,640]{3,2,1,0:T(8,128)(2,1)} %bitcast.44, ...), kind=kOutput, calls=%fused_computation.25 | convolution fusion | flops 672858112 | bytes 6815873 | tf_op jit(solution)/shard_map/rh,hxcf->rxcf/dot_general | solution.py:94
  57.1 1.8 %select_bitcast_fusion.1 = bf16[128,2,640]{2,0,1:T(8,128)(2,1)} fusion(pred[]{:T(512)S(6)} %eq.75, bf16[128,2,2,640]{3,0,1,2:T(8,128)(2,1)} %fusion.27), kind=kLoop, calls=%fused_computation.79 | loop fusion | flops 163840 | bytes 983041 | tf_op jit(solution)/shard_map/jit(_where)/select_n | solution.py:59
  59.5 2.7 %fusion.39 = f32[128,512]{1,0:T(8,128)S(1)} fusion(bf16[2,2,640,512]{3,2,1,0:T(8,128)(2,1)} %bitcast.195, bf16[1,2,128,640]{3,2,1,0:T(8,128)(2,1)} %bitcast.28, bf16[1,2,128,640]{3,2,1,0:T(8,128)(2,1)} %maximum_select_fusion.6, pred[]{:T(512)S(6)} %eq.75), kind=kOutput, calls=%fused_computation.29 | convolution fusion | flops 336527360 | bytes 3538945 | tf_op jit(solution)/shard_map/cxrf,xcfh->rh/dot_general | solution.py:90
  62.1 4.0 %fusion.24 = bf16[128,2,2,640]{3,0,1,2:T(8,128)(2,1)} fusion(bf16[512,2,2,640]{3,2,1,0:T(2,128)(2,1)} %reshape_squeeze.11, bf16[2,2,640,512]{3,2,1,0:T(8,128)(2,1)S(1)} %bitcast.184, f32[128,512]{1,0:T(8,128)S(1)} %fusion.39, pred[128]{0:T(512)(128)(4,1)S(1)} %compare_bitcast_fusion.2, bf16[1,2,128,640]{3,2,1,0:T(8,128)(2,1)} %bitcast.28, ...), kind=kOutput, calls=%fused_computation.24 | convolution fusion | flops 672858112 | bytes 6815873 | tf_op jit(solution)/shard_map/rh,hxcf->rxcf/dot_general | solution.py:94
  66.1 1.2 %select_bitcast_fusion.2 = bf16[128,2,640]{2,0,1:T(8,128)(2,1)S(1)} fusion(pred[]{:T(512)S(6)} %eq.75, bf16[128,2,2,640]{3,0,1,2:T(8,128)(2,1)} %fusion.24), kind=kLoop, calls=%fused_computation.81 | loop fusion | flops 163840 | bytes 983041 | tf_op jit(solution)/shard_map/jit(_where)/select_n | solution.py:59
  67.4 1.1 %convert_add_fusion.3 = f32[128,2,640]{2,0,1:T(8,128)S(1)} fusion(bf16[128,2,640]{2,0,1:T(8,128)(2,1)} %collective-permute-done.2, pred[]{:T(512)S(6)} %eq.75, bf16[128,2,2,640]{3,0,2,1:T(8,128)(2,1)S(1)} %fusion.33), kind=kLoop, calls=%fused_computation.50 | loop fusion | flops 655360 | bytes 1638401 | tf_op jit(solution)/shard_map/add | solution.py:60
  68.6 1.0 %collective-permute-start.3 = (bf16[128,640]{1,0:T(8,128)(2,1)S(1)}, bf16[128,640]{1,0:T(8,128)(2,1)S(1)}, u32[]{:S(2)}, u32[]{:S(2)}) collective-permute-start(bf16[128,640]{1,0:T(8,128)(2,1)S(1)} %fusion.99), channel_id=1, source_target_pairs={{0,2},{1,3},{2,0},{3,1},{4,6},{5,7},{6,4},{7,5},{8,10},{9,11},{10,... | collective-permute-start | bytes 491528 | tf_op jit(solution)/shard_map/ppermute | solution.py:64
  69.6 1.1 %convert_add_fusion = f32[128,2,640]{2,0,1:T(8,128)S(1)} fusion(bf16[128,2,640]{2,0,1:T(8,128)(2,1)} %collective-permute-done.19, pred[]{:T(512)S(6)} %eq.75, bf16[128,2,2,640]{3,0,1,2:T(8,128)(2,1)S(1)} %copy-done.1), kind=kLoop, calls=%fused_computation.47 | loop fusion | flops 655360 | bytes 1638401 | tf_op jit(solution)/shard_map/add | solution.py:60
  70.8 1.1 %collective-permute-start.20 = (bf16[128,640]{1,0:T(8,128)(2,1)S(1)}, bf16[128,640]{1,0:T(8,128)(2,1)S(1)}, u32[]{:S(2)}, u32[]{:S(2)}) collective-permute-start(bf16[128,640]{1,0:T(8,128)(2,1)S(1)} %fusion.102), channel_id=1, source_target_pairs={{0,2},{1,3},{2,0},{3,1},{4,6},{5,7},{6,4},{7,5},{8,10},{9,11},{10,... | collective-permute-start | bytes 491528 | tf_op jit(solution)/shard_map/ppermute | solution.py:64
  71.9 1.1 %convert_add_fusion.1 = f32[128,2,640]{2,0,1:T(8,128)S(1)} fusion(bf16[128,2,640]{2,0,1:T(8,128)(2,1)} %collective-permute-done.13, pred[]{:T(512)S(6)} %eq.75, bf16[128,2,2,640]{3,0,1,2:T(8,128)(2,1)S(1)} %copy-done.2), kind=kLoop, calls=%fused_computation.48 | loop fusion | flops 655360 | bytes 1638401 | tf_op jit(solution)/shard_map/add | solution.py:60
  73.0 1.0 %collective-permute-start.14 = (bf16[128,640]{1,0:T(8,128)(2,1)S(1)}, bf16[128,640]{1,0:T(8,128)(2,1)S(1)}, u32[]{:S(2)}, u32[]{:S(2)}) collective-permute-start(bf16[128,640]{1,0:T(8,128)(2,1)S(1)} %fusion.101), channel_id=1, source_target_pairs={{0,2},{1,3},{2,0},{3,1},{4,6},{5,7},{6,4},{7,5},{8,10},{9,11},{10,... | collective-permute-start | bytes 491528 | tf_op jit(solution)/shard_map/ppermute | solution.py:64
  74.2 1.1 %collective-permute-start.8 = (bf16[128,640]{1,0:T(8,128)(2,1)S(1)}, bf16[128,640]{1,0:T(8,128)(2,1)S(1)}, u32[]{:S(2)}, u32[]{:S(2)}) collective-permute-start(bf16[128,640]{1,0:T(8,128)(2,1)S(1)} %fusion.100), channel_id=1, source_target_pairs={{0,2},{1,3},{2,0},{3,1},{4,6},{5,7},{6,4},{7,5},{8,10},{9,11},{10,... | collective-permute-start | bytes 491528 | tf_op jit(solution)/shard_map/ppermute | solution.py:64
  75.3 3.8 %collective-permute-done.20 = bf16[128,640]{1,0:T(8,128)(2,1)S(1)} collective-permute-done((bf16[128,640]{1,0:T(8,128)(2,1)S(1)}, bf16[128,640]{1,0:T(8,128)(2,1)S(1)}, u32[]{:S(2)}, u32[]{:S(2)}) %collective-permute-start.20) | collective-permute-done | bytes 163872 | tf_op jit(solution)/shard_map/ppermute | solution.py:64
  79.2 3.7 %collective-permute-start.21 = (bf16[128,640]{1,0:T(8,128)(2,1)S(1)}, bf16[128,640]{1,0:T(8,128)(2,1)S(1)}, u32[]{:S(2)}, u32[]{:S(2)}) collective-permute-start(bf16[128,640]{1,0:T(8,128)(2,1)S(1)} %fusion.86), channel_id=1, source_target_pairs={{0,12},{4,8},{8,4},{12,0},{1,13},{5,9},{9,5},{13,1},{2,14},{6,10},... | collective-permute-start | bytes 491528 | tf_op jit(solution)/shard_map/ppermute | solution.py:97
  82.9 2.0 %collective-permute-start.15 = (bf16[128,640]{1,0:T(8,128)(2,1)S(1)}, bf16[128,640]{1,0:T(8,128)(2,1)S(1)}, u32[]{:S(2)}, u32[]{:S(2)}) collective-permute-start(bf16[128,640]{1,0:T(8,128)(2,1)S(1)} %fusion.87), channel_id=1, source_target_pairs={{0,8},{4,12},{8,0},{12,4},{1,9},{5,13},{9,1},{13,5},{2,10},{6,14},... | collective-permute-start | bytes 491528 | tf_op jit(solution)/shard_map/ppermute | solution.py:97
  84.9 0.9 collective-permute-done.8
  85.8 1.3 %collective-permute-start.9 = (bf16[128,640]{1,0:T(8,128)(2,1)S(1)}, bf16[128,640]{1,0:T(8,128)(2,1)S(1)}, u32[]{:S(2)}, u32[]{:S(2)}) collective-permute-start(bf16[128,640]{1,0:T(8,128)(2,1)S(1)} %fusion.88), channel_id=1, source_target_pairs={{0,4},{4,0},{8,12},{12,8},{1,5},{5,1},{9,13},{13,9},{2,6},{6,2},{1... | collective-permute-start | bytes 491528 | tf_op jit(solution)/shard_map/ppermute | solution.py:97
  87.3 8.5 %collective-permute-done.15 = bf16[128,640]{1,0:T(8,128)(2,1)S(1)} collective-permute-done((bf16[128,640]{1,0:T(8,128)(2,1)S(1)}, bf16[128,640]{1,0:T(8,128)(2,1)S(1)}, u32[]{:S(2)}, u32[]{:S(2)}) %collective-permute-start.15) | collective-permute-done | bytes 163872 | tf_op jit(solution)/shard_map/ppermute | solution.py:97
  95.9 0.8 fusion.92
  (57 shorter events, 4.4 us)
Async XLA Ops:
  0.0 37.4 %copy-start = (bf16[1,2560,512]{2,1,0:T(8,128)(2,1)S(1)}, bf16[1,2560,512]{2,1,0:T(8,128)(2,1)}, u32[]{:S(2)}) copy-start(bf16[1,2560,512]{2,1,0:T(8,128)(2,1)} %param.12) | copy-start | bytes 7864324
  1.9 16.4 %collective-permute-start.16 = (bf16[144,640]{1,0:T(8,128)(2,1)S(1)}, bf16[144,640]{1,0:T(8,128)(2,1)}, u32[]{:S(2)}, u32[]{:S(2)}) collective-permute-start(bf16[144,640]{1,0:T(8,128)(2,1)S(1)} %fusion.98), channel_id=1, source_target_pairs={{0,12},{4,8},{8,4},{12,0},{1,13},{5,9},{9,5},{13,1},{2,14},{6,10},... | collective-permute-start | bytes 552968 | tf_op jit(solution)/shard_map/ppermute | solution.py:80
  7.0 15.7 %collective-permute-start.10 = (bf16[144,640]{1,0:T(8,128)(2,1)S(1)}, bf16[144,640]{1,0:T(8,128)(2,1)}, u32[]{:S(2)}, u32[]{:S(2)}) collective-permute-start(bf16[144,640]{1,0:T(8,128)(2,1)S(1)} %fusion.98), channel_id=1, source_target_pairs={{0,8},{4,12},{8,0},{12,4},{1,9},{5,13},{9,1},{13,5},{2,10},{6,14},... | collective-permute-start | bytes 552968 | tf_op jit(solution)/shard_map/ppermute | solution.py:80
  7.0 18.3 %collective-permute-start.4 = (bf16[144,640]{1,0:T(8,128)(2,1)S(1)}, bf16[144,640]{1,0:T(8,128)(2,1)}, u32[]{:S(2)}, u32[]{:S(2)}) collective-permute-start(bf16[144,640]{1,0:T(8,128)(2,1)S(1)} %fusion.98), channel_id=1, source_target_pairs={{0,4},{4,0},{8,12},{12,8},{1,5},{5,1},{9,13},{13,9},{2,6},{6,2},{1... | collective-permute-start | bytes 552968 | tf_op jit(solution)/shard_map/ppermute | solution.py:80
  7.6 10.4 %collective-permute-start = (bf16[128,640]{1,0:T(8,128)(2,1)S(1)}, bf16[128,640]{1,0:T(8,128)(2,1)S(1)}, u32[]{:S(2)}, u32[]{:S(2)}) collective-permute-start(bf16[128,640]{1,0:T(8,128)(2,1)S(1)} %multiply_convert_fusion), channel_id=1, source_target_pairs={{0,2},{1,3},{2,0},{3,1},{4,6},{5,7},{6,4},{7,5},{8,10},{9,11},{10,... | collective-permute-start | bytes 491528 | tf_op jit(solution)/shard_map/ppermute | solution.py:51
  11.3 6.7 %copy-start.7 = (s32[128,1]{0,1:T(1,128)S(1)}, s32[128,1]{0,1:T(1,128)}, u32[]{:S(2)}) copy-start(s32[128,1]{0,1:T(1,128)} %param.10) | copy-start | bytes 1540
  18.1 18.1 %collective-permute-start.1 = (bf16[2,128,640]{2,1,0:T(8,128)(2,1)S(1)}, bf16[2,128,640]{2,1,0:T(8,128)(2,1)S(1)}, u32[]{:S(2)}, u32[]{:S(2)}) collective-permute-start(bf16[2,128,640]{2,1,0:T(8,128)(2,1)S(1)} %maximum_select_fusion.5), channel_id=1, source_target_pairs={{0,1},{1,0},{2,3},{3,2},{4,5},{5,4},{6,7},{7,6},{8,9},{9,8},{10,11... | collective-permute-start | bytes 983048 | tf_op jit(solution)/shard_map/ppermute | solution.py:53
  18.2 18.0 %copy-start.4 = (bf16[1,2,128,640]{3,2,1,0:T(8,128)(2,1)}, bf16[1,2,128,640]{3,2,1,0:T(8,128)(2,1)S(1)}, u32[]{:S(2)}) copy-start(bf16[1,2,128,640]{3,2,1,0:T(8,128)(2,1)S(1)} %maximum_select_fusion.4) | copy-start | bytes 983044
  19.3 16.9 %copy-start.5 = (bf16[1,2560,512]{2,1,0:T(8,128)(2,1)S(1)}, bf16[1,2560,512]{2,1,0:T(8,128)(2,1)}, u32[]{:S(2)}) copy-start(bf16[1,2560,512]{2,1,0:T(8,128)(2,1)} %param.11) | copy-start | bytes 7864324
  19.3 9.5 %collective-permute-start.17 = (bf16[128,640]{1,0:T(8,128)(2,1)S(1)}, bf16[128,640]{1,0:T(8,128)(2,1)S(1)}, u32[]{:S(2)}, u32[]{:S(2)}) collective-permute-start(bf16[128,640]{1,0:T(8,128)(2,1)S(1)} %get-tuple-element.25), channel_id=1, source_target_pairs={{0,2},{1,3},{2,0},{3,1},{4,6},{5,7},{6,4},{7,5},{8,10},{9,11},{10,... | collective-permute-start | bytes 491528 | tf_op jit(solution)/shard_map/ppermute | solution.py:51
  23.7 7.2 %collective-permute-start.11 = (bf16[128,640]{1,0:T(8,128)(2,1)S(1)}, bf16[128,640]{1,0:T(8,128)(2,1)S(1)}, u32[]{:S(2)}, u32[]{:S(2)}) collective-permute-start(bf16[128,640]{1,0:T(8,128)(2,1)S(1)} %get-tuple-element.22), channel_id=1, source_target_pairs={{0,2},{1,3},{2,0},{3,1},{4,6},{5,7},{6,4},{7,5},{8,10},{9,11},{10,... | collective-permute-start | bytes 491528 | tf_op jit(solution)/shard_map/ppermute | solution.py:51
  26.2 6.8 %collective-permute-start.5 = (bf16[128,640]{1,0:T(8,128)(2,1)S(1)}, bf16[128,640]{1,0:T(8,128)(2,1)S(1)}, u32[]{:S(2)}, u32[]{:S(2)}) collective-permute-start(bf16[128,640]{1,0:T(8,128)(2,1)S(1)} %get-tuple-element.19), channel_id=1, source_target_pairs={{0,2},{1,3},{2,0},{3,1},{4,6},{5,7},{6,4},{7,5},{8,10},{9,11},{10,... | collective-permute-start | bytes 491528 | tf_op jit(solution)/shard_map/ppermute | solution.py:51
  29.6 12.3 %collective-permute-start.18 = (bf16[2,128,640]{2,1,0:T(8,128)(2,1)}, bf16[2,128,640]{2,1,0:T(8,128)(2,1)}, u32[]{:S(2)}, u32[]{:S(2)}) collective-permute-start(bf16[2,128,640]{2,1,0:T(8,128)(2,1)} %maximum_select_fusion.11), channel_id=1, source_target_pairs={{0,1},{1,0},{2,3},{3,2},{4,5},{5,4},{6,7},{7,6},{8,9},{9,8},{10,11... | collective-permute-start | bytes 983048 | tf_op jit(solution)/shard_map/ppermute | solution.py:53
  31.7 18.8 %collective-permute-start.12 = (bf16[2,128,640]{2,1,0:T(8,128)(2,1)}, bf16[2,128,640]{2,1,0:T(8,128)(2,1)}, u32[]{:S(2)}, u32[]{:S(2)}) collective-permute-start(bf16[2,128,640]{2,1,0:T(8,128)(2,1)} %maximum_select_fusion.9), channel_id=1, source_target_pairs={{0,1},{1,0},{2,3},{3,2},{4,5},{5,4},{6,7},{7,6},{8,9},{9,8},{10,11... | collective-permute-start | bytes 983048 | tf_op jit(solution)/shard_map/ppermute | solution.py:53
  33.8 25.7 %collective-permute-start.6 = (bf16[2,128,640]{2,1,0:T(8,128)(2,1)}, bf16[2,128,640]{2,1,0:T(8,128)(2,1)}, u32[]{:S(2)}, u32[]{:S(2)}) collective-permute-start(bf16[2,128,640]{2,1,0:T(8,128)(2,1)} %maximum_select_fusion.7), channel_id=1, source_target_pairs={{0,1},{1,0},{2,3},{3,2},{4,5},{5,4},{6,7},{7,6},{8,9},{9,8},{10,11... | collective-permute-start | bytes 983048 | tf_op jit(solution)/shard_map/ppermute | solution.py:53
  36.2 1.2 %copy-start.6 = (bf16[2,128,640]{2,1,0:T(8,128)(2,1)}, bf16[2,128,640]{2,1,0:T(8,128)(2,1)S(1)}, u32[]{:S(2)}) copy-start(bf16[2,128,640]{2,1,0:T(8,128)(2,1)S(1)} %collective-permute-done.1) | copy-start | bytes 983044
  41.4 26.0 %collective-permute-start.2 = (bf16[128,2,640]{2,0,1:T(8,128)(2,1)}, bf16[128,2,640]{2,0,1:T(8,128)(2,1)}, u32[]{:S(2)}, u32[]{:S(2)}) collective-permute-start(bf16[128,2,640]{2,0,1:T(8,128)(2,1)} %fusion.84), channel_id=1, source_target_pairs={{0,1},{1,0},{2,3},{3,2},{4,5},{5,4},{6,7},{7,6},{8,9},{9,8},{10,11... | collective-permute-start | bytes 983048 | tf_op jit(solution)/shard_map/ppermute | solution.py:60
  50.4 19.2 %collective-permute-start.19 = (bf16[128,2,640]{2,0,1:T(8,128)(2,1)}, bf16[128,2,640]{2,0,1:T(8,128)(2,1)}, u32[]{:S(2)}, u32[]{:S(2)}) collective-permute-start(bf16[128,2,640]{2,0,1:T(8,128)(2,1)} %select_bitcast_fusion), channel_id=1, source_target_pairs={{0,1},{1,0},{2,3},{3,2},{4,5},{5,4},{6,7},{7,6},{8,9},{9,8},{10,11... | collective-permute-start | bytes 983048 | tf_op jit(solution)/shard_map/ppermute | solution.py:60
  58.9 12.9 %collective-permute-start.13 = (bf16[128,2,640]{2,0,1:T(8,128)(2,1)}, bf16[128,2,640]{2,0,1:T(8,128)(2,1)}, u32[]{:S(2)}, u32[]{:S(2)}) collective-permute-start(bf16[128,2,640]{2,0,1:T(8,128)(2,1)} %select_bitcast_fusion.1), channel_id=1, source_target_pairs={{0,1},{1,0},{2,3},{3,2},{4,5},{5,4},{6,7},{7,6},{8,9},{9,8},{10,11... | collective-permute-start | bytes 983048 | tf_op jit(solution)/shard_map/ppermute | solution.py:60
  66.1 3.5 %copy-start.1 = (bf16[128,2,2,640]{3,0,1,2:T(8,128)(2,1)S(1)}, bf16[128,2,2,640]{3,0,1,2:T(8,128)(2,1)}, u32[]{:S(2)}) copy-start(bf16[128,2,2,640]{3,0,1,2:T(8,128)(2,1)} %fusion.30) | copy-start | bytes 1966084
  66.1 5.7 %copy-start.2 = (bf16[128,2,2,640]{3,0,1,2:T(8,128)(2,1)S(1)}, bf16[128,2,2,640]{3,0,1,2:T(8,128)(2,1)}, u32[]{:S(2)}) copy-start(bf16[128,2,2,640]{3,0,1,2:T(8,128)(2,1)} %fusion.27) | copy-start | bytes 1966084
  67.3 6.7 %collective-permute-start.7 = (bf16[128,2,640]{2,0,1:T(8,128)(2,1)S(1)}, bf16[128,2,640]{2,0,1:T(8,128)(2,1)S(1)}, u32[]{:S(2)}, u32[]{:S(2)}) collective-permute-start(bf16[128,2,640]{2,0,1:T(8,128)(2,1)S(1)} %select_bitcast_fusion.2), channel_id=1, source_target_pairs={{0,1},{1,0},{2,3},{3,2},{4,5},{5,4},{6,7},{7,6},{8,9},{9,8},{10,11... | collective-permute-start | bytes 983048 | tf_op jit(solution)/shard_map/ppermute | solution.py:60
  68.5 5.5 %copy-start.3 = (bf16[128,2,2,640]{3,0,1,2:T(8,128)(2,1)S(1)}, bf16[128,2,2,640]{3,0,1,2:T(8,128)(2,1)}, u32[]{:S(2)}) copy-start(bf16[128,2,2,640]{3,0,1,2:T(8,128)(2,1)} %fusion.24) | copy-start | bytes 1966084
  68.6 18.5 %collective-permute-start.3 = (bf16[128,640]{1,0:T(8,128)(2,1)S(1)}, bf16[128,640]{1,0:T(8,128)(2,1)S(1)}, u32[]{:S(2)}, u32[]{:S(2)}) collective-permute-start(bf16[128,640]{1,0:T(8,128)(2,1)S(1)} %fusion.99), channel_id=1, source_target_pairs={{0,2},{1,3},{2,0},{3,1},{4,6},{5,7},{6,4},{7,5},{8,10},{9,11},{10,... | collective-permute-start | bytes 491528 | tf_op jit(solution)/shard_map/ppermute | solution.py:64
  70.8 8.4 %collective-permute-start.20 = (bf16[128,640]{1,0:T(8,128)(2,1)S(1)}, bf16[128,640]{1,0:T(8,128)(2,1)S(1)}, u32[]{:S(2)}, u32[]{:S(2)}) collective-permute-start(bf16[128,640]{1,0:T(8,128)(2,1)S(1)} %fusion.102), channel_id=1, source_target_pairs={{0,2},{1,3},{2,0},{3,1},{4,6},{5,7},{6,4},{7,5},{8,10},{9,11},{10,... | collective-permute-start | bytes 491528 | tf_op jit(solution)/shard_map/ppermute | solution.py:64
  73.0 9.8 %collective-permute-start.14 = (bf16[128,640]{1,0:T(8,128)(2,1)S(1)}, bf16[128,640]{1,0:T(8,128)(2,1)S(1)}, u32[]{:S(2)}, u32[]{:S(2)}) collective-permute-start(bf16[128,640]{1,0:T(8,128)(2,1)S(1)} %fusion.101), channel_id=1, source_target_pairs={{0,2},{1,3},{2,0},{3,1},{4,6},{5,7},{6,4},{7,5},{8,10},{9,11},{10,... | collective-permute-start | bytes 491528 | tf_op jit(solution)/shard_map/ppermute | solution.py:64
  74.2 11.5 %collective-permute-start.8 = (bf16[128,640]{1,0:T(8,128)(2,1)S(1)}, bf16[128,640]{1,0:T(8,128)(2,1)S(1)}, u32[]{:S(2)}, u32[]{:S(2)}) collective-permute-start(bf16[128,640]{1,0:T(8,128)(2,1)S(1)} %fusion.100), channel_id=1, source_target_pairs={{0,2},{1,3},{2,0},{3,1},{4,6},{5,7},{6,4},{7,5},{8,10},{9,11},{10,... | collective-permute-start | bytes 491528 | tf_op jit(solution)/shard_map/ppermute | solution.py:64
  79.2 8.2 %collective-permute-start.21 = (bf16[128,640]{1,0:T(8,128)(2,1)S(1)}, bf16[128,640]{1,0:T(8,128)(2,1)S(1)}, u32[]{:S(2)}, u32[]{:S(2)}) collective-permute-start(bf16[128,640]{1,0:T(8,128)(2,1)S(1)} %fusion.86), channel_id=1, source_target_pairs={{0,12},{4,8},{8,4},{12,0},{1,13},{5,9},{9,5},{13,1},{2,14},{6,10},... | collective-permute-start | bytes 491528 | tf_op jit(solution)/shard_map/ppermute | solution.py:97
  82.9 13.0 %collective-permute-start.15 = (bf16[128,640]{1,0:T(8,128)(2,1)S(1)}, bf16[128,640]{1,0:T(8,128)(2,1)S(1)}, u32[]{:S(2)}, u32[]{:S(2)}) collective-permute-start(bf16[128,640]{1,0:T(8,128)(2,1)S(1)} %fusion.87), channel_id=1, source_target_pairs={{0,8},{4,12},{8,0},{12,4},{1,9},{5,13},{9,1},{13,5},{2,10},{6,14},... | collective-permute-start | bytes 491528 | tf_op jit(solution)/shard_map/ppermute | solution.py:97
  85.8 10.1 %collective-permute-start.9 = (bf16[128,640]{1,0:T(8,128)(2,1)S(1)}, bf16[128,640]{1,0:T(8,128)(2,1)S(1)}, u32[]{:S(2)}, u32[]{:S(2)}) collective-permute-start(bf16[128,640]{1,0:T(8,128)(2,1)S(1)} %fusion.88), channel_id=1, source_target_pairs={{0,4},{4,0},{8,12},{12,8},{1,5},{5,1},{9,13},{13,9},{2,6},{6,2},{1... | collective-permute-start | bytes 491528 | tf_op jit(solution)/shard_map/ppermute | solution.py:97

commit v4 on v3

--- a/solution.py
+++ b/solution.py
@@ -47,21 +47,12 @@
     return [(i, i ^ k) for i in range(size)]
 
 
-def _full_rows(piece, x, c, n_tensor):
-    other_x = lax.ppermute(piece, "tensor", _xor_pairs(n_tensor, 2))
-    by_x = jnp.where(x == 0, jnp.stack([piece, other_x]), jnp.stack([other_x, piece]))
-    other_c = lax.ppermute(by_x, "tensor", _xor_pairs(n_tensor, 1))
-    return jnp.where(c == 0, jnp.stack([by_x, other_c]), jnp.stack([other_c, by_x]))
+_ORDER = (0, 2, 1, 3)
 
 
-def _unit_sum(partial_value, x, c, n_tensor):
-    mine_c = jnp.where(c == 0, partial_value[:, :, 0], partial_value[:, :, 1])
-    send_c = jnp.where(c == 0, partial_value[:, :, 1], partial_value[:, :, 0])
-    over_c = mine_c.astype(jnp.float32) + lax.ppermute(
-        send_c, "tensor", _xor_pairs(n_tensor, 1)).astype(jnp.float32)
-    mine_x = jnp.where(x == 0, over_c[:, 0], over_c[:, 1])
-    send_x = jnp.where(x == 0, over_c[:, 1], over_c[:, 0]).astype(jnp.bfloat16)
-    return mine_x + lax.ppermute(send_x, "tensor", _xor_pairs(n_tensor, 2)).astype(jnp.float32)
+def _slots(weight, t, width, axis):
+    return jnp.concatenate(
+        [lax.dynamic_slice_in_dim(weight, (t ^ k) * width, width, axis=axis) for k in _ORDER], axis=axis)
 
 
 def gathered(tokens, route_scale, expert_ids, gate_weight, up_weight, down_weight):
@@ -70,7 +61,6 @@
     n_tensor = lax.axis_size("tensor")
     me = lax.axis_index("expert")
     t = lax.axis_index("tensor")
-    x, c = t // 2, t % 2
     expert = (me // SPAN).astype(jnp.bfloat16)
     scaled = (tokens.astype(jnp.float32) * route_scale[:, None]).astype(jnp.bfloat16)
     id_rows = jnp.zeros((16, width), jnp.bfloat16)
@@ -79,20 +69,26 @@
     blocks = [block] + [
         lax.ppermute(block, "expert", _xor_pairs(n_expert, k)) for k in range(1, n_expert)
     ]
-    hid = gate_weight.shape[2]
-    gate_w = gate_weight[0].reshape(2, 2, width, hid)
-    up_w = up_weight[0].reshape(2, 2, width, hid)
-    down_w = down_weight[0].reshape(hid, 2, 2, width)
+    gate_w = _slots(gate_weight[0], t, width, 0)
+    up_w = _slots(up_weight[0], t, width, 0)
+    down_w = _slots(down_weight[0], t, width, 1)
     total = None
     for k, blk in enumerate(blocks):
         routed = blk[tok_rows, :tok_rows]
-        rows = _full_rows(blk[:tok_rows], x, c, n_tensor)
-        gate_act = jnp.einsum("cxrf,xcfh->rh", rows, gate_w, preferred_element_type=jnp.float32)
-        up_act = jnp.einsum("cxrf,xcfh->rh", rows, up_w, preferred_element_type=jnp.float32)
+        piece = blk[:tok_rows]
+        pair = jnp.concatenate(
+            [piece, lax.ppermute(piece, "tensor", _xor_pairs(n_tensor, 2))], axis=1)
+        rows = jnp.concatenate(
+            [pair, lax.ppermute(pair, "tensor", _xor_pairs(n_tensor, 1))], axis=1)
+        gate_act = jnp.dot(rows, gate_w, preferred_element_type=jnp.float32)
+        up_act = jnp.dot(rows, up_w, preferred_element_type=jnp.float32)
         mine = (routed == expert)[:, None]
         hidden = jnp.where(mine, jax.nn.silu(gate_act) * up_act, 0.0).astype(jnp.bfloat16)
-        partial_value = jnp.einsum("rh,hxcf->rxcf", hidden, down_w, preferred_element_type=jnp.float32)
-        summed = _unit_sum(partial_value.astype(jnp.bfloat16), x, c, n_tensor)
+        partial_value = jnp.dot(hidden, down_w, preferred_element_type=jnp.float32).astype(jnp.bfloat16)
+        over_c = partial_value[:, :2 * width].astype(jnp.float32) + lax.ppermute(
+            partial_value[:, 2 * width:], "tensor", _xor_pairs(n_tensor, 1)).astype(jnp.float32)
+        summed = over_c[:, :width] + lax.ppermute(
+            over_c[:, width:].astype(jnp.bfloat16), "tensor", _xor_pairs(n_tensor, 2)).astype(jnp.float32)
         if k:
             summed = lax.ppermute(
                 summed.astype(jnp.bfloat16), "expert", _xor_pairs(n_expert, k)).astype(jnp.float32)

time: 97.3 us -> 97.4 us (level)
  other arithmetic: 20.8 us -> 12.6 us
  local copies, waits for them, and re-layouts: 9.68 us -> 14.2 us
  matrix products: 24.4 us -> 26.5 us
  waiting for transfers between devices: 19 us -> 20.7 us
    select_n x12 -> x0, other arithmetic: 10.5 us -> none  [the longest x4 5.67 us: _unit_sum(): send_c = jnp.where(c == 0, partial_value[:, :, 1], partial_value[:, :, 0])]
    another operation x4 -> x0, local copies, waits for them, and re-layouts: 9.64 us -> none  [the longest x1 6.66 us: gathered(): down_w = down_weight[0].reshape(hid, 2, 2, width)]
    slice x0 -> x11, local copies, waits for them, and re-layouts: none -> 9.14 us  [the longest x4 6.26 us: gathered(): partial_value[:, 2 * width:]]
    dynamic_slice x0 -> x2, local copies, waits for them, and re-layouts: none -> 4.94 us  [_slots(): lax.dynamic_slice_in_dim(weight, (t ^ k) * width, width, axis=axis)]
    concatenate x0 -> x4, other arithmetic: none -> 3.39 us  [gathered(): jnp.concatenate([piece, lax.ppermute(piece, 'tensor', _xor_pairs(n_tensor...]
    dot_general x8, matrix products: 24.4 us -> 26.5 us  [the longest x4 15.6 us: gathered(): jnp.dot(hidden, down_w, preferred_element_type=jnp.float32)]
    another operation x2 -> x0, other arithmetic: 2.05 us -> none  [_full_rows(): jnp.stack([piece, other_x])]
    ppermute x16, waiting for transfers between devices: 7.33 us -> 8.77 us  [the longest x4 7.68 us: gathered(): lax.ppermute(over_c[:, width:].astype(jnp.bfloat16), 'tensor', _xor_pairs...]
  transfers between devices with their start and end apart: 22 -> 22, of which waited for: 7 -> 7; matrix products, arithmetic and copies ran while one was open for 54% -> 52% of each run, Pallas kernels for 0% -> 0%
where the time goes in v4:
time: 97.4 us; the launch traced here: 96.4 us
  matrix products  26.5 us (27%)
  starting transfers between devices  22 us (23%)
  waiting for transfers between devices  20.7 us (21%)
  local copies, waits for them, and re-layouts  14.2 us (15%)
  other arithmetic  12.6 us (13%)
    dot_general x4, matrix products, gathered(): jnp.dot(hidden, down_w, preferred_element_type=jnp.float32)  15.6 us
    dot_general x4, matrix products, gathered(): up_act = jnp.dot(rows, up_w, preferred_element_type=jnp.float32)  11 us
    ppermute x3, waiting for transfers between devices, gathered(): lax.ppermute(summed.astype(jnp.bfloat16), 'expert', _xor_pairs(n_expert, k))  7.73 us
    ppermute x4, waiting for transfers between devices, gathered(): lax.ppermute(over_c[:, width:].astype(jnp.bfloat16), 'tensor', _xor_pairs...  7.68 us
    ppermute x3, starting transfers between devices, gathered(): lax.ppermute(summed.astype(jnp.bfloat16), 'expert', _xor_pairs(n_expert, k))  6.43 us
    slice x4, local copies, waits for them, and re-layouts, gathered(): partial_value[:, 2 * width:]  6.26 us
    ppermute x3, starting transfers between devices, gathered(): lax.ppermute(block, 'expert', _xor_pairs(n_expert, k))  5.62 us
    dynamic_slice x2, local copies, waits for them, and re-layouts, _slots(): lax.dynamic_slice_in_dim(weight, (t ^ k) * width, width, axis=axis)  4.94 us
  transfers between devices with their start and end apart: 22, of which 7 were waited for; matrix products, arithmetic and copies ran while one was open for 52% of the time, Pallas kernels for 0%

profile of v4, /device:TPU:0, one launch (start us, length us, event | category | flops | bytes accessed | tf_op | source)
XLA Modules:
  0.0 96.4 jit_solution(5721820409581370909)
XLA Ops:
  0.7 1.0 %multiply_convert_fusion = bf16[128,640]{1,0:T(8,128)(2,1)S(1)} fusion(bf16[128,640]{1,0:T(8,128)(2,1)} %param.8, f32[128]{0:T(128)} %param.9), kind=kLoop, calls=%fused_computation.48 | loop fusion | flops 245760 | bytes 328192 | tf_op jit(solution)/shard_map/convert_element_type | solution.py:65
  1.7 0.7 fusion.16
  2.4 3.0 %collective-permute-start.4 = (bf16[144,640]{1,0:T(8,128)(2,1)}, bf16[144,640]{1,0:T(8,128)(2,1)}, u32[]{:S(2)}, u32[]{:S(2)}) collective-permute-start(bf16[144,640]{1,0:T(8,128)(2,1)} %fusion.16), channel_id=1, source_target_pairs={{0,4},{4,0},{8,12},{12,8},{1,5},{5,1},{9,13},{13,9},{2,6},{6,2},{1... | collective-permute-start | bytes 552968 | tf_op jit(solution)/shard_map/ppermute | solution.py:70
  5.4 2.6 %collective-permute-start.10 = (bf16[144,640]{1,0:T(8,128)(2,1)}, bf16[144,640]{1,0:T(8,128)(2,1)}, u32[]{:S(2)}, u32[]{:S(2)}) collective-permute-start(bf16[144,640]{1,0:T(8,128)(2,1)} %fusion.16), channel_id=1, source_target_pairs={{0,8},{4,12},{8,0},{12,4},{1,9},{5,13},{9,1},{13,5},{2,10},{6,14},... | collective-permute-start | bytes 552968 | tf_op jit(solution)/shard_map/ppermute | solution.py:70
  8.0 1.7 %collective-permute-start = (bf16[128,640]{1,0:T(8,128)(2,1)S(1)}, bf16[128,640]{1,0:T(8,128)(2,1)}, u32[]{:S(2)}, u32[]{:S(2)}) collective-permute-start(bf16[128,640]{1,0:T(8,128)(2,1)S(1)} %multiply_convert_fusion), channel_id=1, source_target_pairs={{0,2},{1,3},{2,0},{3,1},{4,6},{5,7},{6,4},{7,5},{8,10},{9,11},{10,... | collective-permute-start | bytes 491528 | tf_op jit(solution)/shard_map/ppermute | solution.py:80
  9.7 0.7 compare_bitcast_fusion.3
  10.4 3.2 %dynamic-slice_bitcast_fusion.7 = (bf16[640,512]{1,0:T(8,128)(2,1)S(1)}, bf16[640,512]{1,0:T(8,128)(2,1)S(1)}, bf16[640,512]{1,0:T(8,128)(2,1)S(1)}, bf16[640,51...) fusion(bf16[1,2560,512]{2,1,0:T(8,128)(2,1)} %param.12, ...), kind=kLoop, calls=%fused_computation.22 | loop fusion | bytes 10485776 | tf_op jit(solution)/shard_map/dynamic_slice | solution.py:55
  13.7 1.8 %dynamic-slice_bitcast_fusion.3 = (bf16[512,640]{1,0:T(8,128)(2,1)}, bf16[512,640]{1,0:T(8,128)(2,1)}, bf16[512,640]{1,0:T(8,128)(2,1)}, bf16[512,640]{1,0:T(8,128)(2,1)}) fusion(bf16[1,512,2560]{2,1,0:T(8,128)(2,1)S(1)} %copy-done, s32[]{:T(128)S(6)} %select_n.39, s32[]{:T(128)S(6)} %select_n.40, s32[]{:T(128)S(6)} %select_n.42, s32[]{:T(128)S(6)} %select_n.41), kind=kLoop, calls=%fused_computation.18 | loop fusion | bytes 5242896 | tf_op jit(solution)/shard_map/dynamic_slice | solution.py:55
  15.4 0.9 pad_maximum_fusion.7
  16.5 0.9 slice.114
  17.8 4.2 %collective-permute-done.10 = bf16[144,640]{1,0:T(8,128)(2,1)} collective-permute-done((bf16[144,640]{1,0:T(8,128)(2,1)}, bf16[144,640]{1,0:T(8,128)(2,1)}, u32[]{:S(2)}, u32[]{:S(2)}) %collective-permute-start.10) | collective-permute-done | bytes 184352 | tf_op jit(solution)/shard_map/ppermute | solution.py:70
  22.1 0.9 slice.120
  23.0 1.6 %collective-permute-start.11 = (bf16[128,640]{1,0:T(8,128)(2,1)S(1)}, bf16[128,640]{1,0:T(8,128)(2,1)S(1)}, u32[]{:S(2)}, u32[]{:S(2)}) collective-permute-start(bf16[128,640]{1,0:T(8,128)(2,1)S(1)} %slice.120), channel_id=1, source_target_pairs={{0,2},{1,3},{2,0},{3,1},{4,6},{5,7},{6,4},{7,5},{8,10},{9,11},{10,... | collective-permute-start | bytes 491528 | tf_op jit(solution)/shard_map/ppermute | solution.py:80
  24.6 0.9 slice.126
  26.1 0.7 compare_bitcast_fusion.2
  26.8 0.7 compare_bitcast_fusion.1
  27.5 0.7 compare_bitcast_fusion
  28.2 0.8 pad_maximum_fusion.8
  29.3 0.8 pad_maximum_fusion.9
  30.4 0.7 collective-permute-done.17
  31.1 0.8 pad_maximum_fusion.10
  32.0 2.2 %fusion.14 = f32[128,512]{1,0:T(8,128)} fusion(bf16[128,1280]{1,0:T(8,128)(2,1)S(1)} %collective-permute-done.1, bf16[128,640]{1,0:T(8,128)(2,1)} %collective-permute-done, bf16[128,640]{1,0:T(8,128)(2,1)S(1)} %multiply_convert_fusion, bf16[640,512]{1,0:T(8,128)(2,1)S(1)} %get-tuple-element.27, bf16[640,512]{1,0:T(8,128)(2,1)S(1)} %get-tuple-element.28, ...), kind=kOutput, calls=%fused_computation.55 | convolution fusion | flops 347996160 | bytes 3538944 | tf_op jit(solution)/shard_map/dot_general | solution.py:84
  34.2 3.8 %convolution_convert_fusion.3 = bf16[128,2560]{1,0:T(8,128)(2,1)} fusion(f32[128,512]{1,0:T(8,128)} %fusion.14, bf16[128,1280]{1,0:T(8,128)(2,1)} %copy-done.15, bf16[128,640]{1,0:T(8,128)(2,1)} %collective-permute-done, bf16[128,640]{1,0:T(8,128)(2,1)S(1)} %multiply_convert_fusion, pred[128]{0:T(512)(128)(4,1)S(1)} %compare_bitcast_fusion.3, ...), kind=kOutput, calls=%fused_computation.3 | convolution fusion | flops 694812672 | bytes 6815872 | tf_op jit(solution)/shard_map/dot_general | solution.py:87
  38.0 1.7 %slice.110 = bf16[128,1280]{1,0:T(8,128)(2,1)} slice(bf16[128,2560]{1,0:T(8,128)(2,1)} %convolution_convert_fusion.3), slice={[0:128], [1280:2560]} | slice | bytes 655360 | tf_op jit(solution)/shard_map/slice | solution.py:89
  40.2 3.0 %fusion.12 = f32[128,512]{1,0:T(8,128)} fusion(bf16[128,1280]{1,0:T(8,128)(2,1)} %collective-permute-done.6, bf16[128,640]{1,0:T(8,128)(2,1)} %copy-done.14, bf16[128,640]{1,0:T(8,128)(2,1)} %copy-done.11, bf16[640,512]{1,0:T(8,128)(2,1)} %copy-done.2, bf16[640,512]{1,0:T(8,128)(2,1)} %copy-done.3, bf16[640,512]{1,0:T(8,128)(2,1)} %copy-done.1, ...), kind=kOutput, calls=%fused_computation.53 | convolution fusion | flops 347996160 | bytes 3538944 | tf_op jit(solution)/shard_map/dot_general | solution.py:84
  43.2 3.9 %convolution_convert_fusion.2 = bf16[128,2560]{1,0:T(8,128)(2,1)} fusion(f32[128,512]{1,0:T(8,128)} %fusion.12, bf16[128,1280]{1,0:T(8,128)(2,1)} %collective-permute-done.6, bf16[128,640]{1,0:T(8,128)(2,1)} %copy-done.14, bf16[128,640]{1,0:T(8,128)(2,1)} %copy-done.11, pred[128]{0:T(512)(128)(4,1)S(1)} %compare_bitcast_fusion.2, ...), kind=kOutput, calls=%fused_computation.2 | convolution fusion | flops 694812672 | bytes 6815872 | tf_op jit(solution)/shard_map/dot_general | solution.py:87
  47.1 1.7 %slice.116 = bf16[128,1280]{1,0:T(8,128)(2,1)} slice(bf16[128,2560]{1,0:T(8,128)(2,1)} %convolution_convert_fusion.2), slice={[0:128], [1280:2560]} | slice | bytes 655360 | tf_op jit(solution)/shard_map/slice | solution.py:89
  48.9 2.9 %fusion.10 = f32[128,512]{1,0:T(8,128)} fusion(bf16[128,1280]{1,0:T(8,128)(2,1)} %collective-permute-done.12, bf16[128,640]{1,0:T(8,128)(2,1)} %copy-done.13, bf16[128,640]{1,0:T(8,128)(2,1)S(1)} %copy-done.10, bf16[640,512]{1,0:T(8,128)(2,1)} %copy-done.2, bf16[640,512]{1,0:T(8,128)(2,1)} %copy-done.3, bf16[640,512]{1,0:T(8,128)(2,1)} %copy-done.1, ...), kind=kOutput, calls=%fused_computation.51 | convolution fusion | flops 347996160 | bytes 3538944 | tf_op jit(solution)/shard_map/dot_general | solution.py:84
  51.8 4.0 %convolution_convert_fusion.1 = bf16[128,2560]{1,0:T(8,128)(2,1)} fusion(f32[128,512]{1,0:T(8,128)} %fusion.10, bf16[128,1280]{1,0:T(8,128)(2,1)} %collective-permute-done.12, bf16[128,640]{1,0:T(8,128)(2,1)} %copy-done.13, bf16[128,640]{1,0:T(8,128)(2,1)} %copy-done.9, pred[128]{0:T(512)(128)(4,1)S(1)} %compare_bitcast_fusion.1, ...), kind=kOutput, calls=%fused_computation.1 | convolution fusion | flops 694812672 | bytes 6815872 | tf_op jit(solution)/shard_map/dot_general | solution.py:87
  55.8 1.7 %slice.122 = bf16[128,1280]{1,0:T(8,128)(2,1)} slice(bf16[128,2560]{1,0:T(8,128)(2,1)} %convolution_convert_fusion.1), slice={[0:128], [1280:2560]} | slice | bytes 655360 | tf_op jit(solution)/shard_map/slice | solution.py:89
  58.0 2.9 %fusion.8 = f32[128,512]{1,0:T(8,128)} fusion(bf16[128,1280]{1,0:T(8,128)(2,1)} %collective-permute-done.18, bf16[128,640]{1,0:T(8,128)(2,1)} %copy-done.12, bf16[128,640]{1,0:T(8,128)(2,1)S(1)} %copy-done.8, bf16[640,512]{1,0:T(8,128)(2,1)} %copy-done.2, bf16[640,512]{1,0:T(8,128)(2,1)} %copy-done.3, bf16[640,512]{1,0:T(8,128)(2,1)} %copy-done.1, ...), kind=kOutput, calls=%fused_computation.49 | convolution fusion | flops 347996160 | bytes 3538944 | tf_op jit(solution)/shard_map/dot_general | solution.py:84
  60.9 3.9 %convolution_convert_fusion = bf16[128,2560]{1,0:T(8,128)(2,1)} fusion(f32[128,512]{1,0:T(8,128)} %fusion.8, bf16[128,1280]{1,0:T(8,128)(2,1)} %collective-permute-done.18, bf16[128,640]{1,0:T(8,128)(2,1)} %copy-done.12, bf16[128,640]{1,0:T(8,128)(2,1)S(1)} %copy-done.8, pred[128]{0:T(512)(128)(4,1)S(1)} %compare_bitcast_fusion, ...), kind=kOutput, calls=%fused_computation | convolution fusion | flops 694812672 | bytes 6815872 | tf_op jit(solution)/shard_map/dot_general | solution.py:87
  64.7 1.1 %slice.128 = bf16[128,1280]{1,0:T(8,128)(2,1)S(1)} slice(bf16[128,2560]{1,0:T(8,128)(2,1)} %convolution_convert_fusion), slice={[0:128], [1280:2560]} | slice | bytes 655360 | tf_op jit(solution)/shard_map/slice | solution.py:89
  65.9 1.0 %convert_add_fusion.3 = f32[128,1280]{1,0:T(8,128)S(1)} fusion(bf16[128,1280]{1,0:T(8,128)(2,1)} %collective-permute-done.2, bf16[128,2560]{1,0:T(8,128)(2,1)S(1)} %copy-done.4), kind=kLoop, calls=%fused_computation.14 | loop fusion | flops 491520 | bytes 1310720 | tf_op jit(solution)/shard_map/add | solution.py:88
  67.0 0.8 collective-permute-start.3
  67.8 1.1 %convert_add_fusion.2 = f32[128,1280]{1,0:T(8,128)S(1)} fusion(bf16[128,1280]{1,0:T(8,128)(2,1)} %collective-permute-done.7, bf16[128,2560]{1,0:T(8,128)(2,1)} %convolution_convert_fusion.2), kind=kLoop, calls=%fused_computation.13 | loop fusion | flops 491520 | bytes 1310720 | tf_op jit(solution)/shard_map/add | solution.py:88
  69.0 1.3 %collective-permute-start.8 = (bf16[128,640]{1,0:T(8,128)(2,1)S(1)}, bf16[128,640]{1,0:T(8,128)(2,1)S(1)}, u32[]{:S(2)}, u32[]{:S(2)}) collective-permute-start(bf16[128,640]{1,0:T(8,128)(2,1)S(1)} %slice.162), channel_id=1, source_target_pairs={{0,2},{1,3},{2,0},{3,1},{4,6},{5,7},{6,4},{7,5},{8,10},{9,11},{10,... | collective-permute-start | bytes 491528 | tf_op jit(solution)/shard_map/ppermute | solution.py:90
  70.3 1.1 %convert_add_fusion.1 = f32[128,1280]{1,0:T(8,128)S(1)} fusion(bf16[128,1280]{1,0:T(8,128)(2,1)} %collective-permute-done.13, bf16[128,2560]{1,0:T(8,128)(2,1)S(1)} %copy-done.5), kind=kLoop, calls=%fused_computation.12 | loop fusion | flops 491520 | bytes 1310720 | tf_op jit(solution)/shard_map/add | solution.py:88
  71.4 0.8 collective-permute-start.14
  72.3 1.3 %collective-permute-start.20 = (bf16[128,640]{1,0:T(8,128)(2,1)S(1)}, bf16[128,640]{1,0:T(8,128)(2,1)S(1)}, u32[]{:S(2)}, u32[]{:S(2)}) collective-permute-start(bf16[128,640]{1,0:T(8,128)(2,1)S(1)} %slice.160), channel_id=1, source_target_pairs={{0,2},{1,3},{2,0},{3,1},{4,6},{5,7},{6,4},{7,5},{8,10},{9,11},{10,... | collective-permute-start | bytes 491528 | tf_op jit(solution)/shard_map/ppermute | solution.py:90
  73.7 3.9 %collective-permute-done.8 = bf16[128,640]{1,0:T(8,128)(2,1)S(1)} collective-permute-done((bf16[128,640]{1,0:T(8,128)(2,1)S(1)}, bf16[128,640]{1,0:T(8,128)(2,1)S(1)}, u32[]{:S(2)}, u32[]{:S(2)}) %collective-permute-start.8) | collective-permute-done | bytes 163872 | tf_op jit(solution)/shard_map/ppermute | solution.py:90
  77.6 0.9 collective-permute-start.9
  78.5 2.6 %collective-permute-done.14 = bf16[128,640]{1,0:T(8,128)(2,1)S(1)} collective-permute-done((bf16[128,640]{1,0:T(8,128)(2,1)S(1)}, bf16[128,640]{1,0:T(8,128)(2,1)S(1)}, u32[]{:S(2)}, u32[]{:S(2)}) %collective-permute-start.14) | collective-permute-done | bytes 163872 | tf_op jit(solution)/shard_map/ppermute | solution.py:90
  81.1 1.9 %collective-permute-start.15 = (bf16[128,640]{1,0:T(8,128)(2,1)S(1)}, bf16[128,640]{1,0:T(8,128)(2,1)S(1)}, u32[]{:S(2)}, u32[]{:S(2)}) collective-permute-start(bf16[128,640]{1,0:T(8,128)(2,1)S(1)} %fusion.2), channel_id=1, source_target_pairs={{0,8},{4,12},{8,0},{12,4},{1,9},{5,13},{9,1},{13,5},{2,10},{6,14},... | collective-permute-start | bytes 491528 | tf_op jit(solution)/shard_map/ppermute | solution.py:93
  83.0 1.2 %collective-permute-done.20 = bf16[128,640]{1,0:T(8,128)(2,1)S(1)} collective-permute-done((bf16[128,640]{1,0:T(8,128)(2,1)S(1)}, bf16[128,640]{1,0:T(8,128)(2,1)S(1)}, u32[]{:S(2)}, u32[]{:S(2)}) %collective-permute-start.20) | collective-permute-done | bytes 163872 | tf_op jit(solution)/shard_map/ppermute | solution.py:90
  84.2 3.7 %collective-permute-start.21 = (bf16[128,640]{1,0:T(8,128)(2,1)S(1)}, bf16[128,640]{1,0:T(8,128)(2,1)S(1)}, u32[]{:S(2)}, u32[]{:S(2)}) collective-permute-start(bf16[128,640]{1,0:T(8,128)(2,1)S(1)} %fusion.1), channel_id=1, source_target_pairs={{0,12},{4,8},{8,4},{12,0},{1,13},{5,9},{9,5},{13,1},{2,14},{6,10},... | collective-permute-start | bytes 491528 | tf_op jit(solution)/shard_map/ppermute | solution.py:93
  87.9 7.7 %collective-permute-done.15 = bf16[128,640]{1,0:T(8,128)(2,1)S(1)} collective-permute-done((bf16[128,640]{1,0:T(8,128)(2,1)S(1)}, bf16[128,640]{1,0:T(8,128)(2,1)S(1)}, u32[]{:S(2)}, u32[]{:S(2)}) %collective-permute-start.15) | collective-permute-done | bytes 163872 | tf_op jit(solution)/shard_map/ppermute | solution.py:93
  95.6 0.8 fusion.7
  (68 shorter events, 3.8 us)
Async XLA Ops:
  2.4 14.1 %collective-permute-start.4 = (bf16[144,640]{1,0:T(8,128)(2,1)}, bf16[144,640]{1,0:T(8,128)(2,1)}, u32[]{:S(2)}, u32[]{:S(2)}) collective-permute-start(bf16[144,640]{1,0:T(8,128)(2,1)} %fusion.16), channel_id=1, source_target_pairs={{0,4},{4,0},{8,12},{12,8},{1,5},{5,1},{9,13},{13,9},{2,6},{6,2},{1... | collective-permute-start | bytes 552968 | tf_op jit(solution)/shard_map/ppermute | solution.py:70
  5.4 16.7 %collective-permute-start.10 = (bf16[144,640]{1,0:T(8,128)(2,1)}, bf16[144,640]{1,0:T(8,128)(2,1)}, u32[]{:S(2)}, u32[]{:S(2)}) collective-permute-start(bf16[144,640]{1,0:T(8,128)(2,1)} %fusion.16), channel_id=1, source_target_pairs={{0,8},{4,12},{8,0},{12,4},{1,9},{5,13},{9,1},{13,5},{2,10},{6,14},... | collective-permute-start | bytes 552968 | tf_op jit(solution)/shard_map/ppermute | solution.py:70
  8.0 16.6 %collective-permute-start.16 = (bf16[144,640]{1,0:T(8,128)(2,1)}, bf16[144,640]{1,0:T(8,128)(2,1)}, u32[]{:S(2)}, u32[]{:S(2)}) collective-permute-start(bf16[144,640]{1,0:T(8,128)(2,1)} %fusion.16), channel_id=1, source_target_pairs={{0,12},{4,8},{8,4},{12,0},{1,13},{5,9},{9,5},{13,1},{2,14},{6,10},... | collective-permute-start | bytes 552968 | tf_op jit(solution)/shard_map/ppermute | solution.py:70
  8.0 7.4 %collective-permute-start = (bf16[128,640]{1,0:T(8,128)(2,1)S(1)}, bf16[128,640]{1,0:T(8,128)(2,1)}, u32[]{:S(2)}, u32[]{:S(2)}) collective-permute-start(bf16[128,640]{1,0:T(8,128)(2,1)S(1)} %multiply_convert_fusion), channel_id=1, source_target_pairs={{0,2},{1,3},{2,0},{3,1},{4,6},{5,7},{6,4},{7,5},{8,10},{9,11},{10,... | collective-permute-start | bytes 491528 | tf_op jit(solution)/shard_map/ppermute | solution.py:80
  10.4 3.3 %copy-start = (bf16[1,512,2560]{2,1,0:T(8,128)(2,1)S(1)}, bf16[1,512,2560]{2,1,0:T(8,128)(2,1)}, u32[]{:S(2)}) copy-start(bf16[1,512,2560]{2,1,0:T(8,128)(2,1)} %param.13) | copy-start | bytes 7864324
  13.7 18.3 %copy-start.1 = (bf16[640,512]{1,0:T(8,128)(2,1)}, bf16[640,512]{1,0:T(8,128)(2,1)S(1)}, u32[]{:S(2)}) copy-start(bf16[640,512]{1,0:T(8,128)(2,1)S(1)} %get-tuple-element.26) | copy-start | bytes 1966084
  13.7 18.3 %copy-start.2 = (bf16[640,512]{1,0:T(8,128)(2,1)}, bf16[640,512]{1,0:T(8,128)(2,1)S(1)}, u32[]{:S(2)}) copy-start(bf16[640,512]{1,0:T(8,128)(2,1)S(1)} %get-tuple-element.27) | copy-start | bytes 1966084
  13.7 18.3 %copy-start.3 = (bf16[640,512]{1,0:T(8,128)(2,1)}, bf16[640,512]{1,0:T(8,128)(2,1)S(1)}, u32[]{:S(2)}) copy-start(bf16[640,512]{1,0:T(8,128)(2,1)S(1)} %get-tuple-element.28) | copy-start | bytes 1966084
  16.4 15.5 %collective-permute-start.1 = (bf16[128,1280]{1,0:T(8,128)(2,1)S(1)}, bf16[128,1280]{1,0:T(8,128)(2,1)S(1)}, u32[]{:S(2)}, u32[]{:S(2)}) collective-permute-start(bf16[128,1280]{1,0:T(8,128)(2,1)S(1)} %pad_maximum_fusion.7), channel_id=1, source_target_pairs={{0,1},{1,0},{2,3},{3,2},{4,5},{5,4},{6,7},{7,6},{8,9},{9,8},{10,11... | collective-permute-start | bytes 983048 | tf_op jit(solution)/shard_map/ppermute | solution.py:82
  17.4 14.5 %copy-start.11 = (bf16[128,640]{1,0:T(8,128)(2,1)}, bf16[128,640]{1,0:T(8,128)(2,1)S(1)}, u32[]{:S(2)}) copy-start(bf16[128,640]{1,0:T(8,128)(2,1)S(1)} %slice.114) | copy-start | bytes 491524
  17.4 10.8 %collective-permute-start.5 = (bf16[128,640]{1,0:T(8,128)(2,1)S(1)}, bf16[128,640]{1,0:T(8,128)(2,1)S(1)}, u32[]{:S(2)}, u32[]{:S(2)}) collective-permute-start(bf16[128,640]{1,0:T(8,128)(2,1)S(1)} %slice.114), channel_id=1, source_target_pairs={{0,2},{1,3},{2,0},{3,1},{4,6},{5,7},{6,4},{7,5},{8,10},{9,11},{10,... | collective-permute-start | bytes 491528 | tf_op jit(solution)/shard_map/ppermute | solution.py:80
  23.0 8.9 %copy-start.9 = (bf16[128,640]{1,0:T(8,128)(2,1)}, bf16[128,640]{1,0:T(8,128)(2,1)S(1)}, u32[]{:S(2)}) copy-start(bf16[128,640]{1,0:T(8,128)(2,1)S(1)} %slice.120) | copy-start | bytes 491524
  23.0 6.3 %collective-permute-start.11 = (bf16[128,640]{1,0:T(8,128)(2,1)S(1)}, bf16[128,640]{1,0:T(8,128)(2,1)S(1)}, u32[]{:S(2)}, u32[]{:S(2)}) collective-permute-start(bf16[128,640]{1,0:T(8,128)(2,1)S(1)} %slice.120), channel_id=1, source_target_pairs={{0,2},{1,3},{2,0},{3,1},{4,6},{5,7},{6,4},{7,5},{8,10},{9,11},{10,... | collective-permute-start | bytes 491528 | tf_op jit(solution)/shard_map/ppermute | solution.py:80
  25.5 5.6 %copy-start.7 = (bf16[128,640]{1,0:T(8,128)(2,1)}, bf16[128,640]{1,0:T(8,128)(2,1)S(1)}, u32[]{:S(2)}) copy-start(bf16[128,640]{1,0:T(8,128)(2,1)S(1)} %slice.126) | copy-start | bytes 491524
  25.5 5.6 %collective-permute-start.17 = (bf16[128,640]{1,0:T(8,128)(2,1)S(1)}, bf16[128,640]{1,0:T(8,128)(2,1)S(1)}, u32[]{:S(2)}, u32[]{:S(2)}) collective-permute-start(bf16[128,640]{1,0:T(8,128)(2,1)S(1)} %slice.126), channel_id=1, source_target_pairs={{0,2},{1,3},{2,0},{3,1},{4,6},{5,7},{6,4},{7,5},{8,10},{9,11},{10,... | collective-permute-start | bytes 491528 | tf_op jit(solution)/shard_map/ppermute | solution.py:80
  28.2 3.8 %copy-start.14 = (bf16[128,640]{1,0:T(8,128)(2,1)}, bf16[128,640]{1,0:T(8,128)(2,1)S(1)}, u32[]{:S(2)}) copy-start(bf16[128,640]{1,0:T(8,128)(2,1)S(1)} %collective-permute-done.5) | copy-start | bytes 491524
  29.0 11.2 %collective-permute-start.6 = (bf16[128,1280]{1,0:T(8,128)(2,1)}, bf16[128,1280]{1,0:T(8,128)(2,1)}, u32[]{:S(2)}, u32[]{:S(2)}) collective-permute-start(bf16[128,1280]{1,0:T(8,128)(2,1)} %pad_maximum_fusion.8), channel_id=1, source_target_pairs={{0,1},{1,0},{2,3},{3,2},{4,5},{5,4},{6,7},{7,6},{8,9},{9,8},{10,11... | collective-permute-start | bytes 983048 | tf_op jit(solution)/shard_map/ppermute | solution.py:82
  29.3 2.6 %copy-start.13 = (bf16[128,640]{1,0:T(8,128)(2,1)}, bf16[128,640]{1,0:T(8,128)(2,1)S(1)}, u32[]{:S(2)}) copy-start(bf16[128,640]{1,0:T(8,128)(2,1)S(1)} %collective-permute-done.11) | copy-start | bytes 491524
  30.2 18.7 %collective-permute-start.12 = (bf16[128,1280]{1,0:T(8,128)(2,1)}, bf16[128,1280]{1,0:T(8,128)(2,1)}, u32[]{:S(2)}, u32[]{:S(2)}) collective-permute-start(bf16[128,1280]{1,0:T(8,128)(2,1)} %pad_maximum_fusion.9), channel_id=1, source_target_pairs={{0,1},{1,0},{2,3},{3,2},{4,5},{5,4},{6,7},{7,6},{8,9},{9,8},{10,11... | collective-permute-start | bytes 983048 | tf_op jit(solution)/shard_map/ppermute | solution.py:82
  31.1 0.8 copy-start.12
  31.9 26.1 %collective-permute-start.18 = (bf16[128,1280]{1,0:T(8,128)(2,1)}, bf16[128,1280]{1,0:T(8,128)(2,1)}, u32[]{:S(2)}, u32[]{:S(2)}) collective-permute-start(bf16[128,1280]{1,0:T(8,128)(2,1)} %pad_maximum_fusion.10), channel_id=1, source_target_pairs={{0,1},{1,0},{2,3},{3,2},{4,5},{5,4},{6,7},{7,6},{8,9},{9,8},{10,11... | collective-permute-start | bytes 983048 | tf_op jit(solution)/shard_map/ppermute | solution.py:82
  31.9 2.3 %copy-start.15 = (bf16[128,1280]{1,0:T(8,128)(2,1)}, bf16[128,1280]{1,0:T(8,128)(2,1)S(1)}, u32[]{:S(2)}) copy-start(bf16[128,1280]{1,0:T(8,128)(2,1)S(1)} %collective-permute-done.1) | copy-start | bytes 983044
  39.7 26.2 %collective-permute-start.2 = (bf16[128,1280]{1,0:T(8,128)(2,1)}, bf16[128,1280]{1,0:T(8,128)(2,1)}, u32[]{:S(2)}, u32[]{:S(2)}) collective-permute-start(bf16[128,1280]{1,0:T(8,128)(2,1)} %slice.110), channel_id=1, source_target_pairs={{0,1},{1,0},{2,3},{3,2},{4,5},{5,4},{6,7},{7,6},{8,9},{9,8},{10,11... | collective-permute-start | bytes 983048 | tf_op jit(solution)/shard_map/ppermute | solution.py:88
  43.2 5.7 %copy-start.10 = (bf16[128,640]{1,0:T(8,128)(2,1)S(1)}, bf16[128,640]{1,0:T(8,128)(2,1)}, u32[]{:S(2)}) copy-start(bf16[128,640]{1,0:T(8,128)(2,1)} %copy-done.9) | copy-start | bytes 491524
  48.9 18.9 %collective-permute-start.7 = (bf16[128,1280]{1,0:T(8,128)(2,1)}, bf16[128,1280]{1,0:T(8,128)(2,1)}, u32[]{:S(2)}, u32[]{:S(2)}) collective-permute-start(bf16[128,1280]{1,0:T(8,128)(2,1)} %slice.116), channel_id=1, source_target_pairs={{0,1},{1,0},{2,3},{3,2},{4,5},{5,4},{6,7},{7,6},{8,9},{9,8},{10,11... | collective-permute-start | bytes 983048 | tf_op jit(solution)/shard_map/ppermute | solution.py:88
  51.8 6.2 %copy-start.8 = (bf16[128,640]{1,0:T(8,128)(2,1)S(1)}, bf16[128,640]{1,0:T(8,128)(2,1)}, u32[]{:S(2)}) copy-start(bf16[128,640]{1,0:T(8,128)(2,1)} %copy-done.7) | copy-start | bytes 491524
  57.5 12.9 %collective-permute-start.13 = (bf16[128,1280]{1,0:T(8,128)(2,1)}, bf16[128,1280]{1,0:T(8,128)(2,1)}, u32[]{:S(2)}, u32[]{:S(2)}) collective-permute-start(bf16[128,1280]{1,0:T(8,128)(2,1)} %slice.122), channel_id=1, source_target_pairs={{0,1},{1,0},{2,3},{3,2},{4,5},{5,4},{6,7},{7,6},{8,9},{9,8},{10,11... | collective-permute-start | bytes 983048 | tf_op jit(solution)/shard_map/ppermute | solution.py:88
  60.8 5.1 %copy-start.4 = (bf16[128,2560]{1,0:T(8,128)(2,1)S(1)}, bf16[128,2560]{1,0:T(8,128)(2,1)}, u32[]{:S(2)}) copy-start(bf16[128,2560]{1,0:T(8,128)(2,1)} %convolution_convert_fusion.3) | copy-start | bytes 1966084
  64.7 5.6 %copy-start.5 = (bf16[128,2560]{1,0:T(8,128)(2,1)S(1)}, bf16[128,2560]{1,0:T(8,128)(2,1)}, u32[]{:S(2)}) copy-start(bf16[128,2560]{1,0:T(8,128)(2,1)} %convolution_convert_fusion.1) | copy-start | bytes 1966084
  64.7 7.5 %copy-start.6 = (bf16[128,2560]{1,0:T(8,128)(2,1)S(1)}, bf16[128,2560]{1,0:T(8,128)(2,1)}, u32[]{:S(2)}) copy-start(bf16[128,2560]{1,0:T(8,128)(2,1)} %convolution_convert_fusion) | copy-start | bytes 1966084
  65.8 6.4 %collective-permute-start.19 = (bf16[128,1280]{1,0:T(8,128)(2,1)S(1)}, bf16[128,1280]{1,0:T(8,128)(2,1)S(1)}, u32[]{:S(2)}, u32[]{:S(2)}) collective-permute-start(bf16[128,1280]{1,0:T(8,128)(2,1)S(1)} %slice.128), channel_id=1, source_target_pairs={{0,1},{1,0},{2,3},{3,2},{4,5},{5,4},{6,7},{7,6},{8,9},{9,8},{10,11... | collective-permute-start | bytes 983048 | tf_op jit(solution)/shard_map/ppermute | solution.py:88
  67.0 20.9 %collective-permute-start.3 = (bf16[128,640]{1,0:T(8,128)(2,1)S(1)}, bf16[128,640]{1,0:T(8,128)(2,1)S(1)}, u32[]{:S(2)}, u32[]{:S(2)}) collective-permute-start(bf16[128,640]{1,0:T(8,128)(2,1)S(1)} %slice.163), channel_id=1, source_target_pairs={{0,2},{1,3},{2,0},{3,1},{4,6},{5,7},{6,4},{7,5},{8,10},{9,11},{10,... | collective-permute-start | bytes 491528 | tf_op jit(solution)/shard_map/ppermute | solution.py:90
  69.0 8.6 %collective-permute-start.8 = (bf16[128,640]{1,0:T(8,128)(2,1)S(1)}, bf16[128,640]{1,0:T(8,128)(2,1)S(1)}, u32[]{:S(2)}, u32[]{:S(2)}) collective-permute-start(bf16[128,640]{1,0:T(8,128)(2,1)S(1)} %slice.162), channel_id=1, source_target_pairs={{0,2},{1,3},{2,0},{3,1},{4,6},{5,7},{6,4},{7,5},{8,10},{9,11},{10,... | collective-permute-start | bytes 491528 | tf_op jit(solution)/shard_map/ppermute | solution.py:90
  71.4 9.7 %collective-permute-start.14 = (bf16[128,640]{1,0:T(8,128)(2,1)S(1)}, bf16[128,640]{1,0:T(8,128)(2,1)S(1)}, u32[]{:S(2)}, u32[]{:S(2)}) collective-permute-start(bf16[128,640]{1,0:T(8,128)(2,1)S(1)} %slice.161), channel_id=1, source_target_pairs={{0,2},{1,3},{2,0},{3,1},{4,6},{5,7},{6,4},{7,5},{8,10},{9,11},{10,... | collective-permute-start | bytes 491528 | tf_op jit(solution)/shard_map/ppermute | solution.py:90
  72.3 11.8 %collective-permute-start.20 = (bf16[128,640]{1,0:T(8,128)(2,1)S(1)}, bf16[128,640]{1,0:T(8,128)(2,1)S(1)}, u32[]{:S(2)}, u32[]{:S(2)}) collective-permute-start(bf16[128,640]{1,0:T(8,128)(2,1)S(1)} %slice.160), channel_id=1, source_target_pairs={{0,2},{1,3},{2,0},{3,1},{4,6},{5,7},{6,4},{7,5},{8,10},{9,11},{10,... | collective-permute-start | bytes 491528 | tf_op jit(solution)/shard_map/ppermute | solution.py:90
  77.6 10.3 %collective-permute-start.9 = (bf16[128,640]{1,0:T(8,128)(2,1)S(1)}, bf16[128,640]{1,0:T(8,128)(2,1)S(1)}, u32[]{:S(2)}, u32[]{:S(2)}) collective-permute-start(bf16[128,640]{1,0:T(8,128)(2,1)S(1)} %fusion.3), channel_id=1, source_target_pairs={{0,4},{4,0},{8,12},{12,8},{1,5},{5,1},{9,13},{13,9},{2,6},{6,2},{1... | collective-permute-start | bytes 491528 | tf_op jit(solution)/shard_map/ppermute | solution.py:93
  81.1 14.5 %collective-permute-start.15 = (bf16[128,640]{1,0:T(8,128)(2,1)S(1)}, bf16[128,640]{1,0:T(8,128)(2,1)S(1)}, u32[]{:S(2)}, u32[]{:S(2)}) collective-permute-start(bf16[128,640]{1,0:T(8,128)(2,1)S(1)} %fusion.2), channel_id=1, source_target_pairs={{0,8},{4,12},{8,0},{12,4},{1,9},{5,13},{9,1},{13,5},{2,10},{6,14},... | collective-permute-start | bytes 491528 | tf_op jit(solution)/shard_map/ppermute | solution.py:93
  84.2 11.4 %collective-permute-start.21 = (bf16[128,640]{1,0:T(8,128)(2,1)S(1)}, bf16[128,640]{1,0:T(8,128)(2,1)S(1)}, u32[]{:S(2)}, u32[]{:S(2)}) collective-permute-start(bf16[128,640]{1,0:T(8,128)(2,1)S(1)} %fusion.1), channel_id=1, source_target_pairs={{0,12},{4,8},{8,4},{12,0},{1,13},{5,9},{9,5},{13,1},{2,14},{6,10},... | collective-permute-start | bytes 491528 | tf_op jit(solution)/shard_map/ppermute | solution.py:93

commit v5 on v4

--- a/solution.py
+++ b/solution.py
@@ -72,10 +72,11 @@
     gate_w = _slots(gate_weight[0], t, width, 0)
     up_w = _slots(up_weight[0], t, width, 0)
     down_w = _slots(down_weight[0], t, width, 1)
+    waves = [blocks[:1], blocks[1:]] if n_expert > 1 else [blocks]
     total = None
-    for k, blk in enumerate(blocks):
-        routed = blk[tok_rows, :tok_rows]
-        piece = blk[:tok_rows]
+    for wave in waves:
+        routed = jnp.concatenate([blk[tok_rows, :tok_rows] for blk in wave])
+        piece = jnp.concatenate([blk[:tok_rows] for blk in wave])
         pair = jnp.concatenate(
             [piece, lax.ppermute(piece, "tensor", _xor_pairs(n_tensor, 2))], axis=1)
         rows = jnp.concatenate(
@@ -89,10 +90,12 @@
             partial_value[:, 2 * width:], "tensor", _xor_pairs(n_tensor, 1)).astype(jnp.float32)
         summed = over_c[:, :width] + lax.ppermute(
             over_c[:, width:].astype(jnp.bfloat16), "tensor", _xor_pairs(n_tensor, 2)).astype(jnp.float32)
-        if k:
-            summed = lax.ppermute(
-                summed.astype(jnp.bfloat16), "expert", _xor_pairs(n_expert, k)).astype(jnp.float32)
-        total = summed if total is None else total + summed
+        if total is None:
+            total = summed
+            continue
+        for k in range(1, n_expert):
+            part = summed[(k - 1) * tok_rows:k * tok_rows].astype(jnp.bfloat16)
+            total = total + lax.ppermute(part, "expert", _xor_pairs(n_expert, k)).astype(jnp.float32)
     return total.astype(jnp.bfloat16)
 
 

time: 97.4 us -> 94.7 us (0.972)
  waiting for transfers between devices: 20.7 us -> 42.4 us
  matrix products: 26.5 us -> 16.2 us
  starting transfers between devices: 22 us -> 15.7 us
  other arithmetic: 12.6 us -> 6.91 us
  local copies, waits for them, and re-layouts: 14.2 us -> 12.8 us
    ppermute x3, waiting for transfers between devices: 4.24 us -> 12.5 us  [gathered(): lax.ppermute(block, 'expert', _xor_pairs(n_expert, k))]
    dot_general x4 -> x1, matrix products: 11 us -> 3.12 us  [gathered(): up_act = jnp.dot(rows, up_w, preferred_element_type=jnp.float32)]
    dot_general x4 -> x2, matrix products: 15.6 us -> 9.64 us  [gathered(): jnp.dot(hidden, down_w, preferred_element_type=jnp.float32)]
    ppermute x3, waiting for transfers between devices: 7.73 us -> 12.8 us  [gathered(): lax.ppermute(part, 'expert', _xor_pairs(n_expert, k)).astype(jnp.float32)]
    slice x4 -> x2, local copies, waits for them, and re-layouts: 6.26 us -> 2.03 us  [gathered(): partial_value[:, 2 * width:]]
    ppermute x4 -> x2, waiting for transfers between devices: 7.68 us -> 11.9 us  [gathered(): lax.ppermute(over_c[:, width:].astype(jnp.bfloat16), 'tensor', _xor_pairs...]
    ppermute x4 -> x2, waiting for transfers between devices: 1.07 us -> 5.24 us  [gathered(): lax.ppermute(piece, 'tensor', _xor_pairs(n_tensor, 2))]
    dot_general x0 -> x1, matrix products: none -> 3.47 us  [gathered(): gate_act = jnp.dot(rows, gate_w, preferred_element_type=jnp.float32)]
  transfers between devices with their start and end apart: 22 -> 14, of which waited for: 7 -> 7; matrix products, arithmetic and copies ran while one was open for 52% -> 35% of each run, Pallas kernels for 0% -> 0%
where the time goes in v5:
time: 94.7 us; the launch traced here: 94.3 us
  waiting for transfers between devices  42.4 us (45%)
  matrix products  16.2 us (17%)
  starting transfers between devices  15.7 us (17%)
  local copies, waits for them, and re-layouts  12.8 us (14%)
  other arithmetic  6.91 us (7%)
    ppermute x3, waiting for transfers between devices, gathered(): lax.ppermute(part, 'expert', _xor_pairs(n_expert, k)).astype(jnp.float32)  12.8 us
    ppermute x3, waiting for transfers between devices, gathered(): lax.ppermute(block, 'expert', _xor_pairs(n_expert, k))  12.5 us
    ppermute x2, waiting for transfers between devices, gathered(): lax.ppermute(over_c[:, width:].astype(jnp.bfloat16), 'tensor', _xor_pairs...  11.9 us
    dot_general x2, matrix products, gathered(): jnp.dot(hidden, down_w, preferred_element_type=jnp.float32)  9.64 us
    dynamic_slice x2, local copies, waits for them, and re-layouts, _slots(): lax.dynamic_slice_in_dim(weight, (t ^ k) * width, width, axis=axis)  5.84 us
    ppermute x3, starting transfers between devices, gathered(): lax.ppermute(block, 'expert', _xor_pairs(n_expert, k))  5.76 us
    ppermute x2, waiting for transfers between devices, gathered(): lax.ppermute(piece, 'tensor', _xor_pairs(n_tensor, 2))  5.24 us
    ppermute x3, starting transfers between devices, gathered(): lax.ppermute(part, 'expert', _xor_pairs(n_expert, k)).astype(jnp.float32)  3.55 us
  transfers between devices with their start and end apart: 14, of which 7 were waited for; matrix products, arithmetic and copies ran while one was open for 35% of the time, Pallas kernels for 0%

profile of v5, /device:TPU:0, one launch (start us, length us, event | category | flops | bytes accessed | tf_op | source)
XLA Modules:
  0.0 94.3 jit_solution(2432774424833999966)
XLA Ops:
  0.0 0.8 convert_bitcast_fusion
  0.8 1.0 %multiply_convert_fusion = bf16[128,640]{1,0:T(8,128)(2,1)S(1)} fusion(bf16[128,640]{1,0:T(8,128)(2,1)} %param.8, f32[128]{0:T(128)} %param.9), kind=kLoop, calls=%fused_computation.43 | loop fusion | flops 245760 | bytes 328192 | tf_op jit(solution)/shard_map/convert_element_type | solution.py:65
  1.9 5.1 %collective-permute-start.6 = (bf16[144,640]{1,0:T(8,128)(2,1)S(1)}, bf16[144,640]{1,0:T(8,128)(2,1)}, u32[]{:S(2)}, u32[]{:S(2)}) collective-permute-start(bf16[144,640]{1,0:T(8,128)(2,1)S(1)} %fusion.13), channel_id=1, source_target_pairs={{0,12},{4,8},{8,4},{12,0},{1,13},{5,9},{9,5},{13,1},{2,14},{6,10},... | collective-permute-start | bytes 552968 | tf_op jit(solution)/shard_map/ppermute | solution.py:70
  7.0 0.6 collective-permute-start.4
  7.6 1.6 %collective-permute-start = (bf16[128,640]{1,0:T(8,128)(2,1)S(1)}, bf16[128,640]{1,0:T(8,128)(2,1)S(1)}, u32[]{:S(2)}, u32[]{:S(2)}) collective-permute-start(bf16[128,640]{1,0:T(8,128)(2,1)S(1)} %multiply_convert_fusion), channel_id=1, source_target_pairs={{0,2},{1,3},{2,0},{3,1},{4,6},{5,7},{6,4},{7,5},{8,10},{9,11},{10,... | collective-permute-start | bytes 491528 | tf_op jit(solution)/shard_map/ppermute | solution.py:81
  9.2 3.4 %collective-permute-done.6 = bf16[144,640]{1,0:T(8,128)(2,1)} collective-permute-done((bf16[144,640]{1,0:T(8,128)(2,1)S(1)}, bf16[144,640]{1,0:T(8,128)(2,1)}, u32[]{:S(2)}, u32[]{:S(2)}) %collective-permute-start.6) | collective-permute-done | bytes 184352 | tf_op jit(solution)/shard_map/ppermute | solution.py:70
  12.7 0.9 slice.99
  13.6 9.1 %collective-permute-done.5 = bf16[144,640]{1,0:T(8,128)(2,1)} collective-permute-done((bf16[144,640]{1,0:T(8,128)(2,1)S(1)}, bf16[144,640]{1,0:T(8,128)(2,1)}, u32[]{:S(2)}, u32[]{:S(2)}) %collective-permute-start.5) | collective-permute-done | bytes 184352 | tf_op jit(solution)/shard_map/ppermute | solution.py:70
  22.7 0.9 slice.98
  23.6 0.0 collective-permute-done.4
  23.7 0.9 slice.97
  24.6 0.8 pad_maximum_fusion.6
  25.4 1.5 %collective-permute-start.7 = (bf16[384,640]{1,0:T(8,128)(2,1)}, bf16[384,640]{1,0:T(8,128)(2,1)}, u32[]{:S(2)}, u32[]{:S(2)}) collective-permute-start(bf16[384,640]{1,0:T(8,128)(2,1)} %pad_maximum_fusion.6), channel_id=1, source_target_pairs={{0,2},{1,3},{2,0},{3,1},{4,6},{5,7},{6,4},{7,5},{8,10},{9,11},{10,... | collective-permute-start | bytes 1474568 | tf_op jit(solution)/shard_map/ppermute | solution.py:81
  26.9 1.5 %dynamic-slice_bitcast_fusion.3 = (bf16[512,640]{1,0:T(8,128)(2,1)}, bf16[512,640]{1,0:T(8,128)(2,1)}, bf16[512,640]{1,0:T(8,128)(2,1)}, bf16[512,640]{1,0:T(8,128)(2,1)}) fusion(bf16[1,512,2560]{2,1,0:T(8,128)(2,1)S(1)} %copy-done, s32[]{:T(128)S(6)} %select_n.34, s32[]{:T(128)S(6)} %select_n.35, s32[]{:T(128)S(6)} %select_n.37, s32[]{:T(128)S(6)} %select_n.36), kind=kLoop, calls=%fused_computation.17 | loop fusion | bytes 5242896 | tf_op jit(solution)/shard_map/dynamic_slice | solution.py:55
  28.5 4.3 %dynamic-slice_bitcast_fusion.7 = (bf16[640,512]{1,0:T(8,128)(2,1)}, bf16[640,512]{1,0:T(8,128)(2,1)}, bf16[640,512]{1,0:T(8,128)(2,1)}, bf16[640,512]{1,0:T(8,1...) fusion(bf16[1,2560,512]{2,1,0:T(8,128)(2,1)} %param.12, ...), kind=kLoop, calls=%fused_computation.21 | loop fusion | bytes 10485776 | tf_op jit(solution)/shard_map/dynamic_slice | solution.py:55
  32.8 5.2 %collective-permute-done.7 = bf16[384,640]{1,0:T(8,128)(2,1)} collective-permute-done((bf16[384,640]{1,0:T(8,128)(2,1)}, bf16[384,640]{1,0:T(8,128)(2,1)}, u32[]{:S(2)}, u32[]{:S(2)}) %collective-permute-start.7) | collective-permute-done | bytes 491552 | tf_op jit(solution)/shard_map/ppermute | solution.py:81
  38.0 1.1 %pad_maximum_fusion.4 = bf16[384,1280]{1,0:T(8,128)(2,1)S(1)} fusion(bf16[384,640]{1,0:T(8,128)(2,1)} %collective-permute-done.7, bf16[128,640]{1,0:T(8,128)(2,1)S(1)} %slice.99, bf16[128,640]{1,0:T(8,128)(2,1)S(1)} %slice.98, bf16[128,640]{1,0:T(8,128)(2,1)S(1)} %slice.97), kind=kLoop, calls=%fused_computation.10 | loop fusion | flops 3932160 | bytes 1966080 | tf_op jit(solution)/shard_map/concatenate | solution.py:80
  39.1 0.1 collective-permute-start.8
  39.2 0.0 collective-permute-done
  39.2 0.0 copy-start.6
  39.2 0.8 pad_maximum_fusion.17
  40.0 0.5 collective-permute-start.1
  40.5 0.7 slice_bitcast_fusion
  41.2 0.7 slice_bitcast_fusion.1
  41.8 0.7 slice_bitcast_fusion.2
  42.5 3.5 %fusion.3 = f32[384,512]{1,0:T(8,128)} fusion(bf16[640,512]{1,0:T(8,128)(2,1)S(1)} %get-tuple-element.33, bf16[640,512]{1,0:T(8,128)(2,1)S(1)} %get-tuple-element.32, bf16[640,512]{1,0:T(8,128)(2,1)S(1)} %get-tuple-element.34, bf16[640,512]{1,0:T(8,128)(2,1)S(1)} %get-tuple-element.35, bf16[384,1280]{1,0:T(8,128)(2,1)S(1)} %collective-permute-done.8, ...), kind=kOutput, calls=%fused_computation.29 | convolution fusion | flops 1026949120 | bytes 5373952 | tf_op jit(solution)/shard_map/dot_general | solution.py:84
  46.0 5.4 %convolution_convert_fusion = bf16[384,2560]{1,0:T(8,128)(2,1)S(1)} fusion(bf16[512,640]{1,0:T(8,128)(2,1)} %get-tuple-element.27, bf16[512,640]{1,0:T(8,128)(2,1)} %get-tuple-element.28, bf16[512,640]{1,0:T(8,128)(2,1)} %get-tuple-element.26, bf16[512,640]{1,0:T(8,128)(2,1)} %get-tuple-element.25, f32[384,512]{1,0:T(8,128)} %fusion.3, ...), kind=kOutput, calls=%fused_computation | convolution fusion | flops 2046427136 | bytes 9961856 | tf_op jit(solution)/shard_map/dot_general | solution.py:88
  51.5 1.0 %slice.101 = bf16[384,1280]{1,0:T(8,128)(2,1)} slice(bf16[384,2560]{1,0:T(8,128)(2,1)S(1)} %convolution_convert_fusion), slice={[0:384], [1280:2560]} | slice | bytes 1966080 | tf_op jit(solution)/shard_map/slice | solution.py:90
  52.5 0.0 collective-permute-start.9
  52.5 0.0 collective-permute-done.1
  52.5 3.1 %fusion.2 = f32[128,512]{1,0:T(8,128)} fusion(bf16[640,512]{1,0:T(8,128)(2,1)} %get-tuple-element.23, bf16[640,512]{1,0:T(8,128)(2,1)} %get-tuple-element.24, bf16[640,512]{1,0:T(8,128)(2,1)} %get-tuple-element.22, bf16[640,512]{1,0:T(8,128)(2,1)} %get-tuple-element.21, bf16[128,1280]{1,0:T(8,128)(2,1)} %collective-permute-done.1, ...), kind=kOutput, calls=%fused_computation.28 | convolution fusion | flops 347996160 | bytes 3538944 | tf_op jit(solution)/shard_map/dot_general | solution.py:85
  55.7 4.2 %convolution_convert_fusion.1 = bf16[128,2560]{1,0:T(8,128)(2,1)} fusion(bf16[512,640]{1,0:T(8,128)(2,1)} %get-tuple-element.27, bf16[512,640]{1,0:T(8,128)(2,1)} %get-tuple-element.28, bf16[512,640]{1,0:T(8,128)(2,1)} %get-tuple-element.26, bf16[512,640]{1,0:T(8,128)(2,1)} %get-tuple-element.25, f32[128,512]{1,0:T(8,128)} %fusion.2, ...), kind=kOutput, calls=%fused_computation.1 | convolution fusion | flops 694812672 | bytes 6815872 | tf_op jit(solution)/shard_map/dot_general | solution.py:88
  59.9 1.0 %slice.91 = bf16[128,1280]{1,0:T(8,128)(2,1)S(1)} slice(bf16[128,2560]{1,0:T(8,128)(2,1)} %convolution_convert_fusion.1), slice={[0:128], [1280:2560]} | slice | bytes 655360 | tf_op jit(solution)/shard_map/slice | solution.py:90
  60.9 0.5 collective-permute-start.2
  61.4 1.4 %convert_add_fusion = f32[384,1280]{1,0:T(8,128)S(1)} fusion(bf16[384,1280]{1,0:T(8,128)(2,1)} %collective-permute-done.9, bf16[384,2560]{1,0:T(8,128)(2,1)S(1)} %convolution_convert_fusion), kind=kLoop, calls=%fused_computation.6 | loop fusion | flops 1474560 | bytes 3932160 | tf_op jit(solution)/shard_map/add | solution.py:89
  62.8 0.1 slice.126
  62.9 1.6 %collective-permute-start.10 = (bf16[384,640]{1,0:T(8,128)(2,1)S(1)}, bf16[384,640]{1,0:T(8,128)(2,1)S(1)}, u32[]{:S(2)}, u32[]{:S(2)}) collective-permute-start(bf16[384,640]{1,0:T(8,128)(2,1)S(1)} %slice.126), channel_id=1, source_target_pairs={{0,2},{1,3},{2,0},{3,1},{4,6},{5,7},{6,4},{7,5},{8,10},{9,11},{10,... | collective-permute-start | bytes 1474568 | tf_op jit(solution)/shard_map/ppermute | solution.py:91
  64.4 0.1 convert_add_fusion.1
  64.5 0.6 collective-permute-start.3
  65.1 11.9 %collective-permute-done.10 = bf16[384,640]{1,0:T(8,128)(2,1)S(1)} collective-permute-done((bf16[384,640]{1,0:T(8,128)(2,1)S(1)}, bf16[384,640]{1,0:T(8,128)(2,1)S(1)}, u32[]{:S(2)}, u32[]{:S(2)}) %collective-permute-start.10) | collective-permute-done | bytes 491552 | tf_op jit(solution)/shard_map/ppermute | solution.py:91
  77.0 0.1 fusion
  77.2 0.1 collective-permute-start.11
  77.2 2.4 %collective-permute-start.13 = (bf16[128,640]{1,0:T(8,128)(2,1)S(1)}, bf16[128,640]{1,0:T(8,128)(2,1)S(1)}, u32[]{:S(2)}, u32[]{:S(2)}) collective-permute-start(bf16[128,640]{1,0:T(8,128)(2,1)S(1)} %get-tuple-element.30), channel_id=1, source_target_pairs={{0,12},{4,8},{8,4},{12,0},{1,13},{5,9},{9,5},{13,1},{2,14},{6,10},... | collective-permute-start | bytes 491528 | tf_op jit(solution)/shard_map/ppermute | solution.py:98
  79.6 1.1 %collective-permute-start.12 = (bf16[128,640]{1,0:T(8,128)(2,1)S(1)}, bf16[128,640]{1,0:T(8,128)(2,1)S(1)}, u32[]{:S(2)}, u32[]{:S(2)}) collective-permute-start(bf16[128,640]{1,0:T(8,128)(2,1)S(1)} %get-tuple-element.31), channel_id=1, source_target_pairs={{0,8},{4,12},{8,0},{12,4},{1,9},{5,13},{9,1},{13,5},{2,10},{6,14},... | collective-permute-start | bytes 491528 | tf_op jit(solution)/shard_map/ppermute | solution.py:98
  80.7 4.2 %collective-permute-done.11 = bf16[128,640]{1,0:T(8,128)(2,1)S(1)} collective-permute-done((bf16[128,640]{1,0:T(8,128)(2,1)S(1)}, bf16[128,640]{1,0:T(8,128)(2,1)S(1)}, u32[]{:S(2)}, u32[]{:S(2)}) %collective-permute-start.11) | collective-permute-done | bytes 163872 | tf_op jit(solution)/shard_map/ppermute | solution.py:98
  84.9 2.7 %collective-permute-done.13 = bf16[128,640]{1,0:T(8,128)(2,1)S(1)} collective-permute-done((bf16[128,640]{1,0:T(8,128)(2,1)S(1)}, bf16[128,640]{1,0:T(8,128)(2,1)S(1)}, u32[]{:S(2)}, u32[]{:S(2)}) %collective-permute-start.13) | collective-permute-done | bytes 163872 | tf_op jit(solution)/shard_map/ppermute | solution.py:98
  87.6 5.9 %collective-permute-done.12 = bf16[128,640]{1,0:T(8,128)(2,1)S(1)} collective-permute-done((bf16[128,640]{1,0:T(8,128)(2,1)S(1)}, bf16[128,640]{1,0:T(8,128)(2,1)S(1)}, u32[]{:S(2)}, u32[]{:S(2)}) %collective-permute-start.12) | collective-permute-done | bytes 163872 | tf_op jit(solution)/shard_map/ppermute | solution.py:98
  93.5 0.8 fusion.12
  (27 shorter events, 0.1 us)
Async XLA Ops:
  0.0 26.9 %copy-start = (bf16[1,512,2560]{2,1,0:T(8,128)(2,1)S(1)}, bf16[1,512,2560]{2,1,0:T(8,128)(2,1)}, u32[]{:S(2)}) copy-start(bf16[1,512,2560]{2,1,0:T(8,128)(2,1)} %param.13) | copy-start | bytes 7864324
  1.9 10.8 %collective-permute-start.6 = (bf16[144,640]{1,0:T(8,128)(2,1)S(1)}, bf16[144,640]{1,0:T(8,128)(2,1)}, u32[]{:S(2)}, u32[]{:S(2)}) collective-permute-start(bf16[144,640]{1,0:T(8,128)(2,1)S(1)} %fusion.13), channel_id=1, source_target_pairs={{0,12},{4,8},{8,4},{12,0},{1,13},{5,9},{9,5},{13,1},{2,14},{6,10},... | collective-permute-start | bytes 552968 | tf_op jit(solution)/shard_map/ppermute | solution.py:70
  7.0 15.7 %collective-permute-start.5 = (bf16[144,640]{1,0:T(8,128)(2,1)S(1)}, bf16[144,640]{1,0:T(8,128)(2,1)}, u32[]{:S(2)}, u32[]{:S(2)}) collective-permute-start(bf16[144,640]{1,0:T(8,128)(2,1)S(1)} %fusion.13), channel_id=1, source_target_pairs={{0,8},{4,12},{8,0},{12,4},{1,9},{5,13},{9,1},{13,5},{2,10},{6,14},... | collective-permute-start | bytes 552968 | tf_op jit(solution)/shard_map/ppermute | solution.py:70
  7.0 16.7 %collective-permute-start.4 = (bf16[144,640]{1,0:T(8,128)(2,1)S(1)}, bf16[144,640]{1,0:T(8,128)(2,1)}, u32[]{:S(2)}, u32[]{:S(2)}) collective-permute-start(bf16[144,640]{1,0:T(8,128)(2,1)S(1)} %fusion.13), channel_id=1, source_target_pairs={{0,4},{4,0},{8,12},{12,8},{1,5},{5,1},{9,13},{13,9},{2,6},{6,2},{1... | collective-permute-start | bytes 552968 | tf_op jit(solution)/shard_map/ppermute | solution.py:70
  7.6 31.6 %collective-permute-start = (bf16[128,640]{1,0:T(8,128)(2,1)S(1)}, bf16[128,640]{1,0:T(8,128)(2,1)S(1)}, u32[]{:S(2)}, u32[]{:S(2)}) collective-permute-start(bf16[128,640]{1,0:T(8,128)(2,1)S(1)} %multiply_convert_fusion), channel_id=1, source_target_pairs={{0,2},{1,3},{2,0},{3,1},{4,6},{5,7},{6,4},{7,5},{8,10},{9,11},{10,... | collective-permute-start | bytes 491528 | tf_op jit(solution)/shard_map/ppermute | solution.py:81
  25.4 3.0 %copy-start.8 = (s32[128,1]{0,1:T(1,128)S(1)}, s32[128,1]{0,1:T(1,128)}, u32[]{:S(2)}) copy-start(s32[128,1]{0,1:T(1,128)} %param.10) | copy-start | bytes 1540
  25.4 12.6 %collective-permute-start.7 = (bf16[384,640]{1,0:T(8,128)(2,1)}, bf16[384,640]{1,0:T(8,128)(2,1)}, u32[]{:S(2)}, u32[]{:S(2)}) collective-permute-start(bf16[384,640]{1,0:T(8,128)(2,1)} %pad_maximum_fusion.6), channel_id=1, source_target_pairs={{0,2},{1,3},{2,0},{3,1},{4,6},{5,7},{6,4},{7,5},{8,10},{9,11},{10,... | collective-permute-start | bytes 1474568 | tf_op jit(solution)/shard_map/ppermute | solution.py:81
  32.8 13.2 %copy-start.1 = (bf16[640,512]{1,0:T(8,128)(2,1)}, bf16[640,512]{1,0:T(8,128)(2,1)S(1)}, u32[]{:S(2)}) copy-start(bf16[640,512]{1,0:T(8,128)(2,1)S(1)} %get-tuple-element.33) | copy-start | bytes 1966084
  32.8 13.2 %copy-start.3 = (bf16[640,512]{1,0:T(8,128)(2,1)}, bf16[640,512]{1,0:T(8,128)(2,1)S(1)}, u32[]{:S(2)}) copy-start(bf16[640,512]{1,0:T(8,128)(2,1)S(1)} %get-tuple-element.34) | copy-start | bytes 1966084
  32.8 13.2 %copy-start.4 = (bf16[640,512]{1,0:T(8,128)(2,1)}, bf16[640,512]{1,0:T(8,128)(2,1)S(1)}, u32[]{:S(2)}) copy-start(bf16[640,512]{1,0:T(8,128)(2,1)S(1)} %get-tuple-element.35) | copy-start | bytes 1966084
  39.1 3.4 %collective-permute-start.8 = (bf16[384,1280]{1,0:T(8,128)(2,1)S(1)}, bf16[384,1280]{1,0:T(8,128)(2,1)S(1)}, u32[]{:S(2)}, u32[]{:S(2)}) collective-permute-start(bf16[384,1280]{1,0:T(8,128)(2,1)S(1)} %pad_maximum_fusion.4), channel_id=1, source_target_pairs={{0,1},{1,0},{2,3},{3,2},{4,5},{5,4},{6,7},{7,6},{8,9},{9,8},{10,11... | collective-permute-start | bytes 2949128 | tf_op jit(solution)/shard_map/ppermute | solution.py:83
  39.2 6.8 %copy-start.6 = (bf16[128,640]{1,0:T(8,128)(2,1)}, bf16[128,640]{1,0:T(8,128)(2,1)S(1)}, u32[]{:S(2)}) copy-start(bf16[128,640]{1,0:T(8,128)(2,1)S(1)} %collective-permute-done) | copy-start | bytes 491524
  40.0 12.5 %collective-permute-start.1 = (bf16[128,1280]{1,0:T(8,128)(2,1)}, bf16[128,1280]{1,0:T(8,128)(2,1)}, u32[]{:S(2)}, u32[]{:S(2)}) collective-permute-start(bf16[128,1280]{1,0:T(8,128)(2,1)} %pad_maximum_fusion.17), channel_id=1, source_target_pairs={{0,1},{1,0},{2,3},{3,2},{4,5},{5,4},{6,7},{7,6},{8,9},{9,8},{10,11... | collective-permute-start | bytes 983048 | tf_op jit(solution)/shard_map/ppermute | solution.py:83
  42.5 3.5 %copy-start.7 = (bf16[384,1280]{1,0:T(8,128)(2,1)}, bf16[384,1280]{1,0:T(8,128)(2,1)S(1)}, u32[]{:S(2)}) copy-start(bf16[384,1280]{1,0:T(8,128)(2,1)S(1)} %collective-permute-done.8) | copy-start | bytes 2949124
  52.5 3.2 %copy-start.2 = (bf16[640,512]{1,0:T(8,128)(2,1)S(1)}, bf16[640,512]{1,0:T(8,128)(2,1)}, u32[]{:S(2)}) copy-start(bf16[640,512]{1,0:T(8,128)(2,1)} %copy-done.1) | copy-start | bytes 1966084
  52.5 8.9 %collective-permute-start.9 = (bf16[384,1280]{1,0:T(8,128)(2,1)}, bf16[384,1280]{1,0:T(8,128)(2,1)}, u32[]{:S(2)}, u32[]{:S(2)}) collective-permute-start(bf16[384,1280]{1,0:T(8,128)(2,1)} %slice.101), channel_id=1, source_target_pairs={{0,1},{1,0},{2,3},{3,2},{4,5},{5,4},{6,7},{7,6},{8,9},{9,8},{10,11... | collective-permute-start | bytes 2949128 | tf_op jit(solution)/shard_map/ppermute | solution.py:89
  60.9 3.6 %copy-start.5 = (bf16[128,2560]{1,0:T(8,128)(2,1)S(1)}, bf16[128,2560]{1,0:T(8,128)(2,1)}, u32[]{:S(2)}) copy-start(bf16[128,2560]{1,0:T(8,128)(2,1)} %convolution_convert_fusion.1) | copy-start | bytes 1966084
  60.9 3.5 %collective-permute-start.2 = (bf16[128,1280]{1,0:T(8,128)(2,1)S(1)}, bf16[128,1280]{1,0:T(8,128)(2,1)S(1)}, u32[]{:S(2)}, u32[]{:S(2)}) collective-permute-start(bf16[128,1280]{1,0:T(8,128)(2,1)S(1)} %slice.91), channel_id=1, source_target_pairs={{0,1},{1,0},{2,3},{3,2},{4,5},{5,4},{6,7},{7,6},{8,9},{9,8},{10,11... | collective-permute-start | bytes 983048 | tf_op jit(solution)/shard_map/ppermute | solution.py:89
  62.9 14.1 %collective-permute-start.10 = (bf16[384,640]{1,0:T(8,128)(2,1)S(1)}, bf16[384,640]{1,0:T(8,128)(2,1)S(1)}, u32[]{:S(2)}, u32[]{:S(2)}) collective-permute-start(bf16[384,640]{1,0:T(8,128)(2,1)S(1)} %slice.126), channel_id=1, source_target_pairs={{0,2},{1,3},{2,0},{3,1},{4,6},{5,7},{6,4},{7,5},{8,10},{9,11},{10,... | collective-permute-start | bytes 1474568 | tf_op jit(solution)/shard_map/ppermute | solution.py:91
  64.5 16.2 %collective-permute-start.3 = (bf16[128,640]{1,0:T(8,128)(2,1)S(1)}, bf16[128,640]{1,0:T(8,128)(2,1)S(1)}, u32[]{:S(2)}, u32[]{:S(2)}) collective-permute-start(bf16[128,640]{1,0:T(8,128)(2,1)S(1)} %slice.127), channel_id=1, source_target_pairs={{0,2},{1,3},{2,0},{3,1},{4,6},{5,7},{6,4},{7,5},{8,10},{9,11},{10,... | collective-permute-start | bytes 491528 | tf_op jit(solution)/shard_map/ppermute | solution.py:91
  77.2 7.7 %collective-permute-start.11 = (bf16[128,640]{1,0:T(8,128)(2,1)S(1)}, bf16[128,640]{1,0:T(8,128)(2,1)S(1)}, u32[]{:S(2)}, u32[]{:S(2)}) collective-permute-start(bf16[128,640]{1,0:T(8,128)(2,1)S(1)} %get-tuple-element.29), channel_id=1, source_target_pairs={{0,4},{4,0},{8,12},{12,8},{1,5},{5,1},{9,13},{13,9},{2,6},{6,2},{1... | collective-permute-start | bytes 491528 | tf_op jit(solution)/shard_map/ppermute | solution.py:98
  77.2 10.4 %collective-permute-start.13 = (bf16[128,640]{1,0:T(8,128)(2,1)S(1)}, bf16[128,640]{1,0:T(8,128)(2,1)S(1)}, u32[]{:S(2)}, u32[]{:S(2)}) collective-permute-start(bf16[128,640]{1,0:T(8,128)(2,1)S(1)} %get-tuple-element.30), channel_id=1, source_target_pairs={{0,12},{4,8},{8,4},{12,0},{1,13},{5,9},{9,5},{13,1},{2,14},{6,10},... | collective-permute-start | bytes 491528 | tf_op jit(solution)/shard_map/ppermute | solution.py:98
  79.6 13.9 %collective-permute-start.12 = (bf16[128,640]{1,0:T(8,128)(2,1)S(1)}, bf16[128,640]{1,0:T(8,128)(2,1)S(1)}, u32[]{:S(2)}, u32[]{:S(2)}) collective-permute-start(bf16[128,640]{1,0:T(8,128)(2,1)S(1)} %get-tuple-element.31), channel_id=1, source_target_pairs={{0,8},{4,12},{8,0},{12,4},{1,9},{5,13},{9,1},{13,5},{2,10},{6,14},... | collective-permute-start | bytes 491528 | tf_op jit(solution)/shard_map/ppermute | solution.py:98

commit v6 on v4

--- a/solution.py
+++ b/solution.py
@@ -50,9 +50,9 @@
 _ORDER = (0, 2, 1, 3)
 
 
-def _slots(weight, t, width, axis):
+def _slots(weight, t, width, axis, order=_ORDER):
     return jnp.concatenate(
-        [lax.dynamic_slice_in_dim(weight, (t ^ k) * width, width, axis=axis) for k in _ORDER], axis=axis)
+        [lax.dynamic_slice_in_dim(weight, (t ^ k) * width, width, axis=axis) for k in order], axis=axis)
 
 
 def gathered(tokens, route_scale, expert_ids, gate_weight, up_weight, down_weight):
@@ -71,28 +71,37 @@
     ]
     gate_w = _slots(gate_weight[0], t, width, 0)
     up_w = _slots(up_weight[0], t, width, 0)
-    down_w = _slots(down_weight[0], t, width, 1)
+    down_keep = _slots(down_weight[0], t, width, 1, _ORDER[:2])
+    down_send = _slots(down_weight[0], t, width, 1, _ORDER[2:])
+    waves = [[0], [1], list(range(2, n_expert))][:max(1, min(3, n_expert))]
     total = None
-    for k, blk in enumerate(blocks):
-        routed = blk[tok_rows, :tok_rows]
-        piece = blk[:tok_rows]
+    previous = None
+    for wave in waves:
+        routed = jnp.concatenate([blocks[k][tok_rows, :tok_rows] for k in wave])
+        piece = jnp.concatenate([blocks[k][:tok_rows] for k in wave])
         pair = jnp.concatenate(
             [piece, lax.ppermute(piece, "tensor", _xor_pairs(n_tensor, 2))], axis=1)
         rows = jnp.concatenate(
             [pair, lax.ppermute(pair, "tensor", _xor_pairs(n_tensor, 1))], axis=1)
+        if previous is not None:
+            rows, routed, _ = lax.optimization_barrier((rows, routed, previous))
         gate_act = jnp.dot(rows, gate_w, preferred_element_type=jnp.float32)
         up_act = jnp.dot(rows, up_w, preferred_element_type=jnp.float32)
         mine = (routed == expert)[:, None]
         hidden = jnp.where(mine, jax.nn.silu(gate_act) * up_act, 0.0).astype(jnp.bfloat16)
-        partial_value = jnp.dot(hidden, down_w, preferred_element_type=jnp.float32).astype(jnp.bfloat16)
-        over_c = partial_value[:, :2 * width].astype(jnp.float32) + lax.ppermute(
-            partial_value[:, 2 * width:], "tensor", _xor_pairs(n_tensor, 1)).astype(jnp.float32)
+        keep = jnp.dot(hidden, down_keep, preferred_element_type=jnp.float32).astype(jnp.bfloat16)
+        send = jnp.dot(hidden, down_send, preferred_element_type=jnp.float32).astype(jnp.bfloat16)
+        previous = keep
+        over_c = keep.astype(jnp.float32) + lax.ppermute(
+            send, "tensor", _xor_pairs(n_tensor, 1)).astype(jnp.float32)
         summed = over_c[:, :width] + lax.ppermute(
             over_c[:, width:].astype(jnp.bfloat16), "tensor", _xor_pairs(n_tensor, 2)).astype(jnp.float32)
-        if k:
-            summed = lax.ppermute(
-                summed.astype(jnp.bfloat16), "expert", _xor_pairs(n_expert, k)).astype(jnp.float32)
-        total = summed if total is None else total + summed
+        for i, k in enumerate(wave):
+            part = summed[i * tok_rows:(i + 1) * tok_rows]
+            if k:
+                part = lax.ppermute(
+                    part.astype(jnp.bfloat16), "expert", _xor_pairs(n_expert, k)).astype(jnp.float32)
+            total = part if total is None else total + part
     return total.astype(jnp.bfloat16)
 
 

time: 97.4 us -> 69.2 us (0.71)
  matrix products: 26.5 us -> 6.71 us
  waiting for transfers between devices: 20.7 us -> 35.6 us
  local copies, waits for them, and re-layouts: 14.2 us -> 3.69 us
  other arithmetic: 12.6 us -> 3.52 us
  starting transfers between devices: 22 us -> 19.3 us
    dot_general x4 -> x9, matrix products: 15.6 us -> 4.81 us  [the longest x3 2.34 us: gathered(): gate_act = jnp.dot(rows, gate_w, preferred_element_type=jnp.float32)]
    dot_general x4 -> x3, matrix products: 11 us -> 1.9 us  [gathered(): up_act = jnp.dot(rows, up_w, preferred_element_type=jnp.float32)]
    slice x7 -> x4, local copies, waits for them, and re-layouts: 9.06 us -> 0.07 us  [the longest x3 0.04 us: gathered(): piece = jnp.concatenate([blocks[k][:tok_rows] for k in wave])]
    ppermute x3, waiting for transfers between devices: 4.24 us -> 9.6 us  [gathered(): lax.ppermute(block, 'expert', _xor_pairs(n_expert, k))]
    ppermute x4 -> x3, waiting for transfers between devices: 1.07 us -> 6.13 us  [gathered(): lax.ppermute(piece, 'tensor', _xor_pairs(n_tensor, 2))]
    ppermute x7 -> x6, waiting for transfers between devices: 7.74 us -> 12.1 us  [the longest x3 9.73 us: gathered(): lax.ppermute(part.astype(jnp.bfloat16), 'expert', _xor_pairs(n_expert, k))]
    add x4 -> x0, other arithmetic: 3.3 us -> none  [gathered(): partial_value[:, :2 * width].astype(jnp.float32)]
    concatenate x4 -> x3, other arithmetic: 3.39 us -> 0.1 us  [gathered(): jnp.concatenate([piece, lax.ppermute(piece, 'tensor', _xor_pairs(n_tensor...]
  transfers between devices with their start and end apart: 22 -> 18, of which waited for: 7 -> 9; matrix products, arithmetic and copies ran while one was open for 52% -> 14% of each run, Pallas kernels for 0% -> 0%
where the time goes in v6:
time: 69.2 us; the launch traced here: 69 us
  waiting for transfers between devices  35.6 us (51%)
  starting transfers between devices  19.3 us (28%)
  matrix products  6.71 us (10%)
  local copies, waits for them, and re-layouts  3.69 us (5%)
  other arithmetic  3.52 us (5%)
    ppermute x3, waiting for transfers between devices, gathered(): lax.ppermute(part.astype(jnp.bfloat16), 'expert', _xor_pairs(n_expert, k))  9.73 us
    ppermute x3, waiting for transfers between devices, gathered(): lax.ppermute(block, 'expert', _xor_pairs(n_expert, k))  9.6 us
    ppermute x3, waiting for transfers between devices, gathered(): lax.ppermute(over_c[:, width:].astype(jnp.bfloat16), 'tensor', _xor_pairs...  7.76 us
    ppermute x3, waiting for transfers between devices, gathered(): lax.ppermute(piece, 'tensor', _xor_pairs(n_tensor, 2))  6.13 us
    ppermute x3, starting transfers between devices, gathered(): lax.ppermute(part.astype(jnp.bfloat16), 'expert', _xor_pairs(n_expert, k))  6.08 us
    ppermute x3, starting transfers between devices, gathered(): lax.ppermute(block, 'expert', _xor_pairs(n_expert, k))  4.45 us
    ppermute x3, starting transfers between devices, gathered(): lax.ppermute(piece, 'tensor', _xor_pairs(n_tensor, 2))  4.2 us
    dynamic_slice x2, local copies, waits for them, and re-layouts, _slots(): lax.dynamic_slice_in_dim(weight, (t ^ k) * width, width, axis=axis)  3.42 us
  transfers between devices with their start and end apart: 18, of which 9 were waited for; matrix products, arithmetic and copies ran while one was open for 14% of the time, Pallas kernels for 0%

profile of v6, /device:TPU:0, one launch (start us, length us, event | category | flops | bytes accessed | tf_op | source)
XLA Modules:
  0.0 69.0 jit_solution(13326312219679828887)
XLA Ops:
  0.0 1.0 %multiply_convert_fusion = bf16[128,640]{1,0:T(8,128)(2,1)S(1)} fusion(bf16[128,640]{1,0:T(8,128)(2,1)} %param.8, f32[128]{0:T(128)} %param.9), kind=kLoop, calls=%fused_computation.53 | loop fusion | flops 245760 | bytes 328192 | tf_op jit(solution)/shard_map/convert_element_type | solution.py:65
  1.0 3.0 %collective-permute-start = (bf16[128,640]{1,0:T(8,128)(2,1)S(1)}, bf16[128,640]{1,0:T(8,128)(2,1)S(1)}, u32[]{:S(2)}, u32[]{:S(2)}) collective-permute-start(bf16[128,640]{1,0:T(8,128)(2,1)S(1)} %multiply_convert_fusion), channel_id=1, source_target_pairs={{0,2},{1,3},{2,0},{3,1},{4,6},{5,7},{6,4},{7,5},{8,10},{9,11},{10,... | collective-permute-start | bytes 491528 | tf_op jit(solution)/shard_map/ppermute | solution.py:83
  4.0 0.7 convert_bitcast_fusion
  4.7 3.7 %collective-permute-start.11 = (bf16[144,640]{1,0:T(8,128)(2,1)S(1)}, bf16[144,640]{1,0:T(8,128)(2,1)S(1)}, u32[]{:S(2)}, u32[]{:S(2)}) collective-permute-start(bf16[144,640]{1,0:T(8,128)(2,1)S(1)} %fusion.14), channel_id=1, source_target_pairs={{0,12},{4,8},{8,4},{12,0},{1,13},{5,9},{9,5},{13,1},{2,14},{6,10},... | collective-permute-start | bytes 552968 | tf_op jit(solution)/shard_map/ppermute | solution.py:70
  8.4 0.0 collective-permute-start.10
  8.4 0.8 %collective-permute-start.4 = (bf16[144,640]{1,0:T(8,128)(2,1)S(1)}, bf16[144,640]{1,0:T(8,128)(2,1)S(1)}, u32[]{:S(2)}, u32[]{:S(2)}) collective-permute-start(bf16[144,640]{1,0:T(8,128)(2,1)S(1)} %fusion.14), channel_id=1, source_target_pairs={{0,4},{4,0},{8,12},{12,8},{1,5},{5,1},{9,13},{13,9},{2,6},{6,2},{1... | collective-permute-start | bytes 552968 | tf_op jit(solution)/shard_map/ppermute | solution.py:70
  9.2 0.7 compare_bitcast_fusion
  9.8 3.2 %dynamic-slice_bitcast_fusion.7 = (bf16[640,512]{1,0:T(8,128)(2,1)S(1)}, bf16[640,512]{1,0:T(8,128)(2,1)S(1)}, bf16[640,512]{1,0:T(8,128)(2,1)S(1)}, bf16[640,51...) fusion(bf16[1,2560,512]{2,1,0:T(8,128)(2,1)} %param.12, ...), kind=kLoop, calls=%fused_computation.34 | loop fusion | bytes 10485776 | tf_op jit(solution)/shard_map/dynamic_slice | solution.py:55
  13.0 0.1 copy-done
  13.1 0.2 dynamic-slice_bitcast_fusion.3
  13.4 0.1 collective-permute-start.1
  13.5 6.5 %collective-permute-done.4 = bf16[144,640]{1,0:T(8,128)(2,1)S(1)} collective-permute-done((bf16[144,640]{1,0:T(8,128)(2,1)S(1)}, bf16[144,640]{1,0:T(8,128)(2,1)S(1)}, u32[]{:S(2)}, u32[]{:S(2)}) %collective-permute-start.4) | collective-permute-done | bytes 184352 | tf_op jit(solution)/shard_map/ppermute | solution.py:70
  20.0 0.6 collective-permute-start.5
  20.6 3.1 %collective-permute-done.10 = bf16[144,640]{1,0:T(8,128)(2,1)S(1)} collective-permute-done((bf16[144,640]{1,0:T(8,128)(2,1)S(1)}, bf16[144,640]{1,0:T(8,128)(2,1)S(1)}, u32[]{:S(2)}, u32[]{:S(2)}) %collective-permute-start.10) | collective-permute-done | bytes 184352 | tf_op jit(solution)/shard_map/ppermute | solution.py:70
  23.8 0.6 collective-permute-start.12
  24.4 1.0 %collective-permute-done.5 = bf16[128,640]{1,0:T(8,128)(2,1)S(1)} collective-permute-done((bf16[128,640]{1,0:T(8,128)(2,1)S(1)}, bf16[128,640]{1,0:T(8,128)(2,1)S(1)}, u32[]{:S(2)}, u32[]{:S(2)}) %collective-permute-start.5) | collective-permute-done | bytes 163872 | tf_op jit(solution)/shard_map/ppermute | solution.py:83
  25.4 0.1 collective-permute-start.6
  25.5 0.5 fusion.13
  26.0 0.5 select_convert_fusion
  26.5 0.3 convolution_convert_fusion.4
  26.9 0.6 collective-permute-start.2
  27.4 5.1 %collective-permute-done.12 = bf16[256,640]{1,0:T(8,128)(2,1)S(1)} collective-permute-done((bf16[256,640]{1,0:T(8,128)(2,1)S(1)}, bf16[256,640]{1,0:T(8,128)(2,1)S(1)}, u32[]{:S(2)}, u32[]{:S(2)}) %collective-permute-start.12) | collective-permute-done | bytes 327712 | tf_op jit(solution)/shard_map/ppermute | solution.py:83
  32.6 0.1 collective-permute-start.13
  32.8 0.3 convert_add_fusion.2
  33.2 0.8 %fusion.24 = f32[128,512]{1,0:T(8,128)S(1)} fusion(bf16[128,2560]{1,0:T(8,128)(2,1)S(1)} %pad_maximum_fusion.6, bf16[640,512]{1,0:T(8,128)(2,1)S(1)} %get-tuple-element.44, bf16[640,512]{1,0:T(8,128)(2,1)S(1)} %get-tuple-element.43, bf16[640,512]{1,0:T(8,128)(2,1)S(1)} %get-tuple-element.45, bf16[640,512]{1,0:T(8,128)(2,1)S(1)} %get-tuple-element.46), kind=kOutput, calls=%fused_computation.75 | convolution fusion | flops 346030080 | bytes 3538944 | tf_op jit(solution)/shard_map/dot_general | solution.py:88
  33.9 0.5 fusion.4
  34.4 0.4 convolution_convert_fusion.2
  34.8 0.5 collective-permute-start.7
  35.4 1.2 %collective-permute-done.7 = bf16[128,1280]{1,0:T(8,128)(2,1)S(1)} collective-permute-done((bf16[128,1280]{1,0:T(8,128)(2,1)S(1)}, bf16[128,1280]{1,0:T(8,128)(2,1)S(1)}, u32[]{:S(2)}, u32[]{:S(2)}) %collective-permute-start.7) | collective-permute-done | bytes 327712 | tf_op jit(solution)/shard_map/ppermute | solution.py:95
  36.6 0.3 convert_add_fusion.1
  37.0 0.1 pad_maximum_fusion.4
  37.1 1.1 %fusion.23 = f32[256,512]{1,0:T(8,128)S(1)} fusion(bf16[256,2560]{1,0:T(8,128)(2,1)S(1)} %pad_maximum_fusion.4, bf16[640,512]{1,0:T(8,128)(2,1)S(1)} %get-tuple-element.44, bf16[640,512]{1,0:T(8,128)(2,1)S(1)} %get-tuple-element.43, bf16[640,512]{1,0:T(8,128)(2,1)S(1)} %get-tuple-element.45, bf16[640,512]{1,0:T(8,128)(2,1)S(1)} %get-tuple-element.46), kind=kOutput, calls=%fused_computation.74 | convolution fusion | flops 681574400 | bytes 4456448 | tf_op jit(solution)/shard_map/dot_general | solution.py:88
  38.2 0.9 %fusion.2 = bf16[256,512]{1,0:T(8,128)(2,1)S(1)} fusion(bf16[256,2560]{1,0:T(8,128)(2,1)S(1)} %pad_maximum_fusion.4, f32[256,512]{1,0:T(8,128)S(1)} %fusion.23, pred[256]{0:T(512)(128)(4,1)S(1)} %broadcast_compare_fusion, bf16[640,512]{1,0:T(8,128)(2,1)S(1)} %get-tuple-element.31, bf16[640,512]{1,0:T(8,128)(2,1)S(1)} %get-tuple-element.32, ...), kind=kOutput, calls=%fused_computation.15 | convolution fusion | flops 682491904 | bytes 4718848 | tf_op jit(solution)/shard_map/dot_general | solution.py:89
  39.1 0.5 convolution_convert_fusion
  39.6 0.4 collective-permute-start.14
  40.1 0.6 collective-permute-start.8
  40.7 1.1 %collective-permute-done.14 = bf16[256,1280]{1,0:T(8,128)(2,1)S(1)} collective-permute-done((bf16[256,1280]{1,0:T(8,128)(2,1)S(1)}, bf16[256,1280]{1,0:T(8,128)(2,1)S(1)}, u32[]{:S(2)}, u32[]{:S(2)}) %collective-permute-start.14) | collective-permute-done | bytes 655392 | tf_op jit(solution)/shard_map/ppermute | solution.py:95
  41.8 0.5 convert_add_fusion
  42.4 0.6 collective-permute-start.15
  43.0 1.6 %collective-permute-start.3 = (bf16[128,640]{1,0:T(8,128)(2,1)S(1)}, bf16[128,640]{1,0:T(8,128)(2,1)S(1)}, u32[]{:S(2)}, u32[]{:S(2)}) collective-permute-start(bf16[128,640]{1,0:T(8,128)(2,1)S(1)} %slice.115), channel_id=1, source_target_pairs={{0,2},{1,3},{2,0},{3,1},{4,6},{5,7},{6,4},{7,5},{8,10},{9,11},{10,... | collective-permute-start | bytes 491528 | tf_op jit(solution)/shard_map/ppermute | solution.py:97
  44.6 2.6 %collective-permute-done.8 = bf16[128,640]{1,0:T(8,128)(2,1)S(1)} collective-permute-done((bf16[128,640]{1,0:T(8,128)(2,1)S(1)}, bf16[128,640]{1,0:T(8,128)(2,1)S(1)}, u32[]{:S(2)}, u32[]{:S(2)}) %collective-permute-start.8) | collective-permute-done | bytes 163872 | tf_op jit(solution)/shard_map/ppermute | solution.py:97
  47.2 1.9 %collective-permute-start.9 = (bf16[128,640]{1,0:T(8,128)(2,1)S(1)}, bf16[128,640]{1,0:T(8,128)(2,1)S(1)}, u32[]{:S(2)}, u32[]{:S(2)}) collective-permute-start(bf16[128,640]{1,0:T(8,128)(2,1)S(1)} %fusion.7), channel_id=1, source_target_pairs={{0,4},{4,0},{8,12},{12,8},{1,5},{5,1},{9,13},{13,9},{2,6},{6,2},{1... | collective-permute-start | bytes 491528 | tf_op jit(solution)/shard_map/ppermute | solution.py:102
  49.1 5.1 %collective-permute-done.15 = bf16[256,640]{1,0:T(8,128)(2,1)S(1)} collective-permute-done((bf16[256,640]{1,0:T(8,128)(2,1)S(1)}, bf16[256,640]{1,0:T(8,128)(2,1)S(1)}, u32[]{:S(2)}, u32[]{:S(2)}) %collective-permute-start.15) | collective-permute-done | bytes 327712 | tf_op jit(solution)/shard_map/ppermute | solution.py:97
  54.2 0.1 fusion.5
  54.3 1.2 %collective-permute-start.16 = (bf16[128,640]{1,0:T(8,128)(2,1)S(1)}, bf16[128,640]{1,0:T(8,128)(2,1)S(1)}, u32[]{:S(2)}, u32[]{:S(2)}) collective-permute-start(bf16[128,640]{1,0:T(8,128)(2,1)S(1)} %get-tuple-element.37), channel_id=1, source_target_pairs={{0,8},{4,12},{8,0},{12,4},{1,9},{5,13},{9,1},{13,5},{2,10},{6,14},... | collective-permute-start | bytes 491528 | tf_op jit(solution)/shard_map/ppermute | solution.py:102
  55.5 3.1 %collective-permute-start.17 = (bf16[128,640]{1,0:T(8,128)(2,1)S(1)}, bf16[128,640]{1,0:T(8,128)(2,1)S(1)}, u32[]{:S(2)}, u32[]{:S(2)}) collective-permute-start(bf16[128,640]{1,0:T(8,128)(2,1)S(1)} %get-tuple-element.38), channel_id=1, source_target_pairs={{0,12},{4,8},{8,4},{12,0},{1,13},{5,9},{9,5},{13,1},{2,14},{6,10},... | collective-permute-start | bytes 491528 | tf_op jit(solution)/shard_map/ppermute | solution.py:102
  58.5 9.7 %collective-permute-done.16 = bf16[128,640]{1,0:T(8,128)(2,1)S(1)} collective-permute-done((bf16[128,640]{1,0:T(8,128)(2,1)S(1)}, bf16[128,640]{1,0:T(8,128)(2,1)S(1)}, u32[]{:S(2)}, u32[]{:S(2)}) %collective-permute-start.16) | collective-permute-done | bytes 163872 | tf_op jit(solution)/shard_map/ppermute | solution.py:102
  68.3 0.8 %fusion.11 = bf16[128,640]{1,0:T(8,128)(2,1)} fusion(f32[128,1280]{1,0:T(8,128)S(1)} %convert_add_fusion.2, bf16[128,640]{1,0:T(8,128)(2,1)S(1)} %collective-permute-done.17, bf16[128,640]{1,0:T(8,128)(2,1)S(1)} %collective-permute-done.16, bf16[128,640]{1,0:T(8,128)(2,1)S(1)} %collective-permute-done.9, bf16[128,640]{1,0:T(8,128)(2,1)S(1)} %collective-permute-done.3), kind=kLoop, calls=%fused_computation.49 | loop fusion | flops 737280 | bytes 1146880 | tf_op jit(solution)/shard_map/convert_element_type | solution.py:105
  (30 shorter events, 0.4 us)
Async XLA Ops:
  1.0 12.3 %collective-permute-start = (bf16[128,640]{1,0:T(8,128)(2,1)S(1)}, bf16[128,640]{1,0:T(8,128)(2,1)S(1)}, u32[]{:S(2)}, u32[]{:S(2)}) collective-permute-start(bf16[128,640]{1,0:T(8,128)(2,1)S(1)} %multiply_convert_fusion), channel_id=1, source_target_pairs={{0,2},{1,3},{2,0},{3,1},{4,6},{5,7},{6,4},{7,5},{8,10},{9,11},{10,... | collective-permute-start | bytes 491528 | tf_op jit(solution)/shard_map/ppermute | solution.py:83
  4.7 15.9 %collective-permute-start.11 = (bf16[144,640]{1,0:T(8,128)(2,1)S(1)}, bf16[144,640]{1,0:T(8,128)(2,1)S(1)}, u32[]{:S(2)}, u32[]{:S(2)}) collective-permute-start(bf16[144,640]{1,0:T(8,128)(2,1)S(1)} %fusion.14), channel_id=1, source_target_pairs={{0,12},{4,8},{8,4},{12,0},{1,13},{5,9},{9,5},{13,1},{2,14},{6,10},... | collective-permute-start | bytes 552968 | tf_op jit(solution)/shard_map/ppermute | solution.py:70
  8.4 15.4 %collective-permute-start.10 = (bf16[144,640]{1,0:T(8,128)(2,1)S(1)}, bf16[144,640]{1,0:T(8,128)(2,1)S(1)}, u32[]{:S(2)}, u32[]{:S(2)}) collective-permute-start(bf16[144,640]{1,0:T(8,128)(2,1)S(1)} %fusion.14), channel_id=1, source_target_pairs={{0,8},{4,12},{8,0},{12,4},{1,9},{5,13},{9,1},{13,5},{2,10},{6,14},... | collective-permute-start | bytes 552968 | tf_op jit(solution)/shard_map/ppermute | solution.py:70
  8.4 11.6 %collective-permute-start.4 = (bf16[144,640]{1,0:T(8,128)(2,1)S(1)}, bf16[144,640]{1,0:T(8,128)(2,1)S(1)}, u32[]{:S(2)}, u32[]{:S(2)}) collective-permute-start(bf16[144,640]{1,0:T(8,128)(2,1)S(1)} %fusion.14), channel_id=1, source_target_pairs={{0,4},{4,0},{8,12},{12,8},{1,5},{5,1},{9,13},{13,9},{2,6},{6,2},{1... | collective-permute-start | bytes 552968 | tf_op jit(solution)/shard_map/ppermute | solution.py:70
  9.8 3.3 %copy-start = (bf16[1,512,2560]{2,1,0:T(8,128)(2,1)S(1)}, bf16[1,512,2560]{2,1,0:T(8,128)(2,1)}, u32[]{:S(2)}) copy-start(bf16[1,512,2560]{2,1,0:T(8,128)(2,1)} %param.13) | copy-start | bytes 7864324
  13.4 12.1 %collective-permute-start.1 = (bf16[128,1280]{1,0:T(8,128)(2,1)S(1)}, bf16[128,1280]{1,0:T(8,128)(2,1)S(1)}, u32[]{:S(2)}, u32[]{:S(2)}) collective-permute-start(bf16[128,1280]{1,0:T(8,128)(2,1)S(1)} %pad_maximum_fusion.16), channel_id=1, source_target_pairs={{0,1},{1,0},{2,3},{3,2},{4,5},{5,4},{6,7},{7,6},{8,9},{9,8},{10,11... | collective-permute-start | bytes 983048 | tf_op jit(solution)/shard_map/ppermute | solution.py:85
  20.0 5.4 %collective-permute-start.5 = (bf16[128,640]{1,0:T(8,128)(2,1)S(1)}, bf16[128,640]{1,0:T(8,128)(2,1)S(1)}, u32[]{:S(2)}, u32[]{:S(2)}) collective-permute-start(bf16[128,640]{1,0:T(8,128)(2,1)S(1)} %slice.80), channel_id=1, source_target_pairs={{0,2},{1,3},{2,0},{3,1},{4,6},{5,7},{6,4},{7,5},{8,10},{9,11},{10,... | collective-permute-start | bytes 491528 | tf_op jit(solution)/shard_map/ppermute | solution.py:83
  23.8 8.8 %collective-permute-start.12 = (bf16[256,640]{1,0:T(8,128)(2,1)S(1)}, bf16[256,640]{1,0:T(8,128)(2,1)S(1)}, u32[]{:S(2)}, u32[]{:S(2)}) collective-permute-start(bf16[256,640]{1,0:T(8,128)(2,1)S(1)} %pad_maximum_fusion.18), channel_id=1, source_target_pairs={{0,2},{1,3},{2,0},{3,1},{4,6},{5,7},{6,4},{7,5},{8,10},{9,11},{10,... | collective-permute-start | bytes 983048 | tf_op jit(solution)/shard_map/ppermute | solution.py:83
  25.4 7.3 %collective-permute-start.6 = (bf16[128,1280]{1,0:T(8,128)(2,1)S(1)}, bf16[128,1280]{1,0:T(8,128)(2,1)S(1)}, u32[]{:S(2)}, u32[]{:S(2)}) collective-permute-start(bf16[128,1280]{1,0:T(8,128)(2,1)S(1)} %pad_maximum_fusion.17), channel_id=1, source_target_pairs={{0,1},{1,0},{2,3},{3,2},{4,5},{5,4},{6,7},{7,6},{8,9},{9,8},{10,11... | collective-permute-start | bytes 983048 | tf_op jit(solution)/shard_map/ppermute | solution.py:85
  26.9 5.9 %collective-permute-start.2 = (bf16[128,1280]{1,0:T(8,128)(2,1)S(1)}, bf16[128,1280]{1,0:T(8,128)(2,1)S(1)}, u32[]{:S(2)}, u32[]{:S(2)}) collective-permute-start(bf16[128,1280]{1,0:T(8,128)(2,1)S(1)} %convolution_convert_fusion.4), channel_id=1, source_target_pairs={{0,1},{1,0},{2,3},{3,2},{4,5},{5,4},{6,7},{7,6},{8,9},{9,8},{10,11... | collective-permute-start | bytes 983048 | tf_op jit(solution)/shard_map/ppermute | solution.py:95
  32.6 4.3 %collective-permute-start.13 = (bf16[256,1280]{1,0:T(8,128)(2,1)S(1)}, bf16[256,1280]{1,0:T(8,128)(2,1)S(1)}, u32[]{:S(2)}, u32[]{:S(2)}) collective-permute-start(bf16[256,1280]{1,0:T(8,128)(2,1)S(1)} %pad_maximum_fusion.7), channel_id=1, source_target_pairs={{0,1},{1,0},{2,3},{3,2},{4,5},{5,4},{6,7},{7,6},{8,9},{9,8},{10,11... | collective-permute-start | bytes 1966088 | tf_op jit(solution)/shard_map/ppermute | solution.py:85
  34.8 1.8 %collective-permute-start.7 = (bf16[128,1280]{1,0:T(8,128)(2,1)S(1)}, bf16[128,1280]{1,0:T(8,128)(2,1)S(1)}, u32[]{:S(2)}, u32[]{:S(2)}) collective-permute-start(bf16[128,1280]{1,0:T(8,128)(2,1)S(1)} %convolution_convert_fusion.2), channel_id=1, source_target_pairs={{0,1},{1,0},{2,3},{3,2},{4,5},{5,4},{6,7},{7,6},{8,9},{9,8},{10,11... | collective-permute-start | bytes 983048 | tf_op jit(solution)/shard_map/ppermute | solution.py:95
  39.6 2.2 %collective-permute-start.14 = (bf16[256,1280]{1,0:T(8,128)(2,1)S(1)}, bf16[256,1280]{1,0:T(8,128)(2,1)S(1)}, u32[]{:S(2)}, u32[]{:S(2)}) collective-permute-start(bf16[256,1280]{1,0:T(8,128)(2,1)S(1)} %convolution_convert_fusion), channel_id=1, source_target_pairs={{0,1},{1,0},{2,3},{3,2},{4,5},{5,4},{6,7},{7,6},{8,9},{9,8},{10,11... | collective-permute-start | bytes 1966088 | tf_op jit(solution)/shard_map/ppermute | solution.py:95
  40.1 7.1 %collective-permute-start.8 = (bf16[128,640]{1,0:T(8,128)(2,1)S(1)}, bf16[128,640]{1,0:T(8,128)(2,1)S(1)}, u32[]{:S(2)}, u32[]{:S(2)}) collective-permute-start(bf16[128,640]{1,0:T(8,128)(2,1)S(1)} %slice.114), channel_id=1, source_target_pairs={{0,2},{1,3},{2,0},{3,1},{4,6},{5,7},{6,4},{7,5},{8,10},{9,11},{10,... | collective-permute-start | bytes 491528 | tf_op jit(solution)/shard_map/ppermute | solution.py:97
  42.4 11.8 %collective-permute-start.15 = (bf16[256,640]{1,0:T(8,128)(2,1)S(1)}, bf16[256,640]{1,0:T(8,128)(2,1)S(1)}, u32[]{:S(2)}, u32[]{:S(2)}) collective-permute-start(bf16[256,640]{1,0:T(8,128)(2,1)S(1)} %slice.113), channel_id=1, source_target_pairs={{0,2},{1,3},{2,0},{3,1},{4,6},{5,7},{6,4},{7,5},{8,10},{9,11},{10,... | collective-permute-start | bytes 983048 | tf_op jit(solution)/shard_map/ppermute | solution.py:97
  43.0 15.5 %collective-permute-start.3 = (bf16[128,640]{1,0:T(8,128)(2,1)S(1)}, bf16[128,640]{1,0:T(8,128)(2,1)S(1)}, u32[]{:S(2)}, u32[]{:S(2)}) collective-permute-start(bf16[128,640]{1,0:T(8,128)(2,1)S(1)} %slice.115), channel_id=1, source_target_pairs={{0,2},{1,3},{2,0},{3,1},{4,6},{5,7},{6,4},{7,5},{8,10},{9,11},{10,... | collective-permute-start | bytes 491528 | tf_op jit(solution)/shard_map/ppermute | solution.py:97
  47.2 11.3 %collective-permute-start.9 = (bf16[128,640]{1,0:T(8,128)(2,1)S(1)}, bf16[128,640]{1,0:T(8,128)(2,1)S(1)}, u32[]{:S(2)}, u32[]{:S(2)}) collective-permute-start(bf16[128,640]{1,0:T(8,128)(2,1)S(1)} %fusion.7), channel_id=1, source_target_pairs={{0,4},{4,0},{8,12},{12,8},{1,5},{5,1},{9,13},{13,9},{2,6},{6,2},{1... | collective-permute-start | bytes 491528 | tf_op jit(solution)/shard_map/ppermute | solution.py:102
  54.3 13.9 %collective-permute-start.16 = (bf16[128,640]{1,0:T(8,128)(2,1)S(1)}, bf16[128,640]{1,0:T(8,128)(2,1)S(1)}, u32[]{:S(2)}, u32[]{:S(2)}) collective-permute-start(bf16[128,640]{1,0:T(8,128)(2,1)S(1)} %get-tuple-element.37), channel_id=1, source_target_pairs={{0,8},{4,12},{8,0},{12,4},{1,9},{5,13},{9,1},{13,5},{2,10},{6,14},... | collective-permute-start | bytes 491528 | tf_op jit(solution)/shard_map/ppermute | solution.py:102
  55.5 12.8 %collective-permute-start.17 = (bf16[128,640]{1,0:T(8,128)(2,1)S(1)}, bf16[128,640]{1,0:T(8,128)(2,1)S(1)}, u32[]{:S(2)}, u32[]{:S(2)}) collective-permute-start(bf16[128,640]{1,0:T(8,128)(2,1)S(1)} %get-tuple-element.38), channel_id=1, source_target_pairs={{0,12},{4,8},{8,4},{12,0},{1,13},{5,9},{9,5},{13,1},{2,14},{6,10},... | collective-permute-start | bytes 491528 | tf_op jit(solution)/shard_map/ppermute | solution.py:102

commit v7 on v6

--- a/solution.py
+++ b/solution.py
@@ -73,7 +73,7 @@
     up_w = _slots(up_weight[0], t, width, 0)
     down_keep = _slots(down_weight[0], t, width, 1, _ORDER[:2])
     down_send = _slots(down_weight[0], t, width, 1, _ORDER[2:])
-    waves = [[0], [1], list(range(2, n_expert))][:max(1, min(3, n_expert))]
+    waves = [[k] for k in range(n_expert)]
     total = None
     previous = None
     for wave in waves:

time: 69.2 us -> 67.7 us (0.978)
  waiting for transfers between devices: 35.6 us -> 31.3 us
  starting transfers between devices: 19.3 us -> 20.7 us
  local copies, waits for them, and re-layouts: 3.69 us -> 4.55 us
    ppermute x3, waiting for transfers between devices: 9.6 us -> 7.69 us  [gathered(): lax.ppermute(block, 'expert', _xor_pairs(n_expert, k))]
    unnamed x2 -> x4, local copies, waits for them, and re-layouts: 0.11 us -> 2.02 us
    ppermute x3 -> x4, waiting for transfers between devices: 6.13 us -> 4.73 us  [gathered(): lax.ppermute(piece, 'tensor', _xor_pairs(n_tensor, 2))]
    ppermute x3 -> x4, starting transfers between devices: 4.2 us -> 5.54 us  [gathered(): lax.ppermute(piece, 'tensor', _xor_pairs(n_tensor, 2))]
    ppermute x3, waiting for transfers between devices: 9.73 us -> 8.65 us  [gathered(): lax.ppermute(part.astype(jnp.bfloat16), 'expert', _xor_pairs(n_expert, k))]
    dynamic_slice x2 -> x3, local copies, waits for them, and re-layouts: 3.42 us -> 2.39 us  [_slots(): lax.dynamic_slice_in_dim(weight, (t ^ k) * width, width, axis=axis)]
    ppermute x3, starting transfers between devices: 6.08 us -> 5.18 us  [gathered(): lax.ppermute(part.astype(jnp.bfloat16), 'expert', _xor_pairs(n_expert, k))]
    ppermute x3 -> x4, starting transfers between devices: 2.77 us -> 3.4 us  [gathered(): lax.ppermute(over_c[:, width:].astype(jnp.bfloat16), 'tensor', _xor_pairs...]
  transfers between devices with their start and end apart: 18 -> 22, of which waited for: 9 -> 10; matrix products, arithmetic and copies ran while one was open for 14% -> 17% of each run, Pallas kernels for 0% -> 0%
where the time goes in v7:
time: 67.7 us; the launch traced here: 67.5 us
  waiting for transfers between devices  31.3 us (46%)
  starting transfers between devices  20.7 us (31%)
  matrix products  6.85 us (10%)
  local copies, waits for them, and re-layouts  4.55 us (7%)
  other arithmetic  3.7 us (5%)
    ppermute x3, waiting for transfers between devices, gathered(): lax.ppermute(part.astype(jnp.bfloat16), 'expert', _xor_pairs(n_expert, k))  8.65 us
    ppermute x3, waiting for transfers between devices, gathered(): lax.ppermute(block, 'expert', _xor_pairs(n_expert, k))  7.69 us
    ppermute x4, waiting for transfers between devices, gathered(): lax.ppermute(over_c[:, width:].astype(jnp.bfloat16), 'tensor', _xor_pairs...  7.27 us
    ppermute x4, starting transfers between devices, gathered(): lax.ppermute(piece, 'tensor', _xor_pairs(n_tensor, 2))  5.54 us
    ppermute x3, starting transfers between devices, gathered(): lax.ppermute(part.astype(jnp.bfloat16), 'expert', _xor_pairs(n_expert, k))  5.18 us
    ppermute x4, waiting for transfers between devices, gathered(): lax.ppermute(piece, 'tensor', _xor_pairs(n_tensor, 2))  4.73 us
    ppermute x3, starting transfers between devices, gathered(): lax.ppermute(block, 'expert', _xor_pairs(n_expert, k))  4.45 us
    ppermute x4, starting transfers between devices, gathered(): lax.ppermute(over_c[:, width:].astype(jnp.bfloat16), 'tensor', _xor_pairs...  3.4 us
  transfers between devices with their start and end apart: 22, of which 10 were waited for; matrix products, arithmetic and copies ran while one was open for 17% of the time, Pallas kernels for 0%

profile of v7, /device:TPU:0, one launch (start us, length us, event | category | flops | bytes accessed | tf_op | source)
XLA Modules:
  0.0 67.5 jit_solution(3587203329574613531)
XLA Ops:
  0.0 1.0 %multiply_convert_fusion = bf16[128,640]{1,0:T(8,128)(2,1)S(1)} fusion(bf16[128,640]{1,0:T(8,128)(2,1)} %param.8, f32[128]{0:T(128)} %param.9), kind=kLoop, calls=%fused_computation.63 | loop fusion | flops 245760 | bytes 328192 | tf_op jit(solution)/shard_map/convert_element_type | solution.py:65
  1.0 3.0 %collective-permute-start = (bf16[128,640]{1,0:T(8,128)(2,1)S(1)}, bf16[128,640]{1,0:T(8,128)(2,1)S(1)}, u32[]{:S(2)}, u32[]{:S(2)}) collective-permute-start(bf16[128,640]{1,0:T(8,128)(2,1)S(1)} %multiply_convert_fusion), channel_id=1, source_target_pairs={{0,2},{1,3},{2,0},{3,1},{4,6},{5,7},{6,4},{7,5},{8,10},{9,11},{10,... | collective-permute-start | bytes 491528 | tf_op jit(solution)/shard_map/ppermute | solution.py:83
  4.0 0.7 convert_bitcast_fusion
  4.7 1.6 %collective-permute-start.4 = (bf16[144,640]{1,0:T(8,128)(2,1)S(1)}, bf16[144,640]{1,0:T(8,128)(2,1)S(1)}, u32[]{:S(2)}, u32[]{:S(2)}) collective-permute-start(bf16[144,640]{1,0:T(8,128)(2,1)S(1)} %fusion.17), channel_id=1, source_target_pairs={{0,4},{4,0},{8,12},{12,8},{1,5},{5,1},{9,13},{13,9},{2,6},{6,2},{1... | collective-permute-start | bytes 552968 | tf_op jit(solution)/shard_map/ppermute | solution.py:70
  6.3 2.6 %collective-permute-start.10 = (bf16[144,640]{1,0:T(8,128)(2,1)S(1)}, bf16[144,640]{1,0:T(8,128)(2,1)S(1)}, u32[]{:S(2)}, u32[]{:S(2)}) collective-permute-start(bf16[144,640]{1,0:T(8,128)(2,1)S(1)} %fusion.17), channel_id=1, source_target_pairs={{0,8},{4,12},{8,0},{12,4},{1,9},{5,13},{9,1},{13,5},{2,10},{6,14},... | collective-permute-start | bytes 552968 | tf_op jit(solution)/shard_map/ppermute | solution.py:70
  9.2 0.7 compare_bitcast_fusion
  9.8 2.0 %dynamic-slice_bitcast_fusion.11 = (bf16[640,512]{1,0:T(8,128)(2,1)S(1)}, bf16[640,512]{1,0:T(8,128)(2,1)S(1)}, bf16[640,512]{1,0:T(8,128)(2,1)S(1)}, bf16[640,512]{1,0:T(8,128)(2,1)S(1)}) fusion(bf16[1,2560,512]{2,1,0:T(8,128)(2,1)} %param.11, s32[]{:T(128)S(6)} %select_n.39, s32[]{:T(128)S(6)} %select_n.40, s32[]{:T(128)S(6)} %select_n.42, s32[]{:T(128)S(6)} %select_n.41), kind=kLoop, calls=%fused_computation.41 | loop fusion | bytes 5242896 | tf_op jit(solution)/shard_map/dynamic_slice | solution.py:55
  11.8 0.5 copy-done
  12.8 1.5 %copy-done.1 = bf16[1,512,2560]{2,1,0:T(8,128)(2,1)S(1)} copy-done((bf16[1,512,2560]{2,1,0:T(8,128)(2,1)S(1)}, bf16[1,512,2560]{2,1,0:T(8,128)(2,1)}, u32[]{:S(2)}) %copy-start.1) | copy-done | bytes 2621464
  14.7 0.4 collective-permute-start.5
  15.0 7.7 %collective-permute-done.10 = bf16[144,640]{1,0:T(8,128)(2,1)S(1)} collective-permute-done((bf16[144,640]{1,0:T(8,128)(2,1)S(1)}, bf16[144,640]{1,0:T(8,128)(2,1)S(1)}, u32[]{:S(2)}, u32[]{:S(2)}) %collective-permute-start.10) | collective-permute-done | bytes 184352 | tf_op jit(solution)/shard_map/ppermute | solution.py:70
  22.7 0.6 collective-permute-start.11
  23.4 1.6 %collective-permute-start.17 = (bf16[128,640]{1,0:T(8,128)(2,1)S(1)}, bf16[128,640]{1,0:T(8,128)(2,1)S(1)}, u32[]{:S(2)}, u32[]{:S(2)}) collective-permute-start(bf16[128,640]{1,0:T(8,128)(2,1)S(1)} %slice.87), channel_id=1, source_target_pairs={{0,2},{1,3},{2,0},{3,1},{4,6},{5,7},{6,4},{7,5},{8,10},{9,11},{10,... | collective-permute-start | bytes 491528 | tf_op jit(solution)/shard_map/ppermute | solution.py:83
  25.0 3.1 %collective-permute-done.11 = bf16[128,640]{1,0:T(8,128)(2,1)S(1)} collective-permute-done((bf16[128,640]{1,0:T(8,128)(2,1)S(1)}, bf16[128,640]{1,0:T(8,128)(2,1)S(1)}, u32[]{:S(2)}, u32[]{:S(2)}) %collective-permute-start.11) | collective-permute-done | bytes 163872 | tf_op jit(solution)/shard_map/ppermute | solution.py:83
  28.2 1.6 %collective-permute-done.17 = bf16[128,640]{1,0:T(8,128)(2,1)S(1)} collective-permute-done((bf16[128,640]{1,0:T(8,128)(2,1)S(1)}, bf16[128,640]{1,0:T(8,128)(2,1)S(1)}, u32[]{:S(2)}, u32[]{:S(2)}) %collective-permute-start.17) | collective-permute-done | bytes 163872 | tf_op jit(solution)/shard_map/ppermute | solution.py:83
  30.0 0.5 fusion.16
  30.5 0.5 select_convert_fusion
  31.0 0.3 convolution_convert_fusion.6
  31.4 0.6 collective-permute-start.2
  32.0 1.2 %collective-permute-done.2 = bf16[128,1280]{1,0:T(8,128)(2,1)S(1)} collective-permute-done((bf16[128,1280]{1,0:T(8,128)(2,1)S(1)}, bf16[128,1280]{1,0:T(8,128)(2,1)S(1)}, u32[]{:S(2)}, u32[]{:S(2)}) %collective-permute-start.2) | collective-permute-done | bytes 327712 | tf_op jit(solution)/shard_map/ppermute | solution.py:95
  33.2 0.3 convert_add_fusion.3
  33.6 0.5 fusion.20
  34.1 0.5 fusion.4
  34.6 0.3 convolution_convert_fusion.4
  35.0 0.4 collective-permute-start.7
  35.5 1.2 %collective-permute-done.7 = bf16[128,1280]{1,0:T(8,128)(2,1)S(1)} collective-permute-done((bf16[128,1280]{1,0:T(8,128)(2,1)S(1)}, bf16[128,1280]{1,0:T(8,128)(2,1)S(1)}, u32[]{:S(2)}, u32[]{:S(2)}) %collective-permute-start.7) | collective-permute-done | bytes 327712 | tf_op jit(solution)/shard_map/ppermute | solution.py:95
  37.0 0.5 fusion.21
  37.5 0.5 fusion.5
  38.1 0.3 convolution_convert_fusion.2
  38.4 0.4 collective-permute-start.13
  38.9 0.6 collective-permute-start.8
  39.5 0.6 collective-permute-done.13
  40.1 0.3 convert_add_fusion.1
  40.5 0.5 fusion.22
  41.0 0.5 fusion.6
  41.5 0.3 convolution_convert_fusion
  41.9 0.4 collective-permute-start.19
  42.3 0.6 collective-permute-start.3
  43.0 2.3 %collective-permute-done.8 = bf16[128,640]{1,0:T(8,128)(2,1)S(1)} collective-permute-done((bf16[128,640]{1,0:T(8,128)(2,1)S(1)}, bf16[128,640]{1,0:T(8,128)(2,1)S(1)}, u32[]{:S(2)}, u32[]{:S(2)}) %collective-permute-start.8) | collective-permute-done | bytes 163872 | tf_op jit(solution)/shard_map/ppermute | solution.py:97
  45.3 1.2 %collective-permute-start.9 = (bf16[128,640]{1,0:T(8,128)(2,1)S(1)}, bf16[128,640]{1,0:T(8,128)(2,1)S(1)}, u32[]{:S(2)}, u32[]{:S(2)}) collective-permute-start(bf16[128,640]{1,0:T(8,128)(2,1)S(1)} %fusion.10), channel_id=1, source_target_pairs={{0,4},{4,0},{8,12},{12,8},{1,5},{5,1},{9,13},{13,9},{2,6},{6,2},{1... | collective-permute-start | bytes 491528 | tf_op jit(solution)/shard_map/ppermute | solution.py:102
  46.6 0.6 collective-permute-start.14
  47.1 0.3 convert_add_fusion
  47.5 1.6 %collective-permute-start.20 = (bf16[128,640]{1,0:T(8,128)(2,1)S(1)}, bf16[128,640]{1,0:T(8,128)(2,1)S(1)}, u32[]{:S(2)}, u32[]{:S(2)}) collective-permute-start(bf16[128,640]{1,0:T(8,128)(2,1)S(1)} %slice.116), channel_id=1, source_target_pairs={{0,2},{1,3},{2,0},{3,1},{4,6},{5,7},{6,4},{7,5},{8,10},{9,11},{10,... | collective-permute-start | bytes 491528 | tf_op jit(solution)/shard_map/ppermute | solution.py:97
  49.1 4.7 %collective-permute-done.14 = bf16[128,640]{1,0:T(8,128)(2,1)S(1)} collective-permute-done((bf16[128,640]{1,0:T(8,128)(2,1)S(1)}, bf16[128,640]{1,0:T(8,128)(2,1)S(1)}, u32[]{:S(2)}, u32[]{:S(2)}) %collective-permute-start.14) | collective-permute-done | bytes 163872 | tf_op jit(solution)/shard_map/ppermute | solution.py:97
  53.8 1.7 %collective-permute-start.15 = (bf16[128,640]{1,0:T(8,128)(2,1)S(1)}, bf16[128,640]{1,0:T(8,128)(2,1)S(1)}, u32[]{:S(2)}, u32[]{:S(2)}) collective-permute-start(bf16[128,640]{1,0:T(8,128)(2,1)S(1)} %fusion.9), channel_id=1, source_target_pairs={{0,8},{4,12},{8,0},{12,4},{1,9},{5,13},{9,1},{13,5},{2,10},{6,14},... | collective-permute-start | bytes 491528 | tf_op jit(solution)/shard_map/ppermute | solution.py:102
  55.8 2.3 %collective-permute-start.21 = (bf16[128,640]{1,0:T(8,128)(2,1)S(1)}, bf16[128,640]{1,0:T(8,128)(2,1)S(1)}, u32[]{:S(2)}, u32[]{:S(2)}) collective-permute-start(bf16[128,640]{1,0:T(8,128)(2,1)S(1)} %fusion.8), channel_id=1, source_target_pairs={{0,12},{4,8},{8,4},{12,0},{1,13},{5,9},{9,5},{13,1},{2,14},{6,10},... | collective-permute-start | bytes 491528 | tf_op jit(solution)/shard_map/ppermute | solution.py:102
  58.1 8.6 %collective-permute-done.15 = bf16[128,640]{1,0:T(8,128)(2,1)S(1)} collective-permute-done((bf16[128,640]{1,0:T(8,128)(2,1)S(1)}, bf16[128,640]{1,0:T(8,128)(2,1)S(1)}, u32[]{:S(2)}, u32[]{:S(2)}) %collective-permute-start.15) | collective-permute-done | bytes 163872 | tf_op jit(solution)/shard_map/ppermute | solution.py:102
  66.7 0.8 %fusion.14 = bf16[128,640]{1,0:T(8,128)(2,1)} fusion(f32[128,1280]{1,0:T(8,128)S(1)} %convert_add_fusion.3, bf16[128,640]{1,0:T(8,128)(2,1)S(1)} %collective-permute-done.21, bf16[128,640]{1,0:T(8,128)(2,1)S(1)} %collective-permute-done.15, bf16[128,640]{1,0:T(8,128)(2,1)S(1)} %collective-permute-done.9, bf16[128,640]{1,0:T(8,128)(2,1)S(1)} %collective-permute-done.3), kind=kLoop, calls=%fused_computation.58 | loop fusion | flops 737280 | bytes 1146880 | tf_op jit(solution)/shard_map/convert_element_type | solution.py:105
  (48 shorter events, 2.3 us)
Async XLA Ops:
  1.0 13.5 %collective-permute-start = (bf16[128,640]{1,0:T(8,128)(2,1)S(1)}, bf16[128,640]{1,0:T(8,128)(2,1)S(1)}, u32[]{:S(2)}, u32[]{:S(2)}) collective-permute-start(bf16[128,640]{1,0:T(8,128)(2,1)S(1)} %multiply_convert_fusion), channel_id=1, source_target_pairs={{0,2},{1,3},{2,0},{3,1},{4,6},{5,7},{6,4},{7,5},{8,10},{9,11},{10,... | collective-permute-start | bytes 491528 | tf_op jit(solution)/shard_map/ppermute | solution.py:83
  4.7 9.9 %collective-permute-start.4 = (bf16[144,640]{1,0:T(8,128)(2,1)S(1)}, bf16[144,640]{1,0:T(8,128)(2,1)S(1)}, u32[]{:S(2)}, u32[]{:S(2)}) collective-permute-start(bf16[144,640]{1,0:T(8,128)(2,1)S(1)} %fusion.17), channel_id=1, source_target_pairs={{0,4},{4,0},{8,12},{12,8},{1,5},{5,1},{9,13},{13,9},{2,6},{6,2},{1... | collective-permute-start | bytes 552968 | tf_op jit(solution)/shard_map/ppermute | solution.py:70
  6.3 16.4 %collective-permute-start.10 = (bf16[144,640]{1,0:T(8,128)(2,1)S(1)}, bf16[144,640]{1,0:T(8,128)(2,1)S(1)}, u32[]{:S(2)}, u32[]{:S(2)}) collective-permute-start(bf16[144,640]{1,0:T(8,128)(2,1)S(1)} %fusion.17), channel_id=1, source_target_pairs={{0,8},{4,12},{8,0},{12,4},{1,9},{5,13},{9,1},{13,5},{2,10},{6,14},... | collective-permute-start | bytes 552968 | tf_op jit(solution)/shard_map/ppermute | solution.py:70
  8.9 14.4 %collective-permute-start.16 = (bf16[144,640]{1,0:T(8,128)(2,1)S(1)}, bf16[144,640]{1,0:T(8,128)(2,1)S(1)}, u32[]{:S(2)}, u32[]{:S(2)}) collective-permute-start(bf16[144,640]{1,0:T(8,128)(2,1)S(1)} %fusion.17), channel_id=1, source_target_pairs={{0,12},{4,8},{8,4},{12,0},{1,13},{5,9},{9,5},{13,1},{2,14},{6,10},... | collective-permute-start | bytes 552968 | tf_op jit(solution)/shard_map/ppermute | solution.py:70
  9.8 2.5 %copy-start = (bf16[1,2560,512]{2,1,0:T(8,128)(2,1)S(1)}, bf16[1,2560,512]{2,1,0:T(8,128)(2,1)}, u32[]{:S(2)}) copy-start(bf16[1,2560,512]{2,1,0:T(8,128)(2,1)} %param.12) | copy-start | bytes 7864324
  12.5 1.7 %copy-start.1 = (bf16[1,512,2560]{2,1,0:T(8,128)(2,1)S(1)}, bf16[1,512,2560]{2,1,0:T(8,128)(2,1)}, u32[]{:S(2)}) copy-start(bf16[1,512,2560]{2,1,0:T(8,128)(2,1)} %param.13) | copy-start | bytes 7864324
  14.5 15.5 %collective-permute-start.1 = (bf16[128,1280]{1,0:T(8,128)(2,1)S(1)}, bf16[128,1280]{1,0:T(8,128)(2,1)S(1)}, u32[]{:S(2)}, u32[]{:S(2)}) collective-permute-start(bf16[128,1280]{1,0:T(8,128)(2,1)S(1)} %pad_maximum_fusion.8), channel_id=1, source_target_pairs={{0,1},{1,0},{2,3},{3,2},{4,5},{5,4},{6,7},{7,6},{8,9},{9,8},{10,11... | collective-permute-start | bytes 983048 | tf_op jit(solution)/shard_map/ppermute | solution.py:85
  14.7 10.3 %collective-permute-start.5 = (bf16[128,640]{1,0:T(8,128)(2,1)S(1)}, bf16[128,640]{1,0:T(8,128)(2,1)S(1)}, u32[]{:S(2)}, u32[]{:S(2)}) collective-permute-start(bf16[128,640]{1,0:T(8,128)(2,1)S(1)} %slice.79), channel_id=1, source_target_pairs={{0,2},{1,3},{2,0},{3,1},{4,6},{5,7},{6,4},{7,5},{8,10},{9,11},{10,... | collective-permute-start | bytes 491528 | tf_op jit(solution)/shard_map/ppermute | solution.py:83
  22.7 5.4 %collective-permute-start.11 = (bf16[128,640]{1,0:T(8,128)(2,1)S(1)}, bf16[128,640]{1,0:T(8,128)(2,1)S(1)}, u32[]{:S(2)}, u32[]{:S(2)}) collective-permute-start(bf16[128,640]{1,0:T(8,128)(2,1)S(1)} %slice.83), channel_id=1, source_target_pairs={{0,2},{1,3},{2,0},{3,1},{4,6},{5,7},{6,4},{7,5},{8,10},{9,11},{10,... | collective-permute-start | bytes 491528 | tf_op jit(solution)/shard_map/ppermute | solution.py:83
  23.4 6.5 %collective-permute-start.17 = (bf16[128,640]{1,0:T(8,128)(2,1)S(1)}, bf16[128,640]{1,0:T(8,128)(2,1)S(1)}, u32[]{:S(2)}, u32[]{:S(2)}) collective-permute-start(bf16[128,640]{1,0:T(8,128)(2,1)S(1)} %slice.87), channel_id=1, source_target_pairs={{0,2},{1,3},{2,0},{3,1},{4,6},{5,7},{6,4},{7,5},{8,10},{9,11},{10,... | collective-permute-start | bytes 491528 | tf_op jit(solution)/shard_map/ppermute | solution.py:83
  25.0 7.0 %collective-permute-start.6 = (bf16[128,1280]{1,0:T(8,128)(2,1)S(1)}, bf16[128,1280]{1,0:T(8,128)(2,1)S(1)}, u32[]{:S(2)}, u32[]{:S(2)}) collective-permute-start(bf16[128,1280]{1,0:T(8,128)(2,1)S(1)} %pad_maximum_fusion.9), channel_id=1, source_target_pairs={{0,1},{1,0},{2,3},{3,2},{4,5},{5,4},{6,7},{7,6},{8,9},{9,8},{10,11... | collective-permute-start | bytes 983048 | tf_op jit(solution)/shard_map/ppermute | solution.py:85
  28.2 7.3 %collective-permute-start.12 = (bf16[128,1280]{1,0:T(8,128)(2,1)S(1)}, bf16[128,1280]{1,0:T(8,128)(2,1)S(1)}, u32[]{:S(2)}, u32[]{:S(2)}) collective-permute-start(bf16[128,1280]{1,0:T(8,128)(2,1)S(1)} %pad_maximum_fusion.10), channel_id=1, source_target_pairs={{0,1},{1,0},{2,3},{3,2},{4,5},{5,4},{6,7},{7,6},{8,9},{9,8},{10,11... | collective-permute-start | bytes 983048 | tf_op jit(solution)/shard_map/ppermute | solution.py:85
  29.9 8.9 %collective-permute-start.18 = (bf16[128,1280]{1,0:T(8,128)(2,1)S(1)}, bf16[128,1280]{1,0:T(8,128)(2,1)S(1)}, u32[]{:S(2)}, u32[]{:S(2)}) collective-permute-start(bf16[128,1280]{1,0:T(8,128)(2,1)S(1)} %pad_maximum_fusion.11), channel_id=1, source_target_pairs={{0,1},{1,0},{2,3},{3,2},{4,5},{5,4},{6,7},{7,6},{8,9},{9,8},{10,11... | collective-permute-start | bytes 983048 | tf_op jit(solution)/shard_map/ppermute | solution.py:85
  31.4 1.8 %collective-permute-start.2 = (bf16[128,1280]{1,0:T(8,128)(2,1)S(1)}, bf16[128,1280]{1,0:T(8,128)(2,1)S(1)}, u32[]{:S(2)}, u32[]{:S(2)}) collective-permute-start(bf16[128,1280]{1,0:T(8,128)(2,1)S(1)} %convolution_convert_fusion.6), channel_id=1, source_target_pairs={{0,1},{1,0},{2,3},{3,2},{4,5},{5,4},{6,7},{7,6},{8,9},{9,8},{10,11... | collective-permute-start | bytes 983048 | tf_op jit(solution)/shard_map/ppermute | solution.py:95
  35.0 1.7 %collective-permute-start.7 = (bf16[128,1280]{1,0:T(8,128)(2,1)S(1)}, bf16[128,1280]{1,0:T(8,128)(2,1)S(1)}, u32[]{:S(2)}, u32[]{:S(2)}) collective-permute-start(bf16[128,1280]{1,0:T(8,128)(2,1)S(1)} %convolution_convert_fusion.4), channel_id=1, source_target_pairs={{0,1},{1,0},{2,3},{3,2},{4,5},{5,4},{6,7},{7,6},{8,9},{9,8},{10,11... | collective-permute-start | bytes 983048 | tf_op jit(solution)/shard_map/ppermute | solution.py:95
  38.4 1.7 %collective-permute-start.13 = (bf16[128,1280]{1,0:T(8,128)(2,1)S(1)}, bf16[128,1280]{1,0:T(8,128)(2,1)S(1)}, u32[]{:S(2)}, u32[]{:S(2)}) collective-permute-start(bf16[128,1280]{1,0:T(8,128)(2,1)S(1)} %convolution_convert_fusion.2), channel_id=1, source_target_pairs={{0,1},{1,0},{2,3},{3,2},{4,5},{5,4},{6,7},{7,6},{8,9},{9,8},{10,11... | collective-permute-start | bytes 983048 | tf_op jit(solution)/shard_map/ppermute | solution.py:95
  38.9 6.4 %collective-permute-start.8 = (bf16[128,640]{1,0:T(8,128)(2,1)S(1)}, bf16[128,640]{1,0:T(8,128)(2,1)S(1)}, u32[]{:S(2)}, u32[]{:S(2)}) collective-permute-start(bf16[128,640]{1,0:T(8,128)(2,1)S(1)} %slice.118), channel_id=1, source_target_pairs={{0,2},{1,3},{2,0},{3,1},{4,6},{5,7},{6,4},{7,5},{8,10},{9,11},{10,... | collective-permute-start | bytes 491528 | tf_op jit(solution)/shard_map/ppermute | solution.py:97
  41.9 5.3 %collective-permute-start.19 = (bf16[128,1280]{1,0:T(8,128)(2,1)S(1)}, bf16[128,1280]{1,0:T(8,128)(2,1)S(1)}, u32[]{:S(2)}, u32[]{:S(2)}) collective-permute-start(bf16[128,1280]{1,0:T(8,128)(2,1)S(1)} %convolution_convert_fusion), channel_id=1, source_target_pairs={{0,1},{1,0},{2,3},{3,2},{4,5},{5,4},{6,7},{7,6},{8,9},{9,8},{10,11... | collective-permute-start | bytes 983048 | tf_op jit(solution)/shard_map/ppermute | solution.py:95
  42.3 15.8 %collective-permute-start.3 = (bf16[128,640]{1,0:T(8,128)(2,1)S(1)}, bf16[128,640]{1,0:T(8,128)(2,1)S(1)}, u32[]{:S(2)}, u32[]{:S(2)}) collective-permute-start(bf16[128,640]{1,0:T(8,128)(2,1)S(1)} %slice.119), channel_id=1, source_target_pairs={{0,2},{1,3},{2,0},{3,1},{4,6},{5,7},{6,4},{7,5},{8,10},{9,11},{10,... | collective-permute-start | bytes 491528 | tf_op jit(solution)/shard_map/ppermute | solution.py:97
  45.3 12.8 %collective-permute-start.9 = (bf16[128,640]{1,0:T(8,128)(2,1)S(1)}, bf16[128,640]{1,0:T(8,128)(2,1)S(1)}, u32[]{:S(2)}, u32[]{:S(2)}) collective-permute-start(bf16[128,640]{1,0:T(8,128)(2,1)S(1)} %fusion.10), channel_id=1, source_target_pairs={{0,4},{4,0},{8,12},{12,8},{1,5},{5,1},{9,13},{13,9},{2,6},{6,2},{1... | collective-permute-start | bytes 491528 | tf_op jit(solution)/shard_map/ppermute | solution.py:102
  46.6 7.2 %collective-permute-start.14 = (bf16[128,640]{1,0:T(8,128)(2,1)S(1)}, bf16[128,640]{1,0:T(8,128)(2,1)S(1)}, u32[]{:S(2)}, u32[]{:S(2)}) collective-permute-start(bf16[128,640]{1,0:T(8,128)(2,1)S(1)} %slice.117), channel_id=1, source_target_pairs={{0,2},{1,3},{2,0},{3,1},{4,6},{5,7},{6,4},{7,5},{8,10},{9,11},{10,... | collective-permute-start | bytes 491528 | tf_op jit(solution)/shard_map/ppermute | solution.py:97
  47.5 8.3 %collective-permute-start.20 = (bf16[128,640]{1,0:T(8,128)(2,1)S(1)}, bf16[128,640]{1,0:T(8,128)(2,1)S(1)}, u32[]{:S(2)}, u32[]{:S(2)}) collective-permute-start(bf16[128,640]{1,0:T(8,128)(2,1)S(1)} %slice.116), channel_id=1, source_target_pairs={{0,2},{1,3},{2,0},{3,1},{4,6},{5,7},{6,4},{7,5},{8,10},{9,11},{10,... | collective-permute-start | bytes 491528 | tf_op jit(solution)/shard_map/ppermute | solution.py:97
  53.8 12.9 %collective-permute-start.15 = (bf16[128,640]{1,0:T(8,128)(2,1)S(1)}, bf16[128,640]{1,0:T(8,128)(2,1)S(1)}, u32[]{:S(2)}, u32[]{:S(2)}) collective-permute-start(bf16[128,640]{1,0:T(8,128)(2,1)S(1)} %fusion.9), channel_id=1, source_target_pairs={{0,8},{4,12},{8,0},{12,4},{1,9},{5,13},{9,1},{13,5},{2,10},{6,14},... | collective-permute-start | bytes 491528 | tf_op jit(solution)/shard_map/ppermute | solution.py:102
  55.8 10.9 %collective-permute-start.21 = (bf16[128,640]{1,0:T(8,128)(2,1)S(1)}, bf16[128,640]{1,0:T(8,128)(2,1)S(1)}, u32[]{:S(2)}, u32[]{:S(2)}) collective-permute-start(bf16[128,640]{1,0:T(8,128)(2,1)S(1)} %fusion.8), channel_id=1, source_target_pairs={{0,12},{4,8},{8,4},{12,0},{1,13},{5,9},{9,5},{13,1},{2,14},{6,10},... | collective-permute-start | bytes 491528 | tf_op jit(solution)/shard_map/ppermute | solution.py:102

commit v8 on v7

--- a/solution.py
+++ b/solution.py
@@ -61,14 +61,11 @@
     n_tensor = lax.axis_size("tensor")
     me = lax.axis_index("expert")
     t = lax.axis_index("tensor")
-    expert = (me // SPAN).astype(jnp.bfloat16)
     scaled = (tokens.astype(jnp.float32) * route_scale[:, None]).astype(jnp.bfloat16)
-    id_rows = jnp.zeros((16, width), jnp.bfloat16)
-    id_rows = id_rows.at[0, :tok_rows].set(expert_ids[:, 0].astype(jnp.bfloat16))
-    block = jnp.concatenate([scaled, id_rows], axis=0)
-    blocks = [block] + [
-        lax.ppermute(block, "expert", _xor_pairs(n_expert, k)) for k in range(1, n_expert)
+    blocks = [scaled] + [
+        lax.ppermute(scaled, "expert", _xor_pairs(n_expert, k)) for k in range(1, n_expert)
     ]
+    routed = expert_ids[:, 0][:, None]
     gate_w = _slots(gate_weight[0], t, width, 0)
     up_w = _slots(up_weight[0], t, width, 0)
     down_keep = _slots(down_weight[0], t, width, 1, _ORDER[:2])
@@ -77,18 +74,16 @@
     total = None
     previous = None
     for wave in waves:
-        routed = jnp.concatenate([blocks[k][tok_rows, :tok_rows] for k in wave])
-        piece = jnp.concatenate([blocks[k][:tok_rows] for k in wave])
+        piece = jnp.concatenate([blocks[k] for k in wave])
         pair = jnp.concatenate(
             [piece, lax.ppermute(piece, "tensor", _xor_pairs(n_tensor, 2))], axis=1)
         rows = jnp.concatenate(
             [pair, lax.ppermute(pair, "tensor", _xor_pairs(n_tensor, 1))], axis=1)
         if previous is not None:
-            rows, routed, _ = lax.optimization_barrier((rows, routed, previous))
+            rows, _ = lax.optimization_barrier((rows, previous))
         gate_act = jnp.dot(rows, gate_w, preferred_element_type=jnp.float32)
         up_act = jnp.dot(rows, up_w, preferred_element_type=jnp.float32)
-        mine = (routed == expert)[:, None]
-        hidden = jnp.where(mine, jax.nn.silu(gate_act) * up_act, 0.0).astype(jnp.bfloat16)
+        hidden = (jax.nn.silu(gate_act) * up_act).astype(jnp.bfloat16)
         keep = jnp.dot(hidden, down_keep, preferred_element_type=jnp.float32).astype(jnp.bfloat16)
         send = jnp.dot(hidden, down_send, preferred_element_type=jnp.float32).astype(jnp.bfloat16)
         previous = keep
@@ -101,6 +96,7 @@
             if k:
                 part = lax.ppermute(
                     part.astype(jnp.bfloat16), "expert", _xor_pairs(n_expert, k)).astype(jnp.float32)
+            part = jnp.where(routed == (me ^ k) // SPAN, part, 0.0)
             total = part if total is None else total + part
     return total.astype(jnp.bfloat16)
 

time: 67.7 us -> 67.3 us (level)
  waiting for transfers between devices: 31.3 us -> 28.8 us
  matrix products: 6.85 us -> 9.28 us
  other arithmetic: 3.7 us -> 2.46 us
    ppermute x4, waiting for transfers between devices: 7.27 us -> 5.65 us  [gathered(): lax.ppermute(over_c[:, width:].astype(jnp.bfloat16), 'tensor', _xor_pairs...]
    dot_general x4, matrix products: 1.39 us -> 2.44 us  [gathered(): jnp.dot(hidden, down_keep, preferred_element_type=jnp.float32)]
    dot_general x4, matrix products: 1.4 us -> 2.12 us  [gathered(): jnp.dot(hidden, down_send, preferred_element_type=jnp.float32)]
    unnamed x4 -> x8, local copies, waits for them, and re-layouts: 2.02 us -> 2.04 us
  transfers between devices with their start and end apart: 22 -> 22, of which waited for: 10 -> 9; matrix products, arithmetic and copies ran while one was open for 17% -> 19% of each run, Pallas kernels for 0% -> 0%
where the time goes in v8:
time: 67.3 us; the launch traced here: 66.8 us
  waiting for transfers between devices  28.8 us (43%)
  starting transfers between devices  20.8 us (31%)
  matrix products  9.28 us (14%)
  local copies, waits for them, and re-layouts  5.18 us (8%)
  other arithmetic  2.46 us (4%)
    ppermute x3, waiting for transfers between devices, gathered(): lax.ppermute(part.astype(jnp.bfloat16), 'expert', _xor_pairs(n_expert, k))  8.84 us
    ppermute x3, waiting for transfers between devices, gathered(): lax.ppermute(scaled, 'expert', _xor_pairs(n_expert, k))  7.07 us
    ppermute x4, waiting for transfers between devices, gathered(): lax.ppermute(over_c[:, width:].astype(jnp.bfloat16), 'tensor', _xor_pairs...  5.65 us
    ppermute x4, starting transfers between devices, gathered(): lax.ppermute(piece, 'tensor', _xor_pairs(n_tensor, 2))  5.41 us
    ppermute x3, starting transfers between devices, gathered(): lax.ppermute(part.astype(jnp.bfloat16), 'expert', _xor_pairs(n_expert, k))  5.02 us
    ppermute x4, waiting for transfers between devices, gathered(): lax.ppermute(piece, 'tensor', _xor_pairs(n_tensor, 2))  4.83 us
    ppermute x3, starting transfers between devices, gathered(): lax.ppermute(scaled, 'expert', _xor_pairs(n_expert, k))  4.39 us
    ppermute x4, starting transfers between devices, gathered(): lax.ppermute(over_c[:, width:].astype(jnp.bfloat16), 'tensor', _xor_pairs...  3.91 us
  transfers between devices with their start and end apart: 22, of which 9 were waited for; matrix products, arithmetic and copies ran while one was open for 19% of the time, Pallas kernels for 0%

profile of v8, /device:TPU:0, one launch (start us, length us, event | category | flops | bytes accessed | tf_op | source)
XLA Modules:
  0.0 66.8 jit_solution(2318922312819624135)
XLA Ops:
  0.0 1.0 %multiply_convert_fusion = bf16[128,640]{1,0:T(8,128)(2,1)S(1)} fusion(bf16[128,640]{1,0:T(8,128)(2,1)} %param.6, f32[128]{0:T(128)} %param.7), kind=kLoop, calls=%fused_computation.59 | loop fusion | flops 245760 | bytes 328192 | tf_op jit(solution)/shard_map/convert_element_type | solution.py:64
  1.0 3.0 %collective-permute-start = (bf16[128,640]{1,0:T(8,128)(2,1)S(1)}, bf16[128,640]{1,0:T(8,128)(2,1)S(1)}, u32[]{:S(2)}, u32[]{:S(2)}) collective-permute-start(bf16[128,640]{1,0:T(8,128)(2,1)S(1)} %multiply_convert_fusion), channel_id=1, source_target_pairs={{0,2},{1,3},{2,0},{3,1},{4,6},{5,7},{6,4},{7,5},{8,10},{9,11},{10,... | collective-permute-start | bytes 491528 | tf_op jit(solution)/shard_map/ppermute | solution.py:79
  4.0 1.6 %collective-permute-start.4 = (bf16[128,640]{1,0:T(8,128)(2,1)S(1)}, bf16[128,640]{1,0:T(8,128)(2,1)S(1)}, u32[]{:S(2)}, u32[]{:S(2)}) collective-permute-start(bf16[128,640]{1,0:T(8,128)(2,1)S(1)} %multiply_convert_fusion), channel_id=1, source_target_pairs={{0,4},{4,0},{8,12},{12,8},{1,5},{5,1},{9,13},{13,9},{2,6},{6,2},{1... | collective-permute-start | bytes 491528 | tf_op jit(solution)/shard_map/ppermute | solution.py:66
  5.6 2.6 %collective-permute-start.10 = (bf16[128,640]{1,0:T(8,128)(2,1)S(1)}, bf16[128,640]{1,0:T(8,128)(2,1)S(1)}, u32[]{:S(2)}, u32[]{:S(2)}) collective-permute-start(bf16[128,640]{1,0:T(8,128)(2,1)S(1)} %multiply_convert_fusion), channel_id=1, source_target_pairs={{0,8},{4,12},{8,0},{12,4},{1,9},{5,13},{9,1},{13,5},{2,10},{6,14},... | collective-permute-start | bytes 491528 | tf_op jit(solution)/shard_map/ppermute | solution.py:66
  8.4 2.0 %dynamic-slice_bitcast_fusion.11 = (bf16[640,512]{1,0:T(8,128)(2,1)S(1)}, bf16[640,512]{1,0:T(8,128)(2,1)S(1)}, bf16[640,512]{1,0:T(8,128)(2,1)S(1)}, bf16[640,512]{1,0:T(8,128)(2,1)S(1)}) fusion(bf16[1,2560,512]{2,1,0:T(8,128)(2,1)} %param.9, s32[]{:T(128)S(6)} %select_n.48, s32[]{:T(128)S(6)} %select_n.49, s32[]{:T(128)S(6)} %select_n.51, s32[]{:T(128)S(6)} %select_n.50), kind=kLoop, calls=%fused_computation.38 | loop fusion | bytes 5242896 | tf_op jit(solution)/shard_map/dynamic_slice | solution.py:55
  10.4 0.5 copy-done
  11.4 1.5 %copy-done.1 = bf16[1,512,2560]{2,1,0:T(8,128)(2,1)S(1)} copy-done((bf16[1,512,2560]{2,1,0:T(8,128)(2,1)S(1)}, bf16[1,512,2560]{2,1,0:T(8,128)(2,1)}, u32[]{:S(2)}) %copy-start.1) | copy-done | bytes 2621464
  13.1 0.4 collective-permute-start.5
  13.6 7.1 %collective-permute-done.10 = bf16[128,640]{1,0:T(8,128)(2,1)S(1)} collective-permute-done((bf16[128,640]{1,0:T(8,128)(2,1)S(1)}, bf16[128,640]{1,0:T(8,128)(2,1)S(1)}, u32[]{:S(2)}, u32[]{:S(2)}) %collective-permute-start.10) | collective-permute-done | bytes 163872 | tf_op jit(solution)/shard_map/ppermute | solution.py:66
  20.7 0.5 collective-permute-start.11
  21.2 1.5 %collective-permute-start.17 = (bf16[128,640]{1,0:T(8,128)(2,1)S(1)}, bf16[128,640]{1,0:T(8,128)(2,1)S(1)}, u32[]{:S(2)}, u32[]{:S(2)}) collective-permute-start(bf16[128,640]{1,0:T(8,128)(2,1)S(1)} %collective-permute-done.16), channel_id=1, source_target_pairs={{0,2},{1,3},{2,0},{3,1},{4,6},{5,7},{6,4},{7,5},{8,10},{9,11},{10,... | collective-permute-start | bytes 491528 | tf_op jit(solution)/shard_map/ppermute | solution.py:79
  22.8 3.2 %collective-permute-done.11 = bf16[128,640]{1,0:T(8,128)(2,1)S(1)} collective-permute-done((bf16[128,640]{1,0:T(8,128)(2,1)S(1)}, bf16[128,640]{1,0:T(8,128)(2,1)S(1)}, u32[]{:S(2)}, u32[]{:S(2)}) %collective-permute-start.11) | collective-permute-done | bytes 163872 | tf_op jit(solution)/shard_map/ppermute | solution.py:79
  26.1 1.6 %collective-permute-done.17 = bf16[128,640]{1,0:T(8,128)(2,1)S(1)} collective-permute-done((bf16[128,640]{1,0:T(8,128)(2,1)S(1)}, bf16[128,640]{1,0:T(8,128)(2,1)S(1)}, u32[]{:S(2)}, u32[]{:S(2)}) %collective-permute-start.17) | collective-permute-done | bytes 163872 | tf_op jit(solution)/shard_map/ppermute | solution.py:79
  27.9 0.5 fusion.13
  28.4 0.5 multiply_convert_fusion.1
  28.9 0.3 convolution_convert_fusion.6
  29.2 0.6 collective-permute-start.2
  29.8 1.2 %collective-permute-done.2 = bf16[128,1280]{1,0:T(8,128)(2,1)S(1)} collective-permute-done((bf16[128,1280]{1,0:T(8,128)(2,1)S(1)}, bf16[128,1280]{1,0:T(8,128)(2,1)S(1)}, u32[]{:S(2)}, u32[]{:S(2)}) %collective-permute-start.2) | collective-permute-done | bytes 327712 | tf_op jit(solution)/shard_map/ppermute | solution.py:90
  31.0 0.3 convert_add_fusion.3
  31.4 0.5 fusion.16
  31.9 0.7 %fusion.1 = bf16[128,512]{1,0:T(8,128)(2,1)S(1)} fusion(bf16[128,2560]{1,0:T(8,128)(2,1)S(1)} %pad_maximum_fusion.5, f32[128,512]{1,0:T(8,128)S(1)} %fusion.16, bf16[640,512]{1,0:T(8,128)(2,1)S(1)} %get-tuple-element.17, bf16[640,512]{1,0:T(8,128)(2,1)S(1)} %get-tuple-element.18, bf16[640,512]{1,0:T(8,128)(2,1)S(1)} %get-tuple-element.16, ...), kind=kOutput, calls=%fused_computation.16 | convolution fusion | flops 346423296 | bytes 3670016 | tf_op jit(solution)/shard_map/dot_general | solution.py:85
  32.6 0.3 convolution_convert_fusion.4
  33.0 0.4 collective-permute-start.7
  33.5 1.2 %collective-permute-done.7 = bf16[128,1280]{1,0:T(8,128)(2,1)S(1)} collective-permute-done((bf16[128,1280]{1,0:T(8,128)(2,1)S(1)}, bf16[128,1280]{1,0:T(8,128)(2,1)S(1)}, u32[]{:S(2)}, u32[]{:S(2)}) %collective-permute-start.7) | collective-permute-done | bytes 327712 | tf_op jit(solution)/shard_map/ppermute | solution.py:90
  34.7 0.3 convert_add_fusion.2
  35.1 0.5 fusion.17
  35.6 0.7 %fusion.2 = bf16[128,512]{1,0:T(8,128)(2,1)S(1)} fusion(bf16[128,2560]{1,0:T(8,128)(2,1)S(1)} %pad_maximum_fusion.6, f32[128,512]{1,0:T(8,128)S(1)} %fusion.17, bf16[640,512]{1,0:T(8,128)(2,1)S(1)} %get-tuple-element.17, bf16[640,512]{1,0:T(8,128)(2,1)S(1)} %get-tuple-element.18, bf16[640,512]{1,0:T(8,128)(2,1)S(1)} %get-tuple-element.16, ...), kind=kOutput, calls=%fused_computation.17 | convolution fusion | flops 346423296 | bytes 3670016 | tf_op jit(solution)/shard_map/dot_general | solution.py:85
  36.3 0.3 convolution_convert_fusion.2
  36.7 0.4 collective-permute-start.13
  37.2 0.7 %slice.70 = bf16[128,640]{1,0:T(8,128)(2,1)} slice(f32[128,1280]{1,0:T(8,128)S(1)} %convert_add_fusion.2), slice={[0:128], [640:1280]} | slice | bytes 327680 | tf_op jit(solution)/shard_map/slice | solution.py:93
  37.8 0.5 collective-permute-start.8
  38.4 0.3 convert_add_fusion.1
  38.7 0.5 fusion.18
  39.2 0.7 %fusion.3 = bf16[128,512]{1,0:T(8,128)(2,1)S(1)} fusion(bf16[128,2560]{1,0:T(8,128)(2,1)S(1)} %pad_maximum_fusion.7, f32[128,512]{1,0:T(8,128)S(1)} %fusion.18, bf16[640,512]{1,0:T(8,128)(2,1)S(1)} %get-tuple-element.17, bf16[640,512]{1,0:T(8,128)(2,1)S(1)} %get-tuple-element.18, bf16[640,512]{1,0:T(8,128)(2,1)S(1)} %get-tuple-element.16, ...), kind=kOutput, calls=%fused_computation.18 | convolution fusion | flops 346423296 | bytes 3670016 | tf_op jit(solution)/shard_map/dot_general | solution.py:85
  40.0 1.1 %convolution_convert_fusion = bf16[128,1280]{1,0:T(8,128)(2,1)} fusion(bf16[128,512]{1,0:T(8,128)(2,1)S(1)} %fusion.3, bf16[512,640]{1,0:T(8,128)(2,1)S(1)} %get-tuple-element.13, bf16[512,640]{1,0:T(8,128)(2,1)S(1)} %get-tuple-element.14), kind=kOutput, calls=%fused_computation.2 | convolution fusion | flops 170557440 | bytes 1769472 | tf_op jit(solution)/shard_map/dot_general | solution.py:88
  41.1 0.3 collective-permute-start.19
  41.5 1.2 %collective-permute-start.3 = (bf16[128,640]{1,0:T(8,128)(2,1)S(1)}, bf16[128,640]{1,0:T(8,128)(2,1)S(1)}, u32[]{:S(2)}, u32[]{:S(2)}) collective-permute-start(bf16[128,640]{1,0:T(8,128)(2,1)S(1)} %slice.71), channel_id=1, source_target_pairs={{0,2},{1,3},{2,0},{3,1},{4,6},{5,7},{6,4},{7,5},{8,10},{9,11},{10,... | collective-permute-start | bytes 491528 | tf_op jit(solution)/shard_map/ppermute | solution.py:92
  42.7 1.6 %collective-permute-done.8 = bf16[128,640]{1,0:T(8,128)(2,1)S(1)} collective-permute-done((bf16[128,640]{1,0:T(8,128)(2,1)}, bf16[128,640]{1,0:T(8,128)(2,1)S(1)}, u32[]{:S(2)}, u32[]{:S(2)}) %collective-permute-start.8) | collective-permute-done | bytes 163872 | tf_op jit(solution)/shard_map/ppermute | solution.py:92
  44.3 1.1 %collective-permute-start.9 = (bf16[128,640]{1,0:T(8,128)(2,1)S(1)}, bf16[128,640]{1,0:T(8,128)(2,1)S(1)}, u32[]{:S(2)}, u32[]{:S(2)}) collective-permute-start(bf16[128,640]{1,0:T(8,128)(2,1)S(1)} %fusion.6), channel_id=1, source_target_pairs={{0,4},{4,0},{8,12},{12,8},{1,5},{5,1},{9,13},{13,9},{2,6},{6,2},{1... | collective-permute-start | bytes 491528 | tf_op jit(solution)/shard_map/ppermute | solution.py:97
  45.5 0.6 collective-permute-start.14
  46.1 1.4 %convert_add_fusion = f32[128,1280]{1,0:T(8,128)S(1)} fusion(bf16[128,1280]{1,0:T(8,128)(2,1)} %collective-permute-done.19, bf16[128,512]{1,0:T(8,128)(2,1)} %copy-done.3, bf16[512,640]{1,0:T(8,128)(2,1)S(1)} %get-tuple-element.12, bf16[512,640]{1,0:T(8,128)(2,1)S(1)} %get-tuple-element.11), kind=kOutput, calls=%fused_computation.23 | convolution fusion | flops 171048960 | bytes 2424832 | tf_op jit(solution)/shard_map/dot_general | solution.py:87
  47.5 1.5 %collective-permute-start.20 = (bf16[128,640]{1,0:T(8,128)(2,1)S(1)}, bf16[128,640]{1,0:T(8,128)(2,1)S(1)}, u32[]{:S(2)}, u32[]{:S(2)}) collective-permute-start(bf16[128,640]{1,0:T(8,128)(2,1)S(1)} %slice.68), channel_id=1, source_target_pairs={{0,2},{1,3},{2,0},{3,1},{4,6},{5,7},{6,4},{7,5},{8,10},{9,11},{10,... | collective-permute-start | bytes 491528 | tf_op jit(solution)/shard_map/ppermute | solution.py:92
  49.1 3.6 %collective-permute-done.14 = bf16[128,640]{1,0:T(8,128)(2,1)S(1)} collective-permute-done((bf16[128,640]{1,0:T(8,128)(2,1)S(1)}, bf16[128,640]{1,0:T(8,128)(2,1)S(1)}, u32[]{:S(2)}, u32[]{:S(2)}) %collective-permute-start.14) | collective-permute-done | bytes 163872 | tf_op jit(solution)/shard_map/ppermute | solution.py:92
  52.7 1.7 %collective-permute-start.15 = (bf16[128,640]{1,0:T(8,128)(2,1)S(1)}, bf16[128,640]{1,0:T(8,128)(2,1)S(1)}, u32[]{:S(2)}, u32[]{:S(2)}) collective-permute-start(bf16[128,640]{1,0:T(8,128)(2,1)S(1)} %fusion.5), channel_id=1, source_target_pairs={{0,8},{4,12},{8,0},{12,4},{1,9},{5,13},{9,1},{13,5},{2,10},{6,14},... | collective-permute-start | bytes 491528 | tf_op jit(solution)/shard_map/ppermute | solution.py:97
  54.4 0.4 collective-permute-done.20
  54.9 2.2 %collective-permute-start.21 = (bf16[128,640]{1,0:T(8,128)(2,1)S(1)}, bf16[128,640]{1,0:T(8,128)(2,1)S(1)}, u32[]{:S(2)}, u32[]{:S(2)}) collective-permute-start(bf16[128,640]{1,0:T(8,128)(2,1)S(1)} %fusion.4), channel_id=1, source_target_pairs={{0,12},{4,8},{8,4},{12,0},{1,13},{5,9},{9,5},{13,1},{2,14},{6,10},... | collective-permute-start | bytes 491528 | tf_op jit(solution)/shard_map/ppermute | solution.py:97
  57.1 8.8 %collective-permute-done.15 = bf16[128,640]{1,0:T(8,128)(2,1)S(1)} collective-permute-done((bf16[128,640]{1,0:T(8,128)(2,1)S(1)}, bf16[128,640]{1,0:T(8,128)(2,1)S(1)}, u32[]{:S(2)}, u32[]{:S(2)}) %collective-permute-start.15) | collective-permute-done | bytes 163872 | tf_op jit(solution)/shard_map/ppermute | solution.py:97
  65.9 0.9 %fusion.11 = bf16[128,640]{1,0:T(8,128)(2,1)} fusion(f32[128,1280]{1,0:T(8,128)S(1)} %convert_add_fusion.3, bf16[128,640]{1,0:T(8,128)(2,1)S(1)} %collective-permute-done.21, bf16[128,640]{1,0:T(8,128)(2,1)S(1)} %collective-permute-done.15, bf16[128,640]{1,0:T(8,128)(2,1)S(1)} %collective-permute-done.9, bf16[128,640]{1,0:T(8,128)(2,1)S(1)} %collective-permute-done.3, ...), kind=kLoop, calls=%fused_computation.54 | loop fusion | flops 1064960 | bytes 1147392 | tf_op jit(solution)/shard_map/convert_element_type | solution.py:101
  (41 shorter events, 1.6 us)
Async XLA Ops:
  1.0 12.5 %collective-permute-start = (bf16[128,640]{1,0:T(8,128)(2,1)S(1)}, bf16[128,640]{1,0:T(8,128)(2,1)S(1)}, u32[]{:S(2)}, u32[]{:S(2)}) collective-permute-start(bf16[128,640]{1,0:T(8,128)(2,1)S(1)} %multiply_convert_fusion), channel_id=1, source_target_pairs={{0,2},{1,3},{2,0},{3,1},{4,6},{5,7},{6,4},{7,5},{8,10},{9,11},{10,... | collective-permute-start | bytes 491528 | tf_op jit(solution)/shard_map/ppermute | solution.py:79
  4.0 9.1 %collective-permute-start.4 = (bf16[128,640]{1,0:T(8,128)(2,1)S(1)}, bf16[128,640]{1,0:T(8,128)(2,1)S(1)}, u32[]{:S(2)}, u32[]{:S(2)}) collective-permute-start(bf16[128,640]{1,0:T(8,128)(2,1)S(1)} %multiply_convert_fusion), channel_id=1, source_target_pairs={{0,4},{4,0},{8,12},{12,8},{1,5},{5,1},{9,13},{13,9},{2,6},{6,2},{1... | collective-permute-start | bytes 491528 | tf_op jit(solution)/shard_map/ppermute | solution.py:66
  5.6 15.1 %collective-permute-start.10 = (bf16[128,640]{1,0:T(8,128)(2,1)S(1)}, bf16[128,640]{1,0:T(8,128)(2,1)S(1)}, u32[]{:S(2)}, u32[]{:S(2)}) collective-permute-start(bf16[128,640]{1,0:T(8,128)(2,1)S(1)} %multiply_convert_fusion), channel_id=1, source_target_pairs={{0,8},{4,12},{8,0},{12,4},{1,9},{5,13},{9,1},{13,5},{2,10},{6,14},... | collective-permute-start | bytes 491528 | tf_op jit(solution)/shard_map/ppermute | solution.py:66
  8.2 13.0 %collective-permute-start.16 = (bf16[128,640]{1,0:T(8,128)(2,1)S(1)}, bf16[128,640]{1,0:T(8,128)(2,1)S(1)}, u32[]{:S(2)}, u32[]{:S(2)}) collective-permute-start(bf16[128,640]{1,0:T(8,128)(2,1)S(1)} %multiply_convert_fusion), channel_id=1, source_target_pairs={{0,12},{4,8},{8,4},{12,0},{1,13},{5,9},{9,5},{13,1},{2,14},{6,10},... | collective-permute-start | bytes 491528 | tf_op jit(solution)/shard_map/ppermute | solution.py:66
  8.4 2.5 %copy-start = (bf16[1,2560,512]{2,1,0:T(8,128)(2,1)S(1)}, bf16[1,2560,512]{2,1,0:T(8,128)(2,1)}, u32[]{:S(2)}) copy-start(bf16[1,2560,512]{2,1,0:T(8,128)(2,1)} %param.10) | copy-start | bytes 7864324
  11.1 1.7 %copy-start.1 = (bf16[1,512,2560]{2,1,0:T(8,128)(2,1)S(1)}, bf16[1,512,2560]{2,1,0:T(8,128)(2,1)}, u32[]{:S(2)}) copy-start(bf16[1,512,2560]{2,1,0:T(8,128)(2,1)} %param.11) | copy-start | bytes 7864324
  13.1 9.6 %collective-permute-start.5 = (bf16[128,640]{1,0:T(8,128)(2,1)S(1)}, bf16[128,640]{1,0:T(8,128)(2,1)S(1)}, u32[]{:S(2)}, u32[]{:S(2)}) collective-permute-start(bf16[128,640]{1,0:T(8,128)(2,1)S(1)} %collective-permute-done.4), channel_id=1, source_target_pairs={{0,2},{1,3},{2,0},{3,1},{4,6},{5,7},{6,4},{7,5},{8,10},{9,11},{10,... | collective-permute-start | bytes 491528 | tf_op jit(solution)/shard_map/ppermute | solution.py:79
  13.5 14.3 %collective-permute-start.1 = (bf16[128,1280]{1,0:T(8,128)(2,1)S(1)}, bf16[128,1280]{1,0:T(8,128)(2,1)S(1)}, u32[]{:S(2)}, u32[]{:S(2)}) collective-permute-start(bf16[128,1280]{1,0:T(8,128)(2,1)S(1)} %pad_maximum_fusion.8), channel_id=1, source_target_pairs={{0,1},{1,0},{2,3},{3,2},{4,5},{5,4},{6,7},{7,6},{8,9},{9,8},{10,11... | collective-permute-start | bytes 983048 | tf_op jit(solution)/shard_map/ppermute | solution.py:81
  20.7 5.3 %collective-permute-start.11 = (bf16[128,640]{1,0:T(8,128)(2,1)S(1)}, bf16[128,640]{1,0:T(8,128)(2,1)S(1)}, u32[]{:S(2)}, u32[]{:S(2)}) collective-permute-start(bf16[128,640]{1,0:T(8,128)(2,1)S(1)} %collective-permute-done.10), channel_id=1, source_target_pairs={{0,2},{1,3},{2,0},{3,1},{4,6},{5,7},{6,4},{7,5},{8,10},{9,11},{10,... | collective-permute-start | bytes 491528 | tf_op jit(solution)/shard_map/ppermute | solution.py:79
  21.2 6.5 %collective-permute-start.17 = (bf16[128,640]{1,0:T(8,128)(2,1)S(1)}, bf16[128,640]{1,0:T(8,128)(2,1)S(1)}, u32[]{:S(2)}, u32[]{:S(2)}) collective-permute-start(bf16[128,640]{1,0:T(8,128)(2,1)S(1)} %collective-permute-done.16), channel_id=1, source_target_pairs={{0,2},{1,3},{2,0},{3,1},{4,6},{5,7},{6,4},{7,5},{8,10},{9,11},{10,... | collective-permute-start | bytes 491528 | tf_op jit(solution)/shard_map/ppermute | solution.py:79
  22.7 7.1 %collective-permute-start.6 = (bf16[128,1280]{1,0:T(8,128)(2,1)S(1)}, bf16[128,1280]{1,0:T(8,128)(2,1)S(1)}, u32[]{:S(2)}, u32[]{:S(2)}) collective-permute-start(bf16[128,1280]{1,0:T(8,128)(2,1)S(1)} %pad_maximum_fusion.9), channel_id=1, source_target_pairs={{0,1},{1,0},{2,3},{3,2},{4,5},{5,4},{6,7},{7,6},{8,9},{9,8},{10,11... | collective-permute-start | bytes 983048 | tf_op jit(solution)/shard_map/ppermute | solution.py:81
  26.0 7.4 %collective-permute-start.12 = (bf16[128,1280]{1,0:T(8,128)(2,1)S(1)}, bf16[128,1280]{1,0:T(8,128)(2,1)S(1)}, u32[]{:S(2)}, u32[]{:S(2)}) collective-permute-start(bf16[128,1280]{1,0:T(8,128)(2,1)S(1)} %pad_maximum_fusion.10), channel_id=1, source_target_pairs={{0,1},{1,0},{2,3},{3,2},{4,5},{5,4},{6,7},{7,6},{8,9},{9,8},{10,11... | collective-permute-start | bytes 983048 | tf_op jit(solution)/shard_map/ppermute | solution.py:81
  27.8 9.3 %collective-permute-start.18 = (bf16[128,1280]{1,0:T(8,128)(2,1)S(1)}, bf16[128,1280]{1,0:T(8,128)(2,1)S(1)}, u32[]{:S(2)}, u32[]{:S(2)}) collective-permute-start(bf16[128,1280]{1,0:T(8,128)(2,1)S(1)} %pad_maximum_fusion.11), channel_id=1, source_target_pairs={{0,1},{1,0},{2,3},{3,2},{4,5},{5,4},{6,7},{7,6},{8,9},{9,8},{10,11... | collective-permute-start | bytes 983048 | tf_op jit(solution)/shard_map/ppermute | solution.py:81
  29.2 1.8 %collective-permute-start.2 = (bf16[128,1280]{1,0:T(8,128)(2,1)S(1)}, bf16[128,1280]{1,0:T(8,128)(2,1)S(1)}, u32[]{:S(2)}, u32[]{:S(2)}) collective-permute-start(bf16[128,1280]{1,0:T(8,128)(2,1)S(1)} %convolution_convert_fusion.6), channel_id=1, source_target_pairs={{0,1},{1,0},{2,3},{3,2},{4,5},{5,4},{6,7},{7,6},{8,9},{9,8},{10,11... | collective-permute-start | bytes 983048 | tf_op jit(solution)/shard_map/ppermute | solution.py:90
  33.0 1.7 %collective-permute-start.7 = (bf16[128,1280]{1,0:T(8,128)(2,1)S(1)}, bf16[128,1280]{1,0:T(8,128)(2,1)S(1)}, u32[]{:S(2)}, u32[]{:S(2)}) collective-permute-start(bf16[128,1280]{1,0:T(8,128)(2,1)S(1)} %convolution_convert_fusion.4), channel_id=1, source_target_pairs={{0,1},{1,0},{2,3},{3,2},{4,5},{5,4},{6,7},{7,6},{8,9},{9,8},{10,11... | collective-permute-start | bytes 983048 | tf_op jit(solution)/shard_map/ppermute | solution.py:90
  36.7 1.7 %collective-permute-start.13 = (bf16[128,1280]{1,0:T(8,128)(2,1)S(1)}, bf16[128,1280]{1,0:T(8,128)(2,1)S(1)}, u32[]{:S(2)}, u32[]{:S(2)}) collective-permute-start(bf16[128,1280]{1,0:T(8,128)(2,1)S(1)} %convolution_convert_fusion.2), channel_id=1, source_target_pairs={{0,1},{1,0},{2,3},{3,2},{4,5},{5,4},{6,7},{7,6},{8,9},{9,8},{10,11... | collective-permute-start | bytes 983048 | tf_op jit(solution)/shard_map/ppermute | solution.py:90
  37.8 6.5 %collective-permute-start.8 = (bf16[128,640]{1,0:T(8,128)(2,1)}, bf16[128,640]{1,0:T(8,128)(2,1)S(1)}, u32[]{:S(2)}, u32[]{:S(2)}) collective-permute-start(bf16[128,640]{1,0:T(8,128)(2,1)} %slice.70), channel_id=1, source_target_pairs={{0,2},{1,3},{2,0},{3,1},{4,6},{5,7},{6,4},{7,5},{8,10},{9,11},{10,... | collective-permute-start | bytes 491528 | tf_op jit(solution)/shard_map/ppermute | solution.py:92
  40.0 1.1 %copy-start.3 = (bf16[128,512]{1,0:T(8,128)(2,1)}, bf16[128,512]{1,0:T(8,128)(2,1)S(1)}, u32[]{:S(2)}) copy-start(bf16[128,512]{1,0:T(8,128)(2,1)S(1)} %fusion.3) | copy-start | bytes 393220
  41.1 5.0 %collective-permute-start.19 = (bf16[128,1280]{1,0:T(8,128)(2,1)}, bf16[128,1280]{1,0:T(8,128)(2,1)}, u32[]{:S(2)}, u32[]{:S(2)}) collective-permute-start(bf16[128,1280]{1,0:T(8,128)(2,1)} %convolution_convert_fusion), channel_id=1, source_target_pairs={{0,1},{1,0},{2,3},{3,2},{4,5},{5,4},{6,7},{7,6},{8,9},{9,8},{10,11... | collective-permute-start | bytes 983048 | tf_op jit(solution)/shard_map/ppermute | solution.py:90
  41.4 15.6 %copy-start.2 = (s32[128,1]{0,1:T(1,128)S(1)}, s32[128,1]{0,1:T(1,128)}, u32[]{:S(2)}) copy-start(s32[128,1]{0,1:T(1,128)} %param.8) | copy-start | bytes 1540
  41.5 15.6 %collective-permute-start.3 = (bf16[128,640]{1,0:T(8,128)(2,1)S(1)}, bf16[128,640]{1,0:T(8,128)(2,1)S(1)}, u32[]{:S(2)}, u32[]{:S(2)}) collective-permute-start(bf16[128,640]{1,0:T(8,128)(2,1)S(1)} %slice.71), channel_id=1, source_target_pairs={{0,2},{1,3},{2,0},{3,1},{4,6},{5,7},{6,4},{7,5},{8,10},{9,11},{10,... | collective-permute-start | bytes 491528 | tf_op jit(solution)/shard_map/ppermute | solution.py:92
  44.3 12.8 %collective-permute-start.9 = (bf16[128,640]{1,0:T(8,128)(2,1)S(1)}, bf16[128,640]{1,0:T(8,128)(2,1)S(1)}, u32[]{:S(2)}, u32[]{:S(2)}) collective-permute-start(bf16[128,640]{1,0:T(8,128)(2,1)S(1)} %fusion.6), channel_id=1, source_target_pairs={{0,4},{4,0},{8,12},{12,8},{1,5},{5,1},{9,13},{13,9},{2,6},{6,2},{1... | collective-permute-start | bytes 491528 | tf_op jit(solution)/shard_map/ppermute | solution.py:97
  45.5 7.2 %collective-permute-start.14 = (bf16[128,640]{1,0:T(8,128)(2,1)S(1)}, bf16[128,640]{1,0:T(8,128)(2,1)S(1)}, u32[]{:S(2)}, u32[]{:S(2)}) collective-permute-start(bf16[128,640]{1,0:T(8,128)(2,1)S(1)} %slice.69), channel_id=1, source_target_pairs={{0,2},{1,3},{2,0},{3,1},{4,6},{5,7},{6,4},{7,5},{8,10},{9,11},{10,... | collective-permute-start | bytes 491528 | tf_op jit(solution)/shard_map/ppermute | solution.py:92
  47.5 7.3 %collective-permute-start.20 = (bf16[128,640]{1,0:T(8,128)(2,1)S(1)}, bf16[128,640]{1,0:T(8,128)(2,1)S(1)}, u32[]{:S(2)}, u32[]{:S(2)}) collective-permute-start(bf16[128,640]{1,0:T(8,128)(2,1)S(1)} %slice.68), channel_id=1, source_target_pairs={{0,2},{1,3},{2,0},{3,1},{4,6},{5,7},{6,4},{7,5},{8,10},{9,11},{10,... | collective-permute-start | bytes 491528 | tf_op jit(solution)/shard_map/ppermute | solution.py:92
  52.7 13.2 %collective-permute-start.15 = (bf16[128,640]{1,0:T(8,128)(2,1)S(1)}, bf16[128,640]{1,0:T(8,128)(2,1)S(1)}, u32[]{:S(2)}, u32[]{:S(2)}) collective-permute-start(bf16[128,640]{1,0:T(8,128)(2,1)S(1)} %fusion.5), channel_id=1, source_target_pairs={{0,8},{4,12},{8,0},{12,4},{1,9},{5,13},{9,1},{13,5},{2,10},{6,14},... | collective-permute-start | bytes 491528 | tf_op jit(solution)/shard_map/ppermute | solution.py:97
  54.9 11.1 %collective-permute-start.21 = (bf16[128,640]{1,0:T(8,128)(2,1)S(1)}, bf16[128,640]{1,0:T(8,128)(2,1)S(1)}, u32[]{:S(2)}, u32[]{:S(2)}) collective-permute-start(bf16[128,640]{1,0:T(8,128)(2,1)S(1)} %fusion.4), channel_id=1, source_target_pairs={{0,12},{4,8},{8,4},{12,0},{1,13},{5,9},{9,5},{13,1},{2,14},{6,10},... | collective-permute-start | bytes 491528 | tf_op jit(solution)/shard_map/ppermute | solution.py:97

commit v9 on v8

--- a/solution.py
+++ b/solution.py
@@ -86,11 +86,11 @@
         hidden = (jax.nn.silu(gate_act) * up_act).astype(jnp.bfloat16)
         keep = jnp.dot(hidden, down_keep, preferred_element_type=jnp.float32).astype(jnp.bfloat16)
         send = jnp.dot(hidden, down_send, preferred_element_type=jnp.float32).astype(jnp.bfloat16)
-        previous = keep
         over_c = keep.astype(jnp.float32) + lax.ppermute(
             send, "tensor", _xor_pairs(n_tensor, 1)).astype(jnp.float32)
         summed = over_c[:, :width] + lax.ppermute(
             over_c[:, width:].astype(jnp.bfloat16), "tensor", _xor_pairs(n_tensor, 2)).astype(jnp.float32)
+        previous = summed
         for i, k in enumerate(wave):
             part = summed[i * tok_rows:(i + 1) * tok_rows]
             if k:

time: 67.3 us -> 86.3 us (1.28)
  waiting for transfers between devices: 28.8 us -> 45.1 us
  starting transfers between devices: 20.8 us -> 26.7 us
  matrix products: 9.28 us -> 7.51 us
  local copies, waits for them, and re-layouts: 5.18 us -> 4.01 us
    ppermute x4, waiting for transfers between devices: 5.65 us -> 21.2 us  [gathered(): lax.ppermute(over_c[:, width:].astype(jnp.bfloat16), 'tensor', _xor_pairs...]
    ppermute x3, waiting for transfers between devices: 7.07 us -> 12.7 us  [gathered(): lax.ppermute(scaled, 'expert', _xor_pairs(n_expert, k))]
    ppermute x4, waiting for transfers between devices: 4.83 us -> 0.53 us  [gathered(): lax.ppermute(piece, 'tensor', _xor_pairs(n_tensor, 2))]
    ppermute x3, starting transfers between devices: 4.39 us -> 8.18 us  [gathered(): lax.ppermute(scaled, 'expert', _xor_pairs(n_expert, k))]
    ppermute x3, starting transfers between devices: 5.02 us -> 7.41 us  [gathered(): lax.ppermute(part.astype(jnp.bfloat16), 'expert', _xor_pairs(n_expert, k))]
    ppermute x4, starting transfers between devices: 1.77 us -> 0.28 us  [gathered(): lax.ppermute(send, 'tensor', _xor_pairs(n_tensor, 1)).astype(jnp.float32)]
    dot_general x4, matrix products: 2.44 us -> 1.39 us  [gathered(): jnp.dot(hidden, down_keep, preferred_element_type=jnp.float32)]
    ppermute x3, waiting for transfers between devices: 8.84 us -> 7.88 us  [gathered(): lax.ppermute(part.astype(jnp.bfloat16), 'expert', _xor_pairs(n_expert, k))]
  transfers between devices with their start and end apart: 22 -> 22, of which waited for: 9 -> 10; matrix products, arithmetic and copies ran while one was open for 19% -> 10% of each run, Pallas kernels for 0% -> 0%
where the time goes in v9:
time: 86.3 us; the launch traced here: 86.1 us
  waiting for transfers between devices  45.1 us (52%)
  starting transfers between devices  26.7 us (31%)
  matrix products  7.51 us (9%)
  local copies, waits for them, and re-layouts  4.01 us (5%)
  other arithmetic  2.48 us (3%)
    ppermute x4, waiting for transfers between devices, gathered(): lax.ppermute(over_c[:, width:].astype(jnp.bfloat16), 'tensor', _xor_pairs...  21.2 us
    ppermute x3, waiting for transfers between devices, gathered(): lax.ppermute(scaled, 'expert', _xor_pairs(n_expert, k))  12.7 us
    ppermute x3, starting transfers between devices, gathered(): lax.ppermute(scaled, 'expert', _xor_pairs(n_expert, k))  8.18 us
    ppermute x3, waiting for transfers between devices, gathered(): lax.ppermute(part.astype(jnp.bfloat16), 'expert', _xor_pairs(n_expert, k))  7.88 us
    ppermute x3, starting transfers between devices, gathered(): lax.ppermute(part.astype(jnp.bfloat16), 'expert', _xor_pairs(n_expert, k))  7.41 us
    ppermute x4, starting transfers between devices, gathered(): lax.ppermute(piece, 'tensor', _xor_pairs(n_tensor, 2))  5.78 us
    ppermute x4, starting transfers between devices, gathered(): lax.ppermute(over_c[:, width:].astype(jnp.bfloat16), 'tensor', _xor_pairs...  3.92 us
    dot_general x4, matrix products, gathered(): up_act = jnp.dot(rows, up_w, preferred_element_type=jnp.float32)  2.71 us
  transfers between devices with their start and end apart: 22, of which 10 were waited for; matrix products, arithmetic and copies ran while one was open for 10% of the time, Pallas kernels for 0%

profile of v9, /device:TPU:0, one launch (start us, length us, event | category | flops | bytes accessed | tf_op | source)
XLA Modules:
  0.0 86.1 jit_solution(15576965738972180401)
XLA Ops:
  0.0 1.0 %multiply_convert_fusion = bf16[128,640]{1,0:T(8,128)(2,1)S(1)} fusion(bf16[128,640]{1,0:T(8,128)(2,1)} %param.6, f32[128]{0:T(128)} %param.7), kind=kLoop, calls=%fused_computation.56 | loop fusion | flops 245760 | bytes 328192 | tf_op jit(solution)/shard_map/convert_element_type | solution.py:64
  1.0 3.0 %collective-permute-start = (bf16[128,640]{1,0:T(8,128)(2,1)S(1)}, bf16[128,640]{1,0:T(8,128)(2,1)S(1)}, u32[]{:S(2)}, u32[]{:S(2)}) collective-permute-start(bf16[128,640]{1,0:T(8,128)(2,1)S(1)} %multiply_convert_fusion), channel_id=1, source_target_pairs={{0,2},{1,3},{2,0},{3,1},{4,6},{5,7},{6,4},{7,5},{8,10},{9,11},{10,... | collective-permute-start | bytes 491528 | tf_op jit(solution)/shard_map/ppermute | solution.py:79
  4.0 1.6 %collective-permute-start.4 = (bf16[128,640]{1,0:T(8,128)(2,1)S(1)}, bf16[128,640]{1,0:T(8,128)(2,1)S(1)}, u32[]{:S(2)}, u32[]{:S(2)}) collective-permute-start(bf16[128,640]{1,0:T(8,128)(2,1)S(1)} %multiply_convert_fusion), channel_id=1, source_target_pairs={{0,4},{4,0},{8,12},{12,8},{1,5},{5,1},{9,13},{13,9},{2,6},{6,2},{1... | collective-permute-start | bytes 491528 | tf_op jit(solution)/shard_map/ppermute | solution.py:66
  5.6 1.8 %dynamic-slice_bitcast_fusion.11 = (bf16[640,512]{1,0:T(8,128)(2,1)S(1)}, bf16[640,512]{1,0:T(8,128)(2,1)S(1)}, bf16[640,512]{1,0:T(8,128)(2,1)S(1)}, bf16[640,512]{1,0:T(8,128)(2,1)S(1)}) fusion(bf16[1,2560,512]{2,1,0:T(8,128)(2,1)} %param.9, s32[]{:T(128)S(6)} %select_n.48, s32[]{:T(128)S(6)} %select_n.49, s32[]{:T(128)S(6)} %select_n.51, s32[]{:T(128)S(6)} %select_n.50), kind=kLoop, calls=%fused_computation.41 | loop fusion | bytes 5242896 | tf_op jit(solution)/shard_map/dynamic_slice | solution.py:55
  7.7 0.5 collective-permute-done
  8.3 0.9 copy-done
  9.4 0.8 copy-done.1
  10.4 1.6 %collective-permute-start.5 = (bf16[128,640]{1,0:T(8,128)(2,1)S(1)}, bf16[128,640]{1,0:T(8,128)(2,1)S(1)}, u32[]{:S(2)}, u32[]{:S(2)}) collective-permute-start(bf16[128,640]{1,0:T(8,128)(2,1)S(1)} %collective-permute-done.4), channel_id=1, source_target_pairs={{0,2},{1,3},{2,0},{3,1},{4,6},{5,7},{6,4},{7,5},{8,10},{9,11},{10,... | collective-permute-start | bytes 491528 | tf_op jit(solution)/shard_map/ppermute | solution.py:79
  12.0 0.5 fusion.9
  12.6 0.5 multiply_convert_fusion.1
  13.1 0.3 convolution_convert_fusion.6
  13.5 2.6 %collective-permute-start.10 = (bf16[128,640]{1,0:T(8,128)(2,1)S(1)}, bf16[128,640]{1,0:T(8,128)(2,1)S(1)}, u32[]{:S(2)}, u32[]{:S(2)}) collective-permute-start(bf16[128,640]{1,0:T(8,128)(2,1)S(1)} %multiply_convert_fusion), channel_id=1, source_target_pairs={{0,8},{4,12},{8,0},{12,4},{1,9},{5,13},{9,1},{13,5},{2,10},{6,14},... | collective-permute-start | bytes 491528 | tf_op jit(solution)/shard_map/ppermute | solution.py:66
  16.2 0.2 collective-permute-start.6
  16.4 8.1 %collective-permute-done.10 = bf16[128,640]{1,0:T(8,128)(2,1)S(1)} collective-permute-done((bf16[128,640]{1,0:T(8,128)(2,1)S(1)}, bf16[128,640]{1,0:T(8,128)(2,1)S(1)}, u32[]{:S(2)}, u32[]{:S(2)}) %collective-permute-start.10) | collective-permute-done | bytes 163872 | tf_op jit(solution)/shard_map/ppermute | solution.py:66
  24.5 0.6 collective-permute-start.11
  25.2 0.3 convert_add_fusion.3
  25.6 1.5 %collective-permute-start.3 = (bf16[128,640]{1,0:T(8,128)(2,1)S(1)}, bf16[128,640]{1,0:T(8,128)(2,1)S(1)}, u32[]{:S(2)}, u32[]{:S(2)}) collective-permute-start(bf16[128,640]{1,0:T(8,128)(2,1)S(1)} %slice.57), channel_id=1, source_target_pairs={{0,2},{1,3},{2,0},{3,1},{4,6},{5,7},{6,4},{7,5},{8,10},{9,11},{10,... | collective-permute-start | bytes 491528 | tf_op jit(solution)/shard_map/ppermute | solution.py:91
  27.1 6.7 %collective-permute-done.3 = bf16[128,640]{1,0:T(8,128)(2,1)S(1)} collective-permute-done((bf16[128,640]{1,0:T(8,128)(2,1)S(1)}, bf16[128,640]{1,0:T(8,128)(2,1)S(1)}, u32[]{:S(2)}, u32[]{:S(2)}) %collective-permute-start.3) | collective-permute-done | bytes 163872 | tf_op jit(solution)/shard_map/ppermute | solution.py:91
  33.8 0.5 fusion.12
  34.4 0.7 fusion.4
  35.1 0.3 convolution_convert_fusion.4
  35.5 4.0 %collective-permute-start.16 = (bf16[128,640]{1,0:T(8,128)(2,1)S(1)}, bf16[128,640]{1,0:T(8,128)(2,1)S(1)}, u32[]{:S(2)}, u32[]{:S(2)}) collective-permute-start(bf16[128,640]{1,0:T(8,128)(2,1)S(1)} %multiply_convert_fusion), channel_id=1, source_target_pairs={{0,12},{4,8},{8,4},{12,0},{1,13},{5,9},{9,5},{13,1},{2,14},{6,10},... | collective-permute-start | bytes 491528 | tf_op jit(solution)/shard_map/ppermute | solution.py:66
  39.5 0.2 collective-permute-start.12
  39.8 4.6 %collective-permute-done.16 = bf16[128,640]{1,0:T(8,128)(2,1)S(1)} collective-permute-done((bf16[128,640]{1,0:T(8,128)(2,1)S(1)}, bf16[128,640]{1,0:T(8,128)(2,1)S(1)}, u32[]{:S(2)}, u32[]{:S(2)}) %collective-permute-start.16) | collective-permute-done | bytes 163872 | tf_op jit(solution)/shard_map/ppermute | solution.py:66
  44.4 0.5 collective-permute-start.17
  44.9 0.3 convert_add_fusion.2
  45.3 1.6 %collective-permute-start.8 = (bf16[128,640]{1,0:T(8,128)(2,1)S(1)}, bf16[128,640]{1,0:T(8,128)(2,1)S(1)}, u32[]{:S(2)}, u32[]{:S(2)}) collective-permute-start(bf16[128,640]{1,0:T(8,128)(2,1)S(1)} %slice.56), channel_id=1, source_target_pairs={{0,2},{1,3},{2,0},{3,1},{4,6},{5,7},{6,4},{7,5},{8,10},{9,11},{10,... | collective-permute-start | bytes 491528 | tf_op jit(solution)/shard_map/ppermute | solution.py:91
  46.9 6.9 %collective-permute-done.8 = bf16[128,640]{1,0:T(8,128)(2,1)S(1)} collective-permute-done((bf16[128,640]{1,0:T(8,128)(2,1)S(1)}, bf16[128,640]{1,0:T(8,128)(2,1)S(1)}, u32[]{:S(2)}, u32[]{:S(2)}) %collective-permute-start.8) | collective-permute-done | bytes 163872 | tf_op jit(solution)/shard_map/ppermute | solution.py:91
  53.8 0.5 fusion.13
  54.3 0.7 fusion.5
  55.1 0.3 convolution_convert_fusion.2
  55.6 0.5 collective-permute-start.18
  56.1 1.0 %collective-permute-done.13 = bf16[128,1280]{1,0:T(8,128)(2,1)S(1)} collective-permute-done((bf16[128,1280]{1,0:T(8,128)(2,1)S(1)}, bf16[128,1280]{1,0:T(8,128)(2,1)S(1)}, u32[]{:S(2)}, u32[]{:S(2)}) %collective-permute-start.13) | collective-permute-done | bytes 327712 | tf_op jit(solution)/shard_map/ppermute | solution.py:89
  57.1 0.3 convert_add_fusion.1
  57.5 0.5 collective-permute-start.14
  58.0 5.8 %collective-permute-done.14 = bf16[128,640]{1,0:T(8,128)(2,1)S(1)} collective-permute-done((bf16[128,640]{1,0:T(8,128)(2,1)S(1)}, bf16[128,640]{1,0:T(8,128)(2,1)S(1)}, u32[]{:S(2)}, u32[]{:S(2)}) %collective-permute-start.14) | collective-permute-done | bytes 163872 | tf_op jit(solution)/shard_map/ppermute | solution.py:91
  63.9 0.5 fusion.14
  64.4 0.7 fusion.6
  65.1 0.3 convolution_convert_fusion
  65.6 1.6 %collective-permute-done.19 = bf16[128,1280]{1,0:T(8,128)(2,1)S(1)} collective-permute-done((bf16[128,1280]{1,0:T(8,128)(2,1)S(1)}, bf16[128,1280]{1,0:T(8,128)(2,1)S(1)}, u32[]{:S(2)}, u32[]{:S(2)}) %collective-permute-start.19) | collective-permute-done | bytes 327712 | tf_op jit(solution)/shard_map/ppermute | solution.py:89
  67.2 0.3 convert_add_fusion
  67.6 0.5 collective-permute-start.20
  68.0 2.4 %collective-permute-start.9 = (bf16[128,640]{1,0:T(8,128)(2,1)S(1)}, bf16[128,640]{1,0:T(8,128)(2,1)S(1)}, u32[]{:S(2)}, u32[]{:S(2)}) collective-permute-start(bf16[128,640]{1,0:T(8,128)(2,1)S(1)} %slice_add_fusion.2), channel_id=1, source_target_pairs={{0,4},{4,0},{8,12},{12,8},{1,5},{5,1},{9,13},{13,9},{2,6},{6,2},{1... | collective-permute-start | bytes 491528 | tf_op jit(solution)/shard_map/ppermute | solution.py:97
  70.4 1.7 %collective-permute-start.15 = (bf16[128,640]{1,0:T(8,128)(2,1)S(1)}, bf16[128,640]{1,0:T(8,128)(2,1)S(1)}, u32[]{:S(2)}, u32[]{:S(2)}) collective-permute-start(bf16[128,640]{1,0:T(8,128)(2,1)S(1)} %slice_add_fusion.1), channel_id=1, source_target_pairs={{0,8},{4,12},{8,0},{12,4},{1,9},{5,13},{9,1},{13,5},{2,10},{6,14},... | collective-permute-start | bytes 491528 | tf_op jit(solution)/shard_map/ppermute | solution.py:97
  72.0 1.8 %collective-permute-done.20 = bf16[128,640]{1,0:T(8,128)(2,1)S(1)} collective-permute-done((bf16[128,640]{1,0:T(8,128)(2,1)S(1)}, bf16[128,640]{1,0:T(8,128)(2,1)S(1)}, u32[]{:S(2)}, u32[]{:S(2)}) %collective-permute-start.20) | collective-permute-done | bytes 163872 | tf_op jit(solution)/shard_map/ppermute | solution.py:91
  73.9 3.4 %collective-permute-start.21 = (bf16[128,640]{1,0:T(8,128)(2,1)S(1)}, bf16[128,640]{1,0:T(8,128)(2,1)S(1)}, u32[]{:S(2)}, u32[]{:S(2)}) collective-permute-start(bf16[128,640]{1,0:T(8,128)(2,1)S(1)} %fusion.7), channel_id=1, source_target_pairs={{0,12},{4,8},{8,4},{12,0},{1,13},{5,9},{9,5},{13,1},{2,14},{6,10},... | collective-permute-start | bytes 491528 | tf_op jit(solution)/shard_map/ppermute | solution.py:97
  77.3 7.9 %collective-permute-done.15 = bf16[128,640]{1,0:T(8,128)(2,1)S(1)} collective-permute-done((bf16[128,640]{1,0:T(8,128)(2,1)S(1)}, bf16[128,640]{1,0:T(8,128)(2,1)S(1)}, u32[]{:S(2)}, u32[]{:S(2)}) %collective-permute-start.15) | collective-permute-done | bytes 163872 | tf_op jit(solution)/shard_map/ppermute | solution.py:97
  85.2 0.9 %add_convert_fusion = bf16[128,640]{1,0:T(8,128)(2,1)} fusion(bf16[128,640]{1,0:T(8,128)(2,1)S(1)} %collective-permute-done.21, bf16[128,640]{1,0:T(8,128)(2,1)S(1)} %collective-permute-done.15, bf16[128,640]{1,0:T(8,128)(2,1)S(1)} %collective-permute-done.9, f32[128,640]{1,0:T(8,128)S(1)} %slice_add_fusion.3, pred[128]{0:T(512)(128)(4,1)S(1)} %get-tuple-element.25, ...), kind=kLoop, calls=%fused_computation.55 | loop fusion | flops 901120 | bytes 983552 | tf_op jit(solution)/shard_map/convert_element_type | solution.py:101
  (40 shorter events, 1.5 us)
Async XLA Ops:
  1.0 7.2 %collective-permute-start = (bf16[128,640]{1,0:T(8,128)(2,1)S(1)}, bf16[128,640]{1,0:T(8,128)(2,1)S(1)}, u32[]{:S(2)}, u32[]{:S(2)}) collective-permute-start(bf16[128,640]{1,0:T(8,128)(2,1)S(1)} %multiply_convert_fusion), channel_id=1, source_target_pairs={{0,2},{1,3},{2,0},{3,1},{4,6},{5,7},{6,4},{7,5},{8,10},{9,11},{10,... | collective-permute-start | bytes 491528 | tf_op jit(solution)/shard_map/ppermute | solution.py:79
  4.0 6.4 %collective-permute-start.4 = (bf16[128,640]{1,0:T(8,128)(2,1)S(1)}, bf16[128,640]{1,0:T(8,128)(2,1)S(1)}, u32[]{:S(2)}, u32[]{:S(2)}) collective-permute-start(bf16[128,640]{1,0:T(8,128)(2,1)S(1)} %multiply_convert_fusion), channel_id=1, source_target_pairs={{0,4},{4,0},{8,12},{12,8},{1,5},{5,1},{9,13},{13,9},{2,6},{6,2},{1... | collective-permute-start | bytes 491528 | tf_op jit(solution)/shard_map/ppermute | solution.py:66
  7.5 1.7 %copy-start = (bf16[1,2560,512]{2,1,0:T(8,128)(2,1)S(1)}, bf16[1,2560,512]{2,1,0:T(8,128)(2,1)}, u32[]{:S(2)}) copy-start(bf16[1,2560,512]{2,1,0:T(8,128)(2,1)} %param.10) | copy-start | bytes 7864324
  8.2 1.9 %copy-start.1 = (bf16[1,512,2560]{2,1,0:T(8,128)(2,1)S(1)}, bf16[1,512,2560]{2,1,0:T(8,128)(2,1)}, u32[]{:S(2)}) copy-start(bf16[1,512,2560]{2,1,0:T(8,128)(2,1)} %param.11) | copy-start | bytes 7864324
  8.3 3.8 %collective-permute-start.1 = (bf16[128,1280]{1,0:T(8,128)(2,1)S(1)}, bf16[128,1280]{1,0:T(8,128)(2,1)S(1)}, u32[]{:S(2)}, u32[]{:S(2)}) collective-permute-start(bf16[128,1280]{1,0:T(8,128)(2,1)S(1)} %pad_maximum_fusion.8), channel_id=1, source_target_pairs={{0,1},{1,0},{2,3},{3,2},{4,5},{5,4},{6,7},{7,6},{8,9},{9,8},{10,11... | collective-permute-start | bytes 983048 | tf_op jit(solution)/shard_map/ppermute | solution.py:81
  10.4 5.7 %collective-permute-start.5 = (bf16[128,640]{1,0:T(8,128)(2,1)S(1)}, bf16[128,640]{1,0:T(8,128)(2,1)S(1)}, u32[]{:S(2)}, u32[]{:S(2)}) collective-permute-start(bf16[128,640]{1,0:T(8,128)(2,1)S(1)} %collective-permute-done.4), channel_id=1, source_target_pairs={{0,2},{1,3},{2,0},{3,1},{4,6},{5,7},{6,4},{7,5},{8,10},{9,11},{10,... | collective-permute-start | bytes 491528 | tf_op jit(solution)/shard_map/ppermute | solution.py:79
  13.4 11.7 %collective-permute-start.2 = (bf16[128,1280]{1,0:T(8,128)(2,1)S(1)}, bf16[128,1280]{1,0:T(8,128)(2,1)S(1)}, u32[]{:S(2)}, u32[]{:S(2)}) collective-permute-start(bf16[128,1280]{1,0:T(8,128)(2,1)S(1)} %convolution_convert_fusion.6), channel_id=1, source_target_pairs={{0,1},{1,0},{2,3},{3,2},{4,5},{5,4},{6,7},{7,6},{8,9},{9,8},{10,11... | collective-permute-start | bytes 983048 | tf_op jit(solution)/shard_map/ppermute | solution.py:89
  13.5 11.0 %collective-permute-start.10 = (bf16[128,640]{1,0:T(8,128)(2,1)S(1)}, bf16[128,640]{1,0:T(8,128)(2,1)S(1)}, u32[]{:S(2)}, u32[]{:S(2)}) collective-permute-start(bf16[128,640]{1,0:T(8,128)(2,1)S(1)} %multiply_convert_fusion), channel_id=1, source_target_pairs={{0,8},{4,12},{8,0},{12,4},{1,9},{5,13},{9,1},{13,5},{2,10},{6,14},... | collective-permute-start | bytes 491528 | tf_op jit(solution)/shard_map/ppermute | solution.py:66
  16.2 10.8 %collective-permute-start.6 = (bf16[128,1280]{1,0:T(8,128)(2,1)S(1)}, bf16[128,1280]{1,0:T(8,128)(2,1)S(1)}, u32[]{:S(2)}, u32[]{:S(2)}) collective-permute-start(bf16[128,1280]{1,0:T(8,128)(2,1)S(1)} %pad_maximum_fusion.9), channel_id=1, source_target_pairs={{0,1},{1,0},{2,3},{3,2},{4,5},{5,4},{6,7},{7,6},{8,9},{9,8},{10,11... | collective-permute-start | bytes 983048 | tf_op jit(solution)/shard_map/ppermute | solution.py:81
  24.5 15.0 %collective-permute-start.11 = (bf16[128,640]{1,0:T(8,128)(2,1)S(1)}, bf16[128,640]{1,0:T(8,128)(2,1)S(1)}, u32[]{:S(2)}, u32[]{:S(2)}) collective-permute-start(bf16[128,640]{1,0:T(8,128)(2,1)S(1)} %collective-permute-done.10), channel_id=1, source_target_pairs={{0,2},{1,3},{2,0},{3,1},{4,6},{5,7},{6,4},{7,5},{8,10},{9,11},{10,... | collective-permute-start | bytes 491528 | tf_op jit(solution)/shard_map/ppermute | solution.py:79
  25.6 8.2 %collective-permute-start.3 = (bf16[128,640]{1,0:T(8,128)(2,1)S(1)}, bf16[128,640]{1,0:T(8,128)(2,1)S(1)}, u32[]{:S(2)}, u32[]{:S(2)}) collective-permute-start(bf16[128,640]{1,0:T(8,128)(2,1)S(1)} %slice.57), channel_id=1, source_target_pairs={{0,2},{1,3},{2,0},{3,1},{4,6},{5,7},{6,4},{7,5},{8,10},{9,11},{10,... | collective-permute-start | bytes 491528 | tf_op jit(solution)/shard_map/ppermute | solution.py:91
  35.5 9.5 %collective-permute-start.7 = (bf16[128,1280]{1,0:T(8,128)(2,1)S(1)}, bf16[128,1280]{1,0:T(8,128)(2,1)S(1)}, u32[]{:S(2)}, u32[]{:S(2)}) collective-permute-start(bf16[128,1280]{1,0:T(8,128)(2,1)S(1)} %convolution_convert_fusion.4), channel_id=1, source_target_pairs={{0,1},{1,0},{2,3},{3,2},{4,5},{5,4},{6,7},{7,6},{8,9},{9,8},{10,11... | collective-permute-start | bytes 983048 | tf_op jit(solution)/shard_map/ppermute | solution.py:89
  35.5 8.9 %collective-permute-start.16 = (bf16[128,640]{1,0:T(8,128)(2,1)S(1)}, bf16[128,640]{1,0:T(8,128)(2,1)S(1)}, u32[]{:S(2)}, u32[]{:S(2)}) collective-permute-start(bf16[128,640]{1,0:T(8,128)(2,1)S(1)} %multiply_convert_fusion), channel_id=1, source_target_pairs={{0,12},{4,8},{8,4},{12,0},{1,13},{5,9},{9,5},{13,1},{2,14},{6,10},... | collective-permute-start | bytes 491528 | tf_op jit(solution)/shard_map/ppermute | solution.py:66
  39.5 7.3 %collective-permute-start.12 = (bf16[128,1280]{1,0:T(8,128)(2,1)S(1)}, bf16[128,1280]{1,0:T(8,128)(2,1)S(1)}, u32[]{:S(2)}, u32[]{:S(2)}) collective-permute-start(bf16[128,1280]{1,0:T(8,128)(2,1)S(1)} %pad_maximum_fusion.10), channel_id=1, source_target_pairs={{0,1},{1,0},{2,3},{3,2},{4,5},{5,4},{6,7},{7,6},{8,9},{9,8},{10,11... | collective-permute-start | bytes 983048 | tf_op jit(solution)/shard_map/ppermute | solution.py:81
  44.4 11.1 %collective-permute-start.17 = (bf16[128,640]{1,0:T(8,128)(2,1)S(1)}, bf16[128,640]{1,0:T(8,128)(2,1)S(1)}, u32[]{:S(2)}, u32[]{:S(2)}) collective-permute-start(bf16[128,640]{1,0:T(8,128)(2,1)S(1)} %collective-permute-done.16), channel_id=1, source_target_pairs={{0,2},{1,3},{2,0},{3,1},{4,6},{5,7},{6,4},{7,5},{8,10},{9,11},{10,... | collective-permute-start | bytes 491528 | tf_op jit(solution)/shard_map/ppermute | solution.py:79
  45.3 8.5 %collective-permute-start.8 = (bf16[128,640]{1,0:T(8,128)(2,1)S(1)}, bf16[128,640]{1,0:T(8,128)(2,1)S(1)}, u32[]{:S(2)}, u32[]{:S(2)}) collective-permute-start(bf16[128,640]{1,0:T(8,128)(2,1)S(1)} %slice.56), channel_id=1, source_target_pairs={{0,2},{1,3},{2,0},{3,1},{4,6},{5,7},{6,4},{7,5},{8,10},{9,11},{10,... | collective-permute-start | bytes 491528 | tf_op jit(solution)/shard_map/ppermute | solution.py:91
  55.4 1.7 %collective-permute-start.13 = (bf16[128,1280]{1,0:T(8,128)(2,1)S(1)}, bf16[128,1280]{1,0:T(8,128)(2,1)S(1)}, u32[]{:S(2)}, u32[]{:S(2)}) collective-permute-start(bf16[128,1280]{1,0:T(8,128)(2,1)S(1)} %convolution_convert_fusion.2), channel_id=1, source_target_pairs={{0,1},{1,0},{2,3},{3,2},{4,5},{5,4},{6,7},{7,6},{8,9},{9,8},{10,11... | collective-permute-start | bytes 983048 | tf_op jit(solution)/shard_map/ppermute | solution.py:89
  55.6 2.4 %collective-permute-start.18 = (bf16[128,1280]{1,0:T(8,128)(2,1)S(1)}, bf16[128,1280]{1,0:T(8,128)(2,1)S(1)}, u32[]{:S(2)}, u32[]{:S(2)}) collective-permute-start(bf16[128,1280]{1,0:T(8,128)(2,1)S(1)} %pad_maximum_fusion.11), channel_id=1, source_target_pairs={{0,1},{1,0},{2,3},{3,2},{4,5},{5,4},{6,7},{7,6},{8,9},{9,8},{10,11... | collective-permute-start | bytes 983048 | tf_op jit(solution)/shard_map/ppermute | solution.py:81
  57.5 6.3 %collective-permute-start.14 = (bf16[128,640]{1,0:T(8,128)(2,1)S(1)}, bf16[128,640]{1,0:T(8,128)(2,1)S(1)}, u32[]{:S(2)}, u32[]{:S(2)}) collective-permute-start(bf16[128,640]{1,0:T(8,128)(2,1)S(1)} %slice.55), channel_id=1, source_target_pairs={{0,2},{1,3},{2,0},{3,1},{4,6},{5,7},{6,4},{7,5},{8,10},{9,11},{10,... | collective-permute-start | bytes 491528 | tf_op jit(solution)/shard_map/ppermute | solution.py:91
  65.1 12.2 %copy-start.2 = (s32[128,1]{0,1:T(1,128)S(1)}, s32[128,1]{0,1:T(1,128)}, u32[]{:S(2)}) copy-start(s32[128,1]{0,1:T(1,128)} %param.8) | copy-start | bytes 1540
  65.5 1.7 %collective-permute-start.19 = (bf16[128,1280]{1,0:T(8,128)(2,1)S(1)}, bf16[128,1280]{1,0:T(8,128)(2,1)S(1)}, u32[]{:S(2)}, u32[]{:S(2)}) collective-permute-start(bf16[128,1280]{1,0:T(8,128)(2,1)S(1)} %convolution_convert_fusion), channel_id=1, source_target_pairs={{0,1},{1,0},{2,3},{3,2},{4,5},{5,4},{6,7},{7,6},{8,9},{9,8},{10,11... | collective-permute-start | bytes 983048 | tf_op jit(solution)/shard_map/ppermute | solution.py:89
  67.6 6.3 %collective-permute-start.20 = (bf16[128,640]{1,0:T(8,128)(2,1)S(1)}, bf16[128,640]{1,0:T(8,128)(2,1)S(1)}, u32[]{:S(2)}, u32[]{:S(2)}) collective-permute-start(bf16[128,640]{1,0:T(8,128)(2,1)S(1)} %slice.54), channel_id=1, source_target_pairs={{0,2},{1,3},{2,0},{3,1},{4,6},{5,7},{6,4},{7,5},{8,10},{9,11},{10,... | collective-permute-start | bytes 491528 | tf_op jit(solution)/shard_map/ppermute | solution.py:91
  68.0 9.3 %collective-permute-start.9 = (bf16[128,640]{1,0:T(8,128)(2,1)S(1)}, bf16[128,640]{1,0:T(8,128)(2,1)S(1)}, u32[]{:S(2)}, u32[]{:S(2)}) collective-permute-start(bf16[128,640]{1,0:T(8,128)(2,1)S(1)} %slice_add_fusion.2), channel_id=1, source_target_pairs={{0,4},{4,0},{8,12},{12,8},{1,5},{5,1},{9,13},{13,9},{2,6},{6,2},{1... | collective-permute-start | bytes 491528 | tf_op jit(solution)/shard_map/ppermute | solution.py:97
  70.4 14.8 %collective-permute-start.15 = (bf16[128,640]{1,0:T(8,128)(2,1)S(1)}, bf16[128,640]{1,0:T(8,128)(2,1)S(1)}, u32[]{:S(2)}, u32[]{:S(2)}) collective-permute-start(bf16[128,640]{1,0:T(8,128)(2,1)S(1)} %slice_add_fusion.1), channel_id=1, source_target_pairs={{0,8},{4,12},{8,0},{12,4},{1,9},{5,13},{9,1},{13,5},{2,10},{6,14},... | collective-permute-start | bytes 491528 | tf_op jit(solution)/shard_map/ppermute | solution.py:97
  73.9 11.3 %collective-permute-start.21 = (bf16[128,640]{1,0:T(8,128)(2,1)S(1)}, bf16[128,640]{1,0:T(8,128)(2,1)S(1)}, u32[]{:S(2)}, u32[]{:S(2)}) collective-permute-start(bf16[128,640]{1,0:T(8,128)(2,1)S(1)} %fusion.7), channel_id=1, source_target_pairs={{0,12},{4,8},{8,4},{12,0},{1,13},{5,9},{9,5},{13,1},{2,14},{6,10},... | collective-permute-start | bytes 491528 | tf_op jit(solution)/shard_map/ppermute | solution.py:97

commit v10 on v8

--- a/solution.py
+++ b/solution.py
@@ -70,7 +70,7 @@
     up_w = _slots(up_weight[0], t, width, 0)
     down_keep = _slots(down_weight[0], t, width, 1, _ORDER[:2])
     down_send = _slots(down_weight[0], t, width, 1, _ORDER[2:])
-    waves = [[k] for k in range(n_expert)]
+    waves = [[k] for k in [0] + list(range(2, n_expert)) + [1][:n_expert - 1]]
     total = None
     previous = None
     for wave in waves:

time: 67.3 us -> 67 us (level)
    ppermute x4, waiting for transfers between devices: 4.83 us -> 9.45 us  [gathered(): lax.ppermute(piece, 'tensor', _xor_pairs(n_tensor, 2))]
    ppermute x3, waiting for transfers between devices: 8.84 us -> 5.58 us  [gathered(): lax.ppermute(part.astype(jnp.bfloat16), 'expert', _xor_pairs(n_expert, k))]
    ppermute x3, waiting for transfers between devices: 7.07 us -> 5.9 us  [gathered(): lax.ppermute(scaled, 'expert', _xor_pairs(n_expert, k))]
  transfers between devices with their start and end apart: 22 -> 22, of which waited for: 9 -> 12; matrix products, arithmetic and copies ran while one was open for 19% -> 19% of each run, Pallas kernels for 0% -> 0%
where the time goes in v10:
time: 67 us; the launch traced here: 66.8 us
  waiting for transfers between devices  28.5 us (43%)
  starting transfers between devices  21.1 us (31%)
  matrix products  9.28 us (14%)
  local copies, waits for them, and re-layouts  5.18 us (8%)
  other arithmetic  2.46 us (4%)
    ppermute x4, waiting for transfers between devices, gathered(): lax.ppermute(piece, 'tensor', _xor_pairs(n_tensor, 2))  9.45 us
    ppermute x3, waiting for transfers between devices, gathered(): lax.ppermute(scaled, 'expert', _xor_pairs(n_expert, k))  5.9 us
    ppermute x3, waiting for transfers between devices, gathered(): lax.ppermute(part.astype(jnp.bfloat16), 'expert', _xor_pairs(n_expert, k))  5.58 us
    ppermute x4, starting transfers between devices, gathered(): lax.ppermute(piece, 'tensor', _xor_pairs(n_tensor, 2))  5.55 us
    ppermute x3, starting transfers between devices, gathered(): lax.ppermute(part.astype(jnp.bfloat16), 'expert', _xor_pairs(n_expert, k))  5.53 us
    ppermute x4, waiting for transfers between devices, gathered(): lax.ppermute(over_c[:, width:].astype(jnp.bfloat16), 'tensor', _xor_pairs...  5.05 us
    ppermute x3, starting transfers between devices, gathered(): lax.ppermute(scaled, 'expert', _xor_pairs(n_expert, k))  4.17 us
    ppermute x4, starting transfers between devices, gathered(): lax.ppermute(over_c[:, width:].astype(jnp.bfloat16), 'tensor', _xor_pairs...  3.82 us
  transfers between devices with their start and end apart: 22, of which 12 were waited for; matrix products, arithmetic and copies ran while one was open for 19% of the time, Pallas kernels for 0%

profile of v10, /device:TPU:0, one launch (start us, length us, event | category | flops | bytes accessed | tf_op | source)
XLA Modules:
  0.0 66.8 jit_solution(694309491824602760)
XLA Ops:
  0.0 1.0 %multiply_convert_fusion = bf16[128,640]{1,0:T(8,128)(2,1)S(1)} fusion(bf16[128,640]{1,0:T(8,128)(2,1)} %param.6, f32[128]{0:T(128)} %param.7), kind=kLoop, calls=%fused_computation.59 | loop fusion | flops 245760 | bytes 328192 | tf_op jit(solution)/shard_map/convert_element_type | solution.py:64
  1.0 3.0 %collective-permute-start = (bf16[128,640]{1,0:T(8,128)(2,1)S(1)}, bf16[128,640]{1,0:T(8,128)(2,1)S(1)}, u32[]{:S(2)}, u32[]{:S(2)}) collective-permute-start(bf16[128,640]{1,0:T(8,128)(2,1)S(1)} %multiply_convert_fusion), channel_id=1, source_target_pairs={{0,2},{1,3},{2,0},{3,1},{4,6},{5,7},{6,4},{7,5},{8,10},{9,11},{10,... | collective-permute-start | bytes 491528 | tf_op jit(solution)/shard_map/ppermute | solution.py:79
  4.0 2.6 %collective-permute-start.4 = (bf16[128,640]{1,0:T(8,128)(2,1)S(1)}, bf16[128,640]{1,0:T(8,128)(2,1)S(1)}, u32[]{:S(2)}, u32[]{:S(2)}) collective-permute-start(bf16[128,640]{1,0:T(8,128)(2,1)S(1)} %multiply_convert_fusion), channel_id=1, source_target_pairs={{0,8},{4,12},{8,0},{12,4},{1,9},{5,13},{9,1},{13,5},{2,10},{6,14},... | collective-permute-start | bytes 491528 | tf_op jit(solution)/shard_map/ppermute | solution.py:66
  6.6 1.3 %collective-permute-start.10 = (bf16[128,640]{1,0:T(8,128)(2,1)S(1)}, bf16[128,640]{1,0:T(8,128)(2,1)S(1)}, u32[]{:S(2)}, u32[]{:S(2)}) collective-permute-start(bf16[128,640]{1,0:T(8,128)(2,1)S(1)} %multiply_convert_fusion), channel_id=1, source_target_pairs={{0,12},{4,8},{8,4},{12,0},{1,13},{5,9},{9,5},{13,1},{2,14},{6,10},... | collective-permute-start | bytes 491528 | tf_op jit(solution)/shard_map/ppermute | solution.py:66
  8.2 2.0 %dynamic-slice_bitcast_fusion.11 = (bf16[640,512]{1,0:T(8,128)(2,1)S(1)}, bf16[640,512]{1,0:T(8,128)(2,1)S(1)}, bf16[640,512]{1,0:T(8,128)(2,1)S(1)}, bf16[640,512]{1,0:T(8,128)(2,1)S(1)}) fusion(bf16[1,2560,512]{2,1,0:T(8,128)(2,1)} %param.9, s32[]{:T(128)S(6)} %select_n.48, s32[]{:T(128)S(6)} %select_n.49, s32[]{:T(128)S(6)} %select_n.51, s32[]{:T(128)S(6)} %select_n.50), kind=kLoop, calls=%fused_computation.38 | loop fusion | bytes 5242896 | tf_op jit(solution)/shard_map/dynamic_slice | solution.py:55
  10.2 0.5 copy-done
  11.1 1.5 %copy-done.1 = bf16[1,512,2560]{2,1,0:T(8,128)(2,1)S(1)} copy-done((bf16[1,512,2560]{2,1,0:T(8,128)(2,1)S(1)}, bf16[1,512,2560]{2,1,0:T(8,128)(2,1)}, u32[]{:S(2)}) %copy-start.1) | copy-done | bytes 2621464
  12.9 5.9 %collective-permute-done.4 = bf16[128,640]{1,0:T(8,128)(2,1)S(1)} collective-permute-done((bf16[128,640]{1,0:T(8,128)(2,1)S(1)}, bf16[128,640]{1,0:T(8,128)(2,1)S(1)}, u32[]{:S(2)}, u32[]{:S(2)}) %collective-permute-start.4) | collective-permute-done | bytes 163872 | tf_op jit(solution)/shard_map/ppermute | solution.py:66
  18.8 0.5 collective-permute-start.5
  19.3 1.6 %collective-permute-start.11 = (bf16[128,640]{1,0:T(8,128)(2,1)S(1)}, bf16[128,640]{1,0:T(8,128)(2,1)S(1)}, u32[]{:S(2)}, u32[]{:S(2)}) collective-permute-start(bf16[128,640]{1,0:T(8,128)(2,1)S(1)} %collective-permute-done.10), channel_id=1, source_target_pairs={{0,2},{1,3},{2,0},{3,1},{4,6},{5,7},{6,4},{7,5},{8,10},{9,11},{10,... | collective-permute-start | bytes 491528 | tf_op jit(solution)/shard_map/ppermute | solution.py:79
  21.0 0.5 collective-permute-start.17
  21.4 4.3 %collective-permute-done.5 = bf16[128,640]{1,0:T(8,128)(2,1)S(1)} collective-permute-done((bf16[128,640]{1,0:T(8,128)(2,1)S(1)}, bf16[128,640]{1,0:T(8,128)(2,1)S(1)}, u32[]{:S(2)}, u32[]{:S(2)}) %collective-permute-start.5) | collective-permute-done | bytes 163872 | tf_op jit(solution)/shard_map/ppermute | solution.py:79
  25.8 3.4 %collective-permute-done.11 = bf16[128,640]{1,0:T(8,128)(2,1)S(1)} collective-permute-done((bf16[128,640]{1,0:T(8,128)(2,1)S(1)}, bf16[128,640]{1,0:T(8,128)(2,1)S(1)}, u32[]{:S(2)}, u32[]{:S(2)}) %collective-permute-start.11) | collective-permute-done | bytes 163872 | tf_op jit(solution)/shard_map/ppermute | solution.py:79
  29.3 1.8 %collective-permute-done.17 = bf16[128,640]{1,0:T(8,128)(2,1)S(1)} collective-permute-done((bf16[128,640]{1,0:T(8,128)(2,1)S(1)}, bf16[128,640]{1,0:T(8,128)(2,1)S(1)}, u32[]{:S(2)}, u32[]{:S(2)}) %collective-permute-start.17) | collective-permute-done | bytes 163872 | tf_op jit(solution)/shard_map/ppermute | solution.py:79
  31.2 0.5 fusion.13
  31.7 0.5 multiply_convert_fusion.1
  32.3 0.3 convolution_convert_fusion.6
  32.6 0.5 collective-permute-start.2
  33.2 1.2 %collective-permute-done.2 = bf16[128,1280]{1,0:T(8,128)(2,1)S(1)} collective-permute-done((bf16[128,1280]{1,0:T(8,128)(2,1)S(1)}, bf16[128,1280]{1,0:T(8,128)(2,1)S(1)}, u32[]{:S(2)}, u32[]{:S(2)}) %collective-permute-start.2) | collective-permute-done | bytes 327712 | tf_op jit(solution)/shard_map/ppermute | solution.py:90
  34.8 0.5 fusion.16
  35.3 0.7 %fusion.1 = bf16[128,512]{1,0:T(8,128)(2,1)S(1)} fusion(bf16[128,2560]{1,0:T(8,128)(2,1)S(1)} %pad_maximum_fusion.5, f32[128,512]{1,0:T(8,128)S(1)} %fusion.16, bf16[640,512]{1,0:T(8,128)(2,1)S(1)} %get-tuple-element.17, bf16[640,512]{1,0:T(8,128)(2,1)S(1)} %get-tuple-element.18, bf16[640,512]{1,0:T(8,128)(2,1)S(1)} %get-tuple-element.16, ...), kind=kOutput, calls=%fused_computation.16 | convolution fusion | flops 346423296 | bytes 3670016 | tf_op jit(solution)/shard_map/dot_general | solution.py:85
  36.0 0.3 convolution_convert_fusion.4
  36.4 0.4 collective-permute-start.7
  36.9 1.2 %collective-permute-done.7 = bf16[128,1280]{1,0:T(8,128)(2,1)S(1)} collective-permute-done((bf16[128,1280]{1,0:T(8,128)(2,1)S(1)}, bf16[128,1280]{1,0:T(8,128)(2,1)S(1)}, u32[]{:S(2)}, u32[]{:S(2)}) %collective-permute-start.7) | collective-permute-done | bytes 327712 | tf_op jit(solution)/shard_map/ppermute | solution.py:90
  38.1 0.3 convert_add_fusion.2
  38.4 0.5 fusion.17
  38.9 0.7 %fusion.2 = bf16[128,512]{1,0:T(8,128)(2,1)S(1)} fusion(bf16[128,2560]{1,0:T(8,128)(2,1)S(1)} %pad_maximum_fusion.6, f32[128,512]{1,0:T(8,128)S(1)} %fusion.17, bf16[640,512]{1,0:T(8,128)(2,1)S(1)} %get-tuple-element.17, bf16[640,512]{1,0:T(8,128)(2,1)S(1)} %get-tuple-element.18, bf16[640,512]{1,0:T(8,128)(2,1)S(1)} %get-tuple-element.16, ...), kind=kOutput, calls=%fused_computation.17 | convolution fusion | flops 346423296 | bytes 3670016 | tf_op jit(solution)/shard_map/dot_general | solution.py:85
  39.7 0.3 convolution_convert_fusion.2
  40.0 0.4 collective-permute-start.13
  40.5 0.7 %slice.70 = bf16[128,640]{1,0:T(8,128)(2,1)} slice(f32[128,1280]{1,0:T(8,128)S(1)} %convert_add_fusion.2), slice={[0:128], [640:1280]} | slice | bytes 327680 | tf_op jit(solution)/shard_map/slice | solution.py:93
  41.2 0.5 collective-permute-start.8
  41.7 0.3 convert_add_fusion.1
  42.1 0.5 fusion.18
  42.6 0.7 %fusion.3 = bf16[128,512]{1,0:T(8,128)(2,1)S(1)} fusion(bf16[128,2560]{1,0:T(8,128)(2,1)S(1)} %pad_maximum_fusion.7, f32[128,512]{1,0:T(8,128)S(1)} %fusion.18, bf16[640,512]{1,0:T(8,128)(2,1)S(1)} %get-tuple-element.17, bf16[640,512]{1,0:T(8,128)(2,1)S(1)} %get-tuple-element.18, bf16[640,512]{1,0:T(8,128)(2,1)S(1)} %get-tuple-element.16, ...), kind=kOutput, calls=%fused_computation.18 | convolution fusion | flops 346423296 | bytes 3670016 | tf_op jit(solution)/shard_map/dot_general | solution.py:85
  43.4 1.1 %convolution_convert_fusion = bf16[128,1280]{1,0:T(8,128)(2,1)} fusion(bf16[128,512]{1,0:T(8,128)(2,1)S(1)} %fusion.3, bf16[512,640]{1,0:T(8,128)(2,1)S(1)} %get-tuple-element.13, bf16[512,640]{1,0:T(8,128)(2,1)S(1)} %get-tuple-element.14), kind=kOutput, calls=%fused_computation.2 | convolution fusion | flops 170557440 | bytes 1769472 | tf_op jit(solution)/shard_map/dot_general | solution.py:88
  44.4 0.4 collective-permute-start.19
  44.8 1.2 %collective-permute-start.3 = (bf16[128,640]{1,0:T(8,128)(2,1)S(1)}, bf16[128,640]{1,0:T(8,128)(2,1)S(1)}, u32[]{:S(2)}, u32[]{:S(2)}) collective-permute-start(bf16[128,640]{1,0:T(8,128)(2,1)S(1)} %slice.71), channel_id=1, source_target_pairs={{0,2},{1,3},{2,0},{3,1},{4,6},{5,7},{6,4},{7,5},{8,10},{9,11},{10,... | collective-permute-start | bytes 491528 | tf_op jit(solution)/shard_map/ppermute | solution.py:92
  46.0 1.6 %collective-permute-done.8 = bf16[128,640]{1,0:T(8,128)(2,1)S(1)} collective-permute-done((bf16[128,640]{1,0:T(8,128)(2,1)}, bf16[128,640]{1,0:T(8,128)(2,1)S(1)}, u32[]{:S(2)}, u32[]{:S(2)}) %collective-permute-start.8) | collective-permute-done | bytes 163872 | tf_op jit(solution)/shard_map/ppermute | solution.py:92
  47.7 2.4 %collective-permute-start.9 = (bf16[128,640]{1,0:T(8,128)(2,1)S(1)}, bf16[128,640]{1,0:T(8,128)(2,1)S(1)}, u32[]{:S(2)}, u32[]{:S(2)}) collective-permute-start(bf16[128,640]{1,0:T(8,128)(2,1)S(1)} %fusion.6), channel_id=1, source_target_pairs={{0,8},{4,12},{8,0},{12,4},{1,9},{5,13},{9,1},{13,5},{2,10},{6,14},... | collective-permute-start | bytes 491528 | tf_op jit(solution)/shard_map/ppermute | solution.py:97
  50.1 0.6 collective-permute-start.14
  50.7 1.4 %convert_add_fusion = f32[128,1280]{1,0:T(8,128)S(1)} fusion(bf16[128,1280]{1,0:T(8,128)(2,1)} %collective-permute-done.19, bf16[128,512]{1,0:T(8,128)(2,1)} %copy-done.3, bf16[512,640]{1,0:T(8,128)(2,1)S(1)} %get-tuple-element.12, bf16[512,640]{1,0:T(8,128)(2,1)S(1)} %get-tuple-element.11), kind=kOutput, calls=%fused_computation.23 | convolution fusion | flops 171048960 | bytes 2424832 | tf_op jit(solution)/shard_map/dot_general | solution.py:87
  52.1 1.6 %collective-permute-start.20 = (bf16[128,640]{1,0:T(8,128)(2,1)S(1)}, bf16[128,640]{1,0:T(8,128)(2,1)S(1)}, u32[]{:S(2)}, u32[]{:S(2)}) collective-permute-start(bf16[128,640]{1,0:T(8,128)(2,1)S(1)} %slice.68), channel_id=1, source_target_pairs={{0,2},{1,3},{2,0},{3,1},{4,6},{5,7},{6,4},{7,5},{8,10},{9,11},{10,... | collective-permute-start | bytes 491528 | tf_op jit(solution)/shard_map/ppermute | solution.py:92
  53.7 3.4 %collective-permute-done.14 = bf16[128,640]{1,0:T(8,128)(2,1)S(1)} collective-permute-done((bf16[128,640]{1,0:T(8,128)(2,1)S(1)}, bf16[128,640]{1,0:T(8,128)(2,1)S(1)}, u32[]{:S(2)}, u32[]{:S(2)}) %collective-permute-start.14) | collective-permute-done | bytes 163872 | tf_op jit(solution)/shard_map/ppermute | solution.py:92
  57.1 1.7 %collective-permute-start.15 = (bf16[128,640]{1,0:T(8,128)(2,1)S(1)}, bf16[128,640]{1,0:T(8,128)(2,1)S(1)}, u32[]{:S(2)}, u32[]{:S(2)}) collective-permute-start(bf16[128,640]{1,0:T(8,128)(2,1)S(1)} %fusion.5), channel_id=1, source_target_pairs={{0,12},{4,8},{8,4},{12,0},{1,13},{5,9},{9,5},{13,1},{2,14},{6,10},... | collective-permute-start | bytes 491528 | tf_op jit(solution)/shard_map/ppermute | solution.py:97
  58.8 1.5 %collective-permute-start.21 = (bf16[128,640]{1,0:T(8,128)(2,1)S(1)}, bf16[128,640]{1,0:T(8,128)(2,1)S(1)}, u32[]{:S(2)}, u32[]{:S(2)}) collective-permute-start(bf16[128,640]{1,0:T(8,128)(2,1)S(1)} %fusion.4), channel_id=1, source_target_pairs={{0,4},{4,0},{8,12},{12,8},{1,5},{5,1},{9,13},{13,9},{2,6},{6,2},{1... | collective-permute-start | bytes 491528 | tf_op jit(solution)/shard_map/ppermute | solution.py:97
  60.4 5.0 %collective-permute-done.15 = bf16[128,640]{1,0:T(8,128)(2,1)S(1)} collective-permute-done((bf16[128,640]{1,0:T(8,128)(2,1)S(1)}, bf16[128,640]{1,0:T(8,128)(2,1)S(1)}, u32[]{:S(2)}, u32[]{:S(2)}) %collective-permute-start.15) | collective-permute-done | bytes 163872 | tf_op jit(solution)/shard_map/ppermute | solution.py:97
  65.4 0.6 collective-permute-done.21
  66.0 0.9 %fusion.11 = bf16[128,640]{1,0:T(8,128)(2,1)} fusion(f32[128,1280]{1,0:T(8,128)S(1)} %convert_add_fusion.3, bf16[128,640]{1,0:T(8,128)(2,1)S(1)} %collective-permute-done.21, bf16[128,640]{1,0:T(8,128)(2,1)S(1)} %collective-permute-done.15, bf16[128,640]{1,0:T(8,128)(2,1)S(1)} %collective-permute-done.9, bf16[128,640]{1,0:T(8,128)(2,1)S(1)} %collective-permute-done.3, ...), kind=kLoop, calls=%fused_computation.54 | loop fusion | flops 1064960 | bytes 1147392 | tf_op jit(solution)/shard_map/convert_element_type | solution.py:101
  (41 shorter events, 2.1 us)
Async XLA Ops:
  1.0 18.2 %collective-permute-start = (bf16[128,640]{1,0:T(8,128)(2,1)S(1)}, bf16[128,640]{1,0:T(8,128)(2,1)S(1)}, u32[]{:S(2)}, u32[]{:S(2)}) collective-permute-start(bf16[128,640]{1,0:T(8,128)(2,1)S(1)} %multiply_convert_fusion), channel_id=1, source_target_pairs={{0,2},{1,3},{2,0},{3,1},{4,6},{5,7},{6,4},{7,5},{8,10},{9,11},{10,... | collective-permute-start | bytes 491528 | tf_op jit(solution)/shard_map/ppermute | solution.py:79
  4.0 14.7 %collective-permute-start.4 = (bf16[128,640]{1,0:T(8,128)(2,1)S(1)}, bf16[128,640]{1,0:T(8,128)(2,1)S(1)}, u32[]{:S(2)}, u32[]{:S(2)}) collective-permute-start(bf16[128,640]{1,0:T(8,128)(2,1)S(1)} %multiply_convert_fusion), channel_id=1, source_target_pairs={{0,8},{4,12},{8,0},{12,4},{1,9},{5,13},{9,1},{13,5},{2,10},{6,14},... | collective-permute-start | bytes 491528 | tf_op jit(solution)/shard_map/ppermute | solution.py:66
  6.6 12.7 %collective-permute-start.10 = (bf16[128,640]{1,0:T(8,128)(2,1)S(1)}, bf16[128,640]{1,0:T(8,128)(2,1)S(1)}, u32[]{:S(2)}, u32[]{:S(2)}) collective-permute-start(bf16[128,640]{1,0:T(8,128)(2,1)S(1)} %multiply_convert_fusion), channel_id=1, source_target_pairs={{0,12},{4,8},{8,4},{12,0},{1,13},{5,9},{9,5},{13,1},{2,14},{6,10},... | collective-permute-start | bytes 491528 | tf_op jit(solution)/shard_map/ppermute | solution.py:66
  8.0 13.0 %collective-permute-start.16 = (bf16[128,640]{1,0:T(8,128)(2,1)S(1)}, bf16[128,640]{1,0:T(8,128)(2,1)S(1)}, u32[]{:S(2)}, u32[]{:S(2)}) collective-permute-start(bf16[128,640]{1,0:T(8,128)(2,1)S(1)} %multiply_convert_fusion), channel_id=1, source_target_pairs={{0,4},{4,0},{8,12},{12,8},{1,5},{5,1},{9,13},{13,9},{2,6},{6,2},{1... | collective-permute-start | bytes 491528 | tf_op jit(solution)/shard_map/ppermute | solution.py:66
  8.2 2.5 %copy-start = (bf16[1,2560,512]{2,1,0:T(8,128)(2,1)S(1)}, bf16[1,2560,512]{2,1,0:T(8,128)(2,1)}, u32[]{:S(2)}) copy-start(bf16[1,2560,512]{2,1,0:T(8,128)(2,1)} %param.10) | copy-start | bytes 7864324
  10.9 1.7 %copy-start.1 = (bf16[1,512,2560]{2,1,0:T(8,128)(2,1)S(1)}, bf16[1,512,2560]{2,1,0:T(8,128)(2,1)}, u32[]{:S(2)}) copy-start(bf16[1,512,2560]{2,1,0:T(8,128)(2,1)} %param.11) | copy-start | bytes 7864324
  18.8 7.0 %collective-permute-start.5 = (bf16[128,640]{1,0:T(8,128)(2,1)S(1)}, bf16[128,640]{1,0:T(8,128)(2,1)S(1)}, u32[]{:S(2)}, u32[]{:S(2)}) collective-permute-start(bf16[128,640]{1,0:T(8,128)(2,1)S(1)} %collective-permute-done.4), channel_id=1, source_target_pairs={{0,2},{1,3},{2,0},{3,1},{4,6},{5,7},{6,4},{7,5},{8,10},{9,11},{10,... | collective-permute-start | bytes 491528 | tf_op jit(solution)/shard_map/ppermute | solution.py:79
  19.3 12.0 %collective-permute-start.1 = (bf16[128,1280]{1,0:T(8,128)(2,1)S(1)}, bf16[128,1280]{1,0:T(8,128)(2,1)S(1)}, u32[]{:S(2)}, u32[]{:S(2)}) collective-permute-start(bf16[128,1280]{1,0:T(8,128)(2,1)S(1)} %pad_maximum_fusion.8), channel_id=1, source_target_pairs={{0,1},{1,0},{2,3},{3,2},{4,5},{5,4},{6,7},{7,6},{8,9},{9,8},{10,11... | collective-permute-start | bytes 983048 | tf_op jit(solution)/shard_map/ppermute | solution.py:81
  19.3 9.9 %collective-permute-start.11 = (bf16[128,640]{1,0:T(8,128)(2,1)S(1)}, bf16[128,640]{1,0:T(8,128)(2,1)S(1)}, u32[]{:S(2)}, u32[]{:S(2)}) collective-permute-start(bf16[128,640]{1,0:T(8,128)(2,1)S(1)} %collective-permute-done.10), channel_id=1, source_target_pairs={{0,2},{1,3},{2,0},{3,1},{4,6},{5,7},{6,4},{7,5},{8,10},{9,11},{10,... | collective-permute-start | bytes 491528 | tf_op jit(solution)/shard_map/ppermute | solution.py:79
  21.0 10.1 %collective-permute-start.17 = (bf16[128,640]{1,0:T(8,128)(2,1)S(1)}, bf16[128,640]{1,0:T(8,128)(2,1)S(1)}, u32[]{:S(2)}, u32[]{:S(2)}) collective-permute-start(bf16[128,640]{1,0:T(8,128)(2,1)S(1)} %collective-permute-done.16), channel_id=1, source_target_pairs={{0,2},{1,3},{2,0},{3,1},{4,6},{5,7},{6,4},{7,5},{8,10},{9,11},{10,... | collective-permute-start | bytes 491528 | tf_op jit(solution)/shard_map/ppermute | solution.py:79
  25.8 7.4 %collective-permute-start.6 = (bf16[128,1280]{1,0:T(8,128)(2,1)S(1)}, bf16[128,1280]{1,0:T(8,128)(2,1)S(1)}, u32[]{:S(2)}, u32[]{:S(2)}) collective-permute-start(bf16[128,1280]{1,0:T(8,128)(2,1)S(1)} %pad_maximum_fusion.9), channel_id=1, source_target_pairs={{0,1},{1,0},{2,3},{3,2},{4,5},{5,4},{6,7},{7,6},{8,9},{9,8},{10,11... | collective-permute-start | bytes 983048 | tf_op jit(solution)/shard_map/ppermute | solution.py:81
  29.3 7.6 %collective-permute-start.12 = (bf16[128,1280]{1,0:T(8,128)(2,1)S(1)}, bf16[128,1280]{1,0:T(8,128)(2,1)S(1)}, u32[]{:S(2)}, u32[]{:S(2)}) collective-permute-start(bf16[128,1280]{1,0:T(8,128)(2,1)S(1)} %pad_maximum_fusion.10), channel_id=1, source_target_pairs={{0,1},{1,0},{2,3},{3,2},{4,5},{5,4},{6,7},{7,6},{8,9},{9,8},{10,11... | collective-permute-start | bytes 983048 | tf_op jit(solution)/shard_map/ppermute | solution.py:81
  31.1 9.3 %collective-permute-start.18 = (bf16[128,1280]{1,0:T(8,128)(2,1)S(1)}, bf16[128,1280]{1,0:T(8,128)(2,1)S(1)}, u32[]{:S(2)}, u32[]{:S(2)}) collective-permute-start(bf16[128,1280]{1,0:T(8,128)(2,1)S(1)} %pad_maximum_fusion.11), channel_id=1, source_target_pairs={{0,1},{1,0},{2,3},{3,2},{4,5},{5,4},{6,7},{7,6},{8,9},{9,8},{10,11... | collective-permute-start | bytes 983048 | tf_op jit(solution)/shard_map/ppermute | solution.py:81
  32.6 1.8 %collective-permute-start.2 = (bf16[128,1280]{1,0:T(8,128)(2,1)S(1)}, bf16[128,1280]{1,0:T(8,128)(2,1)S(1)}, u32[]{:S(2)}, u32[]{:S(2)}) collective-permute-start(bf16[128,1280]{1,0:T(8,128)(2,1)S(1)} %convolution_convert_fusion.6), channel_id=1, source_target_pairs={{0,1},{1,0},{2,3},{3,2},{4,5},{5,4},{6,7},{7,6},{8,9},{9,8},{10,11... | collective-permute-start | bytes 983048 | tf_op jit(solution)/shard_map/ppermute | solution.py:90
  36.4 1.7 %collective-permute-start.7 = (bf16[128,1280]{1,0:T(8,128)(2,1)S(1)}, bf16[128,1280]{1,0:T(8,128)(2,1)S(1)}, u32[]{:S(2)}, u32[]{:S(2)}) collective-permute-start(bf16[128,1280]{1,0:T(8,128)(2,1)S(1)} %convolution_convert_fusion.4), channel_id=1, source_target_pairs={{0,1},{1,0},{2,3},{3,2},{4,5},{5,4},{6,7},{7,6},{8,9},{9,8},{10,11... | collective-permute-start | bytes 983048 | tf_op jit(solution)/shard_map/ppermute | solution.py:90
  40.0 1.7 %collective-permute-start.13 = (bf16[128,1280]{1,0:T(8,128)(2,1)S(1)}, bf16[128,1280]{1,0:T(8,128)(2,1)S(1)}, u32[]{:S(2)}, u32[]{:S(2)}) collective-permute-start(bf16[128,1280]{1,0:T(8,128)(2,1)S(1)} %convolution_convert_fusion.2), channel_id=1, source_target_pairs={{0,1},{1,0},{2,3},{3,2},{4,5},{5,4},{6,7},{7,6},{8,9},{9,8},{10,11... | collective-permute-start | bytes 983048 | tf_op jit(solution)/shard_map/ppermute | solution.py:90
  41.2 6.5 %collective-permute-start.8 = (bf16[128,640]{1,0:T(8,128)(2,1)}, bf16[128,640]{1,0:T(8,128)(2,1)S(1)}, u32[]{:S(2)}, u32[]{:S(2)}) collective-permute-start(bf16[128,640]{1,0:T(8,128)(2,1)} %slice.70), channel_id=1, source_target_pairs={{0,2},{1,3},{2,0},{3,1},{4,6},{5,7},{6,4},{7,5},{8,10},{9,11},{10,... | collective-permute-start | bytes 491528 | tf_op jit(solution)/shard_map/ppermute | solution.py:92
  43.3 1.1 %copy-start.3 = (bf16[128,512]{1,0:T(8,128)(2,1)}, bf16[128,512]{1,0:T(8,128)(2,1)S(1)}, u32[]{:S(2)}) copy-start(bf16[128,512]{1,0:T(8,128)(2,1)S(1)} %fusion.3) | copy-start | bytes 393220
  44.4 6.2 %collective-permute-start.19 = (bf16[128,1280]{1,0:T(8,128)(2,1)}, bf16[128,1280]{1,0:T(8,128)(2,1)}, u32[]{:S(2)}, u32[]{:S(2)}) collective-permute-start(bf16[128,1280]{1,0:T(8,128)(2,1)} %convolution_convert_fusion), channel_id=1, source_target_pairs={{0,1},{1,0},{2,3},{3,2},{4,5},{5,4},{6,7},{7,6},{8,9},{9,8},{10,11... | collective-permute-start | bytes 983048 | tf_op jit(solution)/shard_map/ppermute | solution.py:90
  44.8 15.5 %copy-start.2 = (s32[128,1]{0,1:T(1,128)S(1)}, s32[128,1]{0,1:T(1,128)}, u32[]{:S(2)}) copy-start(s32[128,1]{0,1:T(1,128)} %param.8) | copy-start | bytes 1540
  44.8 15.5 %collective-permute-start.3 = (bf16[128,640]{1,0:T(8,128)(2,1)S(1)}, bf16[128,640]{1,0:T(8,128)(2,1)S(1)}, u32[]{:S(2)}, u32[]{:S(2)}) collective-permute-start(bf16[128,640]{1,0:T(8,128)(2,1)S(1)} %slice.71), channel_id=1, source_target_pairs={{0,2},{1,3},{2,0},{3,1},{4,6},{5,7},{6,4},{7,5},{8,10},{9,11},{10,... | collective-permute-start | bytes 491528 | tf_op jit(solution)/shard_map/ppermute | solution.py:92
  47.7 12.7 %collective-permute-start.9 = (bf16[128,640]{1,0:T(8,128)(2,1)S(1)}, bf16[128,640]{1,0:T(8,128)(2,1)S(1)}, u32[]{:S(2)}, u32[]{:S(2)}) collective-permute-start(bf16[128,640]{1,0:T(8,128)(2,1)S(1)} %fusion.6), channel_id=1, source_target_pairs={{0,8},{4,12},{8,0},{12,4},{1,9},{5,13},{9,1},{13,5},{2,10},{6,14},... | collective-permute-start | bytes 491528 | tf_op jit(solution)/shard_map/ppermute | solution.py:97
  50.1 6.9 %collective-permute-start.14 = (bf16[128,640]{1,0:T(8,128)(2,1)S(1)}, bf16[128,640]{1,0:T(8,128)(2,1)S(1)}, u32[]{:S(2)}, u32[]{:S(2)}) collective-permute-start(bf16[128,640]{1,0:T(8,128)(2,1)S(1)} %slice.69), channel_id=1, source_target_pairs={{0,2},{1,3},{2,0},{3,1},{4,6},{5,7},{6,4},{7,5},{8,10},{9,11},{10,... | collective-permute-start | bytes 491528 | tf_op jit(solution)/shard_map/ppermute | solution.py:92
  52.1 6.7 %collective-permute-start.20 = (bf16[128,640]{1,0:T(8,128)(2,1)S(1)}, bf16[128,640]{1,0:T(8,128)(2,1)S(1)}, u32[]{:S(2)}, u32[]{:S(2)}) collective-permute-start(bf16[128,640]{1,0:T(8,128)(2,1)S(1)} %slice.68), channel_id=1, source_target_pairs={{0,2},{1,3},{2,0},{3,1},{4,6},{5,7},{6,4},{7,5},{8,10},{9,11},{10,... | collective-permute-start | bytes 491528 | tf_op jit(solution)/shard_map/ppermute | solution.py:92
  57.1 8.3 %collective-permute-start.15 = (bf16[128,640]{1,0:T(8,128)(2,1)S(1)}, bf16[128,640]{1,0:T(8,128)(2,1)S(1)}, u32[]{:S(2)}, u32[]{:S(2)}) collective-permute-start(bf16[128,640]{1,0:T(8,128)(2,1)S(1)} %fusion.5), channel_id=1, source_target_pairs={{0,12},{4,8},{8,4},{12,0},{1,13},{5,9},{9,5},{13,1},{2,14},{6,10},... | collective-permute-start | bytes 491528 | tf_op jit(solution)/shard_map/ppermute | solution.py:97
  58.8 7.1 %collective-permute-start.21 = (bf16[128,640]{1,0:T(8,128)(2,1)S(1)}, bf16[128,640]{1,0:T(8,128)(2,1)S(1)}, u32[]{:S(2)}, u32[]{:S(2)}) collective-permute-start(bf16[128,640]{1,0:T(8,128)(2,1)S(1)} %fusion.4), channel_id=1, source_target_pairs={{0,4},{4,0},{8,12},{12,8},{1,5},{5,1},{9,13},{13,9},{2,6},{6,2},{1... | collective-permute-start | bytes 491528 | tf_op jit(solution)/shard_map/ppermute | solution.py:97

commit v11 on v10

--- a/solution.py
+++ b/solution.py
@@ -62,15 +62,18 @@
     me = lax.axis_index("expert")
     t = lax.axis_index("tensor")
     scaled = (tokens.astype(jnp.float32) * route_scale[:, None]).astype(jnp.bfloat16)
-    blocks = [scaled] + [
-        lax.ppermute(scaled, "expert", _xor_pairs(n_expert, k)) for k in range(1, n_expert)
-    ]
     routed = expert_ids[:, 0][:, None]
     gate_w = _slots(gate_weight[0], t, width, 0)
     up_w = _slots(up_weight[0], t, width, 0)
     down_keep = _slots(down_weight[0], t, width, 1, _ORDER[:2])
     down_send = _slots(down_weight[0], t, width, 1, _ORDER[2:])
     waves = [[k] for k in [0] + list(range(2, n_expert)) + [1][:n_expert - 1]]
+    blocks = {0: scaled}
+    source = scaled
+    for wave in waves[1:]:
+        k = wave[0]
+        blocks[k] = lax.ppermute(source, "expert", _xor_pairs(n_expert, k))
+        source, _ = lax.optimization_barrier((scaled, blocks[k]))
     total = None
     previous = None
     for wave in waves:

time: 67 us -> 67.2 us (level)
  starting transfers between devices: 21.1 us -> 25.9 us
  waiting for transfers between devices: 28.5 us -> 24.4 us
    ppermute x3, starting transfers between devices: 4.17 us -> 8.53 us  [gathered(): blocks[k] = lax.ppermute(source, 'expert', _xor_pairs(n_expert, k))]
    ppermute x4, waiting for transfers between devices: 9.45 us -> 5.67 us  [gathered(): lax.ppermute(piece, 'tensor', _xor_pairs(n_tensor, 2))]
    ppermute x4, waiting for transfers between devices: 2.47 us -> 1.21 us  [gathered(): lax.ppermute(send, 'tensor', _xor_pairs(n_tensor, 1)).astype(jnp.float32)]
    ppermute x3, waiting for transfers between devices: 5.9 us -> 6.94 us  [gathered(): blocks[k] = lax.ppermute(source, 'expert', _xor_pairs(n_expert, k))]
    ppermute x4, starting transfers between devices: 5.55 us -> 6.47 us  [gathered(): lax.ppermute(piece, 'tensor', _xor_pairs(n_tensor, 2))]
  transfers between devices with their start and end apart: 22 -> 22, of which waited for: 12 -> 11; matrix products, arithmetic and copies ran while one was open for 19% -> 19% of each run, Pallas kernels for 0% -> 0%
where the time goes in v11:
time: 67.2 us; the launch traced here: 67 us
  starting transfers between devices  25.9 us (39%)
  waiting for transfers between devices  24.4 us (36%)
  matrix products  9.28 us (14%)
  local copies, waits for them, and re-layouts  4.58 us (7%)
  other arithmetic  2.46 us (4%)
    ppermute x3, starting transfers between devices, gathered(): blocks[k] = lax.ppermute(source, 'expert', _xor_pairs(n_expert, k))  8.53 us
    ppermute x3, waiting for transfers between devices, gathered(): blocks[k] = lax.ppermute(source, 'expert', _xor_pairs(n_expert, k))  6.94 us
    ppermute x4, starting transfers between devices, gathered(): lax.ppermute(piece, 'tensor', _xor_pairs(n_tensor, 2))  6.47 us
    ppermute x4, waiting for transfers between devices, gathered(): lax.ppermute(piece, 'tensor', _xor_pairs(n_tensor, 2))  5.67 us
    ppermute x3, waiting for transfers between devices, gathered(): lax.ppermute(part.astype(jnp.bfloat16), 'expert', _xor_pairs(n_expert, k))  5.34 us
    ppermute x3, starting transfers between devices, gathered(): lax.ppermute(part.astype(jnp.bfloat16), 'expert', _xor_pairs(n_expert, k))  5.33 us
    ppermute x4, waiting for transfers between devices, gathered(): lax.ppermute(over_c[:, width:].astype(jnp.bfloat16), 'tensor', _xor_pairs...  5.23 us
    ppermute x4, starting transfers between devices, gathered(): lax.ppermute(over_c[:, width:].astype(jnp.bfloat16), 'tensor', _xor_pairs...  4.13 us
  transfers between devices with their start and end apart: 22, of which 11 were waited for; matrix products, arithmetic and copies ran while one was open for 19% of the time, Pallas kernels for 0%

profile of v11, /device:TPU:0, one launch (start us, length us, event | category | flops | bytes accessed | tf_op | source)
XLA Modules:
  0.0 67.0 jit_solution(17640234088740590003)
XLA Ops:
  0.0 1.0 %multiply_convert_fusion = bf16[128,640]{1,0:T(8,128)(2,1)S(1)} fusion(bf16[128,640]{1,0:T(8,128)(2,1)} %param.6, f32[128]{0:T(128)} %param.7), kind=kLoop, calls=%fused_computation.59 | loop fusion | flops 245760 | bytes 328192 | tf_op jit(solution)/shard_map/convert_element_type | solution.py:64
  1.0 3.0 %collective-permute-start = (bf16[128,640]{1,0:T(8,128)(2,1)S(1)}, bf16[128,640]{1,0:T(8,128)(2,1)S(1)}, u32[]{:S(2)}, u32[]{:S(2)}) collective-permute-start(bf16[128,640]{1,0:T(8,128)(2,1)S(1)} %multiply_convert_fusion), channel_id=1, source_target_pairs={{0,2},{1,3},{2,0},{3,1},{4,6},{5,7},{6,4},{7,5},{8,10},{9,11},{10,... | collective-permute-start | bytes 491528 | tf_op jit(solution)/shard_map/ppermute | solution.py:82
  4.0 2.6 %collective-permute-start.4 = (bf16[128,640]{1,0:T(8,128)(2,1)S(1)}, bf16[128,640]{1,0:T(8,128)(2,1)S(1)}, u32[]{:S(2)}, u32[]{:S(2)}) collective-permute-start(bf16[128,640]{1,0:T(8,128)(2,1)S(1)} %multiply_convert_fusion), channel_id=1, source_target_pairs={{0,8},{4,12},{8,0},{12,4},{1,9},{5,13},{9,1},{13,5},{2,10},{6,14},... | collective-permute-start | bytes 491528 | tf_op jit(solution)/shard_map/ppermute | solution.py:75
  6.6 1.9 %dynamic-slice_bitcast_fusion.11 = (bf16[640,512]{1,0:T(8,128)(2,1)S(1)}, bf16[640,512]{1,0:T(8,128)(2,1)S(1)}, bf16[640,512]{1,0:T(8,128)(2,1)S(1)}, bf16[640,512]{1,0:T(8,128)(2,1)S(1)}) fusion(bf16[1,2560,512]{2,1,0:T(8,128)(2,1)} %param.9, s32[]{:T(128)S(6)} %select_n.48, s32[]{:T(128)S(6)} %select_n.49, s32[]{:T(128)S(6)} %select_n.51, s32[]{:T(128)S(6)} %select_n.50), kind=kLoop, calls=%fused_computation.38 | loop fusion | bytes 5242896 | tf_op jit(solution)/shard_map/dynamic_slice | solution.py:55
  8.8 1.5 %copy-done = bf16[1,2560,512]{2,1,0:T(8,128)(2,1)S(1)} copy-done((bf16[1,2560,512]{2,1,0:T(8,128)(2,1)S(1)}, bf16[1,2560,512]{2,1,0:T(8,128)(2,1)}, u32[]{:S(2)}) %copy-start) | copy-done | bytes 2621464
  10.6 3.5 %collective-permute-done.4 = bf16[128,640]{1,0:T(8,128)(2,1)S(1)} collective-permute-done((bf16[128,640]{1,0:T(8,128)(2,1)S(1)}, bf16[128,640]{1,0:T(8,128)(2,1)S(1)}, u32[]{:S(2)}, u32[]{:S(2)}) %collective-permute-start.4) | collective-permute-done | bytes 163872 | tf_op jit(solution)/shard_map/ppermute | solution.py:75
  14.1 0.5 collective-permute-start.5
  14.8 3.6 %collective-permute-start.10 = (bf16[128,640]{1,0:T(8,128)(2,1)S(1)}, bf16[128,640]{1,0:T(8,128)(2,1)S(1)}, u32[]{:S(2)}, u32[]{:S(2)}) collective-permute-start(bf16[128,640]{1,0:T(8,128)(2,1)S(1)} %multiply_convert_fusion), channel_id=1, source_target_pairs={{0,12},{4,8},{8,4},{12,0},{1,13},{5,9},{9,5},{13,1},{2,14},{6,10},... | collective-permute-start | bytes 491528 | tf_op jit(solution)/shard_map/ppermute | solution.py:75
  18.4 1.0 %collective-permute-done.5 = bf16[128,640]{1,0:T(8,128)(2,1)S(1)} collective-permute-done((bf16[128,640]{1,0:T(8,128)(2,1)S(1)}, bf16[128,640]{1,0:T(8,128)(2,1)S(1)}, u32[]{:S(2)}, u32[]{:S(2)}) %collective-permute-start.5) | collective-permute-done | bytes 163872 | tf_op jit(solution)/shard_map/ppermute | solution.py:82
  19.5 3.1 %collective-permute-done.10 = bf16[128,640]{1,0:T(8,128)(2,1)S(1)} collective-permute-done((bf16[128,640]{1,0:T(8,128)(2,1)S(1)}, bf16[128,640]{1,0:T(8,128)(2,1)S(1)}, u32[]{:S(2)}, u32[]{:S(2)}) %collective-permute-start.10) | collective-permute-done | bytes 163872 | tf_op jit(solution)/shard_map/ppermute | solution.py:75
  22.6 2.3 %collective-permute-start.16 = (bf16[128,640]{1,0:T(8,128)(2,1)S(1)}, bf16[128,640]{1,0:T(8,128)(2,1)S(1)}, u32[]{:S(2)}, u32[]{:S(2)}) collective-permute-start(bf16[128,640]{1,0:T(8,128)(2,1)S(1)} %multiply_convert_fusion), channel_id=1, source_target_pairs={{0,4},{4,0},{8,12},{12,8},{1,5},{5,1},{9,13},{13,9},{2,6},{6,2},{1... | collective-permute-start | bytes 491528 | tf_op jit(solution)/shard_map/ppermute | solution.py:75
  24.9 1.5 %collective-permute-start.11 = (bf16[128,640]{1,0:T(8,128)(2,1)S(1)}, bf16[128,640]{1,0:T(8,128)(2,1)S(1)}, u32[]{:S(2)}, u32[]{:S(2)}) collective-permute-start(bf16[128,640]{1,0:T(8,128)(2,1)S(1)} %collective-permute-done.10), channel_id=1, source_target_pairs={{0,2},{1,3},{2,0},{3,1},{4,6},{5,7},{6,4},{7,5},{8,10},{9,11},{10,... | collective-permute-start | bytes 491528 | tf_op jit(solution)/shard_map/ppermute | solution.py:82
  26.4 0.5 fusion.13
  27.0 0.5 multiply_convert_fusion.1
  27.5 0.3 convolution_convert_fusion.6
  27.9 0.3 collective-permute-done.16
  28.2 1.5 %collective-permute-start.17 = (bf16[128,640]{1,0:T(8,128)(2,1)S(1)}, bf16[128,640]{1,0:T(8,128)(2,1)S(1)}, u32[]{:S(2)}, u32[]{:S(2)}) collective-permute-start(bf16[128,640]{1,0:T(8,128)(2,1)S(1)} %collective-permute-done.16), channel_id=1, source_target_pairs={{0,2},{1,3},{2,0},{3,1},{4,6},{5,7},{6,4},{7,5},{8,10},{9,11},{10,... | collective-permute-start | bytes 491528 | tf_op jit(solution)/shard_map/ppermute | solution.py:82
  29.7 0.5 collective-permute-done.11
  30.4 4.1 %collective-permute-done.17 = bf16[128,640]{1,0:T(8,128)(2,1)S(1)} collective-permute-done((bf16[128,640]{1,0:T(8,128)(2,1)S(1)}, bf16[128,640]{1,0:T(8,128)(2,1)S(1)}, u32[]{:S(2)}, u32[]{:S(2)}) %collective-permute-start.17) | collective-permute-done | bytes 163872 | tf_op jit(solution)/shard_map/ppermute | solution.py:82
  34.7 0.3 convert_add_fusion.3
  35.1 0.5 fusion.16
  35.6 0.7 %fusion.1 = bf16[128,512]{1,0:T(8,128)(2,1)S(1)} fusion(bf16[128,2560]{1,0:T(8,128)(2,1)S(1)} %pad_maximum_fusion.5, f32[128,512]{1,0:T(8,128)S(1)} %fusion.16, bf16[640,512]{1,0:T(8,128)(2,1)S(1)} %get-tuple-element.21, bf16[640,512]{1,0:T(8,128)(2,1)S(1)} %get-tuple-element.22, bf16[640,512]{1,0:T(8,128)(2,1)S(1)} %get-tuple-element.20, ...), kind=kOutput, calls=%fused_computation.16 | convolution fusion | flops 346423296 | bytes 3670016 | tf_op jit(solution)/shard_map/dot_general | solution.py:88
  36.3 0.3 convolution_convert_fusion.4
  36.7 0.6 collective-permute-start.7
  37.3 1.2 %collective-permute-done.7 = bf16[128,1280]{1,0:T(8,128)(2,1)S(1)} collective-permute-done((bf16[128,1280]{1,0:T(8,128)(2,1)S(1)}, bf16[128,1280]{1,0:T(8,128)(2,1)S(1)}, u32[]{:S(2)}, u32[]{:S(2)}) %collective-permute-start.7) | collective-permute-done | bytes 327712 | tf_op jit(solution)/shard_map/ppermute | solution.py:93
  38.5 0.3 convert_add_fusion.2
  38.8 0.5 fusion.17
  39.3 0.7 %fusion.2 = bf16[128,512]{1,0:T(8,128)(2,1)S(1)} fusion(bf16[128,2560]{1,0:T(8,128)(2,1)S(1)} %pad_maximum_fusion.6, f32[128,512]{1,0:T(8,128)S(1)} %fusion.17, bf16[640,512]{1,0:T(8,128)(2,1)S(1)} %get-tuple-element.21, bf16[640,512]{1,0:T(8,128)(2,1)S(1)} %get-tuple-element.22, bf16[640,512]{1,0:T(8,128)(2,1)S(1)} %get-tuple-element.20, ...), kind=kOutput, calls=%fused_computation.17 | convolution fusion | flops 346423296 | bytes 3670016 | tf_op jit(solution)/shard_map/dot_general | solution.py:88
  40.1 0.3 convolution_convert_fusion.2
  40.4 0.4 collective-permute-start.13
  40.9 0.7 %slice.70 = bf16[128,640]{1,0:T(8,128)(2,1)} slice(f32[128,1280]{1,0:T(8,128)S(1)} %convert_add_fusion.2), slice={[0:128], [640:1280]} | slice | bytes 327680 | tf_op jit(solution)/shard_map/slice | solution.py:96
  41.6 0.8 %collective-permute-start.8 = (bf16[128,640]{1,0:T(8,128)(2,1)}, bf16[128,640]{1,0:T(8,128)(2,1)S(1)}, u32[]{:S(2)}, u32[]{:S(2)}) collective-permute-start(bf16[128,640]{1,0:T(8,128)(2,1)} %slice.70), channel_id=1, source_target_pairs={{0,2},{1,3},{2,0},{3,1},{4,6},{5,7},{6,4},{7,5},{8,10},{9,11},{10,... | collective-permute-start | bytes 491528 | tf_op jit(solution)/shard_map/ppermute | solution.py:95
  42.4 0.3 convert_add_fusion.1
  42.7 0.5 fusion.18
  43.2 0.7 %fusion.3 = bf16[128,512]{1,0:T(8,128)(2,1)S(1)} fusion(bf16[128,2560]{1,0:T(8,128)(2,1)S(1)} %pad_maximum_fusion.7, f32[128,512]{1,0:T(8,128)S(1)} %fusion.18, bf16[640,512]{1,0:T(8,128)(2,1)S(1)} %get-tuple-element.21, bf16[640,512]{1,0:T(8,128)(2,1)S(1)} %get-tuple-element.22, bf16[640,512]{1,0:T(8,128)(2,1)S(1)} %get-tuple-element.20, ...), kind=kOutput, calls=%fused_computation.18 | convolution fusion | flops 346423296 | bytes 3670016 | tf_op jit(solution)/shard_map/dot_general | solution.py:88
  44.0 1.1 %convolution_convert_fusion = bf16[128,1280]{1,0:T(8,128)(2,1)} fusion(bf16[128,512]{1,0:T(8,128)(2,1)S(1)} %fusion.3, bf16[512,640]{1,0:T(8,128)(2,1)S(1)} %get-tuple-element.17, bf16[512,640]{1,0:T(8,128)(2,1)S(1)} %get-tuple-element.18), kind=kOutput, calls=%fused_computation.2 | convolution fusion | flops 170557440 | bytes 1769472 | tf_op jit(solution)/shard_map/dot_general | solution.py:91
  45.2 1.2 %collective-permute-start.3 = (bf16[128,640]{1,0:T(8,128)(2,1)S(1)}, bf16[128,640]{1,0:T(8,128)(2,1)S(1)}, u32[]{:S(2)}, u32[]{:S(2)}) collective-permute-start(bf16[128,640]{1,0:T(8,128)(2,1)S(1)} %slice.71), channel_id=1, source_target_pairs={{0,2},{1,3},{2,0},{3,1},{4,6},{5,7},{6,4},{7,5},{8,10},{9,11},{10,... | collective-permute-start | bytes 491528 | tf_op jit(solution)/shard_map/ppermute | solution.py:95
  46.4 1.6 %collective-permute-done.8 = bf16[128,640]{1,0:T(8,128)(2,1)S(1)} collective-permute-done((bf16[128,640]{1,0:T(8,128)(2,1)}, bf16[128,640]{1,0:T(8,128)(2,1)S(1)}, u32[]{:S(2)}, u32[]{:S(2)}) %collective-permute-start.8) | collective-permute-done | bytes 163872 | tf_op jit(solution)/shard_map/ppermute | solution.py:95
  48.1 1.7 %collective-permute-start.9 = (bf16[128,640]{1,0:T(8,128)(2,1)S(1)}, bf16[128,640]{1,0:T(8,128)(2,1)S(1)}, u32[]{:S(2)}, u32[]{:S(2)}) collective-permute-start(bf16[128,640]{1,0:T(8,128)(2,1)S(1)} %fusion.6), channel_id=1, source_target_pairs={{0,8},{4,12},{8,0},{12,4},{1,9},{5,13},{9,1},{13,5},{2,10},{6,14},... | collective-permute-start | bytes 491528 | tf_op jit(solution)/shard_map/ppermute | solution.py:100
  49.9 0.8 %collective-permute-start.14 = (bf16[128,640]{1,0:T(8,128)(2,1)S(1)}, bf16[128,640]{1,0:T(8,128)(2,1)S(1)}, u32[]{:S(2)}, u32[]{:S(2)}) collective-permute-start(bf16[128,640]{1,0:T(8,128)(2,1)S(1)} %slice.69), channel_id=1, source_target_pairs={{0,2},{1,3},{2,0},{3,1},{4,6},{5,7},{6,4},{7,5},{8,10},{9,11},{10,... | collective-permute-start | bytes 491528 | tf_op jit(solution)/shard_map/ppermute | solution.py:95
  50.7 1.4 %convert_add_fusion = f32[128,1280]{1,0:T(8,128)S(1)} fusion(bf16[128,1280]{1,0:T(8,128)(2,1)} %collective-permute-done.19, bf16[128,512]{1,0:T(8,128)(2,1)} %copy-done.3, bf16[512,640]{1,0:T(8,128)(2,1)S(1)} %get-tuple-element.16, bf16[512,640]{1,0:T(8,128)(2,1)S(1)} %get-tuple-element.15), kind=kOutput, calls=%fused_computation.23 | convolution fusion | flops 171048960 | bytes 2424832 | tf_op jit(solution)/shard_map/dot_general | solution.py:90
  52.1 1.3 %collective-permute-start.20 = (bf16[128,640]{1,0:T(8,128)(2,1)S(1)}, bf16[128,640]{1,0:T(8,128)(2,1)S(1)}, u32[]{:S(2)}, u32[]{:S(2)}) collective-permute-start(bf16[128,640]{1,0:T(8,128)(2,1)S(1)} %slice.68), channel_id=1, source_target_pairs={{0,2},{1,3},{2,0},{3,1},{4,6},{5,7},{6,4},{7,5},{8,10},{9,11},{10,... | collective-permute-start | bytes 491528 | tf_op jit(solution)/shard_map/ppermute | solution.py:95
  53.4 3.6 %collective-permute-done.14 = bf16[128,640]{1,0:T(8,128)(2,1)S(1)} collective-permute-done((bf16[128,640]{1,0:T(8,128)(2,1)S(1)}, bf16[128,640]{1,0:T(8,128)(2,1)S(1)}, u32[]{:S(2)}, u32[]{:S(2)}) %collective-permute-start.14) | collective-permute-done | bytes 163872 | tf_op jit(solution)/shard_map/ppermute | solution.py:95
  57.1 1.8 %collective-permute-start.15 = (bf16[128,640]{1,0:T(8,128)(2,1)S(1)}, bf16[128,640]{1,0:T(8,128)(2,1)S(1)}, u32[]{:S(2)}, u32[]{:S(2)}) collective-permute-start(bf16[128,640]{1,0:T(8,128)(2,1)S(1)} %fusion.5), channel_id=1, source_target_pairs={{0,12},{4,8},{8,4},{12,0},{1,13},{5,9},{9,5},{13,1},{2,14},{6,10},... | collective-permute-start | bytes 491528 | tf_op jit(solution)/shard_map/ppermute | solution.py:100
  59.0 1.8 %collective-permute-start.21 = (bf16[128,640]{1,0:T(8,128)(2,1)S(1)}, bf16[128,640]{1,0:T(8,128)(2,1)S(1)}, u32[]{:S(2)}, u32[]{:S(2)}) collective-permute-start(bf16[128,640]{1,0:T(8,128)(2,1)S(1)} %fusion.4), channel_id=1, source_target_pairs={{0,4},{4,0},{8,12},{12,8},{1,5},{5,1},{9,13},{13,9},{2,6},{6,2},{1... | collective-permute-start | bytes 491528 | tf_op jit(solution)/shard_map/ppermute | solution.py:100
  60.8 4.9 %collective-permute-done.15 = bf16[128,640]{1,0:T(8,128)(2,1)S(1)} collective-permute-done((bf16[128,640]{1,0:T(8,128)(2,1)S(1)}, bf16[128,640]{1,0:T(8,128)(2,1)S(1)}, u32[]{:S(2)}, u32[]{:S(2)}) %collective-permute-start.15) | collective-permute-done | bytes 163872 | tf_op jit(solution)/shard_map/ppermute | solution.py:100
  65.7 0.4 collective-permute-done.21
  66.1 0.9 %fusion.11 = bf16[128,640]{1,0:T(8,128)(2,1)} fusion(f32[128,1280]{1,0:T(8,128)S(1)} %convert_add_fusion.3, bf16[128,640]{1,0:T(8,128)(2,1)S(1)} %collective-permute-done.21, bf16[128,640]{1,0:T(8,128)(2,1)S(1)} %collective-permute-done.15, bf16[128,640]{1,0:T(8,128)(2,1)S(1)} %collective-permute-done.9, bf16[128,640]{1,0:T(8,128)(2,1)S(1)} %collective-permute-done.3, ...), kind=kLoop, calls=%fused_computation.54 | loop fusion | flops 1064960 | bytes 1147392 | tf_op jit(solution)/shard_map/convert_element_type | solution.py:104
  (41 shorter events, 1.6 us)
Async XLA Ops:
  1.0 9.4 %collective-permute-start = (bf16[128,640]{1,0:T(8,128)(2,1)S(1)}, bf16[128,640]{1,0:T(8,128)(2,1)S(1)}, u32[]{:S(2)}, u32[]{:S(2)}) collective-permute-start(bf16[128,640]{1,0:T(8,128)(2,1)S(1)} %multiply_convert_fusion), channel_id=1, source_target_pairs={{0,2},{1,3},{2,0},{3,1},{4,6},{5,7},{6,4},{7,5},{8,10},{9,11},{10,... | collective-permute-start | bytes 491528 | tf_op jit(solution)/shard_map/ppermute | solution.py:82
  4.0 10.1 %collective-permute-start.4 = (bf16[128,640]{1,0:T(8,128)(2,1)S(1)}, bf16[128,640]{1,0:T(8,128)(2,1)S(1)}, u32[]{:S(2)}, u32[]{:S(2)}) collective-permute-start(bf16[128,640]{1,0:T(8,128)(2,1)S(1)} %multiply_convert_fusion), channel_id=1, source_target_pairs={{0,8},{4,12},{8,0},{12,4},{1,9},{5,13},{9,1},{13,5},{2,10},{6,14},... | collective-permute-start | bytes 491528 | tf_op jit(solution)/shard_map/ppermute | solution.py:75
  8.5 1.7 %copy-start = (bf16[1,2560,512]{2,1,0:T(8,128)(2,1)S(1)}, bf16[1,2560,512]{2,1,0:T(8,128)(2,1)}, u32[]{:S(2)}) copy-start(bf16[1,2560,512]{2,1,0:T(8,128)(2,1)} %param.10) | copy-start | bytes 7864324
  10.3 4.3 %copy-start.1 = (bf16[1,512,2560]{2,1,0:T(8,128)(2,1)S(1)}, bf16[1,512,2560]{2,1,0:T(8,128)(2,1)}, u32[]{:S(2)}) copy-start(bf16[1,512,2560]{2,1,0:T(8,128)(2,1)} %param.11) | copy-start | bytes 7864324
  10.5 15.9 %collective-permute-start.1 = (bf16[128,1280]{1,0:T(8,128)(2,1)S(1)}, bf16[128,1280]{1,0:T(8,128)(2,1)S(1)}, u32[]{:S(2)}, u32[]{:S(2)}) collective-permute-start(bf16[128,1280]{1,0:T(8,128)(2,1)S(1)} %pad_maximum_fusion.8), channel_id=1, source_target_pairs={{0,1},{1,0},{2,3},{3,2},{4,5},{5,4},{6,7},{7,6},{8,9},{9,8},{10,11... | collective-permute-start | bytes 983048 | tf_op jit(solution)/shard_map/ppermute | solution.py:84
  14.1 5.3 %collective-permute-start.5 = (bf16[128,640]{1,0:T(8,128)(2,1)S(1)}, bf16[128,640]{1,0:T(8,128)(2,1)S(1)}, u32[]{:S(2)}, u32[]{:S(2)}) collective-permute-start(bf16[128,640]{1,0:T(8,128)(2,1)S(1)} %collective-permute-done.4), channel_id=1, source_target_pairs={{0,2},{1,3},{2,0},{3,1},{4,6},{5,7},{6,4},{7,5},{8,10},{9,11},{10,... | collective-permute-start | bytes 491528 | tf_op jit(solution)/shard_map/ppermute | solution.py:82
  14.8 7.8 %collective-permute-start.10 = (bf16[128,640]{1,0:T(8,128)(2,1)S(1)}, bf16[128,640]{1,0:T(8,128)(2,1)S(1)}, u32[]{:S(2)}, u32[]{:S(2)}) collective-permute-start(bf16[128,640]{1,0:T(8,128)(2,1)S(1)} %multiply_convert_fusion), channel_id=1, source_target_pairs={{0,12},{4,8},{8,4},{12,0},{1,13},{5,9},{9,5},{13,1},{2,14},{6,10},... | collective-permute-start | bytes 491528 | tf_op jit(solution)/shard_map/ppermute | solution.py:75
  19.4 15.2 %collective-permute-start.6 = (bf16[128,1280]{1,0:T(8,128)(2,1)S(1)}, bf16[128,1280]{1,0:T(8,128)(2,1)S(1)}, u32[]{:S(2)}, u32[]{:S(2)}) collective-permute-start(bf16[128,1280]{1,0:T(8,128)(2,1)S(1)} %pad_maximum_fusion.9), channel_id=1, source_target_pairs={{0,1},{1,0},{2,3},{3,2},{4,5},{5,4},{6,7},{7,6},{8,9},{9,8},{10,11... | collective-permute-start | bytes 983048 | tf_op jit(solution)/shard_map/ppermute | solution.py:84
  22.6 5.6 %collective-permute-start.16 = (bf16[128,640]{1,0:T(8,128)(2,1)S(1)}, bf16[128,640]{1,0:T(8,128)(2,1)S(1)}, u32[]{:S(2)}, u32[]{:S(2)}) collective-permute-start(bf16[128,640]{1,0:T(8,128)(2,1)S(1)} %multiply_convert_fusion), channel_id=1, source_target_pairs={{0,4},{4,0},{8,12},{12,8},{1,5},{5,1},{9,13},{13,9},{2,6},{6,2},{1... | collective-permute-start | bytes 491528 | tf_op jit(solution)/shard_map/ppermute | solution.py:75
  24.9 5.3 %collective-permute-start.11 = (bf16[128,640]{1,0:T(8,128)(2,1)S(1)}, bf16[128,640]{1,0:T(8,128)(2,1)S(1)}, u32[]{:S(2)}, u32[]{:S(2)}) collective-permute-start(bf16[128,640]{1,0:T(8,128)(2,1)S(1)} %collective-permute-done.10), channel_id=1, source_target_pairs={{0,2},{1,3},{2,0},{3,1},{4,6},{5,7},{6,4},{7,5},{8,10},{9,11},{10,... | collective-permute-start | bytes 491528 | tf_op jit(solution)/shard_map/ppermute | solution.py:82
  27.8 6.9 %collective-permute-start.2 = (bf16[128,1280]{1,0:T(8,128)(2,1)S(1)}, bf16[128,1280]{1,0:T(8,128)(2,1)S(1)}, u32[]{:S(2)}, u32[]{:S(2)}) collective-permute-start(bf16[128,1280]{1,0:T(8,128)(2,1)S(1)} %convolution_convert_fusion.6), channel_id=1, source_target_pairs={{0,1},{1,0},{2,3},{3,2},{4,5},{5,4},{6,7},{7,6},{8,9},{9,8},{10,11... | collective-permute-start | bytes 983048 | tf_op jit(solution)/shard_map/ppermute | solution.py:93
  28.2 6.3 %collective-permute-start.17 = (bf16[128,640]{1,0:T(8,128)(2,1)S(1)}, bf16[128,640]{1,0:T(8,128)(2,1)S(1)}, u32[]{:S(2)}, u32[]{:S(2)}) collective-permute-start(bf16[128,640]{1,0:T(8,128)(2,1)S(1)} %collective-permute-done.16), channel_id=1, source_target_pairs={{0,2},{1,3},{2,0},{3,1},{4,6},{5,7},{6,4},{7,5},{8,10},{9,11},{10,... | collective-permute-start | bytes 491528 | tf_op jit(solution)/shard_map/ppermute | solution.py:82
  30.3 6.9 %collective-permute-start.12 = (bf16[128,1280]{1,0:T(8,128)(2,1)S(1)}, bf16[128,1280]{1,0:T(8,128)(2,1)S(1)}, u32[]{:S(2)}, u32[]{:S(2)}) collective-permute-start(bf16[128,1280]{1,0:T(8,128)(2,1)S(1)} %pad_maximum_fusion.10), channel_id=1, source_target_pairs={{0,1},{1,0},{2,3},{3,2},{4,5},{5,4},{6,7},{7,6},{8,9},{9,8},{10,11... | collective-permute-start | bytes 983048 | tf_op jit(solution)/shard_map/ppermute | solution.py:84
  34.5 6.3 %collective-permute-start.18 = (bf16[128,1280]{1,0:T(8,128)(2,1)S(1)}, bf16[128,1280]{1,0:T(8,128)(2,1)S(1)}, u32[]{:S(2)}, u32[]{:S(2)}) collective-permute-start(bf16[128,1280]{1,0:T(8,128)(2,1)S(1)} %pad_maximum_fusion.11), channel_id=1, source_target_pairs={{0,1},{1,0},{2,3},{3,2},{4,5},{5,4},{6,7},{7,6},{8,9},{9,8},{10,11... | collective-permute-start | bytes 983048 | tf_op jit(solution)/shard_map/ppermute | solution.py:84
  36.7 1.8 %collective-permute-start.7 = (bf16[128,1280]{1,0:T(8,128)(2,1)S(1)}, bf16[128,1280]{1,0:T(8,128)(2,1)S(1)}, u32[]{:S(2)}, u32[]{:S(2)}) collective-permute-start(bf16[128,1280]{1,0:T(8,128)(2,1)S(1)} %convolution_convert_fusion.4), channel_id=1, source_target_pairs={{0,1},{1,0},{2,3},{3,2},{4,5},{5,4},{6,7},{7,6},{8,9},{9,8},{10,11... | collective-permute-start | bytes 983048 | tf_op jit(solution)/shard_map/ppermute | solution.py:93
  40.4 1.9 %collective-permute-start.13 = (bf16[128,1280]{1,0:T(8,128)(2,1)S(1)}, bf16[128,1280]{1,0:T(8,128)(2,1)S(1)}, u32[]{:S(2)}, u32[]{:S(2)}) collective-permute-start(bf16[128,1280]{1,0:T(8,128)(2,1)S(1)} %convolution_convert_fusion.2), channel_id=1, source_target_pairs={{0,1},{1,0},{2,3},{3,2},{4,5},{5,4},{6,7},{7,6},{8,9},{9,8},{10,11... | collective-permute-start | bytes 983048 | tf_op jit(solution)/shard_map/ppermute | solution.py:93
  41.6 6.5 %collective-permute-start.8 = (bf16[128,640]{1,0:T(8,128)(2,1)}, bf16[128,640]{1,0:T(8,128)(2,1)S(1)}, u32[]{:S(2)}, u32[]{:S(2)}) collective-permute-start(bf16[128,640]{1,0:T(8,128)(2,1)} %slice.70), channel_id=1, source_target_pairs={{0,2},{1,3},{2,0},{3,1},{4,6},{5,7},{6,4},{7,5},{8,10},{9,11},{10,... | collective-permute-start | bytes 491528 | tf_op jit(solution)/shard_map/ppermute | solution.py:95
  44.0 1.1 %copy-start.3 = (bf16[128,512]{1,0:T(8,128)(2,1)}, bf16[128,512]{1,0:T(8,128)(2,1)S(1)}, u32[]{:S(2)}) copy-start(bf16[128,512]{1,0:T(8,128)(2,1)S(1)} %fusion.3) | copy-start | bytes 393220
  45.1 5.6 %collective-permute-start.19 = (bf16[128,1280]{1,0:T(8,128)(2,1)}, bf16[128,1280]{1,0:T(8,128)(2,1)}, u32[]{:S(2)}, u32[]{:S(2)}) collective-permute-start(bf16[128,1280]{1,0:T(8,128)(2,1)} %convolution_convert_fusion), channel_id=1, source_target_pairs={{0,1},{1,0},{2,3},{3,2},{4,5},{5,4},{6,7},{7,6},{8,9},{9,8},{10,11... | collective-permute-start | bytes 983048 | tf_op jit(solution)/shard_map/ppermute | solution.py:93
  45.2 15.5 %copy-start.2 = (s32[128,1]{0,1:T(1,128)S(1)}, s32[128,1]{0,1:T(1,128)}, u32[]{:S(2)}) copy-start(s32[128,1]{0,1:T(1,128)} %param.8) | copy-start | bytes 1540
  45.2 15.5 %collective-permute-start.3 = (bf16[128,640]{1,0:T(8,128)(2,1)S(1)}, bf16[128,640]{1,0:T(8,128)(2,1)S(1)}, u32[]{:S(2)}, u32[]{:S(2)}) collective-permute-start(bf16[128,640]{1,0:T(8,128)(2,1)S(1)} %slice.71), channel_id=1, source_target_pairs={{0,2},{1,3},{2,0},{3,1},{4,6},{5,7},{6,4},{7,5},{8,10},{9,11},{10,... | collective-permute-start | bytes 491528 | tf_op jit(solution)/shard_map/ppermute | solution.py:95
  48.1 12.7 %collective-permute-start.9 = (bf16[128,640]{1,0:T(8,128)(2,1)S(1)}, bf16[128,640]{1,0:T(8,128)(2,1)S(1)}, u32[]{:S(2)}, u32[]{:S(2)}) collective-permute-start(bf16[128,640]{1,0:T(8,128)(2,1)S(1)} %fusion.6), channel_id=1, source_target_pairs={{0,8},{4,12},{8,0},{12,4},{1,9},{5,13},{9,1},{13,5},{2,10},{6,14},... | collective-permute-start | bytes 491528 | tf_op jit(solution)/shard_map/ppermute | solution.py:100
  49.9 7.2 %collective-permute-start.14 = (bf16[128,640]{1,0:T(8,128)(2,1)S(1)}, bf16[128,640]{1,0:T(8,128)(2,1)S(1)}, u32[]{:S(2)}, u32[]{:S(2)}) collective-permute-start(bf16[128,640]{1,0:T(8,128)(2,1)S(1)} %slice.69), channel_id=1, source_target_pairs={{0,2},{1,3},{2,0},{3,1},{4,6},{5,7},{6,4},{7,5},{8,10},{9,11},{10,... | collective-permute-start | bytes 491528 | tf_op jit(solution)/shard_map/ppermute | solution.py:95
  52.1 6.8 %collective-permute-start.20 = (bf16[128,640]{1,0:T(8,128)(2,1)S(1)}, bf16[128,640]{1,0:T(8,128)(2,1)S(1)}, u32[]{:S(2)}, u32[]{:S(2)}) collective-permute-start(bf16[128,640]{1,0:T(8,128)(2,1)S(1)} %slice.68), channel_id=1, source_target_pairs={{0,2},{1,3},{2,0},{3,1},{4,6},{5,7},{6,4},{7,5},{8,10},{9,11},{10,... | collective-permute-start | bytes 491528 | tf_op jit(solution)/shard_map/ppermute | solution.py:95
  57.1 8.6 %collective-permute-start.15 = (bf16[128,640]{1,0:T(8,128)(2,1)S(1)}, bf16[128,640]{1,0:T(8,128)(2,1)S(1)}, u32[]{:S(2)}, u32[]{:S(2)}) collective-permute-start(bf16[128,640]{1,0:T(8,128)(2,1)S(1)} %fusion.5), channel_id=1, source_target_pairs={{0,12},{4,8},{8,4},{12,0},{1,13},{5,9},{9,5},{13,1},{2,14},{6,10},... | collective-permute-start | bytes 491528 | tf_op jit(solution)/shard_map/ppermute | solution.py:100
  59.0 7.1 %collective-permute-start.21 = (bf16[128,640]{1,0:T(8,128)(2,1)S(1)}, bf16[128,640]{1,0:T(8,128)(2,1)S(1)}, u32[]{:S(2)}, u32[]{:S(2)}) collective-permute-start(bf16[128,640]{1,0:T(8,128)(2,1)S(1)} %fusion.4), channel_id=1, source_target_pairs={{0,4},{4,0},{8,12},{12,8},{1,5},{5,1},{9,13},{13,9},{2,6},{6,2},{1... | collective-permute-start | bytes 491528 | tf_op jit(solution)/shard_map/ppermute | solution.py:100

commit v12 on v10

--- a/solution.py
+++ b/solution.py
@@ -89,6 +89,17 @@
         previous = keep
         over_c = keep.astype(jnp.float32) + lax.ppermute(
             send, "tensor", _xor_pairs(n_tensor, 1)).astype(jnp.float32)
+        k = wave[-1]
+        if k and wave is waves[-1] and len(wave) == 1:
+            diagonal = [(z * n_tensor + u, (z ^ k) * n_tensor + (u ^ 2))
+                        for z in range(n_expert) for u in range(n_tensor)]
+            part = lax.ppermute(
+                over_c[:, :width].astype(jnp.bfloat16), "expert", _xor_pairs(n_expert, k)).astype(jnp.float32)
+            part = part + lax.ppermute(
+                over_c[:, width:].astype(jnp.bfloat16), ("expert", "tensor"), diagonal).astype(jnp.float32)
+            part = jnp.where(routed == (me ^ k) // SPAN, part, 0.0)
+            total = part if total is None else total + part
+            continue
         summed = over_c[:, :width] + lax.ppermute(
             over_c[:, width:].astype(jnp.bfloat16), "tensor", _xor_pairs(n_tensor, 2)).astype(jnp.float32)
         for i, k in enumerate(wave):

time: 67 us -> 75.6 us (1.13)
  other arithmetic: 2.46 us -> 7.73 us
  waiting for transfers between devices: 28.5 us -> 29.8 us
  starting transfers between devices: 21.1 us -> 22.2 us
    ppermute x0 -> x2, waiting for transfers between devices: none -> 6.58 us  [the longest x1 3.81 us: gathered(): lax.ppermute(over_c[:, width:].astype(jnp.bfloat16), ('expert', 'tensor')...]
    concatenate x4, other arithmetic: 0.1 us -> 2.93 us  [gathered(): jnp.concatenate([piece, lax.ppermute(piece, 'tensor', _xor_pairs(n_tensor...]
    ppermute x4, waiting for transfers between devices: 9.45 us -> 6.79 us  [gathered(): lax.ppermute(piece, 'tensor', _xor_pairs(n_tensor, 2))]
    ppermute x0 -> x2, starting transfers between devices: none -> 2.07 us  [the longest x1 2 us: gathered(): lax.ppermute(over_c[:, width:].astype(jnp.bfloat16), ('expert', 'tensor')...]
    ppermute x4, waiting for transfers between devices: 2.47 us -> 0.58 us  [gathered(): lax.ppermute(send, 'tensor', _xor_pairs(n_tensor, 1)).astype(jnp.float32)]
    concatenate x3, other arithmetic: 0.14 us -> 1.97 us  [gathered(): jnp.concatenate([pair, lax.ppermute(pair, 'tensor', _xor_pairs(n_tensor,...]
    dynamic_slice x3, local copies, waits for them, and re-layouts: 2.4 us -> 3.53 us  [_slots(): lax.dynamic_slice_in_dim(weight, (t ^ k) * width, width, axis=axis)]
    dot_general x4, matrix products: 2.43 us -> 1.4 us  [gathered(): jnp.dot(hidden, down_keep, preferred_element_type=jnp.float32)]
  transfers between devices with their start and end apart: 22 -> 22, of which waited for: 12 -> 11; matrix products, arithmetic and copies ran while one was open for 19% -> 24% of each run, Pallas kernels for 0% -> 0%
where the time goes in v12:
time: 75.6 us; the launch traced here: 75.3 us
  waiting for transfers between devices  29.8 us (39%)
  starting transfers between devices  22.2 us (29%)
  matrix products  9.5 us (13%)
  other arithmetic  7.73 us (10%)
  local copies, waits for them, and re-layouts  5.7 us (8%)
    ppermute x4, waiting for transfers between devices, gathered(): lax.ppermute(piece, 'tensor', _xor_pairs(n_tensor, 2))  6.79 us
    ppermute x3, waiting for transfers between devices, gathered(): lax.ppermute(over_c[:, width:].astype(jnp.bfloat16), 'tensor', _xor_pairs...  5.7 us
    ppermute x2, starting transfers between devices, gathered(): lax.ppermute(part.astype(jnp.bfloat16), 'expert', _xor_pairs(n_expert, k))  5.54 us
    ppermute x4, starting transfers between devices, gathered(): lax.ppermute(piece, 'tensor', _xor_pairs(n_tensor, 2))  5.5 us
    ppermute x3, waiting for transfers between devices, gathered(): lax.ppermute(scaled, 'expert', _xor_pairs(n_expert, k))  5.11 us
    ppermute x2, waiting for transfers between devices, gathered(): lax.ppermute(part.astype(jnp.bfloat16), 'expert', _xor_pairs(n_expert, k))  4.98 us
    ppermute x3, starting transfers between devices, gathered(): lax.ppermute(scaled, 'expert', _xor_pairs(n_expert, k))  4.17 us
    ppermute x1, waiting for transfers between devices, gathered(): lax.ppermute(over_c[:, width:].astype(jnp.bfloat16), ('expert', 'tensor')...  3.81 us
  transfers between devices with their start and end apart: 22, of which 11 were waited for; matrix products, arithmetic and copies ran while one was open for 24% of the time, Pallas kernels for 0%

profile of v12, /device:TPU:0, one launch (start us, length us, event | category | flops | bytes accessed | tf_op | source)
XLA Modules:
  0.0 75.3 jit_solution(16963191638814425051)
XLA Ops:
  0.0 1.7 %multiply_convert_fusion = bf16[128,640]{1,0:T(8,128)(2,1)} fusion(bf16[128,640]{1,0:T(8,128)(2,1)} %param.6, f32[128]{0:T(128)} %param.7), kind=kLoop, calls=%fused_computation.56 | loop fusion | flops 245760 | bytes 328192 | tf_op jit(solution)/shard_map/convert_element_type | solution.py:64
  1.7 2.9 %collective-permute-start = (bf16[128,640]{1,0:T(8,128)(2,1)}, bf16[128,640]{1,0:T(8,128)(2,1)}, u32[]{:S(2)}, u32[]{:S(2)}) collective-permute-start(bf16[128,640]{1,0:T(8,128)(2,1)} %multiply_convert_fusion), channel_id=1, source_target_pairs={{0,2},{1,3},{2,0},{3,1},{4,6},{5,7},{6,4},{7,5},{8,10},{9,11},{10,... | collective-permute-start | bytes 491528 | tf_op jit(solution)/shard_map/ppermute | solution.py:79
  4.6 2.6 %collective-permute-start.4 = (bf16[128,640]{1,0:T(8,128)(2,1)}, bf16[128,640]{1,0:T(8,128)(2,1)}, u32[]{:S(2)}, u32[]{:S(2)}) collective-permute-start(bf16[128,640]{1,0:T(8,128)(2,1)} %multiply_convert_fusion), channel_id=1, source_target_pairs={{0,8},{4,12},{8,0},{12,4},{1,9},{5,13},{9,1},{13,5},{2,10},{6,14},... | collective-permute-start | bytes 491528 | tf_op jit(solution)/shard_map/ppermute | solution.py:66
  7.2 1.3 %collective-permute-start.10 = (bf16[128,640]{1,0:T(8,128)(2,1)}, bf16[128,640]{1,0:T(8,128)(2,1)}, u32[]{:S(2)}, u32[]{:S(2)}) collective-permute-start(bf16[128,640]{1,0:T(8,128)(2,1)} %multiply_convert_fusion), channel_id=1, source_target_pairs={{0,12},{4,8},{8,4},{12,0},{1,13},{5,9},{9,5},{13,1},{2,14},{6,10},... | collective-permute-start | bytes 491528 | tf_op jit(solution)/shard_map/ppermute | solution.py:66
  8.8 2.0 %dynamic-slice_bitcast_fusion.11 = (bf16[640,512]{1,0:T(8,128)(2,1)S(1)}, bf16[640,512]{1,0:T(8,128)(2,1)S(1)}, bf16[640,512]{1,0:T(8,128)(2,1)S(1)}, bf16[640,512]{1,0:T(8,128)(2,1)S(1)}) fusion(bf16[1,2560,512]{2,1,0:T(8,128)(2,1)} %param.9, s32[]{:T(128)S(6)} %select_n.48, s32[]{:T(128)S(6)} %select_n.49, s32[]{:T(128)S(6)} %select_n.51, s32[]{:T(128)S(6)} %select_n.50), kind=kLoop, calls=%fused_computation.38 | loop fusion | bytes 5242896 | tf_op jit(solution)/shard_map/dynamic_slice | solution.py:55
  10.8 0.5 copy-done
  11.3 1.3 %dynamic-slice_bitcast_fusion.7 = (bf16[640,512]{1,0:T(8,128)(2,1)S(1)}, bf16[640,512]{1,0:T(8,128)(2,1)}, bf16[640,512]{1,0:T(8,128)(2,1)}, bf16[640,512]{1,0:T(8,128)(2,1)}) fusion(bf16[1,2560,512]{2,1,0:T(8,128)(2,1)S(1)} %copy-done, s32[]{:T(128)S(6)} %select_n.48, s32[]{:T(128)S(6)} %select_n.49, s32[]{:T(128)S(6)} %select_n.51, s32[]{:T(128)S(6)} %select_n.50), kind=kLoop, calls=%fused_computation.34 | loop fusion | bytes 5242896 | tf_op jit(solution)/shard_map/dynamic_slice | solution.py:55
  12.8 1.5 %copy-done.1 = bf16[1,512,2560]{2,1,0:T(8,128)(2,1)S(1)} copy-done((bf16[1,512,2560]{2,1,0:T(8,128)(2,1)S(1)}, bf16[1,512,2560]{2,1,0:T(8,128)(2,1)}, u32[]{:S(2)}) %copy-start.1) | copy-done | bytes 2621464
  14.6 5.1 %collective-permute-done.4 = bf16[128,640]{1,0:T(8,128)(2,1)} collective-permute-done((bf16[128,640]{1,0:T(8,128)(2,1)}, bf16[128,640]{1,0:T(8,128)(2,1)}, u32[]{:S(2)}, u32[]{:S(2)}) %collective-permute-start.4) | collective-permute-done | bytes 163872 | tf_op jit(solution)/shard_map/ppermute | solution.py:66
  19.7 0.5 collective-permute-start.5
  20.2 1.0 %pad_maximum_fusion.8 = bf16[128,1280]{1,0:T(8,128)(2,1)S(1)} fusion(bf16[128,640]{1,0:T(8,128)(2,1)} %collective-permute-done, bf16[128,640]{1,0:T(8,128)(2,1)} %multiply_convert_fusion), kind=kLoop, calls=%fused_computation.52 | loop fusion | flops 655360 | bytes 655360 | tf_op jit(solution)/shard_map/concatenate | solution.py:78
  21.3 1.6 %collective-permute-start.11 = (bf16[128,640]{1,0:T(8,128)(2,1)}, bf16[128,640]{1,0:T(8,128)(2,1)S(1)}, u32[]{:S(2)}, u32[]{:S(2)}) collective-permute-start(bf16[128,640]{1,0:T(8,128)(2,1)} %collective-permute-done.10), channel_id=1, source_target_pairs={{0,2},{1,3},{2,0},{3,1},{4,6},{5,7},{6,4},{7,5},{8,10},{9,11},{10,... | collective-permute-start | bytes 491528 | tf_op jit(solution)/shard_map/ppermute | solution.py:79
  22.9 0.5 collective-permute-start.17
  23.4 2.5 %collective-permute-done.5 = bf16[128,640]{1,0:T(8,128)(2,1)S(1)} collective-permute-done((bf16[128,640]{1,0:T(8,128)(2,1)}, bf16[128,640]{1,0:T(8,128)(2,1)S(1)}, u32[]{:S(2)}, u32[]{:S(2)}) %collective-permute-start.5) | collective-permute-done | bytes 163872 | tf_op jit(solution)/shard_map/ppermute | solution.py:79
  25.8 0.9 %pad_maximum_fusion.9 = bf16[128,1280]{1,0:T(8,128)(2,1)S(1)} fusion(bf16[128,640]{1,0:T(8,128)(2,1)S(1)} %collective-permute-done.5, bf16[128,640]{1,0:T(8,128)(2,1)} %collective-permute-done.4), kind=kLoop, calls=%fused_computation.53 | loop fusion | flops 655360 | bytes 655360 | tf_op jit(solution)/shard_map/concatenate | solution.py:78
  26.9 2.5 %collective-permute-done.11 = bf16[128,640]{1,0:T(8,128)(2,1)S(1)} collective-permute-done((bf16[128,640]{1,0:T(8,128)(2,1)}, bf16[128,640]{1,0:T(8,128)(2,1)S(1)}, u32[]{:S(2)}, u32[]{:S(2)}) %collective-permute-start.11) | collective-permute-done | bytes 163872 | tf_op jit(solution)/shard_map/ppermute | solution.py:79
  29.4 0.9 %pad_maximum_fusion.10 = bf16[128,1280]{1,0:T(8,128)(2,1)S(1)} fusion(bf16[128,640]{1,0:T(8,128)(2,1)S(1)} %collective-permute-done.11, bf16[128,640]{1,0:T(8,128)(2,1)} %collective-permute-done.10), kind=kLoop, calls=%fused_computation.54 | loop fusion | flops 655360 | bytes 655360 | tf_op jit(solution)/shard_map/concatenate | solution.py:78
  30.4 1.9 %collective-permute-done.17 = bf16[128,640]{1,0:T(8,128)(2,1)S(1)} collective-permute-done((bf16[128,640]{1,0:T(8,128)(2,1)S(1)}, bf16[128,640]{1,0:T(8,128)(2,1)S(1)}, u32[]{:S(2)}, u32[]{:S(2)}) %collective-permute-start.17) | collective-permute-done | bytes 163872 | tf_op jit(solution)/shard_map/ppermute | solution.py:79
  32.4 1.5 %fusion.12 = f32[128,512]{1,0:T(8,128)S(1)} fusion(bf16[2560,512]{1,0:T(8,128)(2,1)S(1)} %pad_maximum_fusion, bf16[128,1280]{1,0:T(8,128)(2,1)S(1)} %collective-permute-done.1, bf16[128,640]{1,0:T(8,128)(2,1)} %collective-permute-done, bf16[128,640]{1,0:T(8,128)(2,1)} %multiply_convert_fusion), kind=kOutput, calls=%fused_computation.58 | convolution fusion | flops 337510400 | bytes 3538944 | tf_op jit(solution)/shard_map/dot_general | solution.py:84
  33.9 1.5 %multiply_convert_fusion.1 = bf16[128,512]{1,0:T(8,128)(2,1)S(1)} fusion(f32[128,512]{1,0:T(8,128)S(1)} %fusion.12, bf16[128,1280]{1,0:T(8,128)(2,1)S(1)} %collective-permute-done.1, bf16[128,640]{1,0:T(8,128)(2,1)} %collective-permute-done, bf16[128,640]{1,0:T(8,128)(2,1)} %multiply_convert_fusion, bf16[640,512]{1,0:T(8,128)(2,1)S(1)} %copy-done.3, ...), kind=kOutput, calls=%fused_computation.59 | convolution fusion | flops 348389376 | bytes 3670016 | tf_op jit(solution)/shard_map/dot_general | solution.py:85
  35.4 0.3 convolution_convert_fusion.6
  35.8 0.6 collective-permute-start.2
  36.3 1.0 %pad_maximum_fusion.5 = bf16[128,2560]{1,0:T(8,128)(2,1)S(1)} fusion(bf16[128,1280]{1,0:T(8,128)(2,1)S(1)} %collective-permute-done.6, bf16[128,640]{1,0:T(8,128)(2,1)S(1)} %collective-permute-done.5, bf16[128,640]{1,0:T(8,128)(2,1)} %collective-permute-done.4), kind=kLoop, calls=%fused_computation.20 | loop fusion | flops 1966080 | bytes 1310720 | tf_op jit(solution)/shard_map/concatenate | solution.py:80
  37.9 0.5 fusion.16
  38.4 0.7 fusion.1
  39.2 0.3 convolution_convert_fusion.4
  39.5 0.4 collective-permute-start.7
  40.0 1.0 %pad_maximum_fusion.6 = bf16[128,2560]{1,0:T(8,128)(2,1)S(1)} fusion(bf16[128,1280]{1,0:T(8,128)(2,1)S(1)} %collective-permute-done.12, bf16[128,640]{1,0:T(8,128)(2,1)S(1)} %collective-permute-done.11, bf16[128,640]{1,0:T(8,128)(2,1)} %collective-permute-done.10), kind=kLoop, calls=%fused_computation.21 | loop fusion | flops 1966080 | bytes 1310720 | tf_op jit(solution)/shard_map/concatenate | solution.py:80
  41.6 0.5 fusion.17
  42.1 0.7 fusion.2
  42.8 0.3 convolution_convert_fusion.2
  43.2 0.4 collective-permute-start.13
  43.7 1.0 %collective-permute-start.3 = (bf16[128,640]{1,0:T(8,128)(2,1)S(1)}, bf16[128,640]{1,0:T(8,128)(2,1)S(1)}, u32[]{:S(2)}, u32[]{:S(2)}) collective-permute-start(bf16[128,640]{1,0:T(8,128)(2,1)S(1)} %slice.67), channel_id=1, source_target_pairs={{0,2},{1,3},{2,0},{3,1},{4,6},{5,7},{6,4},{7,5},{8,10},{9,11},{10,... | collective-permute-start | bytes 491528 | tf_op jit(solution)/shard_map/ppermute | solution.py:103
  44.7 1.2 %collective-permute-start.8 = (bf16[128,640]{1,0:T(8,128)(2,1)S(1)}, bf16[128,640]{1,0:T(8,128)(2,1)S(1)}, u32[]{:S(2)}, u32[]{:S(2)}) collective-permute-start(bf16[128,640]{1,0:T(8,128)(2,1)S(1)} %slice.66), channel_id=1, source_target_pairs={{0,2},{1,3},{2,0},{3,1},{4,6},{5,7},{6,4},{7,5},{8,10},{9,11},{10,... | collective-permute-start | bytes 491528 | tf_op jit(solution)/shard_map/ppermute | solution.py:103
  45.9 0.3 convert_add_fusion
  46.3 1.0 %collective-permute-start.14 = (bf16[128,640]{1,0:T(8,128)(2,1)S(1)}, bf16[128,640]{1,0:T(8,128)(2,1)S(1)}, u32[]{:S(2)}, u32[]{:S(2)}) collective-permute-start(bf16[128,640]{1,0:T(8,128)(2,1)S(1)} %slice.65), channel_id=1, source_target_pairs={{0,2},{1,3},{2,0},{3,1},{4,6},{5,7},{6,4},{7,5},{8,10},{9,11},{10,... | collective-permute-start | bytes 491528 | tf_op jit(solution)/shard_map/ppermute | solution.py:103
  47.3 0.5 fusion.18
  47.8 0.7 fusion.3
  48.5 0.4 convolution_convert_fusion
  49.0 5.4 %collective-permute-done.8 = bf16[128,640]{1,0:T(8,128)(2,1)S(1)} collective-permute-done((bf16[128,640]{1,0:T(8,128)(2,1)S(1)}, bf16[128,640]{1,0:T(8,128)(2,1)S(1)}, u32[]{:S(2)}, u32[]{:S(2)}) %collective-permute-start.8) | collective-permute-done | bytes 163872 | tf_op jit(solution)/shard_map/ppermute | solution.py:103
  54.4 2.3 %collective-permute-start.9 = (bf16[128,640]{1,0:T(8,128)(2,1)S(1)}, bf16[128,640]{1,0:T(8,128)(2,1)S(1)}, u32[]{:S(2)}, u32[]{:S(2)}) collective-permute-start(bf16[128,640]{1,0:T(8,128)(2,1)S(1)} %fusion.5), channel_id=1, source_target_pairs={{0,8},{4,12},{8,0},{12,4},{1,9},{5,13},{9,1},{13,5},{2,10},{6,14},... | collective-permute-start | bytes 491528 | tf_op jit(solution)/shard_map/ppermute | solution.py:108
  57.1 3.2 %collective-permute-start.15 = (bf16[128,640]{1,0:T(8,128)(2,1)S(1)}, bf16[128,640]{1,0:T(8,128)(2,1)S(1)}, u32[]{:S(2)}, u32[]{:S(2)}) collective-permute-start(bf16[128,640]{1,0:T(8,128)(2,1)S(1)} %fusion.4), channel_id=1, source_target_pairs={{0,12},{4,8},{8,4},{12,0},{1,13},{5,9},{9,5},{13,1},{2,14},{6,10},... | collective-permute-start | bytes 491528 | tf_op jit(solution)/shard_map/ppermute | solution.py:108
  60.3 0.4 add_convert_fusion
  60.8 2.0 %collective-permute-start.21 = (bf16[128,640]{1,0:T(8,128)(2,1)S(1)}, bf16[128,640]{1,0:T(8,128)(2,1)S(1)}, u32[]{:S(2)}, u32[]{:S(2)}) collective-permute-start(bf16[128,640]{1,0:T(8,128)(2,1)S(1)} %get-tuple-element.24), channel_id=1, source_target_pairs={{0,6},{1,7},{2,4},{3,5},{4,2},{5,3},{6,0},{7,1},{8,14},{9,15},{10,... | collective-permute-start | bytes 491528 | tf_op jit(solution)/shard_map/ppermute | solution.py:98
  62.8 5.0 %collective-permute-done.9 = bf16[128,640]{1,0:T(8,128)(2,1)S(1)} collective-permute-done((bf16[128,640]{1,0:T(8,128)(2,1)S(1)}, bf16[128,640]{1,0:T(8,128)(2,1)S(1)}, u32[]{:S(2)}, u32[]{:S(2)}) %collective-permute-start.9) | collective-permute-done | bytes 163872 | tf_op jit(solution)/shard_map/ppermute | solution.py:108
  67.8 2.8 %collective-permute-done.20 = bf16[128,640]{1,0:T(8,128)(2,1)S(1)} collective-permute-done((bf16[128,640]{1,0:T(8,128)(2,1)S(1)}, bf16[128,640]{1,0:T(8,128)(2,1)S(1)}, u32[]{:S(2)}, u32[]{:S(2)}) %collective-permute-start.20) | collective-permute-done | bytes 163872 | tf_op jit(solution)/shard_map/ppermute | solution.py:96
  70.6 3.8 %collective-permute-done.21 = bf16[128,640]{1,0:T(8,128)(2,1)S(1)} collective-permute-done((bf16[128,640]{1,0:T(8,128)(2,1)S(1)}, bf16[128,640]{1,0:T(8,128)(2,1)S(1)}, u32[]{:S(2)}, u32[]{:S(2)}) %collective-permute-start.21) | collective-permute-done | bytes 163872 | tf_op jit(solution)/shard_map/ppermute | solution.py:98
  74.4 0.9 %fusion.10 = bf16[128,640]{1,0:T(8,128)(2,1)} fusion(f32[128,1280]{1,0:T(8,128)S(1)} %convert_add_fusion.2, bf16[128,640]{1,0:T(8,128)(2,1)S(1)} %collective-permute-done.21, bf16[128,640]{1,0:T(8,128)(2,1)S(1)} %collective-permute-done.20, bf16[128,640]{1,0:T(8,128)(2,1)S(1)} %collective-permute-done.15, bf16[128,640]{1,0:T(8,128)(2,1)S(1)} %collective-permute-done.9, ...), kind=kLoop, calls=%fused_computation.51 | loop fusion | flops 1228800 | bytes 1311232 | tf_op jit(solution)/shard_map/convert_element_type | solution.py:112
  (44 shorter events, 3.0 us)
Async XLA Ops:
  1.7 18.5 %collective-permute-start = (bf16[128,640]{1,0:T(8,128)(2,1)}, bf16[128,640]{1,0:T(8,128)(2,1)}, u32[]{:S(2)}, u32[]{:S(2)}) collective-permute-start(bf16[128,640]{1,0:T(8,128)(2,1)} %multiply_convert_fusion), channel_id=1, source_target_pairs={{0,2},{1,3},{2,0},{3,1},{4,6},{5,7},{6,4},{7,5},{8,10},{9,11},{10,... | collective-permute-start | bytes 491528 | tf_op jit(solution)/shard_map/ppermute | solution.py:79
  4.6 15.1 %collective-permute-start.4 = (bf16[128,640]{1,0:T(8,128)(2,1)}, bf16[128,640]{1,0:T(8,128)(2,1)}, u32[]{:S(2)}, u32[]{:S(2)}) collective-permute-start(bf16[128,640]{1,0:T(8,128)(2,1)} %multiply_convert_fusion), channel_id=1, source_target_pairs={{0,8},{4,12},{8,0},{12,4},{1,9},{5,13},{9,1},{13,5},{2,10},{6,14},... | collective-permute-start | bytes 491528 | tf_op jit(solution)/shard_map/ppermute | solution.py:66
  7.2 14.1 %collective-permute-start.10 = (bf16[128,640]{1,0:T(8,128)(2,1)}, bf16[128,640]{1,0:T(8,128)(2,1)}, u32[]{:S(2)}, u32[]{:S(2)}) collective-permute-start(bf16[128,640]{1,0:T(8,128)(2,1)} %multiply_convert_fusion), channel_id=1, source_target_pairs={{0,12},{4,8},{8,4},{12,0},{1,13},{5,9},{9,5},{13,1},{2,14},{6,10},... | collective-permute-start | bytes 491528 | tf_op jit(solution)/shard_map/ppermute | solution.py:66
  8.6 14.4 %collective-permute-start.16 = (bf16[128,640]{1,0:T(8,128)(2,1)}, bf16[128,640]{1,0:T(8,128)(2,1)S(1)}, u32[]{:S(2)}, u32[]{:S(2)}) collective-permute-start(bf16[128,640]{1,0:T(8,128)(2,1)} %multiply_convert_fusion), channel_id=1, source_target_pairs={{0,4},{4,0},{8,12},{12,8},{1,5},{5,1},{9,13},{13,9},{2,6},{6,2},{1... | collective-permute-start | bytes 491528 | tf_op jit(solution)/shard_map/ppermute | solution.py:66
  8.8 2.5 %copy-start = (bf16[1,2560,512]{2,1,0:T(8,128)(2,1)S(1)}, bf16[1,2560,512]{2,1,0:T(8,128)(2,1)}, u32[]{:S(2)}) copy-start(bf16[1,2560,512]{2,1,0:T(8,128)(2,1)} %param.10) | copy-start | bytes 7864324
  12.6 1.7 %copy-start.1 = (bf16[1,512,2560]{2,1,0:T(8,128)(2,1)S(1)}, bf16[1,512,2560]{2,1,0:T(8,128)(2,1)}, u32[]{:S(2)}) copy-start(bf16[1,512,2560]{2,1,0:T(8,128)(2,1)} %param.11) | copy-start | bytes 7864324
  19.7 6.1 %collective-permute-start.5 = (bf16[128,640]{1,0:T(8,128)(2,1)}, bf16[128,640]{1,0:T(8,128)(2,1)S(1)}, u32[]{:S(2)}, u32[]{:S(2)}) collective-permute-start(bf16[128,640]{1,0:T(8,128)(2,1)} %collective-permute-done.4), channel_id=1, source_target_pairs={{0,2},{1,3},{2,0},{3,1},{4,6},{5,7},{6,4},{7,5},{8,10},{9,11},{10,... | collective-permute-start | bytes 491528 | tf_op jit(solution)/shard_map/ppermute | solution.py:79
  21.2 11.2 %collective-permute-start.1 = (bf16[128,1280]{1,0:T(8,128)(2,1)S(1)}, bf16[128,1280]{1,0:T(8,128)(2,1)S(1)}, u32[]{:S(2)}, u32[]{:S(2)}) collective-permute-start(bf16[128,1280]{1,0:T(8,128)(2,1)S(1)} %pad_maximum_fusion.8), channel_id=1, source_target_pairs={{0,1},{1,0},{2,3},{3,2},{4,5},{5,4},{6,7},{7,6},{8,9},{9,8},{10,11... | collective-permute-start | bytes 983048 | tf_op jit(solution)/shard_map/ppermute | solution.py:81
  21.3 8.1 %collective-permute-start.11 = (bf16[128,640]{1,0:T(8,128)(2,1)}, bf16[128,640]{1,0:T(8,128)(2,1)S(1)}, u32[]{:S(2)}, u32[]{:S(2)}) collective-permute-start(bf16[128,640]{1,0:T(8,128)(2,1)} %collective-permute-done.10), channel_id=1, source_target_pairs={{0,2},{1,3},{2,0},{3,1},{4,6},{5,7},{6,4},{7,5},{8,10},{9,11},{10,... | collective-permute-start | bytes 491528 | tf_op jit(solution)/shard_map/ppermute | solution.py:79
  22.9 9.3 %collective-permute-start.17 = (bf16[128,640]{1,0:T(8,128)(2,1)S(1)}, bf16[128,640]{1,0:T(8,128)(2,1)S(1)}, u32[]{:S(2)}, u32[]{:S(2)}) collective-permute-start(bf16[128,640]{1,0:T(8,128)(2,1)S(1)} %collective-permute-done.16), channel_id=1, source_target_pairs={{0,2},{1,3},{2,0},{3,1},{4,6},{5,7},{6,4},{7,5},{8,10},{9,11},{10,... | collective-permute-start | bytes 491528 | tf_op jit(solution)/shard_map/ppermute | solution.py:79
  26.8 7.1 %copy-start.2 = (bf16[640,512]{1,0:T(8,128)(2,1)S(1)}, bf16[640,512]{1,0:T(8,128)(2,1)}, u32[]{:S(2)}) copy-start(bf16[640,512]{1,0:T(8,128)(2,1)} %get-tuple-element.16) | copy-start | bytes 1966084
  26.8 7.1 %copy-start.3 = (bf16[640,512]{1,0:T(8,128)(2,1)S(1)}, bf16[640,512]{1,0:T(8,128)(2,1)}, u32[]{:S(2)}) copy-start(bf16[640,512]{1,0:T(8,128)(2,1)} %get-tuple-element.17) | copy-start | bytes 1966084
  26.8 7.1 %copy-start.4 = (bf16[640,512]{1,0:T(8,128)(2,1)S(1)}, bf16[640,512]{1,0:T(8,128)(2,1)}, u32[]{:S(2)}) copy-start(bf16[640,512]{1,0:T(8,128)(2,1)} %get-tuple-element.18) | copy-start | bytes 1966084
  26.8 9.5 %collective-permute-start.6 = (bf16[128,1280]{1,0:T(8,128)(2,1)S(1)}, bf16[128,1280]{1,0:T(8,128)(2,1)S(1)}, u32[]{:S(2)}, u32[]{:S(2)}) collective-permute-start(bf16[128,1280]{1,0:T(8,128)(2,1)S(1)} %pad_maximum_fusion.9), channel_id=1, source_target_pairs={{0,1},{1,0},{2,3},{3,2},{4,5},{5,4},{6,7},{7,6},{8,9},{9,8},{10,11... | collective-permute-start | bytes 983048 | tf_op jit(solution)/shard_map/ppermute | solution.py:81
  30.3 9.7 %collective-permute-start.12 = (bf16[128,1280]{1,0:T(8,128)(2,1)S(1)}, bf16[128,1280]{1,0:T(8,128)(2,1)S(1)}, u32[]{:S(2)}, u32[]{:S(2)}) collective-permute-start(bf16[128,1280]{1,0:T(8,128)(2,1)S(1)} %pad_maximum_fusion.10), channel_id=1, source_target_pairs={{0,1},{1,0},{2,3},{3,2},{4,5},{5,4},{6,7},{7,6},{8,9},{9,8},{10,11... | collective-permute-start | bytes 983048 | tf_op jit(solution)/shard_map/ppermute | solution.py:81
  32.3 11.4 %collective-permute-start.18 = (bf16[128,1280]{1,0:T(8,128)(2,1)S(1)}, bf16[128,1280]{1,0:T(8,128)(2,1)S(1)}, u32[]{:S(2)}, u32[]{:S(2)}) collective-permute-start(bf16[128,1280]{1,0:T(8,128)(2,1)S(1)} %pad_maximum_fusion.11), channel_id=1, source_target_pairs={{0,1},{1,0},{2,3},{3,2},{4,5},{5,4},{6,7},{7,6},{8,9},{9,8},{10,11... | collective-permute-start | bytes 983048 | tf_op jit(solution)/shard_map/ppermute | solution.py:81
  35.8 1.8 %collective-permute-start.2 = (bf16[128,1280]{1,0:T(8,128)(2,1)S(1)}, bf16[128,1280]{1,0:T(8,128)(2,1)S(1)}, u32[]{:S(2)}, u32[]{:S(2)}) collective-permute-start(bf16[128,1280]{1,0:T(8,128)(2,1)S(1)} %convolution_convert_fusion.6), channel_id=1, source_target_pairs={{0,1},{1,0},{2,3},{3,2},{4,5},{5,4},{6,7},{7,6},{8,9},{9,8},{10,11... | collective-permute-start | bytes 983048 | tf_op jit(solution)/shard_map/ppermute | solution.py:90
  39.5 1.7 %collective-permute-start.7 = (bf16[128,1280]{1,0:T(8,128)(2,1)S(1)}, bf16[128,1280]{1,0:T(8,128)(2,1)S(1)}, u32[]{:S(2)}, u32[]{:S(2)}) collective-permute-start(bf16[128,1280]{1,0:T(8,128)(2,1)S(1)} %convolution_convert_fusion.4), channel_id=1, source_target_pairs={{0,1},{1,0},{2,3},{3,2},{4,5},{5,4},{6,7},{7,6},{8,9},{9,8},{10,11... | collective-permute-start | bytes 983048 | tf_op jit(solution)/shard_map/ppermute | solution.py:90
  43.2 2.7 %collective-permute-start.13 = (bf16[128,1280]{1,0:T(8,128)(2,1)S(1)}, bf16[128,1280]{1,0:T(8,128)(2,1)S(1)}, u32[]{:S(2)}, u32[]{:S(2)}) collective-permute-start(bf16[128,1280]{1,0:T(8,128)(2,1)S(1)} %convolution_convert_fusion.2), channel_id=1, source_target_pairs={{0,1},{1,0},{2,3},{3,2},{4,5},{5,4},{6,7},{7,6},{8,9},{9,8},{10,11... | collective-permute-start | bytes 983048 | tf_op jit(solution)/shard_map/ppermute | solution.py:90
  43.7 19.1 %collective-permute-start.3 = (bf16[128,640]{1,0:T(8,128)(2,1)S(1)}, bf16[128,640]{1,0:T(8,128)(2,1)S(1)}, u32[]{:S(2)}, u32[]{:S(2)}) collective-permute-start(bf16[128,640]{1,0:T(8,128)(2,1)S(1)} %slice.67), channel_id=1, source_target_pairs={{0,2},{1,3},{2,0},{3,1},{4,6},{5,7},{6,4},{7,5},{8,10},{9,11},{10,... | collective-permute-start | bytes 491528 | tf_op jit(solution)/shard_map/ppermute | solution.py:103
  44.7 9.6 %collective-permute-start.8 = (bf16[128,640]{1,0:T(8,128)(2,1)S(1)}, bf16[128,640]{1,0:T(8,128)(2,1)S(1)}, u32[]{:S(2)}, u32[]{:S(2)}) collective-permute-start(bf16[128,640]{1,0:T(8,128)(2,1)S(1)} %slice.66), channel_id=1, source_target_pairs={{0,2},{1,3},{2,0},{3,1},{4,6},{5,7},{6,4},{7,5},{8,10},{9,11},{10,... | collective-permute-start | bytes 491528 | tf_op jit(solution)/shard_map/ppermute | solution.py:103
  46.3 10.8 %collective-permute-start.14 = (bf16[128,640]{1,0:T(8,128)(2,1)S(1)}, bf16[128,640]{1,0:T(8,128)(2,1)S(1)}, u32[]{:S(2)}, u32[]{:S(2)}) collective-permute-start(bf16[128,640]{1,0:T(8,128)(2,1)S(1)} %slice.65), channel_id=1, source_target_pairs={{0,2},{1,3},{2,0},{3,1},{4,6},{5,7},{6,4},{7,5},{8,10},{9,11},{10,... | collective-permute-start | bytes 491528 | tf_op jit(solution)/shard_map/ppermute | solution.py:103
  48.9 13.9 %copy-start.5 = (s32[128,1]{0,1:T(1,128)S(1)}, s32[128,1]{0,1:T(1,128)}, u32[]{:S(2)}) copy-start(s32[128,1]{0,1:T(1,128)} %param.8) | copy-start | bytes 1540
  48.9 11.4 %collective-permute-start.19 = (bf16[128,1280]{1,0:T(8,128)(2,1)S(1)}, bf16[128,1280]{1,0:T(8,128)(2,1)S(1)}, u32[]{:S(2)}, u32[]{:S(2)}) collective-permute-start(bf16[128,1280]{1,0:T(8,128)(2,1)S(1)} %convolution_convert_fusion), channel_id=1, source_target_pairs={{0,1},{1,0},{2,3},{3,2},{4,5},{5,4},{6,7},{7,6},{8,9},{9,8},{10,11... | collective-permute-start | bytes 983048 | tf_op jit(solution)/shard_map/ppermute | solution.py:90
  54.4 13.4 %collective-permute-start.9 = (bf16[128,640]{1,0:T(8,128)(2,1)S(1)}, bf16[128,640]{1,0:T(8,128)(2,1)S(1)}, u32[]{:S(2)}, u32[]{:S(2)}) collective-permute-start(bf16[128,640]{1,0:T(8,128)(2,1)S(1)} %fusion.5), channel_id=1, source_target_pairs={{0,8},{4,12},{8,0},{12,4},{1,9},{5,13},{9,1},{13,5},{2,10},{6,14},... | collective-permute-start | bytes 491528 | tf_op jit(solution)/shard_map/ppermute | solution.py:108
  57.1 10.7 %collective-permute-start.15 = (bf16[128,640]{1,0:T(8,128)(2,1)S(1)}, bf16[128,640]{1,0:T(8,128)(2,1)S(1)}, u32[]{:S(2)}, u32[]{:S(2)}) collective-permute-start(bf16[128,640]{1,0:T(8,128)(2,1)S(1)} %fusion.4), channel_id=1, source_target_pairs={{0,12},{4,8},{8,4},{12,0},{1,13},{5,9},{9,5},{13,1},{2,14},{6,10},... | collective-permute-start | bytes 491528 | tf_op jit(solution)/shard_map/ppermute | solution.py:108
  60.7 9.9 %collective-permute-start.20 = (bf16[128,640]{1,0:T(8,128)(2,1)S(1)}, bf16[128,640]{1,0:T(8,128)(2,1)S(1)}, u32[]{:S(2)}, u32[]{:S(2)}) collective-permute-start(bf16[128,640]{1,0:T(8,128)(2,1)S(1)} %get-tuple-element.23), channel_id=1, source_target_pairs={{0,4},{4,0},{8,12},{12,8},{1,5},{5,1},{9,13},{13,9},{2,6},{6,2},{1... | collective-permute-start | bytes 491528 | tf_op jit(solution)/shard_map/ppermute | solution.py:96
  60.8 13.6 %collective-permute-start.21 = (bf16[128,640]{1,0:T(8,128)(2,1)S(1)}, bf16[128,640]{1,0:T(8,128)(2,1)S(1)}, u32[]{:S(2)}, u32[]{:S(2)}) collective-permute-start(bf16[128,640]{1,0:T(8,128)(2,1)S(1)} %get-tuple-element.24), channel_id=1, source_target_pairs={{0,6},{1,7},{2,4},{3,5},{4,2},{5,3},{6,0},{7,1},{8,14},{9,15},{10,... | collective-permute-start | bytes 491528 | tf_op jit(solution)/shard_map/ppermute | solution.py:98

commit v13 on v10

--- a/solution.py
+++ b/solution.py
@@ -87,6 +87,9 @@
         keep = jnp.dot(hidden, down_keep, preferred_element_type=jnp.float32).astype(jnp.bfloat16)
         send = jnp.dot(hidden, down_send, preferred_element_type=jnp.float32).astype(jnp.bfloat16)
         previous = keep
+        if wave is waves[0] and len(waves) > 1:
+            others, _ = lax.optimization_barrier(([blocks[k] for k in range(1, n_expert)], keep))
+            blocks = [blocks[0]] + others
         over_c = keep.astype(jnp.float32) + lax.ppermute(
             send, "tensor", _xor_pairs(n_tensor, 1)).astype(jnp.float32)
         summed = over_c[:, :width] + lax.ppermute(

time: 67 us -> 75.6 us (1.13)
  waiting for transfers between devices: 28.5 us -> 33.5 us
  starting transfers between devices: 21.1 us -> 24.6 us
    ppermute x3, waiting for transfers between devices: 5.9 us -> 11.9 us  [gathered(): lax.ppermute(scaled, 'expert', _xor_pairs(n_expert, k))]
    ppermute x3, starting transfers between devices: 5.53 us -> 7.78 us  [gathered(): lax.ppermute(part.astype(jnp.bfloat16), 'expert', _xor_pairs(n_expert, k))]
    ppermute x4, waiting for transfers between devices: 9.45 us -> 7.99 us  [gathered(): lax.ppermute(piece, 'tensor', _xor_pairs(n_tensor, 2))]
    ppermute x4, waiting for transfers between devices: 0.01 us -> 1.39 us  [gathered(): lax.ppermute(pair, 'tensor', _xor_pairs(n_tensor, 1))]
    ppermute x4, waiting for transfers between devices: 2.47 us -> 1.21 us  [gathered(): lax.ppermute(send, 'tensor', _xor_pairs(n_tensor, 1)).astype(jnp.float32)]
    ppermute x4, starting transfers between devices: 5.55 us -> 6.45 us  [gathered(): lax.ppermute(piece, 'tensor', _xor_pairs(n_tensor, 2))]
  transfers between devices with their start and end apart: 22 -> 22, of which waited for: 12 -> 12; matrix products, arithmetic and copies ran while one was open for 19% -> 15% of each run, Pallas kernels for 0% -> 0%
where the time goes in v13:
time: 75.6 us; the launch traced here: 75.4 us
  waiting for transfers between devices  33.5 us (44%)
  starting transfers between devices  24.6 us (33%)
  matrix products  9.28 us (12%)
  local copies, waits for them, and re-layouts  5.24 us (7%)
  other arithmetic  2.46 us (3%)
    ppermute x3, waiting for transfers between devices, gathered(): lax.ppermute(scaled, 'expert', _xor_pairs(n_expert, k))  11.9 us
    ppermute x4, waiting for transfers between devices, gathered(): lax.ppermute(piece, 'tensor', _xor_pairs(n_tensor, 2))  7.99 us
    ppermute x3, starting transfers between devices, gathered(): lax.ppermute(part.astype(jnp.bfloat16), 'expert', _xor_pairs(n_expert, k))  7.78 us
    ppermute x4, starting transfers between devices, gathered(): lax.ppermute(piece, 'tensor', _xor_pairs(n_tensor, 2))  6.45 us
    ppermute x3, waiting for transfers between devices, gathered(): lax.ppermute(part.astype(jnp.bfloat16), 'expert', _xor_pairs(n_expert, k))  5.81 us
    ppermute x4, waiting for transfers between devices, gathered(): lax.ppermute(over_c[:, width:].astype(jnp.bfloat16), 'tensor', _xor_pairs...  5.26 us
    ppermute x4, starting transfers between devices, gathered(): lax.ppermute(over_c[:, width:].astype(jnp.bfloat16), 'tensor', _xor_pairs...  4.51 us
    ppermute x3, starting transfers between devices, gathered(): lax.ppermute(scaled, 'expert', _xor_pairs(n_expert, k))  4.4 us
  transfers between devices with their start and end apart: 22, of which 12 were waited for; matrix products, arithmetic and copies ran while one was open for 15% of the time, Pallas kernels for 0%

profile of v13, /device:TPU:0, one launch (start us, length us, event | category | flops | bytes accessed | tf_op | source)
XLA Modules:
  0.0 75.4 jit_solution(1901821916443308692)
XLA Ops:
  0.0 1.0 %multiply_convert_fusion = bf16[128,640]{1,0:T(8,128)(2,1)S(1)} fusion(bf16[128,640]{1,0:T(8,128)(2,1)} %param.6, f32[128]{0:T(128)} %param.7), kind=kLoop, calls=%fused_computation.59 | loop fusion | flops 245760 | bytes 328192 | tf_op jit(solution)/shard_map/convert_element_type | solution.py:64
  1.0 3.0 %collective-permute-start = (bf16[128,640]{1,0:T(8,128)(2,1)S(1)}, bf16[128,640]{1,0:T(8,128)(2,1)S(1)}, u32[]{:S(2)}, u32[]{:S(2)}) collective-permute-start(bf16[128,640]{1,0:T(8,128)(2,1)S(1)} %multiply_convert_fusion), channel_id=1, source_target_pairs={{0,2},{1,3},{2,0},{3,1},{4,6},{5,7},{6,4},{7,5},{8,10},{9,11},{10,... | collective-permute-start | bytes 491528 | tf_op jit(solution)/shard_map/ppermute | solution.py:79
  4.0 2.0 %dynamic-slice_bitcast_fusion.11 = (bf16[640,512]{1,0:T(8,128)(2,1)S(1)}, bf16[640,512]{1,0:T(8,128)(2,1)S(1)}, bf16[640,512]{1,0:T(8,128)(2,1)S(1)}, bf16[640,512]{1,0:T(8,128)(2,1)S(1)}) fusion(bf16[1,2560,512]{2,1,0:T(8,128)(2,1)} %param.9, s32[]{:T(128)S(6)} %select_n.48, s32[]{:T(128)S(6)} %select_n.49, s32[]{:T(128)S(6)} %select_n.51, s32[]{:T(128)S(6)} %select_n.50), kind=kLoop, calls=%fused_computation.38 | loop fusion | bytes 5242896 | tf_op jit(solution)/shard_map/dynamic_slice | solution.py:55
  6.0 0.5 copy-done
  6.7 1.6 %copy-done.1 = bf16[1,512,2560]{2,1,0:T(8,128)(2,1)S(1)} copy-done((bf16[1,512,2560]{2,1,0:T(8,128)(2,1)S(1)}, bf16[1,512,2560]{2,1,0:T(8,128)(2,1)}, u32[]{:S(2)}) %copy-start.1) | copy-done | bytes 2621464
  8.9 1.4 %collective-permute-done.1 = bf16[128,1280]{1,0:T(8,128)(2,1)S(1)} collective-permute-done((bf16[128,1280]{1,0:T(8,128)(2,1)S(1)}, bf16[128,1280]{1,0:T(8,128)(2,1)S(1)}, u32[]{:S(2)}, u32[]{:S(2)}) %collective-permute-start.1) | collective-permute-done | bytes 327712 | tf_op jit(solution)/shard_map/ppermute | solution.py:81
  10.3 0.5 fusion.13
  10.8 0.5 multiply_convert_fusion.1
  11.3 0.3 convolution_convert_fusion.6
  11.8 1.6 %collective-permute-start.4 = (bf16[128,640]{1,0:T(8,128)(2,1)S(1)}, bf16[128,640]{1,0:T(8,128)(2,1)S(1)}, u32[]{:S(2)}, u32[]{:S(2)}) collective-permute-start(bf16[128,640]{1,0:T(8,128)(2,1)S(1)} %multiply_convert_fusion), channel_id=1, source_target_pairs={{0,4},{4,0},{8,12},{12,8},{1,5},{5,1},{9,13},{13,9},{2,6},{6,2},{1... | collective-permute-start | bytes 491528 | tf_op jit(solution)/shard_map/ppermute | solution.py:66
  13.4 2.6 %collective-permute-start.5 = (bf16[128,640]{1,0:T(8,128)(2,1)S(1)}, bf16[128,640]{1,0:T(8,128)(2,1)S(1)}, u32[]{:S(2)}, u32[]{:S(2)}) collective-permute-start(bf16[128,640]{1,0:T(8,128)(2,1)S(1)} %multiply_convert_fusion), channel_id=1, source_target_pairs={{0,8},{4,12},{8,0},{12,4},{1,9},{5,13},{9,1},{13,5},{2,10},{6,14},... | collective-permute-start | bytes 491528 | tf_op jit(solution)/shard_map/ppermute | solution.py:66
  16.3 0.3 convert_add_fusion.3
  16.6 4.7 %collective-permute-done.4 = bf16[128,640]{1,0:T(8,128)(2,1)S(1)} collective-permute-done((bf16[128,640]{1,0:T(8,128)(2,1)S(1)}, bf16[128,640]{1,0:T(8,128)(2,1)S(1)}, u32[]{:S(2)}, u32[]{:S(2)}) %collective-permute-start.4) | collective-permute-done | bytes 163872 | tf_op jit(solution)/shard_map/ppermute | solution.py:66
  21.3 7.1 %collective-permute-done.5 = bf16[128,640]{1,0:T(8,128)(2,1)S(1)} collective-permute-done((bf16[128,640]{1,0:T(8,128)(2,1)S(1)}, bf16[128,640]{1,0:T(8,128)(2,1)S(1)}, u32[]{:S(2)}, u32[]{:S(2)}) %collective-permute-start.5) | collective-permute-done | bytes 163872 | tf_op jit(solution)/shard_map/ppermute | solution.py:66
  28.5 1.4 %collective-permute-start.7 = (bf16[128,640]{1,0:T(8,128)(2,1)S(1)}, bf16[128,640]{1,0:T(8,128)(2,1)S(1)}, u32[]{:S(2)}, u32[]{:S(2)}) collective-permute-start(bf16[128,640]{1,0:T(8,128)(2,1)S(1)} %collective-permute-done.5), channel_id=1, source_target_pairs={{0,2},{1,3},{2,0},{3,1},{4,6},{5,7},{6,4},{7,5},{8,10},{9,11},{10,... | collective-permute-start | bytes 491528 | tf_op jit(solution)/shard_map/ppermute | solution.py:79
  29.9 0.6 collective-permute-start.12
  30.5 1.4 %collective-permute-start.17 = (bf16[128,640]{1,0:T(8,128)(2,1)S(1)}, bf16[128,640]{1,0:T(8,128)(2,1)S(1)}, u32[]{:S(2)}, u32[]{:S(2)}) collective-permute-start(bf16[128,640]{1,0:T(8,128)(2,1)S(1)} %collective-permute-done.4), channel_id=1, source_target_pairs={{0,2},{1,3},{2,0},{3,1},{4,6},{5,7},{6,4},{7,5},{8,10},{9,11},{10,... | collective-permute-start | bytes 491528 | tf_op jit(solution)/shard_map/ppermute | solution.py:79
  31.9 3.7 %collective-permute-done.7 = bf16[128,640]{1,0:T(8,128)(2,1)S(1)} collective-permute-done((bf16[128,640]{1,0:T(8,128)(2,1)S(1)}, bf16[128,640]{1,0:T(8,128)(2,1)S(1)}, u32[]{:S(2)}, u32[]{:S(2)}) %collective-permute-start.7) | collective-permute-done | bytes 163872 | tf_op jit(solution)/shard_map/ppermute | solution.py:79
  35.7 2.6 %collective-permute-done.12 = bf16[128,640]{1,0:T(8,128)(2,1)S(1)} collective-permute-done((bf16[128,640]{1,0:T(8,128)(2,1)S(1)}, bf16[128,640]{1,0:T(8,128)(2,1)S(1)}, u32[]{:S(2)}, u32[]{:S(2)}) %collective-permute-start.12) | collective-permute-done | bytes 163872 | tf_op jit(solution)/shard_map/ppermute | solution.py:79
  38.5 1.6 %collective-permute-done.17 = bf16[128,640]{1,0:T(8,128)(2,1)S(1)} collective-permute-done((bf16[128,640]{1,0:T(8,128)(2,1)S(1)}, bf16[128,640]{1,0:T(8,128)(2,1)S(1)}, u32[]{:S(2)}, u32[]{:S(2)}) %collective-permute-start.17) | collective-permute-done | bytes 163872 | tf_op jit(solution)/shard_map/ppermute | solution.py:79
  40.3 0.5 fusion.16
  40.8 0.7 fusion.1
  41.5 0.3 convolution_convert_fusion.4
  41.9 0.6 collective-permute-start.9
  42.5 1.2 %collective-permute-done.9 = bf16[128,1280]{1,0:T(8,128)(2,1)S(1)} collective-permute-done((bf16[128,1280]{1,0:T(8,128)(2,1)S(1)}, bf16[128,1280]{1,0:T(8,128)(2,1)S(1)}, u32[]{:S(2)}, u32[]{:S(2)}) %collective-permute-start.9) | collective-permute-done | bytes 327712 | tf_op jit(solution)/shard_map/ppermute | solution.py:93
  44.1 0.5 fusion.17
  44.6 0.7 fusion.2
  45.3 0.3 convolution_convert_fusion.2
  45.7 0.4 collective-permute-start.14
  46.2 0.7 slice.70
  46.9 1.4 %collective-permute-start.10 = (bf16[128,640]{1,0:T(8,128)(2,1)}, bf16[128,640]{1,0:T(8,128)(2,1)S(1)}, u32[]{:S(2)}, u32[]{:S(2)}) collective-permute-start(bf16[128,640]{1,0:T(8,128)(2,1)} %slice.70), channel_id=1, source_target_pairs={{0,2},{1,3},{2,0},{3,1},{4,6},{5,7},{6,4},{7,5},{8,10},{9,11},{10,... | collective-permute-start | bytes 491528 | tf_op jit(solution)/shard_map/ppermute | solution.py:95
  48.3 0.3 convert_add_fusion.1
  48.6 0.5 fusion.18
  49.1 0.7 fusion.3
  49.9 1.1 %convolution_convert_fusion = bf16[128,1280]{1,0:T(8,128)(2,1)} fusion(bf16[128,512]{1,0:T(8,128)(2,1)S(1)} %fusion.3, bf16[512,640]{1,0:T(8,128)(2,1)S(1)} %get-tuple-element.19, bf16[512,640]{1,0:T(8,128)(2,1)S(1)} %get-tuple-element.20), kind=kOutput, calls=%fused_computation.2 | convolution fusion | flops 170557440 | bytes 1769472 | tf_op jit(solution)/shard_map/dot_general | solution.py:88
  51.0 0.9 %collective-permute-start.3 = (bf16[128,640]{1,0:T(8,128)(2,1)S(1)}, bf16[128,640]{1,0:T(8,128)(2,1)S(1)}, u32[]{:S(2)}, u32[]{:S(2)}) collective-permute-start(bf16[128,640]{1,0:T(8,128)(2,1)S(1)} %slice.71), channel_id=1, source_target_pairs={{0,2},{1,3},{2,0},{3,1},{4,6},{5,7},{6,4},{7,5},{8,10},{9,11},{10,... | collective-permute-start | bytes 491528 | tf_op jit(solution)/shard_map/ppermute | solution.py:95
  51.9 1.4 %collective-permute-done.10 = bf16[128,640]{1,0:T(8,128)(2,1)S(1)} collective-permute-done((bf16[128,640]{1,0:T(8,128)(2,1)}, bf16[128,640]{1,0:T(8,128)(2,1)S(1)}, u32[]{:S(2)}, u32[]{:S(2)}) %collective-permute-start.10) | collective-permute-done | bytes 163872 | tf_op jit(solution)/shard_map/ppermute | solution.py:95
  53.3 5.0 %collective-permute-start.11 = (bf16[128,640]{1,0:T(8,128)(2,1)S(1)}, bf16[128,640]{1,0:T(8,128)(2,1)S(1)}, u32[]{:S(2)}, u32[]{:S(2)}) collective-permute-start(bf16[128,640]{1,0:T(8,128)(2,1)S(1)} %fusion.6), channel_id=1, source_target_pairs={{0,8},{4,12},{8,0},{12,4},{1,9},{5,13},{9,1},{13,5},{2,10},{6,14},... | collective-permute-start | bytes 491528 | tf_op jit(solution)/shard_map/ppermute | solution.py:100
  58.4 1.5 %collective-permute-start.15 = (bf16[128,640]{1,0:T(8,128)(2,1)S(1)}, bf16[128,640]{1,0:T(8,128)(2,1)S(1)}, u32[]{:S(2)}, u32[]{:S(2)}) collective-permute-start(bf16[128,640]{1,0:T(8,128)(2,1)S(1)} %slice.69), channel_id=1, source_target_pairs={{0,2},{1,3},{2,0},{3,1},{4,6},{5,7},{6,4},{7,5},{8,10},{9,11},{10,... | collective-permute-start | bytes 491528 | tf_op jit(solution)/shard_map/ppermute | solution.py:95
  59.8 1.4 %convert_add_fusion = f32[128,1280]{1,0:T(8,128)S(1)} fusion(bf16[128,1280]{1,0:T(8,128)(2,1)} %collective-permute-done.19, bf16[128,512]{1,0:T(8,128)(2,1)} %copy-done.3, bf16[512,640]{1,0:T(8,128)(2,1)S(1)} %get-tuple-element.18, bf16[512,640]{1,0:T(8,128)(2,1)S(1)} %get-tuple-element.17), kind=kOutput, calls=%fused_computation.23 | convolution fusion | flops 171048960 | bytes 2424832 | tf_op jit(solution)/shard_map/dot_general | solution.py:87
  61.3 0.7 collective-permute-start.20
  62.0 2.9 %collective-permute-done.15 = bf16[128,640]{1,0:T(8,128)(2,1)S(1)} collective-permute-done((bf16[128,640]{1,0:T(8,128)(2,1)S(1)}, bf16[128,640]{1,0:T(8,128)(2,1)S(1)}, u32[]{:S(2)}, u32[]{:S(2)}) %collective-permute-start.15) | collective-permute-done | bytes 163872 | tf_op jit(solution)/shard_map/ppermute | solution.py:95
  64.9 1.4 %collective-permute-start.16 = (bf16[128,640]{1,0:T(8,128)(2,1)S(1)}, bf16[128,640]{1,0:T(8,128)(2,1)S(1)}, u32[]{:S(2)}, u32[]{:S(2)}) collective-permute-start(bf16[128,640]{1,0:T(8,128)(2,1)S(1)} %fusion.5), channel_id=1, source_target_pairs={{0,12},{4,8},{8,4},{12,0},{1,13},{5,9},{9,5},{13,1},{2,14},{6,10},... | collective-permute-start | bytes 491528 | tf_op jit(solution)/shard_map/ppermute | solution.py:100
  66.3 1.0 %collective-permute-done.20 = bf16[128,640]{1,0:T(8,128)(2,1)S(1)} collective-permute-done((bf16[128,640]{1,0:T(8,128)(2,1)S(1)}, bf16[128,640]{1,0:T(8,128)(2,1)S(1)}, u32[]{:S(2)}, u32[]{:S(2)}) %collective-permute-start.20) | collective-permute-done | bytes 163872 | tf_op jit(solution)/shard_map/ppermute | solution.py:95
  67.3 1.4 %collective-permute-start.21 = (bf16[128,640]{1,0:T(8,128)(2,1)S(1)}, bf16[128,640]{1,0:T(8,128)(2,1)S(1)}, u32[]{:S(2)}, u32[]{:S(2)}) collective-permute-start(bf16[128,640]{1,0:T(8,128)(2,1)S(1)} %fusion.4), channel_id=1, source_target_pairs={{0,4},{4,0},{8,12},{12,8},{1,5},{5,1},{9,13},{13,9},{2,6},{6,2},{1... | collective-permute-start | bytes 491528 | tf_op jit(solution)/shard_map/ppermute | solution.py:100
  68.8 4.0 %collective-permute-done.16 = bf16[128,640]{1,0:T(8,128)(2,1)S(1)} collective-permute-done((bf16[128,640]{1,0:T(8,128)(2,1)S(1)}, bf16[128,640]{1,0:T(8,128)(2,1)S(1)}, u32[]{:S(2)}, u32[]{:S(2)}) %collective-permute-start.16) | collective-permute-done | bytes 163872 | tf_op jit(solution)/shard_map/ppermute | solution.py:100
  72.8 1.8 %collective-permute-done.21 = bf16[128,640]{1,0:T(8,128)(2,1)S(1)} collective-permute-done((bf16[128,640]{1,0:T(8,128)(2,1)S(1)}, bf16[128,640]{1,0:T(8,128)(2,1)S(1)}, u32[]{:S(2)}, u32[]{:S(2)}) %collective-permute-start.21) | collective-permute-done | bytes 163872 | tf_op jit(solution)/shard_map/ppermute | solution.py:100
  74.6 0.9 %fusion.11 = bf16[128,640]{1,0:T(8,128)(2,1)} fusion(f32[128,1280]{1,0:T(8,128)S(1)} %convert_add_fusion.3, bf16[128,640]{1,0:T(8,128)(2,1)S(1)} %collective-permute-done.21, bf16[128,640]{1,0:T(8,128)(2,1)S(1)} %collective-permute-done.16, bf16[128,640]{1,0:T(8,128)(2,1)S(1)} %collective-permute-done.11, bf16[128,640]{1,0:T(8,128)(2,1)S(1)} %collective-permute-done.3, ...), kind=kLoop, calls=%fused_computation.54 | loop fusion | flops 1064960 | bytes 1147392 | tf_op jit(solution)/shard_map/convert_element_type | solution.py:104
  (41 shorter events, 2.1 us)
Async XLA Ops:
  1.0 7.5 %collective-permute-start = (bf16[128,640]{1,0:T(8,128)(2,1)S(1)}, bf16[128,640]{1,0:T(8,128)(2,1)S(1)}, u32[]{:S(2)}, u32[]{:S(2)}) collective-permute-start(bf16[128,640]{1,0:T(8,128)(2,1)S(1)} %multiply_convert_fusion), channel_id=1, source_target_pairs={{0,2},{1,3},{2,0},{3,1},{4,6},{5,7},{6,4},{7,5},{8,10},{9,11},{10,... | collective-permute-start | bytes 491528 | tf_op jit(solution)/shard_map/ppermute | solution.py:79
  4.0 2.5 %copy-start = (bf16[1,2560,512]{2,1,0:T(8,128)(2,1)S(1)}, bf16[1,2560,512]{2,1,0:T(8,128)(2,1)}, u32[]{:S(2)}) copy-start(bf16[1,2560,512]{2,1,0:T(8,128)(2,1)} %param.10) | copy-start | bytes 7864324
  6.5 1.7 %copy-start.1 = (bf16[1,512,2560]{2,1,0:T(8,128)(2,1)S(1)}, bf16[1,512,2560]{2,1,0:T(8,128)(2,1)}, u32[]{:S(2)}) copy-start(bf16[1,512,2560]{2,1,0:T(8,128)(2,1)} %param.11) | copy-start | bytes 7864324
  8.6 1.7 %collective-permute-start.1 = (bf16[128,1280]{1,0:T(8,128)(2,1)S(1)}, bf16[128,1280]{1,0:T(8,128)(2,1)S(1)}, u32[]{:S(2)}, u32[]{:S(2)}) collective-permute-start(bf16[128,1280]{1,0:T(8,128)(2,1)S(1)} %pad_maximum_fusion.8), channel_id=1, source_target_pairs={{0,1},{1,0},{2,3},{3,2},{4,5},{5,4},{6,7},{7,6},{8,9},{9,8},{10,11... | collective-permute-start | bytes 983048 | tf_op jit(solution)/shard_map/ppermute | solution.py:81
  11.6 4.6 %collective-permute-start.2 = (bf16[128,1280]{1,0:T(8,128)(2,1)S(1)}, bf16[128,1280]{1,0:T(8,128)(2,1)S(1)}, u32[]{:S(2)}, u32[]{:S(2)}) collective-permute-start(bf16[128,1280]{1,0:T(8,128)(2,1)S(1)} %convolution_convert_fusion.6), channel_id=1, source_target_pairs={{0,1},{1,0},{2,3},{3,2},{4,5},{5,4},{6,7},{7,6},{8,9},{9,8},{10,11... | collective-permute-start | bytes 983048 | tf_op jit(solution)/shard_map/ppermute | solution.py:93
  11.8 9.5 %collective-permute-start.4 = (bf16[128,640]{1,0:T(8,128)(2,1)S(1)}, bf16[128,640]{1,0:T(8,128)(2,1)S(1)}, u32[]{:S(2)}, u32[]{:S(2)}) collective-permute-start(bf16[128,640]{1,0:T(8,128)(2,1)S(1)} %multiply_convert_fusion), channel_id=1, source_target_pairs={{0,4},{4,0},{8,12},{12,8},{1,5},{5,1},{9,13},{13,9},{2,6},{6,2},{1... | collective-permute-start | bytes 491528 | tf_op jit(solution)/shard_map/ppermute | solution.py:66
  13.4 15.0 %collective-permute-start.5 = (bf16[128,640]{1,0:T(8,128)(2,1)S(1)}, bf16[128,640]{1,0:T(8,128)(2,1)S(1)}, u32[]{:S(2)}, u32[]{:S(2)}) collective-permute-start(bf16[128,640]{1,0:T(8,128)(2,1)S(1)} %multiply_convert_fusion), channel_id=1, source_target_pairs={{0,8},{4,12},{8,0},{12,4},{1,9},{5,13},{9,1},{13,5},{2,10},{6,14},... | collective-permute-start | bytes 491528 | tf_op jit(solution)/shard_map/ppermute | solution.py:66
  16.0 12.4 %collective-permute-start.6 = (bf16[128,640]{1,0:T(8,128)(2,1)S(1)}, bf16[128,640]{1,0:T(8,128)(2,1)S(1)}, u32[]{:S(2)}, u32[]{:S(2)}) collective-permute-start(bf16[128,640]{1,0:T(8,128)(2,1)S(1)} %multiply_convert_fusion), channel_id=1, source_target_pairs={{0,12},{4,8},{8,4},{12,0},{1,13},{5,9},{9,5},{13,1},{2,14},{6,10},... | collective-permute-start | bytes 491528 | tf_op jit(solution)/shard_map/ppermute | solution.py:66
  28.5 7.1 %collective-permute-start.7 = (bf16[128,640]{1,0:T(8,128)(2,1)S(1)}, bf16[128,640]{1,0:T(8,128)(2,1)S(1)}, u32[]{:S(2)}, u32[]{:S(2)}) collective-permute-start(bf16[128,640]{1,0:T(8,128)(2,1)S(1)} %collective-permute-done.5), channel_id=1, source_target_pairs={{0,2},{1,3},{2,0},{3,1},{4,6},{5,7},{6,4},{7,5},{8,10},{9,11},{10,... | collective-permute-start | bytes 491528 | tf_op jit(solution)/shard_map/ppermute | solution.py:79
  29.9 8.5 %collective-permute-start.12 = (bf16[128,640]{1,0:T(8,128)(2,1)S(1)}, bf16[128,640]{1,0:T(8,128)(2,1)S(1)}, u32[]{:S(2)}, u32[]{:S(2)}) collective-permute-start(bf16[128,640]{1,0:T(8,128)(2,1)S(1)} %collective-permute-done.6), channel_id=1, source_target_pairs={{0,2},{1,3},{2,0},{3,1},{4,6},{5,7},{6,4},{7,5},{8,10},{9,11},{10,... | collective-permute-start | bytes 491528 | tf_op jit(solution)/shard_map/ppermute | solution.py:79
  30.5 9.6 %collective-permute-start.17 = (bf16[128,640]{1,0:T(8,128)(2,1)S(1)}, bf16[128,640]{1,0:T(8,128)(2,1)S(1)}, u32[]{:S(2)}, u32[]{:S(2)}) collective-permute-start(bf16[128,640]{1,0:T(8,128)(2,1)S(1)} %collective-permute-done.4), channel_id=1, source_target_pairs={{0,2},{1,3},{2,0},{3,1},{4,6},{5,7},{6,4},{7,5},{8,10},{9,11},{10,... | collective-permute-start | bytes 491528 | tf_op jit(solution)/shard_map/ppermute | solution.py:79
  35.6 4.6 %collective-permute-start.8 = (bf16[128,1280]{1,0:T(8,128)(2,1)S(1)}, bf16[128,1280]{1,0:T(8,128)(2,1)S(1)}, u32[]{:S(2)}, u32[]{:S(2)}) collective-permute-start(bf16[128,1280]{1,0:T(8,128)(2,1)S(1)} %pad_maximum_fusion.9), channel_id=1, source_target_pairs={{0,1},{1,0},{2,3},{3,2},{4,5},{5,4},{6,7},{7,6},{8,9},{9,8},{10,11... | collective-permute-start | bytes 983048 | tf_op jit(solution)/shard_map/ppermute | solution.py:81
  38.4 4.1 %collective-permute-start.13 = (bf16[128,1280]{1,0:T(8,128)(2,1)S(1)}, bf16[128,1280]{1,0:T(8,128)(2,1)S(1)}, u32[]{:S(2)}, u32[]{:S(2)}) collective-permute-start(bf16[128,1280]{1,0:T(8,128)(2,1)S(1)} %pad_maximum_fusion.10), channel_id=1, source_target_pairs={{0,1},{1,0},{2,3},{3,2},{4,5},{5,4},{6,7},{7,6},{8,9},{9,8},{10,11... | collective-permute-start | bytes 983048 | tf_op jit(solution)/shard_map/ppermute | solution.py:81
  40.1 6.0 %collective-permute-start.18 = (bf16[128,1280]{1,0:T(8,128)(2,1)S(1)}, bf16[128,1280]{1,0:T(8,128)(2,1)S(1)}, u32[]{:S(2)}, u32[]{:S(2)}) collective-permute-start(bf16[128,1280]{1,0:T(8,128)(2,1)S(1)} %pad_maximum_fusion.11), channel_id=1, source_target_pairs={{0,1},{1,0},{2,3},{3,2},{4,5},{5,4},{6,7},{7,6},{8,9},{9,8},{10,11... | collective-permute-start | bytes 983048 | tf_op jit(solution)/shard_map/ppermute | solution.py:81
  41.9 1.8 %collective-permute-start.9 = (bf16[128,1280]{1,0:T(8,128)(2,1)S(1)}, bf16[128,1280]{1,0:T(8,128)(2,1)S(1)}, u32[]{:S(2)}, u32[]{:S(2)}) collective-permute-start(bf16[128,1280]{1,0:T(8,128)(2,1)S(1)} %convolution_convert_fusion.4), channel_id=1, source_target_pairs={{0,1},{1,0},{2,3},{3,2},{4,5},{5,4},{6,7},{7,6},{8,9},{9,8},{10,11... | collective-permute-start | bytes 983048 | tf_op jit(solution)/shard_map/ppermute | solution.py:93
  45.7 2.6 %collective-permute-start.14 = (bf16[128,1280]{1,0:T(8,128)(2,1)S(1)}, bf16[128,1280]{1,0:T(8,128)(2,1)S(1)}, u32[]{:S(2)}, u32[]{:S(2)}) collective-permute-start(bf16[128,1280]{1,0:T(8,128)(2,1)S(1)} %convolution_convert_fusion.2), channel_id=1, source_target_pairs={{0,1},{1,0},{2,3},{3,2},{4,5},{5,4},{6,7},{7,6},{8,9},{9,8},{10,11... | collective-permute-start | bytes 983048 | tf_op jit(solution)/shard_map/ppermute | solution.py:93
  46.9 6.5 %collective-permute-start.10 = (bf16[128,640]{1,0:T(8,128)(2,1)}, bf16[128,640]{1,0:T(8,128)(2,1)S(1)}, u32[]{:S(2)}, u32[]{:S(2)}) collective-permute-start(bf16[128,640]{1,0:T(8,128)(2,1)} %slice.70), channel_id=1, source_target_pairs={{0,2},{1,3},{2,0},{3,1},{4,6},{5,7},{6,4},{7,5},{8,10},{9,11},{10,... | collective-permute-start | bytes 491528 | tf_op jit(solution)/shard_map/ppermute | solution.py:95
  49.9 1.1 %copy-start.3 = (bf16[128,512]{1,0:T(8,128)(2,1)}, bf16[128,512]{1,0:T(8,128)(2,1)S(1)}, u32[]{:S(2)}) copy-start(bf16[128,512]{1,0:T(8,128)(2,1)S(1)} %fusion.3) | copy-start | bytes 393220
  51.0 8.9 %collective-permute-start.19 = (bf16[128,1280]{1,0:T(8,128)(2,1)}, bf16[128,1280]{1,0:T(8,128)(2,1)}, u32[]{:S(2)}, u32[]{:S(2)}) collective-permute-start(bf16[128,1280]{1,0:T(8,128)(2,1)} %convolution_convert_fusion), channel_id=1, source_target_pairs={{0,1},{1,0},{2,3},{3,2},{4,5},{5,4},{6,7},{7,6},{8,9},{9,8},{10,11... | collective-permute-start | bytes 983048 | tf_op jit(solution)/shard_map/ppermute | solution.py:93
  51.0 17.7 %copy-start.2 = (s32[128,1]{0,1:T(1,128)S(1)}, s32[128,1]{0,1:T(1,128)}, u32[]{:S(2)}) copy-start(s32[128,1]{0,1:T(1,128)} %param.8) | copy-start | bytes 1540
  51.0 17.7 %collective-permute-start.3 = (bf16[128,640]{1,0:T(8,128)(2,1)S(1)}, bf16[128,640]{1,0:T(8,128)(2,1)S(1)}, u32[]{:S(2)}, u32[]{:S(2)}) collective-permute-start(bf16[128,640]{1,0:T(8,128)(2,1)S(1)} %slice.71), channel_id=1, source_target_pairs={{0,2},{1,3},{2,0},{3,1},{4,6},{5,7},{6,4},{7,5},{8,10},{9,11},{10,... | collective-permute-start | bytes 491528 | tf_op jit(solution)/shard_map/ppermute | solution.py:95
  53.3 15.4 %collective-permute-start.11 = (bf16[128,640]{1,0:T(8,128)(2,1)S(1)}, bf16[128,640]{1,0:T(8,128)(2,1)S(1)}, u32[]{:S(2)}, u32[]{:S(2)}) collective-permute-start(bf16[128,640]{1,0:T(8,128)(2,1)S(1)} %fusion.6), channel_id=1, source_target_pairs={{0,8},{4,12},{8,0},{12,4},{1,9},{5,13},{9,1},{13,5},{2,10},{6,14},... | collective-permute-start | bytes 491528 | tf_op jit(solution)/shard_map/ppermute | solution.py:100
  58.4 6.5 %collective-permute-start.15 = (bf16[128,640]{1,0:T(8,128)(2,1)S(1)}, bf16[128,640]{1,0:T(8,128)(2,1)S(1)}, u32[]{:S(2)}, u32[]{:S(2)}) collective-permute-start(bf16[128,640]{1,0:T(8,128)(2,1)S(1)} %slice.69), channel_id=1, source_target_pairs={{0,2},{1,3},{2,0},{3,1},{4,6},{5,7},{6,4},{7,5},{8,10},{9,11},{10,... | collective-permute-start | bytes 491528 | tf_op jit(solution)/shard_map/ppermute | solution.py:95
  61.3 6.0 %collective-permute-start.20 = (bf16[128,640]{1,0:T(8,128)(2,1)S(1)}, bf16[128,640]{1,0:T(8,128)(2,1)S(1)}, u32[]{:S(2)}, u32[]{:S(2)}) collective-permute-start(bf16[128,640]{1,0:T(8,128)(2,1)S(1)} %slice.68), channel_id=1, source_target_pairs={{0,2},{1,3},{2,0},{3,1},{4,6},{5,7},{6,4},{7,5},{8,10},{9,11},{10,... | collective-permute-start | bytes 491528 | tf_op jit(solution)/shard_map/ppermute | solution.py:95
  64.9 7.8 %collective-permute-start.16 = (bf16[128,640]{1,0:T(8,128)(2,1)S(1)}, bf16[128,640]{1,0:T(8,128)(2,1)S(1)}, u32[]{:S(2)}, u32[]{:S(2)}) collective-permute-start(bf16[128,640]{1,0:T(8,128)(2,1)S(1)} %fusion.5), channel_id=1, source_target_pairs={{0,12},{4,8},{8,4},{12,0},{1,13},{5,9},{9,5},{13,1},{2,14},{6,10},... | collective-permute-start | bytes 491528 | tf_op jit(solution)/shard_map/ppermute | solution.py:100
  67.3 7.3 %collective-permute-start.21 = (bf16[128,640]{1,0:T(8,128)(2,1)S(1)}, bf16[128,640]{1,0:T(8,128)(2,1)S(1)}, u32[]{:S(2)}, u32[]{:S(2)}) collective-permute-start(bf16[128,640]{1,0:T(8,128)(2,1)S(1)} %fusion.4), channel_id=1, source_target_pairs={{0,4},{4,0},{8,12},{12,8},{1,5},{5,1},{9,13},{13,9},{2,6},{6,2},{1... | collective-permute-start | bytes 491528 | tf_op jit(solution)/shard_map/ppermute | solution.py:100

commit v14 on v10

--- a/solution.py
+++ b/solution.py
@@ -70,7 +70,8 @@
     up_w = _slots(up_weight[0], t, width, 0)
     down_keep = _slots(down_weight[0], t, width, 1, _ORDER[:2])
     down_send = _slots(down_weight[0], t, width, 1, _ORDER[2:])
-    waves = [[k] for k in [0] + list(range(2, n_expert)) + [1][:n_expert - 1]]
+    waves = [[0], list(range(2, n_expert)), [1][:n_expert - 1]]
+    waves = [wave for wave in waves if wave]
     total = None
     previous = None
     for wave in waves:

time: 67 us -> 72.9 us (1.088)
  waiting for transfers between devices: 28.5 us -> 33 us
  starting transfers between devices: 21.1 us -> 23.2 us
  local copies, waits for them, and re-layouts: 5.18 us -> 4.32 us
  other arithmetic: 2.46 us -> 3.2 us
    ppermute x3, starting transfers between devices: 5.53 us -> 9.67 us  [gathered(): lax.ppermute(part.astype(jnp.bfloat16), 'expert', _xor_pairs(n_expert, k))]
    ppermute x3, waiting for transfers between devices: 5.58 us -> 9.36 us  [gathered(): lax.ppermute(part.astype(jnp.bfloat16), 'expert', _xor_pairs(n_expert, k))]
    ppermute x4 -> x3, waiting for transfers between devices: 9.45 us -> 6.57 us  [gathered(): lax.ppermute(piece, 'tensor', _xor_pairs(n_tensor, 2))]
    unnamed x8 -> x5, local copies, waits for them, and re-layouts: 2.04 us -> 0.02 us
    ppermute x4 -> x3, waiting for transfers between devices: 5.05 us -> 6.85 us  [gathered(): lax.ppermute(over_c[:, width:].astype(jnp.bfloat16), 'tensor', _xor_pairs...]
    ppermute x3, waiting for transfers between devices: 5.9 us -> 7.38 us  [gathered(): lax.ppermute(scaled, 'expert', _xor_pairs(n_expert, k))]
    ppermute x4 -> x3, starting transfers between devices: 3.82 us -> 2.63 us  [gathered(): lax.ppermute(over_c[:, width:].astype(jnp.bfloat16), 'tensor', _xor_pairs...]
    dynamic_slice x3 -> x2, local copies, waits for them, and re-layouts: 2.4 us -> 3.43 us  [_slots(): lax.dynamic_slice_in_dim(weight, (t ^ k) * width, width, axis=axis)]
  transfers between devices with their start and end apart: 22 -> 18, of which waited for: 12 -> 7; matrix products, arithmetic and copies ran while one was open for 19% -> 16% of each run, Pallas kernels for 0% -> 0%
where the time goes in v14:
time: 72.9 us; the launch traced here: 72.7 us
  waiting for transfers between devices  33 us (45%)
  starting transfers between devices  23.2 us (32%)
  matrix products  8.75 us (12%)
  local copies, waits for them, and re-layouts  4.32 us (6%)
  other arithmetic  3.2 us (4%)
    ppermute x3, starting transfers between devices, gathered(): lax.ppermute(part.astype(jnp.bfloat16), 'expert', _xor_pairs(n_expert, k))  9.67 us
    ppermute x3, waiting for transfers between devices, gathered(): lax.ppermute(part.astype(jnp.bfloat16), 'expert', _xor_pairs(n_expert, k))  9.36 us
    ppermute x3, waiting for transfers between devices, gathered(): lax.ppermute(scaled, 'expert', _xor_pairs(n_expert, k))  7.38 us
    ppermute x3, waiting for transfers between devices, gathered(): lax.ppermute(over_c[:, width:].astype(jnp.bfloat16), 'tensor', _xor_pairs...  6.85 us
    ppermute x3, waiting for transfers between devices, gathered(): lax.ppermute(piece, 'tensor', _xor_pairs(n_tensor, 2))  6.57 us
    ppermute x3, starting transfers between devices, gathered(): lax.ppermute(piece, 'tensor', _xor_pairs(n_tensor, 2))  5.16 us
    ppermute x3, starting transfers between devices, gathered(): lax.ppermute(scaled, 'expert', _xor_pairs(n_expert, k))  4.17 us
    dynamic_slice x2, local copies, waits for them, and re-layouts, _slots(): lax.dynamic_slice_in_dim(weight, (t ^ k) * width, width, axis=axis)  3.43 us
  transfers between devices with their start and end apart: 18, of which 7 were waited for; matrix products, arithmetic and copies ran while one was open for 16% of the time, Pallas kernels for 0%

profile of v14, /device:TPU:0, one launch (start us, length us, event | category | flops | bytes accessed | tf_op | source)
XLA Modules:
  0.0 72.7 jit_solution(2683855292853600116)
XLA Ops:
  0.0 1.0 %multiply_convert_fusion = bf16[128,640]{1,0:T(8,128)(2,1)S(1)} fusion(bf16[128,640]{1,0:T(8,128)(2,1)} %param.6, f32[128]{0:T(128)} %param.7), kind=kLoop, calls=%fused_computation.49 | loop fusion | flops 245760 | bytes 328192 | tf_op jit(solution)/shard_map/convert_element_type | solution.py:64
  1.0 3.0 %collective-permute-start = (bf16[128,640]{1,0:T(8,128)(2,1)S(1)}, bf16[128,640]{1,0:T(8,128)(2,1)S(1)}, u32[]{:S(2)}, u32[]{:S(2)}) collective-permute-start(bf16[128,640]{1,0:T(8,128)(2,1)S(1)} %multiply_convert_fusion), channel_id=1, source_target_pairs={{0,2},{1,3},{2,0},{3,1},{4,6},{5,7},{6,4},{7,5},{8,10},{9,11},{10,... | collective-permute-start | bytes 491528 | tf_op jit(solution)/shard_map/ppermute | solution.py:80
  4.0 2.6 %collective-permute-start.4 = (bf16[128,640]{1,0:T(8,128)(2,1)S(1)}, bf16[128,640]{1,0:T(8,128)(2,1)S(1)}, u32[]{:S(2)}, u32[]{:S(2)}) collective-permute-start(bf16[128,640]{1,0:T(8,128)(2,1)S(1)} %multiply_convert_fusion), channel_id=1, source_target_pairs={{0,8},{4,12},{8,0},{12,4},{1,9},{5,13},{9,1},{13,5},{2,10},{6,14},... | collective-permute-start | bytes 491528 | tf_op jit(solution)/shard_map/ppermute | solution.py:66
  6.6 1.3 %collective-permute-start.5 = (bf16[128,640]{1,0:T(8,128)(2,1)S(1)}, bf16[128,640]{1,0:T(8,128)(2,1)S(1)}, u32[]{:S(2)}, u32[]{:S(2)}) collective-permute-start(bf16[128,640]{1,0:T(8,128)(2,1)S(1)} %multiply_convert_fusion), channel_id=1, source_target_pairs={{0,12},{4,8},{8,4},{12,0},{1,13},{5,9},{9,5},{13,1},{2,14},{6,10},... | collective-permute-start | bytes 491528 | tf_op jit(solution)/shard_map/ppermute | solution.py:66
  8.0 0.2 collective-permute-start.12
  8.2 3.2 %dynamic-slice_bitcast_fusion.7 = (bf16[640,512]{1,0:T(8,128)(2,1)S(1)}, bf16[640,512]{1,0:T(8,128)(2,1)S(1)}, bf16[640,512]{1,0:T(8,128)(2,1)S(1)}, bf16[640,51...) fusion(bf16[1,2560,512]{2,1,0:T(8,128)(2,1)} %param.10, ...), kind=kLoop, calls=%fused_computation.32 | loop fusion | bytes 10485776 | tf_op jit(solution)/shard_map/dynamic_slice | solution.py:55
  11.4 7.4 %collective-permute-done.4 = bf16[128,640]{1,0:T(8,128)(2,1)S(1)} collective-permute-done((bf16[128,640]{1,0:T(8,128)(2,1)S(1)}, bf16[128,640]{1,0:T(8,128)(2,1)S(1)}, u32[]{:S(2)}, u32[]{:S(2)}) %collective-permute-start.4) | collective-permute-done | bytes 163872 | tf_op jit(solution)/shard_map/ppermute | solution.py:66
  18.8 0.0 collective-permute-done.5
  18.8 0.5 collective-permute-start.6
  19.4 0.1 collective-permute-start.1
  19.5 0.2 dynamic-slice_bitcast_fusion.3
  19.7 1.6 %collective-permute-start.13 = (bf16[128,640]{1,0:T(8,128)(2,1)S(1)}, bf16[128,640]{1,0:T(8,128)(2,1)S(1)}, u32[]{:S(2)}, u32[]{:S(2)}) collective-permute-start(bf16[128,640]{1,0:T(8,128)(2,1)S(1)} %collective-permute-done.12), channel_id=1, source_target_pairs={{0,2},{1,3},{2,0},{3,1},{4,6},{5,7},{6,4},{7,5},{8,10},{9,11},{10,... | collective-permute-start | bytes 491528 | tf_op jit(solution)/shard_map/ppermute | solution.py:80
  21.4 6.6 %collective-permute-done.6 = bf16[256,640]{1,0:T(8,128)(2,1)S(1)} collective-permute-done((bf16[256,640]{1,0:T(8,128)(2,1)S(1)}, bf16[256,640]{1,0:T(8,128)(2,1)S(1)}, u32[]{:S(2)}, u32[]{:S(2)}) %collective-permute-start.6) | collective-permute-done | bytes 327712 | tf_op jit(solution)/shard_map/ppermute | solution.py:80
  28.0 0.1 collective-permute-start.7
  28.1 0.5 fusion.11
  28.6 0.5 multiply_convert_fusion.1
  29.1 0.3 convolution_convert_fusion.4
  29.5 0.6 collective-permute-start.2
  30.1 0.1 collective-permute-start.14
  30.1 1.1 %collective-permute-done.2 = bf16[128,1280]{1,0:T(8,128)(2,1)S(1)} collective-permute-done((bf16[128,1280]{1,0:T(8,128)(2,1)S(1)}, bf16[128,1280]{1,0:T(8,128)(2,1)S(1)}, u32[]{:S(2)}, u32[]{:S(2)}) %collective-permute-start.2) | collective-permute-done | bytes 327712 | tf_op jit(solution)/shard_map/ppermute | solution.py:91
  31.3 0.3 convert_add_fusion.2
  31.6 0.0 collective-permute-done.7
  31.6 0.1 pad_maximum_fusion.4
  31.7 1.1 %fusion.21 = f32[256,512]{1,0:T(8,128)S(1)} fusion(bf16[256,2560]{1,0:T(8,128)(2,1)S(1)} %pad_maximum_fusion.4, bf16[640,512]{1,0:T(8,128)(2,1)S(1)} %get-tuple-element.32, bf16[640,512]{1,0:T(8,128)(2,1)S(1)} %get-tuple-element.31, bf16[640,512]{1,0:T(8,128)(2,1)S(1)} %get-tuple-element.33, bf16[640,512]{1,0:T(8,128)(2,1)S(1)} %get-tuple-element.34), kind=kOutput, calls=%fused_computation.68 | convolution fusion | flops 681574400 | bytes 4456448 | tf_op jit(solution)/shard_map/dot_general | solution.py:85
  32.8 1.1 %fusion.1 = bf16[256,512]{1,0:T(8,128)(2,1)S(1)} fusion(bf16[256,2560]{1,0:T(8,128)(2,1)S(1)} %pad_maximum_fusion.4, f32[256,512]{1,0:T(8,128)S(1)} %fusion.21, bf16[640,512]{1,0:T(8,128)(2,1)S(1)} %get-tuple-element.15, bf16[640,512]{1,0:T(8,128)(2,1)S(1)} %get-tuple-element.16, bf16[640,512]{1,0:T(8,128)(2,1)S(1)} %get-tuple-element.14, ...), kind=kOutput, calls=%fused_computation.14 | convolution fusion | flops 682360832 | bytes 4718592 | tf_op jit(solution)/shard_map/dot_general | solution.py:86
  33.9 0.5 convolution_convert_fusion
  34.4 0.4 collective-permute-start.8
  34.9 0.0 collective-permute-done.14
  34.9 1.7 %collective-permute-done.8 = bf16[256,1280]{1,0:T(8,128)(2,1)S(1)} collective-permute-done((bf16[256,1280]{1,0:T(8,128)(2,1)S(1)}, bf16[256,1280]{1,0:T(8,128)(2,1)S(1)}, u32[]{:S(2)}, u32[]{:S(2)}) %collective-permute-start.8) | collective-permute-done | bytes 655392 | tf_op jit(solution)/shard_map/ppermute | solution.py:91
  36.6 0.5 convert_add_fusion
  37.1 0.7 %fusion.20 = f32[128,512]{1,0:T(8,128)S(1)} fusion(bf16[128,2560]{1,0:T(8,128)(2,1)S(1)} %pad_maximum_fusion.7, bf16[640,512]{1,0:T(8,128)(2,1)S(1)} %get-tuple-element.32, bf16[640,512]{1,0:T(8,128)(2,1)S(1)} %get-tuple-element.31, bf16[640,512]{1,0:T(8,128)(2,1)S(1)} %get-tuple-element.33, bf16[640,512]{1,0:T(8,128)(2,1)S(1)} %get-tuple-element.34), kind=kOutput, calls=%fused_computation.67 | convolution fusion | flops 346030080 | bytes 3538944 | tf_op jit(solution)/shard_map/dot_general | solution.py:85
  37.9 0.7 %fusion.2 = bf16[128,512]{1,0:T(8,128)(2,1)S(1)} fusion(bf16[128,2560]{1,0:T(8,128)(2,1)S(1)} %pad_maximum_fusion.7, f32[128,512]{1,0:T(8,128)S(1)} %fusion.20, bf16[640,512]{1,0:T(8,128)(2,1)S(1)} %get-tuple-element.15, bf16[640,512]{1,0:T(8,128)(2,1)S(1)} %get-tuple-element.16, bf16[640,512]{1,0:T(8,128)(2,1)S(1)} %get-tuple-element.14, ...), kind=kOutput, calls=%fused_computation.16 | convolution fusion | flops 346423296 | bytes 3670016 | tf_op jit(solution)/shard_map/dot_general | solution.py:86
  38.6 1.1 %convolution_convert_fusion.2 = bf16[128,1280]{1,0:T(8,128)(2,1)} fusion(bf16[128,512]{1,0:T(8,128)(2,1)S(1)} %fusion.2, bf16[512,640]{1,0:T(8,128)(2,1)S(1)} %get-tuple-element.11, bf16[512,640]{1,0:T(8,128)(2,1)S(1)} %get-tuple-element.12), kind=kOutput, calls=%fused_computation.4 | convolution fusion | flops 170557440 | bytes 1769472 | tf_op jit(solution)/shard_map/dot_general | solution.py:89
  39.7 0.4 collective-permute-start.15
  40.0 0.8 %slice.65 = bf16[256,640]{1,0:T(8,128)(2,1)} slice(f32[256,1280]{1,0:T(8,128)S(1)} %convert_add_fusion), slice={[0:256], [640:1280]} | slice | bytes 655360 | tf_op jit(solution)/shard_map/slice | solution.py:94
  40.8 0.5 collective-permute-start.9
  41.3 0.0 copy-start.1
  41.3 1.6 %collective-permute-start.3 = (bf16[128,640]{1,0:T(8,128)(2,1)S(1)}, bf16[128,640]{1,0:T(8,128)(2,1)S(1)}, u32[]{:S(2)}, u32[]{:S(2)}) collective-permute-start(bf16[128,640]{1,0:T(8,128)(2,1)S(1)} %slice.67), channel_id=1, source_target_pairs={{0,2},{1,3},{2,0},{3,1},{4,6},{5,7},{6,4},{7,5},{8,10},{9,11},{10,... | collective-permute-start | bytes 491528 | tf_op jit(solution)/shard_map/ppermute | solution.py:93
  42.9 1.3 %convert_add_fusion.1 = f32[128,1280]{1,0:T(8,128)S(1)} fusion(bf16[128,1280]{1,0:T(8,128)(2,1)} %collective-permute-done.15, bf16[128,512]{1,0:T(8,128)(2,1)S(1)} %fusion.2, bf16[512,640]{1,0:T(8,128)(2,1)S(1)} %get-tuple-element.10, bf16[512,640]{1,0:T(8,128)(2,1)S(1)} %get-tuple-element.9), kind=kOutput, calls=%fused_computation.23 | convolution fusion | flops 171048960 | bytes 2424832 | tf_op jit(solution)/shard_map/dot_general | solution.py:88
  44.3 0.5 collective-permute-start.16
  44.8 6.8 %collective-permute-done.9 = bf16[256,640]{1,0:T(8,128)(2,1)} collective-permute-done((bf16[256,640]{1,0:T(8,128)(2,1)}, bf16[256,640]{1,0:T(8,128)(2,1)}, u32[]{:S(2)}, u32[]{:S(2)}) %collective-permute-start.9) | collective-permute-done | bytes 327712 | tf_op jit(solution)/shard_map/ppermute | solution.py:93
  51.7 1.0 %fusion.3 = bf16[256,640]{1,0:T(8,128)(2,1)S(1)} fusion(f32[256,1280]{1,0:T(8,128)S(1)} %convert_add_fusion, bf16[256,640]{1,0:T(8,128)(2,1)} %collective-permute-done.9), kind=kLoop, calls=%fused_computation.19 | loop fusion | flops 491520 | bytes 1310720 | tf_op jit(solution)/shard_map/convert.2
  52.8 6.6 %collective-permute-start.10 = (bf16[128,640]{1,0:T(8,128)(2,1)S(1)}, bf16[128,640]{1,0:T(8,128)(2,1)S(1)}, u32[]{:S(2)}, u32[]{:S(2)}) collective-permute-start(bf16[128,640]{1,0:T(8,128)(2,1)S(1)} %get-tuple-element.21), channel_id=1, source_target_pairs={{0,8},{4,12},{8,0},{12,4},{1,9},{5,13},{9,1},{13,5},{2,10},{6,14},... | collective-permute-start | bytes 491528 | tf_op jit(solution)/shard_map/ppermute | solution.py:98
  59.3 0.4 collective-permute-start.11
  59.8 2.7 %collective-permute-start.17 = (bf16[128,640]{1,0:T(8,128)(2,1)S(1)}, bf16[128,640]{1,0:T(8,128)(2,1)S(1)}, u32[]{:S(2)}, u32[]{:S(2)}) collective-permute-start(bf16[128,640]{1,0:T(8,128)(2,1)S(1)} %fusion.4), channel_id=1, source_target_pairs={{0,4},{4,0},{8,12},{12,8},{1,5},{5,1},{9,13},{13,9},{2,6},{6,2},{1... | collective-permute-start | bytes 491528 | tf_op jit(solution)/shard_map/ppermute | solution.py:98
  62.5 7.2 %collective-permute-done.10 = bf16[128,640]{1,0:T(8,128)(2,1)S(1)} collective-permute-done((bf16[128,640]{1,0:T(8,128)(2,1)S(1)}, bf16[128,640]{1,0:T(8,128)(2,1)S(1)}, u32[]{:S(2)}, u32[]{:S(2)}) %collective-permute-start.10) | collective-permute-done | bytes 163872 | tf_op jit(solution)/shard_map/ppermute | solution.py:98
  69.7 2.1 %collective-permute-done.17 = bf16[128,640]{1,0:T(8,128)(2,1)S(1)} collective-permute-done((bf16[128,640]{1,0:T(8,128)(2,1)S(1)}, bf16[128,640]{1,0:T(8,128)(2,1)S(1)}, u32[]{:S(2)}, u32[]{:S(2)}) %collective-permute-start.17) | collective-permute-done | bytes 163872 | tf_op jit(solution)/shard_map/ppermute | solution.py:98
  71.8 0.9 %fusion.9 = bf16[128,640]{1,0:T(8,128)(2,1)} fusion(f32[128,1280]{1,0:T(8,128)S(1)} %convert_add_fusion.2, bf16[128,640]{1,0:T(8,128)(2,1)S(1)} %collective-permute-done.17, bf16[128,640]{1,0:T(8,128)(2,1)S(1)} %collective-permute-done.11, bf16[128,640]{1,0:T(8,128)(2,1)S(1)} %collective-permute-done.10, bf16[128,640]{1,0:T(8,128)(2,1)S(1)} %collective-permute-done.3, ...), kind=kLoop, calls=%fused_computation.46 | loop fusion | flops 1064960 | bytes 1147392 | tf_op jit(solution)/shard_map/convert_element_type | solution.py:102
  (22 shorter events, 0.3 us)
Async XLA Ops:
  1.0 18.3 %collective-permute-start = (bf16[128,640]{1,0:T(8,128)(2,1)S(1)}, bf16[128,640]{1,0:T(8,128)(2,1)S(1)}, u32[]{:S(2)}, u32[]{:S(2)}) collective-permute-start(bf16[128,640]{1,0:T(8,128)(2,1)S(1)} %multiply_convert_fusion), channel_id=1, source_target_pairs={{0,2},{1,3},{2,0},{3,1},{4,6},{5,7},{6,4},{7,5},{8,10},{9,11},{10,... | collective-permute-start | bytes 491528 | tf_op jit(solution)/shard_map/ppermute | solution.py:80
  4.0 14.7 %collective-permute-start.4 = (bf16[128,640]{1,0:T(8,128)(2,1)S(1)}, bf16[128,640]{1,0:T(8,128)(2,1)S(1)}, u32[]{:S(2)}, u32[]{:S(2)}) collective-permute-start(bf16[128,640]{1,0:T(8,128)(2,1)S(1)} %multiply_convert_fusion), channel_id=1, source_target_pairs={{0,8},{4,12},{8,0},{12,4},{1,9},{5,13},{9,1},{13,5},{2,10},{6,14},... | collective-permute-start | bytes 491528 | tf_op jit(solution)/shard_map/ppermute | solution.py:66
  6.6 12.2 %collective-permute-start.5 = (bf16[128,640]{1,0:T(8,128)(2,1)S(1)}, bf16[128,640]{1,0:T(8,128)(2,1)S(1)}, u32[]{:S(2)}, u32[]{:S(2)}) collective-permute-start(bf16[128,640]{1,0:T(8,128)(2,1)S(1)} %multiply_convert_fusion), channel_id=1, source_target_pairs={{0,12},{4,8},{8,4},{12,0},{1,13},{5,9},{9,5},{13,1},{2,14},{6,10},... | collective-permute-start | bytes 491528 | tf_op jit(solution)/shard_map/ppermute | solution.py:66
  8.0 11.8 %collective-permute-start.12 = (bf16[128,640]{1,0:T(8,128)(2,1)S(1)}, bf16[128,640]{1,0:T(8,128)(2,1)S(1)}, u32[]{:S(2)}, u32[]{:S(2)}) collective-permute-start(bf16[128,640]{1,0:T(8,128)(2,1)S(1)} %multiply_convert_fusion), channel_id=1, source_target_pairs={{0,4},{4,0},{8,12},{12,8},{1,5},{5,1},{9,13},{13,9},{2,6},{6,2},{1... | collective-permute-start | bytes 491528 | tf_op jit(solution)/shard_map/ppermute | solution.py:66
  8.2 11.3 %copy-start = (bf16[1,512,2560]{2,1,0:T(8,128)(2,1)S(1)}, bf16[1,512,2560]{2,1,0:T(8,128)(2,1)}, u32[]{:S(2)}) copy-start(bf16[1,512,2560]{2,1,0:T(8,128)(2,1)} %param.11) | copy-start | bytes 7864324
  18.8 9.1 %collective-permute-start.6 = (bf16[256,640]{1,0:T(8,128)(2,1)S(1)}, bf16[256,640]{1,0:T(8,128)(2,1)S(1)}, u32[]{:S(2)}, u32[]{:S(2)}) collective-permute-start(bf16[256,640]{1,0:T(8,128)(2,1)S(1)} %constant_dynamic-update-slice_fusion), channel_id=1, source_target_pairs={{0,2},{1,3},{2,0},{3,1},{4,6},{5,7},{6,4},{7,5},{8,10},{9,11},{10,... | collective-permute-start | bytes 983048 | tf_op jit(solution)/shard_map/ppermute | solution.py:80
  19.4 8.7 %collective-permute-start.1 = (bf16[128,1280]{1,0:T(8,128)(2,1)S(1)}, bf16[128,1280]{1,0:T(8,128)(2,1)S(1)}, u32[]{:S(2)}, u32[]{:S(2)}) collective-permute-start(bf16[128,1280]{1,0:T(8,128)(2,1)S(1)} %pad_maximum_fusion.16), channel_id=1, source_target_pairs={{0,1},{1,0},{2,3},{3,2},{4,5},{5,4},{6,7},{7,6},{8,9},{9,8},{10,11... | collective-permute-start | bytes 983048 | tf_op jit(solution)/shard_map/ppermute | solution.py:82
  19.7 10.3 %collective-permute-start.13 = (bf16[128,640]{1,0:T(8,128)(2,1)S(1)}, bf16[128,640]{1,0:T(8,128)(2,1)S(1)}, u32[]{:S(2)}, u32[]{:S(2)}) collective-permute-start(bf16[128,640]{1,0:T(8,128)(2,1)S(1)} %collective-permute-done.12), channel_id=1, source_target_pairs={{0,2},{1,3},{2,0},{3,1},{4,6},{5,7},{6,4},{7,5},{8,10},{9,11},{10,... | collective-permute-start | bytes 491528 | tf_op jit(solution)/shard_map/ppermute | solution.py:80
  28.0 3.7 %collective-permute-start.7 = (bf16[256,1280]{1,0:T(8,128)(2,1)S(1)}, bf16[256,1280]{1,0:T(8,128)(2,1)S(1)}, u32[]{:S(2)}, u32[]{:S(2)}) collective-permute-start(bf16[256,1280]{1,0:T(8,128)(2,1)S(1)} %pad_maximum_fusion.6), channel_id=1, source_target_pairs={{0,1},{1,0},{2,3},{3,2},{4,5},{5,4},{6,7},{7,6},{8,9},{9,8},{10,11... | collective-permute-start | bytes 1966088 | tf_op jit(solution)/shard_map/ppermute | solution.py:82
  29.5 1.8 %collective-permute-start.2 = (bf16[128,1280]{1,0:T(8,128)(2,1)S(1)}, bf16[128,1280]{1,0:T(8,128)(2,1)S(1)}, u32[]{:S(2)}, u32[]{:S(2)}) collective-permute-start(bf16[128,1280]{1,0:T(8,128)(2,1)S(1)} %convolution_convert_fusion.4), channel_id=1, source_target_pairs={{0,1},{1,0},{2,3},{3,2},{4,5},{5,4},{6,7},{7,6},{8,9},{9,8},{10,11... | collective-permute-start | bytes 983048 | tf_op jit(solution)/shard_map/ppermute | solution.py:91
  30.1 4.8 %collective-permute-start.14 = (bf16[128,1280]{1,0:T(8,128)(2,1)S(1)}, bf16[128,1280]{1,0:T(8,128)(2,1)S(1)}, u32[]{:S(2)}, u32[]{:S(2)}) collective-permute-start(bf16[128,1280]{1,0:T(8,128)(2,1)S(1)} %pad_maximum_fusion.17), channel_id=1, source_target_pairs={{0,1},{1,0},{2,3},{3,2},{4,5},{5,4},{6,7},{7,6},{8,9},{9,8},{10,11... | collective-permute-start | bytes 983048 | tf_op jit(solution)/shard_map/ppermute | solution.py:82
  34.4 2.2 %collective-permute-start.8 = (bf16[256,1280]{1,0:T(8,128)(2,1)S(1)}, bf16[256,1280]{1,0:T(8,128)(2,1)S(1)}, u32[]{:S(2)}, u32[]{:S(2)}) collective-permute-start(bf16[256,1280]{1,0:T(8,128)(2,1)S(1)} %convolution_convert_fusion), channel_id=1, source_target_pairs={{0,1},{1,0},{2,3},{3,2},{4,5},{5,4},{6,7},{7,6},{8,9},{9,8},{10,11... | collective-permute-start | bytes 1966088 | tf_op jit(solution)/shard_map/ppermute | solution.py:91
  39.7 3.3 %collective-permute-start.15 = (bf16[128,1280]{1,0:T(8,128)(2,1)}, bf16[128,1280]{1,0:T(8,128)(2,1)}, u32[]{:S(2)}, u32[]{:S(2)}) collective-permute-start(bf16[128,1280]{1,0:T(8,128)(2,1)} %convolution_convert_fusion.2), channel_id=1, source_target_pairs={{0,1},{1,0},{2,3},{3,2},{4,5},{5,4},{6,7},{7,6},{8,9},{9,8},{10,11... | collective-permute-start | bytes 983048 | tf_op jit(solution)/shard_map/ppermute | solution.py:91
  40.8 10.9 %collective-permute-start.9 = (bf16[256,640]{1,0:T(8,128)(2,1)}, bf16[256,640]{1,0:T(8,128)(2,1)}, u32[]{:S(2)}, u32[]{:S(2)}) collective-permute-start(bf16[256,640]{1,0:T(8,128)(2,1)} %slice.65), channel_id=1, source_target_pairs={{0,2},{1,3},{2,0},{3,1},{4,6},{5,7},{6,4},{7,5},{8,10},{9,11},{10,... | collective-permute-start | bytes 983048 | tf_op jit(solution)/shard_map/ppermute | solution.py:93
  41.3 21.2 %copy-start.1 = (s32[128,1]{0,1:T(1,128)S(1)}, s32[128,1]{0,1:T(1,128)}, u32[]{:S(2)}) copy-start(s32[128,1]{0,1:T(1,128)} %param.8) | copy-start | bytes 1540
  41.3 21.2 %collective-permute-start.3 = (bf16[128,640]{1,0:T(8,128)(2,1)S(1)}, bf16[128,640]{1,0:T(8,128)(2,1)S(1)}, u32[]{:S(2)}, u32[]{:S(2)}) collective-permute-start(bf16[128,640]{1,0:T(8,128)(2,1)S(1)} %slice.67), channel_id=1, source_target_pairs={{0,2},{1,3},{2,0},{3,1},{4,6},{5,7},{6,4},{7,5},{8,10},{9,11},{10,... | collective-permute-start | bytes 491528 | tf_op jit(solution)/shard_map/ppermute | solution.py:93
  44.3 15.4 %collective-permute-start.16 = (bf16[128,640]{1,0:T(8,128)(2,1)S(1)}, bf16[128,640]{1,0:T(8,128)(2,1)S(1)}, u32[]{:S(2)}, u32[]{:S(2)}) collective-permute-start(bf16[128,640]{1,0:T(8,128)(2,1)S(1)} %slice.66), channel_id=1, source_target_pairs={{0,2},{1,3},{2,0},{3,1},{4,6},{5,7},{6,4},{7,5},{8,10},{9,11},{10,... | collective-permute-start | bytes 491528 | tf_op jit(solution)/shard_map/ppermute | solution.py:93
  52.8 17.0 %collective-permute-start.10 = (bf16[128,640]{1,0:T(8,128)(2,1)S(1)}, bf16[128,640]{1,0:T(8,128)(2,1)S(1)}, u32[]{:S(2)}, u32[]{:S(2)}) collective-permute-start(bf16[128,640]{1,0:T(8,128)(2,1)S(1)} %get-tuple-element.21), channel_id=1, source_target_pairs={{0,8},{4,12},{8,0},{12,4},{1,9},{5,13},{9,1},{13,5},{2,10},{6,14},... | collective-permute-start | bytes 491528 | tf_op jit(solution)/shard_map/ppermute | solution.py:98
  59.3 10.4 %collective-permute-start.11 = (bf16[128,640]{1,0:T(8,128)(2,1)S(1)}, bf16[128,640]{1,0:T(8,128)(2,1)S(1)}, u32[]{:S(2)}, u32[]{:S(2)}) collective-permute-start(bf16[128,640]{1,0:T(8,128)(2,1)S(1)} %get-tuple-element.22), channel_id=1, source_target_pairs={{0,12},{4,8},{8,4},{12,0},{1,13},{5,9},{9,5},{13,1},{2,14},{6,10},... | collective-permute-start | bytes 491528 | tf_op jit(solution)/shard_map/ppermute | solution.py:98
  59.8 12.1 %collective-permute-start.17 = (bf16[128,640]{1,0:T(8,128)(2,1)S(1)}, bf16[128,640]{1,0:T(8,128)(2,1)S(1)}, u32[]{:S(2)}, u32[]{:S(2)}) collective-permute-start(bf16[128,640]{1,0:T(8,128)(2,1)S(1)} %fusion.4), channel_id=1, source_target_pairs={{0,4},{4,0},{8,12},{12,8},{1,5},{5,1},{9,13},{13,9},{2,6},{6,2},{1... | collective-permute-start | bytes 491528 | tf_op jit(solution)/shard_map/ppermute | solution.py:98

commit v15 on v10

--- a/solution.py
+++ b/solution.py
@@ -70,11 +70,14 @@
     up_w = _slots(up_weight[0], t, width, 0)
     down_keep = _slots(down_weight[0], t, width, 1, _ORDER[:2])
     down_send = _slots(down_weight[0], t, width, 1, _ORDER[2:])
-    waves = [[k] for k in [0] + list(range(2, n_expert)) + [1][:n_expert - 1]]
-    total = None
+    halves = 2 if tok_rows % 32 == 0 else 1
+    rows_h = tok_rows // halves
+    order = [0] + list(range(2, n_expert)) + [1][:n_expert - 1]
+    waves = [(k, h) for k in order for h in range(halves)]
+    totals = [None] * halves
     previous = None
-    for wave in waves:
-        piece = jnp.concatenate([blocks[k] for k in wave])
+    for k, h in waves:
+        piece = blocks[k][h * rows_h:(h + 1) * rows_h]
         pair = jnp.concatenate(
             [piece, lax.ppermute(piece, "tensor", _xor_pairs(n_tensor, 2))], axis=1)
         rows = jnp.concatenate(
@@ -89,15 +92,14 @@
         previous = keep
         over_c = keep.astype(jnp.float32) + lax.ppermute(
             send, "tensor", _xor_pairs(n_tensor, 1)).astype(jnp.float32)
-        summed = over_c[:, :width] + lax.ppermute(
+        part = over_c[:, :width] + lax.ppermute(
             over_c[:, width:].astype(jnp.bfloat16), "tensor", _xor_pairs(n_tensor, 2)).astype(jnp.float32)
-        for i, k in enumerate(wave):
-            part = summed[i * tok_rows:(i + 1) * tok_rows]
-            if k:
-                part = lax.ppermute(
-                    part.astype(jnp.bfloat16), "expert", _xor_pairs(n_expert, k)).astype(jnp.float32)
-            part = jnp.where(routed == (me ^ k) // SPAN, part, 0.0)
-            total = part if total is None else total + part
+        if k:
+            part = lax.ppermute(
+                part.astype(jnp.bfloat16), "expert", _xor_pairs(n_expert, k)).astype(jnp.float32)
+        part = jnp.where(routed[h * rows_h:(h + 1) * rows_h] == (me ^ k) // SPAN, part, 0.0)
+        totals[h] = part if totals[h] is None else totals[h] + part
+    total = jnp.concatenate(totals, axis=0)
     return total.astype(jnp.bfloat16)
 
 

time: 67 us -> 86.5 us (1.29)
  starting transfers between devices: 21.1 us -> 35.3 us
  matrix products: 9.28 us -> 14.6 us
    ppermute x4 -> x8, waiting for transfers between devices: 5.05 us -> 14.5 us  [gathered(): lax.ppermute(over_c[:, width:].astype(jnp.bfloat16), 'tensor', _xor_pairs...]
    ppermute x4 -> x8, waiting for transfers between devices: 9.45 us -> 3.14 us  [gathered(): lax.ppermute(piece, 'tensor', _xor_pairs(n_tensor, 2))]
    ppermute x3 -> x6, starting transfers between devices: 5.53 us -> 10.5 us  [gathered(): lax.ppermute(part.astype(jnp.bfloat16), 'expert', _xor_pairs(n_expert, k))]
    ppermute x4 -> x8, starting transfers between devices: 3.82 us -> 7.61 us  [gathered(): lax.ppermute(over_c[:, width:].astype(jnp.bfloat16), 'tensor', _xor_pairs...]
    ppermute x3, waiting for transfers between devices: 5.9 us -> 2.44 us  [gathered(): lax.ppermute(scaled, 'expert', _xor_pairs(n_expert, k))]
    ppermute x4 -> x8, starting transfers between devices: 5.55 us -> 8.43 us  [gathered(): lax.ppermute(piece, 'tensor', _xor_pairs(n_tensor, 2))]
    dot_general x4 -> x8, matrix products: 2 us -> 4.47 us  [gathered(): gate_act = jnp.dot(rows, gate_w, preferred_element_type=jnp.float32)]
    dot_general x4 -> x8, matrix products: 2.72 us -> 4.54 us  [gathered(): up_act = jnp.dot(rows, up_w, preferred_element_type=jnp.float32)]
  transfers between devices with their start and end apart: 22 -> 41, of which waited for: 12 -> 16; matrix products, arithmetic and copies ran while one was open for 19% -> 22% of each run, Pallas kernels for 0% -> 0%
where the time goes in v15:
time: 86.5 us; the launch traced here: 86.4 us
  starting transfers between devices  35.3 us (41%)
  waiting for transfers between devices  28.1 us (32%)
  matrix products  14.6 us (17%)
  local copies, waits for them, and re-layouts  4.86 us (6%)
  other arithmetic  2.87 us (3%)
    ppermute x8, waiting for transfers between devices, gathered(): lax.ppermute(over_c[:, width:].astype(jnp.bfloat16), 'tensor', _xor_pairs...  14.5 us
    ppermute x6, starting transfers between devices, gathered(): lax.ppermute(part.astype(jnp.bfloat16), 'expert', _xor_pairs(n_expert, k))  10.5 us
    ppermute x8, starting transfers between devices, gathered(): lax.ppermute(piece, 'tensor', _xor_pairs(n_tensor, 2))  8.43 us
    ppermute x8, starting transfers between devices, gathered(): lax.ppermute(over_c[:, width:].astype(jnp.bfloat16), 'tensor', _xor_pairs...  7.61 us
    ppermute x3, starting transfers between devices, gathered(): lax.ppermute(scaled, 'expert', _xor_pairs(n_expert, k))  5.68 us
    ppermute x6, waiting for transfers between devices, gathered(): lax.ppermute(part.astype(jnp.bfloat16), 'expert', _xor_pairs(n_expert, k))  5.45 us
    dot_general x8, matrix products, gathered(): up_act = jnp.dot(rows, up_w, preferred_element_type=jnp.float32)  4.54 us
    dot_general x8, matrix products, gathered(): gate_act = jnp.dot(rows, gate_w, preferred_element_type=jnp.float32)  4.47 us
  transfers between devices with their start and end apart: 41, of which 16 were waited for; matrix products, arithmetic and copies ran while one was open for 22% of the time, Pallas kernels for 0%

profile of v15, /device:TPU:0, one launch (start us, length us, event | category | flops | bytes accessed | tf_op | source)
XLA Modules:
  0.0 86.4 jit_solution(2614657738880847467)
XLA Ops:
  0.0 1.0 %multiply_convert_fusion = bf16[128,640]{1,0:T(8,128)(2,1)S(1)} fusion(bf16[128,640]{1,0:T(8,128)(2,1)} %param.6, f32[128]{0:T(128)} %param.7), kind=kLoop, calls=%fused_computation.63 | loop fusion | flops 245760 | bytes 328192 | tf_op jit(solution)/shard_map/convert_element_type | solution.py:64
  1.0 4.1 %collective-permute-start.4 = (bf16[128,640]{1,0:T(8,128)(2,1)S(1)}, bf16[128,640]{1,0:T(8,128)(2,1)S(1)}, u32[]{:S(2)}, u32[]{:S(2)}) collective-permute-start(bf16[128,640]{1,0:T(8,128)(2,1)S(1)} %multiply_convert_fusion), channel_id=1, source_target_pairs={{0,8},{4,12},{8,0},{12,4},{1,9},{5,13},{9,1},{13,5},{2,10},{6,14},... | collective-permute-start | bytes 491528 | tf_op jit(solution)/shard_map/ppermute | solution.py:66
  5.1 1.3 %collective-permute-start.12 = (bf16[128,640]{1,0:T(8,128)(2,1)S(1)}, bf16[128,640]{1,0:T(8,128)(2,1)S(1)}, u32[]{:S(2)}, u32[]{:S(2)}) collective-permute-start(bf16[128,640]{1,0:T(8,128)(2,1)S(1)} %multiply_convert_fusion), channel_id=1, source_target_pairs={{0,12},{4,8},{8,4},{12,0},{1,13},{5,9},{9,5},{13,1},{2,14},{6,10},... | collective-permute-start | bytes 491528 | tf_op jit(solution)/shard_map/ppermute | solution.py:66
  6.7 1.6 %collective-permute-start = (bf16[64,640]{1,0:T(8,128)(2,1)S(1)}, bf16[64,640]{1,0:T(8,128)(2,1)S(1)}, u32[]{:S(2)}, u32[]{:S(2)}) collective-permute-start(bf16[64,640]{1,0:T(8,128)(2,1)S(1)} %get-tuple-element.37), channel_id=1, source_target_pairs={{0,2},{1,3},{2,0},{3,1},{4,6},{5,7},{6,4},{7,5},{8,10},{9,11},{10,... | collective-permute-start | bytes 245768 | tf_op jit(solution)/shard_map/ppermute | solution.py:82
  8.8 3.0 %dynamic-slice_bitcast_fusion.7 = (bf16[640,512]{1,0:T(8,128)(2,1)S(1)}, bf16[640,512]{1,0:T(8,128)(2,1)S(1)}, bf16[640,512]{1,0:T(8,128)(2,1)S(1)}, bf16[640,51...) fusion(bf16[1,2560,512]{2,1,0:T(8,128)(2,1)} %param.10, ...), kind=kLoop, calls=%fused_computation.42 | loop fusion | bytes 10485776 | tf_op jit(solution)/shard_map/dynamic_slice | solution.py:55
  12.8 1.0 %copy-done = bf16[1,512,2560]{2,1,0:T(8,128)(2,1)S(1)} copy-done((bf16[1,512,2560]{2,1,0:T(8,128)(2,1)S(1)}, bf16[1,512,2560]{2,1,0:T(8,128)(2,1)}, u32[]{:S(2)}) %copy-start) | copy-done | bytes 2621464
  14.8 2.4 %collective-permute-done.4 = bf16[128,640]{1,0:T(8,128)(2,1)S(1)} collective-permute-done((bf16[128,640]{1,0:T(8,128)(2,1)S(1)}, bf16[128,640]{1,0:T(8,128)(2,1)S(1)}, u32[]{:S(2)}, u32[]{:S(2)}) %collective-permute-start.4) | collective-permute-done | bytes 163872 | tf_op jit(solution)/shard_map/ppermute | solution.py:66
  17.2 1.9 %collective-permute-start.5 = (bf16[64,640]{1,0:T(8,128)(2,1)S(1)}, bf16[64,640]{1,0:T(8,128)(2,1)S(1)}, u32[]{:S(2)}, u32[]{:S(2)}) collective-permute-start(bf16[64,640]{1,0:T(8,128)(2,1)S(1)} %get-tuple-element.31), channel_id=1, source_target_pairs={{0,2},{1,3},{2,0},{3,1},{4,6},{5,7},{6,4},{7,5},{8,10},{9,11},{10,... | collective-permute-start | bytes 245768 | tf_op jit(solution)/shard_map/ppermute | solution.py:82
  19.4 1.9 %collective-permute-start.13 = (bf16[64,640]{1,0:T(8,128)(2,1)S(1)}, bf16[64,640]{1,0:T(8,128)(2,1)S(1)}, u32[]{:S(2)}, u32[]{:S(2)}) collective-permute-start(bf16[64,640]{1,0:T(8,128)(2,1)S(1)} %get-tuple-element.33), channel_id=1, source_target_pairs={{0,2},{1,3},{2,0},{3,1},{4,6},{5,7},{6,4},{7,5},{8,10},{9,11},{10,... | collective-permute-start | bytes 245768 | tf_op jit(solution)/shard_map/ppermute | solution.py:82
  21.6 1.1 %collective-permute-done.5 = bf16[64,640]{1,0:T(8,128)(2,1)S(1)} collective-permute-done((bf16[64,640]{1,0:T(8,128)(2,1)S(1)}, bf16[64,640]{1,0:T(8,128)(2,1)S(1)}, u32[]{:S(2)}, u32[]{:S(2)}) %collective-permute-start.5) | collective-permute-done | bytes 81952 | tf_op jit(solution)/shard_map/ppermute | solution.py:82
  22.7 1.8 %collective-permute-start.21 = (bf16[64,640]{1,0:T(8,128)(2,1)S(1)}, bf16[64,640]{1,0:T(8,128)(2,1)S(1)}, u32[]{:S(2)}, u32[]{:S(2)}) collective-permute-start(bf16[64,640]{1,0:T(8,128)(2,1)S(1)} %get-tuple-element.35), channel_id=1, source_target_pairs={{0,2},{1,3},{2,0},{3,1},{4,6},{5,7},{6,4},{7,5},{8,10},{9,11},{10,... | collective-permute-start | bytes 245768 | tf_op jit(solution)/shard_map/ppermute | solution.py:82
  25.4 0.6 multiply_convert_fusion.1
  27.2 0.9 collective-permute-done.21
  28.1 0.9 %collective-permute-done.36 = bf16[64,640]{1,0:T(8,128)(2,1)S(1)} collective-permute-done((bf16[64,640]{1,0:T(8,128)(2,1)S(1)}, bf16[64,640]{1,0:T(8,128)(2,1)S(1)}, u32[]{:S(2)}, u32[]{:S(2)}) %collective-permute-start.36) | collective-permute-done | bytes 81952 | tf_op jit(solution)/shard_map/ppermute | solution.py:82
  29.1 0.6 collective-permute-start.22
  30.6 0.6 fusion.1
  32.2 1.1 %collective-permute-start.3 = (bf16[64,640]{1,0:T(8,128)(2,1)S(1)}, bf16[64,640]{1,0:T(8,128)(2,1)S(1)}, u32[]{:S(2)}, u32[]{:S(2)}) collective-permute-start(bf16[64,640]{1,0:T(8,128)(2,1)S(1)} %slice.205), channel_id=1, source_target_pairs={{0,2},{1,3},{2,0},{3,1},{4,6},{5,7},{6,4},{7,5},{8,10},{9,11},{10,... | collective-permute-start | bytes 245768 | tf_op jit(solution)/shard_map/ppermute | solution.py:95
  34.4 0.6 fusion.2
  35.5 1.2 %collective-permute-done.9 = bf16[64,1280]{1,0:T(8,128)(2,1)S(1)} collective-permute-done((bf16[64,1280]{1,0:T(8,128)(2,1)S(1)}, bf16[64,1280]{1,0:T(8,128)(2,1)S(1)}, u32[]{:S(2)}, u32[]{:S(2)}) %collective-permute-start.9) | collective-permute-done | bytes 163872 | tf_op jit(solution)/shard_map/ppermute | solution.py:93
  37.1 0.6 fusion.34
  37.7 0.6 fusion.3
  38.9 1.1 %collective-permute-start.29 = (bf16[64,640]{1,0:T(8,128)(2,1)S(1)}, bf16[64,640]{1,0:T(8,128)(2,1)S(1)}, u32[]{:S(2)}, u32[]{:S(2)}) collective-permute-start(bf16[64,640]{1,0:T(8,128)(2,1)S(1)} %slice.201), channel_id=1, source_target_pairs={{0,2},{1,3},{2,0},{3,1},{4,6},{5,7},{6,4},{7,5},{8,10},{9,11},{10,... | collective-permute-start | bytes 245768 | tf_op jit(solution)/shard_map/ppermute | solution.py:95
  40.0 1.1 %collective-permute-start.10 = (bf16[64,640]{1,0:T(8,128)(2,1)S(1)}, bf16[64,640]{1,0:T(8,128)(2,1)S(1)}, u32[]{:S(2)}, u32[]{:S(2)}) collective-permute-start(bf16[64,640]{1,0:T(8,128)(2,1)S(1)} %slice.204), channel_id=1, source_target_pairs={{0,2},{1,3},{2,0},{3,1},{4,6},{5,7},{6,4},{7,5},{8,10},{9,11},{10,... | collective-permute-start | bytes 245768 | tf_op jit(solution)/shard_map/ppermute | solution.py:95
  41.4 0.6 fusion.35
  42.0 0.6 fusion.4
  43.0 2.4 %collective-permute-done.10 = bf16[64,640]{1,0:T(8,128)(2,1)S(1)} collective-permute-done((bf16[64,640]{1,0:T(8,128)(2,1)S(1)}, bf16[64,640]{1,0:T(8,128)(2,1)S(1)}, u32[]{:S(2)}, u32[]{:S(2)}) %collective-permute-start.10) | collective-permute-done | bytes 81952 | tf_op jit(solution)/shard_map/ppermute | solution.py:95
  45.4 5.4 %collective-permute-start.11 = (bf16[64,640]{1,0:T(8,128)(2,1)S(1)}, bf16[64,640]{1,0:T(8,128)(2,1)S(1)}, u32[]{:S(2)}, u32[]{:S(2)}) collective-permute-start(bf16[64,640]{1,0:T(8,128)(2,1)S(1)} %fusion.18), channel_id=1, source_target_pairs={{0,8},{4,12},{8,0},{12,4},{1,9},{5,13},{9,1},{13,5},{2,10},{6,14},... | collective-permute-start | bytes 245768 | tf_op jit(solution)/shard_map/ppermute | solution.py:98
  50.8 0.9 %collective-permute-start.31 = (bf16[64,640]{1,0:T(8,128)(2,1)S(1)}, bf16[64,640]{1,0:T(8,128)(2,1)S(1)}, u32[]{:S(2)}, u32[]{:S(2)}) collective-permute-start(bf16[64,640]{1,0:T(8,128)(2,1)S(1)} %slice.200), channel_id=1, source_target_pairs={{0,2},{1,3},{2,0},{3,1},{4,6},{5,7},{6,4},{7,5},{8,10},{9,11},{10,... | collective-permute-start | bytes 245768 | tf_op jit(solution)/shard_map/ppermute | solution.py:95
  52.1 0.6 fusion.36
  52.6 0.6 fusion.5
  53.6 1.7 %collective-permute-done.31 = bf16[64,640]{1,0:T(8,128)(2,1)S(1)} collective-permute-done((bf16[64,640]{1,0:T(8,128)(2,1)S(1)}, bf16[64,640]{1,0:T(8,128)(2,1)S(1)}, u32[]{:S(2)}, u32[]{:S(2)}) %collective-permute-start.31) | collective-permute-done | bytes 81952 | tf_op jit(solution)/shard_map/ppermute | solution.py:95
  55.4 0.9 %collective-permute-start.18 = (bf16[64,640]{1,0:T(8,128)(2,1)S(1)}, bf16[64,640]{1,0:T(8,128)(2,1)S(1)}, u32[]{:S(2)}, u32[]{:S(2)}) collective-permute-start(bf16[64,640]{1,0:T(8,128)(2,1)S(1)} %slice.203), channel_id=1, source_target_pairs={{0,2},{1,3},{2,0},{3,1},{4,6},{5,7},{6,4},{7,5},{8,10},{9,11},{10,... | collective-permute-start | bytes 245768 | tf_op jit(solution)/shard_map/ppermute | solution.py:95
  56.6 0.6 fusion.37
  57.2 0.6 fusion.6
  58.2 1.7 %collective-permute-done.18 = bf16[64,640]{1,0:T(8,128)(2,1)S(1)} collective-permute-done((bf16[64,640]{1,0:T(8,128)(2,1)S(1)}, bf16[64,640]{1,0:T(8,128)(2,1)S(1)}, u32[]{:S(2)}, u32[]{:S(2)}) %collective-permute-start.18) | collective-permute-done | bytes 81952 | tf_op jit(solution)/shard_map/ppermute | solution.py:95
  60.4 0.9 %collective-permute-start.34 = (bf16[64,640]{1,0:T(8,128)(2,1)S(1)}, bf16[64,640]{1,0:T(8,128)(2,1)S(1)}, u32[]{:S(2)}, u32[]{:S(2)}) collective-permute-start(bf16[64,640]{1,0:T(8,128)(2,1)S(1)} %slice.199), channel_id=1, source_target_pairs={{0,2},{1,3},{2,0},{3,1},{4,6},{5,7},{6,4},{7,5},{8,10},{9,11},{10,... | collective-permute-start | bytes 245768 | tf_op jit(solution)/shard_map/ppermute | solution.py:95
  61.7 0.6 fusion.38
  62.2 0.6 fusion.7
  63.2 1.8 %collective-permute-done.34 = bf16[64,640]{1,0:T(8,128)(2,1)S(1)} collective-permute-done((bf16[64,640]{1,0:T(8,128)(2,1)S(1)}, bf16[64,640]{1,0:T(8,128)(2,1)S(1)}, u32[]{:S(2)}, u32[]{:S(2)}) %collective-permute-start.34) | collective-permute-done | bytes 81952 | tf_op jit(solution)/shard_map/ppermute | solution.py:95
  65.0 1.4 %collective-permute-done.38 = bf16[64,1280]{1,0:T(8,128)(2,1)S(1)} collective-permute-done((bf16[64,1280]{1,0:T(8,128)(2,1)S(1)}, bf16[64,1280]{1,0:T(8,128)(2,1)S(1)}, u32[]{:S(2)}, u32[]{:S(2)}) %collective-permute-start.38) | collective-permute-done | bytes 163872 | tf_op jit(solution)/shard_map/ppermute | solution.py:93
  66.3 0.8 collective-permute-start.26
  67.5 3.3 %collective-permute-done.26 = bf16[64,640]{1,0:T(8,128)(2,1)S(1)} collective-permute-done((bf16[64,640]{1,0:T(8,128)(2,1)S(1)}, bf16[64,640]{1,0:T(8,128)(2,1)S(1)}, u32[]{:S(2)}, u32[]{:S(2)}) %collective-permute-start.26) | collective-permute-done | bytes 81952 | tf_op jit(solution)/shard_map/ppermute | solution.py:95
  70.8 0.8 collective-permute-start.39
  71.7 3.6 %collective-permute-done.39 = bf16[64,640]{1,0:T(8,128)(2,1)S(1)} collective-permute-done((bf16[64,640]{1,0:T(8,128)(2,1)S(1)}, bf16[64,640]{1,0:T(8,128)(2,1)S(1)}, u32[]{:S(2)}, u32[]{:S(2)}) %collective-permute-start.39) | collective-permute-done | bytes 81952 | tf_op jit(solution)/shard_map/ppermute | solution.py:95
  75.4 3.9 %collective-permute-start.32 = (bf16[64,640]{1,0:T(8,128)(2,1)S(1)}, bf16[64,640]{1,0:T(8,128)(2,1)S(1)}, u32[]{:S(2)}, u32[]{:S(2)}) collective-permute-start(bf16[64,640]{1,0:T(8,128)(2,1)S(1)} %fusion.10), channel_id=1, source_target_pairs={{0,8},{4,12},{8,0},{12,4},{1,9},{5,13},{9,1},{13,5},{2,10},{6,14},... | collective-permute-start | bytes 245768 | tf_op jit(solution)/shard_map/ppermute | solution.py:98
  80.2 3.3 %collective-permute-done.32 = bf16[64,640]{1,0:T(8,128)(2,1)S(1)} collective-permute-done((bf16[64,640]{1,0:T(8,128)(2,1)S(1)}, bf16[64,640]{1,0:T(8,128)(2,1)S(1)}, u32[]{:S(2)}, u32[]{:S(2)}) %collective-permute-start.32) | collective-permute-done | bytes 81952 | tf_op jit(solution)/shard_map/ppermute | solution.py:98
  83.5 2.0 %collective-permute-done.35 = bf16[64,640]{1,0:T(8,128)(2,1)S(1)} collective-permute-done((bf16[64,640]{1,0:T(8,128)(2,1)S(1)}, bf16[64,640]{1,0:T(8,128)(2,1)S(1)}, u32[]{:S(2)}, u32[]{:S(2)}) %collective-permute-start.35) | collective-permute-done | bytes 81952 | tf_op jit(solution)/shard_map/ppermute | solution.py:98
  85.7 0.7 pad_maximum_fusion.20
  (112 shorter events, 15.0 us)
Async XLA Ops:
  1.0 16.2 %collective-permute-start.4 = (bf16[128,640]{1,0:T(8,128)(2,1)S(1)}, bf16[128,640]{1,0:T(8,128)(2,1)S(1)}, u32[]{:S(2)}, u32[]{:S(2)}) collective-permute-start(bf16[128,640]{1,0:T(8,128)(2,1)S(1)} %multiply_convert_fusion), channel_id=1, source_target_pairs={{0,8},{4,12},{8,0},{12,4},{1,9},{5,13},{9,1},{13,5},{2,10},{6,14},... | collective-permute-start | bytes 491528 | tf_op jit(solution)/shard_map/ppermute | solution.py:66
  5.1 14.0 %collective-permute-start.12 = (bf16[128,640]{1,0:T(8,128)(2,1)S(1)}, bf16[128,640]{1,0:T(8,128)(2,1)S(1)}, u32[]{:S(2)}, u32[]{:S(2)}) collective-permute-start(bf16[128,640]{1,0:T(8,128)(2,1)S(1)} %multiply_convert_fusion), channel_id=1, source_target_pairs={{0,12},{4,8},{8,4},{12,0},{1,13},{5,9},{9,5},{13,1},{2,14},{6,10},... | collective-permute-start | bytes 491528 | tf_op jit(solution)/shard_map/ppermute | solution.py:66
  6.5 12.9 %collective-permute-start.20 = (bf16[128,640]{1,0:T(8,128)(2,1)S(1)}, bf16[128,640]{1,0:T(8,128)(2,1)S(1)}, u32[]{:S(2)}, u32[]{:S(2)}) collective-permute-start(bf16[128,640]{1,0:T(8,128)(2,1)S(1)} %multiply_convert_fusion), channel_id=1, source_target_pairs={{0,4},{4,0},{8,12},{12,8},{1,5},{5,1},{9,13},{13,9},{2,6},{6,2},{1... | collective-permute-start | bytes 491528 | tf_op jit(solution)/shard_map/ppermute | solution.py:66
  6.7 7.4 %collective-permute-start = (bf16[64,640]{1,0:T(8,128)(2,1)S(1)}, bf16[64,640]{1,0:T(8,128)(2,1)S(1)}, u32[]{:S(2)}, u32[]{:S(2)}) collective-permute-start(bf16[64,640]{1,0:T(8,128)(2,1)S(1)} %get-tuple-element.37), channel_id=1, source_target_pairs={{0,2},{1,3},{2,0},{3,1},{4,6},{5,7},{6,4},{7,5},{8,10},{9,11},{10,... | collective-permute-start | bytes 245768 | tf_op jit(solution)/shard_map/ppermute | solution.py:82
  8.3 5.9 %collective-permute-start.7 = (bf16[64,640]{1,0:T(8,128)(2,1)S(1)}, bf16[64,640]{1,0:T(8,128)(2,1)S(1)}, u32[]{:S(2)}, u32[]{:S(2)}) collective-permute-start(bf16[64,640]{1,0:T(8,128)(2,1)S(1)} %get-tuple-element.38), channel_id=1, source_target_pairs={{0,2},{1,3},{2,0},{3,1},{4,6},{5,7},{6,4},{7,5},{8,10},{9,11},{10,... | collective-permute-start | bytes 245768 | tf_op jit(solution)/shard_map/ppermute | solution.py:82
  12.1 0.7 copy-start.1
  12.1 1.7 %copy-start = (bf16[1,512,2560]{2,1,0:T(8,128)(2,1)S(1)}, bf16[1,512,2560]{2,1,0:T(8,128)(2,1)}, u32[]{:S(2)}) copy-start(bf16[1,512,2560]{2,1,0:T(8,128)(2,1)} %param.11) | copy-start | bytes 7864324
  14.1 10.4 %collective-permute-start.1 = (bf16[64,1280]{1,0:T(8,128)(2,1)S(1)}, bf16[64,1280]{1,0:T(8,128)(2,1)S(1)}, u32[]{:S(2)}, u32[]{:S(2)}) collective-permute-start(bf16[64,1280]{1,0:T(8,128)(2,1)S(1)} %pad_maximum_fusion.12), channel_id=1, source_target_pairs={{0,1},{1,0},{2,3},{3,2},{4,5},{5,4},{6,7},{7,6},{8,9},{9,8},{10,11... | collective-permute-start | bytes 491528 | tf_op jit(solution)/shard_map/ppermute | solution.py:84
  14.2 7.1 %collective-permute-start.8 = (bf16[64,1280]{1,0:T(8,128)(2,1)S(1)}, bf16[64,1280]{1,0:T(8,128)(2,1)S(1)}, u32[]{:S(2)}, u32[]{:S(2)}) collective-permute-start(bf16[64,1280]{1,0:T(8,128)(2,1)S(1)} %pad_maximum_fusion.14), channel_id=1, source_target_pairs={{0,1},{1,0},{2,3},{3,2},{4,5},{5,4},{6,7},{7,6},{8,9},{9,8},{10,11... | collective-permute-start | bytes 491528 | tf_op jit(solution)/shard_map/ppermute | solution.py:84
  17.2 5.4 %collective-permute-start.5 = (bf16[64,640]{1,0:T(8,128)(2,1)S(1)}, bf16[64,640]{1,0:T(8,128)(2,1)S(1)}, u32[]{:S(2)}, u32[]{:S(2)}) collective-permute-start(bf16[64,640]{1,0:T(8,128)(2,1)S(1)} %get-tuple-element.31), channel_id=1, source_target_pairs={{0,2},{1,3},{2,0},{3,1},{4,6},{5,7},{6,4},{7,5},{8,10},{9,11},{10,... | collective-permute-start | bytes 245768 | tf_op jit(solution)/shard_map/ppermute | solution.py:82
  19.1 7.2 %collective-permute-start.15 = (bf16[64,640]{1,0:T(8,128)(2,1)S(1)}, bf16[64,640]{1,0:T(8,128)(2,1)S(1)}, u32[]{:S(2)}, u32[]{:S(2)}) collective-permute-start(bf16[64,640]{1,0:T(8,128)(2,1)S(1)} %get-tuple-element.32), channel_id=1, source_target_pairs={{0,2},{1,3},{2,0},{3,1},{4,6},{5,7},{6,4},{7,5},{8,10},{9,11},{10,... | collective-permute-start | bytes 245768 | tf_op jit(solution)/shard_map/ppermute | solution.py:82
  19.4 7.0 %collective-permute-start.13 = (bf16[64,640]{1,0:T(8,128)(2,1)S(1)}, bf16[64,640]{1,0:T(8,128)(2,1)S(1)}, u32[]{:S(2)}, u32[]{:S(2)}) collective-permute-start(bf16[64,640]{1,0:T(8,128)(2,1)S(1)} %get-tuple-element.33), channel_id=1, source_target_pairs={{0,2},{1,3},{2,0},{3,1},{4,6},{5,7},{6,4},{7,5},{8,10},{9,11},{10,... | collective-permute-start | bytes 245768 | tf_op jit(solution)/shard_map/ppermute | solution.py:82
  21.3 5.9 %collective-permute-start.23 = (bf16[64,640]{1,0:T(8,128)(2,1)S(1)}, bf16[64,640]{1,0:T(8,128)(2,1)S(1)}, u32[]{:S(2)}, u32[]{:S(2)}) collective-permute-start(bf16[64,640]{1,0:T(8,128)(2,1)S(1)} %get-tuple-element.34), channel_id=1, source_target_pairs={{0,2},{1,3},{2,0},{3,1},{4,6},{5,7},{6,4},{7,5},{8,10},{9,11},{10,... | collective-permute-start | bytes 245768 | tf_op jit(solution)/shard_map/ppermute | solution.py:82
  22.7 5.4 %collective-permute-start.21 = (bf16[64,640]{1,0:T(8,128)(2,1)S(1)}, bf16[64,640]{1,0:T(8,128)(2,1)S(1)}, u32[]{:S(2)}, u32[]{:S(2)}) collective-permute-start(bf16[64,640]{1,0:T(8,128)(2,1)S(1)} %get-tuple-element.35), channel_id=1, source_target_pairs={{0,2},{1,3},{2,0},{3,1},{4,6},{5,7},{6,4},{7,5},{8,10},{9,11},{10,... | collective-permute-start | bytes 245768 | tf_op jit(solution)/shard_map/ppermute | solution.py:82
  24.5 4.5 %collective-permute-start.36 = (bf16[64,640]{1,0:T(8,128)(2,1)S(1)}, bf16[64,640]{1,0:T(8,128)(2,1)S(1)}, u32[]{:S(2)}, u32[]{:S(2)}) collective-permute-start(bf16[64,640]{1,0:T(8,128)(2,1)S(1)} %get-tuple-element.36), channel_id=1, source_target_pairs={{0,2},{1,3},{2,0},{3,1},{4,6},{5,7},{6,4},{7,5},{8,10},{9,11},{10,... | collective-permute-start | bytes 245768 | tf_op jit(solution)/shard_map/ppermute | solution.py:82
  26.3 2.8 %collective-permute-start.2 = (bf16[64,1280]{1,0:T(8,128)(2,1)S(1)}, bf16[64,1280]{1,0:T(8,128)(2,1)S(1)}, u32[]{:S(2)}, u32[]{:S(2)}) collective-permute-start(bf16[64,1280]{1,0:T(8,128)(2,1)S(1)} %convolution_convert_fusion.14), channel_id=1, source_target_pairs={{0,1},{1,0},{2,3},{3,2},{4,5},{5,4},{6,7},{7,6},{8,9},{9,8},{10,11... | collective-permute-start | bytes 491528 | tf_op jit(solution)/shard_map/ppermute | solution.py:93
  26.4 4.7 %collective-permute-start.6 = (bf16[64,1280]{1,0:T(8,128)(2,1)S(1)}, bf16[64,1280]{1,0:T(8,128)(2,1)S(1)}, u32[]{:S(2)}, u32[]{:S(2)}) collective-permute-start(bf16[64,1280]{1,0:T(8,128)(2,1)S(1)} %pad_maximum_fusion.13), channel_id=1, source_target_pairs={{0,1},{1,0},{2,3},{3,2},{4,5},{5,4},{6,7},{7,6},{8,9},{9,8},{10,11... | collective-permute-start | bytes 491528 | tf_op jit(solution)/shard_map/ppermute | solution.py:84
  27.2 4.4 %collective-permute-start.16 = (bf16[64,1280]{1,0:T(8,128)(2,1)S(1)}, bf16[64,1280]{1,0:T(8,128)(2,1)S(1)}, u32[]{:S(2)}, u32[]{:S(2)}) collective-permute-start(bf16[64,1280]{1,0:T(8,128)(2,1)S(1)} %pad_maximum_fusion.16), channel_id=1, source_target_pairs={{0,1},{1,0},{2,3},{3,2},{4,5},{5,4},{6,7},{7,6},{8,9},{9,8},{10,11... | collective-permute-start | bytes 491528 | tf_op jit(solution)/shard_map/ppermute | solution.py:84
  28.1 4.2 %collective-permute-start.14 = (bf16[64,1280]{1,0:T(8,128)(2,1)S(1)}, bf16[64,1280]{1,0:T(8,128)(2,1)S(1)}, u32[]{:S(2)}, u32[]{:S(2)}) collective-permute-start(bf16[64,1280]{1,0:T(8,128)(2,1)S(1)} %pad_maximum_fusion.15), channel_id=1, source_target_pairs={{0,1},{1,0},{2,3},{3,2},{4,5},{5,4},{6,7},{7,6},{8,9},{9,8},{10,11... | collective-permute-start | bytes 491528 | tf_op jit(solution)/shard_map/ppermute | solution.py:84
  29.0 4.4 %collective-permute-start.24 = (bf16[64,1280]{1,0:T(8,128)(2,1)S(1)}, bf16[64,1280]{1,0:T(8,128)(2,1)S(1)}, u32[]{:S(2)}, u32[]{:S(2)}) collective-permute-start(bf16[64,1280]{1,0:T(8,128)(2,1)S(1)} %pad_maximum_fusion.18), channel_id=1, source_target_pairs={{0,1},{1,0},{2,3},{3,2},{4,5},{5,4},{6,7},{7,6},{8,9},{9,8},{10,11... | collective-permute-start | bytes 491528 | tf_op jit(solution)/shard_map/ppermute | solution.py:84
  29.1 6.4 %collective-permute-start.22 = (bf16[64,1280]{1,0:T(8,128)(2,1)S(1)}, bf16[64,1280]{1,0:T(8,128)(2,1)S(1)}, u32[]{:S(2)}, u32[]{:S(2)}) collective-permute-start(bf16[64,1280]{1,0:T(8,128)(2,1)S(1)} %pad_maximum_fusion.17), channel_id=1, source_target_pairs={{0,1},{1,0},{2,3},{3,2},{4,5},{5,4},{6,7},{7,6},{8,9},{9,8},{10,11... | collective-permute-start | bytes 491528 | tf_op jit(solution)/shard_map/ppermute | solution.py:84
  31.2 7.7 %collective-permute-start.37 = (bf16[64,1280]{1,0:T(8,128)(2,1)S(1)}, bf16[64,1280]{1,0:T(8,128)(2,1)S(1)}, u32[]{:S(2)}, u32[]{:S(2)}) collective-permute-start(bf16[64,1280]{1,0:T(8,128)(2,1)S(1)} %pad_maximum_fusion.19), channel_id=1, source_target_pairs={{0,1},{1,0},{2,3},{3,2},{4,5},{5,4},{6,7},{7,6},{8,9},{9,8},{10,11... | collective-permute-start | bytes 491528 | tf_op jit(solution)/shard_map/ppermute | solution.py:84
  31.6 1.8 %collective-permute-start.28 = (bf16[64,1280]{1,0:T(8,128)(2,1)S(1)}, bf16[64,1280]{1,0:T(8,128)(2,1)S(1)}, u32[]{:S(2)}, u32[]{:S(2)}) collective-permute-start(bf16[64,1280]{1,0:T(8,128)(2,1)S(1)} %convolution_convert_fusion.4), channel_id=1, source_target_pairs={{0,1},{1,0},{2,3},{3,2},{4,5},{5,4},{6,7},{7,6},{8,9},{9,8},{10,11... | collective-permute-start | bytes 491528 | tf_op jit(solution)/shard_map/ppermute | solution.py:93
  32.2 43.2 %collective-permute-start.3 = (bf16[64,640]{1,0:T(8,128)(2,1)S(1)}, bf16[64,640]{1,0:T(8,128)(2,1)S(1)}, u32[]{:S(2)}, u32[]{:S(2)}) collective-permute-start(bf16[64,640]{1,0:T(8,128)(2,1)S(1)} %slice.205), channel_id=1, source_target_pairs={{0,2},{1,3},{2,0},{3,1},{4,6},{5,7},{6,4},{7,5},{8,10},{9,11},{10,... | collective-permute-start | bytes 245768 | tf_op jit(solution)/shard_map/ppermute | solution.py:95
  35.3 1.5 %collective-permute-start.9 = (bf16[64,1280]{1,0:T(8,128)(2,1)S(1)}, bf16[64,1280]{1,0:T(8,128)(2,1)S(1)}, u32[]{:S(2)}, u32[]{:S(2)}) collective-permute-start(bf16[64,1280]{1,0:T(8,128)(2,1)S(1)} %convolution_convert_fusion.11), channel_id=1, source_target_pairs={{0,1},{1,0},{2,3},{3,2},{4,5},{5,4},{6,7},{7,6},{8,9},{9,8},{10,11... | collective-permute-start | bytes 491528 | tf_op jit(solution)/shard_map/ppermute | solution.py:93
  38.6 2.5 %collective-permute-start.30 = (bf16[64,1280]{1,0:T(8,128)(2,1)S(1)}, bf16[64,1280]{1,0:T(8,128)(2,1)S(1)}, u32[]{:S(2)}, u32[]{:S(2)}) collective-permute-start(bf16[64,1280]{1,0:T(8,128)(2,1)S(1)} %convolution_convert_fusion.3), channel_id=1, source_target_pairs={{0,1},{1,0},{2,3},{3,2},{4,5},{5,4},{6,7},{7,6},{8,9},{9,8},{10,11... | collective-permute-start | bytes 491528 | tf_op jit(solution)/shard_map/ppermute | solution.py:93
  38.9 41.4 %collective-permute-start.29 = (bf16[64,640]{1,0:T(8,128)(2,1)S(1)}, bf16[64,640]{1,0:T(8,128)(2,1)S(1)}, u32[]{:S(2)}, u32[]{:S(2)}) collective-permute-start(bf16[64,640]{1,0:T(8,128)(2,1)S(1)} %slice.201), channel_id=1, source_target_pairs={{0,2},{1,3},{2,0},{3,1},{4,6},{5,7},{6,4},{7,5},{8,10},{9,11},{10,... | collective-permute-start | bytes 245768 | tf_op jit(solution)/shard_map/ppermute | solution.py:95
  40.0 5.4 %collective-permute-start.10 = (bf16[64,640]{1,0:T(8,128)(2,1)S(1)}, bf16[64,640]{1,0:T(8,128)(2,1)S(1)}, u32[]{:S(2)}, u32[]{:S(2)}) collective-permute-start(bf16[64,640]{1,0:T(8,128)(2,1)S(1)} %slice.204), channel_id=1, source_target_pairs={{0,2},{1,3},{2,0},{3,1},{4,6},{5,7},{6,4},{7,5},{8,10},{9,11},{10,... | collective-permute-start | bytes 245768 | tf_op jit(solution)/shard_map/ppermute | solution.py:95
  42.9 8.8 %collective-permute-start.17 = (bf16[64,1280]{1,0:T(8,128)(2,1)S(1)}, bf16[64,1280]{1,0:T(8,128)(2,1)S(1)}, u32[]{:S(2)}, u32[]{:S(2)}) collective-permute-start(bf16[64,1280]{1,0:T(8,128)(2,1)S(1)} %convolution_convert_fusion.8), channel_id=1, source_target_pairs={{0,1},{1,0},{2,3},{3,2},{4,5},{5,4},{6,7},{7,6},{8,9},{9,8},{10,11... | collective-permute-start | bytes 491528 | tf_op jit(solution)/shard_map/ppermute | solution.py:93
  45.4 33.9 %collective-permute-start.11 = (bf16[64,640]{1,0:T(8,128)(2,1)S(1)}, bf16[64,640]{1,0:T(8,128)(2,1)S(1)}, u32[]{:S(2)}, u32[]{:S(2)}) collective-permute-start(bf16[64,640]{1,0:T(8,128)(2,1)S(1)} %fusion.18), channel_id=1, source_target_pairs={{0,8},{4,12},{8,0},{12,4},{1,9},{5,13},{9,1},{13,5},{2,10},{6,14},... | collective-permute-start | bytes 245768 | tf_op jit(solution)/shard_map/ppermute | solution.py:98
  50.8 4.5 %collective-permute-start.31 = (bf16[64,640]{1,0:T(8,128)(2,1)S(1)}, bf16[64,640]{1,0:T(8,128)(2,1)S(1)}, u32[]{:S(2)}, u32[]{:S(2)}) collective-permute-start(bf16[64,640]{1,0:T(8,128)(2,1)S(1)} %slice.200), channel_id=1, source_target_pairs={{0,2},{1,3},{2,0},{3,1},{4,6},{5,7},{6,4},{7,5},{8,10},{9,11},{10,... | collective-permute-start | bytes 245768 | tf_op jit(solution)/shard_map/ppermute | solution.py:95
  53.5 2.7 %collective-permute-start.33 = (bf16[64,1280]{1,0:T(8,128)(2,1)S(1)}, bf16[64,1280]{1,0:T(8,128)(2,1)S(1)}, u32[]{:S(2)}, u32[]{:S(2)}) collective-permute-start(bf16[64,1280]{1,0:T(8,128)(2,1)S(1)} %convolution_convert_fusion.2), channel_id=1, source_target_pairs={{0,1},{1,0},{2,3},{3,2},{4,5},{5,4},{6,7},{7,6},{8,9},{9,8},{10,11... | collective-permute-start | bytes 491528 | tf_op jit(solution)/shard_map/ppermute | solution.py:93
  55.4 4.5 %collective-permute-start.18 = (bf16[64,640]{1,0:T(8,128)(2,1)S(1)}, bf16[64,640]{1,0:T(8,128)(2,1)S(1)}, u32[]{:S(2)}, u32[]{:S(2)}) collective-permute-start(bf16[64,640]{1,0:T(8,128)(2,1)S(1)} %slice.203), channel_id=1, source_target_pairs={{0,2},{1,3},{2,0},{3,1},{4,6},{5,7},{6,4},{7,5},{8,10},{9,11},{10,... | collective-permute-start | bytes 245768 | tf_op jit(solution)/shard_map/ppermute | solution.py:95
  58.1 2.3 %collective-permute-start.25 = (bf16[64,1280]{1,0:T(8,128)(2,1)S(1)}, bf16[64,1280]{1,0:T(8,128)(2,1)S(1)}, u32[]{:S(2)}, u32[]{:S(2)}) collective-permute-start(bf16[64,1280]{1,0:T(8,128)(2,1)S(1)} %convolution_convert_fusion.5), channel_id=1, source_target_pairs={{0,1},{1,0},{2,3},{3,2},{4,5},{5,4},{6,7},{7,6},{8,9},{9,8},{10,11... | collective-permute-start | bytes 491528 | tf_op jit(solution)/shard_map/ppermute | solution.py:93
  59.9 19.9 %collective-permute-start.19 = (bf16[64,640]{1,0:T(8,128)(2,1)S(1)}, bf16[64,640]{1,0:T(8,128)(2,1)S(1)}, u32[]{:S(2)}, u32[]{:S(2)}) collective-permute-start(bf16[64,640]{1,0:T(8,128)(2,1)S(1)} %fusion.17), channel_id=1, source_target_pairs={{0,12},{4,8},{8,4},{12,0},{1,13},{5,9},{9,5},{13,1},{2,14},{6,10},... | collective-permute-start | bytes 245768 | tf_op jit(solution)/shard_map/ppermute | solution.py:98
  60.4 4.5 %collective-permute-start.34 = (bf16[64,640]{1,0:T(8,128)(2,1)S(1)}, bf16[64,640]{1,0:T(8,128)(2,1)S(1)}, u32[]{:S(2)}, u32[]{:S(2)}) collective-permute-start(bf16[64,640]{1,0:T(8,128)(2,1)S(1)} %slice.199), channel_id=1, source_target_pairs={{0,2},{1,3},{2,0},{3,1},{4,6},{5,7},{6,4},{7,5},{8,10},{9,11},{10,... | collective-permute-start | bytes 245768 | tf_op jit(solution)/shard_map/ppermute | solution.py:95
  64.9 1.4 %collective-permute-start.38 = (bf16[64,1280]{1,0:T(8,128)(2,1)S(1)}, bf16[64,1280]{1,0:T(8,128)(2,1)S(1)}, u32[]{:S(2)}, u32[]{:S(2)}) collective-permute-start(bf16[64,1280]{1,0:T(8,128)(2,1)S(1)} %convolution_convert_fusion), channel_id=1, source_target_pairs={{0,1},{1,0},{2,3},{3,2},{4,5},{5,4},{6,7},{7,6},{8,9},{9,8},{10,11... | collective-permute-start | bytes 491528 | tf_op jit(solution)/shard_map/ppermute | solution.py:93
  66.3 4.5 %collective-permute-start.26 = (bf16[64,640]{1,0:T(8,128)(2,1)S(1)}, bf16[64,640]{1,0:T(8,128)(2,1)S(1)}, u32[]{:S(2)}, u32[]{:S(2)}) collective-permute-start(bf16[64,640]{1,0:T(8,128)(2,1)S(1)} %slice.202), channel_id=1, source_target_pairs={{0,2},{1,3},{2,0},{3,1},{4,6},{5,7},{6,4},{7,5},{8,10},{9,11},{10,... | collective-permute-start | bytes 245768 | tf_op jit(solution)/shard_map/ppermute | solution.py:95
  70.8 4.4 %collective-permute-start.39 = (bf16[64,640]{1,0:T(8,128)(2,1)S(1)}, bf16[64,640]{1,0:T(8,128)(2,1)S(1)}, u32[]{:S(2)}, u32[]{:S(2)}) collective-permute-start(bf16[64,640]{1,0:T(8,128)(2,1)S(1)} %slice.198), channel_id=1, source_target_pairs={{0,2},{1,3},{2,0},{3,1},{4,6},{5,7},{6,4},{7,5},{8,10},{9,11},{10,... | collective-permute-start | bytes 245768 | tf_op jit(solution)/shard_map/ppermute | solution.py:95
  75.3 4.8 %collective-permute-start.27 = (bf16[64,640]{1,0:T(8,128)(2,1)S(1)}, bf16[64,640]{1,0:T(8,128)(2,1)S(1)}, u32[]{:S(2)}, u32[]{:S(2)}) collective-permute-start(bf16[64,640]{1,0:T(8,128)(2,1)S(1)} %fusion.16), channel_id=1, source_target_pairs={{0,4},{4,0},{8,12},{12,8},{1,5},{5,1},{9,13},{13,9},{2,6},{6,2},{1... | collective-permute-start | bytes 245768 | tf_op jit(solution)/shard_map/ppermute | solution.py:98
  75.4 8.1 %collective-permute-start.32 = (bf16[64,640]{1,0:T(8,128)(2,1)S(1)}, bf16[64,640]{1,0:T(8,128)(2,1)S(1)}, u32[]{:S(2)}, u32[]{:S(2)}) collective-permute-start(bf16[64,640]{1,0:T(8,128)(2,1)S(1)} %fusion.10), channel_id=1, source_target_pairs={{0,8},{4,12},{8,0},{12,4},{1,9},{5,13},{9,1},{13,5},{2,10},{6,14},... | collective-permute-start | bytes 245768 | tf_op jit(solution)/shard_map/ppermute | solution.py:98
  79.3 6.2 %collective-permute-start.35 = (bf16[64,640]{1,0:T(8,128)(2,1)S(1)}, bf16[64,640]{1,0:T(8,128)(2,1)S(1)}, u32[]{:S(2)}, u32[]{:S(2)}) collective-permute-start(bf16[64,640]{1,0:T(8,128)(2,1)S(1)} %fusion.9), channel_id=1, source_target_pairs={{0,12},{4,8},{8,4},{12,0},{1,13},{5,9},{9,5},{13,1},{2,14},{6,10},... | collective-permute-start | bytes 245768 | tf_op jit(solution)/shard_map/ppermute | solution.py:98
  79.8 5.8 %collective-permute-start.40 = (bf16[64,640]{1,0:T(8,128)(2,1)S(1)}, bf16[64,640]{1,0:T(8,128)(2,1)S(1)}, u32[]{:S(2)}, u32[]{:S(2)}) collective-permute-start(bf16[64,640]{1,0:T(8,128)(2,1)S(1)} %fusion.8), channel_id=1, source_target_pairs={{0,4},{4,0},{8,12},{12,8},{1,5},{5,1},{9,13},{13,9},{2,6},{6,2},{1... | collective-permute-start | bytes 245768 | tf_op jit(solution)/shard_map/ppermute | solution.py:98

commit v16 on v10

--- a/solution.py
+++ b/solution.py
@@ -62,9 +62,6 @@
     me = lax.axis_index("expert")
     t = lax.axis_index("tensor")
     scaled = (tokens.astype(jnp.float32) * route_scale[:, None]).astype(jnp.bfloat16)
-    blocks = [scaled] + [
-        lax.ppermute(scaled, "expert", _xor_pairs(n_expert, k)) for k in range(1, n_expert)
-    ]
     routed = expert_ids[:, 0][:, None]
     gate_w = _slots(gate_weight[0], t, width, 0)
     up_w = _slots(up_weight[0], t, width, 0)
@@ -74,7 +71,8 @@
     total = None
     previous = None
     for wave in waves:
-        piece = jnp.concatenate([blocks[k] for k in wave])
+        piece = jnp.concatenate([
+            lax.ppermute(scaled, "expert", _xor_pairs(n_expert, k)) if k else scaled for k in wave])
         pair = jnp.concatenate(
             [piece, lax.ppermute(piece, "tensor", _xor_pairs(n_tensor, 2))], axis=1)
         rows = jnp.concatenate(

time: 67 us -> 67 us (level)
  no operation moved by 1% of the time
where the time goes in v16:
time: 67 us; the launch traced here: 66.8 us
  waiting for transfers between devices  28.5 us (43%)
  starting transfers between devices  21.1 us (31%)
  matrix products  9.28 us (14%)
  local copies, waits for them, and re-layouts  5.18 us (8%)
  other arithmetic  2.46 us (4%)
    ppermute x4, waiting for transfers between devices, gathered(): lax.ppermute(piece, 'tensor', _xor_pairs(n_tensor, 2))  9.45 us
    ppermute x3, waiting for transfers between devices, gathered(): lax.ppermute(scaled, 'expert', _xor_pairs(n_expert, k))  5.9 us
    ppermute x3, waiting for transfers between devices, gathered(): lax.ppermute(part.astype(jnp.bfloat16), 'expert', _xor_pairs(n_expert, k))  5.58 us
    ppermute x4, starting transfers between devices, gathered(): lax.ppermute(piece, 'tensor', _xor_pairs(n_tensor, 2))  5.55 us
    ppermute x3, starting transfers between devices, gathered(): lax.ppermute(part.astype(jnp.bfloat16), 'expert', _xor_pairs(n_expert, k))  5.53 us
    ppermute x4, waiting for transfers between devices, gathered(): lax.ppermute(over_c[:, width:].astype(jnp.bfloat16), 'tensor', _xor_pairs...  5.05 us
    ppermute x3, starting transfers between devices, gathered(): lax.ppermute(scaled, 'expert', _xor_pairs(n_expert, k))  4.17 us
    ppermute x4, starting transfers between devices, gathered(): lax.ppermute(over_c[:, width:].astype(jnp.bfloat16), 'tensor', _xor_pairs...  3.82 us
  transfers between devices with their start and end apart: 22, of which 12 were waited for; matrix products, arithmetic and copies ran while one was open for 19% of the time, Pallas kernels for 0%

profile of v16, /device:TPU:0, one launch (start us, length us, event | category | flops | bytes accessed | tf_op | source)
XLA Modules:
  0.0 66.8 jit_solution(694309491824602760)
XLA Ops:
  0.0 1.0 %multiply_convert_fusion = bf16[128,640]{1,0:T(8,128)(2,1)S(1)} fusion(bf16[128,640]{1,0:T(8,128)(2,1)} %param.6, f32[128]{0:T(128)} %param.7), kind=kLoop, calls=%fused_computation.59 | loop fusion | flops 245760 | bytes 328192 | tf_op jit(solution)/shard_map/convert_element_type | solution.py:64
  1.0 3.0 %collective-permute-start = (bf16[128,640]{1,0:T(8,128)(2,1)S(1)}, bf16[128,640]{1,0:T(8,128)(2,1)S(1)}, u32[]{:S(2)}, u32[]{:S(2)}) collective-permute-start(bf16[128,640]{1,0:T(8,128)(2,1)S(1)} %multiply_convert_fusion), channel_id=1, source_target_pairs={{0,2},{1,3},{2,0},{3,1},{4,6},{5,7},{6,4},{7,5},{8,10},{9,11},{10,... | collective-permute-start | bytes 491528 | tf_op jit(solution)/shard_map/ppermute | solution.py:77
  4.0 2.6 %collective-permute-start.4 = (bf16[128,640]{1,0:T(8,128)(2,1)S(1)}, bf16[128,640]{1,0:T(8,128)(2,1)S(1)}, u32[]{:S(2)}, u32[]{:S(2)}) collective-permute-start(bf16[128,640]{1,0:T(8,128)(2,1)S(1)} %multiply_convert_fusion), channel_id=1, source_target_pairs={{0,8},{4,12},{8,0},{12,4},{1,9},{5,13},{9,1},{13,5},{2,10},{6,14},... | collective-permute-start | bytes 491528 | tf_op jit(solution)/shard_map/ppermute | solution.py:75
  6.6 1.3 %collective-permute-start.10 = (bf16[128,640]{1,0:T(8,128)(2,1)S(1)}, bf16[128,640]{1,0:T(8,128)(2,1)S(1)}, u32[]{:S(2)}, u32[]{:S(2)}) collective-permute-start(bf16[128,640]{1,0:T(8,128)(2,1)S(1)} %multiply_convert_fusion), channel_id=1, source_target_pairs={{0,12},{4,8},{8,4},{12,0},{1,13},{5,9},{9,5},{13,1},{2,14},{6,10},... | collective-permute-start | bytes 491528 | tf_op jit(solution)/shard_map/ppermute | solution.py:75
  8.2 2.0 %dynamic-slice_bitcast_fusion.11 = (bf16[640,512]{1,0:T(8,128)(2,1)S(1)}, bf16[640,512]{1,0:T(8,128)(2,1)S(1)}, bf16[640,512]{1,0:T(8,128)(2,1)S(1)}, bf16[640,512]{1,0:T(8,128)(2,1)S(1)}) fusion(bf16[1,2560,512]{2,1,0:T(8,128)(2,1)} %param.9, s32[]{:T(128)S(6)} %select_n.48, s32[]{:T(128)S(6)} %select_n.49, s32[]{:T(128)S(6)} %select_n.51, s32[]{:T(128)S(6)} %select_n.50), kind=kLoop, calls=%fused_computation.38 | loop fusion | bytes 5242896 | tf_op jit(solution)/shard_map/dynamic_slice | solution.py:55
  10.2 0.5 copy-done
  11.1 1.5 %copy-done.1 = bf16[1,512,2560]{2,1,0:T(8,128)(2,1)S(1)} copy-done((bf16[1,512,2560]{2,1,0:T(8,128)(2,1)S(1)}, bf16[1,512,2560]{2,1,0:T(8,128)(2,1)}, u32[]{:S(2)}) %copy-start.1) | copy-done | bytes 2621464
  12.9 5.9 %collective-permute-done.4 = bf16[128,640]{1,0:T(8,128)(2,1)S(1)} collective-permute-done((bf16[128,640]{1,0:T(8,128)(2,1)S(1)}, bf16[128,640]{1,0:T(8,128)(2,1)S(1)}, u32[]{:S(2)}, u32[]{:S(2)}) %collective-permute-start.4) | collective-permute-done | bytes 163872 | tf_op jit(solution)/shard_map/ppermute | solution.py:75
  18.8 0.5 collective-permute-start.5
  19.3 1.6 %collective-permute-start.11 = (bf16[128,640]{1,0:T(8,128)(2,1)S(1)}, bf16[128,640]{1,0:T(8,128)(2,1)S(1)}, u32[]{:S(2)}, u32[]{:S(2)}) collective-permute-start(bf16[128,640]{1,0:T(8,128)(2,1)S(1)} %collective-permute-done.10), channel_id=1, source_target_pairs={{0,2},{1,3},{2,0},{3,1},{4,6},{5,7},{6,4},{7,5},{8,10},{9,11},{10,... | collective-permute-start | bytes 491528 | tf_op jit(solution)/shard_map/ppermute | solution.py:77
  21.0 0.5 collective-permute-start.17
  21.4 4.3 %collective-permute-done.5 = bf16[128,640]{1,0:T(8,128)(2,1)S(1)} collective-permute-done((bf16[128,640]{1,0:T(8,128)(2,1)S(1)}, bf16[128,640]{1,0:T(8,128)(2,1)S(1)}, u32[]{:S(2)}, u32[]{:S(2)}) %collective-permute-start.5) | collective-permute-done | bytes 163872 | tf_op jit(solution)/shard_map/ppermute | solution.py:77
  25.8 3.4 %collective-permute-done.11 = bf16[128,640]{1,0:T(8,128)(2,1)S(1)} collective-permute-done((bf16[128,640]{1,0:T(8,128)(2,1)S(1)}, bf16[128,640]{1,0:T(8,128)(2,1)S(1)}, u32[]{:S(2)}, u32[]{:S(2)}) %collective-permute-start.11) | collective-permute-done | bytes 163872 | tf_op jit(solution)/shard_map/ppermute | solution.py:77
  29.3 1.8 %collective-permute-done.17 = bf16[128,640]{1,0:T(8,128)(2,1)S(1)} collective-permute-done((bf16[128,640]{1,0:T(8,128)(2,1)S(1)}, bf16[128,640]{1,0:T(8,128)(2,1)S(1)}, u32[]{:S(2)}, u32[]{:S(2)}) %collective-permute-start.17) | collective-permute-done | bytes 163872 | tf_op jit(solution)/shard_map/ppermute | solution.py:77
  31.2 0.5 fusion.13
  31.7 0.5 multiply_convert_fusion.1
  32.3 0.3 convolution_convert_fusion.6
  32.6 0.5 collective-permute-start.2
  33.2 1.2 %collective-permute-done.2 = bf16[128,1280]{1,0:T(8,128)(2,1)S(1)} collective-permute-done((bf16[128,1280]{1,0:T(8,128)(2,1)S(1)}, bf16[128,1280]{1,0:T(8,128)(2,1)S(1)}, u32[]{:S(2)}, u32[]{:S(2)}) %collective-permute-start.2) | collective-permute-done | bytes 327712 | tf_op jit(solution)/shard_map/ppermute | solution.py:88
  34.8 0.5 fusion.16
  35.3 0.7 %fusion.1 = bf16[128,512]{1,0:T(8,128)(2,1)S(1)} fusion(bf16[128,2560]{1,0:T(8,128)(2,1)S(1)} %pad_maximum_fusion.5, f32[128,512]{1,0:T(8,128)S(1)} %fusion.16, bf16[640,512]{1,0:T(8,128)(2,1)S(1)} %get-tuple-element.17, bf16[640,512]{1,0:T(8,128)(2,1)S(1)} %get-tuple-element.18, bf16[640,512]{1,0:T(8,128)(2,1)S(1)} %get-tuple-element.16, ...), kind=kOutput, calls=%fused_computation.16 | convolution fusion | flops 346423296 | bytes 3670016 | tf_op jit(solution)/shard_map/dot_general | solution.py:83
  36.0 0.3 convolution_convert_fusion.4
  36.4 0.4 collective-permute-start.7
  36.9 1.2 %collective-permute-done.7 = bf16[128,1280]{1,0:T(8,128)(2,1)S(1)} collective-permute-done((bf16[128,1280]{1,0:T(8,128)(2,1)S(1)}, bf16[128,1280]{1,0:T(8,128)(2,1)S(1)}, u32[]{:S(2)}, u32[]{:S(2)}) %collective-permute-start.7) | collective-permute-done | bytes 327712 | tf_op jit(solution)/shard_map/ppermute | solution.py:88
  38.1 0.3 convert_add_fusion.2
  38.4 0.5 fusion.17
  38.9 0.7 %fusion.2 = bf16[128,512]{1,0:T(8,128)(2,1)S(1)} fusion(bf16[128,2560]{1,0:T(8,128)(2,1)S(1)} %pad_maximum_fusion.6, f32[128,512]{1,0:T(8,128)S(1)} %fusion.17, bf16[640,512]{1,0:T(8,128)(2,1)S(1)} %get-tuple-element.17, bf16[640,512]{1,0:T(8,128)(2,1)S(1)} %get-tuple-element.18, bf16[640,512]{1,0:T(8,128)(2,1)S(1)} %get-tuple-element.16, ...), kind=kOutput, calls=%fused_computation.17 | convolution fusion | flops 346423296 | bytes 3670016 | tf_op jit(solution)/shard_map/dot_general | solution.py:83
  39.7 0.3 convolution_convert_fusion.2
  40.0 0.4 collective-permute-start.13
  40.5 0.7 %slice.70 = bf16[128,640]{1,0:T(8,128)(2,1)} slice(f32[128,1280]{1,0:T(8,128)S(1)} %convert_add_fusion.2), slice={[0:128], [640:1280]} | slice | bytes 327680 | tf_op jit(solution)/shard_map/slice | solution.py:91
  41.2 0.5 collective-permute-start.8
  41.7 0.3 convert_add_fusion.1
  42.1 0.5 fusion.18
  42.6 0.7 %fusion.3 = bf16[128,512]{1,0:T(8,128)(2,1)S(1)} fusion(bf16[128,2560]{1,0:T(8,128)(2,1)S(1)} %pad_maximum_fusion.7, f32[128,512]{1,0:T(8,128)S(1)} %fusion.18, bf16[640,512]{1,0:T(8,128)(2,1)S(1)} %get-tuple-element.17, bf16[640,512]{1,0:T(8,128)(2,1)S(1)} %get-tuple-element.18, bf16[640,512]{1,0:T(8,128)(2,1)S(1)} %get-tuple-element.16, ...), kind=kOutput, calls=%fused_computation.18 | convolution fusion | flops 346423296 | bytes 3670016 | tf_op jit(solution)/shard_map/dot_general | solution.py:83
  43.4 1.1 %convolution_convert_fusion = bf16[128,1280]{1,0:T(8,128)(2,1)} fusion(bf16[128,512]{1,0:T(8,128)(2,1)S(1)} %fusion.3, bf16[512,640]{1,0:T(8,128)(2,1)S(1)} %get-tuple-element.13, bf16[512,640]{1,0:T(8,128)(2,1)S(1)} %get-tuple-element.14), kind=kOutput, calls=%fused_computation.2 | convolution fusion | flops 170557440 | bytes 1769472 | tf_op jit(solution)/shard_map/dot_general | solution.py:86
  44.4 0.4 collective-permute-start.19
  44.8 1.2 %collective-permute-start.3 = (bf16[128,640]{1,0:T(8,128)(2,1)S(1)}, bf16[128,640]{1,0:T(8,128)(2,1)S(1)}, u32[]{:S(2)}, u32[]{:S(2)}) collective-permute-start(bf16[128,640]{1,0:T(8,128)(2,1)S(1)} %slice.71), channel_id=1, source_target_pairs={{0,2},{1,3},{2,0},{3,1},{4,6},{5,7},{6,4},{7,5},{8,10},{9,11},{10,... | collective-permute-start | bytes 491528 | tf_op jit(solution)/shard_map/ppermute | solution.py:90
  46.0 1.6 %collective-permute-done.8 = bf16[128,640]{1,0:T(8,128)(2,1)S(1)} collective-permute-done((bf16[128,640]{1,0:T(8,128)(2,1)}, bf16[128,640]{1,0:T(8,128)(2,1)S(1)}, u32[]{:S(2)}, u32[]{:S(2)}) %collective-permute-start.8) | collective-permute-done | bytes 163872 | tf_op jit(solution)/shard_map/ppermute | solution.py:90
  47.7 2.4 %collective-permute-start.9 = (bf16[128,640]{1,0:T(8,128)(2,1)S(1)}, bf16[128,640]{1,0:T(8,128)(2,1)S(1)}, u32[]{:S(2)}, u32[]{:S(2)}) collective-permute-start(bf16[128,640]{1,0:T(8,128)(2,1)S(1)} %fusion.6), channel_id=1, source_target_pairs={{0,8},{4,12},{8,0},{12,4},{1,9},{5,13},{9,1},{13,5},{2,10},{6,14},... | collective-permute-start | bytes 491528 | tf_op jit(solution)/shard_map/ppermute | solution.py:95
  50.1 0.6 collective-permute-start.14
  50.7 1.4 %convert_add_fusion = f32[128,1280]{1,0:T(8,128)S(1)} fusion(bf16[128,1280]{1,0:T(8,128)(2,1)} %collective-permute-done.19, bf16[128,512]{1,0:T(8,128)(2,1)} %copy-done.3, bf16[512,640]{1,0:T(8,128)(2,1)S(1)} %get-tuple-element.12, bf16[512,640]{1,0:T(8,128)(2,1)S(1)} %get-tuple-element.11), kind=kOutput, calls=%fused_computation.23 | convolution fusion | flops 171048960 | bytes 2424832 | tf_op jit(solution)/shard_map/dot_general | solution.py:85
  52.1 1.6 %collective-permute-start.20 = (bf16[128,640]{1,0:T(8,128)(2,1)S(1)}, bf16[128,640]{1,0:T(8,128)(2,1)S(1)}, u32[]{:S(2)}, u32[]{:S(2)}) collective-permute-start(bf16[128,640]{1,0:T(8,128)(2,1)S(1)} %slice.68), channel_id=1, source_target_pairs={{0,2},{1,3},{2,0},{3,1},{4,6},{5,7},{6,4},{7,5},{8,10},{9,11},{10,... | collective-permute-start | bytes 491528 | tf_op jit(solution)/shard_map/ppermute | solution.py:90
  53.7 3.4 %collective-permute-done.14 = bf16[128,640]{1,0:T(8,128)(2,1)S(1)} collective-permute-done((bf16[128,640]{1,0:T(8,128)(2,1)S(1)}, bf16[128,640]{1,0:T(8,128)(2,1)S(1)}, u32[]{:S(2)}, u32[]{:S(2)}) %collective-permute-start.14) | collective-permute-done | bytes 163872 | tf_op jit(solution)/shard_map/ppermute | solution.py:90
  57.1 1.7 %collective-permute-start.15 = (bf16[128,640]{1,0:T(8,128)(2,1)S(1)}, bf16[128,640]{1,0:T(8,128)(2,1)S(1)}, u32[]{:S(2)}, u32[]{:S(2)}) collective-permute-start(bf16[128,640]{1,0:T(8,128)(2,1)S(1)} %fusion.5), channel_id=1, source_target_pairs={{0,12},{4,8},{8,4},{12,0},{1,13},{5,9},{9,5},{13,1},{2,14},{6,10},... | collective-permute-start | bytes 491528 | tf_op jit(solution)/shard_map/ppermute | solution.py:95
  58.8 1.5 %collective-permute-start.21 = (bf16[128,640]{1,0:T(8,128)(2,1)S(1)}, bf16[128,640]{1,0:T(8,128)(2,1)S(1)}, u32[]{:S(2)}, u32[]{:S(2)}) collective-permute-start(bf16[128,640]{1,0:T(8,128)(2,1)S(1)} %fusion.4), channel_id=1, source_target_pairs={{0,4},{4,0},{8,12},{12,8},{1,5},{5,1},{9,13},{13,9},{2,6},{6,2},{1... | collective-permute-start | bytes 491528 | tf_op jit(solution)/shard_map/ppermute | solution.py:95
  60.4 5.0 %collective-permute-done.15 = bf16[128,640]{1,0:T(8,128)(2,1)S(1)} collective-permute-done((bf16[128,640]{1,0:T(8,128)(2,1)S(1)}, bf16[128,640]{1,0:T(8,128)(2,1)S(1)}, u32[]{:S(2)}, u32[]{:S(2)}) %collective-permute-start.15) | collective-permute-done | bytes 163872 | tf_op jit(solution)/shard_map/ppermute | solution.py:95
  65.4 0.6 collective-permute-done.21
  66.0 0.9 %fusion.11 = bf16[128,640]{1,0:T(8,128)(2,1)} fusion(f32[128,1280]{1,0:T(8,128)S(1)} %convert_add_fusion.3, bf16[128,640]{1,0:T(8,128)(2,1)S(1)} %collective-permute-done.21, bf16[128,640]{1,0:T(8,128)(2,1)S(1)} %collective-permute-done.15, bf16[128,640]{1,0:T(8,128)(2,1)S(1)} %collective-permute-done.9, bf16[128,640]{1,0:T(8,128)(2,1)S(1)} %collective-permute-done.3, ...), kind=kLoop, calls=%fused_computation.54 | loop fusion | flops 1064960 | bytes 1147392 | tf_op jit(solution)/shard_map/convert_element_type | solution.py:99
  (41 shorter events, 2.1 us)
Async XLA Ops:
  1.0 18.2 %collective-permute-start = (bf16[128,640]{1,0:T(8,128)(2,1)S(1)}, bf16[128,640]{1,0:T(8,128)(2,1)S(1)}, u32[]{:S(2)}, u32[]{:S(2)}) collective-permute-start(bf16[128,640]{1,0:T(8,128)(2,1)S(1)} %multiply_convert_fusion), channel_id=1, source_target_pairs={{0,2},{1,3},{2,0},{3,1},{4,6},{5,7},{6,4},{7,5},{8,10},{9,11},{10,... | collective-permute-start | bytes 491528 | tf_op jit(solution)/shard_map/ppermute | solution.py:77
  4.0 14.7 %collective-permute-start.4 = (bf16[128,640]{1,0:T(8,128)(2,1)S(1)}, bf16[128,640]{1,0:T(8,128)(2,1)S(1)}, u32[]{:S(2)}, u32[]{:S(2)}) collective-permute-start(bf16[128,640]{1,0:T(8,128)(2,1)S(1)} %multiply_convert_fusion), channel_id=1, source_target_pairs={{0,8},{4,12},{8,0},{12,4},{1,9},{5,13},{9,1},{13,5},{2,10},{6,14},... | collective-permute-start | bytes 491528 | tf_op jit(solution)/shard_map/ppermute | solution.py:75
  6.6 12.7 %collective-permute-start.10 = (bf16[128,640]{1,0:T(8,128)(2,1)S(1)}, bf16[128,640]{1,0:T(8,128)(2,1)S(1)}, u32[]{:S(2)}, u32[]{:S(2)}) collective-permute-start(bf16[128,640]{1,0:T(8,128)(2,1)S(1)} %multiply_convert_fusion), channel_id=1, source_target_pairs={{0,12},{4,8},{8,4},{12,0},{1,13},{5,9},{9,5},{13,1},{2,14},{6,10},... | collective-permute-start | bytes 491528 | tf_op jit(solution)/shard_map/ppermute | solution.py:75
  8.0 13.0 %collective-permute-start.16 = (bf16[128,640]{1,0:T(8,128)(2,1)S(1)}, bf16[128,640]{1,0:T(8,128)(2,1)S(1)}, u32[]{:S(2)}, u32[]{:S(2)}) collective-permute-start(bf16[128,640]{1,0:T(8,128)(2,1)S(1)} %multiply_convert_fusion), channel_id=1, source_target_pairs={{0,4},{4,0},{8,12},{12,8},{1,5},{5,1},{9,13},{13,9},{2,6},{6,2},{1... | collective-permute-start | bytes 491528 | tf_op jit(solution)/shard_map/ppermute | solution.py:75
  8.2 2.5 %copy-start = (bf16[1,2560,512]{2,1,0:T(8,128)(2,1)S(1)}, bf16[1,2560,512]{2,1,0:T(8,128)(2,1)}, u32[]{:S(2)}) copy-start(bf16[1,2560,512]{2,1,0:T(8,128)(2,1)} %param.10) | copy-start | bytes 7864324
  10.9 1.7 %copy-start.1 = (bf16[1,512,2560]{2,1,0:T(8,128)(2,1)S(1)}, bf16[1,512,2560]{2,1,0:T(8,128)(2,1)}, u32[]{:S(2)}) copy-start(bf16[1,512,2560]{2,1,0:T(8,128)(2,1)} %param.11) | copy-start | bytes 7864324
  18.8 7.0 %collective-permute-start.5 = (bf16[128,640]{1,0:T(8,128)(2,1)S(1)}, bf16[128,640]{1,0:T(8,128)(2,1)S(1)}, u32[]{:S(2)}, u32[]{:S(2)}) collective-permute-start(bf16[128,640]{1,0:T(8,128)(2,1)S(1)} %collective-permute-done.4), channel_id=1, source_target_pairs={{0,2},{1,3},{2,0},{3,1},{4,6},{5,7},{6,4},{7,5},{8,10},{9,11},{10,... | collective-permute-start | bytes 491528 | tf_op jit(solution)/shard_map/ppermute | solution.py:77
  19.3 12.0 %collective-permute-start.1 = (bf16[128,1280]{1,0:T(8,128)(2,1)S(1)}, bf16[128,1280]{1,0:T(8,128)(2,1)S(1)}, u32[]{:S(2)}, u32[]{:S(2)}) collective-permute-start(bf16[128,1280]{1,0:T(8,128)(2,1)S(1)} %pad_maximum_fusion.8), channel_id=1, source_target_pairs={{0,1},{1,0},{2,3},{3,2},{4,5},{5,4},{6,7},{7,6},{8,9},{9,8},{10,11... | collective-permute-start | bytes 983048 | tf_op jit(solution)/shard_map/ppermute | solution.py:79
  19.3 9.9 %collective-permute-start.11 = (bf16[128,640]{1,0:T(8,128)(2,1)S(1)}, bf16[128,640]{1,0:T(8,128)(2,1)S(1)}, u32[]{:S(2)}, u32[]{:S(2)}) collective-permute-start(bf16[128,640]{1,0:T(8,128)(2,1)S(1)} %collective-permute-done.10), channel_id=1, source_target_pairs={{0,2},{1,3},{2,0},{3,1},{4,6},{5,7},{6,4},{7,5},{8,10},{9,11},{10,... | collective-permute-start | bytes 491528 | tf_op jit(solution)/shard_map/ppermute | solution.py:77
  21.0 10.1 %collective-permute-start.17 = (bf16[128,640]{1,0:T(8,128)(2,1)S(1)}, bf16[128,640]{1,0:T(8,128)(2,1)S(1)}, u32[]{:S(2)}, u32[]{:S(2)}) collective-permute-start(bf16[128,640]{1,0:T(8,128)(2,1)S(1)} %collective-permute-done.16), channel_id=1, source_target_pairs={{0,2},{1,3},{2,0},{3,1},{4,6},{5,7},{6,4},{7,5},{8,10},{9,11},{10,... | collective-permute-start | bytes 491528 | tf_op jit(solution)/shard_map/ppermute | solution.py:77
  25.8 7.4 %collective-permute-start.6 = (bf16[128,1280]{1,0:T(8,128)(2,1)S(1)}, bf16[128,1280]{1,0:T(8,128)(2,1)S(1)}, u32[]{:S(2)}, u32[]{:S(2)}) collective-permute-start(bf16[128,1280]{1,0:T(8,128)(2,1)S(1)} %pad_maximum_fusion.9), channel_id=1, source_target_pairs={{0,1},{1,0},{2,3},{3,2},{4,5},{5,4},{6,7},{7,6},{8,9},{9,8},{10,11... | collective-permute-start | bytes 983048 | tf_op jit(solution)/shard_map/ppermute | solution.py:79
  29.3 7.6 %collective-permute-start.12 = (bf16[128,1280]{1,0:T(8,128)(2,1)S(1)}, bf16[128,1280]{1,0:T(8,128)(2,1)S(1)}, u32[]{:S(2)}, u32[]{:S(2)}) collective-permute-start(bf16[128,1280]{1,0:T(8,128)(2,1)S(1)} %pad_maximum_fusion.10), channel_id=1, source_target_pairs={{0,1},{1,0},{2,3},{3,2},{4,5},{5,4},{6,7},{7,6},{8,9},{9,8},{10,11... | collective-permute-start | bytes 983048 | tf_op jit(solution)/shard_map/ppermute | solution.py:79
  31.1 9.3 %collective-permute-start.18 = (bf16[128,1280]{1,0:T(8,128)(2,1)S(1)}, bf16[128,1280]{1,0:T(8,128)(2,1)S(1)}, u32[]{:S(2)}, u32[]{:S(2)}) collective-permute-start(bf16[128,1280]{1,0:T(8,128)(2,1)S(1)} %pad_maximum_fusion.11), channel_id=1, source_target_pairs={{0,1},{1,0},{2,3},{3,2},{4,5},{5,4},{6,7},{7,6},{8,9},{9,8},{10,11... | collective-permute-start | bytes 983048 | tf_op jit(solution)/shard_map/ppermute | solution.py:79
  32.6 1.8 %collective-permute-start.2 = (bf16[128,1280]{1,0:T(8,128)(2,1)S(1)}, bf16[128,1280]{1,0:T(8,128)(2,1)S(1)}, u32[]{:S(2)}, u32[]{:S(2)}) collective-permute-start(bf16[128,1280]{1,0:T(8,128)(2,1)S(1)} %convolution_convert_fusion.6), channel_id=1, source_target_pairs={{0,1},{1,0},{2,3},{3,2},{4,5},{5,4},{6,7},{7,6},{8,9},{9,8},{10,11... | collective-permute-start | bytes 983048 | tf_op jit(solution)/shard_map/ppermute | solution.py:88
  36.4 1.7 %collective-permute-start.7 = (bf16[128,1280]{1,0:T(8,128)(2,1)S(1)}, bf16[128,1280]{1,0:T(8,128)(2,1)S(1)}, u32[]{:S(2)}, u32[]{:S(2)}) collective-permute-start(bf16[128,1280]{1,0:T(8,128)(2,1)S(1)} %convolution_convert_fusion.4), channel_id=1, source_target_pairs={{0,1},{1,0},{2,3},{3,2},{4,5},{5,4},{6,7},{7,6},{8,9},{9,8},{10,11... | collective-permute-start | bytes 983048 | tf_op jit(solution)/shard_map/ppermute | solution.py:88
  40.0 1.7 %collective-permute-start.13 = (bf16[128,1280]{1,0:T(8,128)(2,1)S(1)}, bf16[128,1280]{1,0:T(8,128)(2,1)S(1)}, u32[]{:S(2)}, u32[]{:S(2)}) collective-permute-start(bf16[128,1280]{1,0:T(8,128)(2,1)S(1)} %convolution_convert_fusion.2), channel_id=1, source_target_pairs={{0,1},{1,0},{2,3},{3,2},{4,5},{5,4},{6,7},{7,6},{8,9},{9,8},{10,11... | collective-permute-start | bytes 983048 | tf_op jit(solution)/shard_map/ppermute | solution.py:88
  41.2 6.5 %collective-permute-start.8 = (bf16[128,640]{1,0:T(8,128)(2,1)}, bf16[128,640]{1,0:T(8,128)(2,1)S(1)}, u32[]{:S(2)}, u32[]{:S(2)}) collective-permute-start(bf16[128,640]{1,0:T(8,128)(2,1)} %slice.70), channel_id=1, source_target_pairs={{0,2},{1,3},{2,0},{3,1},{4,6},{5,7},{6,4},{7,5},{8,10},{9,11},{10,... | collective-permute-start | bytes 491528 | tf_op jit(solution)/shard_map/ppermute | solution.py:90
  43.3 1.1 %copy-start.3 = (bf16[128,512]{1,0:T(8,128)(2,1)}, bf16[128,512]{1,0:T(8,128)(2,1)S(1)}, u32[]{:S(2)}) copy-start(bf16[128,512]{1,0:T(8,128)(2,1)S(1)} %fusion.3) | copy-start | bytes 393220
  44.4 6.2 %collective-permute-start.19 = (bf16[128,1280]{1,0:T(8,128)(2,1)}, bf16[128,1280]{1,0:T(8,128)(2,1)}, u32[]{:S(2)}, u32[]{:S(2)}) collective-permute-start(bf16[128,1280]{1,0:T(8,128)(2,1)} %convolution_convert_fusion), channel_id=1, source_target_pairs={{0,1},{1,0},{2,3},{3,2},{4,5},{5,4},{6,7},{7,6},{8,9},{9,8},{10,11... | collective-permute-start | bytes 983048 | tf_op jit(solution)/shard_map/ppermute | solution.py:88
  44.8 15.5 %copy-start.2 = (s32[128,1]{0,1:T(1,128)S(1)}, s32[128,1]{0,1:T(1,128)}, u32[]{:S(2)}) copy-start(s32[128,1]{0,1:T(1,128)} %param.8) | copy-start | bytes 1540
  44.8 15.5 %collective-permute-start.3 = (bf16[128,640]{1,0:T(8,128)(2,1)S(1)}, bf16[128,640]{1,0:T(8,128)(2,1)S(1)}, u32[]{:S(2)}, u32[]{:S(2)}) collective-permute-start(bf16[128,640]{1,0:T(8,128)(2,1)S(1)} %slice.71), channel_id=1, source_target_pairs={{0,2},{1,3},{2,0},{3,1},{4,6},{5,7},{6,4},{7,5},{8,10},{9,11},{10,... | collective-permute-start | bytes 491528 | tf_op jit(solution)/shard_map/ppermute | solution.py:90
  47.7 12.7 %collective-permute-start.9 = (bf16[128,640]{1,0:T(8,128)(2,1)S(1)}, bf16[128,640]{1,0:T(8,128)(2,1)S(1)}, u32[]{:S(2)}, u32[]{:S(2)}) collective-permute-start(bf16[128,640]{1,0:T(8,128)(2,1)S(1)} %fusion.6), channel_id=1, source_target_pairs={{0,8},{4,12},{8,0},{12,4},{1,9},{5,13},{9,1},{13,5},{2,10},{6,14},... | collective-permute-start | bytes 491528 | tf_op jit(solution)/shard_map/ppermute | solution.py:95
  50.1 6.9 %collective-permute-start.14 = (bf16[128,640]{1,0:T(8,128)(2,1)S(1)}, bf16[128,640]{1,0:T(8,128)(2,1)S(1)}, u32[]{:S(2)}, u32[]{:S(2)}) collective-permute-start(bf16[128,640]{1,0:T(8,128)(2,1)S(1)} %slice.69), channel_id=1, source_target_pairs={{0,2},{1,3},{2,0},{3,1},{4,6},{5,7},{6,4},{7,5},{8,10},{9,11},{10,... | collective-permute-start | bytes 491528 | tf_op jit(solution)/shard_map/ppermute | solution.py:90
  52.1 6.7 %collective-permute-start.20 = (bf16[128,640]{1,0:T(8,128)(2,1)S(1)}, bf16[128,640]{1,0:T(8,128)(2,1)S(1)}, u32[]{:S(2)}, u32[]{:S(2)}) collective-permute-start(bf16[128,640]{1,0:T(8,128)(2,1)S(1)} %slice.68), channel_id=1, source_target_pairs={{0,2},{1,3},{2,0},{3,1},{4,6},{5,7},{6,4},{7,5},{8,10},{9,11},{10,... | collective-permute-start | bytes 491528 | tf_op jit(solution)/shard_map/ppermute | solution.py:90
  57.1 8.3 %collective-permute-start.15 = (bf16[128,640]{1,0:T(8,128)(2,1)S(1)}, bf16[128,640]{1,0:T(8,128)(2,1)S(1)}, u32[]{:S(2)}, u32[]{:S(2)}) collective-permute-start(bf16[128,640]{1,0:T(8,128)(2,1)S(1)} %fusion.5), channel_id=1, source_target_pairs={{0,12},{4,8},{8,4},{12,0},{1,13},{5,9},{9,5},{13,1},{2,14},{6,10},... | collective-permute-start | bytes 491528 | tf_op jit(solution)/shard_map/ppermute | solution.py:95
  58.8 7.1 %collective-permute-start.21 = (bf16[128,640]{1,0:T(8,128)(2,1)S(1)}, bf16[128,640]{1,0:T(8,128)(2,1)S(1)}, u32[]{:S(2)}, u32[]{:S(2)}) collective-permute-start(bf16[128,640]{1,0:T(8,128)(2,1)S(1)} %fusion.4), channel_id=1, source_target_pairs={{0,4},{4,0},{8,12},{12,8},{1,5},{5,1},{9,13},{13,9},{2,6},{6,2},{1... | collective-permute-start | bytes 491528 | tf_op jit(solution)/shard_map/ppermute | solution.py:95

commit v17 on v10

--- a/solution.py
+++ b/solution.py
@@ -73,12 +73,17 @@
     waves = [[k] for k in [0] + list(range(2, n_expert)) + [1][:n_expert - 1]]
     total = None
     previous = None
-    for wave in waves:
-        piece = jnp.concatenate([blocks[k] for k in wave])
+    def full_rows(piece):
         pair = jnp.concatenate(
             [piece, lax.ppermute(piece, "tensor", _xor_pairs(n_tensor, 2))], axis=1)
-        rows = jnp.concatenate(
+        return jnp.concatenate(
             [pair, lax.ppermute(pair, "tensor", _xor_pairs(n_tensor, 1))], axis=1)
+
+    wave_rows = [full_rows(blocks[0])]
+    if len(waves) > 1:
+        rest = full_rows(jnp.concatenate([blocks[wave[0]] for wave in waves[1:]]))
+        wave_rows += [rest[i * tok_rows:(i + 1) * tok_rows] for i in range(len(waves) - 1)]
+    for wave, rows in zip(waves, wave_rows):
         if previous is not None:
             rows, _ = lax.optimization_barrier((rows, previous))
         gate_act = jnp.dot(rows, gate_w, preferred_element_type=jnp.float32)

time: 67 us -> 70.2 us (1.048)
  waiting for transfers between devices: 28.5 us -> 36.5 us
  starting transfers between devices: 21.1 us -> 18.2 us
  local copies, waits for them, and re-layouts: 5.18 us -> 3.23 us
    ppermute x3, waiting for transfers between devices: 5.9 us -> 8.96 us  [gathered(): lax.ppermute(scaled, 'expert', _xor_pairs(n_expert, k))]
    ppermute x8 -> x4, starting transfers between devices: 5.83 us -> 3.19 us  [the longest x2 3.05 us: full_rows(): lax.ppermute(piece, 'tensor', _xor_pairs(n_tensor, 2))]
    unnamed x8 -> x10, local copies, waits for them, and re-layouts: 2.04 us -> 0.06 us
    ppermute x8 -> x4, waiting for transfers between devices: 9.46 us -> 11.4 us  [the longest x2 11.4 us: full_rows(): lax.ppermute(piece, 'tensor', _xor_pairs(n_tensor, 2))]
    ppermute x3, starting transfers between devices: 5.53 us -> 3.67 us  [gathered(): lax.ppermute(part.astype(jnp.bfloat16), 'expert', _xor_pairs(n_expert, k))]
    ppermute x3, starting transfers between devices: 4.17 us -> 5.68 us  [gathered(): lax.ppermute(scaled, 'expert', _xor_pairs(n_expert, k))]
    ppermute x4, waiting for transfers between devices: 5.05 us -> 6.33 us  [gathered(): lax.ppermute(over_c[:, width:].astype(jnp.bfloat16), 'tensor', _xor_pairs...]
    ppermute x3, waiting for transfers between devices: 5.58 us -> 6.67 us  [gathered(): lax.ppermute(part.astype(jnp.bfloat16), 'expert', _xor_pairs(n_expert, k))]
  transfers between devices with their start and end apart: 22 -> 18, of which waited for: 12 -> 10; matrix products, arithmetic and copies ran while one was open for 19% -> 13% of each run, Pallas kernels for 0% -> 0%
where the time goes in v17:
time: 70.2 us; the launch traced here: 70 us
  waiting for transfers between devices  36.5 us (52%)
  starting transfers between devices  18.2 us (26%)
  matrix products  9.32 us (13%)
  local copies, waits for them, and re-layouts  3.23 us (5%)
  other arithmetic  2.46 us (4%)
    ppermute x2, waiting for transfers between devices, full_rows(): lax.ppermute(piece, 'tensor', _xor_pairs(n_tensor, 2))  11.4 us
    ppermute x3, waiting for transfers between devices, gathered(): lax.ppermute(scaled, 'expert', _xor_pairs(n_expert, k))  8.96 us
    ppermute x3, waiting for transfers between devices, gathered(): lax.ppermute(part.astype(jnp.bfloat16), 'expert', _xor_pairs(n_expert, k))  6.67 us
    ppermute x4, waiting for transfers between devices, gathered(): lax.ppermute(over_c[:, width:].astype(jnp.bfloat16), 'tensor', _xor_pairs...  6.33 us
    ppermute x3, starting transfers between devices, gathered(): lax.ppermute(scaled, 'expert', _xor_pairs(n_expert, k))  5.68 us
    ppermute x4, starting transfers between devices, gathered(): lax.ppermute(over_c[:, width:].astype(jnp.bfloat16), 'tensor', _xor_pairs...  4.59 us
    ppermute x3, starting transfers between devices, gathered(): lax.ppermute(part.astype(jnp.bfloat16), 'expert', _xor_pairs(n_expert, k))  3.67 us
    ppermute x4, waiting for transfers between devices, gathered(): lax.ppermute(send, 'tensor', _xor_pairs(n_tensor, 1)).astype(jnp.float32)  3.07 us
  transfers between devices with their start and end apart: 18, of which 10 were waited for; matrix products, arithmetic and copies ran while one was open for 13% of the time, Pallas kernels for 0%

profile of v17, /device:TPU:0, one launch (start us, length us, event | category | flops | bytes accessed | tf_op | source)
XLA Modules:
  0.0 70.0 jit_solution(3241921894580873228)
XLA Ops:
  0.0 1.0 %multiply_convert_fusion = bf16[128,640]{1,0:T(8,128)(2,1)S(1)} fusion(bf16[128,640]{1,0:T(8,128)(2,1)} %param.6, f32[128]{0:T(128)} %param.7), kind=kLoop, calls=%fused_computation.55 | loop fusion | flops 245760 | bytes 328192 | tf_op jit(solution)/shard_map/convert_element_type | solution.py:64
  1.0 3.1 %collective-permute-start.6 = (bf16[128,640]{1,0:T(8,128)(2,1)S(1)}, bf16[128,640]{1,0:T(8,128)(2,1)S(1)}, u32[]{:S(2)}, u32[]{:S(2)}) collective-permute-start(bf16[128,640]{1,0:T(8,128)(2,1)S(1)} %multiply_convert_fusion), channel_id=1, source_target_pairs={{0,4},{4,0},{8,12},{12,8},{1,5},{5,1},{9,13},{13,9},{2,6},{6,2},{1... | collective-permute-start | bytes 491528 | tf_op jit(solution)/shard_map/ppermute | solution.py:66
  4.1 2.5 %collective-permute-start.5 = (bf16[128,640]{1,0:T(8,128)(2,1)S(1)}, bf16[128,640]{1,0:T(8,128)(2,1)S(1)}, u32[]{:S(2)}, u32[]{:S(2)}) collective-permute-start(bf16[128,640]{1,0:T(8,128)(2,1)S(1)} %multiply_convert_fusion), channel_id=1, source_target_pairs={{0,12},{4,8},{8,4},{12,0},{1,13},{5,9},{9,5},{13,1},{2,14},{6,10},... | collective-permute-start | bytes 491528 | tf_op jit(solution)/shard_map/ppermute | solution.py:66
  6.7 1.5 %collective-permute-start = (bf16[128,640]{1,0:T(8,128)(2,1)S(1)}, bf16[128,640]{1,0:T(8,128)(2,1)S(1)}, u32[]{:S(2)}, u32[]{:S(2)}) collective-permute-start(bf16[128,640]{1,0:T(8,128)(2,1)S(1)} %multiply_convert_fusion), channel_id=1, source_target_pairs={{0,2},{1,3},{2,0},{3,1},{4,6},{5,7},{6,4},{7,5},{8,10},{9,11},{10,... | collective-permute-start | bytes 491528 | tf_op jit(solution)/shard_map/ppermute | solution.py:78
  8.2 1.8 %dynamic-slice_bitcast_fusion.11 = (bf16[640,512]{1,0:T(8,128)(2,1)S(1)}, bf16[640,512]{1,0:T(8,128)(2,1)S(1)}, bf16[640,512]{1,0:T(8,128)(2,1)S(1)}, bf16[640,512]{1,0:T(8,128)(2,1)S(1)}) fusion(bf16[1,2560,512]{2,1,0:T(8,128)(2,1)} %param.9, s32[]{:T(128)S(6)} %select_n.48, s32[]{:T(128)S(6)} %select_n.49, s32[]{:T(128)S(6)} %select_n.51, s32[]{:T(128)S(6)} %select_n.50), kind=kLoop, calls=%fused_computation.37 | loop fusion | bytes 5242896 | tf_op jit(solution)/shard_map/dynamic_slice | solution.py:55
  10.1 0.2 pad_maximum_fusion
  10.3 1.8 %collective-permute-done = bf16[128,640]{1,0:T(8,128)(2,1)S(1)} collective-permute-done((bf16[128,640]{1,0:T(8,128)(2,1)S(1)}, bf16[128,640]{1,0:T(8,128)(2,1)S(1)}, u32[]{:S(2)}, u32[]{:S(2)}) %collective-permute-start) | collective-permute-done | bytes 163872 | tf_op jit(solution)/shard_map/ppermute | solution.py:78
  12.2 9.0 %collective-permute-done.4 = bf16[128,640]{1,0:T(8,128)(2,1)S(1)} collective-permute-done((bf16[128,640]{1,0:T(8,128)(2,1)S(1)}, bf16[128,640]{1,0:T(8,128)(2,1)S(1)}, u32[]{:S(2)}, u32[]{:S(2)}) %collective-permute-start.4) | collective-permute-done | bytes 163872 | tf_op jit(solution)/shard_map/ppermute | solution.py:66
  21.3 1.6 %collective-permute-start.7 = (bf16[384,640]{1,0:T(8,128)(2,1)S(1)}, bf16[384,640]{1,0:T(8,128)(2,1)S(1)}, u32[]{:S(2)}, u32[]{:S(2)}) collective-permute-start(bf16[384,640]{1,0:T(8,128)(2,1)S(1)} %constant_dynamic-update-slice_fusion), channel_id=1, source_target_pairs={{0,2},{1,3},{2,0},{3,1},{4,6},{5,7},{6,4},{7,5},{8,10},{9,11},{10,... | collective-permute-start | bytes 1474568 | tf_op jit(solution)/shard_map/ppermute | solution.py:78
  22.8 0.2 dynamic-slice_bitcast_fusion.7
  23.0 0.2 dynamic-slice_bitcast_fusion.3
  23.3 0.5 fusion.13
  23.8 9.6 %collective-permute-done.7 = bf16[384,640]{1,0:T(8,128)(2,1)S(1)} collective-permute-done((bf16[384,640]{1,0:T(8,128)(2,1)S(1)}, bf16[384,640]{1,0:T(8,128)(2,1)S(1)}, u32[]{:S(2)}, u32[]{:S(2)}) %collective-permute-start.7) | collective-permute-done | bytes 491552 | tf_op jit(solution)/shard_map/ppermute | solution.py:78
  33.6 0.5 multiply_convert_fusion.1
  34.1 0.4 convolution_convert_fusion.6
  34.5 0.6 collective-permute-start.2
  35.0 1.6 %collective-permute-done.2 = bf16[128,1280]{1,0:T(8,128)(2,1)S(1)} collective-permute-done((bf16[128,1280]{1,0:T(8,128)(2,1)S(1)}, bf16[128,1280]{1,0:T(8,128)(2,1)S(1)}, u32[]{:S(2)}, u32[]{:S(2)}) %collective-permute-start.2) | collective-permute-done | bytes 327712 | tf_op jit(solution)/shard_map/ppermute | solution.py:95
  36.6 0.3 convert_add_fusion.3
  37.0 0.1 pad_maximum_fusion.2
  37.1 0.1 fusion.16
  37.3 0.5 fusion.17
  37.8 0.7 %fusion.1 = bf16[128,512]{1,0:T(8,128)(2,1)S(1)} fusion(bf16[128,2560]{1,0:T(8,128)(2,1)S(1)} %get-tuple-element.8, f32[128,512]{1,0:T(8,128)S(1)} %fusion.17, bf16[640,512]{1,0:T(8,128)(2,1)S(1)} %get-tuple-element.17, bf16[640,512]{1,0:T(8,128)(2,1)S(1)} %get-tuple-element.18, bf16[640,512]{1,0:T(8,128)(2,1)S(1)} %get-tuple-element.16, ...), kind=kOutput, calls=%fused_computation.17 | convolution fusion | flops 346423296 | bytes 3670016 | tf_op jit(solution)/shard_map/dot_general | solution.py:90
  38.5 0.3 convolution_convert_fusion.4
  38.9 0.2 collective-permute-start.9
  39.1 1.5 %collective-permute-done.9 = bf16[128,1280]{1,0:T(8,128)(2,1)S(1)} collective-permute-done((bf16[128,1280]{1,0:T(8,128)(2,1)S(1)}, bf16[128,1280]{1,0:T(8,128)(2,1)S(1)}, u32[]{:S(2)}, u32[]{:S(2)}) %collective-permute-start.9) | collective-permute-done | bytes 327712 | tf_op jit(solution)/shard_map/ppermute | solution.py:95
  40.6 0.3 convert_add_fusion.2
  40.9 0.5 fusion.18
  41.4 0.7 %fusion.2 = bf16[128,512]{1,0:T(8,128)(2,1)S(1)} fusion(bf16[128,2560]{1,0:T(8,128)(2,1)S(1)} %get-tuple-element.9, f32[128,512]{1,0:T(8,128)S(1)} %fusion.18, bf16[640,512]{1,0:T(8,128)(2,1)S(1)} %get-tuple-element.17, bf16[640,512]{1,0:T(8,128)(2,1)S(1)} %get-tuple-element.18, bf16[640,512]{1,0:T(8,128)(2,1)S(1)} %get-tuple-element.16, ...), kind=kOutput, calls=%fused_computation.18 | convolution fusion | flops 346423296 | bytes 3670016 | tf_op jit(solution)/shard_map/dot_general | solution.py:90
  42.2 0.3 convolution_convert_fusion.2
  42.5 0.2 collective-permute-start.12
  42.7 0.7 slice.85
  43.4 1.5 %collective-permute-start.10 = (bf16[128,640]{1,0:T(8,128)(2,1)}, bf16[128,640]{1,0:T(8,128)(2,1)S(1)}, u32[]{:S(2)}, u32[]{:S(2)}) collective-permute-start(bf16[128,640]{1,0:T(8,128)(2,1)} %slice.85), channel_id=1, source_target_pairs={{0,2},{1,3},{2,0},{3,1},{4,6},{5,7},{6,4},{7,5},{8,10},{9,11},{10,... | collective-permute-start | bytes 491528 | tf_op jit(solution)/shard_map/ppermute | solution.py:97
  44.9 0.3 convert_add_fusion.1
  45.3 0.5 fusion.19
  45.8 0.7 %fusion.3 = bf16[128,512]{1,0:T(8,128)(2,1)S(1)} fusion(bf16[128,2560]{1,0:T(8,128)(2,1)S(1)} %get-tuple-element.10, f32[128,512]{1,0:T(8,128)S(1)} %fusion.19, bf16[640,512]{1,0:T(8,128)(2,1)S(1)} %get-tuple-element.17, bf16[640,512]{1,0:T(8,128)(2,1)S(1)} %get-tuple-element.18, bf16[640,512]{1,0:T(8,128)(2,1)S(1)} %get-tuple-element.16, ...), kind=kOutput, calls=%fused_computation.19 | convolution fusion | flops 346423296 | bytes 3670016 | tf_op jit(solution)/shard_map/dot_general | solution.py:90
  46.6 1.1 %convolution_convert_fusion = bf16[128,1280]{1,0:T(8,128)(2,1)} fusion(bf16[128,512]{1,0:T(8,128)(2,1)S(1)} %fusion.3, bf16[512,640]{1,0:T(8,128)(2,1)S(1)} %get-tuple-element.13, bf16[512,640]{1,0:T(8,128)(2,1)S(1)} %get-tuple-element.14), kind=kOutput, calls=%fused_computation.2 | convolution fusion | flops 170557440 | bytes 1769472 | tf_op jit(solution)/shard_map/dot_general | solution.py:93
  47.8 0.9 %collective-permute-start.3 = (bf16[128,640]{1,0:T(8,128)(2,1)S(1)}, bf16[128,640]{1,0:T(8,128)(2,1)S(1)}, u32[]{:S(2)}, u32[]{:S(2)}) collective-permute-start(bf16[128,640]{1,0:T(8,128)(2,1)S(1)} %slice.86), channel_id=1, source_target_pairs={{0,2},{1,3},{2,0},{3,1},{4,6},{5,7},{6,4},{7,5},{8,10},{9,11},{10,... | collective-permute-start | bytes 491528 | tf_op jit(solution)/shard_map/ppermute | solution.py:97
  48.7 1.4 %collective-permute-done.10 = bf16[128,640]{1,0:T(8,128)(2,1)S(1)} collective-permute-done((bf16[128,640]{1,0:T(8,128)(2,1)}, bf16[128,640]{1,0:T(8,128)(2,1)S(1)}, u32[]{:S(2)}, u32[]{:S(2)}) %collective-permute-start.10) | collective-permute-done | bytes 163872 | tf_op jit(solution)/shard_map/ppermute | solution.py:97
  50.3 1.6 %collective-permute-start.13 = (bf16[128,640]{1,0:T(8,128)(2,1)S(1)}, bf16[128,640]{1,0:T(8,128)(2,1)S(1)}, u32[]{:S(2)}, u32[]{:S(2)}) collective-permute-start(bf16[128,640]{1,0:T(8,128)(2,1)S(1)} %slice.84), channel_id=1, source_target_pairs={{0,2},{1,3},{2,0},{3,1},{4,6},{5,7},{6,4},{7,5},{8,10},{9,11},{10,... | collective-permute-start | bytes 491528 | tf_op jit(solution)/shard_map/ppermute | solution.py:97
  51.8 1.4 %convert_add_fusion = f32[128,1280]{1,0:T(8,128)S(1)} fusion(bf16[128,1280]{1,0:T(8,128)(2,1)} %collective-permute-done.15, bf16[128,512]{1,0:T(8,128)(2,1)} %copy-done.3, bf16[512,640]{1,0:T(8,128)(2,1)S(1)} %get-tuple-element.12, bf16[512,640]{1,0:T(8,128)(2,1)S(1)} %get-tuple-element.11), kind=kOutput, calls=%fused_computation.22 | convolution fusion | flops 171048960 | bytes 2424832 | tf_op jit(solution)/shard_map/dot_general | solution.py:92
  53.3 0.6 collective-permute-start.16
  53.9 4.5 %collective-permute-done.13 = bf16[128,640]{1,0:T(8,128)(2,1)S(1)} collective-permute-done((bf16[128,640]{1,0:T(8,128)(2,1)S(1)}, bf16[128,640]{1,0:T(8,128)(2,1)S(1)}, u32[]{:S(2)}, u32[]{:S(2)}) %collective-permute-start.13) | collective-permute-done | bytes 163872 | tf_op jit(solution)/shard_map/ppermute | solution.py:97
  58.4 2.6 %collective-permute-start.14 = (bf16[128,640]{1,0:T(8,128)(2,1)S(1)}, bf16[128,640]{1,0:T(8,128)(2,1)S(1)}, u32[]{:S(2)}, u32[]{:S(2)}) collective-permute-start(bf16[128,640]{1,0:T(8,128)(2,1)S(1)} %fusion.5), channel_id=1, source_target_pairs={{0,12},{4,8},{8,4},{12,0},{1,13},{5,9},{9,5},{13,1},{2,14},{6,10},... | collective-permute-start | bytes 491528 | tf_op jit(solution)/shard_map/ppermute | solution.py:102
  61.0 0.4 collective-permute-done.16
  61.4 1.0 %collective-permute-start.17 = (bf16[128,640]{1,0:T(8,128)(2,1)S(1)}, bf16[128,640]{1,0:T(8,128)(2,1)S(1)}, u32[]{:S(2)}, u32[]{:S(2)}) collective-permute-start(bf16[128,640]{1,0:T(8,128)(2,1)S(1)} %fusion.4), channel_id=1, source_target_pairs={{0,4},{4,0},{8,12},{12,8},{1,5},{5,1},{9,13},{13,9},{2,6},{6,2},{1... | collective-permute-start | bytes 491528 | tf_op jit(solution)/shard_map/ppermute | solution.py:102
  62.5 4.2 %collective-permute-done.14 = bf16[128,640]{1,0:T(8,128)(2,1)S(1)} collective-permute-done((bf16[128,640]{1,0:T(8,128)(2,1)S(1)}, bf16[128,640]{1,0:T(8,128)(2,1)S(1)}, u32[]{:S(2)}, u32[]{:S(2)}) %collective-permute-start.14) | collective-permute-done | bytes 163872 | tf_op jit(solution)/shard_map/ppermute | solution.py:102
  66.6 2.5 %collective-permute-done.17 = bf16[128,640]{1,0:T(8,128)(2,1)S(1)} collective-permute-done((bf16[128,640]{1,0:T(8,128)(2,1)S(1)}, bf16[128,640]{1,0:T(8,128)(2,1)S(1)}, u32[]{:S(2)}, u32[]{:S(2)}) %collective-permute-start.17) | collective-permute-done | bytes 163872 | tf_op jit(solution)/shard_map/ppermute | solution.py:102
  69.1 0.9 %fusion.11 = bf16[128,640]{1,0:T(8,128)(2,1)} fusion(f32[128,1280]{1,0:T(8,128)S(1)} %convert_add_fusion.3, bf16[128,640]{1,0:T(8,128)(2,1)S(1)} %collective-permute-done.17, bf16[128,640]{1,0:T(8,128)(2,1)S(1)} %collective-permute-done.14, bf16[128,640]{1,0:T(8,128)(2,1)S(1)} %collective-permute-done.11, bf16[128,640]{1,0:T(8,128)(2,1)S(1)} %collective-permute-done.3, ...), kind=kLoop, calls=%fused_computation.53 | loop fusion | flops 1064960 | bytes 1147392 | tf_op jit(solution)/shard_map/convert_element_type | solution.py:106
  (33 shorter events, 0.8 us)
Async XLA Ops:
  1.0 20.2 %collective-permute-start.6 = (bf16[128,640]{1,0:T(8,128)(2,1)S(1)}, bf16[128,640]{1,0:T(8,128)(2,1)S(1)}, u32[]{:S(2)}, u32[]{:S(2)}) collective-permute-start(bf16[128,640]{1,0:T(8,128)(2,1)S(1)} %multiply_convert_fusion), channel_id=1, source_target_pairs={{0,4},{4,0},{8,12},{12,8},{1,5},{5,1},{9,13},{13,9},{2,6},{6,2},{1... | collective-permute-start | bytes 491528 | tf_op jit(solution)/shard_map/ppermute | solution.py:66
  4.1 17.1 %collective-permute-start.5 = (bf16[128,640]{1,0:T(8,128)(2,1)S(1)}, bf16[128,640]{1,0:T(8,128)(2,1)S(1)}, u32[]{:S(2)}, u32[]{:S(2)}) collective-permute-start(bf16[128,640]{1,0:T(8,128)(2,1)S(1)} %multiply_convert_fusion), channel_id=1, source_target_pairs={{0,12},{4,8},{8,4},{12,0},{1,13},{5,9},{9,5},{13,1},{2,14},{6,10},... | collective-permute-start | bytes 491528 | tf_op jit(solution)/shard_map/ppermute | solution.py:66
  6.6 14.6 %collective-permute-start.4 = (bf16[128,640]{1,0:T(8,128)(2,1)S(1)}, bf16[128,640]{1,0:T(8,128)(2,1)S(1)}, u32[]{:S(2)}, u32[]{:S(2)}) collective-permute-start(bf16[128,640]{1,0:T(8,128)(2,1)S(1)} %multiply_convert_fusion), channel_id=1, source_target_pairs={{0,8},{4,12},{8,0},{12,4},{1,9},{5,13},{9,1},{13,5},{2,10},{6,14},... | collective-permute-start | bytes 491528 | tf_op jit(solution)/shard_map/ppermute | solution.py:66
  6.7 5.4 %collective-permute-start = (bf16[128,640]{1,0:T(8,128)(2,1)S(1)}, bf16[128,640]{1,0:T(8,128)(2,1)S(1)}, u32[]{:S(2)}, u32[]{:S(2)}) collective-permute-start(bf16[128,640]{1,0:T(8,128)(2,1)S(1)} %multiply_convert_fusion), channel_id=1, source_target_pairs={{0,2},{1,3},{2,0},{3,1},{4,6},{5,7},{6,4},{7,5},{8,10},{9,11},{10,... | collective-permute-start | bytes 491528 | tf_op jit(solution)/shard_map/ppermute | solution.py:78
  10.0 12.8 %copy-start = (bf16[1,2560,512]{2,1,0:T(8,128)(2,1)S(1)}, bf16[1,2560,512]{2,1,0:T(8,128)(2,1)}, u32[]{:S(2)}) copy-start(bf16[1,2560,512]{2,1,0:T(8,128)(2,1)} %param.10) | copy-start | bytes 7864324
  12.1 11.1 %collective-permute-start.1 = (bf16[128,1280]{1,0:T(8,128)(2,1)S(1)}, bf16[128,1280]{1,0:T(8,128)(2,1)S(1)}, u32[]{:S(2)}, u32[]{:S(2)}) collective-permute-start(bf16[128,1280]{1,0:T(8,128)(2,1)S(1)} %pad_maximum_fusion.7), channel_id=1, source_target_pairs={{0,1},{1,0},{2,3},{3,2},{4,5},{5,4},{6,7},{7,6},{8,9},{9,8},{10,11... | collective-permute-start | bytes 983048 | tf_op jit(solution)/shard_map/ppermute | solution.py:80
  21.2 1.7 %copy-start.1 = (bf16[1,512,2560]{2,1,0:T(8,128)(2,1)S(1)}, bf16[1,512,2560]{2,1,0:T(8,128)(2,1)}, u32[]{:S(2)}) copy-start(bf16[1,512,2560]{2,1,0:T(8,128)(2,1)} %param.11) | copy-start | bytes 7864324
  21.3 12.2 %collective-permute-start.7 = (bf16[384,640]{1,0:T(8,128)(2,1)S(1)}, bf16[384,640]{1,0:T(8,128)(2,1)S(1)}, u32[]{:S(2)}, u32[]{:S(2)}) collective-permute-start(bf16[384,640]{1,0:T(8,128)(2,1)S(1)} %constant_dynamic-update-slice_fusion), channel_id=1, source_target_pairs={{0,2},{1,3},{2,0},{3,1},{4,6},{5,7},{6,4},{7,5},{8,10},{9,11},{10,... | collective-permute-start | bytes 1474568 | tf_op jit(solution)/shard_map/ppermute | solution.py:78
  33.5 3.5 %collective-permute-start.8 = (bf16[384,1280]{1,0:T(8,128)(2,1)S(1)}, bf16[384,1280]{1,0:T(8,128)(2,1)S(1)}, u32[]{:S(2)}, u32[]{:S(2)}) collective-permute-start(bf16[384,1280]{1,0:T(8,128)(2,1)S(1)} %pad_maximum_fusion.5), channel_id=1, source_target_pairs={{0,1},{1,0},{2,3},{3,2},{4,5},{5,4},{6,7},{7,6},{8,9},{9,8},{10,11... | collective-permute-start | bytes 2949128 | tf_op jit(solution)/shard_map/ppermute | solution.py:80
  34.5 2.1 %collective-permute-start.2 = (bf16[128,1280]{1,0:T(8,128)(2,1)S(1)}, bf16[128,1280]{1,0:T(8,128)(2,1)S(1)}, u32[]{:S(2)}, u32[]{:S(2)}) collective-permute-start(bf16[128,1280]{1,0:T(8,128)(2,1)S(1)} %convolution_convert_fusion.6), channel_id=1, source_target_pairs={{0,1},{1,0},{2,3},{3,2},{4,5},{5,4},{6,7},{7,6},{8,9},{9,8},{10,11... | collective-permute-start | bytes 983048 | tf_op jit(solution)/shard_map/ppermute | solution.py:95
  38.9 1.7 %collective-permute-start.9 = (bf16[128,1280]{1,0:T(8,128)(2,1)S(1)}, bf16[128,1280]{1,0:T(8,128)(2,1)S(1)}, u32[]{:S(2)}, u32[]{:S(2)}) collective-permute-start(bf16[128,1280]{1,0:T(8,128)(2,1)S(1)} %convolution_convert_fusion.4), channel_id=1, source_target_pairs={{0,1},{1,0},{2,3},{3,2},{4,5},{5,4},{6,7},{7,6},{8,9},{9,8},{10,11... | collective-permute-start | bytes 983048 | tf_op jit(solution)/shard_map/ppermute | solution.py:95
  42.5 2.4 %collective-permute-start.12 = (bf16[128,1280]{1,0:T(8,128)(2,1)S(1)}, bf16[128,1280]{1,0:T(8,128)(2,1)S(1)}, u32[]{:S(2)}, u32[]{:S(2)}) collective-permute-start(bf16[128,1280]{1,0:T(8,128)(2,1)S(1)} %convolution_convert_fusion.2), channel_id=1, source_target_pairs={{0,1},{1,0},{2,3},{3,2},{4,5},{5,4},{6,7},{7,6},{8,9},{9,8},{10,11... | collective-permute-start | bytes 983048 | tf_op jit(solution)/shard_map/ppermute | solution.py:95
  43.4 6.7 %collective-permute-start.10 = (bf16[128,640]{1,0:T(8,128)(2,1)}, bf16[128,640]{1,0:T(8,128)(2,1)S(1)}, u32[]{:S(2)}, u32[]{:S(2)}) collective-permute-start(bf16[128,640]{1,0:T(8,128)(2,1)} %slice.85), channel_id=1, source_target_pairs={{0,2},{1,3},{2,0},{3,1},{4,6},{5,7},{6,4},{7,5},{8,10},{9,11},{10,... | collective-permute-start | bytes 491528 | tf_op jit(solution)/shard_map/ppermute | solution.py:97
  46.5 1.1 %copy-start.3 = (bf16[128,512]{1,0:T(8,128)(2,1)}, bf16[128,512]{1,0:T(8,128)(2,1)S(1)}, u32[]{:S(2)}) copy-start(bf16[128,512]{1,0:T(8,128)(2,1)S(1)} %fusion.3) | copy-start | bytes 393220
  47.6 4.2 %collective-permute-start.15 = (bf16[128,1280]{1,0:T(8,128)(2,1)}, bf16[128,1280]{1,0:T(8,128)(2,1)}, u32[]{:S(2)}, u32[]{:S(2)}) collective-permute-start(bf16[128,1280]{1,0:T(8,128)(2,1)} %convolution_convert_fusion), channel_id=1, source_target_pairs={{0,1},{1,0},{2,3},{3,2},{4,5},{5,4},{6,7},{7,6},{8,9},{9,8},{10,11... | collective-permute-start | bytes 983048 | tf_op jit(solution)/shard_map/ppermute | solution.py:95
  47.8 14.7 %copy-start.2 = (s32[128,1]{0,1:T(1,128)S(1)}, s32[128,1]{0,1:T(1,128)}, u32[]{:S(2)}) copy-start(s32[128,1]{0,1:T(1,128)} %param.8) | copy-start | bytes 1540
  47.8 14.7 %collective-permute-start.3 = (bf16[128,640]{1,0:T(8,128)(2,1)S(1)}, bf16[128,640]{1,0:T(8,128)(2,1)S(1)}, u32[]{:S(2)}, u32[]{:S(2)}) collective-permute-start(bf16[128,640]{1,0:T(8,128)(2,1)S(1)} %slice.86), channel_id=1, source_target_pairs={{0,2},{1,3},{2,0},{3,1},{4,6},{5,7},{6,4},{7,5},{8,10},{9,11},{10,... | collective-permute-start | bytes 491528 | tf_op jit(solution)/shard_map/ppermute | solution.py:97
  50.2 12.3 %collective-permute-start.11 = (bf16[128,640]{1,0:T(8,128)(2,1)S(1)}, bf16[128,640]{1,0:T(8,128)(2,1)S(1)}, u32[]{:S(2)}, u32[]{:S(2)}) collective-permute-start(bf16[128,640]{1,0:T(8,128)(2,1)S(1)} %fusion.6), channel_id=1, source_target_pairs={{0,8},{4,12},{8,0},{12,4},{1,9},{5,13},{9,1},{13,5},{2,10},{6,14},... | collective-permute-start | bytes 491528 | tf_op jit(solution)/shard_map/ppermute | solution.py:102
  50.3 8.1 %collective-permute-start.13 = (bf16[128,640]{1,0:T(8,128)(2,1)S(1)}, bf16[128,640]{1,0:T(8,128)(2,1)S(1)}, u32[]{:S(2)}, u32[]{:S(2)}) collective-permute-start(bf16[128,640]{1,0:T(8,128)(2,1)S(1)} %slice.84), channel_id=1, source_target_pairs={{0,2},{1,3},{2,0},{3,1},{4,6},{5,7},{6,4},{7,5},{8,10},{9,11},{10,... | collective-permute-start | bytes 491528 | tf_op jit(solution)/shard_map/ppermute | solution.py:97
  53.3 8.1 %collective-permute-start.16 = (bf16[128,640]{1,0:T(8,128)(2,1)S(1)}, bf16[128,640]{1,0:T(8,128)(2,1)S(1)}, u32[]{:S(2)}, u32[]{:S(2)}) collective-permute-start(bf16[128,640]{1,0:T(8,128)(2,1)S(1)} %slice.83), channel_id=1, source_target_pairs={{0,2},{1,3},{2,0},{3,1},{4,6},{5,7},{6,4},{7,5},{8,10},{9,11},{10,... | collective-permute-start | bytes 491528 | tf_op jit(solution)/shard_map/ppermute | solution.py:97
  58.4 8.2 %collective-permute-start.14 = (bf16[128,640]{1,0:T(8,128)(2,1)S(1)}, bf16[128,640]{1,0:T(8,128)(2,1)S(1)}, u32[]{:S(2)}, u32[]{:S(2)}) collective-permute-start(bf16[128,640]{1,0:T(8,128)(2,1)S(1)} %fusion.5), channel_id=1, source_target_pairs={{0,12},{4,8},{8,4},{12,0},{1,13},{5,9},{9,5},{13,1},{2,14},{6,10},... | collective-permute-start | bytes 491528 | tf_op jit(solution)/shard_map/ppermute | solution.py:102
  61.4 7.7 %collective-permute-start.17 = (bf16[128,640]{1,0:T(8,128)(2,1)S(1)}, bf16[128,640]{1,0:T(8,128)(2,1)S(1)}, u32[]{:S(2)}, u32[]{:S(2)}) collective-permute-start(bf16[128,640]{1,0:T(8,128)(2,1)S(1)} %fusion.4), channel_id=1, source_target_pairs={{0,4},{4,0},{8,12},{12,8},{1,5},{5,1},{9,13},{13,9},{2,6},{6,2},{1... | collective-permute-start | bytes 491528 | tf_op jit(solution)/shard_map/ppermute | solution.py:102

commit v18 on v10

--- a/solution.py
+++ b/solution.py
@@ -70,7 +70,7 @@
     up_w = _slots(up_weight[0], t, width, 0)
     down_keep = _slots(down_weight[0], t, width, 1, _ORDER[:2])
     down_send = _slots(down_weight[0], t, width, 1, _ORDER[2:])
-    waves = [[k] for k in [0] + list(range(2, n_expert)) + [1][:n_expert - 1]]
+    waves = [[k] for k in list(range(2, n_expert)) + [1][:n_expert - 1] + [0]]
     total = None
     previous = None
     for wave in waves:

time: 67 us -> 64.5 us (0.963)
  waiting for transfers between devices: 28.5 us -> 18.2 us
  other arithmetic: 2.46 us -> 8.86 us
  matrix products: 9.28 us -> 7.73 us
  local copies, waits for them, and re-layouts: 5.18 us -> 6.68 us
  starting transfers between devices: 21.1 us -> 22.3 us
    ppermute x4, waiting for transfers between devices: 9.45 us -> 5.23 us  [gathered(): lax.ppermute(piece, 'tensor', _xor_pairs(n_tensor, 2))]
    concatenate x4, other arithmetic: 0.1 us -> 3.76 us  [gathered(): jnp.concatenate([piece, lax.ppermute(piece, 'tensor', _xor_pairs(n_tensor...]
    concatenate x3, other arithmetic: 0.14 us -> 2.89 us  [gathered(): jnp.concatenate([pair, lax.ppermute(pair, 'tensor', _xor_pairs(n_tensor,...]
    ppermute x3, waiting for transfers between devices: 5.9 us -> 3.32 us  [gathered(): lax.ppermute(scaled, 'expert', _xor_pairs(n_expert, k))]
    ppermute x4, waiting for transfers between devices: 2.47 us -> 0.29 us  [gathered(): lax.ppermute(send, 'tensor', _xor_pairs(n_tensor, 1)).astype(jnp.float32)]
    ppermute x3, starting transfers between devices: 4.17 us -> 5.68 us  [gathered(): lax.ppermute(scaled, 'expert', _xor_pairs(n_expert, k))]
    ppermute x3, waiting for transfers between devices: 5.58 us -> 4.15 us  [gathered(): lax.ppermute(part.astype(jnp.bfloat16), 'expert', _xor_pairs(n_expert, k))]
    dynamic_slice x3, local copies, waits for them, and re-layouts: 2.4 us -> 3.54 us  [_slots(): lax.dynamic_slice_in_dim(weight, (t ^ k) * width, width, axis=axis)]
  transfers between devices with their start and end apart: 22 -> 22, of which waited for: 12 -> 9; matrix products, arithmetic and copies ran while one was open for 19% -> 30% of each run, Pallas kernels for 0% -> 0%
where the time goes in v18:
time: 64.5 us; the launch traced here: 64.1 us
  starting transfers between devices  22.3 us (35%)
  waiting for transfers between devices  18.2 us (28%)
  other arithmetic  8.86 us (14%)
  matrix products  7.73 us (12%)
  local copies, waits for them, and re-layouts  6.68 us (10%)
    ppermute x3, starting transfers between devices, gathered(): lax.ppermute(scaled, 'expert', _xor_pairs(n_expert, k))  5.68 us
    ppermute x4, starting transfers between devices, gathered(): lax.ppermute(piece, 'tensor', _xor_pairs(n_tensor, 2))  5.42 us
    ppermute x4, waiting for transfers between devices, gathered(): lax.ppermute(piece, 'tensor', _xor_pairs(n_tensor, 2))  5.23 us
    ppermute x4, waiting for transfers between devices, gathered(): lax.ppermute(over_c[:, width:].astype(jnp.bfloat16), 'tensor', _xor_pairs...  5.21 us
    ppermute x4, starting transfers between devices, gathered(): lax.ppermute(over_c[:, width:].astype(jnp.bfloat16), 'tensor', _xor_pairs...  4.92 us
    ppermute x3, starting transfers between devices, gathered(): lax.ppermute(part.astype(jnp.bfloat16), 'expert', _xor_pairs(n_expert, k))  4.8 us
    ppermute x3, waiting for transfers between devices, gathered(): lax.ppermute(part.astype(jnp.bfloat16), 'expert', _xor_pairs(n_expert, k))  4.15 us
    concatenate x4, other arithmetic, gathered(): jnp.concatenate([piece, lax.ppermute(piece, 'tensor', _xor_pairs(n_tensor...  3.76 us
  transfers between devices with their start and end apart: 22, of which 9 were waited for; matrix products, arithmetic and copies ran while one was open for 30% of the time, Pallas kernels for 0%

profile of v18, /device:TPU:0, one launch (start us, length us, event | category | flops | bytes accessed | tf_op | source)
XLA Modules:
  0.0 64.1 jit_solution(1295415893284319055)
XLA Ops:
  0.0 1.0 %multiply_convert_fusion = bf16[128,640]{1,0:T(8,128)(2,1)S(1)} fusion(bf16[128,640]{1,0:T(8,128)(2,1)} %param.6, f32[128]{0:T(128)} %param.7), kind=kLoop, calls=%fused_computation.56 | loop fusion | flops 245760 | bytes 328192 | tf_op jit(solution)/shard_map/convert_element_type | solution.py:64
  1.0 4.1 %collective-permute-start = (bf16[128,640]{1,0:T(8,128)(2,1)S(1)}, bf16[128,640]{1,0:T(8,128)(2,1)}, u32[]{:S(2)}, u32[]{:S(2)}) collective-permute-start(bf16[128,640]{1,0:T(8,128)(2,1)S(1)} %multiply_convert_fusion), channel_id=1, source_target_pairs={{0,8},{4,12},{8,0},{12,4},{1,9},{5,13},{9,1},{13,5},{2,10},{6,14},... | collective-permute-start | bytes 491528 | tf_op jit(solution)/shard_map/ppermute | solution.py:66
  5.1 1.3 %collective-permute-start.6 = (bf16[128,640]{1,0:T(8,128)(2,1)S(1)}, bf16[128,640]{1,0:T(8,128)(2,1)}, u32[]{:S(2)}, u32[]{:S(2)}) collective-permute-start(bf16[128,640]{1,0:T(8,128)(2,1)S(1)} %multiply_convert_fusion), channel_id=1, source_target_pairs={{0,12},{4,8},{8,4},{12,0},{1,13},{5,9},{9,5},{13,1},{2,14},{6,10},... | collective-permute-start | bytes 491528 | tf_op jit(solution)/shard_map/ppermute | solution.py:66
  6.7 1.5 %collective-permute-start.18 = (bf16[128,640]{1,0:T(8,128)(2,1)S(1)}, bf16[128,640]{1,0:T(8,128)(2,1)}, u32[]{:S(2)}, u32[]{:S(2)}) collective-permute-start(bf16[128,640]{1,0:T(8,128)(2,1)S(1)} %multiply_convert_fusion), channel_id=1, source_target_pairs={{0,2},{1,3},{2,0},{3,1},{4,6},{5,7},{6,4},{7,5},{8,10},{9,11},{10,... | collective-permute-start | bytes 491528 | tf_op jit(solution)/shard_map/ppermute | solution.py:79
  8.2 2.0 %dynamic-slice_bitcast_fusion.11 = (bf16[640,512]{1,0:T(8,128)(2,1)S(1)}, bf16[640,512]{1,0:T(8,128)(2,1)S(1)}, bf16[640,512]{1,0:T(8,128)(2,1)S(1)}, bf16[640,512]{1,0:T(8,128)(2,1)S(1)}) fusion(bf16[1,2560,512]{2,1,0:T(8,128)(2,1)} %param.9, s32[]{:T(128)S(6)} %select_n.48, s32[]{:T(128)S(6)} %select_n.49, s32[]{:T(128)S(6)} %select_n.51, s32[]{:T(128)S(6)} %select_n.50), kind=kLoop, calls=%fused_computation.37 | loop fusion | bytes 5242896 | tf_op jit(solution)/shard_map/dynamic_slice | solution.py:55
  10.2 0.5 copy-done
  10.7 1.3 %dynamic-slice_bitcast_fusion.7 = (bf16[640,512]{1,0:T(8,128)(2,1)S(1)}, bf16[640,512]{1,0:T(8,128)(2,1)}, bf16[640,512]{1,0:T(8,128)(2,1)}, bf16[640,512]{1,0:T(8,128)(2,1)}) fusion(bf16[1,2560,512]{2,1,0:T(8,128)(2,1)S(1)} %copy-done, s32[]{:T(128)S(6)} %select_n.48, s32[]{:T(128)S(6)} %select_n.49, s32[]{:T(128)S(6)} %select_n.51, s32[]{:T(128)S(6)} %select_n.50), kind=kLoop, calls=%fused_computation.33 | loop fusion | bytes 5242896 | tf_op jit(solution)/shard_map/dynamic_slice | solution.py:55
  12.2 1.5 %copy-done.1 = bf16[1,512,2560]{2,1,0:T(8,128)(2,1)S(1)} copy-done((bf16[1,512,2560]{2,1,0:T(8,128)(2,1)S(1)}, bf16[1,512,2560]{2,1,0:T(8,128)(2,1)}, u32[]{:S(2)}) %copy-start.1) | copy-done | bytes 2621464
  14.0 3.3 %collective-permute-done = bf16[128,640]{1,0:T(8,128)(2,1)} collective-permute-done((bf16[128,640]{1,0:T(8,128)(2,1)S(1)}, bf16[128,640]{1,0:T(8,128)(2,1)}, u32[]{:S(2)}, u32[]{:S(2)}) %collective-permute-start) | collective-permute-done | bytes 163872 | tf_op jit(solution)/shard_map/ppermute | solution.py:66
  17.3 1.8 %collective-permute-start.1 = (bf16[128,640]{1,0:T(8,128)(2,1)}, bf16[128,640]{1,0:T(8,128)(2,1)S(1)}, u32[]{:S(2)}, u32[]{:S(2)}) collective-permute-start(bf16[128,640]{1,0:T(8,128)(2,1)} %collective-permute-done), channel_id=1, source_target_pairs={{0,2},{1,3},{2,0},{3,1},{4,6},{5,7},{6,4},{7,5},{8,10},{9,11},{10,... | collective-permute-start | bytes 491528 | tf_op jit(solution)/shard_map/ppermute | solution.py:79
  19.2 0.9 %pad_maximum_fusion.10 = bf16[128,1280]{1,0:T(8,128)(2,1)S(1)} fusion(bf16[128,640]{1,0:T(8,128)(2,1)} %collective-permute-done.18, bf16[128,640]{1,0:T(8,128)(2,1)S(1)} %multiply_convert_fusion), kind=kLoop, calls=%fused_computation.55 | loop fusion | flops 655360 | bytes 655360 | tf_op jit(solution)/shard_map/concatenate | solution.py:78
  20.5 1.8 %collective-permute-start.13 = (bf16[128,640]{1,0:T(8,128)(2,1)}, bf16[128,640]{1,0:T(8,128)(2,1)S(1)}, u32[]{:S(2)}, u32[]{:S(2)}) collective-permute-start(bf16[128,640]{1,0:T(8,128)(2,1)} %collective-permute-done.12), channel_id=1, source_target_pairs={{0,2},{1,3},{2,0},{3,1},{4,6},{5,7},{6,4},{7,5},{8,10},{9,11},{10,... | collective-permute-start | bytes 491528 | tf_op jit(solution)/shard_map/ppermute | solution.py:79
  22.3 0.9 %constant_dynamic-update-slice_fusion.2 = bf16[128,2560]{1,0:T(8,128)(2,1)S(1)} fusion(bf16[128,640]{1,0:T(8,128)(2,1)} %collective-permute-done), kind=kLoop, calls=%fused_computation.60 | loop fusion | bytes 327680
  23.2 0.9 %pad_maximum_fusion.7 = bf16[128,1280]{1,0:T(8,128)(2,1)S(1)} fusion(bf16[128,640]{1,0:T(8,128)(2,1)S(1)} %collective-permute-done.1, bf16[128,640]{1,0:T(8,128)(2,1)} %collective-permute-done), kind=kLoop, calls=%fused_computation.52 | loop fusion | flops 655360 | bytes 655360 | tf_op jit(solution)/shard_map/concatenate | solution.py:78
  24.3 3.2 %collective-permute-done.7 = bf16[128,640]{1,0:T(8,128)(2,1)S(1)} collective-permute-done((bf16[128,640]{1,0:T(8,128)(2,1)}, bf16[128,640]{1,0:T(8,128)(2,1)S(1)}, u32[]{:S(2)}, u32[]{:S(2)}) %collective-permute-start.7) | collective-permute-done | bytes 163872 | tf_op jit(solution)/shard_map/ppermute | solution.py:79
  27.5 0.9 %pad_maximum_fusion.8 = bf16[128,1280]{1,0:T(8,128)(2,1)S(1)} fusion(bf16[128,640]{1,0:T(8,128)(2,1)S(1)} %collective-permute-done.7, bf16[128,640]{1,0:T(8,128)(2,1)} %collective-permute-done.6), kind=kLoop, calls=%fused_computation.53 | loop fusion | flops 655360 | bytes 655360 | tf_op jit(solution)/shard_map/concatenate | solution.py:78
  28.5 2.0 %collective-permute-done.13 = bf16[128,640]{1,0:T(8,128)(2,1)S(1)} collective-permute-done((bf16[128,640]{1,0:T(8,128)(2,1)}, bf16[128,640]{1,0:T(8,128)(2,1)S(1)}, u32[]{:S(2)}, u32[]{:S(2)}) %collective-permute-start.13) | collective-permute-done | bytes 163872 | tf_op jit(solution)/shard_map/ppermute | solution.py:79
  30.5 0.9 %pad_maximum_fusion.9 = bf16[128,1280]{1,0:T(8,128)(2,1)S(1)} fusion(bf16[128,640]{1,0:T(8,128)(2,1)S(1)} %collective-permute-done.13, bf16[128,640]{1,0:T(8,128)(2,1)} %collective-permute-done.12), kind=kLoop, calls=%fused_computation.54 | loop fusion | flops 655360 | bytes 655360 | tf_op jit(solution)/shard_map/concatenate | solution.py:78
  31.6 0.5 fusion.11
  32.2 0.7 %multiply_convert_fusion.1 = bf16[128,512]{1,0:T(8,128)(2,1)S(1)} fusion(f32[128,512]{1,0:T(8,128)S(1)} %fusion.11, bf16[128,2560]{1,0:T(8,128)(2,1)S(1)} %constant_dynamic-update-slice_fusion, bf16[640,512]{1,0:T(8,128)(2,1)S(1)} %copy-done.3, bf16[640,512]{1,0:T(8,128)(2,1)S(1)} %copy-done.4, bf16[640,512]{1,0:T(8,128)(2,1)S(1)} %copy-done.2, ...), kind=kOutput, calls=%fused_computation.57 | convolution fusion | flops 346423296 | bytes 3670016 | tf_op jit(solution)/shard_map/dot_general | solution.py:85
  32.9 0.3 convolution_convert_fusion.6
  33.3 0.6 collective-permute-start.3
  33.8 1.0 %pad_maximum_fusion.4 = bf16[128,2560]{1,0:T(8,128)(2,1)S(1)} fusion(bf16[128,1280]{1,0:T(8,128)(2,1)S(1)} %collective-permute-done.8, bf16[128,640]{1,0:T(8,128)(2,1)S(1)} %collective-permute-done.7, bf16[128,640]{1,0:T(8,128)(2,1)} %collective-permute-done.6), kind=kLoop, calls=%fused_computation.19 | loop fusion | flops 1966080 | bytes 1310720 | tf_op jit(solution)/shard_map/concatenate | solution.py:80
  35.4 0.5 fusion.12
  35.9 0.7 %fusion.1 = bf16[128,512]{1,0:T(8,128)(2,1)S(1)} fusion(bf16[128,2560]{1,0:T(8,128)(2,1)S(1)} %pad_maximum_fusion.4, f32[128,512]{1,0:T(8,128)S(1)} %fusion.12, bf16[640,512]{1,0:T(8,128)(2,1)S(1)} %copy-done.3, bf16[640,512]{1,0:T(8,128)(2,1)S(1)} %copy-done.4, bf16[640,512]{1,0:T(8,128)(2,1)S(1)} %copy-done.2, bf16[640,512]{1,0:T(8,128)(2,1)S(1)} %get-tuple-element.15), kind=kOutput, calls=%fused_computation.16 | convolution fusion | flops 346423296 | bytes 3670016 | tf_op jit(solution)/shard_map/dot_general | solution.py:85
  36.7 0.3 convolution_convert_fusion.4
  37.0 0.5 collective-permute-start.9
  37.5 1.0 %pad_maximum_fusion.5 = bf16[128,2560]{1,0:T(8,128)(2,1)S(1)} fusion(bf16[128,1280]{1,0:T(8,128)(2,1)S(1)} %collective-permute-done.14, bf16[128,640]{1,0:T(8,128)(2,1)S(1)} %collective-permute-done.13, bf16[128,640]{1,0:T(8,128)(2,1)} %collective-permute-done.12), kind=kLoop, calls=%fused_computation.20 | loop fusion | flops 1966080 | bytes 1310720 | tf_op jit(solution)/shard_map/concatenate | solution.py:80
  38.5 1.2 %collective-permute-start.4 = (bf16[128,640]{1,0:T(8,128)(2,1)S(1)}, bf16[128,640]{1,0:T(8,128)(2,1)S(1)}, u32[]{:S(2)}, u32[]{:S(2)}) collective-permute-start(bf16[128,640]{1,0:T(8,128)(2,1)S(1)} %slice.67), channel_id=1, source_target_pairs={{0,2},{1,3},{2,0},{3,1},{4,6},{5,7},{6,4},{7,5},{8,10},{9,11},{10,... | collective-permute-start | bytes 491528 | tf_op jit(solution)/shard_map/ppermute | solution.py:92
  39.7 0.3 convert_add_fusion.2
  40.1 0.5 fusion.13
  40.6 0.7 %fusion.2 = bf16[128,512]{1,0:T(8,128)(2,1)S(1)} fusion(bf16[128,2560]{1,0:T(8,128)(2,1)S(1)} %pad_maximum_fusion.5, f32[128,512]{1,0:T(8,128)S(1)} %fusion.13, bf16[640,512]{1,0:T(8,128)(2,1)S(1)} %copy-done.3, bf16[640,512]{1,0:T(8,128)(2,1)S(1)} %copy-done.4, bf16[640,512]{1,0:T(8,128)(2,1)S(1)} %copy-done.2, bf16[640,512]{1,0:T(8,128)(2,1)S(1)} %get-tuple-element.15), kind=kOutput, calls=%fused_computation.17 | convolution fusion | flops 346423296 | bytes 3670016 | tf_op jit(solution)/shard_map/dot_general | solution.py:85
  41.3 0.3 convolution_convert_fusion.2
  41.8 1.0 %pad_maximum_fusion.6 = bf16[128,2560]{1,0:T(8,128)(2,1)S(1)} fusion(bf16[128,1280]{1,0:T(8,128)(2,1)S(1)} %collective-permute-done.19, bf16[128,640]{1,0:T(8,128)(2,1)} %collective-permute-done.18, bf16[128,640]{1,0:T(8,128)(2,1)S(1)} %multiply_convert_fusion), kind=kLoop, calls=%fused_computation.21 | loop fusion | flops 1966080 | bytes 1310720 | tf_op jit(solution)/shard_map/concatenate | solution.py:80
  42.8 2.0 %collective-permute-done.4 = bf16[128,640]{1,0:T(8,128)(2,1)S(1)} collective-permute-done((bf16[128,640]{1,0:T(8,128)(2,1)S(1)}, bf16[128,640]{1,0:T(8,128)(2,1)S(1)}, u32[]{:S(2)}, u32[]{:S(2)}) %collective-permute-start.4) | collective-permute-done | bytes 163872 | tf_op jit(solution)/shard_map/ppermute | solution.py:92
  44.8 2.0 %collective-permute-start.5 = (bf16[128,640]{1,0:T(8,128)(2,1)S(1)}, bf16[128,640]{1,0:T(8,128)(2,1)S(1)}, u32[]{:S(2)}, u32[]{:S(2)}) collective-permute-start(bf16[128,640]{1,0:T(8,128)(2,1)S(1)} %fusion.9), channel_id=1, source_target_pairs={{0,8},{4,12},{8,0},{12,4},{1,9},{5,13},{9,1},{13,5},{2,10},{6,14},... | collective-permute-start | bytes 491528 | tf_op jit(solution)/shard_map/ppermute | solution.py:97
  46.9 1.6 %collective-permute-start.10 = (bf16[128,640]{1,0:T(8,128)(2,1)S(1)}, bf16[128,640]{1,0:T(8,128)(2,1)S(1)}, u32[]{:S(2)}, u32[]{:S(2)}) collective-permute-start(bf16[128,640]{1,0:T(8,128)(2,1)S(1)} %slice.66), channel_id=1, source_target_pairs={{0,2},{1,3},{2,0},{3,1},{4,6},{5,7},{6,4},{7,5},{8,10},{9,11},{10,... | collective-permute-start | bytes 491528 | tf_op jit(solution)/shard_map/ppermute | solution.py:92
  48.8 0.6 collective-permute-start.16
  49.4 0.5 fusion.14
  49.9 0.7 %fusion.3 = bf16[128,512]{1,0:T(8,128)(2,1)S(1)} fusion(bf16[128,2560]{1,0:T(8,128)(2,1)S(1)} %pad_maximum_fusion.6, f32[128,512]{1,0:T(8,128)S(1)} %fusion.14, bf16[640,512]{1,0:T(8,128)(2,1)S(1)} %copy-done.3, bf16[640,512]{1,0:T(8,128)(2,1)S(1)} %copy-done.4, bf16[640,512]{1,0:T(8,128)(2,1)S(1)} %copy-done.2, bf16[640,512]{1,0:T(8,128)(2,1)S(1)} %get-tuple-element.15), kind=kOutput, calls=%fused_computation.18 | convolution fusion | flops 346423296 | bytes 3670016 | tf_op jit(solution)/shard_map/dot_general | solution.py:85
  51.1 2.7 %collective-permute-done.10 = bf16[128,640]{1,0:T(8,128)(2,1)S(1)} collective-permute-done((bf16[128,640]{1,0:T(8,128)(2,1)S(1)}, bf16[128,640]{1,0:T(8,128)(2,1)S(1)}, u32[]{:S(2)}, u32[]{:S(2)}) %collective-permute-start.10) | collective-permute-done | bytes 163872 | tf_op jit(solution)/shard_map/ppermute | solution.py:92
  53.8 1.2 %collective-permute-start.11 = (bf16[128,640]{1,0:T(8,128)(2,1)S(1)}, bf16[128,640]{1,0:T(8,128)(2,1)S(1)}, u32[]{:S(2)}, u32[]{:S(2)}) collective-permute-start(bf16[128,640]{1,0:T(8,128)(2,1)S(1)} %fusion.8), channel_id=1, source_target_pairs={{0,12},{4,8},{8,4},{12,0},{1,13},{5,9},{9,5},{13,1},{2,14},{6,10},... | collective-permute-start | bytes 491528 | tf_op jit(solution)/shard_map/ppermute | solution.py:97
  55.1 0.5 collective-permute-done.16
  55.6 1.5 %collective-permute-start.17 = (bf16[128,640]{1,0:T(8,128)(2,1)S(1)}, bf16[128,640]{1,0:T(8,128)(2,1)S(1)}, u32[]{:S(2)}, u32[]{:S(2)}) collective-permute-start(bf16[128,640]{1,0:T(8,128)(2,1)S(1)} %fusion.7), channel_id=1, source_target_pairs={{0,4},{4,0},{8,12},{12,8},{1,5},{5,1},{9,13},{13,9},{2,6},{6,2},{1... | collective-permute-start | bytes 491528 | tf_op jit(solution)/shard_map/ppermute | solution.py:97
  57.5 1.5 %collective-permute-start.21 = (bf16[128,640]{1,0:T(8,128)(2,1)S(1)}, bf16[128,640]{1,0:T(8,128)(2,1)S(1)}, u32[]{:S(2)}, u32[]{:S(2)}) collective-permute-start(bf16[128,640]{1,0:T(8,128)(2,1)S(1)} %slice.64), channel_id=1, source_target_pairs={{0,2},{1,3},{2,0},{3,1},{4,6},{5,7},{6,4},{7,5},{8,10},{9,11},{10,... | collective-permute-start | bytes 491528 | tf_op jit(solution)/shard_map/ppermute | solution.py:92
  59.1 2.5 %collective-permute-done.11 = bf16[128,640]{1,0:T(8,128)(2,1)S(1)} collective-permute-done((bf16[128,640]{1,0:T(8,128)(2,1)S(1)}, bf16[128,640]{1,0:T(8,128)(2,1)S(1)}, u32[]{:S(2)}, u32[]{:S(2)}) %collective-permute-start.11) | collective-permute-done | bytes 163872 | tf_op jit(solution)/shard_map/ppermute | solution.py:97
  61.6 1.7 %collective-permute-done.17 = bf16[128,640]{1,0:T(8,128)(2,1)S(1)} collective-permute-done((bf16[128,640]{1,0:T(8,128)(2,1)S(1)}, bf16[128,640]{1,0:T(8,128)(2,1)S(1)}, u32[]{:S(2)}, u32[]{:S(2)}) %collective-permute-start.17) | collective-permute-done | bytes 163872 | tf_op jit(solution)/shard_map/ppermute | solution.py:97
  63.2 0.9 %fusion.6 = bf16[128,640]{1,0:T(8,128)(2,1)} fusion(f32[128,1280]{1,0:T(8,128)S(1)} %convert_add_fusion, bf16[128,640]{1,0:T(8,128)(2,1)S(1)} %collective-permute-done.21, bf16[128,640]{1,0:T(8,128)(2,1)S(1)} %collective-permute-done.17, bf16[128,640]{1,0:T(8,128)(2,1)S(1)} %collective-permute-done.11, bf16[128,640]{1,0:T(8,128)(2,1)S(1)} %collective-permute-done.5, ...), kind=kLoop, calls=%fused_computation.42 | loop fusion | flops 1064960 | bytes 1147392 | tf_op jit(solution)/shard_map/convert_element_type | solution.py:101
  (48 shorter events, 3.3 us)
Async XLA Ops:
  1.0 16.3 %collective-permute-start = (bf16[128,640]{1,0:T(8,128)(2,1)S(1)}, bf16[128,640]{1,0:T(8,128)(2,1)}, u32[]{:S(2)}, u32[]{:S(2)}) collective-permute-start(bf16[128,640]{1,0:T(8,128)(2,1)S(1)} %multiply_convert_fusion), channel_id=1, source_target_pairs={{0,8},{4,12},{8,0},{12,4},{1,9},{5,13},{9,1},{13,5},{2,10},{6,14},... | collective-permute-start | bytes 491528 | tf_op jit(solution)/shard_map/ppermute | solution.py:66
  5.1 15.1 %collective-permute-start.6 = (bf16[128,640]{1,0:T(8,128)(2,1)S(1)}, bf16[128,640]{1,0:T(8,128)(2,1)}, u32[]{:S(2)}, u32[]{:S(2)}) collective-permute-start(bf16[128,640]{1,0:T(8,128)(2,1)S(1)} %multiply_convert_fusion), channel_id=1, source_target_pairs={{0,12},{4,8},{8,4},{12,0},{1,13},{5,9},{9,5},{13,1},{2,14},{6,10},... | collective-permute-start | bytes 491528 | tf_op jit(solution)/shard_map/ppermute | solution.py:66
  6.5 14.0 %collective-permute-start.12 = (bf16[128,640]{1,0:T(8,128)(2,1)S(1)}, bf16[128,640]{1,0:T(8,128)(2,1)}, u32[]{:S(2)}, u32[]{:S(2)}) collective-permute-start(bf16[128,640]{1,0:T(8,128)(2,1)S(1)} %multiply_convert_fusion), channel_id=1, source_target_pairs={{0,4},{4,0},{8,12},{12,8},{1,5},{5,1},{9,13},{13,9},{2,6},{6,2},{1... | collective-permute-start | bytes 491528 | tf_op jit(solution)/shard_map/ppermute | solution.py:66
  6.7 12.5 %collective-permute-start.18 = (bf16[128,640]{1,0:T(8,128)(2,1)S(1)}, bf16[128,640]{1,0:T(8,128)(2,1)}, u32[]{:S(2)}, u32[]{:S(2)}) collective-permute-start(bf16[128,640]{1,0:T(8,128)(2,1)S(1)} %multiply_convert_fusion), channel_id=1, source_target_pairs={{0,2},{1,3},{2,0},{3,1},{4,6},{5,7},{6,4},{7,5},{8,10},{9,11},{10,... | collective-permute-start | bytes 491528 | tf_op jit(solution)/shard_map/ppermute | solution.py:79
  8.2 2.5 %copy-start = (bf16[1,2560,512]{2,1,0:T(8,128)(2,1)S(1)}, bf16[1,2560,512]{2,1,0:T(8,128)(2,1)}, u32[]{:S(2)}) copy-start(bf16[1,2560,512]{2,1,0:T(8,128)(2,1)} %param.10) | copy-start | bytes 7864324
  12.0 1.7 %copy-start.1 = (bf16[1,512,2560]{2,1,0:T(8,128)(2,1)S(1)}, bf16[1,512,2560]{2,1,0:T(8,128)(2,1)}, u32[]{:S(2)}) copy-start(bf16[1,512,2560]{2,1,0:T(8,128)(2,1)} %param.11) | copy-start | bytes 7864324
  17.3 5.9 %collective-permute-start.1 = (bf16[128,640]{1,0:T(8,128)(2,1)}, bf16[128,640]{1,0:T(8,128)(2,1)S(1)}, u32[]{:S(2)}, u32[]{:S(2)}) collective-permute-start(bf16[128,640]{1,0:T(8,128)(2,1)} %collective-permute-done), channel_id=1, source_target_pairs={{0,2},{1,3},{2,0},{3,1},{4,6},{5,7},{6,4},{7,5},{8,10},{9,11},{10,... | collective-permute-start | bytes 491528 | tf_op jit(solution)/shard_map/ppermute | solution.py:79
  20.1 21.7 %collective-permute-start.19 = (bf16[128,1280]{1,0:T(8,128)(2,1)S(1)}, bf16[128,1280]{1,0:T(8,128)(2,1)S(1)}, u32[]{:S(2)}, u32[]{:S(2)}) collective-permute-start(bf16[128,1280]{1,0:T(8,128)(2,1)S(1)} %pad_maximum_fusion.10), channel_id=1, source_target_pairs={{0,1},{1,0},{2,3},{3,2},{4,5},{5,4},{6,7},{7,6},{8,9},{9,8},{10,11... | collective-permute-start | bytes 983048 | tf_op jit(solution)/shard_map/ppermute | solution.py:81
  20.2 7.3 %collective-permute-start.7 = (bf16[128,640]{1,0:T(8,128)(2,1)}, bf16[128,640]{1,0:T(8,128)(2,1)S(1)}, u32[]{:S(2)}, u32[]{:S(2)}) collective-permute-start(bf16[128,640]{1,0:T(8,128)(2,1)} %collective-permute-done.6), channel_id=1, source_target_pairs={{0,2},{1,3},{2,0},{3,1},{4,6},{5,7},{6,4},{7,5},{8,10},{9,11},{10,... | collective-permute-start | bytes 491528 | tf_op jit(solution)/shard_map/ppermute | solution.py:79
  20.5 10.1 %collective-permute-start.13 = (bf16[128,640]{1,0:T(8,128)(2,1)}, bf16[128,640]{1,0:T(8,128)(2,1)S(1)}, u32[]{:S(2)}, u32[]{:S(2)}) collective-permute-start(bf16[128,640]{1,0:T(8,128)(2,1)} %collective-permute-done.12), channel_id=1, source_target_pairs={{0,2},{1,3},{2,0},{3,1},{4,6},{5,7},{6,4},{7,5},{8,10},{9,11},{10,... | collective-permute-start | bytes 491528 | tf_op jit(solution)/shard_map/ppermute | solution.py:79
  24.2 7.4 %collective-permute-start.2 = (bf16[128,1280]{1,0:T(8,128)(2,1)S(1)}, bf16[128,1280]{1,0:T(8,128)(2,1)S(1)}, u32[]{:S(2)}, u32[]{:S(2)}) collective-permute-start(bf16[128,1280]{1,0:T(8,128)(2,1)S(1)} %pad_maximum_fusion.7), channel_id=1, source_target_pairs={{0,1},{1,0},{2,3},{3,2},{4,5},{5,4},{6,7},{7,6},{8,9},{9,8},{10,11... | collective-permute-start | bytes 983048 | tf_op jit(solution)/shard_map/ppermute | solution.py:81
  28.4 3.7 %copy-start.2 = (bf16[640,512]{1,0:T(8,128)(2,1)S(1)}, bf16[640,512]{1,0:T(8,128)(2,1)}, u32[]{:S(2)}) copy-start(bf16[640,512]{1,0:T(8,128)(2,1)} %get-tuple-element.16) | copy-start | bytes 1966084
  28.4 3.7 %copy-start.3 = (bf16[640,512]{1,0:T(8,128)(2,1)S(1)}, bf16[640,512]{1,0:T(8,128)(2,1)}, u32[]{:S(2)}) copy-start(bf16[640,512]{1,0:T(8,128)(2,1)} %get-tuple-element.17) | copy-start | bytes 1966084
  28.4 3.7 %copy-start.4 = (bf16[640,512]{1,0:T(8,128)(2,1)S(1)}, bf16[640,512]{1,0:T(8,128)(2,1)}, u32[]{:S(2)}) copy-start(bf16[640,512]{1,0:T(8,128)(2,1)} %get-tuple-element.18) | copy-start | bytes 1966084
  28.4 5.4 %collective-permute-start.8 = (bf16[128,1280]{1,0:T(8,128)(2,1)S(1)}, bf16[128,1280]{1,0:T(8,128)(2,1)S(1)}, u32[]{:S(2)}, u32[]{:S(2)}) collective-permute-start(bf16[128,1280]{1,0:T(8,128)(2,1)S(1)} %pad_maximum_fusion.8), channel_id=1, source_target_pairs={{0,1},{1,0},{2,3},{3,2},{4,5},{5,4},{6,7},{7,6},{8,9},{9,8},{10,11... | collective-permute-start | bytes 983048 | tf_op jit(solution)/shard_map/ppermute | solution.py:81
  31.5 6.0 %collective-permute-start.14 = (bf16[128,1280]{1,0:T(8,128)(2,1)S(1)}, bf16[128,1280]{1,0:T(8,128)(2,1)S(1)}, u32[]{:S(2)}, u32[]{:S(2)}) collective-permute-start(bf16[128,1280]{1,0:T(8,128)(2,1)S(1)} %pad_maximum_fusion.9), channel_id=1, source_target_pairs={{0,1},{1,0},{2,3},{3,2},{4,5},{5,4},{6,7},{7,6},{8,9},{9,8},{10,11... | collective-permute-start | bytes 983048 | tf_op jit(solution)/shard_map/ppermute | solution.py:81
  33.3 1.8 %collective-permute-start.3 = (bf16[128,1280]{1,0:T(8,128)(2,1)S(1)}, bf16[128,1280]{1,0:T(8,128)(2,1)S(1)}, u32[]{:S(2)}, u32[]{:S(2)}) collective-permute-start(bf16[128,1280]{1,0:T(8,128)(2,1)S(1)} %convolution_convert_fusion.6), channel_id=1, source_target_pairs={{0,1},{1,0},{2,3},{3,2},{4,5},{5,4},{6,7},{7,6},{8,9},{9,8},{10,11... | collective-permute-start | bytes 983048 | tf_op jit(solution)/shard_map/ppermute | solution.py:90
  37.0 2.7 %collective-permute-start.9 = (bf16[128,1280]{1,0:T(8,128)(2,1)S(1)}, bf16[128,1280]{1,0:T(8,128)(2,1)S(1)}, u32[]{:S(2)}, u32[]{:S(2)}) collective-permute-start(bf16[128,1280]{1,0:T(8,128)(2,1)S(1)} %convolution_convert_fusion.4), channel_id=1, source_target_pairs={{0,1},{1,0},{2,3},{3,2},{4,5},{5,4},{6,7},{7,6},{8,9},{9,8},{10,11... | collective-permute-start | bytes 983048 | tf_op jit(solution)/shard_map/ppermute | solution.py:90
  38.5 6.3 %collective-permute-start.4 = (bf16[128,640]{1,0:T(8,128)(2,1)S(1)}, bf16[128,640]{1,0:T(8,128)(2,1)S(1)}, u32[]{:S(2)}, u32[]{:S(2)}) collective-permute-start(bf16[128,640]{1,0:T(8,128)(2,1)S(1)} %slice.67), channel_id=1, source_target_pairs={{0,2},{1,3},{2,0},{3,1},{4,6},{5,7},{6,4},{7,5},{8,10},{9,11},{10,... | collective-permute-start | bytes 491528 | tf_op jit(solution)/shard_map/ppermute | solution.py:92
  41.7 6.7 %collective-permute-start.15 = (bf16[128,1280]{1,0:T(8,128)(2,1)S(1)}, bf16[128,1280]{1,0:T(8,128)(2,1)S(1)}, u32[]{:S(2)}, u32[]{:S(2)}) collective-permute-start(bf16[128,1280]{1,0:T(8,128)(2,1)S(1)} %convolution_convert_fusion.2), channel_id=1, source_target_pairs={{0,1},{1,0},{2,3},{3,2},{4,5},{5,4},{6,7},{7,6},{8,9},{9,8},{10,11... | collective-permute-start | bytes 983048 | tf_op jit(solution)/shard_map/ppermute | solution.py:90
  44.8 14.2 %collective-permute-start.5 = (bf16[128,640]{1,0:T(8,128)(2,1)S(1)}, bf16[128,640]{1,0:T(8,128)(2,1)S(1)}, u32[]{:S(2)}, u32[]{:S(2)}) collective-permute-start(bf16[128,640]{1,0:T(8,128)(2,1)S(1)} %fusion.9), channel_id=1, source_target_pairs={{0,8},{4,12},{8,0},{12,4},{1,9},{5,13},{9,1},{13,5},{2,10},{6,14},... | collective-permute-start | bytes 491528 | tf_op jit(solution)/shard_map/ppermute | solution.py:97
  46.9 6.9 %collective-permute-start.10 = (bf16[128,640]{1,0:T(8,128)(2,1)S(1)}, bf16[128,640]{1,0:T(8,128)(2,1)S(1)}, u32[]{:S(2)}, u32[]{:S(2)}) collective-permute-start(bf16[128,640]{1,0:T(8,128)(2,1)S(1)} %slice.66), channel_id=1, source_target_pairs={{0,2},{1,3},{2,0},{3,1},{4,6},{5,7},{6,4},{7,5},{8,10},{9,11},{10,... | collective-permute-start | bytes 491528 | tf_op jit(solution)/shard_map/ppermute | solution.py:92
  48.8 6.8 %collective-permute-start.16 = (bf16[128,640]{1,0:T(8,128)(2,1)S(1)}, bf16[128,640]{1,0:T(8,128)(2,1)S(1)}, u32[]{:S(2)}, u32[]{:S(2)}) collective-permute-start(bf16[128,640]{1,0:T(8,128)(2,1)S(1)} %slice.65), channel_id=1, source_target_pairs={{0,2},{1,3},{2,0},{3,1},{4,6},{5,7},{6,4},{7,5},{8,10},{9,11},{10,... | collective-permute-start | bytes 491528 | tf_op jit(solution)/shard_map/ppermute | solution.py:92
  51.0 8.0 %copy-start.5 = (s32[128,1]{0,1:T(1,128)S(1)}, s32[128,1]{0,1:T(1,128)}, u32[]{:S(2)}) copy-start(s32[128,1]{0,1:T(1,128)} %param.8) | copy-start | bytes 1540
  51.0 6.1 %collective-permute-start.20 = (bf16[128,1280]{1,0:T(8,128)(2,1)S(1)}, bf16[128,1280]{1,0:T(8,128)(2,1)S(1)}, u32[]{:S(2)}, u32[]{:S(2)}) collective-permute-start(bf16[128,1280]{1,0:T(8,128)(2,1)S(1)} %convolution_convert_fusion), channel_id=1, source_target_pairs={{0,1},{1,0},{2,3},{3,2},{4,5},{5,4},{6,7},{7,6},{8,9},{9,8},{10,11... | collective-permute-start | bytes 983048 | tf_op jit(solution)/shard_map/ppermute | solution.py:90
  53.8 7.7 %collective-permute-start.11 = (bf16[128,640]{1,0:T(8,128)(2,1)S(1)}, bf16[128,640]{1,0:T(8,128)(2,1)S(1)}, u32[]{:S(2)}, u32[]{:S(2)}) collective-permute-start(bf16[128,640]{1,0:T(8,128)(2,1)S(1)} %fusion.8), channel_id=1, source_target_pairs={{0,12},{4,8},{8,4},{12,0},{1,13},{5,9},{9,5},{13,1},{2,14},{6,10},... | collective-permute-start | bytes 491528 | tf_op jit(solution)/shard_map/ppermute | solution.py:97
  55.6 7.6 %collective-permute-start.17 = (bf16[128,640]{1,0:T(8,128)(2,1)S(1)}, bf16[128,640]{1,0:T(8,128)(2,1)S(1)}, u32[]{:S(2)}, u32[]{:S(2)}) collective-permute-start(bf16[128,640]{1,0:T(8,128)(2,1)S(1)} %fusion.7), channel_id=1, source_target_pairs={{0,4},{4,0},{8,12},{12,8},{1,5},{5,1},{9,13},{13,9},{2,6},{6,2},{1... | collective-permute-start | bytes 491528 | tf_op jit(solution)/shard_map/ppermute | solution.py:97
  57.5 5.7 %collective-permute-start.21 = (bf16[128,640]{1,0:T(8,128)(2,1)S(1)}, bf16[128,640]{1,0:T(8,128)(2,1)S(1)}, u32[]{:S(2)}, u32[]{:S(2)}) collective-permute-start(bf16[128,640]{1,0:T(8,128)(2,1)S(1)} %slice.64), channel_id=1, source_target_pairs={{0,2},{1,3},{2,0},{3,1},{4,6},{5,7},{6,4},{7,5},{8,10},{9,11},{10,... | collective-permute-start | bytes 491528 | tf_op jit(solution)/shard_map/ppermute | solution.py:92

commit v19 on v18

--- a/solution.py
+++ b/solution.py
@@ -77,12 +77,13 @@
         piece = jnp.concatenate([blocks[k] for k in wave])
         pair = jnp.concatenate(
             [piece, lax.ppermute(piece, "tensor", _xor_pairs(n_tensor, 2))], axis=1)
-        rows = jnp.concatenate(
-            [pair, lax.ppermute(pair, "tensor", _xor_pairs(n_tensor, 1))], axis=1)
+        other = lax.ppermute(pair, "tensor", _xor_pairs(n_tensor, 1))
         if previous is not None:
-            rows, _ = lax.optimization_barrier((rows, previous))
-        gate_act = jnp.dot(rows, gate_w, preferred_element_type=jnp.float32)
-        up_act = jnp.dot(rows, up_w, preferred_element_type=jnp.float32)
+            pair, other, _ = lax.optimization_barrier((pair, other, previous))
+        gate_act = jnp.dot(pair, gate_w[:2 * width], preferred_element_type=jnp.float32) + jnp.dot(
+            other, gate_w[2 * width:], preferred_element_type=jnp.float32)
+        up_act = jnp.dot(pair, up_w[:2 * width], preferred_element_type=jnp.float32) + jnp.dot(
+            other, up_w[2 * width:], preferred_element_type=jnp.float32)
         hidden = (jax.nn.silu(gate_act) * up_act).astype(jnp.bfloat16)
         keep = jnp.dot(hidden, down_keep, preferred_element_type=jnp.float32).astype(jnp.bfloat16)
         send = jnp.dot(hidden, down_send, preferred_element_type=jnp.float32).astype(jnp.bfloat16)

time: 64.5 us -> 72.2 us (1.12)
  matrix products: 7.73 us -> 15.3 us
  other arithmetic: 8.86 us -> 3.03 us
  starting transfers between devices: 22.3 us -> 26.2 us
  waiting for transfers between devices: 18.2 us -> 19.7 us
    ppermute x3, waiting for transfers between devices: 3.32 us -> 11 us  [gathered(): lax.ppermute(scaled, 'expert', _xor_pairs(n_expert, k))]
    dot_general x8 -> x16, matrix products: 4.94 us -> 9.46 us  [the longest x4 2.46 us: gathered(): jnp.dot(pair, up_w[:2 * width], preferred_element_type=jnp.float32)]
    ppermute x4, waiting for transfers between devices: 5.23 us -> 1.24 us  [gathered(): lax.ppermute(piece, 'tensor', _xor_pairs(n_tensor, 2))]
    ppermute x3, starting transfers between devices: 5.68 us -> 9.07 us  [gathered(): lax.ppermute(scaled, 'expert', _xor_pairs(n_expert, k))]
    concatenate x4 -> x0, other arithmetic: 3.09 us -> none  [the longest x3 2.89 us: gathered(): jnp.concatenate([pair, lax.ppermute(pair, 'tensor', _xor_pairs(n_tensor,...]
    concatenate x4 -> x1, other arithmetic: 3.76 us -> 1.03 us  [gathered(): jnp.concatenate([piece, lax.ppermute(piece, 'tensor', _xor_pairs(n_tensor...]
    dot_general x4, matrix products: 1.39 us -> 3.71 us  [gathered(): jnp.dot(hidden, down_keep, preferred_element_type=jnp.float32)]
    ppermute x4, waiting for transfers between devices: 5.21 us -> 3.84 us  [gathered(): lax.ppermute(over_c[:, width:].astype(jnp.bfloat16), 'tensor', _xor_pairs...]
  transfers between devices with their start and end apart: 22 -> 22, of which waited for: 9 -> 10; matrix products, arithmetic and copies ran while one was open for 30% -> 32% of each run, Pallas kernels for 0% -> 0%
where the time goes in v19:
time: 72.2 us; the launch traced here: 71.9 us
  starting transfers between devices  26.2 us (36%)
  waiting for transfers between devices  19.7 us (27%)
  matrix products  15.3 us (21%)
  local copies, waits for them, and re-layouts  7.07 us (10%)
  other arithmetic  3.03 us (4%)
    ppermute x3, waiting for transfers between devices, gathered(): lax.ppermute(scaled, 'expert', _xor_pairs(n_expert, k))  11 us
    ppermute x3, starting transfers between devices, gathered(): lax.ppermute(scaled, 'expert', _xor_pairs(n_expert, k))  9.07 us
    ppermute x3, starting transfers between devices, gathered(): lax.ppermute(part.astype(jnp.bfloat16), 'expert', _xor_pairs(n_expert, k))  5.73 us
    ppermute x4, starting transfers between devices, gathered(): lax.ppermute(piece, 'tensor', _xor_pairs(n_tensor, 2))  5.1 us
    ppermute x4, starting transfers between devices, gathered(): lax.ppermute(over_c[:, width:].astype(jnp.bfloat16), 'tensor', _xor_pairs...  4.81 us
    ppermute x4, waiting for transfers between devices, gathered(): lax.ppermute(over_c[:, width:].astype(jnp.bfloat16), 'tensor', _xor_pairs...  3.84 us
    dot_general x4, matrix products, gathered(): jnp.dot(hidden, down_keep, preferred_element_type=jnp.float32)  3.71 us
    ppermute x3, waiting for transfers between devices, gathered(): lax.ppermute(part.astype(jnp.bfloat16), 'expert', _xor_pairs(n_expert, k))  3.61 us
  transfers between devices with their start and end apart: 22, of which 10 were waited for; matrix products, arithmetic and copies ran while one was open for 32% of the time, Pallas kernels for 0%

profile of v19, /device:TPU:0, one launch (start us, length us, event | category | flops | bytes accessed | tf_op | source)
XLA Modules:
  0.0 71.9 jit_solution(13520555879384475685)
XLA Ops:
  0.0 1.0 %multiply_convert_fusion = bf16[128,640]{1,0:T(8,128)(2,1)S(1)} fusion(bf16[128,640]{1,0:T(8,128)(2,1)} %param.6, f32[128]{0:T(128)} %param.7), kind=kLoop, calls=%fused_computation.60 | loop fusion | flops 245760 | bytes 328192 | tf_op jit(solution)/shard_map/convert_element_type | solution.py:64
  1.0 4.1 %collective-permute-start = (bf16[128,640]{1,0:T(8,128)(2,1)S(1)}, bf16[128,640]{1,0:T(8,128)(2,1)S(1)}, u32[]{:S(2)}, u32[]{:S(2)}) collective-permute-start(bf16[128,640]{1,0:T(8,128)(2,1)S(1)} %multiply_convert_fusion), channel_id=1, source_target_pairs={{0,8},{4,12},{8,0},{12,4},{1,9},{5,13},{9,1},{13,5},{2,10},{6,14},... | collective-permute-start | bytes 491528 | tf_op jit(solution)/shard_map/ppermute | solution.py:66
  5.1 7.7 %collective-permute-done = bf16[128,640]{1,0:T(8,128)(2,1)S(1)} collective-permute-done((bf16[128,640]{1,0:T(8,128)(2,1)S(1)}, bf16[128,640]{1,0:T(8,128)(2,1)S(1)}, u32[]{:S(2)}, u32[]{:S(2)}) %collective-permute-start) | collective-permute-done | bytes 163872 | tf_op jit(solution)/shard_map/ppermute | solution.py:66
  12.8 1.5 %collective-permute-start.1 = (bf16[128,640]{1,0:T(8,128)(2,1)S(1)}, bf16[128,640]{1,0:T(8,128)(2,1)S(1)}, u32[]{:S(2)}, u32[]{:S(2)}) collective-permute-start(bf16[128,640]{1,0:T(8,128)(2,1)S(1)} %collective-permute-done), channel_id=1, source_target_pairs={{0,2},{1,3},{2,0},{3,1},{4,6},{5,7},{6,4},{7,5},{8,10},{9,11},{10,... | collective-permute-start | bytes 491528 | tf_op jit(solution)/shard_map/ppermute | solution.py:79
  14.4 3.5 %collective-permute-start.6 = (bf16[128,640]{1,0:T(8,128)(2,1)S(1)}, bf16[128,640]{1,0:T(8,128)(2,1)}, u32[]{:S(2)}, u32[]{:S(2)}) collective-permute-start(bf16[128,640]{1,0:T(8,128)(2,1)S(1)} %multiply_convert_fusion), channel_id=1, source_target_pairs={{0,12},{4,8},{8,4},{12,0},{1,13},{5,9},{9,5},{13,1},{2,14},{6,10},... | collective-permute-start | bytes 491528 | tf_op jit(solution)/shard_map/ppermute | solution.py:66
  18.3 3.1 %dynamic-slice_bitcast_fusion.7 = (bf16[640,512]{1,0:T(8,128)(2,1)S(1)}, bf16[640,512]{1,0:T(8,128)(2,1)S(1)}, bf16[640,512]{1,0:T(8,128)(2,1)S(1)}, bf16[640,51...) fusion(bf16[1,2560,512]{2,1,0:T(8,128)(2,1)} %param.10, ...), kind=kLoop, calls=%fused_computation.40 | loop fusion | bytes 10485776 | tf_op jit(solution)/shard_map/dynamic_slice | solution.py:55
  22.2 1.3 %collective-permute-start.7 = (bf16[128,640]{1,0:T(8,128)(2,1)}, bf16[128,640]{1,0:T(8,128)(2,1)S(1)}, u32[]{:S(2)}, u32[]{:S(2)}) collective-permute-start(bf16[128,640]{1,0:T(8,128)(2,1)} %collective-permute-done.6), channel_id=1, source_target_pairs={{0,2},{1,3},{2,0},{3,1},{4,6},{5,7},{6,4},{7,5},{8,10},{9,11},{10,... | collective-permute-start | bytes 491528 | tf_op jit(solution)/shard_map/ppermute | solution.py:79
  23.8 0.3 convolution_add_fusion.7
  24.5 0.4 multiply_convert_fusion.1
  24.9 0.3 convolution_convert_fusion.6
  25.5 1.5 %collective-permute-start.12 = (bf16[128,640]{1,0:T(8,128)(2,1)S(1)}, bf16[128,640]{1,0:T(8,128)(2,1)S(1)}, u32[]{:S(2)}, u32[]{:S(2)}) collective-permute-start(bf16[128,640]{1,0:T(8,128)(2,1)S(1)} %multiply_convert_fusion), channel_id=1, source_target_pairs={{0,4},{4,0},{8,12},{12,8},{1,5},{5,1},{9,13},{13,9},{2,6},{6,2},{1... | collective-permute-start | bytes 491528 | tf_op jit(solution)/shard_map/ppermute | solution.py:66
  27.0 0.9 %constant_dynamic-update-slice_fusion.3 = bf16[128,1280]{1,0:T(8,128)(2,1)S(1)} fusion(bf16[128,640]{1,0:T(8,128)(2,1)} %collective-permute-done.6), kind=kLoop, calls=%fused_computation.65 | loop fusion | bytes 327680
  27.9 0.9 %collective-permute-done.7 = bf16[128,640]{1,0:T(8,128)(2,1)S(1)} collective-permute-done((bf16[128,640]{1,0:T(8,128)(2,1)}, bf16[128,640]{1,0:T(8,128)(2,1)S(1)}, u32[]{:S(2)}, u32[]{:S(2)}) %collective-permute-start.7) | collective-permute-done | bytes 163872 | tf_op jit(solution)/shard_map/ppermute | solution.py:79
  28.9 3.0 %collective-permute-done.12 = bf16[128,640]{1,0:T(8,128)(2,1)S(1)} collective-permute-done((bf16[128,640]{1,0:T(8,128)(2,1)S(1)}, bf16[128,640]{1,0:T(8,128)(2,1)S(1)}, u32[]{:S(2)}, u32[]{:S(2)}) %collective-permute-start.12) | collective-permute-done | bytes 163872 | tf_op jit(solution)/shard_map/ppermute | solution.py:66
  31.9 1.3 %collective-permute-start.13 = (bf16[128,640]{1,0:T(8,128)(2,1)S(1)}, bf16[128,640]{1,0:T(8,128)(2,1)S(1)}, u32[]{:S(2)}, u32[]{:S(2)}) collective-permute-start(bf16[128,640]{1,0:T(8,128)(2,1)S(1)} %collective-permute-done.12), channel_id=1, source_target_pairs={{0,2},{1,3},{2,0},{3,1},{4,6},{5,7},{6,4},{7,5},{8,10},{9,11},{10,... | collective-permute-start | bytes 491528 | tf_op jit(solution)/shard_map/ppermute | solution.py:79
  33.2 1.2 %convert_add_fusion.3 = f32[128,1280]{1,0:T(8,128)} fusion(bf16[128,1280]{1,0:T(8,128)(2,1)S(1)} %collective-permute-done.3, bf16[128,512]{1,0:T(8,128)(2,1)S(1)} %multiply_convert_fusion.1, bf16[512,640]{1,0:T(8,128)(2,1)S(1)} %get-tuple-element.18, bf16[512,640]{1,0:T(8,128)(2,1)S(1)} %get-tuple-element.19), kind=kOutput, calls=%fused_computation.32 | convolution fusion | flops 171048960 | bytes 2424832 | tf_op jit(solution)/shard_map/dot_general | solution.py:88
  35.2 0.3 convolution_add_fusion.5
  35.5 0.3 fusion.4
  35.9 1.1 %convolution_convert_fusion.4 = bf16[128,1280]{1,0:T(8,128)(2,1)} fusion(bf16[128,512]{1,0:T(8,128)(2,1)S(1)} %fusion.4, bf16[512,640]{1,0:T(8,128)(2,1)S(1)} %get-tuple-element.20, bf16[512,640]{1,0:T(8,128)(2,1)S(1)} %get-tuple-element.17), kind=kOutput, calls=%fused_computation.5 | convolution fusion | flops 170557440 | bytes 1769472 | tf_op jit(solution)/shard_map/dot_general | solution.py:89
  37.0 0.7 constant_dynamic-update-slice_fusion.5
  37.7 0.7 constant_dynamic-update-slice_fusion.4
  38.4 0.5 collective-permute-start.14
  38.9 0.9 %collective-permute-start.18 = (bf16[128,640]{1,0:T(8,128)(2,1)S(1)}, bf16[128,640]{1,0:T(8,128)(2,1)}, u32[]{:S(2)}, u32[]{:S(2)}) collective-permute-start(bf16[128,640]{1,0:T(8,128)(2,1)S(1)} %multiply_convert_fusion), channel_id=1, source_target_pairs={{0,2},{1,3},{2,0},{3,1},{4,6},{5,7},{6,4},{7,5},{8,10},{9,11},{10,... | collective-permute-start | bytes 491528 | tf_op jit(solution)/shard_map/ppermute | solution.py:79
  39.9 1.0 %slice.87 = bf16[128,640]{1,0:T(8,128)(2,1)S(1)} slice(f32[128,1280]{1,0:T(8,128)} %convert_add_fusion.3), slice={[0:128], [640:1280]} | slice | bytes 327680 | tf_op jit(solution)/shard_map/slice | solution.py:94
  40.9 1.1 %collective-permute-start.4 = (bf16[128,640]{1,0:T(8,128)(2,1)S(1)}, bf16[128,640]{1,0:T(8,128)(2,1)S(1)}, u32[]{:S(2)}, u32[]{:S(2)}) collective-permute-start(bf16[128,640]{1,0:T(8,128)(2,1)S(1)} %slice.87), channel_id=1, source_target_pairs={{0,2},{1,3},{2,0},{3,1},{4,6},{5,7},{6,4},{7,5},{8,10},{9,11},{10,... | collective-permute-start | bytes 491528 | tf_op jit(solution)/shard_map/ppermute | solution.py:93
  42.0 1.8 %convert_add_fusion.2 = f32[128,1280]{1,0:T(8,128)S(1)} fusion(bf16[128,1280]{1,0:T(8,128)(2,1)} %collective-permute-done.9, bf16[128,512]{1,0:T(8,128)(2,1)} %copy-done.17, bf16[512,640]{1,0:T(8,128)(2,1)} %copy-done.7, bf16[512,640]{1,0:T(8,128)(2,1)} %copy-done.9), kind=kOutput, calls=%fused_computation.31 | convolution fusion | flops 171048960 | bytes 2424832 | tf_op jit(solution)/shard_map/dot_general | solution.py:88
  43.9 1.4 %fusion.18 = f32[128,512]{1,0:T(8,128)S(1)} fusion(bf16[128,1280]{1,0:T(8,128)(2,1)} %collective-permute-done.14, bf16[640,512]{1,0:T(8,128)(2,1)S(1)} %copy-done.6, bf16[640,512]{1,0:T(8,128)(2,1)S(1)} %copy-done.4), kind=kOutput, calls=%fused_computation.77 | convolution fusion | flops 170393600 | bytes 1900544 | tf_op jit(solution)/shard_map/dot_general | solution.py:83
  45.3 1.3 %fusion.14 = f32[128,512]{1,0:T(8,128)S(1)} fusion(bf16[128,1280]{1,0:T(8,128)(2,1)} %collective-permute-done.14, bf16[640,512]{1,0:T(8,128)(2,1)S(1)} %get-tuple-element.23, bf16[640,512]{1,0:T(8,128)(2,1)S(1)} %copy-done.2), kind=kOutput, calls=%fused_computation.73 | convolution fusion | flops 170393600 | bytes 1900544 | tf_op jit(solution)/shard_map/dot_general | solution.py:85
  46.6 1.3 %convolution_add_fusion.3 = f32[128,512]{1,0:T(8,128)S(1)} fusion(f32[128,512]{1,0:T(8,128)S(1)} %fusion.18, bf16[128,1280]{1,0:T(8,128)(2,1)} %constant_dynamic-update-slice_fusion.4, bf16[640,512]{1,0:T(8,128)(2,1)S(1)} %get-tuple-element.41, bf16[640,512]{1,0:T(8,128)(2,1)S(1)} %get-tuple-element.42), kind=kOutput, calls=%fused_computation.20 | convolution fusion | flops 170459136 | bytes 2162688 | tf_op jit(solution)/shard_map/dot_general | solution.py:83
  47.9 1.4 %fusion.5 = bf16[128,512]{1,0:T(8,128)(2,1)S(1)} fusion(f32[128,512]{1,0:T(8,128)S(1)} %fusion.14, bf16[128,1280]{1,0:T(8,128)(2,1)} %constant_dynamic-update-slice_fusion.4, f32[128,512]{1,0:T(8,128)S(1)} %convolution_add_fusion.3, bf16[640,512]{1,0:T(8,128)(2,1)S(1)} %get-tuple-element.22, bf16[640,512]{1,0:T(8,128)(2,1)S(1)} %get-tuple-element.21), kind=kOutput, calls=%fused_computation.27 | convolution fusion | flops 170852352 | bytes 2293760 | tf_op jit(solution)/shard_map/dot_general | solution.py:85
  49.4 0.3 convolution_convert_fusion.2
  49.8 1.0 %pad_maximum_fusion.6 = bf16[128,1280]{1,0:T(8,128)(2,1)S(1)} fusion(bf16[128,640]{1,0:T(8,128)(2,1)} %collective-permute-done.18, bf16[128,640]{1,0:T(8,128)(2,1)S(1)} %multiply_convert_fusion), kind=kLoop, calls=%fused_computation.59 | loop fusion | flops 655360 | bytes 655360 | tf_op jit(solution)/shard_map/concatenate | solution.py:78
  50.9 0.5 collective-permute-start.19
  51.4 2.7 %collective-permute-start.5 = (bf16[128,640]{1,0:T(8,128)(2,1)S(1)}, bf16[128,640]{1,0:T(8,128)(2,1)S(1)}, u32[]{:S(2)}, u32[]{:S(2)}) collective-permute-start(bf16[128,640]{1,0:T(8,128)(2,1)S(1)} %fusion.12), channel_id=1, source_target_pairs={{0,8},{4,12},{8,0},{12,4},{1,9},{5,13},{9,1},{13,5},{2,10},{6,14},... | collective-permute-start | bytes 491528 | tf_op jit(solution)/shard_map/ppermute | solution.py:98
  54.1 1.2 %collective-permute-start.10 = (bf16[128,640]{1,0:T(8,128)(2,1)S(1)}, bf16[128,640]{1,0:T(8,128)(2,1)S(1)}, u32[]{:S(2)}, u32[]{:S(2)}) collective-permute-start(bf16[128,640]{1,0:T(8,128)(2,1)S(1)} %slice.86), channel_id=1, source_target_pairs={{0,2},{1,3},{2,0},{3,1},{4,6},{5,7},{6,4},{7,5},{8,10},{9,11},{10,... | collective-permute-start | bytes 491528 | tf_op jit(solution)/shard_map/ppermute | solution.py:93
  55.3 0.3 convert_add_fusion.1
  56.4 1.0 %collective-permute-start.16 = (bf16[128,640]{1,0:T(8,128)(2,1)S(1)}, bf16[128,640]{1,0:T(8,128)(2,1)S(1)}, u32[]{:S(2)}, u32[]{:S(2)}) collective-permute-start(bf16[128,640]{1,0:T(8,128)(2,1)S(1)} %slice.85), channel_id=1, source_target_pairs={{0,2},{1,3},{2,0},{3,1},{4,6},{5,7},{6,4},{7,5},{8,10},{9,11},{10,... | collective-permute-start | bytes 491528 | tf_op jit(solution)/shard_map/ppermute | solution.py:93
  57.7 0.3 fusion.6
  58.1 0.3 convolution_convert_fusion
  58.5 2.8 %collective-permute-done.10 = bf16[128,640]{1,0:T(8,128)(2,1)S(1)} collective-permute-done((bf16[128,640]{1,0:T(8,128)(2,1)S(1)}, bf16[128,640]{1,0:T(8,128)(2,1)S(1)}, u32[]{:S(2)}, u32[]{:S(2)}) %collective-permute-start.10) | collective-permute-done | bytes 163872 | tf_op jit(solution)/shard_map/ppermute | solution.py:93
  61.3 1.5 %collective-permute-start.11 = (bf16[128,640]{1,0:T(8,128)(2,1)S(1)}, bf16[128,640]{1,0:T(8,128)(2,1)S(1)}, u32[]{:S(2)}, u32[]{:S(2)}) collective-permute-start(bf16[128,640]{1,0:T(8,128)(2,1)S(1)} %fusion.11), channel_id=1, source_target_pairs={{0,12},{4,8},{8,4},{12,0},{1,13},{5,9},{9,5},{13,1},{2,14},{6,10},... | collective-permute-start | bytes 491528 | tf_op jit(solution)/shard_map/ppermute | solution.py:98
  62.8 0.8 %collective-permute-done.16 = bf16[128,640]{1,0:T(8,128)(2,1)S(1)} collective-permute-done((bf16[128,640]{1,0:T(8,128)(2,1)S(1)}, bf16[128,640]{1,0:T(8,128)(2,1)S(1)}, u32[]{:S(2)}, u32[]{:S(2)}) %collective-permute-start.16) | collective-permute-done | bytes 163872 | tf_op jit(solution)/shard_map/ppermute | solution.py:93
  63.7 1.5 %collective-permute-start.17 = (bf16[128,640]{1,0:T(8,128)(2,1)S(1)}, bf16[128,640]{1,0:T(8,128)(2,1)S(1)}, u32[]{:S(2)}, u32[]{:S(2)}) collective-permute-start(bf16[128,640]{1,0:T(8,128)(2,1)S(1)} %fusion.10), channel_id=1, source_target_pairs={{0,4},{4,0},{8,12},{12,8},{1,5},{5,1},{9,13},{13,9},{2,6},{6,2},{1... | collective-permute-start | bytes 491528 | tf_op jit(solution)/shard_map/ppermute | solution.py:98
  65.2 0.3 convert_add_fusion
  65.6 1.5 %collective-permute-start.21 = (bf16[128,640]{1,0:T(8,128)(2,1)S(1)}, bf16[128,640]{1,0:T(8,128)(2,1)S(1)}, u32[]{:S(2)}, u32[]{:S(2)}) collective-permute-start(bf16[128,640]{1,0:T(8,128)(2,1)S(1)} %slice.84), channel_id=1, source_target_pairs={{0,2},{1,3},{2,0},{3,1},{4,6},{5,7},{6,4},{7,5},{8,10},{9,11},{10,... | collective-permute-start | bytes 491528 | tf_op jit(solution)/shard_map/ppermute | solution.py:93
  67.1 2.0 %collective-permute-done.11 = bf16[128,640]{1,0:T(8,128)(2,1)S(1)} collective-permute-done((bf16[128,640]{1,0:T(8,128)(2,1)S(1)}, bf16[128,640]{1,0:T(8,128)(2,1)S(1)}, u32[]{:S(2)}, u32[]{:S(2)}) %collective-permute-start.11) | collective-permute-done | bytes 163872 | tf_op jit(solution)/shard_map/ppermute | solution.py:98
  69.1 1.7 %collective-permute-done.17 = bf16[128,640]{1,0:T(8,128)(2,1)S(1)} collective-permute-done((bf16[128,640]{1,0:T(8,128)(2,1)S(1)}, bf16[128,640]{1,0:T(8,128)(2,1)S(1)}, u32[]{:S(2)}, u32[]{:S(2)}) %collective-permute-start.17) | collective-permute-done | bytes 163872 | tf_op jit(solution)/shard_map/ppermute | solution.py:98
  71.0 0.9 %fusion.9 = bf16[128,640]{1,0:T(8,128)(2,1)} fusion(f32[128,1280]{1,0:T(8,128)S(1)} %convert_add_fusion, bf16[128,640]{1,0:T(8,128)(2,1)S(1)} %collective-permute-done.21, bf16[128,640]{1,0:T(8,128)(2,1)S(1)} %collective-permute-done.17, bf16[128,640]{1,0:T(8,128)(2,1)S(1)} %collective-permute-done.11, bf16[128,640]{1,0:T(8,128)(2,1)S(1)} %collective-permute-done.5, ...), kind=kLoop, calls=%fused_computation.49 | loop fusion | flops 1064960 | bytes 1147392 | tf_op jit(solution)/shard_map/convert_element_type | solution.py:102
  (75 shorter events, 4.5 us)
Async XLA Ops:
  1.0 11.8 %collective-permute-start = (bf16[128,640]{1,0:T(8,128)(2,1)S(1)}, bf16[128,640]{1,0:T(8,128)(2,1)S(1)}, u32[]{:S(2)}, u32[]{:S(2)}) collective-permute-start(bf16[128,640]{1,0:T(8,128)(2,1)S(1)} %multiply_convert_fusion), channel_id=1, source_target_pairs={{0,8},{4,12},{8,0},{12,4},{1,9},{5,13},{9,1},{13,5},{2,10},{6,14},... | collective-permute-start | bytes 491528 | tf_op jit(solution)/shard_map/ppermute | solution.py:66
  12.8 5.4 %collective-permute-start.1 = (bf16[128,640]{1,0:T(8,128)(2,1)S(1)}, bf16[128,640]{1,0:T(8,128)(2,1)S(1)}, u32[]{:S(2)}, u32[]{:S(2)}) collective-permute-start(bf16[128,640]{1,0:T(8,128)(2,1)S(1)} %collective-permute-done), channel_id=1, source_target_pairs={{0,2},{1,3},{2,0},{3,1},{4,6},{5,7},{6,4},{7,5},{8,10},{9,11},{10,... | collective-permute-start | bytes 491528 | tf_op jit(solution)/shard_map/ppermute | solution.py:79
  14.4 7.8 %collective-permute-start.6 = (bf16[128,640]{1,0:T(8,128)(2,1)S(1)}, bf16[128,640]{1,0:T(8,128)(2,1)}, u32[]{:S(2)}, u32[]{:S(2)}) collective-permute-start(bf16[128,640]{1,0:T(8,128)(2,1)S(1)} %multiply_convert_fusion), channel_id=1, source_target_pairs={{0,12},{4,8},{8,4},{12,0},{1,13},{5,9},{9,5},{13,1},{2,14},{6,10},... | collective-permute-start | bytes 491528 | tf_op jit(solution)/shard_map/ppermute | solution.py:66
  18.2 5.2 %collective-permute-start.2 = (bf16[128,1280]{1,0:T(8,128)(2,1)S(1)}, bf16[128,1280]{1,0:T(8,128)(2,1)S(1)}, u32[]{:S(2)}, u32[]{:S(2)}) collective-permute-start(bf16[128,1280]{1,0:T(8,128)(2,1)S(1)} %constant_dynamic-update-slice_fusion), channel_id=1, source_target_pairs={{0,1},{1,0},{2,3},{3,2},{4,5},{5,4},{6,7},{7,6},{8,9},{9,8},{10,11... | collective-permute-start | bytes 983048 | tf_op jit(solution)/shard_map/ppermute | solution.py:80
  18.3 3.3 %copy-start = (bf16[1,512,2560]{2,1,0:T(8,128)(2,1)S(1)}, bf16[1,512,2560]{2,1,0:T(8,128)(2,1)}, u32[]{:S(2)}) copy-start(bf16[1,512,2560]{2,1,0:T(8,128)(2,1)} %param.11) | copy-start | bytes 7864324
  21.6 12.8 %copy-start.3 = (bf16[640,512]{1,0:T(8,128)(2,1)}, bf16[640,512]{1,0:T(8,128)(2,1)S(1)}, u32[]{:S(2)}) copy-start(bf16[640,512]{1,0:T(8,128)(2,1)S(1)} %get-tuple-element.39) | copy-start | bytes 1966084
  21.6 12.8 %copy-start.5 = (bf16[640,512]{1,0:T(8,128)(2,1)}, bf16[640,512]{1,0:T(8,128)(2,1)S(1)}, u32[]{:S(2)}) copy-start(bf16[640,512]{1,0:T(8,128)(2,1)S(1)} %get-tuple-element.40) | copy-start | bytes 1966084
  21.6 13.2 %copy-start.1 = (bf16[640,512]{1,0:T(8,128)(2,1)}, bf16[640,512]{1,0:T(8,128)(2,1)S(1)}, u32[]{:S(2)}) copy-start(bf16[640,512]{1,0:T(8,128)(2,1)S(1)} %get-tuple-element.24) | copy-start | bytes 1966084
  21.9 11.4 %copy-start.7 = (bf16[512,640]{1,0:T(8,128)(2,1)}, bf16[512,640]{1,0:T(8,128)(2,1)S(1)}, u32[]{:S(2)}) copy-start(bf16[512,640]{1,0:T(8,128)(2,1)S(1)} %get-tuple-element.18) | copy-start | bytes 1966084
  21.9 11.3 %copy-start.9 = (bf16[512,640]{1,0:T(8,128)(2,1)}, bf16[512,640]{1,0:T(8,128)(2,1)S(1)}, u32[]{:S(2)}) copy-start(bf16[512,640]{1,0:T(8,128)(2,1)S(1)} %get-tuple-element.19) | copy-start | bytes 1966084
  21.9 14.0 %copy-start.11 = (bf16[512,640]{1,0:T(8,128)(2,1)}, bf16[512,640]{1,0:T(8,128)(2,1)S(1)}, u32[]{:S(2)}) copy-start(bf16[512,640]{1,0:T(8,128)(2,1)S(1)} %get-tuple-element.17) | copy-start | bytes 1966084
  21.9 14.0 %copy-start.13 = (bf16[512,640]{1,0:T(8,128)(2,1)}, bf16[512,640]{1,0:T(8,128)(2,1)S(1)}, u32[]{:S(2)}) copy-start(bf16[512,640]{1,0:T(8,128)(2,1)S(1)} %get-tuple-element.20) | copy-start | bytes 1966084
  22.2 6.6 %collective-permute-start.7 = (bf16[128,640]{1,0:T(8,128)(2,1)}, bf16[128,640]{1,0:T(8,128)(2,1)S(1)}, u32[]{:S(2)}, u32[]{:S(2)}) collective-permute-start(bf16[128,640]{1,0:T(8,128)(2,1)} %collective-permute-done.6), channel_id=1, source_target_pairs={{0,2},{1,3},{2,0},{3,1},{4,6},{5,7},{6,4},{7,5},{8,10},{9,11},{10,... | collective-permute-start | bytes 491528 | tf_op jit(solution)/shard_map/ppermute | solution.py:79
  25.2 8.0 %collective-permute-start.3 = (bf16[128,1280]{1,0:T(8,128)(2,1)S(1)}, bf16[128,1280]{1,0:T(8,128)(2,1)S(1)}, u32[]{:S(2)}, u32[]{:S(2)}) collective-permute-start(bf16[128,1280]{1,0:T(8,128)(2,1)S(1)} %convolution_convert_fusion.6), channel_id=1, source_target_pairs={{0,1},{1,0},{2,3},{3,2},{4,5},{5,4},{6,7},{7,6},{8,9},{9,8},{10,11... | collective-permute-start | bytes 983048 | tf_op jit(solution)/shard_map/ppermute | solution.py:91
  25.5 6.4 %collective-permute-start.12 = (bf16[128,640]{1,0:T(8,128)(2,1)S(1)}, bf16[128,640]{1,0:T(8,128)(2,1)S(1)}, u32[]{:S(2)}, u32[]{:S(2)}) collective-permute-start(bf16[128,640]{1,0:T(8,128)(2,1)S(1)} %multiply_convert_fusion), channel_id=1, source_target_pairs={{0,4},{4,0},{8,12},{12,8},{1,5},{5,1},{9,13},{13,9},{2,6},{6,2},{1... | collective-permute-start | bytes 491528 | tf_op jit(solution)/shard_map/ppermute | solution.py:66
  28.8 5.6 %collective-permute-start.8 = (bf16[128,1280]{1,0:T(8,128)(2,1)S(1)}, bf16[128,1280]{1,0:T(8,128)(2,1)S(1)}, u32[]{:S(2)}, u32[]{:S(2)}) collective-permute-start(bf16[128,1280]{1,0:T(8,128)(2,1)S(1)} %constant_dynamic-update-slice_fusion.2), channel_id=1, source_target_pairs={{0,1},{1,0},{2,3},{3,2},{4,5},{5,4},{6,7},{7,6},{8,9},{9,8},{10,11... | collective-permute-start | bytes 983048 | tf_op jit(solution)/shard_map/ppermute | solution.py:80
  31.9 5.8 %collective-permute-start.13 = (bf16[128,640]{1,0:T(8,128)(2,1)S(1)}, bf16[128,640]{1,0:T(8,128)(2,1)S(1)}, u32[]{:S(2)}, u32[]{:S(2)}) collective-permute-start(bf16[128,640]{1,0:T(8,128)(2,1)S(1)} %collective-permute-done.12), channel_id=1, source_target_pairs={{0,2},{1,3},{2,0},{3,1},{4,6},{5,7},{6,4},{7,5},{8,10},{9,11},{10,... | collective-permute-start | bytes 491528 | tf_op jit(solution)/shard_map/ppermute | solution.py:79
  35.9 1.8 %copy-start.17 = (bf16[128,512]{1,0:T(8,128)(2,1)}, bf16[128,512]{1,0:T(8,128)(2,1)S(1)}, u32[]{:S(2)}) copy-start(bf16[128,512]{1,0:T(8,128)(2,1)S(1)} %fusion.4) | copy-start | bytes 393220
  37.0 5.1 %collective-permute-start.9 = (bf16[128,1280]{1,0:T(8,128)(2,1)}, bf16[128,1280]{1,0:T(8,128)(2,1)}, u32[]{:S(2)}, u32[]{:S(2)}) collective-permute-start(bf16[128,1280]{1,0:T(8,128)(2,1)} %convolution_convert_fusion.4), channel_id=1, source_target_pairs={{0,1},{1,0},{2,3},{3,2},{4,5},{5,4},{6,7},{7,6},{8,9},{9,8},{10,11... | collective-permute-start | bytes 983048 | tf_op jit(solution)/shard_map/ppermute | solution.py:91
  38.4 5.4 %collective-permute-start.14 = (bf16[128,1280]{1,0:T(8,128)(2,1)}, bf16[128,1280]{1,0:T(8,128)(2,1)}, u32[]{:S(2)}, u32[]{:S(2)}) collective-permute-start(bf16[128,1280]{1,0:T(8,128)(2,1)} %constant_dynamic-update-slice_fusion.4), channel_id=1, source_target_pairs={{0,1},{1,0},{2,3},{3,2},{4,5},{5,4},{6,7},{7,6},{8,9},{9,8},{10,11... | collective-permute-start | bytes 983048 | tf_op jit(solution)/shard_map/ppermute | solution.py:80
  38.9 10.9 %collective-permute-start.18 = (bf16[128,640]{1,0:T(8,128)(2,1)S(1)}, bf16[128,640]{1,0:T(8,128)(2,1)}, u32[]{:S(2)}, u32[]{:S(2)}) collective-permute-start(bf16[128,640]{1,0:T(8,128)(2,1)S(1)} %multiply_convert_fusion), channel_id=1, source_target_pairs={{0,2},{1,3},{2,0},{3,1},{4,6},{5,7},{6,4},{7,5},{8,10},{9,11},{10,... | collective-permute-start | bytes 491528 | tf_op jit(solution)/shard_map/ppermute | solution.py:79
  40.9 3.0 %copy-start.4 = (bf16[640,512]{1,0:T(8,128)(2,1)S(1)}, bf16[640,512]{1,0:T(8,128)(2,1)}, u32[]{:S(2)}) copy-start(bf16[640,512]{1,0:T(8,128)(2,1)} %copy-done.3) | copy-start | bytes 1966084
  40.9 3.0 %copy-start.6 = (bf16[640,512]{1,0:T(8,128)(2,1)S(1)}, bf16[640,512]{1,0:T(8,128)(2,1)}, u32[]{:S(2)}) copy-start(bf16[640,512]{1,0:T(8,128)(2,1)} %copy-done.5) | copy-start | bytes 1966084
  40.9 10.4 %collective-permute-start.4 = (bf16[128,640]{1,0:T(8,128)(2,1)S(1)}, bf16[128,640]{1,0:T(8,128)(2,1)S(1)}, u32[]{:S(2)}, u32[]{:S(2)}) collective-permute-start(bf16[128,640]{1,0:T(8,128)(2,1)S(1)} %slice.87), channel_id=1, source_target_pairs={{0,2},{1,3},{2,0},{3,1},{4,6},{5,7},{6,4},{7,5},{8,10},{9,11},{10,... | collective-permute-start | bytes 491528 | tf_op jit(solution)/shard_map/ppermute | solution.py:93
  43.8 1.4 %copy-start.2 = (bf16[640,512]{1,0:T(8,128)(2,1)S(1)}, bf16[640,512]{1,0:T(8,128)(2,1)}, u32[]{:S(2)}) copy-start(bf16[640,512]{1,0:T(8,128)(2,1)} %copy-done.1) | copy-start | bytes 1966084
  47.9 1.5 %copy-start.12 = (bf16[512,640]{1,0:T(8,128)(2,1)S(1)}, bf16[512,640]{1,0:T(8,128)(2,1)}, u32[]{:S(2)}) copy-start(bf16[512,640]{1,0:T(8,128)(2,1)} %copy-done.11) | copy-start | bytes 1966084
  47.9 1.5 %copy-start.14 = (bf16[512,640]{1,0:T(8,128)(2,1)S(1)}, bf16[512,640]{1,0:T(8,128)(2,1)}, u32[]{:S(2)}) copy-start(bf16[512,640]{1,0:T(8,128)(2,1)} %copy-done.13) | copy-start | bytes 1966084
  49.4 2.0 %copy-start.15 = (f32[128,1280]{1,0:T(8,128)S(1)}, f32[128,1280]{1,0:T(8,128)}, u32[]{:S(2)}) copy-start(f32[128,1280]{1,0:T(8,128)} %convert_add_fusion.3) | copy-start | bytes 1966084
  49.7 5.6 %copy-start.8 = (bf16[512,640]{1,0:T(8,128)(2,1)S(1)}, bf16[512,640]{1,0:T(8,128)(2,1)}, u32[]{:S(2)}) copy-start(bf16[512,640]{1,0:T(8,128)(2,1)} %copy-done.7) | copy-start | bytes 1966084
  49.7 5.6 %copy-start.10 = (bf16[512,640]{1,0:T(8,128)(2,1)S(1)}, bf16[512,640]{1,0:T(8,128)(2,1)}, u32[]{:S(2)}) copy-start(bf16[512,640]{1,0:T(8,128)(2,1)} %copy-done.9) | copy-start | bytes 1966084
  49.7 5.6 %collective-permute-start.15 = (bf16[128,1280]{1,0:T(8,128)(2,1)S(1)}, bf16[128,1280]{1,0:T(8,128)(2,1)S(1)}, u32[]{:S(2)}, u32[]{:S(2)}) collective-permute-start(bf16[128,1280]{1,0:T(8,128)(2,1)S(1)} %convolution_convert_fusion.2), channel_id=1, source_target_pairs={{0,1},{1,0},{2,3},{3,2},{4,5},{5,4},{6,7},{7,6},{8,9},{9,8},{10,11... | collective-permute-start | bytes 983048 | tf_op jit(solution)/shard_map/ppermute | solution.py:91
  50.9 4.8 %collective-permute-start.19 = (bf16[128,1280]{1,0:T(8,128)(2,1)S(1)}, bf16[128,1280]{1,0:T(8,128)(2,1)S(1)}, u32[]{:S(2)}, u32[]{:S(2)}) collective-permute-start(bf16[128,1280]{1,0:T(8,128)(2,1)S(1)} %pad_maximum_fusion.6), channel_id=1, source_target_pairs={{0,1},{1,0},{2,3},{3,2},{4,5},{5,4},{6,7},{7,6},{8,9},{9,8},{10,11... | collective-permute-start | bytes 983048 | tf_op jit(solution)/shard_map/ppermute | solution.py:80
  51.4 15.7 %collective-permute-start.5 = (bf16[128,640]{1,0:T(8,128)(2,1)S(1)}, bf16[128,640]{1,0:T(8,128)(2,1)S(1)}, u32[]{:S(2)}, u32[]{:S(2)}) collective-permute-start(bf16[128,640]{1,0:T(8,128)(2,1)S(1)} %fusion.12), channel_id=1, source_target_pairs={{0,8},{4,12},{8,0},{12,4},{1,9},{5,13},{9,1},{13,5},{2,10},{6,14},... | collective-permute-start | bytes 491528 | tf_op jit(solution)/shard_map/ppermute | solution.py:98
  54.1 7.2 %collective-permute-start.10 = (bf16[128,640]{1,0:T(8,128)(2,1)S(1)}, bf16[128,640]{1,0:T(8,128)(2,1)S(1)}, u32[]{:S(2)}, u32[]{:S(2)}) collective-permute-start(bf16[128,640]{1,0:T(8,128)(2,1)S(1)} %slice.86), channel_id=1, source_target_pairs={{0,2},{1,3},{2,0},{3,1},{4,6},{5,7},{6,4},{7,5},{8,10},{9,11},{10,... | collective-permute-start | bytes 491528 | tf_op jit(solution)/shard_map/ppermute | solution.py:93
  56.4 7.2 %collective-permute-start.16 = (bf16[128,640]{1,0:T(8,128)(2,1)S(1)}, bf16[128,640]{1,0:T(8,128)(2,1)S(1)}, u32[]{:S(2)}, u32[]{:S(2)}) collective-permute-start(bf16[128,640]{1,0:T(8,128)(2,1)S(1)} %slice.85), channel_id=1, source_target_pairs={{0,2},{1,3},{2,0},{3,1},{4,6},{5,7},{6,4},{7,5},{8,10},{9,11},{10,... | collective-permute-start | bytes 491528 | tf_op jit(solution)/shard_map/ppermute | solution.py:93
  58.4 6.8 %collective-permute-start.20 = (bf16[128,1280]{1,0:T(8,128)(2,1)S(1)}, bf16[128,1280]{1,0:T(8,128)(2,1)S(1)}, u32[]{:S(2)}, u32[]{:S(2)}) collective-permute-start(bf16[128,1280]{1,0:T(8,128)(2,1)S(1)} %convolution_convert_fusion), channel_id=1, source_target_pairs={{0,1},{1,0},{2,3},{3,2},{4,5},{5,4},{6,7},{7,6},{8,9},{9,8},{10,11... | collective-permute-start | bytes 983048 | tf_op jit(solution)/shard_map/ppermute | solution.py:91
  61.3 7.7 %collective-permute-start.11 = (bf16[128,640]{1,0:T(8,128)(2,1)S(1)}, bf16[128,640]{1,0:T(8,128)(2,1)S(1)}, u32[]{:S(2)}, u32[]{:S(2)}) collective-permute-start(bf16[128,640]{1,0:T(8,128)(2,1)S(1)} %fusion.11), channel_id=1, source_target_pairs={{0,12},{4,8},{8,4},{12,0},{1,13},{5,9},{9,5},{13,1},{2,14},{6,10},... | collective-permute-start | bytes 491528 | tf_op jit(solution)/shard_map/ppermute | solution.py:98
  63.7 3.4 %copy-start.16 = (s32[128,1]{0,1:T(1,128)S(1)}, s32[128,1]{0,1:T(1,128)}, u32[]{:S(2)}) copy-start(s32[128,1]{0,1:T(1,128)} %param.8) | copy-start | bytes 1540
  63.7 7.0 %collective-permute-start.17 = (bf16[128,640]{1,0:T(8,128)(2,1)S(1)}, bf16[128,640]{1,0:T(8,128)(2,1)S(1)}, u32[]{:S(2)}, u32[]{:S(2)}) collective-permute-start(bf16[128,640]{1,0:T(8,128)(2,1)S(1)} %fusion.10), channel_id=1, source_target_pairs={{0,4},{4,0},{8,12},{12,8},{1,5},{5,1},{9,13},{13,9},{2,6},{6,2},{1... | collective-permute-start | bytes 491528 | tf_op jit(solution)/shard_map/ppermute | solution.py:98
  65.6 5.4 %collective-permute-start.21 = (bf16[128,640]{1,0:T(8,128)(2,1)S(1)}, bf16[128,640]{1,0:T(8,128)(2,1)S(1)}, u32[]{:S(2)}, u32[]{:S(2)}) collective-permute-start(bf16[128,640]{1,0:T(8,128)(2,1)S(1)} %slice.84), channel_id=1, source_target_pairs={{0,2},{1,3},{2,0},{3,1},{4,6},{5,7},{6,4},{7,5},{8,10},{9,11},{10,... | collective-permute-start | bytes 491528 | tf_op jit(solution)/shard_map/ppermute | solution.py:93

commit v20 on v18

--- a/solution.py
+++ b/solution.py
@@ -71,8 +71,23 @@
     down_keep = _slots(down_weight[0], t, width, 1, _ORDER[:2])
     down_send = _slots(down_weight[0], t, width, 1, _ORDER[2:])
     waves = [[k] for k in list(range(2, n_expert)) + [1][:n_expert - 1] + [0]]
+    def returned(keep, send, wave, total):
+        over_c = keep.astype(jnp.float32) + lax.ppermute(
+            send, "tensor", _xor_pairs(n_tensor, 1)).astype(jnp.float32)
+        summed = over_c[:, :width] + lax.ppermute(
+            over_c[:, width:].astype(jnp.bfloat16), "tensor", _xor_pairs(n_tensor, 2)).astype(jnp.float32)
+        for i, k in enumerate(wave):
+            part = summed[i * tok_rows:(i + 1) * tok_rows]
+            if k:
+                part = lax.ppermute(
+                    part.astype(jnp.bfloat16), "expert", _xor_pairs(n_expert, k)).astype(jnp.float32)
+            part = jnp.where(routed == (me ^ k) // SPAN, part, 0.0)
+            total = part if total is None else total + part
+        return total
+
     total = None
     previous = None
+    pending = None
     for wave in waves:
         piece = jnp.concatenate([blocks[k] for k in wave])
         pair = jnp.concatenate(
@@ -87,17 +102,13 @@
         keep = jnp.dot(hidden, down_keep, preferred_element_type=jnp.float32).astype(jnp.bfloat16)
         send = jnp.dot(hidden, down_send, preferred_element_type=jnp.float32).astype(jnp.bfloat16)
         previous = keep
-        over_c = keep.astype(jnp.float32) + lax.ppermute(
-            send, "tensor", _xor_pairs(n_tensor, 1)).astype(jnp.float32)
-        summed = over_c[:, :width] + lax.ppermute(
-            over_c[:, width:].astype(jnp.bfloat16), "tensor", _xor_pairs(n_tensor, 2)).astype(jnp.float32)
-        for i, k in enumerate(wave):
-            part = summed[i * tok_rows:(i + 1) * tok_rows]
-            if k:
-                part = lax.ppermute(
-                    part.astype(jnp.bfloat16), "expert", _xor_pairs(n_expert, k)).astype(jnp.float32)
-            part = jnp.where(routed == (me ^ k) // SPAN, part, 0.0)
-            total = part if total is None else total + part
+        if len(waves) > 1 and wave is waves[-2]:
+            pending = (keep, send)
+            continue
+        if pending is not None:
+            (held_keep, held_send), _ = lax.optimization_barrier((pending, keep))
+            total = returned(held_keep, held_send, waves[-2], total)
+        total = returned(keep, send, wave, total)
     return total.astype(jnp.bfloat16)
 
 

time: 64.5 us -> 67 us (1.039)
  waiting for transfers between devices: 18.2 us -> 27.4 us
  other arithmetic: 8.86 us -> 2.54 us
  local copies, waits for them, and re-layouts: 6.68 us -> 4.57 us
  starting transfers between devices: 22.3 us -> 24.3 us
    ppermute x11, waiting for transfers between devices: 9.65 us -> 15 us  [the longest x4 8.57 us: returned(): lax.ppermute(over_c[:, width:].astype(jnp.bfloat16), 'tensor', _xor_pairs...]
    concatenate x4, other arithmetic: 3.76 us -> 0.1 us  [gathered(): jnp.concatenate([piece, lax.ppermute(piece, 'tensor', _xor_pairs(n_tensor...]
    ppermute x4, waiting for transfers between devices: 5.23 us -> 8.05 us  [gathered(): lax.ppermute(piece, 'tensor', _xor_pairs(n_tensor, 2))]
    concatenate x3, other arithmetic: 2.89 us -> 0.14 us  [gathered(): jnp.concatenate([pair, lax.ppermute(pair, 'tensor', _xor_pairs(n_tensor,...]
    ppermute x11, starting transfers between devices: 10.9 us -> 12.9 us  [the longest x3 5.81 us: returned(): lax.ppermute(part.astype(jnp.bfloat16), 'expert', _xor_pairs(n_expert, k))]
    dynamic_slice x3, local copies, waits for them, and re-layouts: 3.54 us -> 2.39 us  [_slots(): lax.dynamic_slice_in_dim(weight, (t ^ k) * width, width, axis=axis)]
    ppermute x3, waiting for transfers between devices: 3.32 us -> 4.35 us  [gathered(): lax.ppermute(scaled, 'expert', _xor_pairs(n_expert, k))]
    unnamed x14 -> x8, local copies, waits for them, and re-layouts: 3.03 us -> 2.07 us
  transfers between devices with their start and end apart: 22 -> 22, of which waited for: 9 -> 11; matrix products, arithmetic and copies ran while one was open for 30% -> 11% of each run, Pallas kernels for 0% -> 0%
where the time goes in v20:
time: 67 us; the launch traced here: 66.9 us
  waiting for transfers between devices  27.4 us (41%)
  starting transfers between devices  24.3 us (36%)
  matrix products  7.73 us (12%)
  local copies, waits for them, and re-layouts  4.57 us (7%)
  other arithmetic  2.54 us (4%)
    ppermute x4, waiting for transfers between devices, returned(): lax.ppermute(over_c[:, width:].astype(jnp.bfloat16), 'tensor', _xor_pairs...  8.57 us
    ppermute x4, waiting for transfers between devices, gathered(): lax.ppermute(piece, 'tensor', _xor_pairs(n_tensor, 2))  8.05 us
    ppermute x3, starting transfers between devices, returned(): lax.ppermute(part.astype(jnp.bfloat16), 'expert', _xor_pairs(n_expert, k))  5.81 us
    ppermute x3, starting transfers between devices, gathered(): lax.ppermute(scaled, 'expert', _xor_pairs(n_expert, k))  5.68 us
    ppermute x4, starting transfers between devices, returned(): lax.ppermute(over_c[:, width:].astype(jnp.bfloat16), 'tensor', _xor_pairs...  5.56 us
    ppermute x4, starting transfers between devices, gathered(): lax.ppermute(piece, 'tensor', _xor_pairs(n_tensor, 2))  5.42 us
    ppermute x3, waiting for transfers between devices, gathered(): lax.ppermute(scaled, 'expert', _xor_pairs(n_expert, k))  4.35 us
    ppermute x3, waiting for transfers between devices, returned(): lax.ppermute(part.astype(jnp.bfloat16), 'expert', _xor_pairs(n_expert, k))  3.98 us
  transfers between devices with their start and end apart: 22, of which 11 were waited for; matrix products, arithmetic and copies ran while one was open for 11% of the time, Pallas kernels for 0%

profile of v20, /device:TPU:0, one launch (start us, length us, event | category | flops | bytes accessed | tf_op | source)
XLA Modules:
  0.0 66.9 jit_solution(16954393659860731893)
XLA Ops:
  0.0 1.0 %multiply_convert_fusion = bf16[128,640]{1,0:T(8,128)(2,1)S(1)} fusion(bf16[128,640]{1,0:T(8,128)(2,1)} %param.6, f32[128]{0:T(128)} %param.7), kind=kLoop, calls=%fused_computation.55 | loop fusion | flops 245760 | bytes 328192 | tf_op jit(solution)/shard_map/convert_element_type | solution.py:64
  1.0 4.1 %collective-permute-start = (bf16[128,640]{1,0:T(8,128)(2,1)S(1)}, bf16[128,640]{1,0:T(8,128)(2,1)S(1)}, u32[]{:S(2)}, u32[]{:S(2)}) collective-permute-start(bf16[128,640]{1,0:T(8,128)(2,1)S(1)} %multiply_convert_fusion), channel_id=1, source_target_pairs={{0,8},{4,12},{8,0},{12,4},{1,9},{5,13},{9,1},{13,5},{2,10},{6,14},... | collective-permute-start | bytes 491528 | tf_op jit(solution)/shard_map/ppermute | solution.py:66
  5.1 1.3 %collective-permute-start.6 = (bf16[128,640]{1,0:T(8,128)(2,1)S(1)}, bf16[128,640]{1,0:T(8,128)(2,1)S(1)}, u32[]{:S(2)}, u32[]{:S(2)}) collective-permute-start(bf16[128,640]{1,0:T(8,128)(2,1)S(1)} %multiply_convert_fusion), channel_id=1, source_target_pairs={{0,12},{4,8},{8,4},{12,0},{1,13},{5,9},{9,5},{13,1},{2,14},{6,10},... | collective-permute-start | bytes 491528 | tf_op jit(solution)/shard_map/ppermute | solution.py:66
  6.7 1.5 %collective-permute-start.15 = (bf16[128,640]{1,0:T(8,128)(2,1)S(1)}, bf16[128,640]{1,0:T(8,128)(2,1)S(1)}, u32[]{:S(2)}, u32[]{:S(2)}) collective-permute-start(bf16[128,640]{1,0:T(8,128)(2,1)S(1)} %multiply_convert_fusion), channel_id=1, source_target_pairs={{0,2},{1,3},{2,0},{3,1},{4,6},{5,7},{6,4},{7,5},{8,10},{9,11},{10,... | collective-permute-start | bytes 491528 | tf_op jit(solution)/shard_map/ppermute | solution.py:94
  8.2 2.0 %dynamic-slice_bitcast_fusion.11 = (bf16[640,512]{1,0:T(8,128)(2,1)S(1)}, bf16[640,512]{1,0:T(8,128)(2,1)S(1)}, bf16[640,512]{1,0:T(8,128)(2,1)S(1)}, bf16[640,512]{1,0:T(8,128)(2,1)S(1)}) fusion(bf16[1,2560,512]{2,1,0:T(8,128)(2,1)} %param.9, s32[]{:T(128)S(6)} %select_n.48, s32[]{:T(128)S(6)} %select_n.49, s32[]{:T(128)S(6)} %select_n.51, s32[]{:T(128)S(6)} %select_n.50), kind=kLoop, calls=%fused_computation.36 | loop fusion | bytes 5242896 | tf_op jit(solution)/shard_map/dynamic_slice | solution.py:55
  10.2 0.5 copy-done
  11.1 1.5 %copy-done.1 = bf16[1,512,2560]{2,1,0:T(8,128)(2,1)S(1)} copy-done((bf16[1,512,2560]{2,1,0:T(8,128)(2,1)S(1)}, bf16[1,512,2560]{2,1,0:T(8,128)(2,1)}, u32[]{:S(2)}) %copy-start.1) | copy-done | bytes 2621464
  12.9 4.3 %collective-permute-done = bf16[128,640]{1,0:T(8,128)(2,1)S(1)} collective-permute-done((bf16[128,640]{1,0:T(8,128)(2,1)S(1)}, bf16[128,640]{1,0:T(8,128)(2,1)S(1)}, u32[]{:S(2)}, u32[]{:S(2)}) %collective-permute-start) | collective-permute-done | bytes 163872 | tf_op jit(solution)/shard_map/ppermute | solution.py:66
  17.2 1.8 %collective-permute-start.1 = (bf16[128,640]{1,0:T(8,128)(2,1)S(1)}, bf16[128,640]{1,0:T(8,128)(2,1)S(1)}, u32[]{:S(2)}, u32[]{:S(2)}) collective-permute-start(bf16[128,640]{1,0:T(8,128)(2,1)S(1)} %collective-permute-done), channel_id=1, source_target_pairs={{0,2},{1,3},{2,0},{3,1},{4,6},{5,7},{6,4},{7,5},{8,10},{9,11},{10,... | collective-permute-start | bytes 491528 | tf_op jit(solution)/shard_map/ppermute | solution.py:94
  19.2 0.3 collective-permute-start.7
  19.4 1.8 %collective-permute-start.13 = (bf16[128,640]{1,0:T(8,128)(2,1)S(1)}, bf16[128,640]{1,0:T(8,128)(2,1)S(1)}, u32[]{:S(2)}, u32[]{:S(2)}) collective-permute-start(bf16[128,640]{1,0:T(8,128)(2,1)S(1)} %collective-permute-done.12), channel_id=1, source_target_pairs={{0,2},{1,3},{2,0},{3,1},{4,6},{5,7},{6,4},{7,5},{8,10},{9,11},{10,... | collective-permute-start | bytes 491528 | tf_op jit(solution)/shard_map/ppermute | solution.py:94
  21.3 2.4 %collective-permute-done.1 = bf16[128,640]{1,0:T(8,128)(2,1)S(1)} collective-permute-done((bf16[128,640]{1,0:T(8,128)(2,1)S(1)}, bf16[128,640]{1,0:T(8,128)(2,1)S(1)}, u32[]{:S(2)}, u32[]{:S(2)}) %collective-permute-start.1) | collective-permute-done | bytes 163872 | tf_op jit(solution)/shard_map/ppermute | solution.py:94
  23.7 3.3 %collective-permute-done.7 = bf16[128,640]{1,0:T(8,128)(2,1)S(1)} collective-permute-done((bf16[128,640]{1,0:T(8,128)(2,1)S(1)}, bf16[128,640]{1,0:T(8,128)(2,1)S(1)}, u32[]{:S(2)}, u32[]{:S(2)}) %collective-permute-start.7) | collective-permute-done | bytes 163872 | tf_op jit(solution)/shard_map/ppermute | solution.py:94
  27.2 2.4 %collective-permute-done.13 = bf16[128,640]{1,0:T(8,128)(2,1)S(1)} collective-permute-done((bf16[128,640]{1,0:T(8,128)(2,1)S(1)}, bf16[128,640]{1,0:T(8,128)(2,1)S(1)}, u32[]{:S(2)}, u32[]{:S(2)}) %collective-permute-start.13) | collective-permute-done | bytes 163872 | tf_op jit(solution)/shard_map/ppermute | solution.py:94
  29.8 0.5 fusion.10
  30.3 0.7 %multiply_convert_fusion.1 = bf16[128,512]{1,0:T(8,128)(2,1)S(1)} fusion(f32[128,512]{1,0:T(8,128)S(1)} %fusion.10, bf16[128,2560]{1,0:T(8,128)(2,1)S(1)} %constant_dynamic-update-slice_fusion, bf16[640,512]{1,0:T(8,128)(2,1)S(1)} %get-tuple-element.21, bf16[640,512]{1,0:T(8,128)(2,1)S(1)} %get-tuple-element.22, ...), kind=kOutput, calls=%fused_computation.56 | convolution fusion | flops 346423296 | bytes 3670016 | tf_op jit(solution)/shard_map/dot_general | solution.py:100
  31.0 0.3 convolution_convert_fusion.6
  31.4 0.6 collective-permute-start.3
  32.0 1.2 %collective-permute-done.3 = bf16[128,1280]{1,0:T(8,128)(2,1)S(1)} collective-permute-done((bf16[128,1280]{1,0:T(8,128)(2,1)S(1)}, bf16[128,1280]{1,0:T(8,128)(2,1)S(1)}, u32[]{:S(2)}, u32[]{:S(2)}) %collective-permute-start.3) | collective-permute-done | bytes 327712 | tf_op jit(solution)/shard_map/ppermute | solution.py:75
  33.2 0.3 convert_add_fusion.3
  33.6 0.5 fusion.11
  34.1 0.7 %fusion = bf16[128,512]{1,0:T(8,128)(2,1)S(1)} fusion(bf16[128,2560]{1,0:T(8,128)(2,1)S(1)} %pad_maximum_fusion.4, f32[128,512]{1,0:T(8,128)S(1)} %fusion.11, bf16[640,512]{1,0:T(8,128)(2,1)S(1)} %get-tuple-element.21, bf16[640,512]{1,0:T(8,128)(2,1)S(1)} %get-tuple-element.22, bf16[640,512]{1,0:T(8,128)(2,1)S(1)} %get-tuple-element.20, ...), kind=kOutput, calls=%fused_computation.15 | convolution fusion | flops 346423296 | bytes 3670016 | tf_op jit(solution)/shard_map/dot_general | solution.py:100
  34.8 0.3 convolution_convert_fusion.4
  35.2 0.4 collective-permute-start.9
  35.7 1.2 %collective-permute-done.9 = bf16[128,1280]{1,0:T(8,128)(2,1)S(1)} collective-permute-done((bf16[128,1280]{1,0:T(8,128)(2,1)S(1)}, bf16[128,1280]{1,0:T(8,128)(2,1)S(1)}, u32[]{:S(2)}, u32[]{:S(2)}) %collective-permute-start.9) | collective-permute-done | bytes 327712 | tf_op jit(solution)/shard_map/ppermute | solution.py:75
  36.9 0.3 convert_add_fusion.2
  37.2 0.5 fusion.12
  37.7 0.7 %fusion.1 = bf16[128,512]{1,0:T(8,128)(2,1)S(1)} fusion(bf16[128,2560]{1,0:T(8,128)(2,1)S(1)} %pad_maximum_fusion.5, f32[128,512]{1,0:T(8,128)S(1)} %fusion.12, bf16[640,512]{1,0:T(8,128)(2,1)S(1)} %get-tuple-element.21, bf16[640,512]{1,0:T(8,128)(2,1)S(1)} %get-tuple-element.22, bf16[640,512]{1,0:T(8,128)(2,1)S(1)} %get-tuple-element.20, ...), kind=kOutput, calls=%fused_computation.16 | convolution fusion | flops 346423296 | bytes 3670016 | tf_op jit(solution)/shard_map/dot_general | solution.py:100
  38.5 0.3 convolution_convert_fusion.3
  38.8 0.5 fusion.13
  39.3 0.7 %fusion.2 = bf16[128,512]{1,0:T(8,128)(2,1)S(1)} fusion(bf16[128,2560]{1,0:T(8,128)(2,1)S(1)} %pad_maximum_fusion.6, f32[128,512]{1,0:T(8,128)S(1)} %fusion.13, bf16[640,512]{1,0:T(8,128)(2,1)S(1)} %get-tuple-element.21, bf16[640,512]{1,0:T(8,128)(2,1)S(1)} %get-tuple-element.22, bf16[640,512]{1,0:T(8,128)(2,1)S(1)} %get-tuple-element.20, ...), kind=kOutput, calls=%fused_computation.17 | convolution fusion | flops 346423296 | bytes 3670016 | tf_op jit(solution)/shard_map/dot_general | solution.py:100
  40.1 0.3 convolution_convert_fusion
  40.4 0.4 collective-permute-start.20
  40.9 1.8 %collective-permute-start.4 = (bf16[128,640]{1,0:T(8,128)(2,1)S(1)}, bf16[128,640]{1,0:T(8,128)(2,1)S(1)}, u32[]{:S(2)}, u32[]{:S(2)}) collective-permute-start(bf16[128,640]{1,0:T(8,128)(2,1)S(1)} %slice.67), channel_id=1, source_target_pairs={{0,2},{1,3},{2,0},{3,1},{4,6},{5,7},{6,4},{7,5},{8,10},{9,11},{10,... | collective-permute-start | bytes 491528 | tf_op jit(solution)/shard_map/ppermute | solution.py:77
  42.7 0.3 convolution_convert_fusion.2
  43.1 0.4 convert_add_fusion
  43.6 3.6 %collective-permute-done.4 = bf16[128,640]{1,0:T(8,128)(2,1)S(1)} collective-permute-done((bf16[128,640]{1,0:T(8,128)(2,1)S(1)}, bf16[128,640]{1,0:T(8,128)(2,1)S(1)}, u32[]{:S(2)}, u32[]{:S(2)}) %collective-permute-start.4) | collective-permute-done | bytes 163872 | tf_op jit(solution)/shard_map/ppermute | solution.py:77
  47.3 2.7 %collective-permute-start.5 = (bf16[128,640]{1,0:T(8,128)(2,1)S(1)}, bf16[128,640]{1,0:T(8,128)(2,1)S(1)}, u32[]{:S(2)}, u32[]{:S(2)}) collective-permute-start(bf16[128,640]{1,0:T(8,128)(2,1)S(1)} %fusion.8), channel_id=1, source_target_pairs={{0,8},{4,12},{8,0},{12,4},{1,9},{5,13},{9,1},{13,5},{2,10},{6,14},... | collective-permute-start | bytes 491528 | tf_op jit(solution)/shard_map/ppermute | solution.py:82
  50.0 1.6 %collective-permute-start.10 = (bf16[128,640]{1,0:T(8,128)(2,1)S(1)}, bf16[128,640]{1,0:T(8,128)(2,1)S(1)}, u32[]{:S(2)}, u32[]{:S(2)}) collective-permute-start(bf16[128,640]{1,0:T(8,128)(2,1)S(1)} %slice.66), channel_id=1, source_target_pairs={{0,2},{1,3},{2,0},{3,1},{4,6},{5,7},{6,4},{7,5},{8,10},{9,11},{10,... | collective-permute-start | bytes 491528 | tf_op jit(solution)/shard_map/ppermute | solution.py:77
  51.6 0.6 collective-permute-start.18
  52.2 4.7 %collective-permute-done.10 = bf16[128,640]{1,0:T(8,128)(2,1)S(1)} collective-permute-done((bf16[128,640]{1,0:T(8,128)(2,1)S(1)}, bf16[128,640]{1,0:T(8,128)(2,1)S(1)}, u32[]{:S(2)}, u32[]{:S(2)}) %collective-permute-start.10) | collective-permute-done | bytes 163872 | tf_op jit(solution)/shard_map/ppermute | solution.py:77
  57.0 1.2 %collective-permute-start.11 = (bf16[128,640]{1,0:T(8,128)(2,1)S(1)}, bf16[128,640]{1,0:T(8,128)(2,1)S(1)}, u32[]{:S(2)}, u32[]{:S(2)}) collective-permute-start(bf16[128,640]{1,0:T(8,128)(2,1)S(1)} %fusion.7), channel_id=1, source_target_pairs={{0,12},{4,8},{8,4},{12,0},{1,13},{5,9},{9,5},{13,1},{2,14},{6,10},... | collective-permute-start | bytes 491528 | tf_op jit(solution)/shard_map/ppermute | solution.py:82
  58.2 1.6 %collective-permute-start.21 = (bf16[128,640]{1,0:T(8,128)(2,1)S(1)}, bf16[128,640]{1,0:T(8,128)(2,1)S(1)}, u32[]{:S(2)}, u32[]{:S(2)}) collective-permute-start(bf16[128,640]{1,0:T(8,128)(2,1)S(1)} %slice.64), channel_id=1, source_target_pairs={{0,2},{1,3},{2,0},{3,1},{4,6},{5,7},{6,4},{7,5},{8,10},{9,11},{10,... | collective-permute-start | bytes 491528 | tf_op jit(solution)/shard_map/ppermute | solution.py:77
  59.8 0.2 collective-permute-done.18
  60.1 1.9 %collective-permute-start.19 = (bf16[128,640]{1,0:T(8,128)(2,1)S(1)}, bf16[128,640]{1,0:T(8,128)(2,1)S(1)}, u32[]{:S(2)}, u32[]{:S(2)}) collective-permute-start(bf16[128,640]{1,0:T(8,128)(2,1)S(1)} %fusion.6), channel_id=1, source_target_pairs={{0,4},{4,0},{8,12},{12,8},{1,5},{5,1},{9,13},{13,9},{2,6},{6,2},{1... | collective-permute-start | bytes 491528 | tf_op jit(solution)/shard_map/ppermute | solution.py:82
  62.0 2.3 %collective-permute-done.11 = bf16[128,640]{1,0:T(8,128)(2,1)S(1)} collective-permute-done((bf16[128,640]{1,0:T(8,128)(2,1)S(1)}, bf16[128,640]{1,0:T(8,128)(2,1)S(1)}, u32[]{:S(2)}, u32[]{:S(2)}) %collective-permute-start.11) | collective-permute-done | bytes 163872 | tf_op jit(solution)/shard_map/ppermute | solution.py:82
  64.3 1.7 %collective-permute-done.19 = bf16[128,640]{1,0:T(8,128)(2,1)S(1)} collective-permute-done((bf16[128,640]{1,0:T(8,128)(2,1)S(1)}, bf16[128,640]{1,0:T(8,128)(2,1)S(1)}, u32[]{:S(2)}, u32[]{:S(2)}) %collective-permute-start.19) | collective-permute-done | bytes 163872 | tf_op jit(solution)/shard_map/ppermute | solution.py:82
  66.0 0.9 %fusion.5 = bf16[128,640]{1,0:T(8,128)(2,1)} fusion(f32[128,1280]{1,0:T(8,128)S(1)} %convert_add_fusion, bf16[128,640]{1,0:T(8,128)(2,1)S(1)} %collective-permute-done.21, bf16[128,640]{1,0:T(8,128)(2,1)S(1)} %collective-permute-done.19, bf16[128,640]{1,0:T(8,128)(2,1)S(1)} %collective-permute-done.11, bf16[128,640]{1,0:T(8,128)(2,1)S(1)} %collective-permute-done.5, ...), kind=kLoop, calls=%fused_computation.41 | loop fusion | flops 1064960 | bytes 1147392 | tf_op jit(solution)/shard_map/convert_element_type | solution.py:112
  (43 shorter events, 1.8 us)
Async XLA Ops:
  1.0 16.2 %collective-permute-start = (bf16[128,640]{1,0:T(8,128)(2,1)S(1)}, bf16[128,640]{1,0:T(8,128)(2,1)S(1)}, u32[]{:S(2)}, u32[]{:S(2)}) collective-permute-start(bf16[128,640]{1,0:T(8,128)(2,1)S(1)} %multiply_convert_fusion), channel_id=1, source_target_pairs={{0,8},{4,12},{8,0},{12,4},{1,9},{5,13},{9,1},{13,5},{2,10},{6,14},... | collective-permute-start | bytes 491528 | tf_op jit(solution)/shard_map/ppermute | solution.py:66
  5.1 14.0 %collective-permute-start.6 = (bf16[128,640]{1,0:T(8,128)(2,1)S(1)}, bf16[128,640]{1,0:T(8,128)(2,1)S(1)}, u32[]{:S(2)}, u32[]{:S(2)}) collective-permute-start(bf16[128,640]{1,0:T(8,128)(2,1)S(1)} %multiply_convert_fusion), channel_id=1, source_target_pairs={{0,12},{4,8},{8,4},{12,0},{1,13},{5,9},{9,5},{13,1},{2,14},{6,10},... | collective-permute-start | bytes 491528 | tf_op jit(solution)/shard_map/ppermute | solution.py:66
  6.5 13.0 %collective-permute-start.12 = (bf16[128,640]{1,0:T(8,128)(2,1)S(1)}, bf16[128,640]{1,0:T(8,128)(2,1)S(1)}, u32[]{:S(2)}, u32[]{:S(2)}) collective-permute-start(bf16[128,640]{1,0:T(8,128)(2,1)S(1)} %multiply_convert_fusion), channel_id=1, source_target_pairs={{0,4},{4,0},{8,12},{12,8},{1,5},{5,1},{9,13},{13,9},{2,6},{6,2},{1... | collective-permute-start | bytes 491528 | tf_op jit(solution)/shard_map/ppermute | solution.py:66
  6.7 12.4 %collective-permute-start.15 = (bf16[128,640]{1,0:T(8,128)(2,1)S(1)}, bf16[128,640]{1,0:T(8,128)(2,1)S(1)}, u32[]{:S(2)}, u32[]{:S(2)}) collective-permute-start(bf16[128,640]{1,0:T(8,128)(2,1)S(1)} %multiply_convert_fusion), channel_id=1, source_target_pairs={{0,2},{1,3},{2,0},{3,1},{4,6},{5,7},{6,4},{7,5},{8,10},{9,11},{10,... | collective-permute-start | bytes 491528 | tf_op jit(solution)/shard_map/ppermute | solution.py:94
  8.2 2.5 %copy-start = (bf16[1,2560,512]{2,1,0:T(8,128)(2,1)S(1)}, bf16[1,2560,512]{2,1,0:T(8,128)(2,1)}, u32[]{:S(2)}) copy-start(bf16[1,2560,512]{2,1,0:T(8,128)(2,1)} %param.10) | copy-start | bytes 7864324
  10.9 1.7 %copy-start.1 = (bf16[1,512,2560]{2,1,0:T(8,128)(2,1)S(1)}, bf16[1,512,2560]{2,1,0:T(8,128)(2,1)}, u32[]{:S(2)}) copy-start(bf16[1,512,2560]{2,1,0:T(8,128)(2,1)} %param.11) | copy-start | bytes 7864324
  17.2 6.4 %collective-permute-start.1 = (bf16[128,640]{1,0:T(8,128)(2,1)S(1)}, bf16[128,640]{1,0:T(8,128)(2,1)S(1)}, u32[]{:S(2)}, u32[]{:S(2)}) collective-permute-start(bf16[128,640]{1,0:T(8,128)(2,1)S(1)} %collective-permute-done), channel_id=1, source_target_pairs={{0,2},{1,3},{2,0},{3,1},{4,6},{5,7},{6,4},{7,5},{8,10},{9,11},{10,... | collective-permute-start | bytes 491528 | tf_op jit(solution)/shard_map/ppermute | solution.py:94
  19.1 10.6 %collective-permute-start.16 = (bf16[128,1280]{1,0:T(8,128)(2,1)S(1)}, bf16[128,1280]{1,0:T(8,128)(2,1)S(1)}, u32[]{:S(2)}, u32[]{:S(2)}) collective-permute-start(bf16[128,1280]{1,0:T(8,128)(2,1)S(1)} %pad_maximum_fusion.10), channel_id=1, source_target_pairs={{0,1},{1,0},{2,3},{3,2},{4,5},{5,4},{6,7},{7,6},{8,9},{9,8},{10,11... | collective-permute-start | bytes 983048 | tf_op jit(solution)/shard_map/ppermute | solution.py:96
  19.2 7.9 %collective-permute-start.7 = (bf16[128,640]{1,0:T(8,128)(2,1)S(1)}, bf16[128,640]{1,0:T(8,128)(2,1)S(1)}, u32[]{:S(2)}, u32[]{:S(2)}) collective-permute-start(bf16[128,640]{1,0:T(8,128)(2,1)S(1)} %collective-permute-done.6), channel_id=1, source_target_pairs={{0,2},{1,3},{2,0},{3,1},{4,6},{5,7},{6,4},{7,5},{8,10},{9,11},{10,... | collective-permute-start | bytes 491528 | tf_op jit(solution)/shard_map/ppermute | solution.py:94
  19.4 10.1 %collective-permute-start.13 = (bf16[128,640]{1,0:T(8,128)(2,1)S(1)}, bf16[128,640]{1,0:T(8,128)(2,1)S(1)}, u32[]{:S(2)}, u32[]{:S(2)}) collective-permute-start(bf16[128,640]{1,0:T(8,128)(2,1)S(1)} %collective-permute-done.12), channel_id=1, source_target_pairs={{0,2},{1,3},{2,0},{3,1},{4,6},{5,7},{6,4},{7,5},{8,10},{9,11},{10,... | collective-permute-start | bytes 491528 | tf_op jit(solution)/shard_map/ppermute | solution.py:94
  23.7 6.1 %collective-permute-start.2 = (bf16[128,1280]{1,0:T(8,128)(2,1)S(1)}, bf16[128,1280]{1,0:T(8,128)(2,1)S(1)}, u32[]{:S(2)}, u32[]{:S(2)}) collective-permute-start(bf16[128,1280]{1,0:T(8,128)(2,1)S(1)} %pad_maximum_fusion.7), channel_id=1, source_target_pairs={{0,1},{1,0},{2,3},{3,2},{4,5},{5,4},{6,7},{7,6},{8,9},{9,8},{10,11... | collective-permute-start | bytes 983048 | tf_op jit(solution)/shard_map/ppermute | solution.py:96
  27.1 4.8 %collective-permute-start.8 = (bf16[128,1280]{1,0:T(8,128)(2,1)S(1)}, bf16[128,1280]{1,0:T(8,128)(2,1)S(1)}, u32[]{:S(2)}, u32[]{:S(2)}) collective-permute-start(bf16[128,1280]{1,0:T(8,128)(2,1)S(1)} %pad_maximum_fusion.8), channel_id=1, source_target_pairs={{0,1},{1,0},{2,3},{3,2},{4,5},{5,4},{6,7},{7,6},{8,9},{9,8},{10,11... | collective-permute-start | bytes 983048 | tf_op jit(solution)/shard_map/ppermute | solution.py:96
  29.6 6.0 %collective-permute-start.14 = (bf16[128,1280]{1,0:T(8,128)(2,1)S(1)}, bf16[128,1280]{1,0:T(8,128)(2,1)S(1)}, u32[]{:S(2)}, u32[]{:S(2)}) collective-permute-start(bf16[128,1280]{1,0:T(8,128)(2,1)S(1)} %pad_maximum_fusion.9), channel_id=1, source_target_pairs={{0,1},{1,0},{2,3},{3,2},{4,5},{5,4},{6,7},{7,6},{8,9},{9,8},{10,11... | collective-permute-start | bytes 983048 | tf_op jit(solution)/shard_map/ppermute | solution.py:96
  31.4 1.8 %collective-permute-start.3 = (bf16[128,1280]{1,0:T(8,128)(2,1)S(1)}, bf16[128,1280]{1,0:T(8,128)(2,1)S(1)}, u32[]{:S(2)}, u32[]{:S(2)}) collective-permute-start(bf16[128,1280]{1,0:T(8,128)(2,1)S(1)} %convolution_convert_fusion.6), channel_id=1, source_target_pairs={{0,1},{1,0},{2,3},{3,2},{4,5},{5,4},{6,7},{7,6},{8,9},{9,8},{10,11... | collective-permute-start | bytes 983048 | tf_op jit(solution)/shard_map/ppermute | solution.py:75
  35.2 1.7 %collective-permute-start.9 = (bf16[128,1280]{1,0:T(8,128)(2,1)S(1)}, bf16[128,1280]{1,0:T(8,128)(2,1)S(1)}, u32[]{:S(2)}, u32[]{:S(2)}) collective-permute-start(bf16[128,1280]{1,0:T(8,128)(2,1)S(1)} %convolution_convert_fusion.4), channel_id=1, source_target_pairs={{0,1},{1,0},{2,3},{3,2},{4,5},{5,4},{6,7},{7,6},{8,9},{9,8},{10,11... | collective-permute-start | bytes 983048 | tf_op jit(solution)/shard_map/ppermute | solution.py:75
  40.4 2.6 %collective-permute-start.20 = (bf16[128,1280]{1,0:T(8,128)(2,1)S(1)}, bf16[128,1280]{1,0:T(8,128)(2,1)S(1)}, u32[]{:S(2)}, u32[]{:S(2)}) collective-permute-start(bf16[128,1280]{1,0:T(8,128)(2,1)S(1)} %convolution_convert_fusion), channel_id=1, source_target_pairs={{0,1},{1,0},{2,3},{3,2},{4,5},{5,4},{6,7},{7,6},{8,9},{9,8},{10,11... | collective-permute-start | bytes 983048 | tf_op jit(solution)/shard_map/ppermute | solution.py:75
  40.9 6.3 %collective-permute-start.4 = (bf16[128,640]{1,0:T(8,128)(2,1)S(1)}, bf16[128,640]{1,0:T(8,128)(2,1)S(1)}, u32[]{:S(2)}, u32[]{:S(2)}) collective-permute-start(bf16[128,640]{1,0:T(8,128)(2,1)S(1)} %slice.67), channel_id=1, source_target_pairs={{0,2},{1,3},{2,0},{3,1},{4,6},{5,7},{6,4},{7,5},{8,10},{9,11},{10,... | collective-permute-start | bytes 491528 | tf_op jit(solution)/shard_map/ppermute | solution.py:77
  43.5 18.5 %copy-start.2 = (s32[128,1]{0,1:T(1,128)S(1)}, s32[128,1]{0,1:T(1,128)}, u32[]{:S(2)}) copy-start(s32[128,1]{0,1:T(1,128)} %param.8) | copy-start | bytes 1540
  43.5 8.0 %collective-permute-start.17 = (bf16[128,1280]{1,0:T(8,128)(2,1)S(1)}, bf16[128,1280]{1,0:T(8,128)(2,1)S(1)}, u32[]{:S(2)}, u32[]{:S(2)}) collective-permute-start(bf16[128,1280]{1,0:T(8,128)(2,1)S(1)} %convolution_convert_fusion.2), channel_id=1, source_target_pairs={{0,1},{1,0},{2,3},{3,2},{4,5},{5,4},{6,7},{7,6},{8,9},{9,8},{10,11... | collective-permute-start | bytes 983048 | tf_op jit(solution)/shard_map/ppermute | solution.py:75
  47.3 14.7 %collective-permute-start.5 = (bf16[128,640]{1,0:T(8,128)(2,1)S(1)}, bf16[128,640]{1,0:T(8,128)(2,1)S(1)}, u32[]{:S(2)}, u32[]{:S(2)}) collective-permute-start(bf16[128,640]{1,0:T(8,128)(2,1)S(1)} %fusion.8), channel_id=1, source_target_pairs={{0,8},{4,12},{8,0},{12,4},{1,9},{5,13},{9,1},{13,5},{2,10},{6,14},... | collective-permute-start | bytes 491528 | tf_op jit(solution)/shard_map/ppermute | solution.py:82
  50.0 7.0 %collective-permute-start.10 = (bf16[128,640]{1,0:T(8,128)(2,1)S(1)}, bf16[128,640]{1,0:T(8,128)(2,1)S(1)}, u32[]{:S(2)}, u32[]{:S(2)}) collective-permute-start(bf16[128,640]{1,0:T(8,128)(2,1)S(1)} %slice.66), channel_id=1, source_target_pairs={{0,2},{1,3},{2,0},{3,1},{4,6},{5,7},{6,4},{7,5},{8,10},{9,11},{10,... | collective-permute-start | bytes 491528 | tf_op jit(solution)/shard_map/ppermute | solution.py:77
  51.6 8.4 %collective-permute-start.18 = (bf16[128,640]{1,0:T(8,128)(2,1)S(1)}, bf16[128,640]{1,0:T(8,128)(2,1)S(1)}, u32[]{:S(2)}, u32[]{:S(2)}) collective-permute-start(bf16[128,640]{1,0:T(8,128)(2,1)S(1)} %slice.65), channel_id=1, source_target_pairs={{0,2},{1,3},{2,0},{3,1},{4,6},{5,7},{6,4},{7,5},{8,10},{9,11},{10,... | collective-permute-start | bytes 491528 | tf_op jit(solution)/shard_map/ppermute | solution.py:77
  57.0 7.3 %collective-permute-start.11 = (bf16[128,640]{1,0:T(8,128)(2,1)S(1)}, bf16[128,640]{1,0:T(8,128)(2,1)S(1)}, u32[]{:S(2)}, u32[]{:S(2)}) collective-permute-start(bf16[128,640]{1,0:T(8,128)(2,1)S(1)} %fusion.7), channel_id=1, source_target_pairs={{0,12},{4,8},{8,4},{12,0},{1,13},{5,9},{9,5},{13,1},{2,14},{6,10},... | collective-permute-start | bytes 491528 | tf_op jit(solution)/shard_map/ppermute | solution.py:82
  58.2 6.1 %collective-permute-start.21 = (bf16[128,640]{1,0:T(8,128)(2,1)S(1)}, bf16[128,640]{1,0:T(8,128)(2,1)S(1)}, u32[]{:S(2)}, u32[]{:S(2)}) collective-permute-start(bf16[128,640]{1,0:T(8,128)(2,1)S(1)} %slice.64), channel_id=1, source_target_pairs={{0,2},{1,3},{2,0},{3,1},{4,6},{5,7},{6,4},{7,5},{8,10},{9,11},{10,... | collective-permute-start | bytes 491528 | tf_op jit(solution)/shard_map/ppermute | solution.py:77
  60.1 5.9 %collective-permute-start.19 = (bf16[128,640]{1,0:T(8,128)(2,1)S(1)}, bf16[128,640]{1,0:T(8,128)(2,1)S(1)}, u32[]{:S(2)}, u32[]{:S(2)}) collective-permute-start(bf16[128,640]{1,0:T(8,128)(2,1)S(1)} %fusion.6), channel_id=1, source_target_pairs={{0,4},{4,0},{8,12},{12,8},{1,5},{5,1},{9,13},{13,9},{2,6},{6,2},{1... | collective-permute-start | bytes 491528 | tf_op jit(solution)/shard_map/ppermute | solution.py:82

commit v21 on v18

--- a/solution.py
+++ b/solution.py
@@ -70,7 +70,7 @@
     up_w = _slots(up_weight[0], t, width, 0)
     down_keep = _slots(down_weight[0], t, width, 1, _ORDER[:2])
     down_send = _slots(down_weight[0], t, width, 1, _ORDER[2:])
-    waves = [[k] for k in list(range(2, n_expert)) + [1][:n_expert - 1] + [0]]
+    waves = [[k] for k in list(range(n_expert - 1, 1, -1)) + [1][:n_expert - 1] + [0]]
     total = None
     previous = None
     for wave in waves:

time: 64.5 us -> 62.9 us (0.975)
  starting transfers between devices: 22.3 us -> 21.3 us
    ppermute x4, waiting for transfers between devices: 5.23 us -> 3.91 us  [gathered(): lax.ppermute(piece, 'tensor', _xor_pairs(n_tensor, 2))]
    ppermute x4, starting transfers between devices: 5.42 us -> 4.13 us  [gathered(): lax.ppermute(piece, 'tensor', _xor_pairs(n_tensor, 2))]
    ppermute x3, waiting for transfers between devices: 3.32 us -> 4.4 us  [gathered(): lax.ppermute(scaled, 'expert', _xor_pairs(n_expert, k))]
  transfers between devices with their start and end apart: 22 -> 22, of which waited for: 9 -> 9; matrix products, arithmetic and copies ran while one was open for 30% -> 31% of each run, Pallas kernels for 0% -> 0%
where the time goes in v21:
time: 62.9 us; the launch traced here: 62.6 us
  starting transfers between devices  21.3 us (34%)
  waiting for transfers between devices  17.7 us (28%)
  other arithmetic  8.86 us (14%)
  matrix products  7.73 us (12%)
  local copies, waits for them, and re-layouts  6.68 us (11%)
    ppermute x3, starting transfers between devices, gathered(): lax.ppermute(scaled, 'expert', _xor_pairs(n_expert, k))  5.76 us
    ppermute x4, waiting for transfers between devices, gathered(): lax.ppermute(over_c[:, width:].astype(jnp.bfloat16), 'tensor', _xor_pairs...  5.33 us
    ppermute x3, starting transfers between devices, gathered(): lax.ppermute(part.astype(jnp.bfloat16), 'expert', _xor_pairs(n_expert, k))  5 us
    ppermute x4, starting transfers between devices, gathered(): lax.ppermute(over_c[:, width:].astype(jnp.bfloat16), 'tensor', _xor_pairs...  4.96 us
    ppermute x3, waiting for transfers between devices, gathered(): lax.ppermute(scaled, 'expert', _xor_pairs(n_expert, k))  4.4 us
    ppermute x4, starting transfers between devices, gathered(): lax.ppermute(piece, 'tensor', _xor_pairs(n_tensor, 2))  4.13 us
    ppermute x4, waiting for transfers between devices, gathered(): lax.ppermute(piece, 'tensor', _xor_pairs(n_tensor, 2))  3.91 us
    concatenate x4, other arithmetic, gathered(): jnp.concatenate([piece, lax.ppermute(piece, 'tensor', _xor_pairs(n_tensor...  3.77 us
  transfers between devices with their start and end apart: 22, of which 9 were waited for; matrix products, arithmetic and copies ran while one was open for 31% of the time, Pallas kernels for 0%

profile of v21, /device:TPU:0, one launch (start us, length us, event | category | flops | bytes accessed | tf_op | source)
XLA Modules:
  0.0 62.6 jit_solution(16062551902882049895)
XLA Ops:
  0.0 1.0 %multiply_convert_fusion = bf16[128,640]{1,0:T(8,128)(2,1)S(1)} fusion(bf16[128,640]{1,0:T(8,128)(2,1)} %param.6, f32[128]{0:T(128)} %param.7), kind=kLoop, calls=%fused_computation.56 | loop fusion | flops 245760 | bytes 328192 | tf_op jit(solution)/shard_map/convert_element_type | solution.py:64
  1.0 5.1 %collective-permute-start = (bf16[128,640]{1,0:T(8,128)(2,1)S(1)}, bf16[128,640]{1,0:T(8,128)(2,1)}, u32[]{:S(2)}, u32[]{:S(2)}) collective-permute-start(bf16[128,640]{1,0:T(8,128)(2,1)S(1)} %multiply_convert_fusion), channel_id=1, source_target_pairs={{0,12},{4,8},{8,4},{12,0},{1,13},{5,9},{9,5},{13,1},{2,14},{6,10},... | collective-permute-start | bytes 491528 | tf_op jit(solution)/shard_map/ppermute | solution.py:66
  6.1 0.6 %collective-permute-start.12 = (bf16[128,640]{1,0:T(8,128)(2,1)S(1)}, bf16[128,640]{1,0:T(8,128)(2,1)}, u32[]{:S(2)}, u32[]{:S(2)}) collective-permute-start(bf16[128,640]{1,0:T(8,128)(2,1)S(1)} %multiply_convert_fusion), channel_id=1, source_target_pairs={{0,4},{4,0},{8,12},{12,8},{1,5},{5,1},{9,13},{13,9},{2,6},{6,2},{1... | collective-permute-start | bytes 491528 | tf_op jit(solution)/shard_map/ppermute | solution.py:66
  6.8 1.6 %collective-permute-start.18 = (bf16[128,640]{1,0:T(8,128)(2,1)S(1)}, bf16[128,640]{1,0:T(8,128)(2,1)}, u32[]{:S(2)}, u32[]{:S(2)}) collective-permute-start(bf16[128,640]{1,0:T(8,128)(2,1)S(1)} %multiply_convert_fusion), channel_id=1, source_target_pairs={{0,2},{1,3},{2,0},{3,1},{4,6},{5,7},{6,4},{7,5},{8,10},{9,11},{10,... | collective-permute-start | bytes 491528 | tf_op jit(solution)/shard_map/ppermute | solution.py:79
  8.4 2.0 %dynamic-slice_bitcast_fusion.11 = (bf16[640,512]{1,0:T(8,128)(2,1)S(1)}, bf16[640,512]{1,0:T(8,128)(2,1)S(1)}, bf16[640,512]{1,0:T(8,128)(2,1)S(1)}, bf16[640,512]{1,0:T(8,128)(2,1)S(1)}) fusion(bf16[1,2560,512]{2,1,0:T(8,128)(2,1)} %param.9, s32[]{:T(128)S(6)} %select_n.48, s32[]{:T(128)S(6)} %select_n.49, s32[]{:T(128)S(6)} %select_n.51, s32[]{:T(128)S(6)} %select_n.50), kind=kLoop, calls=%fused_computation.37 | loop fusion | bytes 5242896 | tf_op jit(solution)/shard_map/dynamic_slice | solution.py:55
  10.4 0.5 copy-done
  10.9 1.3 %dynamic-slice_bitcast_fusion.7 = (bf16[640,512]{1,0:T(8,128)(2,1)S(1)}, bf16[640,512]{1,0:T(8,128)(2,1)}, bf16[640,512]{1,0:T(8,128)(2,1)}, bf16[640,512]{1,0:T(8,128)(2,1)}) fusion(bf16[1,2560,512]{2,1,0:T(8,128)(2,1)S(1)} %copy-done, s32[]{:T(128)S(6)} %select_n.48, s32[]{:T(128)S(6)} %select_n.49, s32[]{:T(128)S(6)} %select_n.51, s32[]{:T(128)S(6)} %select_n.50), kind=kLoop, calls=%fused_computation.33 | loop fusion | bytes 5242896 | tf_op jit(solution)/shard_map/dynamic_slice | solution.py:55
  12.5 1.5 %copy-done.1 = bf16[1,512,2560]{2,1,0:T(8,128)(2,1)S(1)} copy-done((bf16[1,512,2560]{2,1,0:T(8,128)(2,1)S(1)}, bf16[1,512,2560]{2,1,0:T(8,128)(2,1)}, u32[]{:S(2)}) %copy-start.1) | copy-done | bytes 2621464
  14.2 0.5 collective-permute-start.1
  14.7 0.9 %pad_maximum_fusion.10 = bf16[128,1280]{1,0:T(8,128)(2,1)S(1)} fusion(bf16[128,640]{1,0:T(8,128)(2,1)} %collective-permute-done.18, bf16[128,640]{1,0:T(8,128)(2,1)S(1)} %multiply_convert_fusion), kind=kLoop, calls=%fused_computation.55 | loop fusion | flops 655360 | bytes 655360 | tf_op jit(solution)/shard_map/concatenate | solution.py:78
  15.7 4.4 %collective-permute-done.6 = bf16[128,640]{1,0:T(8,128)(2,1)} collective-permute-done((bf16[128,640]{1,0:T(8,128)(2,1)S(1)}, bf16[128,640]{1,0:T(8,128)(2,1)}, u32[]{:S(2)}, u32[]{:S(2)}) %collective-permute-start.6) | collective-permute-done | bytes 163872 | tf_op jit(solution)/shard_map/ppermute | solution.py:66
  20.1 1.5 %collective-permute-start.7 = (bf16[128,640]{1,0:T(8,128)(2,1)}, bf16[128,640]{1,0:T(8,128)(2,1)S(1)}, u32[]{:S(2)}, u32[]{:S(2)}) collective-permute-start(bf16[128,640]{1,0:T(8,128)(2,1)} %collective-permute-done.6), channel_id=1, source_target_pairs={{0,2},{1,3},{2,0},{3,1},{4,6},{5,7},{6,4},{7,5},{8,10},{9,11},{10,... | collective-permute-start | bytes 491528 | tf_op jit(solution)/shard_map/ppermute | solution.py:79
  21.6 0.5 collective-permute-start.13
  22.2 0.9 %constant_dynamic-update-slice_fusion.2 = bf16[128,2560]{1,0:T(8,128)(2,1)S(1)} fusion(bf16[128,640]{1,0:T(8,128)(2,1)} %collective-permute-done), kind=kLoop, calls=%fused_computation.60 | loop fusion | bytes 327680
  23.1 0.9 %pad_maximum_fusion.7 = bf16[128,1280]{1,0:T(8,128)(2,1)S(1)} fusion(bf16[128,640]{1,0:T(8,128)(2,1)S(1)} %collective-permute-done.1, bf16[128,640]{1,0:T(8,128)(2,1)} %collective-permute-done), kind=kLoop, calls=%fused_computation.52 | loop fusion | flops 655360 | bytes 655360 | tf_op jit(solution)/shard_map/concatenate | solution.py:78
  24.1 3.2 %collective-permute-done.7 = bf16[128,640]{1,0:T(8,128)(2,1)S(1)} collective-permute-done((bf16[128,640]{1,0:T(8,128)(2,1)}, bf16[128,640]{1,0:T(8,128)(2,1)S(1)}, u32[]{:S(2)}, u32[]{:S(2)}) %collective-permute-start.7) | collective-permute-done | bytes 163872 | tf_op jit(solution)/shard_map/ppermute | solution.py:79
  27.3 0.9 %pad_maximum_fusion.8 = bf16[128,1280]{1,0:T(8,128)(2,1)S(1)} fusion(bf16[128,640]{1,0:T(8,128)(2,1)S(1)} %collective-permute-done.7, bf16[128,640]{1,0:T(8,128)(2,1)} %collective-permute-done.6), kind=kLoop, calls=%fused_computation.53 | loop fusion | flops 655360 | bytes 655360 | tf_op jit(solution)/shard_map/concatenate | solution.py:78
  28.4 0.7 %collective-permute-done.13 = bf16[128,640]{1,0:T(8,128)(2,1)S(1)} collective-permute-done((bf16[128,640]{1,0:T(8,128)(2,1)}, bf16[128,640]{1,0:T(8,128)(2,1)S(1)}, u32[]{:S(2)}, u32[]{:S(2)}) %collective-permute-start.13) | collective-permute-done | bytes 163872 | tf_op jit(solution)/shard_map/ppermute | solution.py:79
  29.1 0.9 %pad_maximum_fusion.9 = bf16[128,1280]{1,0:T(8,128)(2,1)S(1)} fusion(bf16[128,640]{1,0:T(8,128)(2,1)S(1)} %collective-permute-done.13, bf16[128,640]{1,0:T(8,128)(2,1)} %collective-permute-done.12), kind=kLoop, calls=%fused_computation.54 | loop fusion | flops 655360 | bytes 655360 | tf_op jit(solution)/shard_map/concatenate | solution.py:78
  30.2 0.5 fusion.11
  30.7 0.7 %multiply_convert_fusion.1 = bf16[128,512]{1,0:T(8,128)(2,1)S(1)} fusion(f32[128,512]{1,0:T(8,128)S(1)} %fusion.11, bf16[128,2560]{1,0:T(8,128)(2,1)S(1)} %constant_dynamic-update-slice_fusion, bf16[640,512]{1,0:T(8,128)(2,1)S(1)} %copy-done.3, bf16[640,512]{1,0:T(8,128)(2,1)S(1)} %copy-done.4, bf16[640,512]{1,0:T(8,128)(2,1)S(1)} %copy-done.2, ...), kind=kOutput, calls=%fused_computation.57 | convolution fusion | flops 346423296 | bytes 3670016 | tf_op jit(solution)/shard_map/dot_general | solution.py:85
  31.5 0.3 convolution_convert_fusion.6
  31.8 0.6 collective-permute-start.3
  32.4 1.0 %pad_maximum_fusion.4 = bf16[128,2560]{1,0:T(8,128)(2,1)S(1)} fusion(bf16[128,1280]{1,0:T(8,128)(2,1)S(1)} %collective-permute-done.8, bf16[128,640]{1,0:T(8,128)(2,1)S(1)} %collective-permute-done.7, bf16[128,640]{1,0:T(8,128)(2,1)} %collective-permute-done.6), kind=kLoop, calls=%fused_computation.19 | loop fusion | flops 1966080 | bytes 1310720 | tf_op jit(solution)/shard_map/concatenate | solution.py:80
  33.6 0.3 convert_add_fusion.3
  34.0 0.5 fusion.12
  34.5 0.7 %fusion.1 = bf16[128,512]{1,0:T(8,128)(2,1)S(1)} fusion(bf16[128,2560]{1,0:T(8,128)(2,1)S(1)} %pad_maximum_fusion.4, f32[128,512]{1,0:T(8,128)S(1)} %fusion.12, bf16[640,512]{1,0:T(8,128)(2,1)S(1)} %copy-done.3, bf16[640,512]{1,0:T(8,128)(2,1)S(1)} %copy-done.4, bf16[640,512]{1,0:T(8,128)(2,1)S(1)} %copy-done.2, bf16[640,512]{1,0:T(8,128)(2,1)S(1)} %get-tuple-element.15), kind=kOutput, calls=%fused_computation.16 | convolution fusion | flops 346423296 | bytes 3670016 | tf_op jit(solution)/shard_map/dot_general | solution.py:85
  35.6 0.4 collective-permute-start.9
  36.1 1.0 %pad_maximum_fusion.5 = bf16[128,2560]{1,0:T(8,128)(2,1)S(1)} fusion(bf16[128,1280]{1,0:T(8,128)(2,1)S(1)} %collective-permute-done.14, bf16[128,640]{1,0:T(8,128)(2,1)S(1)} %collective-permute-done.13, bf16[128,640]{1,0:T(8,128)(2,1)} %collective-permute-done.12), kind=kLoop, calls=%fused_computation.20 | loop fusion | flops 1966080 | bytes 1310720 | tf_op jit(solution)/shard_map/concatenate | solution.py:80
  37.1 1.6 %collective-permute-start.4 = (bf16[128,640]{1,0:T(8,128)(2,1)S(1)}, bf16[128,640]{1,0:T(8,128)(2,1)S(1)}, u32[]{:S(2)}, u32[]{:S(2)}) collective-permute-start(bf16[128,640]{1,0:T(8,128)(2,1)S(1)} %slice.67), channel_id=1, source_target_pairs={{0,2},{1,3},{2,0},{3,1},{4,6},{5,7},{6,4},{7,5},{8,10},{9,11},{10,... | collective-permute-start | bytes 491528 | tf_op jit(solution)/shard_map/ppermute | solution.py:92
  39.0 0.5 fusion.13
  39.5 0.7 %fusion.2 = bf16[128,512]{1,0:T(8,128)(2,1)S(1)} fusion(bf16[128,2560]{1,0:T(8,128)(2,1)S(1)} %pad_maximum_fusion.5, f32[128,512]{1,0:T(8,128)S(1)} %fusion.13, bf16[640,512]{1,0:T(8,128)(2,1)S(1)} %copy-done.3, bf16[640,512]{1,0:T(8,128)(2,1)S(1)} %copy-done.4, bf16[640,512]{1,0:T(8,128)(2,1)S(1)} %copy-done.2, bf16[640,512]{1,0:T(8,128)(2,1)S(1)} %get-tuple-element.15), kind=kOutput, calls=%fused_computation.17 | convolution fusion | flops 346423296 | bytes 3670016 | tf_op jit(solution)/shard_map/dot_general | solution.py:85
  40.2 0.3 convolution_convert_fusion.2
  40.7 1.0 %pad_maximum_fusion.6 = bf16[128,2560]{1,0:T(8,128)(2,1)S(1)} fusion(bf16[128,1280]{1,0:T(8,128)(2,1)S(1)} %collective-permute-done.19, bf16[128,640]{1,0:T(8,128)(2,1)} %collective-permute-done.18, bf16[128,640]{1,0:T(8,128)(2,1)S(1)} %multiply_convert_fusion), kind=kLoop, calls=%fused_computation.21 | loop fusion | flops 1966080 | bytes 1310720 | tf_op jit(solution)/shard_map/concatenate | solution.py:80
  41.6 1.7 %collective-permute-done.4 = bf16[128,640]{1,0:T(8,128)(2,1)S(1)} collective-permute-done((bf16[128,640]{1,0:T(8,128)(2,1)S(1)}, bf16[128,640]{1,0:T(8,128)(2,1)S(1)}, u32[]{:S(2)}, u32[]{:S(2)}) %collective-permute-start.4) | collective-permute-done | bytes 163872 | tf_op jit(solution)/shard_map/ppermute | solution.py:92
  43.4 2.4 %collective-permute-start.5 = (bf16[128,640]{1,0:T(8,128)(2,1)S(1)}, bf16[128,640]{1,0:T(8,128)(2,1)S(1)}, u32[]{:S(2)}, u32[]{:S(2)}) collective-permute-start(bf16[128,640]{1,0:T(8,128)(2,1)S(1)} %fusion.9), channel_id=1, source_target_pairs={{0,12},{4,8},{8,4},{12,0},{1,13},{5,9},{9,5},{13,1},{2,14},{6,10},... | collective-permute-start | bytes 491528 | tf_op jit(solution)/shard_map/ppermute | solution.py:97
  45.8 1.6 %collective-permute-start.10 = (bf16[128,640]{1,0:T(8,128)(2,1)S(1)}, bf16[128,640]{1,0:T(8,128)(2,1)S(1)}, u32[]{:S(2)}, u32[]{:S(2)}) collective-permute-start(bf16[128,640]{1,0:T(8,128)(2,1)S(1)} %slice.66), channel_id=1, source_target_pairs={{0,2},{1,3},{2,0},{3,1},{4,6},{5,7},{6,4},{7,5},{8,10},{9,11},{10,... | collective-permute-start | bytes 491528 | tf_op jit(solution)/shard_map/ppermute | solution.py:92
  47.7 0.6 collective-permute-start.16
  48.3 0.5 fusion.14
  48.8 0.7 %fusion.3 = bf16[128,512]{1,0:T(8,128)(2,1)S(1)} fusion(bf16[128,2560]{1,0:T(8,128)(2,1)S(1)} %pad_maximum_fusion.6, f32[128,512]{1,0:T(8,128)S(1)} %fusion.14, bf16[640,512]{1,0:T(8,128)(2,1)S(1)} %copy-done.3, bf16[640,512]{1,0:T(8,128)(2,1)S(1)} %copy-done.4, bf16[640,512]{1,0:T(8,128)(2,1)S(1)} %copy-done.2, bf16[640,512]{1,0:T(8,128)(2,1)S(1)} %get-tuple-element.15), kind=kOutput, calls=%fused_computation.18 | convolution fusion | flops 346423296 | bytes 3670016 | tf_op jit(solution)/shard_map/dot_general | solution.py:85
  50.0 2.7 %collective-permute-done.10 = bf16[128,640]{1,0:T(8,128)(2,1)S(1)} collective-permute-done((bf16[128,640]{1,0:T(8,128)(2,1)S(1)}, bf16[128,640]{1,0:T(8,128)(2,1)S(1)}, u32[]{:S(2)}, u32[]{:S(2)}) %collective-permute-start.10) | collective-permute-done | bytes 163872 | tf_op jit(solution)/shard_map/ppermute | solution.py:92
  52.7 1.2 %collective-permute-start.11 = (bf16[128,640]{1,0:T(8,128)(2,1)S(1)}, bf16[128,640]{1,0:T(8,128)(2,1)S(1)}, u32[]{:S(2)}, u32[]{:S(2)}) collective-permute-start(bf16[128,640]{1,0:T(8,128)(2,1)S(1)} %fusion.8), channel_id=1, source_target_pairs={{0,8},{4,12},{8,0},{12,4},{1,9},{5,13},{9,1},{13,5},{2,10},{6,14},... | collective-permute-start | bytes 491528 | tf_op jit(solution)/shard_map/ppermute | solution.py:97
  53.9 0.5 collective-permute-done.16
  54.5 1.5 %collective-permute-start.17 = (bf16[128,640]{1,0:T(8,128)(2,1)S(1)}, bf16[128,640]{1,0:T(8,128)(2,1)S(1)}, u32[]{:S(2)}, u32[]{:S(2)}) collective-permute-start(bf16[128,640]{1,0:T(8,128)(2,1)S(1)} %fusion.7), channel_id=1, source_target_pairs={{0,4},{4,0},{8,12},{12,8},{1,5},{5,1},{9,13},{13,9},{2,6},{6,2},{1... | collective-permute-start | bytes 491528 | tf_op jit(solution)/shard_map/ppermute | solution.py:97
  56.3 1.2 %collective-permute-start.21 = (bf16[128,640]{1,0:T(8,128)(2,1)S(1)}, bf16[128,640]{1,0:T(8,128)(2,1)S(1)}, u32[]{:S(2)}, u32[]{:S(2)}) collective-permute-start(bf16[128,640]{1,0:T(8,128)(2,1)S(1)} %slice.64), channel_id=1, source_target_pairs={{0,2},{1,3},{2,0},{3,1},{4,6},{5,7},{6,4},{7,5},{8,10},{9,11},{10,... | collective-permute-start | bytes 491528 | tf_op jit(solution)/shard_map/ppermute | solution.py:92
  57.6 3.7 %collective-permute-done.11 = bf16[128,640]{1,0:T(8,128)(2,1)S(1)} collective-permute-done((bf16[128,640]{1,0:T(8,128)(2,1)S(1)}, bf16[128,640]{1,0:T(8,128)(2,1)S(1)}, u32[]{:S(2)}, u32[]{:S(2)}) %collective-permute-start.11) | collective-permute-done | bytes 163872 | tf_op jit(solution)/shard_map/ppermute | solution.py:97
  61.3 0.4 collective-permute-done.21
  61.7 0.9 %fusion.6 = bf16[128,640]{1,0:T(8,128)(2,1)} fusion(f32[128,1280]{1,0:T(8,128)S(1)} %convert_add_fusion, bf16[128,640]{1,0:T(8,128)(2,1)S(1)} %collective-permute-done.21, bf16[128,640]{1,0:T(8,128)(2,1)S(1)} %collective-permute-done.17, bf16[128,640]{1,0:T(8,128)(2,1)S(1)} %collective-permute-done.11, bf16[128,640]{1,0:T(8,128)(2,1)S(1)} %collective-permute-done.5, ...), kind=kLoop, calls=%fused_computation.42 | loop fusion | flops 1064960 | bytes 1147392 | tf_op jit(solution)/shard_map/convert_element_type | solution.py:101
  (48 shorter events, 3.2 us)
Async XLA Ops:
  1.0 13.2 %collective-permute-start = (bf16[128,640]{1,0:T(8,128)(2,1)S(1)}, bf16[128,640]{1,0:T(8,128)(2,1)}, u32[]{:S(2)}, u32[]{:S(2)}) collective-permute-start(bf16[128,640]{1,0:T(8,128)(2,1)S(1)} %multiply_convert_fusion), channel_id=1, source_target_pairs={{0,12},{4,8},{8,4},{12,0},{1,13},{5,9},{9,5},{13,1},{2,14},{6,10},... | collective-permute-start | bytes 491528 | tf_op jit(solution)/shard_map/ppermute | solution.py:66
  6.1 14.0 %collective-permute-start.6 = (bf16[128,640]{1,0:T(8,128)(2,1)S(1)}, bf16[128,640]{1,0:T(8,128)(2,1)}, u32[]{:S(2)}, u32[]{:S(2)}) collective-permute-start(bf16[128,640]{1,0:T(8,128)(2,1)S(1)} %multiply_convert_fusion), channel_id=1, source_target_pairs={{0,8},{4,12},{8,0},{12,4},{1,9},{5,13},{9,1},{13,5},{2,10},{6,14},... | collective-permute-start | bytes 491528 | tf_op jit(solution)/shard_map/ppermute | solution.py:66
  6.1 15.5 %collective-permute-start.12 = (bf16[128,640]{1,0:T(8,128)(2,1)S(1)}, bf16[128,640]{1,0:T(8,128)(2,1)}, u32[]{:S(2)}, u32[]{:S(2)}) collective-permute-start(bf16[128,640]{1,0:T(8,128)(2,1)S(1)} %multiply_convert_fusion), channel_id=1, source_target_pairs={{0,4},{4,0},{8,12},{12,8},{1,5},{5,1},{9,13},{13,9},{2,6},{6,2},{1... | collective-permute-start | bytes 491528 | tf_op jit(solution)/shard_map/ppermute | solution.py:66
  6.8 7.9 %collective-permute-start.18 = (bf16[128,640]{1,0:T(8,128)(2,1)S(1)}, bf16[128,640]{1,0:T(8,128)(2,1)}, u32[]{:S(2)}, u32[]{:S(2)}) collective-permute-start(bf16[128,640]{1,0:T(8,128)(2,1)S(1)} %multiply_convert_fusion), channel_id=1, source_target_pairs={{0,2},{1,3},{2,0},{3,1},{4,6},{5,7},{6,4},{7,5},{8,10},{9,11},{10,... | collective-permute-start | bytes 491528 | tf_op jit(solution)/shard_map/ppermute | solution.py:79
  8.4 2.5 %copy-start = (bf16[1,2560,512]{2,1,0:T(8,128)(2,1)S(1)}, bf16[1,2560,512]{2,1,0:T(8,128)(2,1)}, u32[]{:S(2)}) copy-start(bf16[1,2560,512]{2,1,0:T(8,128)(2,1)} %param.10) | copy-start | bytes 7864324
  12.3 1.7 %copy-start.1 = (bf16[1,512,2560]{2,1,0:T(8,128)(2,1)S(1)}, bf16[1,512,2560]{2,1,0:T(8,128)(2,1)}, u32[]{:S(2)}) copy-start(bf16[1,512,2560]{2,1,0:T(8,128)(2,1)} %param.11) | copy-start | bytes 7864324
  14.2 8.9 %collective-permute-start.1 = (bf16[128,640]{1,0:T(8,128)(2,1)}, bf16[128,640]{1,0:T(8,128)(2,1)S(1)}, u32[]{:S(2)}, u32[]{:S(2)}) collective-permute-start(bf16[128,640]{1,0:T(8,128)(2,1)} %collective-permute-done), channel_id=1, source_target_pairs={{0,2},{1,3},{2,0},{3,1},{4,6},{5,7},{6,4},{7,5},{8,10},{9,11},{10,... | collective-permute-start | bytes 491528 | tf_op jit(solution)/shard_map/ppermute | solution.py:79
  15.6 25.0 %collective-permute-start.19 = (bf16[128,1280]{1,0:T(8,128)(2,1)S(1)}, bf16[128,1280]{1,0:T(8,128)(2,1)S(1)}, u32[]{:S(2)}, u32[]{:S(2)}) collective-permute-start(bf16[128,1280]{1,0:T(8,128)(2,1)S(1)} %pad_maximum_fusion.10), channel_id=1, source_target_pairs={{0,1},{1,0},{2,3},{3,2},{4,5},{5,4},{6,7},{7,6},{8,9},{9,8},{10,11... | collective-permute-start | bytes 983048 | tf_op jit(solution)/shard_map/ppermute | solution.py:81
  20.1 7.2 %collective-permute-start.7 = (bf16[128,640]{1,0:T(8,128)(2,1)}, bf16[128,640]{1,0:T(8,128)(2,1)S(1)}, u32[]{:S(2)}, u32[]{:S(2)}) collective-permute-start(bf16[128,640]{1,0:T(8,128)(2,1)} %collective-permute-done.6), channel_id=1, source_target_pairs={{0,2},{1,3},{2,0},{3,1},{4,6},{5,7},{6,4},{7,5},{8,10},{9,11},{10,... | collective-permute-start | bytes 491528 | tf_op jit(solution)/shard_map/ppermute | solution.py:79
  21.6 7.5 %collective-permute-start.13 = (bf16[128,640]{1,0:T(8,128)(2,1)}, bf16[128,640]{1,0:T(8,128)(2,1)S(1)}, u32[]{:S(2)}, u32[]{:S(2)}) collective-permute-start(bf16[128,640]{1,0:T(8,128)(2,1)} %collective-permute-done.12), channel_id=1, source_target_pairs={{0,2},{1,3},{2,0},{3,1},{4,6},{5,7},{6,4},{7,5},{8,10},{9,11},{10,... | collective-permute-start | bytes 491528 | tf_op jit(solution)/shard_map/ppermute | solution.py:79
  24.1 6.1 %collective-permute-start.2 = (bf16[128,1280]{1,0:T(8,128)(2,1)S(1)}, bf16[128,1280]{1,0:T(8,128)(2,1)S(1)}, u32[]{:S(2)}, u32[]{:S(2)}) collective-permute-start(bf16[128,1280]{1,0:T(8,128)(2,1)S(1)} %pad_maximum_fusion.7), channel_id=1, source_target_pairs={{0,1},{1,0},{2,3},{3,2},{4,5},{5,4},{6,7},{7,6},{8,9},{9,8},{10,11... | collective-permute-start | bytes 983048 | tf_op jit(solution)/shard_map/ppermute | solution.py:81
  28.3 2.4 %copy-start.2 = (bf16[640,512]{1,0:T(8,128)(2,1)S(1)}, bf16[640,512]{1,0:T(8,128)(2,1)}, u32[]{:S(2)}) copy-start(bf16[640,512]{1,0:T(8,128)(2,1)} %get-tuple-element.16) | copy-start | bytes 1966084
  28.3 2.4 %copy-start.3 = (bf16[640,512]{1,0:T(8,128)(2,1)S(1)}, bf16[640,512]{1,0:T(8,128)(2,1)}, u32[]{:S(2)}) copy-start(bf16[640,512]{1,0:T(8,128)(2,1)} %get-tuple-element.17) | copy-start | bytes 1966084
  28.3 2.4 %copy-start.4 = (bf16[640,512]{1,0:T(8,128)(2,1)S(1)}, bf16[640,512]{1,0:T(8,128)(2,1)}, u32[]{:S(2)}) copy-start(bf16[640,512]{1,0:T(8,128)(2,1)} %get-tuple-element.18) | copy-start | bytes 1966084
  28.3 4.1 %collective-permute-start.8 = (bf16[128,1280]{1,0:T(8,128)(2,1)S(1)}, bf16[128,1280]{1,0:T(8,128)(2,1)S(1)}, u32[]{:S(2)}, u32[]{:S(2)}) collective-permute-start(bf16[128,1280]{1,0:T(8,128)(2,1)S(1)} %pad_maximum_fusion.8), channel_id=1, source_target_pairs={{0,1},{1,0},{2,3},{3,2},{4,5},{5,4},{6,7},{7,6},{8,9},{9,8},{10,11... | collective-permute-start | bytes 983048 | tf_op jit(solution)/shard_map/ppermute | solution.py:81
  30.0 6.0 %collective-permute-start.14 = (bf16[128,1280]{1,0:T(8,128)(2,1)S(1)}, bf16[128,1280]{1,0:T(8,128)(2,1)S(1)}, u32[]{:S(2)}, u32[]{:S(2)}) collective-permute-start(bf16[128,1280]{1,0:T(8,128)(2,1)S(1)} %pad_maximum_fusion.9), channel_id=1, source_target_pairs={{0,1},{1,0},{2,3},{3,2},{4,5},{5,4},{6,7},{7,6},{8,9},{9,8},{10,11... | collective-permute-start | bytes 983048 | tf_op jit(solution)/shard_map/ppermute | solution.py:81
  31.8 1.8 %collective-permute-start.3 = (bf16[128,1280]{1,0:T(8,128)(2,1)S(1)}, bf16[128,1280]{1,0:T(8,128)(2,1)S(1)}, u32[]{:S(2)}, u32[]{:S(2)}) collective-permute-start(bf16[128,1280]{1,0:T(8,128)(2,1)S(1)} %convolution_convert_fusion.6), channel_id=1, source_target_pairs={{0,1},{1,0},{2,3},{3,2},{4,5},{5,4},{6,7},{7,6},{8,9},{9,8},{10,11... | collective-permute-start | bytes 983048 | tf_op jit(solution)/shard_map/ppermute | solution.py:90
  35.6 3.0 %collective-permute-start.9 = (bf16[128,1280]{1,0:T(8,128)(2,1)S(1)}, bf16[128,1280]{1,0:T(8,128)(2,1)S(1)}, u32[]{:S(2)}, u32[]{:S(2)}) collective-permute-start(bf16[128,1280]{1,0:T(8,128)(2,1)S(1)} %convolution_convert_fusion.4), channel_id=1, source_target_pairs={{0,1},{1,0},{2,3},{3,2},{4,5},{5,4},{6,7},{7,6},{8,9},{9,8},{10,11... | collective-permute-start | bytes 983048 | tf_op jit(solution)/shard_map/ppermute | solution.py:90
  37.1 6.3 %collective-permute-start.4 = (bf16[128,640]{1,0:T(8,128)(2,1)S(1)}, bf16[128,640]{1,0:T(8,128)(2,1)S(1)}, u32[]{:S(2)}, u32[]{:S(2)}) collective-permute-start(bf16[128,640]{1,0:T(8,128)(2,1)S(1)} %slice.67), channel_id=1, source_target_pairs={{0,2},{1,3},{2,0},{3,1},{4,6},{5,7},{6,4},{7,5},{8,10},{9,11},{10,... | collective-permute-start | bytes 491528 | tf_op jit(solution)/shard_map/ppermute | solution.py:92
  40.6 6.7 %collective-permute-start.15 = (bf16[128,1280]{1,0:T(8,128)(2,1)S(1)}, bf16[128,1280]{1,0:T(8,128)(2,1)S(1)}, u32[]{:S(2)}, u32[]{:S(2)}) collective-permute-start(bf16[128,1280]{1,0:T(8,128)(2,1)S(1)} %convolution_convert_fusion.2), channel_id=1, source_target_pairs={{0,1},{1,0},{2,3},{3,2},{4,5},{5,4},{6,7},{7,6},{8,9},{9,8},{10,11... | collective-permute-start | bytes 983048 | tf_op jit(solution)/shard_map/ppermute | solution.py:90
  43.4 14.2 %collective-permute-start.5 = (bf16[128,640]{1,0:T(8,128)(2,1)S(1)}, bf16[128,640]{1,0:T(8,128)(2,1)S(1)}, u32[]{:S(2)}, u32[]{:S(2)}) collective-permute-start(bf16[128,640]{1,0:T(8,128)(2,1)S(1)} %fusion.9), channel_id=1, source_target_pairs={{0,12},{4,8},{8,4},{12,0},{1,13},{5,9},{9,5},{13,1},{2,14},{6,10},... | collective-permute-start | bytes 491528 | tf_op jit(solution)/shard_map/ppermute | solution.py:97
  45.8 6.9 %collective-permute-start.10 = (bf16[128,640]{1,0:T(8,128)(2,1)S(1)}, bf16[128,640]{1,0:T(8,128)(2,1)S(1)}, u32[]{:S(2)}, u32[]{:S(2)}) collective-permute-start(bf16[128,640]{1,0:T(8,128)(2,1)S(1)} %slice.66), channel_id=1, source_target_pairs={{0,2},{1,3},{2,0},{3,1},{4,6},{5,7},{6,4},{7,5},{8,10},{9,11},{10,... | collective-permute-start | bytes 491528 | tf_op jit(solution)/shard_map/ppermute | solution.py:92
  47.7 6.7 %collective-permute-start.16 = (bf16[128,640]{1,0:T(8,128)(2,1)S(1)}, bf16[128,640]{1,0:T(8,128)(2,1)S(1)}, u32[]{:S(2)}, u32[]{:S(2)}) collective-permute-start(bf16[128,640]{1,0:T(8,128)(2,1)S(1)} %slice.65), channel_id=1, source_target_pairs={{0,2},{1,3},{2,0},{3,1},{4,6},{5,7},{6,4},{7,5},{8,10},{9,11},{10,... | collective-permute-start | bytes 491528 | tf_op jit(solution)/shard_map/ppermute | solution.py:92
  49.9 7.7 %copy-start.5 = (s32[128,1]{0,1:T(1,128)S(1)}, s32[128,1]{0,1:T(1,128)}, u32[]{:S(2)}) copy-start(s32[128,1]{0,1:T(1,128)} %param.8) | copy-start | bytes 1540
  49.9 6.0 %collective-permute-start.20 = (bf16[128,1280]{1,0:T(8,128)(2,1)S(1)}, bf16[128,1280]{1,0:T(8,128)(2,1)S(1)}, u32[]{:S(2)}, u32[]{:S(2)}) collective-permute-start(bf16[128,1280]{1,0:T(8,128)(2,1)S(1)} %convolution_convert_fusion), channel_id=1, source_target_pairs={{0,1},{1,0},{2,3},{3,2},{4,5},{5,4},{6,7},{7,6},{8,9},{9,8},{10,11... | collective-permute-start | bytes 983048 | tf_op jit(solution)/shard_map/ppermute | solution.py:90
  52.7 8.5 %collective-permute-start.11 = (bf16[128,640]{1,0:T(8,128)(2,1)S(1)}, bf16[128,640]{1,0:T(8,128)(2,1)S(1)}, u32[]{:S(2)}, u32[]{:S(2)}) collective-permute-start(bf16[128,640]{1,0:T(8,128)(2,1)S(1)} %fusion.8), channel_id=1, source_target_pairs={{0,8},{4,12},{8,0},{12,4},{1,9},{5,13},{9,1},{13,5},{2,10},{6,14},... | collective-permute-start | bytes 491528 | tf_op jit(solution)/shard_map/ppermute | solution.py:97
  54.5 6.8 %collective-permute-start.17 = (bf16[128,640]{1,0:T(8,128)(2,1)S(1)}, bf16[128,640]{1,0:T(8,128)(2,1)S(1)}, u32[]{:S(2)}, u32[]{:S(2)}) collective-permute-start(bf16[128,640]{1,0:T(8,128)(2,1)S(1)} %fusion.7), channel_id=1, source_target_pairs={{0,4},{4,0},{8,12},{12,8},{1,5},{5,1},{9,13},{13,9},{2,6},{6,2},{1... | collective-permute-start | bytes 491528 | tf_op jit(solution)/shard_map/ppermute | solution.py:97
  56.3 5.4 %collective-permute-start.21 = (bf16[128,640]{1,0:T(8,128)(2,1)S(1)}, bf16[128,640]{1,0:T(8,128)(2,1)S(1)}, u32[]{:S(2)}, u32[]{:S(2)}) collective-permute-start(bf16[128,640]{1,0:T(8,128)(2,1)S(1)} %slice.64), channel_id=1, source_target_pairs={{0,2},{1,3},{2,0},{3,1},{4,6},{5,7},{6,4},{7,5},{8,10},{9,11},{10,... | collective-permute-start | bytes 491528 | tf_op jit(solution)/shard_map/ppermute | solution.py:92

commit v22 on v21

--- a/solution.py
+++ b/solution.py
@@ -71,6 +71,8 @@
     down_keep = _slots(down_weight[0], t, width, 1, _ORDER[:2])
     down_send = _slots(down_weight[0], t, width, 1, _ORDER[2:])
     waves = [[k] for k in list(range(n_expert - 1, 1, -1)) + [1][:n_expert - 1] + [0]]
+    if len(waves) > 1:
+        blocks[0], _ = lax.optimization_barrier((blocks[0], blocks[waves[0][0]]))
     total = None
     previous = None
     for wave in waves:

time: 62.9 us -> 67 us (1.065)
  starting transfers between devices: 21.3 us -> 23.7 us
  local copies, waits for them, and re-layouts: 6.68 us -> 8.86 us
  other arithmetic: 8.86 us -> 7.14 us
  waiting for transfers between devices: 17.7 us -> 18.7 us
    ppermute x3, starting transfers between devices: 5 us -> 7.18 us  [gathered(): lax.ppermute(part.astype(jnp.bfloat16), 'expert', _xor_pairs(n_expert, k))]
    ppermute x4, waiting for transfers between devices: 5.33 us -> 6.65 us  [gathered(): lax.ppermute(over_c[:, width:].astype(jnp.bfloat16), 'tensor', _xor_pairs...]
    dynamic_slice x3, local copies, waits for them, and re-layouts: 3.54 us -> 4.76 us  [_slots(): lax.dynamic_slice_in_dim(weight, (t ^ k) * width, width, axis=axis)]
    unnamed x14 -> x22, local copies, waits for them, and re-layouts: 3.03 us -> 4 us
    concatenate x3, other arithmetic: 2.89 us -> 1.97 us  [gathered(): jnp.concatenate([pair, lax.ppermute(pair, 'tensor', _xor_pairs(n_tensor,...]
    concatenate x4, other arithmetic: 3.77 us -> 2.93 us  [gathered(): jnp.concatenate([piece, lax.ppermute(piece, 'tensor', _xor_pairs(n_tensor...]
    ppermute x4, starting transfers between devices: 4.13 us -> 4.81 us  [gathered(): lax.ppermute(piece, 'tensor', _xor_pairs(n_tensor, 2))]
  transfers between devices with their start and end apart: 22 -> 22, of which waited for: 9 -> 9; matrix products, arithmetic and copies ran while one was open for 31% -> 30% of each run, Pallas kernels for 0% -> 0%
where the time goes in v22:
time: 67 us; the launch traced here: 66.6 us
  starting transfers between devices  23.7 us (35%)
  waiting for transfers between devices  18.7 us (28%)
  local copies, waits for them, and re-layouts  8.86 us (13%)
  matrix products  7.74 us (12%)
  other arithmetic  7.14 us (11%)
    ppermute x3, starting transfers between devices, gathered(): lax.ppermute(part.astype(jnp.bfloat16), 'expert', _xor_pairs(n_expert, k))  7.18 us
    ppermute x4, waiting for transfers between devices, gathered(): lax.ppermute(over_c[:, width:].astype(jnp.bfloat16), 'tensor', _xor_pairs...  6.65 us
    ppermute x3, starting transfers between devices, gathered(): lax.ppermute(scaled, 'expert', _xor_pairs(n_expert, k))  5.76 us
    ppermute x4, starting transfers between devices, gathered(): lax.ppermute(piece, 'tensor', _xor_pairs(n_tensor, 2))  4.81 us
    dynamic_slice x3, local copies, waits for them, and re-layouts, _slots(): lax.dynamic_slice_in_dim(weight, (t ^ k) * width, width, axis=axis)  4.76 us
    ppermute x4, starting transfers between devices, gathered(): lax.ppermute(over_c[:, width:].astype(jnp.bfloat16), 'tensor', _xor_pairs...  4.69 us
    ppermute x3, waiting for transfers between devices, gathered(): lax.ppermute(scaled, 'expert', _xor_pairs(n_expert, k))  4.06 us
    unnamed x22, local copies, waits for them, and re-layouts  4 us
  transfers between devices with their start and end apart: 22, of which 9 were waited for; matrix products, arithmetic and copies ran while one was open for 30% of the time, Pallas kernels for 0%

profile of v22, /device:TPU:0, one launch (start us, length us, event | category | flops | bytes accessed | tf_op | source)
XLA Modules:
  0.0 66.6 jit_solution(12959043961511802985)
XLA Ops:
  0.0 1.0 %multiply_convert_fusion = bf16[128,640]{1,0:T(8,128)(2,1)S(1)} fusion(bf16[128,640]{1,0:T(8,128)(2,1)} %param.6, f32[128]{0:T(128)} %param.7), kind=kLoop, calls=%fused_computation.56 | loop fusion | flops 245760 | bytes 328192 | tf_op jit(solution)/shard_map/convert_element_type | solution.py:64
  1.0 5.1 %collective-permute-start = (bf16[128,640]{1,0:T(8,128)(2,1)S(1)}, bf16[128,640]{1,0:T(8,128)(2,1)}, u32[]{:S(2)}, u32[]{:S(2)}) collective-permute-start(bf16[128,640]{1,0:T(8,128)(2,1)S(1)} %multiply_convert_fusion), channel_id=1, source_target_pairs={{0,12},{4,8},{8,4},{12,0},{1,13},{5,9},{9,5},{13,1},{2,14},{6,10},... | collective-permute-start | bytes 491528 | tf_op jit(solution)/shard_map/ppermute | solution.py:66
  6.1 0.6 collective-permute-start.12
  6.8 1.8 %dynamic-slice_bitcast_fusion.11 = (bf16[640,512]{1,0:T(8,128)(2,1)S(1)}, bf16[640,512]{1,0:T(8,128)(2,1)S(1)}, bf16[640,512]{1,0:T(8,128)(2,1)S(1)}, bf16[640,512]{1,0:T(8,128)(2,1)S(1)}) fusion(bf16[1,2560,512]{2,1,0:T(8,128)(2,1)} %param.9, s32[]{:T(128)S(6)} %select_n.48, s32[]{:T(128)S(6)} %select_n.49, s32[]{:T(128)S(6)} %select_n.51, s32[]{:T(128)S(6)} %select_n.50), kind=kLoop, calls=%fused_computation.37 | loop fusion | bytes 5242896 | tf_op jit(solution)/shard_map/dynamic_slice | solution.py:55
  8.9 1.5 %copy-done = bf16[1,2560,512]{2,1,0:T(8,128)(2,1)S(1)} copy-done((bf16[1,2560,512]{2,1,0:T(8,128)(2,1)S(1)}, bf16[1,2560,512]{2,1,0:T(8,128)(2,1)}, u32[]{:S(2)}) %copy-start) | copy-done | bytes 2621464
  10.4 1.5 %dynamic-slice_bitcast_fusion.7 = (bf16[640,512]{1,0:T(8,128)(2,1)}, bf16[640,512]{1,0:T(8,128)(2,1)}, bf16[640,512]{1,0:T(8,128)(2,1)}, bf16[640,512]{1,0:T(8,128)(2,1)}) fusion(bf16[1,2560,512]{2,1,0:T(8,128)(2,1)S(1)} %copy-done, s32[]{:T(128)S(6)} %select_n.48, s32[]{:T(128)S(6)} %select_n.49, s32[]{:T(128)S(6)} %select_n.51, s32[]{:T(128)S(6)} %select_n.50), kind=kLoop, calls=%fused_computation.33 | loop fusion | bytes 5242896 | tf_op jit(solution)/shard_map/dynamic_slice | solution.py:55
  11.9 1.6 %collective-permute-start.1 = (bf16[128,640]{1,0:T(8,128)(2,1)}, bf16[128,640]{1,0:T(8,128)(2,1)}, u32[]{:S(2)}, u32[]{:S(2)}) collective-permute-start(bf16[128,640]{1,0:T(8,128)(2,1)} %collective-permute-done), channel_id=1, source_target_pairs={{0,2},{1,3},{2,0},{3,1},{4,6},{5,7},{6,4},{7,5},{8,10},{9,11},{10,... | collective-permute-start | bytes 491528 | tf_op jit(solution)/shard_map/ppermute | solution.py:81
  13.6 1.4 %dynamic-slice_bitcast_fusion.1 = (bf16[512,640]{1,0:T(8,128)(2,1)}, bf16[512,640]{1,0:T(8,128)(2,1)S(1)}, bf16[512,640]{1,0:T(8,128)(2,1)}, bf16[512,640]{1,0:T(8,128)(2,1)}) fusion(bf16[1,512,2560]{2,1,0:T(8,128)(2,1)S(1)} %copy-done.1, s32[]{:T(128)S(6)} %select_n.50, s32[]{:T(128)S(6)} %select_n.49, s32[]{:T(128)S(6)} %select_n.48, s32[]{:T(128)S(6)} %select_n.51), kind=kLoop, calls=%fused_computation.27 | loop fusion | bytes 5242896 | tf_op jit(solution)/shard_map/dynamic_slice | solution.py:55
  14.9 1.1 %collective-permute-start.18 = (bf16[128,640]{1,0:T(8,128)(2,1)S(1)}, bf16[128,640]{1,0:T(8,128)(2,1)S(1)}, u32[]{:S(2)}, u32[]{:S(2)}) collective-permute-start(bf16[128,640]{1,0:T(8,128)(2,1)S(1)} %multiply_convert_fusion), channel_id=1, source_target_pairs={{0,2},{1,3},{2,0},{3,1},{4,6},{5,7},{6,4},{7,5},{8,10},{9,11},{10,... | collective-permute-start | bytes 491528 | tf_op jit(solution)/shard_map/ppermute | solution.py:81
  16.1 4.1 %collective-permute-done.6 = bf16[128,640]{1,0:T(8,128)(2,1)} collective-permute-done((bf16[128,640]{1,0:T(8,128)(2,1)S(1)}, bf16[128,640]{1,0:T(8,128)(2,1)}, u32[]{:S(2)}, u32[]{:S(2)}) %collective-permute-start.6) | collective-permute-done | bytes 163872 | tf_op jit(solution)/shard_map/ppermute | solution.py:66
  20.1 1.5 %collective-permute-start.7 = (bf16[128,640]{1,0:T(8,128)(2,1)}, bf16[128,640]{1,0:T(8,128)(2,1)S(1)}, u32[]{:S(2)}, u32[]{:S(2)}) collective-permute-start(bf16[128,640]{1,0:T(8,128)(2,1)} %collective-permute-done.6), channel_id=1, source_target_pairs={{0,2},{1,3},{2,0},{3,1},{4,6},{5,7},{6,4},{7,5},{8,10},{9,11},{10,... | collective-permute-start | bytes 491528 | tf_op jit(solution)/shard_map/ppermute | solution.py:81
  21.6 0.5 collective-permute-start.13
  22.2 0.9 %constant_dynamic-update-slice_fusion.2 = bf16[128,2560]{1,0:T(8,128)(2,1)S(1)} fusion(bf16[128,640]{1,0:T(8,128)(2,1)} %collective-permute-done), kind=kLoop, calls=%fused_computation.60 | loop fusion | bytes 327680
  23.1 1.0 %pad_maximum_fusion.7 = bf16[128,1280]{1,0:T(8,128)(2,1)S(1)} fusion(bf16[128,640]{1,0:T(8,128)(2,1)} %collective-permute-done.1, bf16[128,640]{1,0:T(8,128)(2,1)} %collective-permute-done), kind=kLoop, calls=%fused_computation.52 | loop fusion | flops 655360 | bytes 655360 | tf_op jit(solution)/shard_map/concatenate | solution.py:80
  24.2 3.1 %collective-permute-done.7 = bf16[128,640]{1,0:T(8,128)(2,1)S(1)} collective-permute-done((bf16[128,640]{1,0:T(8,128)(2,1)}, bf16[128,640]{1,0:T(8,128)(2,1)S(1)}, u32[]{:S(2)}, u32[]{:S(2)}) %collective-permute-start.7) | collective-permute-done | bytes 163872 | tf_op jit(solution)/shard_map/ppermute | solution.py:81
  27.3 0.9 %pad_maximum_fusion.8 = bf16[128,1280]{1,0:T(8,128)(2,1)S(1)} fusion(bf16[128,640]{1,0:T(8,128)(2,1)S(1)} %collective-permute-done.7, bf16[128,640]{1,0:T(8,128)(2,1)} %collective-permute-done.6), kind=kLoop, calls=%fused_computation.53 | loop fusion | flops 655360 | bytes 655360 | tf_op jit(solution)/shard_map/concatenate | solution.py:80
  28.4 0.7 %collective-permute-done.13 = bf16[128,640]{1,0:T(8,128)(2,1)S(1)} collective-permute-done((bf16[128,640]{1,0:T(8,128)(2,1)}, bf16[128,640]{1,0:T(8,128)(2,1)S(1)}, u32[]{:S(2)}, u32[]{:S(2)}) %collective-permute-start.13) | collective-permute-done | bytes 163872 | tf_op jit(solution)/shard_map/ppermute | solution.py:81
  29.1 0.9 %pad_maximum_fusion.9 = bf16[128,1280]{1,0:T(8,128)(2,1)S(1)} fusion(bf16[128,640]{1,0:T(8,128)(2,1)S(1)} %collective-permute-done.13, bf16[128,640]{1,0:T(8,128)(2,1)} %collective-permute-done.12), kind=kLoop, calls=%fused_computation.54 | loop fusion | flops 655360 | bytes 655360 | tf_op jit(solution)/shard_map/concatenate | solution.py:80
  30.2 0.5 collective-permute-start.19
  30.8 1.0 %constant_dynamic-update-slice_fusion.1 = bf16[128,2560]{1,0:T(8,128)(2,1)S(1)} fusion(bf16[128,2560]{1,0:T(8,128)(2,1)S(1)} %constant_dynamic-update-slice_fusion.2, bf16[128,640]{1,0:T(8,128)(2,1)} %collective-permute-done.1), kind=kLoop, calls=%fused_computation.59 | loop fusion | bytes 327680
  31.8 0.5 fusion.11
  32.4 0.7 %multiply_convert_fusion.1 = bf16[128,512]{1,0:T(8,128)(2,1)S(1)} fusion(f32[128,512]{1,0:T(8,128)S(1)} %fusion.11, bf16[128,2560]{1,0:T(8,128)(2,1)S(1)} %constant_dynamic-update-slice_fusion, bf16[640,512]{1,0:T(8,128)(2,1)S(1)} %copy-done.5, bf16[640,512]{1,0:T(8,128)(2,1)S(1)} %copy-done.6, bf16[640,512]{1,0:T(8,128)(2,1)S(1)} %copy-done.4, ...), kind=kOutput, calls=%fused_computation.57 | convolution fusion | flops 346423296 | bytes 3670016 | tf_op jit(solution)/shard_map/dot_general | solution.py:87
  34.1 1.0 %pad_maximum_fusion.4 = bf16[128,2560]{1,0:T(8,128)(2,1)S(1)} fusion(bf16[128,1280]{1,0:T(8,128)(2,1)S(1)} %collective-permute-done.8, bf16[128,640]{1,0:T(8,128)(2,1)S(1)} %collective-permute-done.7, bf16[128,640]{1,0:T(8,128)(2,1)} %collective-permute-done.6), kind=kLoop, calls=%fused_computation.19 | loop fusion | flops 1966080 | bytes 1310720 | tf_op jit(solution)/shard_map/concatenate | solution.py:82
  35.1 0.6 collective-permute-done.3
  35.7 0.4 convert_add_fusion.3
  36.1 0.5 fusion.12
  36.6 0.7 %fusion.1 = bf16[128,512]{1,0:T(8,128)(2,1)S(1)} fusion(bf16[128,2560]{1,0:T(8,128)(2,1)S(1)} %pad_maximum_fusion.4, f32[128,512]{1,0:T(8,128)S(1)} %fusion.12, bf16[640,512]{1,0:T(8,128)(2,1)S(1)} %copy-done.5, bf16[640,512]{1,0:T(8,128)(2,1)S(1)} %copy-done.6, bf16[640,512]{1,0:T(8,128)(2,1)S(1)} %copy-done.4, bf16[640,512]{1,0:T(8,128)(2,1)S(1)} %copy-done.3), kind=kOutput, calls=%fused_computation.16 | convolution fusion | flops 346423296 | bytes 3670016 | tf_op jit(solution)/shard_map/dot_general | solution.py:87
  37.9 1.0 %pad_maximum_fusion.5 = bf16[128,2560]{1,0:T(8,128)(2,1)S(1)} fusion(bf16[128,1280]{1,0:T(8,128)(2,1)S(1)} %collective-permute-done.14, bf16[128,640]{1,0:T(8,128)(2,1)S(1)} %collective-permute-done.13, bf16[128,640]{1,0:T(8,128)(2,1)} %collective-permute-done.12), kind=kLoop, calls=%fused_computation.20 | loop fusion | flops 1966080 | bytes 1310720 | tf_op jit(solution)/shard_map/concatenate | solution.py:82
  38.9 1.6 %collective-permute-start.4 = (bf16[128,640]{1,0:T(8,128)(2,1)S(1)}, bf16[128,640]{1,0:T(8,128)(2,1)S(1)}, u32[]{:S(2)}, u32[]{:S(2)}) collective-permute-start(bf16[128,640]{1,0:T(8,128)(2,1)S(1)} %slice.67), channel_id=1, source_target_pairs={{0,2},{1,3},{2,0},{3,1},{4,6},{5,7},{6,4},{7,5},{8,10},{9,11},{10,... | collective-permute-start | bytes 491528 | tf_op jit(solution)/shard_map/ppermute | solution.py:94
  40.4 0.4 convert_add_fusion.2
  40.8 0.5 fusion.13
  41.3 0.7 %fusion.2 = bf16[128,512]{1,0:T(8,128)(2,1)S(1)} fusion(bf16[128,2560]{1,0:T(8,128)(2,1)S(1)} %pad_maximum_fusion.5, f32[128,512]{1,0:T(8,128)S(1)} %fusion.13, bf16[640,512]{1,0:T(8,128)(2,1)S(1)} %copy-done.5, bf16[640,512]{1,0:T(8,128)(2,1)S(1)} %copy-done.6, bf16[640,512]{1,0:T(8,128)(2,1)S(1)} %copy-done.4, bf16[640,512]{1,0:T(8,128)(2,1)S(1)} %copy-done.3), kind=kOutput, calls=%fused_computation.17 | convolution fusion | flops 346423296 | bytes 3670016 | tf_op jit(solution)/shard_map/dot_general | solution.py:87
  42.6 2.8 %collective-permute-done.4 = bf16[128,640]{1,0:T(8,128)(2,1)S(1)} collective-permute-done((bf16[128,640]{1,0:T(8,128)(2,1)S(1)}, bf16[128,640]{1,0:T(8,128)(2,1)S(1)}, u32[]{:S(2)}, u32[]{:S(2)}) %collective-permute-start.4) | collective-permute-done | bytes 163872 | tf_op jit(solution)/shard_map/ppermute | solution.py:94
  45.4 2.7 %collective-permute-start.5 = (bf16[128,640]{1,0:T(8,128)(2,1)S(1)}, bf16[128,640]{1,0:T(8,128)(2,1)S(1)}, u32[]{:S(2)}, u32[]{:S(2)}) collective-permute-start(bf16[128,640]{1,0:T(8,128)(2,1)S(1)} %fusion.9), channel_id=1, source_target_pairs={{0,12},{4,8},{8,4},{12,0},{1,13},{5,9},{9,5},{13,1},{2,14},{6,10},... | collective-permute-start | bytes 491528 | tf_op jit(solution)/shard_map/ppermute | solution.py:99
  48.2 1.6 %collective-permute-start.10 = (bf16[128,640]{1,0:T(8,128)(2,1)S(1)}, bf16[128,640]{1,0:T(8,128)(2,1)S(1)}, u32[]{:S(2)}, u32[]{:S(2)}) collective-permute-start(bf16[128,640]{1,0:T(8,128)(2,1)S(1)} %slice.66), channel_id=1, source_target_pairs={{0,2},{1,3},{2,0},{3,1},{4,6},{5,7},{6,4},{7,5},{8,10},{9,11},{10,... | collective-permute-start | bytes 491528 | tf_op jit(solution)/shard_map/ppermute | solution.py:94
  49.7 0.4 convert_add_fusion.1
  50.1 0.6 collective-permute-start.16
  50.7 0.5 fusion.14
  51.2 0.7 %fusion.3 = bf16[128,512]{1,0:T(8,128)(2,1)S(1)} fusion(bf16[128,2560]{1,0:T(8,128)(2,1)S(1)} %pad_maximum_fusion.6, f32[128,512]{1,0:T(8,128)S(1)} %fusion.14, bf16[640,512]{1,0:T(8,128)(2,1)S(1)} %copy-done.5, bf16[640,512]{1,0:T(8,128)(2,1)S(1)} %copy-done.6, bf16[640,512]{1,0:T(8,128)(2,1)S(1)} %copy-done.4, bf16[640,512]{1,0:T(8,128)(2,1)S(1)} %copy-done.3), kind=kOutput, calls=%fused_computation.18 | convolution fusion | flops 346423296 | bytes 3670016 | tf_op jit(solution)/shard_map/dot_general | solution.py:87
  52.4 2.9 %collective-permute-done.10 = bf16[128,640]{1,0:T(8,128)(2,1)S(1)} collective-permute-done((bf16[128,640]{1,0:T(8,128)(2,1)S(1)}, bf16[128,640]{1,0:T(8,128)(2,1)S(1)}, u32[]{:S(2)}, u32[]{:S(2)}) %collective-permute-start.10) | collective-permute-done | bytes 163872 | tf_op jit(solution)/shard_map/ppermute | solution.py:94
  55.4 3.6 %collective-permute-start.11 = (bf16[128,640]{1,0:T(8,128)(2,1)S(1)}, bf16[128,640]{1,0:T(8,128)(2,1)S(1)}, u32[]{:S(2)}, u32[]{:S(2)}) collective-permute-start(bf16[128,640]{1,0:T(8,128)(2,1)S(1)} %fusion.8), channel_id=1, source_target_pairs={{0,8},{4,12},{8,0},{12,4},{1,9},{5,13},{9,1},{13,5},{2,10},{6,14},... | collective-permute-start | bytes 491528 | tf_op jit(solution)/shard_map/ppermute | solution.py:99
  59.0 0.9 %collective-permute-start.17 = (bf16[128,640]{1,0:T(8,128)(2,1)S(1)}, bf16[128,640]{1,0:T(8,128)(2,1)S(1)}, u32[]{:S(2)}, u32[]{:S(2)}) collective-permute-start(bf16[128,640]{1,0:T(8,128)(2,1)S(1)} %fusion.7), channel_id=1, source_target_pairs={{0,4},{4,0},{8,12},{12,8},{1,5},{5,1},{9,13},{13,9},{2,6},{6,2},{1... | collective-permute-start | bytes 491528 | tf_op jit(solution)/shard_map/ppermute | solution.py:99
  59.9 0.4 convert_add_fusion
  60.3 1.0 %collective-permute-start.21 = (bf16[128,640]{1,0:T(8,128)(2,1)S(1)}, bf16[128,640]{1,0:T(8,128)(2,1)S(1)}, u32[]{:S(2)}, u32[]{:S(2)}) collective-permute-start(bf16[128,640]{1,0:T(8,128)(2,1)S(1)} %slice.64), channel_id=1, source_target_pairs={{0,2},{1,3},{2,0},{3,1},{4,6},{5,7},{6,4},{7,5},{8,10},{9,11},{10,... | collective-permute-start | bytes 491528 | tf_op jit(solution)/shard_map/ppermute | solution.py:94
  61.3 2.1 %collective-permute-done.11 = bf16[128,640]{1,0:T(8,128)(2,1)S(1)} collective-permute-done((bf16[128,640]{1,0:T(8,128)(2,1)S(1)}, bf16[128,640]{1,0:T(8,128)(2,1)S(1)}, u32[]{:S(2)}, u32[]{:S(2)}) %collective-permute-start.11) | collective-permute-done | bytes 163872 | tf_op jit(solution)/shard_map/ppermute | solution.py:99
  63.4 1.4 %collective-permute-done.17 = bf16[128,640]{1,0:T(8,128)(2,1)S(1)} collective-permute-done((bf16[128,640]{1,0:T(8,128)(2,1)S(1)}, bf16[128,640]{1,0:T(8,128)(2,1)S(1)}, u32[]{:S(2)}, u32[]{:S(2)}) %collective-permute-start.17) | collective-permute-done | bytes 163872 | tf_op jit(solution)/shard_map/ppermute | solution.py:99
  64.8 0.9 %collective-permute-done.21 = bf16[128,640]{1,0:T(8,128)(2,1)S(1)} collective-permute-done((bf16[128,640]{1,0:T(8,128)(2,1)S(1)}, bf16[128,640]{1,0:T(8,128)(2,1)S(1)}, u32[]{:S(2)}, u32[]{:S(2)}) %collective-permute-start.21) | collective-permute-done | bytes 163872 | tf_op jit(solution)/shard_map/ppermute | solution.py:94
  65.7 0.9 %fusion.6 = bf16[128,640]{1,0:T(8,128)(2,1)} fusion(f32[128,1280]{1,0:T(8,128)S(1)} %convert_add_fusion, bf16[128,640]{1,0:T(8,128)(2,1)S(1)} %collective-permute-done.21, bf16[128,640]{1,0:T(8,128)(2,1)S(1)} %collective-permute-done.17, bf16[128,640]{1,0:T(8,128)(2,1)S(1)} %collective-permute-done.11, bf16[128,640]{1,0:T(8,128)(2,1)S(1)} %collective-permute-done.5, ...), kind=kLoop, calls=%fused_computation.42 | loop fusion | flops 1064960 | bytes 1147392 | tf_op jit(solution)/shard_map/convert_element_type | solution.py:103
  (56 shorter events, 3.2 us)
Async XLA Ops:
  1.0 10.9 %collective-permute-start = (bf16[128,640]{1,0:T(8,128)(2,1)S(1)}, bf16[128,640]{1,0:T(8,128)(2,1)}, u32[]{:S(2)}, u32[]{:S(2)}) collective-permute-start(bf16[128,640]{1,0:T(8,128)(2,1)S(1)} %multiply_convert_fusion), channel_id=1, source_target_pairs={{0,12},{4,8},{8,4},{12,0},{1,13},{5,9},{9,5},{13,1},{2,14},{6,10},... | collective-permute-start | bytes 491528 | tf_op jit(solution)/shard_map/ppermute | solution.py:66
  6.1 14.0 %collective-permute-start.6 = (bf16[128,640]{1,0:T(8,128)(2,1)S(1)}, bf16[128,640]{1,0:T(8,128)(2,1)}, u32[]{:S(2)}, u32[]{:S(2)}) collective-permute-start(bf16[128,640]{1,0:T(8,128)(2,1)S(1)} %multiply_convert_fusion), channel_id=1, source_target_pairs={{0,8},{4,12},{8,0},{12,4},{1,9},{5,13},{9,1},{13,5},{2,10},{6,14},... | collective-permute-start | bytes 491528 | tf_op jit(solution)/shard_map/ppermute | solution.py:66
  6.1 15.5 %collective-permute-start.12 = (bf16[128,640]{1,0:T(8,128)(2,1)S(1)}, bf16[128,640]{1,0:T(8,128)(2,1)}, u32[]{:S(2)}, u32[]{:S(2)}) collective-permute-start(bf16[128,640]{1,0:T(8,128)(2,1)S(1)} %multiply_convert_fusion), channel_id=1, source_target_pairs={{0,4},{4,0},{8,12},{12,8},{1,5},{5,1},{9,13},{13,9},{2,6},{6,2},{1... | collective-permute-start | bytes 491528 | tf_op jit(solution)/shard_map/ppermute | solution.py:66
  8.6 1.7 %copy-start = (bf16[1,2560,512]{2,1,0:T(8,128)(2,1)S(1)}, bf16[1,2560,512]{2,1,0:T(8,128)(2,1)}, u32[]{:S(2)}) copy-start(bf16[1,2560,512]{2,1,0:T(8,128)(2,1)} %param.10) | copy-start | bytes 7864324
  10.4 3.2 %copy-start.1 = (bf16[1,512,2560]{2,1,0:T(8,128)(2,1)S(1)}, bf16[1,512,2560]{2,1,0:T(8,128)(2,1)}, u32[]{:S(2)}) copy-start(bf16[1,512,2560]{2,1,0:T(8,128)(2,1)} %param.11) | copy-start | bytes 7864324
  11.9 11.2 %collective-permute-start.1 = (bf16[128,640]{1,0:T(8,128)(2,1)}, bf16[128,640]{1,0:T(8,128)(2,1)}, u32[]{:S(2)}, u32[]{:S(2)}) collective-permute-start(bf16[128,640]{1,0:T(8,128)(2,1)} %collective-permute-done), channel_id=1, source_target_pairs={{0,2},{1,3},{2,0},{3,1},{4,6},{5,7},{6,4},{7,5},{8,10},{9,11},{10,... | collective-permute-start | bytes 491528 | tf_op jit(solution)/shard_map/ppermute | solution.py:81
  14.9 15.2 %collective-permute-start.18 = (bf16[128,640]{1,0:T(8,128)(2,1)S(1)}, bf16[128,640]{1,0:T(8,128)(2,1)S(1)}, u32[]{:S(2)}, u32[]{:S(2)}) collective-permute-start(bf16[128,640]{1,0:T(8,128)(2,1)S(1)} %multiply_convert_fusion), channel_id=1, source_target_pairs={{0,2},{1,3},{2,0},{3,1},{4,6},{5,7},{6,4},{7,5},{8,10},{9,11},{10,... | collective-permute-start | bytes 491528 | tf_op jit(solution)/shard_map/ppermute | solution.py:81
  20.1 7.2 %collective-permute-start.7 = (bf16[128,640]{1,0:T(8,128)(2,1)}, bf16[128,640]{1,0:T(8,128)(2,1)S(1)}, u32[]{:S(2)}, u32[]{:S(2)}) collective-permute-start(bf16[128,640]{1,0:T(8,128)(2,1)} %collective-permute-done.6), channel_id=1, source_target_pairs={{0,2},{1,3},{2,0},{3,1},{4,6},{5,7},{6,4},{7,5},{8,10},{9,11},{10,... | collective-permute-start | bytes 491528 | tf_op jit(solution)/shard_map/ppermute | solution.py:81
  21.6 7.5 %collective-permute-start.13 = (bf16[128,640]{1,0:T(8,128)(2,1)}, bf16[128,640]{1,0:T(8,128)(2,1)S(1)}, u32[]{:S(2)}, u32[]{:S(2)}) collective-permute-start(bf16[128,640]{1,0:T(8,128)(2,1)} %collective-permute-done.12), channel_id=1, source_target_pairs={{0,2},{1,3},{2,0},{3,1},{4,6},{5,7},{6,4},{7,5},{8,10},{9,11},{10,... | collective-permute-start | bytes 491528 | tf_op jit(solution)/shard_map/ppermute | solution.py:81
  24.1 7.6 %collective-permute-start.2 = (bf16[128,1280]{1,0:T(8,128)(2,1)S(1)}, bf16[128,1280]{1,0:T(8,128)(2,1)S(1)}, u32[]{:S(2)}, u32[]{:S(2)}) collective-permute-start(bf16[128,1280]{1,0:T(8,128)(2,1)S(1)} %pad_maximum_fusion.7), channel_id=1, source_target_pairs={{0,1},{1,0},{2,3},{3,2},{4,5},{5,4},{6,7},{7,6},{8,9},{9,8},{10,11... | collective-permute-start | bytes 983048 | tf_op jit(solution)/shard_map/ppermute | solution.py:83
  28.3 5.8 %collective-permute-start.8 = (bf16[128,1280]{1,0:T(8,128)(2,1)S(1)}, bf16[128,1280]{1,0:T(8,128)(2,1)S(1)}, u32[]{:S(2)}, u32[]{:S(2)}) collective-permute-start(bf16[128,1280]{1,0:T(8,128)(2,1)S(1)} %pad_maximum_fusion.8), channel_id=1, source_target_pairs={{0,1},{1,0},{2,3},{3,2},{4,5},{5,4},{6,7},{7,6},{8,9},{9,8},{10,11... | collective-permute-start | bytes 983048 | tf_op jit(solution)/shard_map/ppermute | solution.py:83
  30.0 2.3 %copy-start.3 = (bf16[640,512]{1,0:T(8,128)(2,1)S(1)}, bf16[640,512]{1,0:T(8,128)(2,1)}, u32[]{:S(2)}) copy-start(bf16[640,512]{1,0:T(8,128)(2,1)} %get-tuple-element.17) | copy-start | bytes 1966084
  30.1 2.3 %copy-start.4 = (bf16[640,512]{1,0:T(8,128)(2,1)S(1)}, bf16[640,512]{1,0:T(8,128)(2,1)}, u32[]{:S(2)}) copy-start(bf16[640,512]{1,0:T(8,128)(2,1)} %get-tuple-element.18) | copy-start | bytes 1966084
  30.1 2.3 %copy-start.5 = (bf16[640,512]{1,0:T(8,128)(2,1)S(1)}, bf16[640,512]{1,0:T(8,128)(2,1)}, u32[]{:S(2)}) copy-start(bf16[640,512]{1,0:T(8,128)(2,1)} %get-tuple-element.19) | copy-start | bytes 1966084
  30.1 2.3 %copy-start.6 = (bf16[640,512]{1,0:T(8,128)(2,1)S(1)}, bf16[640,512]{1,0:T(8,128)(2,1)}, u32[]{:S(2)}) copy-start(bf16[640,512]{1,0:T(8,128)(2,1)} %get-tuple-element.20) | copy-start | bytes 1966084
  30.1 7.8 %collective-permute-start.14 = (bf16[128,1280]{1,0:T(8,128)(2,1)S(1)}, bf16[128,1280]{1,0:T(8,128)(2,1)S(1)}, u32[]{:S(2)}, u32[]{:S(2)}) collective-permute-start(bf16[128,1280]{1,0:T(8,128)(2,1)S(1)} %pad_maximum_fusion.9), channel_id=1, source_target_pairs={{0,1},{1,0},{2,3},{3,2},{4,5},{5,4},{6,7},{7,6},{8,9},{9,8},{10,11... | collective-permute-start | bytes 983048 | tf_op jit(solution)/shard_map/ppermute | solution.py:83
  30.2 12.4 %collective-permute-start.19 = (bf16[128,1280]{1,0:T(8,128)(2,1)S(1)}, bf16[128,1280]{1,0:T(8,128)(2,1)S(1)}, u32[]{:S(2)}, u32[]{:S(2)}) collective-permute-start(bf16[128,1280]{1,0:T(8,128)(2,1)S(1)} %pad_maximum_fusion.10), channel_id=1, source_target_pairs={{0,1},{1,0},{2,3},{3,2},{4,5},{5,4},{6,7},{7,6},{8,9},{9,8},{10,11... | collective-permute-start | bytes 983048 | tf_op jit(solution)/shard_map/ppermute | solution.py:83
  32.4 1.1 %copy-start.7 = (bf16[512,640]{1,0:T(8,128)(2,1)S(1)}, bf16[512,640]{1,0:T(8,128)(2,1)}, u32[]{:S(2)}) copy-start(bf16[512,640]{1,0:T(8,128)(2,1)} %get-tuple-element.13) | copy-start | bytes 1966084
  32.4 1.3 %copy-start.8 = (bf16[512,640]{1,0:T(8,128)(2,1)S(1)}, bf16[512,640]{1,0:T(8,128)(2,1)}, u32[]{:S(2)}) copy-start(bf16[512,640]{1,0:T(8,128)(2,1)} %get-tuple-element.16) | copy-start | bytes 1966084
  33.1 2.6 %copy-start.2 = (bf16[512,640]{1,0:T(8,128)(2,1)S(1)}, bf16[512,640]{1,0:T(8,128)(2,1)}, u32[]{:S(2)}) copy-start(bf16[512,640]{1,0:T(8,128)(2,1)} %get-tuple-element.15) | copy-start | bytes 1966084
  34.0 1.7 %collective-permute-start.3 = (bf16[128,1280]{1,0:T(8,128)(2,1)S(1)}, bf16[128,1280]{1,0:T(8,128)(2,1)S(1)}, u32[]{:S(2)}, u32[]{:S(2)}) collective-permute-start(bf16[128,1280]{1,0:T(8,128)(2,1)S(1)} %convolution_convert_fusion.6), channel_id=1, source_target_pairs={{0,1},{1,0},{2,3},{3,2},{4,5},{5,4},{6,7},{7,6},{8,9},{9,8},{10,11... | collective-permute-start | bytes 983048 | tf_op jit(solution)/shard_map/ppermute | solution.py:92
  37.7 2.8 %collective-permute-start.9 = (bf16[128,1280]{1,0:T(8,128)(2,1)S(1)}, bf16[128,1280]{1,0:T(8,128)(2,1)S(1)}, u32[]{:S(2)}, u32[]{:S(2)}) collective-permute-start(bf16[128,1280]{1,0:T(8,128)(2,1)S(1)} %convolution_convert_fusion.4), channel_id=1, source_target_pairs={{0,1},{1,0},{2,3},{3,2},{4,5},{5,4},{6,7},{7,6},{8,9},{9,8},{10,11... | collective-permute-start | bytes 983048 | tf_op jit(solution)/shard_map/ppermute | solution.py:92
  38.9 6.5 %collective-permute-start.4 = (bf16[128,640]{1,0:T(8,128)(2,1)S(1)}, bf16[128,640]{1,0:T(8,128)(2,1)S(1)}, u32[]{:S(2)}, u32[]{:S(2)}) collective-permute-start(bf16[128,640]{1,0:T(8,128)(2,1)S(1)} %slice.67), channel_id=1, source_target_pairs={{0,2},{1,3},{2,0},{3,1},{4,6},{5,7},{6,4},{7,5},{8,10},{9,11},{10,... | collective-permute-start | bytes 491528 | tf_op jit(solution)/shard_map/ppermute | solution.py:94
  42.4 7.3 %collective-permute-start.15 = (bf16[128,1280]{1,0:T(8,128)(2,1)S(1)}, bf16[128,1280]{1,0:T(8,128)(2,1)S(1)}, u32[]{:S(2)}, u32[]{:S(2)}) collective-permute-start(bf16[128,1280]{1,0:T(8,128)(2,1)S(1)} %convolution_convert_fusion.2), channel_id=1, source_target_pairs={{0,1},{1,0},{2,3},{3,2},{4,5},{5,4},{6,7},{7,6},{8,9},{9,8},{10,11... | collective-permute-start | bytes 983048 | tf_op jit(solution)/shard_map/ppermute | solution.py:92
  45.4 15.8 %collective-permute-start.5 = (bf16[128,640]{1,0:T(8,128)(2,1)S(1)}, bf16[128,640]{1,0:T(8,128)(2,1)S(1)}, u32[]{:S(2)}, u32[]{:S(2)}) collective-permute-start(bf16[128,640]{1,0:T(8,128)(2,1)S(1)} %fusion.9), channel_id=1, source_target_pairs={{0,12},{4,8},{8,4},{12,0},{1,13},{5,9},{9,5},{13,1},{2,14},{6,10},... | collective-permute-start | bytes 491528 | tf_op jit(solution)/shard_map/ppermute | solution.py:99
  48.2 7.2 %collective-permute-start.10 = (bf16[128,640]{1,0:T(8,128)(2,1)S(1)}, bf16[128,640]{1,0:T(8,128)(2,1)S(1)}, u32[]{:S(2)}, u32[]{:S(2)}) collective-permute-start(bf16[128,640]{1,0:T(8,128)(2,1)S(1)} %slice.66), channel_id=1, source_target_pairs={{0,2},{1,3},{2,0},{3,1},{4,6},{5,7},{6,4},{7,5},{8,10},{9,11},{10,... | collective-permute-start | bytes 491528 | tf_op jit(solution)/shard_map/ppermute | solution.py:94
  50.1 8.9 %collective-permute-start.16 = (bf16[128,640]{1,0:T(8,128)(2,1)S(1)}, bf16[128,640]{1,0:T(8,128)(2,1)S(1)}, u32[]{:S(2)}, u32[]{:S(2)}) collective-permute-start(bf16[128,640]{1,0:T(8,128)(2,1)S(1)} %slice.65), channel_id=1, source_target_pairs={{0,2},{1,3},{2,0},{3,1},{4,6},{5,7},{6,4},{7,5},{8,10},{9,11},{10,... | collective-permute-start | bytes 491528 | tf_op jit(solution)/shard_map/ppermute | solution.py:94
  52.3 8.9 %copy-start.9 = (s32[128,1]{0,1:T(1,128)S(1)}, s32[128,1]{0,1:T(1,128)}, u32[]{:S(2)}) copy-start(s32[128,1]{0,1:T(1,128)} %param.8) | copy-start | bytes 1540
  52.3 7.6 %collective-permute-start.20 = (bf16[128,1280]{1,0:T(8,128)(2,1)S(1)}, bf16[128,1280]{1,0:T(8,128)(2,1)S(1)}, u32[]{:S(2)}, u32[]{:S(2)}) collective-permute-start(bf16[128,1280]{1,0:T(8,128)(2,1)S(1)} %convolution_convert_fusion), channel_id=1, source_target_pairs={{0,1},{1,0},{2,3},{3,2},{4,5},{5,4},{6,7},{7,6},{8,9},{9,8},{10,11... | collective-permute-start | bytes 983048 | tf_op jit(solution)/shard_map/ppermute | solution.py:92
  55.4 8.0 %collective-permute-start.11 = (bf16[128,640]{1,0:T(8,128)(2,1)S(1)}, bf16[128,640]{1,0:T(8,128)(2,1)S(1)}, u32[]{:S(2)}, u32[]{:S(2)}) collective-permute-start(bf16[128,640]{1,0:T(8,128)(2,1)S(1)} %fusion.8), channel_id=1, source_target_pairs={{0,8},{4,12},{8,0},{12,4},{1,9},{5,13},{9,1},{13,5},{2,10},{6,14},... | collective-permute-start | bytes 491528 | tf_op jit(solution)/shard_map/ppermute | solution.py:99
  59.0 5.8 %collective-permute-start.17 = (bf16[128,640]{1,0:T(8,128)(2,1)S(1)}, bf16[128,640]{1,0:T(8,128)(2,1)S(1)}, u32[]{:S(2)}, u32[]{:S(2)}) collective-permute-start(bf16[128,640]{1,0:T(8,128)(2,1)S(1)} %fusion.7), channel_id=1, source_target_pairs={{0,4},{4,0},{8,12},{12,8},{1,5},{5,1},{9,13},{13,9},{2,6},{6,2},{1... | collective-permute-start | bytes 491528 | tf_op jit(solution)/shard_map/ppermute | solution.py:99
  60.3 5.4 %collective-permute-start.21 = (bf16[128,640]{1,0:T(8,128)(2,1)S(1)}, bf16[128,640]{1,0:T(8,128)(2,1)S(1)}, u32[]{:S(2)}, u32[]{:S(2)}) collective-permute-start(bf16[128,640]{1,0:T(8,128)(2,1)S(1)} %slice.64), channel_id=1, source_target_pairs={{0,2},{1,3},{2,0},{3,1},{4,6},{5,7},{6,4},{7,5},{8,10},{9,11},{10,... | collective-permute-start | bytes 491528 | tf_op jit(solution)/shard_map/ppermute | solution.py:94

commit v23 on v21

--- a/solution.py
+++ b/solution.py
@@ -70,7 +70,7 @@
     up_w = _slots(up_weight[0], t, width, 0)
     down_keep = _slots(down_weight[0], t, width, 1, _ORDER[:2])
     down_send = _slots(down_weight[0], t, width, 1, _ORDER[2:])
-    waves = [[k] for k in list(range(n_expert - 1, 1, -1)) + [1][:n_expert - 1] + [0]]
+    waves = [[k] for k in (n_expert - 1,) + tuple(range(1, n_expert - 1)) + (0,)] if n_expert > 1 else [[0]]
     total = None
     previous = None
     for wave in waves:

time: 62.9 us -> 63.1 us (level)
  waiting for transfers between devices: 17.7 us -> 18.8 us
  starting transfers between devices: 21.3 us -> 20.3 us
    ppermute x3, waiting for transfers between devices: 3.72 us -> 6.87 us  [gathered(): lax.ppermute(part.astype(jnp.bfloat16), 'expert', _xor_pairs(n_expert, k))]
    ppermute x3, waiting for transfers between devices: 4.4 us -> 2.69 us  [gathered(): lax.ppermute(scaled, 'expert', _xor_pairs(n_expert, k))]
    ppermute x4, waiting for transfers between devices: 3.91 us -> 2.22 us  [gathered(): lax.ppermute(piece, 'tensor', _xor_pairs(n_tensor, 2))]
    ppermute x4, waiting for transfers between devices: 5.33 us -> 6.69 us  [gathered(): lax.ppermute(over_c[:, width:].astype(jnp.bfloat16), 'tensor', _xor_pairs...]
    ppermute x3, starting transfers between devices: 5 us -> 3.81 us  [gathered(): lax.ppermute(part.astype(jnp.bfloat16), 'expert', _xor_pairs(n_expert, k))]
    ppermute x4, starting transfers between devices: 4.13 us -> 5.28 us  [gathered(): lax.ppermute(piece, 'tensor', _xor_pairs(n_tensor, 2))]
    ppermute x4, starting transfers between devices: 4.96 us -> 4.01 us  [gathered(): lax.ppermute(over_c[:, width:].astype(jnp.bfloat16), 'tensor', _xor_pairs...]
where the time goes in v23:
time: 63.1 us; the launch traced here: 62.7 us
  starting transfers between devices  20.3 us (32%)
  waiting for transfers between devices  18.8 us (30%)
  other arithmetic  8.86 us (14%)
  matrix products  7.72 us (12%)
  local copies, waits for them, and re-layouts  6.68 us (11%)
    ppermute x3, waiting for transfers between devices, gathered(): lax.ppermute(part.astype(jnp.bfloat16), 'expert', _xor_pairs(n_expert, k))  6.87 us
    ppermute x4, waiting for transfers between devices, gathered(): lax.ppermute(over_c[:, width:].astype(jnp.bfloat16), 'tensor', _xor_pairs...  6.69 us
    ppermute x3, starting transfers between devices, gathered(): lax.ppermute(scaled, 'expert', _xor_pairs(n_expert, k))  5.76 us
    ppermute x4, starting transfers between devices, gathered(): lax.ppermute(piece, 'tensor', _xor_pairs(n_tensor, 2))  5.28 us
    ppermute x4, starting transfers between devices, gathered(): lax.ppermute(over_c[:, width:].astype(jnp.bfloat16), 'tensor', _xor_pairs...  4.01 us
    ppermute x3, starting transfers between devices, gathered(): lax.ppermute(part.astype(jnp.bfloat16), 'expert', _xor_pairs(n_expert, k))  3.81 us
    concatenate x4, other arithmetic, gathered(): jnp.concatenate([piece, lax.ppermute(piece, 'tensor', _xor_pairs(n_tensor...  3.77 us
    dynamic_slice x3, local copies, waits for them, and re-layouts, _slots(): lax.dynamic_slice_in_dim(weight, (t ^ k) * width, width, axis=axis)  3.54 us
  transfers between devices with their start and end apart: 22, of which 9 were waited for; matrix products, arithmetic and copies ran while one was open for 31% of the time, Pallas kernels for 0%

profile of v23, /device:TPU:0, one launch (start us, length us, event | category | flops | bytes accessed | tf_op | source)
XLA Modules:
  0.0 62.7 jit_solution(4907800540612804621)
XLA Ops:
  0.0 1.0 %multiply_convert_fusion = bf16[128,640]{1,0:T(8,128)(2,1)S(1)} fusion(bf16[128,640]{1,0:T(8,128)(2,1)} %param.6, f32[128]{0:T(128)} %param.7), kind=kLoop, calls=%fused_computation.56 | loop fusion | flops 245760 | bytes 328192 | tf_op jit(solution)/shard_map/convert_element_type | solution.py:64
  1.0 5.1 %collective-permute-start = (bf16[128,640]{1,0:T(8,128)(2,1)S(1)}, bf16[128,640]{1,0:T(8,128)(2,1)}, u32[]{:S(2)}, u32[]{:S(2)}) collective-permute-start(bf16[128,640]{1,0:T(8,128)(2,1)S(1)} %multiply_convert_fusion), channel_id=1, source_target_pairs={{0,12},{4,8},{8,4},{12,0},{1,13},{5,9},{9,5},{13,1},{2,14},{6,10},... | collective-permute-start | bytes 491528 | tf_op jit(solution)/shard_map/ppermute | solution.py:66
  6.1 0.6 %collective-permute-start.12 = (bf16[128,640]{1,0:T(8,128)(2,1)S(1)}, bf16[128,640]{1,0:T(8,128)(2,1)}, u32[]{:S(2)}, u32[]{:S(2)}) collective-permute-start(bf16[128,640]{1,0:T(8,128)(2,1)S(1)} %multiply_convert_fusion), channel_id=1, source_target_pairs={{0,8},{4,12},{8,0},{12,4},{1,9},{5,13},{9,1},{13,5},{2,10},{6,14},... | collective-permute-start | bytes 491528 | tf_op jit(solution)/shard_map/ppermute | solution.py:66
  6.8 1.6 %collective-permute-start.18 = (bf16[128,640]{1,0:T(8,128)(2,1)S(1)}, bf16[128,640]{1,0:T(8,128)(2,1)}, u32[]{:S(2)}, u32[]{:S(2)}) collective-permute-start(bf16[128,640]{1,0:T(8,128)(2,1)S(1)} %multiply_convert_fusion), channel_id=1, source_target_pairs={{0,2},{1,3},{2,0},{3,1},{4,6},{5,7},{6,4},{7,5},{8,10},{9,11},{10,... | collective-permute-start | bytes 491528 | tf_op jit(solution)/shard_map/ppermute | solution.py:79
  8.4 2.0 %dynamic-slice_bitcast_fusion.11 = (bf16[640,512]{1,0:T(8,128)(2,1)S(1)}, bf16[640,512]{1,0:T(8,128)(2,1)S(1)}, bf16[640,512]{1,0:T(8,128)(2,1)S(1)}, bf16[640,512]{1,0:T(8,128)(2,1)S(1)}) fusion(bf16[1,2560,512]{2,1,0:T(8,128)(2,1)} %param.9, s32[]{:T(128)S(6)} %select_n.48, s32[]{:T(128)S(6)} %select_n.49, s32[]{:T(128)S(6)} %select_n.51, s32[]{:T(128)S(6)} %select_n.50), kind=kLoop, calls=%fused_computation.37 | loop fusion | bytes 5242896 | tf_op jit(solution)/shard_map/dynamic_slice | solution.py:55
  10.4 0.5 copy-done
  10.9 1.3 %dynamic-slice_bitcast_fusion.7 = (bf16[640,512]{1,0:T(8,128)(2,1)S(1)}, bf16[640,512]{1,0:T(8,128)(2,1)}, bf16[640,512]{1,0:T(8,128)(2,1)}, bf16[640,512]{1,0:T(8,128)(2,1)}) fusion(bf16[1,2560,512]{2,1,0:T(8,128)(2,1)S(1)} %copy-done, s32[]{:T(128)S(6)} %select_n.48, s32[]{:T(128)S(6)} %select_n.49, s32[]{:T(128)S(6)} %select_n.51, s32[]{:T(128)S(6)} %select_n.50), kind=kLoop, calls=%fused_computation.33 | loop fusion | bytes 5242896 | tf_op jit(solution)/shard_map/dynamic_slice | solution.py:55
  12.5 1.5 %copy-done.1 = bf16[1,512,2560]{2,1,0:T(8,128)(2,1)S(1)} copy-done((bf16[1,512,2560]{2,1,0:T(8,128)(2,1)S(1)}, bf16[1,512,2560]{2,1,0:T(8,128)(2,1)}, u32[]{:S(2)}) %copy-start.1) | copy-done | bytes 2621464
  14.2 0.5 collective-permute-start.1
  14.7 0.9 %pad_maximum_fusion.10 = bf16[128,1280]{1,0:T(8,128)(2,1)S(1)} fusion(bf16[128,640]{1,0:T(8,128)(2,1)} %collective-permute-done.18, bf16[128,640]{1,0:T(8,128)(2,1)S(1)} %multiply_convert_fusion), kind=kLoop, calls=%fused_computation.55 | loop fusion | flops 655360 | bytes 655360 | tf_op jit(solution)/shard_map/concatenate | solution.py:78
  15.7 1.7 %collective-permute-start.7 = (bf16[128,640]{1,0:T(8,128)(2,1)}, bf16[128,640]{1,0:T(8,128)(2,1)S(1)}, u32[]{:S(2)}, u32[]{:S(2)}) collective-permute-start(bf16[128,640]{1,0:T(8,128)(2,1)} %collective-permute-done.6), channel_id=1, source_target_pairs={{0,2},{1,3},{2,0},{3,1},{4,6},{5,7},{6,4},{7,5},{8,10},{9,11},{10,... | collective-permute-start | bytes 491528 | tf_op jit(solution)/shard_map/ppermute | solution.py:79
  17.4 2.7 %collective-permute-done.12 = bf16[128,640]{1,0:T(8,128)(2,1)} collective-permute-done((bf16[128,640]{1,0:T(8,128)(2,1)S(1)}, bf16[128,640]{1,0:T(8,128)(2,1)}, u32[]{:S(2)}, u32[]{:S(2)}) %collective-permute-start.12) | collective-permute-done | bytes 163872 | tf_op jit(solution)/shard_map/ppermute | solution.py:66
  20.1 1.5 %collective-permute-start.13 = (bf16[128,640]{1,0:T(8,128)(2,1)}, bf16[128,640]{1,0:T(8,128)(2,1)S(1)}, u32[]{:S(2)}, u32[]{:S(2)}) collective-permute-start(bf16[128,640]{1,0:T(8,128)(2,1)} %collective-permute-done.12), channel_id=1, source_target_pairs={{0,2},{1,3},{2,0},{3,1},{4,6},{5,7},{6,4},{7,5},{8,10},{9,11},{10,... | collective-permute-start | bytes 491528 | tf_op jit(solution)/shard_map/ppermute | solution.py:79
  21.6 0.9 %constant_dynamic-update-slice_fusion.2 = bf16[128,2560]{1,0:T(8,128)(2,1)S(1)} fusion(bf16[128,640]{1,0:T(8,128)(2,1)} %collective-permute-done), kind=kLoop, calls=%fused_computation.60 | loop fusion | bytes 327680
  22.6 0.9 %pad_maximum_fusion.7 = bf16[128,1280]{1,0:T(8,128)(2,1)S(1)} fusion(bf16[128,640]{1,0:T(8,128)(2,1)S(1)} %collective-permute-done.1, bf16[128,640]{1,0:T(8,128)(2,1)} %collective-permute-done), kind=kLoop, calls=%fused_computation.52 | loop fusion | flops 655360 | bytes 655360 | tf_op jit(solution)/shard_map/concatenate | solution.py:78
  23.6 0.6 collective-permute-done.7
  24.1 0.9 %pad_maximum_fusion.8 = bf16[128,1280]{1,0:T(8,128)(2,1)S(1)} fusion(bf16[128,640]{1,0:T(8,128)(2,1)S(1)} %collective-permute-done.7, bf16[128,640]{1,0:T(8,128)(2,1)} %collective-permute-done.6), kind=kLoop, calls=%fused_computation.53 | loop fusion | flops 655360 | bytes 655360 | tf_op jit(solution)/shard_map/concatenate | solution.py:78
  25.2 1.7 %collective-permute-done.13 = bf16[128,640]{1,0:T(8,128)(2,1)S(1)} collective-permute-done((bf16[128,640]{1,0:T(8,128)(2,1)}, bf16[128,640]{1,0:T(8,128)(2,1)S(1)}, u32[]{:S(2)}, u32[]{:S(2)}) %collective-permute-start.13) | collective-permute-done | bytes 163872 | tf_op jit(solution)/shard_map/ppermute | solution.py:79
  26.9 0.9 %pad_maximum_fusion.9 = bf16[128,1280]{1,0:T(8,128)(2,1)S(1)} fusion(bf16[128,640]{1,0:T(8,128)(2,1)S(1)} %collective-permute-done.13, bf16[128,640]{1,0:T(8,128)(2,1)} %collective-permute-done.12), kind=kLoop, calls=%fused_computation.54 | loop fusion | flops 655360 | bytes 655360 | tf_op jit(solution)/shard_map/concatenate | solution.py:78
  27.9 0.5 fusion.11
  28.5 0.7 %multiply_convert_fusion.1 = bf16[128,512]{1,0:T(8,128)(2,1)S(1)} fusion(f32[128,512]{1,0:T(8,128)S(1)} %fusion.11, bf16[128,2560]{1,0:T(8,128)(2,1)S(1)} %constant_dynamic-update-slice_fusion, bf16[640,512]{1,0:T(8,128)(2,1)S(1)} %copy-done.3, bf16[640,512]{1,0:T(8,128)(2,1)S(1)} %copy-done.4, bf16[640,512]{1,0:T(8,128)(2,1)S(1)} %copy-done.2, ...), kind=kOutput, calls=%fused_computation.57 | convolution fusion | flops 346423296 | bytes 3670016 | tf_op jit(solution)/shard_map/dot_general | solution.py:85
  29.2 0.3 convolution_convert_fusion.6
  29.6 0.6 collective-permute-start.3
  30.1 1.0 %pad_maximum_fusion.4 = bf16[128,2560]{1,0:T(8,128)(2,1)S(1)} fusion(bf16[128,1280]{1,0:T(8,128)(2,1)S(1)} %collective-permute-done.8, bf16[128,640]{1,0:T(8,128)(2,1)S(1)} %collective-permute-done.7, bf16[128,640]{1,0:T(8,128)(2,1)} %collective-permute-done.6), kind=kLoop, calls=%fused_computation.19 | loop fusion | flops 1966080 | bytes 1310720 | tf_op jit(solution)/shard_map/concatenate | solution.py:80
  31.8 0.5 fusion.12
  32.3 0.7 %fusion.1 = bf16[128,512]{1,0:T(8,128)(2,1)S(1)} fusion(bf16[128,2560]{1,0:T(8,128)(2,1)S(1)} %pad_maximum_fusion.4, f32[128,512]{1,0:T(8,128)S(1)} %fusion.12, bf16[640,512]{1,0:T(8,128)(2,1)S(1)} %copy-done.3, bf16[640,512]{1,0:T(8,128)(2,1)S(1)} %copy-done.4, bf16[640,512]{1,0:T(8,128)(2,1)S(1)} %copy-done.2, bf16[640,512]{1,0:T(8,128)(2,1)S(1)} %get-tuple-element.15), kind=kOutput, calls=%fused_computation.16 | convolution fusion | flops 346423296 | bytes 3670016 | tf_op jit(solution)/shard_map/dot_general | solution.py:85
  33.0 0.3 convolution_convert_fusion.4
  33.4 0.4 collective-permute-start.9
  33.8 1.0 %pad_maximum_fusion.5 = bf16[128,2560]{1,0:T(8,128)(2,1)S(1)} fusion(bf16[128,1280]{1,0:T(8,128)(2,1)S(1)} %collective-permute-done.14, bf16[128,640]{1,0:T(8,128)(2,1)S(1)} %collective-permute-done.13, bf16[128,640]{1,0:T(8,128)(2,1)} %collective-permute-done.12), kind=kLoop, calls=%fused_computation.20 | loop fusion | flops 1966080 | bytes 1310720 | tf_op jit(solution)/shard_map/concatenate | solution.py:80
  34.8 0.9 %collective-permute-start.4 = (bf16[128,640]{1,0:T(8,128)(2,1)S(1)}, bf16[128,640]{1,0:T(8,128)(2,1)S(1)}, u32[]{:S(2)}, u32[]{:S(2)}) collective-permute-start(bf16[128,640]{1,0:T(8,128)(2,1)S(1)} %slice.67), channel_id=1, source_target_pairs={{0,2},{1,3},{2,0},{3,1},{4,6},{5,7},{6,4},{7,5},{8,10},{9,11},{10,... | collective-permute-start | bytes 491528 | tf_op jit(solution)/shard_map/ppermute | solution.py:92
  35.7 0.3 convert_add_fusion.2
  36.1 0.5 fusion.13
  36.6 0.7 %fusion.2 = bf16[128,512]{1,0:T(8,128)(2,1)S(1)} fusion(bf16[128,2560]{1,0:T(8,128)(2,1)S(1)} %pad_maximum_fusion.5, f32[128,512]{1,0:T(8,128)S(1)} %fusion.13, bf16[640,512]{1,0:T(8,128)(2,1)S(1)} %copy-done.3, bf16[640,512]{1,0:T(8,128)(2,1)S(1)} %copy-done.4, bf16[640,512]{1,0:T(8,128)(2,1)S(1)} %copy-done.2, bf16[640,512]{1,0:T(8,128)(2,1)S(1)} %get-tuple-element.15), kind=kOutput, calls=%fused_computation.17 | convolution fusion | flops 346423296 | bytes 3670016 | tf_op jit(solution)/shard_map/dot_general | solution.py:85
  37.3 0.3 convolution_convert_fusion.2
  37.8 1.0 %pad_maximum_fusion.6 = bf16[128,2560]{1,0:T(8,128)(2,1)S(1)} fusion(bf16[128,1280]{1,0:T(8,128)(2,1)S(1)} %collective-permute-done.19, bf16[128,640]{1,0:T(8,128)(2,1)} %collective-permute-done.18, bf16[128,640]{1,0:T(8,128)(2,1)S(1)} %multiply_convert_fusion), kind=kLoop, calls=%fused_computation.21 | loop fusion | flops 1966080 | bytes 1310720 | tf_op jit(solution)/shard_map/concatenate | solution.py:80
  38.7 2.4 %collective-permute-done.4 = bf16[128,640]{1,0:T(8,128)(2,1)S(1)} collective-permute-done((bf16[128,640]{1,0:T(8,128)(2,1)S(1)}, bf16[128,640]{1,0:T(8,128)(2,1)S(1)}, u32[]{:S(2)}, u32[]{:S(2)}) %collective-permute-start.4) | collective-permute-done | bytes 163872 | tf_op jit(solution)/shard_map/ppermute | solution.py:92
  41.1 3.7 %collective-permute-start.5 = (bf16[128,640]{1,0:T(8,128)(2,1)S(1)}, bf16[128,640]{1,0:T(8,128)(2,1)S(1)}, u32[]{:S(2)}, u32[]{:S(2)}) collective-permute-start(bf16[128,640]{1,0:T(8,128)(2,1)S(1)} %fusion.9), channel_id=1, source_target_pairs={{0,12},{4,8},{8,4},{12,0},{1,13},{5,9},{9,5},{13,1},{2,14},{6,10},... | collective-permute-start | bytes 491528 | tf_op jit(solution)/shard_map/ppermute | solution.py:97
  44.8 0.9 %collective-permute-start.10 = (bf16[128,640]{1,0:T(8,128)(2,1)S(1)}, bf16[128,640]{1,0:T(8,128)(2,1)S(1)}, u32[]{:S(2)}, u32[]{:S(2)}) collective-permute-start(bf16[128,640]{1,0:T(8,128)(2,1)S(1)} %slice.66), channel_id=1, source_target_pairs={{0,2},{1,3},{2,0},{3,1},{4,6},{5,7},{6,4},{7,5},{8,10},{9,11},{10,... | collective-permute-start | bytes 491528 | tf_op jit(solution)/shard_map/ppermute | solution.py:92
  46.1 1.2 %collective-permute-start.16 = (bf16[128,640]{1,0:T(8,128)(2,1)S(1)}, bf16[128,640]{1,0:T(8,128)(2,1)S(1)}, u32[]{:S(2)}, u32[]{:S(2)}) collective-permute-start(bf16[128,640]{1,0:T(8,128)(2,1)S(1)} %slice.65), channel_id=1, source_target_pairs={{0,2},{1,3},{2,0},{3,1},{4,6},{5,7},{6,4},{7,5},{8,10},{9,11},{10,... | collective-permute-start | bytes 491528 | tf_op jit(solution)/shard_map/ppermute | solution.py:92
  47.4 0.5 fusion.14
  47.9 0.7 %fusion.3 = bf16[128,512]{1,0:T(8,128)(2,1)S(1)} fusion(bf16[128,2560]{1,0:T(8,128)(2,1)S(1)} %pad_maximum_fusion.6, f32[128,512]{1,0:T(8,128)S(1)} %fusion.14, bf16[640,512]{1,0:T(8,128)(2,1)S(1)} %copy-done.3, bf16[640,512]{1,0:T(8,128)(2,1)S(1)} %copy-done.4, bf16[640,512]{1,0:T(8,128)(2,1)S(1)} %copy-done.2, bf16[640,512]{1,0:T(8,128)(2,1)S(1)} %get-tuple-element.15), kind=kOutput, calls=%fused_computation.18 | convolution fusion | flops 346423296 | bytes 3670016 | tf_op jit(solution)/shard_map/dot_general | solution.py:85
  48.6 0.3 convolution_convert_fusion
  49.1 2.7 %collective-permute-done.10 = bf16[128,640]{1,0:T(8,128)(2,1)S(1)} collective-permute-done((bf16[128,640]{1,0:T(8,128)(2,1)S(1)}, bf16[128,640]{1,0:T(8,128)(2,1)S(1)}, u32[]{:S(2)}, u32[]{:S(2)}) %collective-permute-start.10) | collective-permute-done | bytes 163872 | tf_op jit(solution)/shard_map/ppermute | solution.py:92
  51.9 1.6 %collective-permute-done.16 = bf16[128,640]{1,0:T(8,128)(2,1)S(1)} collective-permute-done((bf16[128,640]{1,0:T(8,128)(2,1)S(1)}, bf16[128,640]{1,0:T(8,128)(2,1)S(1)}, u32[]{:S(2)}, u32[]{:S(2)}) %collective-permute-start.16) | collective-permute-done | bytes 163872 | tf_op jit(solution)/shard_map/ppermute | solution.py:92
  54.0 0.9 %collective-permute-start.21 = (bf16[128,640]{1,0:T(8,128)(2,1)S(1)}, bf16[128,640]{1,0:T(8,128)(2,1)S(1)}, u32[]{:S(2)}, u32[]{:S(2)}) collective-permute-start(bf16[128,640]{1,0:T(8,128)(2,1)S(1)} %slice.64), channel_id=1, source_target_pairs={{0,2},{1,3},{2,0},{3,1},{4,6},{5,7},{6,4},{7,5},{8,10},{9,11},{10,... | collective-permute-start | bytes 491528 | tf_op jit(solution)/shard_map/ppermute | solution.py:92
  55.0 3.5 %collective-permute-done.11 = bf16[128,640]{1,0:T(8,128)(2,1)S(1)} collective-permute-done((bf16[128,640]{1,0:T(8,128)(2,1)S(1)}, bf16[128,640]{1,0:T(8,128)(2,1)S(1)}, u32[]{:S(2)}, u32[]{:S(2)}) %collective-permute-start.11) | collective-permute-done | bytes 163872 | tf_op jit(solution)/shard_map/ppermute | solution.py:97
  58.5 3.4 %collective-permute-done.17 = bf16[128,640]{1,0:T(8,128)(2,1)S(1)} collective-permute-done((bf16[128,640]{1,0:T(8,128)(2,1)S(1)}, bf16[128,640]{1,0:T(8,128)(2,1)S(1)}, u32[]{:S(2)}, u32[]{:S(2)}) %collective-permute-start.17) | collective-permute-done | bytes 163872 | tf_op jit(solution)/shard_map/ppermute | solution.py:97
  61.8 0.9 %fusion.6 = bf16[128,640]{1,0:T(8,128)(2,1)} fusion(f32[128,1280]{1,0:T(8,128)S(1)} %convert_add_fusion, bf16[128,640]{1,0:T(8,128)(2,1)S(1)} %collective-permute-done.21, bf16[128,640]{1,0:T(8,128)(2,1)S(1)} %collective-permute-done.17, bf16[128,640]{1,0:T(8,128)(2,1)S(1)} %collective-permute-done.11, bf16[128,640]{1,0:T(8,128)(2,1)S(1)} %collective-permute-done.5, ...), kind=kLoop, calls=%fused_computation.42 | loop fusion | flops 1064960 | bytes 1147392 | tf_op jit(solution)/shard_map/convert_element_type | solution.py:101
  (48 shorter events, 2.6 us)
Async XLA Ops:
  1.0 13.2 %collective-permute-start = (bf16[128,640]{1,0:T(8,128)(2,1)S(1)}, bf16[128,640]{1,0:T(8,128)(2,1)}, u32[]{:S(2)}, u32[]{:S(2)}) collective-permute-start(bf16[128,640]{1,0:T(8,128)(2,1)S(1)} %multiply_convert_fusion), channel_id=1, source_target_pairs={{0,12},{4,8},{8,4},{12,0},{1,13},{5,9},{9,5},{13,1},{2,14},{6,10},... | collective-permute-start | bytes 491528 | tf_op jit(solution)/shard_map/ppermute | solution.py:66
  6.1 9.6 %collective-permute-start.6 = (bf16[128,640]{1,0:T(8,128)(2,1)S(1)}, bf16[128,640]{1,0:T(8,128)(2,1)}, u32[]{:S(2)}, u32[]{:S(2)}) collective-permute-start(bf16[128,640]{1,0:T(8,128)(2,1)S(1)} %multiply_convert_fusion), channel_id=1, source_target_pairs={{0,4},{4,0},{8,12},{12,8},{1,5},{5,1},{9,13},{13,9},{2,6},{6,2},{1... | collective-permute-start | bytes 491528 | tf_op jit(solution)/shard_map/ppermute | solution.py:66
  6.1 14.0 %collective-permute-start.12 = (bf16[128,640]{1,0:T(8,128)(2,1)S(1)}, bf16[128,640]{1,0:T(8,128)(2,1)}, u32[]{:S(2)}, u32[]{:S(2)}) collective-permute-start(bf16[128,640]{1,0:T(8,128)(2,1)S(1)} %multiply_convert_fusion), channel_id=1, source_target_pairs={{0,8},{4,12},{8,0},{12,4},{1,9},{5,13},{9,1},{13,5},{2,10},{6,14},... | collective-permute-start | bytes 491528 | tf_op jit(solution)/shard_map/ppermute | solution.py:66
  6.8 7.9 %collective-permute-start.18 = (bf16[128,640]{1,0:T(8,128)(2,1)S(1)}, bf16[128,640]{1,0:T(8,128)(2,1)}, u32[]{:S(2)}, u32[]{:S(2)}) collective-permute-start(bf16[128,640]{1,0:T(8,128)(2,1)S(1)} %multiply_convert_fusion), channel_id=1, source_target_pairs={{0,2},{1,3},{2,0},{3,1},{4,6},{5,7},{6,4},{7,5},{8,10},{9,11},{10,... | collective-permute-start | bytes 491528 | tf_op jit(solution)/shard_map/ppermute | solution.py:79
  8.4 2.5 %copy-start = (bf16[1,2560,512]{2,1,0:T(8,128)(2,1)S(1)}, bf16[1,2560,512]{2,1,0:T(8,128)(2,1)}, u32[]{:S(2)}) copy-start(bf16[1,2560,512]{2,1,0:T(8,128)(2,1)} %param.10) | copy-start | bytes 7864324
  12.3 1.7 %copy-start.1 = (bf16[1,512,2560]{2,1,0:T(8,128)(2,1)S(1)}, bf16[1,512,2560]{2,1,0:T(8,128)(2,1)}, u32[]{:S(2)}) copy-start(bf16[1,512,2560]{2,1,0:T(8,128)(2,1)} %param.11) | copy-start | bytes 7864324
  14.2 8.3 %collective-permute-start.1 = (bf16[128,640]{1,0:T(8,128)(2,1)}, bf16[128,640]{1,0:T(8,128)(2,1)S(1)}, u32[]{:S(2)}, u32[]{:S(2)}) collective-permute-start(bf16[128,640]{1,0:T(8,128)(2,1)} %collective-permute-done), channel_id=1, source_target_pairs={{0,2},{1,3},{2,0},{3,1},{4,6},{5,7},{6,4},{7,5},{8,10},{9,11},{10,... | collective-permute-start | bytes 491528 | tf_op jit(solution)/shard_map/ppermute | solution.py:79
  15.6 22.1 %collective-permute-start.19 = (bf16[128,1280]{1,0:T(8,128)(2,1)S(1)}, bf16[128,1280]{1,0:T(8,128)(2,1)S(1)}, u32[]{:S(2)}, u32[]{:S(2)}) collective-permute-start(bf16[128,1280]{1,0:T(8,128)(2,1)S(1)} %pad_maximum_fusion.10), channel_id=1, source_target_pairs={{0,1},{1,0},{2,3},{3,2},{4,5},{5,4},{6,7},{7,6},{8,9},{9,8},{10,11... | collective-permute-start | bytes 983048 | tf_op jit(solution)/shard_map/ppermute | solution.py:81
  15.7 8.4 %collective-permute-start.7 = (bf16[128,640]{1,0:T(8,128)(2,1)}, bf16[128,640]{1,0:T(8,128)(2,1)S(1)}, u32[]{:S(2)}, u32[]{:S(2)}) collective-permute-start(bf16[128,640]{1,0:T(8,128)(2,1)} %collective-permute-done.6), channel_id=1, source_target_pairs={{0,2},{1,3},{2,0},{3,1},{4,6},{5,7},{6,4},{7,5},{8,10},{9,11},{10,... | collective-permute-start | bytes 491528 | tf_op jit(solution)/shard_map/ppermute | solution.py:79
  20.1 6.7 %collective-permute-start.13 = (bf16[128,640]{1,0:T(8,128)(2,1)}, bf16[128,640]{1,0:T(8,128)(2,1)S(1)}, u32[]{:S(2)}, u32[]{:S(2)}) collective-permute-start(bf16[128,640]{1,0:T(8,128)(2,1)} %collective-permute-done.12), channel_id=1, source_target_pairs={{0,2},{1,3},{2,0},{3,1},{4,6},{5,7},{6,4},{7,5},{8,10},{9,11},{10,... | collective-permute-start | bytes 491528 | tf_op jit(solution)/shard_map/ppermute | solution.py:79
  23.5 4.4 %collective-permute-start.2 = (bf16[128,1280]{1,0:T(8,128)(2,1)S(1)}, bf16[128,1280]{1,0:T(8,128)(2,1)S(1)}, u32[]{:S(2)}, u32[]{:S(2)}) collective-permute-start(bf16[128,1280]{1,0:T(8,128)(2,1)S(1)} %pad_maximum_fusion.7), channel_id=1, source_target_pairs={{0,1},{1,0},{2,3},{3,2},{4,5},{5,4},{6,7},{7,6},{8,9},{9,8},{10,11... | collective-permute-start | bytes 983048 | tf_op jit(solution)/shard_map/ppermute | solution.py:81
  25.1 3.4 %copy-start.2 = (bf16[640,512]{1,0:T(8,128)(2,1)S(1)}, bf16[640,512]{1,0:T(8,128)(2,1)}, u32[]{:S(2)}) copy-start(bf16[640,512]{1,0:T(8,128)(2,1)} %get-tuple-element.16) | copy-start | bytes 1966084
  25.1 3.4 %copy-start.3 = (bf16[640,512]{1,0:T(8,128)(2,1)S(1)}, bf16[640,512]{1,0:T(8,128)(2,1)}, u32[]{:S(2)}) copy-start(bf16[640,512]{1,0:T(8,128)(2,1)} %get-tuple-element.17) | copy-start | bytes 1966084
  25.1 3.4 %copy-start.4 = (bf16[640,512]{1,0:T(8,128)(2,1)S(1)}, bf16[640,512]{1,0:T(8,128)(2,1)}, u32[]{:S(2)}) copy-start(bf16[640,512]{1,0:T(8,128)(2,1)} %get-tuple-element.18) | copy-start | bytes 1966084
  25.1 5.0 %collective-permute-start.8 = (bf16[128,1280]{1,0:T(8,128)(2,1)S(1)}, bf16[128,1280]{1,0:T(8,128)(2,1)S(1)}, u32[]{:S(2)}, u32[]{:S(2)}) collective-permute-start(bf16[128,1280]{1,0:T(8,128)(2,1)S(1)} %pad_maximum_fusion.8), channel_id=1, source_target_pairs={{0,1},{1,0},{2,3},{3,2},{4,5},{5,4},{6,7},{7,6},{8,9},{9,8},{10,11... | collective-permute-start | bytes 983048 | tf_op jit(solution)/shard_map/ppermute | solution.py:81
  27.8 6.0 %collective-permute-start.14 = (bf16[128,1280]{1,0:T(8,128)(2,1)S(1)}, bf16[128,1280]{1,0:T(8,128)(2,1)S(1)}, u32[]{:S(2)}, u32[]{:S(2)}) collective-permute-start(bf16[128,1280]{1,0:T(8,128)(2,1)S(1)} %pad_maximum_fusion.9), channel_id=1, source_target_pairs={{0,1},{1,0},{2,3},{3,2},{4,5},{5,4},{6,7},{7,6},{8,9},{9,8},{10,11... | collective-permute-start | bytes 983048 | tf_op jit(solution)/shard_map/ppermute | solution.py:81
  29.6 1.8 %collective-permute-start.3 = (bf16[128,1280]{1,0:T(8,128)(2,1)S(1)}, bf16[128,1280]{1,0:T(8,128)(2,1)S(1)}, u32[]{:S(2)}, u32[]{:S(2)}) collective-permute-start(bf16[128,1280]{1,0:T(8,128)(2,1)S(1)} %convolution_convert_fusion.6), channel_id=1, source_target_pairs={{0,1},{1,0},{2,3},{3,2},{4,5},{5,4},{6,7},{7,6},{8,9},{9,8},{10,11... | collective-permute-start | bytes 983048 | tf_op jit(solution)/shard_map/ppermute | solution.py:90
  33.4 2.4 %collective-permute-start.9 = (bf16[128,1280]{1,0:T(8,128)(2,1)S(1)}, bf16[128,1280]{1,0:T(8,128)(2,1)S(1)}, u32[]{:S(2)}, u32[]{:S(2)}) collective-permute-start(bf16[128,1280]{1,0:T(8,128)(2,1)S(1)} %convolution_convert_fusion.4), channel_id=1, source_target_pairs={{0,1},{1,0},{2,3},{3,2},{4,5},{5,4},{6,7},{7,6},{8,9},{9,8},{10,11... | collective-permute-start | bytes 983048 | tf_op jit(solution)/shard_map/ppermute | solution.py:90
  34.8 6.3 %collective-permute-start.4 = (bf16[128,640]{1,0:T(8,128)(2,1)S(1)}, bf16[128,640]{1,0:T(8,128)(2,1)S(1)}, u32[]{:S(2)}, u32[]{:S(2)}) collective-permute-start(bf16[128,640]{1,0:T(8,128)(2,1)S(1)} %slice.67), channel_id=1, source_target_pairs={{0,2},{1,3},{2,0},{3,1},{4,6},{5,7},{6,4},{7,5},{8,10},{9,11},{10,... | collective-permute-start | bytes 491528 | tf_op jit(solution)/shard_map/ppermute | solution.py:92
  37.7 8.1 %collective-permute-start.15 = (bf16[128,1280]{1,0:T(8,128)(2,1)S(1)}, bf16[128,1280]{1,0:T(8,128)(2,1)S(1)}, u32[]{:S(2)}, u32[]{:S(2)}) collective-permute-start(bf16[128,1280]{1,0:T(8,128)(2,1)S(1)} %convolution_convert_fusion.2), channel_id=1, source_target_pairs={{0,1},{1,0},{2,3},{3,2},{4,5},{5,4},{6,7},{7,6},{8,9},{9,8},{10,11... | collective-permute-start | bytes 983048 | tf_op jit(solution)/shard_map/ppermute | solution.py:90
  41.1 13.8 %collective-permute-start.5 = (bf16[128,640]{1,0:T(8,128)(2,1)S(1)}, bf16[128,640]{1,0:T(8,128)(2,1)S(1)}, u32[]{:S(2)}, u32[]{:S(2)}) collective-permute-start(bf16[128,640]{1,0:T(8,128)(2,1)S(1)} %fusion.9), channel_id=1, source_target_pairs={{0,12},{4,8},{8,4},{12,0},{1,13},{5,9},{9,5},{13,1},{2,14},{6,10},... | collective-permute-start | bytes 491528 | tf_op jit(solution)/shard_map/ppermute | solution.py:97
  44.8 6.9 %collective-permute-start.10 = (bf16[128,640]{1,0:T(8,128)(2,1)S(1)}, bf16[128,640]{1,0:T(8,128)(2,1)S(1)}, u32[]{:S(2)}, u32[]{:S(2)}) collective-permute-start(bf16[128,640]{1,0:T(8,128)(2,1)S(1)} %slice.66), channel_id=1, source_target_pairs={{0,2},{1,3},{2,0},{3,1},{4,6},{5,7},{6,4},{7,5},{8,10},{9,11},{10,... | collective-permute-start | bytes 491528 | tf_op jit(solution)/shard_map/ppermute | solution.py:92
  46.1 7.4 %collective-permute-start.16 = (bf16[128,640]{1,0:T(8,128)(2,1)S(1)}, bf16[128,640]{1,0:T(8,128)(2,1)S(1)}, u32[]{:S(2)}, u32[]{:S(2)}) collective-permute-start(bf16[128,640]{1,0:T(8,128)(2,1)S(1)} %slice.65), channel_id=1, source_target_pairs={{0,2},{1,3},{2,0},{3,1},{4,6},{5,7},{6,4},{7,5},{8,10},{9,11},{10,... | collective-permute-start | bytes 491528 | tf_op jit(solution)/shard_map/ppermute | solution.py:92
  49.0 6.0 %copy-start.5 = (s32[128,1]{0,1:T(1,128)S(1)}, s32[128,1]{0,1:T(1,128)}, u32[]{:S(2)}) copy-start(s32[128,1]{0,1:T(1,128)} %param.8) | copy-start | bytes 1540
  49.0 4.6 %collective-permute-start.20 = (bf16[128,1280]{1,0:T(8,128)(2,1)S(1)}, bf16[128,1280]{1,0:T(8,128)(2,1)S(1)}, u32[]{:S(2)}, u32[]{:S(2)}) collective-permute-start(bf16[128,1280]{1,0:T(8,128)(2,1)S(1)} %convolution_convert_fusion), channel_id=1, source_target_pairs={{0,1},{1,0},{2,3},{3,2},{4,5},{5,4},{6,7},{7,6},{8,9},{9,8},{10,11... | collective-permute-start | bytes 983048 | tf_op jit(solution)/shard_map/ppermute | solution.py:90
  51.8 6.7 %collective-permute-start.11 = (bf16[128,640]{1,0:T(8,128)(2,1)S(1)}, bf16[128,640]{1,0:T(8,128)(2,1)S(1)}, u32[]{:S(2)}, u32[]{:S(2)}) collective-permute-start(bf16[128,640]{1,0:T(8,128)(2,1)S(1)} %fusion.8), channel_id=1, source_target_pairs={{0,4},{4,0},{8,12},{12,8},{1,5},{5,1},{9,13},{13,9},{2,6},{6,2},{1... | collective-permute-start | bytes 491528 | tf_op jit(solution)/shard_map/ppermute | solution.py:97
  53.5 8.3 %collective-permute-start.17 = (bf16[128,640]{1,0:T(8,128)(2,1)S(1)}, bf16[128,640]{1,0:T(8,128)(2,1)S(1)}, u32[]{:S(2)}, u32[]{:S(2)}) collective-permute-start(bf16[128,640]{1,0:T(8,128)(2,1)S(1)} %fusion.7), channel_id=1, source_target_pairs={{0,8},{4,12},{8,0},{12,4},{1,9},{5,13},{9,1},{13,5},{2,10},{6,14},... | collective-permute-start | bytes 491528 | tf_op jit(solution)/shard_map/ppermute | solution.py:97
  54.0 7.8 %collective-permute-start.21 = (bf16[128,640]{1,0:T(8,128)(2,1)S(1)}, bf16[128,640]{1,0:T(8,128)(2,1)S(1)}, u32[]{:S(2)}, u32[]{:S(2)}) collective-permute-start(bf16[128,640]{1,0:T(8,128)(2,1)S(1)} %slice.64), channel_id=1, source_target_pairs={{0,2},{1,3},{2,0},{3,1},{4,6},{5,7},{6,4},{7,5},{8,10},{9,11},{10,... | collective-permute-start | bytes 491528 | tf_op jit(solution)/shard_map/ppermute | solution.py:92

commit v24 on v21

--- a/solution.py
+++ b/solution.py
@@ -87,6 +87,13 @@
         keep = jnp.dot(hidden, down_keep, preferred_element_type=jnp.float32).astype(jnp.bfloat16)
         send = jnp.dot(hidden, down_send, preferred_element_type=jnp.float32).astype(jnp.bfloat16)
         previous = keep
+        if wave == [0] and n_expert > 1:
+            part = keep[:, :width].astype(jnp.float32)
+            for values, k in [(keep[:, width:], 2), (send[:, :width], 1), (send[:, width:], 3)]:
+                part = part + lax.ppermute(values, "tensor", _xor_pairs(n_tensor, k)).astype(jnp.float32)
+            part = jnp.where(routed == me // SPAN, part, 0.0)
+            total = part if total is None else total + part
+            continue
         over_c = keep.astype(jnp.float32) + lax.ppermute(
             send, "tensor", _xor_pairs(n_tensor, 1)).astype(jnp.float32)
         summed = over_c[:, :width] + lax.ppermute(

time: 62.9 us -> 68.7 us (1.092)
  waiting for transfers between devices: 17.7 us -> 23.2 us
    ppermute x0 -> x3, waiting for transfers between devices: none -> 4.84 us  [gathered(): lax.ppermute(values, 'tensor', _xor_pairs(n_tensor, k)).astype(jnp.float32)]
    ppermute x4 -> x3, waiting for transfers between devices: 5.33 us -> 7.84 us  [gathered(): lax.ppermute(over_c[:, width:].astype(jnp.bfloat16), 'tensor', _xor_pairs...]
    ppermute x3, waiting for transfers between devices: 3.72 us -> 1.89 us  [gathered(): lax.ppermute(part.astype(jnp.bfloat16), 'expert', _xor_pairs(n_expert, k))]
    ppermute x4 -> x3, starting transfers between devices: 4.96 us -> 3.41 us  [gathered(): lax.ppermute(over_c[:, width:].astype(jnp.bfloat16), 'tensor', _xor_pairs...]
    ppermute x0 -> x3, starting transfers between devices: none -> 0.98 us  [gathered(): lax.ppermute(values, 'tensor', _xor_pairs(n_tensor, k)).astype(jnp.float32)]
  transfers between devices with their start and end apart: 22 -> 23, of which waited for: 9 -> 11; matrix products, arithmetic and copies ran while one was open for 31% -> 28% of each run, Pallas kernels for 0% -> 0%
where the time goes in v24:
time: 68.7 us; the launch traced here: 68.3 us
  waiting for transfers between devices  23.2 us (34%)
  starting transfers between devices  21.2 us (31%)
  other arithmetic  9.04 us (13%)
  matrix products  7.73 us (11%)
  local copies, waits for them, and re-layouts  6.67 us (10%)
    ppermute x3, waiting for transfers between devices, gathered(): lax.ppermute(over_c[:, width:].astype(jnp.bfloat16), 'tensor', _xor_pairs...  7.84 us
    ppermute x3, starting transfers between devices, gathered(): lax.ppermute(scaled, 'expert', _xor_pairs(n_expert, k))  5.76 us
    ppermute x3, starting transfers between devices, gathered(): lax.ppermute(part.astype(jnp.bfloat16), 'expert', _xor_pairs(n_expert, k))  5.61 us
    ppermute x3, waiting for transfers between devices, gathered(): lax.ppermute(values, 'tensor', _xor_pairs(n_tensor, k)).astype(jnp.float32)  4.84 us
    ppermute x3, waiting for transfers between devices, gathered(): lax.ppermute(scaled, 'expert', _xor_pairs(n_expert, k))  4.44 us
    ppermute x4, starting transfers between devices, gathered(): lax.ppermute(piece, 'tensor', _xor_pairs(n_tensor, 2))  4.13 us
    ppermute x4, waiting for transfers between devices, gathered(): lax.ppermute(piece, 'tensor', _xor_pairs(n_tensor, 2))  3.94 us
    concatenate x4, other arithmetic, gathered(): jnp.concatenate([piece, lax.ppermute(piece, 'tensor', _xor_pairs(n_tensor...  3.77 us
  transfers between devices with their start and end apart: 23, of which 11 were waited for; matrix products, arithmetic and copies ran while one was open for 28% of the time, Pallas kernels for 0%

profile of v24, /device:TPU:0, one launch (start us, length us, event | category | flops | bytes accessed | tf_op | source)
XLA Modules:
  0.0 68.3 jit_solution(9159847307602558332)
XLA Ops:
  0.0 1.0 %multiply_convert_fusion = bf16[128,640]{1,0:T(8,128)(2,1)S(1)} fusion(bf16[128,640]{1,0:T(8,128)(2,1)} %param.6, f32[128]{0:T(128)} %param.7), kind=kLoop, calls=%fused_computation.50 | loop fusion | flops 245760 | bytes 328192 | tf_op jit(solution)/shard_map/convert_element_type | solution.py:64
  1.0 5.1 %collective-permute-start = (bf16[128,640]{1,0:T(8,128)(2,1)S(1)}, bf16[128,640]{1,0:T(8,128)(2,1)}, u32[]{:S(2)}, u32[]{:S(2)}) collective-permute-start(bf16[128,640]{1,0:T(8,128)(2,1)S(1)} %multiply_convert_fusion), channel_id=1, source_target_pairs={{0,12},{4,8},{8,4},{12,0},{1,13},{5,9},{9,5},{13,1},{2,14},{6,10},... | collective-permute-start | bytes 491528 | tf_op jit(solution)/shard_map/ppermute | solution.py:66
  6.1 0.6 collective-permute-start.12
  6.8 1.6 %collective-permute-start.18 = (bf16[128,640]{1,0:T(8,128)(2,1)S(1)}, bf16[128,640]{1,0:T(8,128)(2,1)}, u32[]{:S(2)}, u32[]{:S(2)}) collective-permute-start(bf16[128,640]{1,0:T(8,128)(2,1)S(1)} %multiply_convert_fusion), channel_id=1, source_target_pairs={{0,2},{1,3},{2,0},{3,1},{4,6},{5,7},{6,4},{7,5},{8,10},{9,11},{10,... | collective-permute-start | bytes 491528 | tf_op jit(solution)/shard_map/ppermute | solution.py:79
  8.4 2.0 %dynamic-slice_bitcast_fusion.11 = (bf16[640,512]{1,0:T(8,128)(2,1)S(1)}, bf16[640,512]{1,0:T(8,128)(2,1)S(1)}, bf16[640,512]{1,0:T(8,128)(2,1)S(1)}, bf16[640,512]{1,0:T(8,128)(2,1)S(1)}) fusion(bf16[1,2560,512]{2,1,0:T(8,128)(2,1)} %param.9, s32[]{:T(128)S(6)} %select_n.48, s32[]{:T(128)S(6)} %select_n.49, s32[]{:T(128)S(6)} %select_n.51, s32[]{:T(128)S(6)} %select_n.50), kind=kLoop, calls=%fused_computation.35 | loop fusion | bytes 5242896 | tf_op jit(solution)/shard_map/dynamic_slice | solution.py:55
  10.4 0.5 copy-done
  10.9 1.3 %dynamic-slice_bitcast_fusion.7 = (bf16[640,512]{1,0:T(8,128)(2,1)S(1)}, bf16[640,512]{1,0:T(8,128)(2,1)}, bf16[640,512]{1,0:T(8,128)(2,1)}, bf16[640,512]{1,0:T(8,128)(2,1)}) fusion(bf16[1,2560,512]{2,1,0:T(8,128)(2,1)S(1)} %copy-done, s32[]{:T(128)S(6)} %select_n.48, s32[]{:T(128)S(6)} %select_n.49, s32[]{:T(128)S(6)} %select_n.51, s32[]{:T(128)S(6)} %select_n.50), kind=kLoop, calls=%fused_computation.31 | loop fusion | bytes 5242896 | tf_op jit(solution)/shard_map/dynamic_slice | solution.py:55
  12.4 1.5 %copy-done.1 = bf16[1,512,2560]{2,1,0:T(8,128)(2,1)S(1)} copy-done((bf16[1,512,2560]{2,1,0:T(8,128)(2,1)S(1)}, bf16[1,512,2560]{2,1,0:T(8,128)(2,1)}, u32[]{:S(2)}) %copy-start.1) | copy-done | bytes 2621464
  14.2 0.5 collective-permute-start.1
  14.7 0.9 %pad_maximum_fusion.10 = bf16[128,1280]{1,0:T(8,128)(2,1)S(1)} fusion(bf16[128,640]{1,0:T(8,128)(2,1)} %collective-permute-done.18, bf16[128,640]{1,0:T(8,128)(2,1)S(1)} %multiply_convert_fusion), kind=kLoop, calls=%fused_computation.48 | loop fusion | flops 655360 | bytes 655360 | tf_op jit(solution)/shard_map/concatenate | solution.py:78
  15.7 4.4 %collective-permute-done.6 = bf16[128,640]{1,0:T(8,128)(2,1)} collective-permute-done((bf16[128,640]{1,0:T(8,128)(2,1)S(1)}, bf16[128,640]{1,0:T(8,128)(2,1)}, u32[]{:S(2)}, u32[]{:S(2)}) %collective-permute-start.6) | collective-permute-done | bytes 163872 | tf_op jit(solution)/shard_map/ppermute | solution.py:66
  20.1 1.5 %collective-permute-start.7 = (bf16[128,640]{1,0:T(8,128)(2,1)}, bf16[128,640]{1,0:T(8,128)(2,1)S(1)}, u32[]{:S(2)}, u32[]{:S(2)}) collective-permute-start(bf16[128,640]{1,0:T(8,128)(2,1)} %collective-permute-done.6), channel_id=1, source_target_pairs={{0,2},{1,3},{2,0},{3,1},{4,6},{5,7},{6,4},{7,5},{8,10},{9,11},{10,... | collective-permute-start | bytes 491528 | tf_op jit(solution)/shard_map/ppermute | solution.py:79
  21.6 0.5 collective-permute-start.13
  22.2 0.9 %constant_dynamic-update-slice_fusion.2 = bf16[128,2560]{1,0:T(8,128)(2,1)S(1)} fusion(bf16[128,640]{1,0:T(8,128)(2,1)} %collective-permute-done), kind=kLoop, calls=%fused_computation.54 | loop fusion | bytes 327680
  23.1 0.9 %pad_maximum_fusion.7 = bf16[128,1280]{1,0:T(8,128)(2,1)S(1)} fusion(bf16[128,640]{1,0:T(8,128)(2,1)S(1)} %collective-permute-done.1, bf16[128,640]{1,0:T(8,128)(2,1)} %collective-permute-done), kind=kLoop, calls=%fused_computation.45 | loop fusion | flops 655360 | bytes 655360 | tf_op jit(solution)/shard_map/concatenate | solution.py:78
  24.1 3.2 %collective-permute-done.7 = bf16[128,640]{1,0:T(8,128)(2,1)S(1)} collective-permute-done((bf16[128,640]{1,0:T(8,128)(2,1)}, bf16[128,640]{1,0:T(8,128)(2,1)S(1)}, u32[]{:S(2)}, u32[]{:S(2)}) %collective-permute-start.7) | collective-permute-done | bytes 163872 | tf_op jit(solution)/shard_map/ppermute | solution.py:79
  27.3 0.9 %pad_maximum_fusion.8 = bf16[128,1280]{1,0:T(8,128)(2,1)S(1)} fusion(bf16[128,640]{1,0:T(8,128)(2,1)S(1)} %collective-permute-done.7, bf16[128,640]{1,0:T(8,128)(2,1)} %collective-permute-done.6), kind=kLoop, calls=%fused_computation.46 | loop fusion | flops 655360 | bytes 655360 | tf_op jit(solution)/shard_map/concatenate | solution.py:78
  28.4 0.7 %collective-permute-done.13 = bf16[128,640]{1,0:T(8,128)(2,1)S(1)} collective-permute-done((bf16[128,640]{1,0:T(8,128)(2,1)}, bf16[128,640]{1,0:T(8,128)(2,1)S(1)}, u32[]{:S(2)}, u32[]{:S(2)}) %collective-permute-start.13) | collective-permute-done | bytes 163872 | tf_op jit(solution)/shard_map/ppermute | solution.py:79
  29.1 0.9 %pad_maximum_fusion.9 = bf16[128,1280]{1,0:T(8,128)(2,1)S(1)} fusion(bf16[128,640]{1,0:T(8,128)(2,1)S(1)} %collective-permute-done.13, bf16[128,640]{1,0:T(8,128)(2,1)} %collective-permute-done.12), kind=kLoop, calls=%fused_computation.47 | loop fusion | flops 655360 | bytes 655360 | tf_op jit(solution)/shard_map/concatenate | solution.py:78
  30.2 1.1 %pad_maximum_fusion.6 = bf16[128,2560]{1,0:T(8,128)(2,1)S(1)} fusion(bf16[128,1280]{1,0:T(8,128)(2,1)S(1)} %collective-permute-done.19, bf16[128,640]{1,0:T(8,128)(2,1)} %collective-permute-done.18, bf16[128,640]{1,0:T(8,128)(2,1)S(1)} %multiply_convert_fusion), kind=kLoop, calls=%fused_computation.20 | loop fusion | flops 1966080 | bytes 1310720 | tf_op jit(solution)/shard_map/concatenate | solution.py:80
  31.3 0.5 fusion.8
  31.9 0.7 %multiply_convert_fusion.1 = bf16[128,512]{1,0:T(8,128)(2,1)S(1)} fusion(f32[128,512]{1,0:T(8,128)S(1)} %fusion.8, bf16[128,2560]{1,0:T(8,128)(2,1)S(1)} %constant_dynamic-update-slice_fusion, bf16[640,512]{1,0:T(8,128)(2,1)S(1)} %copy-done.3, bf16[640,512]{1,0:T(8,128)(2,1)S(1)} %copy-done.4, bf16[640,512]{1,0:T(8,128)(2,1)S(1)} %copy-done.2, ...), kind=kOutput, calls=%fused_computation.51 | convolution fusion | flops 346423296 | bytes 3670016 | tf_op jit(solution)/shard_map/dot_general | solution.py:85
  32.6 0.3 convolution_convert_fusion.6
  33.0 0.6 collective-permute-start.3
  33.5 1.0 %pad_maximum_fusion.4 = bf16[128,2560]{1,0:T(8,128)(2,1)S(1)} fusion(bf16[128,1280]{1,0:T(8,128)(2,1)S(1)} %collective-permute-done.8, bf16[128,640]{1,0:T(8,128)(2,1)S(1)} %collective-permute-done.7, bf16[128,640]{1,0:T(8,128)(2,1)} %collective-permute-done.6), kind=kLoop, calls=%fused_computation.18 | loop fusion | flops 1966080 | bytes 1310720 | tf_op jit(solution)/shard_map/concatenate | solution.py:80
  35.1 0.5 fusion.9
  35.6 0.7 %fusion = bf16[128,512]{1,0:T(8,128)(2,1)S(1)} fusion(bf16[128,2560]{1,0:T(8,128)(2,1)S(1)} %pad_maximum_fusion.4, f32[128,512]{1,0:T(8,128)S(1)} %fusion.9, bf16[640,512]{1,0:T(8,128)(2,1)S(1)} %copy-done.3, bf16[640,512]{1,0:T(8,128)(2,1)S(1)} %copy-done.4, bf16[640,512]{1,0:T(8,128)(2,1)S(1)} %copy-done.2, bf16[640,512]{1,0:T(8,128)(2,1)S(1)} %get-tuple-element.15), kind=kOutput, calls=%fused_computation.15 | convolution fusion | flops 346423296 | bytes 3670016 | tf_op jit(solution)/shard_map/dot_general | solution.py:85
  36.4 0.3 convolution_convert_fusion.4
  36.7 0.4 collective-permute-start.9
  37.2 1.0 %pad_maximum_fusion.5 = bf16[128,2560]{1,0:T(8,128)(2,1)S(1)} fusion(bf16[128,1280]{1,0:T(8,128)(2,1)S(1)} %collective-permute-done.14, bf16[128,640]{1,0:T(8,128)(2,1)S(1)} %collective-permute-done.13, bf16[128,640]{1,0:T(8,128)(2,1)} %collective-permute-done.12), kind=kLoop, calls=%fused_computation.19 | loop fusion | flops 1966080 | bytes 1310720 | tf_op jit(solution)/shard_map/concatenate | solution.py:80
  38.2 1.6 %collective-permute-start.4 = (bf16[128,640]{1,0:T(8,128)(2,1)S(1)}, bf16[128,640]{1,0:T(8,128)(2,1)S(1)}, u32[]{:S(2)}, u32[]{:S(2)}) collective-permute-start(bf16[128,640]{1,0:T(8,128)(2,1)S(1)} %slice.68), channel_id=1, source_target_pairs={{0,2},{1,3},{2,0},{3,1},{4,6},{5,7},{6,4},{7,5},{8,10},{9,11},{10,... | collective-permute-start | bytes 491528 | tf_op jit(solution)/shard_map/ppermute | solution.py:99
  40.1 0.6 collective-permute-start.10
  40.7 0.5 fusion.10
  41.2 0.7 %fusion.1 = bf16[128,512]{1,0:T(8,128)(2,1)S(1)} fusion(bf16[128,2560]{1,0:T(8,128)(2,1)S(1)} %pad_maximum_fusion.5, f32[128,512]{1,0:T(8,128)S(1)} %fusion.10, bf16[640,512]{1,0:T(8,128)(2,1)S(1)} %copy-done.3, bf16[640,512]{1,0:T(8,128)(2,1)S(1)} %copy-done.4, bf16[640,512]{1,0:T(8,128)(2,1)S(1)} %copy-done.2, bf16[640,512]{1,0:T(8,128)(2,1)S(1)} %get-tuple-element.15), kind=kOutput, calls=%fused_computation.16 | convolution fusion | flops 346423296 | bytes 3670016 | tf_op jit(solution)/shard_map/dot_general | solution.py:85
  42.4 2.9 %collective-permute-done.4 = bf16[128,640]{1,0:T(8,128)(2,1)S(1)} collective-permute-done((bf16[128,640]{1,0:T(8,128)(2,1)S(1)}, bf16[128,640]{1,0:T(8,128)(2,1)S(1)}, u32[]{:S(2)}, u32[]{:S(2)}) %collective-permute-start.4) | collective-permute-done | bytes 163872 | tf_op jit(solution)/shard_map/ppermute | solution.py:99
  45.3 2.4 %collective-permute-start.5 = (bf16[128,640]{1,0:T(8,128)(2,1)S(1)}, bf16[128,640]{1,0:T(8,128)(2,1)S(1)}, u32[]{:S(2)}, u32[]{:S(2)}) collective-permute-start(bf16[128,640]{1,0:T(8,128)(2,1)S(1)} %fusion.5), channel_id=1, source_target_pairs={{0,12},{4,8},{8,4},{12,0},{1,13},{5,9},{9,5},{13,1},{2,14},{6,10},... | collective-permute-start | bytes 491528 | tf_op jit(solution)/shard_map/ppermute | solution.py:104
  48.0 3.2 %collective-permute-start.11 = (bf16[128,640]{1,0:T(8,128)(2,1)S(1)}, bf16[128,640]{1,0:T(8,128)(2,1)S(1)}, u32[]{:S(2)}, u32[]{:S(2)}) collective-permute-start(bf16[128,640]{1,0:T(8,128)(2,1)S(1)} %fusion.4), channel_id=1, source_target_pairs={{0,8},{4,12},{8,0},{12,4},{1,9},{5,13},{9,1},{13,5},{2,10},{6,14},... | collective-permute-start | bytes 491528 | tf_op jit(solution)/shard_map/ppermute | solution.py:104
  51.2 0.3 convert_add_fusion
  51.6 0.5 fusion.11
  52.1 0.7 %fusion.2 = bf16[128,512]{1,0:T(8,128)(2,1)S(1)} fusion(bf16[128,2560]{1,0:T(8,128)(2,1)S(1)} %pad_maximum_fusion.6, f32[128,512]{1,0:T(8,128)S(1)} %fusion.11, bf16[640,512]{1,0:T(8,128)(2,1)S(1)} %copy-done.3, bf16[640,512]{1,0:T(8,128)(2,1)S(1)} %copy-done.4, bf16[640,512]{1,0:T(8,128)(2,1)S(1)} %copy-done.2, bf16[640,512]{1,0:T(8,128)(2,1)S(1)} %get-tuple-element.15), kind=kOutput, calls=%fused_computation.17 | convolution fusion | flops 346423296 | bytes 3670016 | tf_op jit(solution)/shard_map/dot_general | solution.py:85
  53.6 1.3 %collective-permute-start.16 = (bf16[128,640]{1,0:T(8,128)(2,1)S(1)}, bf16[128,640]{1,0:T(8,128)(2,1)S(1)}, u32[]{:S(2)}, u32[]{:S(2)}) collective-permute-start(bf16[128,640]{1,0:T(8,128)(2,1)S(1)} %slice.66), channel_id=1, source_target_pairs={{0,2},{1,3},{2,0},{3,1},{4,6},{5,7},{6,4},{7,5},{8,10},{9,11},{10,... | collective-permute-start | bytes 491528 | tf_op jit(solution)/shard_map/ppermute | solution.py:99
  54.8 0.9 %collective-permute-start.20 = (bf16[128,640]{1,0:T(8,128)(2,1)S(1)}, bf16[128,640]{1,0:T(8,128)(2,1)S(1)}, u32[]{:S(2)}, u32[]{:S(2)}) collective-permute-start(bf16[128,640]{1,0:T(8,128)(2,1)S(1)} %slice.50), channel_id=1, source_target_pairs={{0,2},{1,3},{2,0},{3,1},{4,6},{5,7},{6,4},{7,5},{8,10},{9,11},{10,... | collective-permute-start | bytes 491528 | tf_op jit(solution)/shard_map/ppermute | solution.py:93
  55.8 4.7 %collective-permute-done.16 = bf16[128,640]{1,0:T(8,128)(2,1)S(1)} collective-permute-done((bf16[128,640]{1,0:T(8,128)(2,1)S(1)}, bf16[128,640]{1,0:T(8,128)(2,1)S(1)}, u32[]{:S(2)}, u32[]{:S(2)}) %collective-permute-start.16) | collective-permute-done | bytes 163872 | tf_op jit(solution)/shard_map/ppermute | solution.py:99
  60.7 1.2 %collective-permute-done.11 = bf16[128,640]{1,0:T(8,128)(2,1)S(1)} collective-permute-done((bf16[128,640]{1,0:T(8,128)(2,1)S(1)}, bf16[128,640]{1,0:T(8,128)(2,1)S(1)}, u32[]{:S(2)}, u32[]{:S(2)}) %collective-permute-start.11) | collective-permute-done | bytes 163872 | tf_op jit(solution)/shard_map/ppermute | solution.py:104
  61.9 0.4 collective-permute-done.20
  62.3 4.5 %collective-permute-done.22 = bf16[128,640]{1,0:T(8,128)(2,1)S(1)} collective-permute-done((bf16[128,640]{1,0:T(8,128)(2,1)S(1)}, bf16[128,640]{1,0:T(8,128)(2,1)S(1)}, u32[]{:S(2)}, u32[]{:S(2)}) %collective-permute-start.22) | collective-permute-done | bytes 163872 | tf_op jit(solution)/shard_map/ppermute | solution.py:93
  66.7 0.7 collective-permute-done.17
  67.4 0.9 %add_convert_fusion = bf16[128,640]{1,0:T(8,128)(2,1)} fusion(bf16[128,640]{1,0:T(8,128)(2,1)S(1)} %collective-permute-done.22, bf16[128,640]{1,0:T(8,128)(2,1)S(1)} %collective-permute-done.21, bf16[128,640]{1,0:T(8,128)(2,1)S(1)} %collective-permute-done.20, bf16[128,640]{1,0:T(8,128)(2,1)S(1)} %collective-permute-done.17, ...), kind=kLoop, calls=%fused_computation.49 | loop fusion | flops 1474560 | bytes 1311232 | tf_op jit(solution)/shard_map/convert_element_type | solution.py:108
  (51 shorter events, 3.6 us)
Async XLA Ops:
  1.0 13.2 %collective-permute-start = (bf16[128,640]{1,0:T(8,128)(2,1)S(1)}, bf16[128,640]{1,0:T(8,128)(2,1)}, u32[]{:S(2)}, u32[]{:S(2)}) collective-permute-start(bf16[128,640]{1,0:T(8,128)(2,1)S(1)} %multiply_convert_fusion), channel_id=1, source_target_pairs={{0,12},{4,8},{8,4},{12,0},{1,13},{5,9},{9,5},{13,1},{2,14},{6,10},... | collective-permute-start | bytes 491528 | tf_op jit(solution)/shard_map/ppermute | solution.py:66
  6.1 14.0 %collective-permute-start.6 = (bf16[128,640]{1,0:T(8,128)(2,1)S(1)}, bf16[128,640]{1,0:T(8,128)(2,1)}, u32[]{:S(2)}, u32[]{:S(2)}) collective-permute-start(bf16[128,640]{1,0:T(8,128)(2,1)S(1)} %multiply_convert_fusion), channel_id=1, source_target_pairs={{0,8},{4,12},{8,0},{12,4},{1,9},{5,13},{9,1},{13,5},{2,10},{6,14},... | collective-permute-start | bytes 491528 | tf_op jit(solution)/shard_map/ppermute | solution.py:66
  6.1 15.5 %collective-permute-start.12 = (bf16[128,640]{1,0:T(8,128)(2,1)S(1)}, bf16[128,640]{1,0:T(8,128)(2,1)}, u32[]{:S(2)}, u32[]{:S(2)}) collective-permute-start(bf16[128,640]{1,0:T(8,128)(2,1)S(1)} %multiply_convert_fusion), channel_id=1, source_target_pairs={{0,4},{4,0},{8,12},{12,8},{1,5},{5,1},{9,13},{13,9},{2,6},{6,2},{1... | collective-permute-start | bytes 491528 | tf_op jit(solution)/shard_map/ppermute | solution.py:66
  6.8 7.9 %collective-permute-start.18 = (bf16[128,640]{1,0:T(8,128)(2,1)S(1)}, bf16[128,640]{1,0:T(8,128)(2,1)}, u32[]{:S(2)}, u32[]{:S(2)}) collective-permute-start(bf16[128,640]{1,0:T(8,128)(2,1)S(1)} %multiply_convert_fusion), channel_id=1, source_target_pairs={{0,2},{1,3},{2,0},{3,1},{4,6},{5,7},{6,4},{7,5},{8,10},{9,11},{10,... | collective-permute-start | bytes 491528 | tf_op jit(solution)/shard_map/ppermute | solution.py:79
  8.4 2.5 %copy-start = (bf16[1,2560,512]{2,1,0:T(8,128)(2,1)S(1)}, bf16[1,2560,512]{2,1,0:T(8,128)(2,1)}, u32[]{:S(2)}) copy-start(bf16[1,2560,512]{2,1,0:T(8,128)(2,1)} %param.10) | copy-start | bytes 7864324
  12.2 1.7 %copy-start.1 = (bf16[1,512,2560]{2,1,0:T(8,128)(2,1)S(1)}, bf16[1,512,2560]{2,1,0:T(8,128)(2,1)}, u32[]{:S(2)}) copy-start(bf16[1,512,2560]{2,1,0:T(8,128)(2,1)} %param.11) | copy-start | bytes 7864324
  14.2 8.9 %collective-permute-start.1 = (bf16[128,640]{1,0:T(8,128)(2,1)}, bf16[128,640]{1,0:T(8,128)(2,1)S(1)}, u32[]{:S(2)}, u32[]{:S(2)}) collective-permute-start(bf16[128,640]{1,0:T(8,128)(2,1)} %collective-permute-done), channel_id=1, source_target_pairs={{0,2},{1,3},{2,0},{3,1},{4,6},{5,7},{6,4},{7,5},{8,10},{9,11},{10,... | collective-permute-start | bytes 491528 | tf_op jit(solution)/shard_map/ppermute | solution.py:79
  15.6 14.6 %collective-permute-start.19 = (bf16[128,1280]{1,0:T(8,128)(2,1)S(1)}, bf16[128,1280]{1,0:T(8,128)(2,1)S(1)}, u32[]{:S(2)}, u32[]{:S(2)}) collective-permute-start(bf16[128,1280]{1,0:T(8,128)(2,1)S(1)} %pad_maximum_fusion.10), channel_id=1, source_target_pairs={{0,1},{1,0},{2,3},{3,2},{4,5},{5,4},{6,7},{7,6},{8,9},{9,8},{10,11... | collective-permute-start | bytes 983048 | tf_op jit(solution)/shard_map/ppermute | solution.py:81
  20.1 7.2 %collective-permute-start.7 = (bf16[128,640]{1,0:T(8,128)(2,1)}, bf16[128,640]{1,0:T(8,128)(2,1)S(1)}, u32[]{:S(2)}, u32[]{:S(2)}) collective-permute-start(bf16[128,640]{1,0:T(8,128)(2,1)} %collective-permute-done.6), channel_id=1, source_target_pairs={{0,2},{1,3},{2,0},{3,1},{4,6},{5,7},{6,4},{7,5},{8,10},{9,11},{10,... | collective-permute-start | bytes 491528 | tf_op jit(solution)/shard_map/ppermute | solution.py:79
  21.6 7.5 %collective-permute-start.13 = (bf16[128,640]{1,0:T(8,128)(2,1)}, bf16[128,640]{1,0:T(8,128)(2,1)S(1)}, u32[]{:S(2)}, u32[]{:S(2)}) collective-permute-start(bf16[128,640]{1,0:T(8,128)(2,1)} %collective-permute-done.12), channel_id=1, source_target_pairs={{0,2},{1,3},{2,0},{3,1},{4,6},{5,7},{6,4},{7,5},{8,10},{9,11},{10,... | collective-permute-start | bytes 491528 | tf_op jit(solution)/shard_map/ppermute | solution.py:79
  24.1 7.2 %collective-permute-start.2 = (bf16[128,1280]{1,0:T(8,128)(2,1)S(1)}, bf16[128,1280]{1,0:T(8,128)(2,1)S(1)}, u32[]{:S(2)}, u32[]{:S(2)}) collective-permute-start(bf16[128,1280]{1,0:T(8,128)(2,1)S(1)} %pad_maximum_fusion.7), channel_id=1, source_target_pairs={{0,1},{1,0},{2,3},{3,2},{4,5},{5,4},{6,7},{7,6},{8,9},{9,8},{10,11... | collective-permute-start | bytes 983048 | tf_op jit(solution)/shard_map/ppermute | solution.py:81
  28.3 5.2 %collective-permute-start.8 = (bf16[128,1280]{1,0:T(8,128)(2,1)S(1)}, bf16[128,1280]{1,0:T(8,128)(2,1)S(1)}, u32[]{:S(2)}, u32[]{:S(2)}) collective-permute-start(bf16[128,1280]{1,0:T(8,128)(2,1)S(1)} %pad_maximum_fusion.8), channel_id=1, source_target_pairs={{0,1},{1,0},{2,3},{3,2},{4,5},{5,4},{6,7},{7,6},{8,9},{9,8},{10,11... | collective-permute-start | bytes 983048 | tf_op jit(solution)/shard_map/ppermute | solution.py:81
  30.0 7.1 %collective-permute-start.14 = (bf16[128,1280]{1,0:T(8,128)(2,1)S(1)}, bf16[128,1280]{1,0:T(8,128)(2,1)S(1)}, u32[]{:S(2)}, u32[]{:S(2)}) collective-permute-start(bf16[128,1280]{1,0:T(8,128)(2,1)S(1)} %pad_maximum_fusion.9), channel_id=1, source_target_pairs={{0,1},{1,0},{2,3},{3,2},{4,5},{5,4},{6,7},{7,6},{8,9},{9,8},{10,11... | collective-permute-start | bytes 983048 | tf_op jit(solution)/shard_map/ppermute | solution.py:81
  30.1 1.7 %copy-start.2 = (bf16[640,512]{1,0:T(8,128)(2,1)S(1)}, bf16[640,512]{1,0:T(8,128)(2,1)}, u32[]{:S(2)}) copy-start(bf16[640,512]{1,0:T(8,128)(2,1)} %get-tuple-element.16) | copy-start | bytes 1966084
  30.2 1.7 %copy-start.3 = (bf16[640,512]{1,0:T(8,128)(2,1)S(1)}, bf16[640,512]{1,0:T(8,128)(2,1)}, u32[]{:S(2)}) copy-start(bf16[640,512]{1,0:T(8,128)(2,1)} %get-tuple-element.17) | copy-start | bytes 1966084
  30.2 1.7 %copy-start.4 = (bf16[640,512]{1,0:T(8,128)(2,1)S(1)}, bf16[640,512]{1,0:T(8,128)(2,1)}, u32[]{:S(2)}) copy-start(bf16[640,512]{1,0:T(8,128)(2,1)} %get-tuple-element.18) | copy-start | bytes 1966084
  33.0 1.8 %collective-permute-start.3 = (bf16[128,1280]{1,0:T(8,128)(2,1)S(1)}, bf16[128,1280]{1,0:T(8,128)(2,1)S(1)}, u32[]{:S(2)}, u32[]{:S(2)}) collective-permute-start(bf16[128,1280]{1,0:T(8,128)(2,1)S(1)} %convolution_convert_fusion.6), channel_id=1, source_target_pairs={{0,1},{1,0},{2,3},{3,2},{4,5},{5,4},{6,7},{7,6},{8,9},{9,8},{10,11... | collective-permute-start | bytes 983048 | tf_op jit(solution)/shard_map/ppermute | solution.py:97
  36.7 3.0 %collective-permute-start.9 = (bf16[128,1280]{1,0:T(8,128)(2,1)S(1)}, bf16[128,1280]{1,0:T(8,128)(2,1)S(1)}, u32[]{:S(2)}, u32[]{:S(2)}) collective-permute-start(bf16[128,1280]{1,0:T(8,128)(2,1)S(1)} %convolution_convert_fusion.4), channel_id=1, source_target_pairs={{0,1},{1,0},{2,3},{3,2},{4,5},{5,4},{6,7},{7,6},{8,9},{9,8},{10,11... | collective-permute-start | bytes 983048 | tf_op jit(solution)/shard_map/ppermute | solution.py:97
  38.2 7.1 %collective-permute-start.4 = (bf16[128,640]{1,0:T(8,128)(2,1)S(1)}, bf16[128,640]{1,0:T(8,128)(2,1)S(1)}, u32[]{:S(2)}, u32[]{:S(2)}) collective-permute-start(bf16[128,640]{1,0:T(8,128)(2,1)S(1)} %slice.68), channel_id=1, source_target_pairs={{0,2},{1,3},{2,0},{3,1},{4,6},{5,7},{6,4},{7,5},{8,10},{9,11},{10,... | collective-permute-start | bytes 491528 | tf_op jit(solution)/shard_map/ppermute | solution.py:99
  40.1 7.8 %collective-permute-start.10 = (bf16[128,640]{1,0:T(8,128)(2,1)S(1)}, bf16[128,640]{1,0:T(8,128)(2,1)S(1)}, u32[]{:S(2)}, u32[]{:S(2)}) collective-permute-start(bf16[128,640]{1,0:T(8,128)(2,1)S(1)} %slice.67), channel_id=1, source_target_pairs={{0,2},{1,3},{2,0},{3,1},{4,6},{5,7},{6,4},{7,5},{8,10},{9,11},{10,... | collective-permute-start | bytes 491528 | tf_op jit(solution)/shard_map/ppermute | solution.py:99
  42.3 8.9 %collective-permute-start.15 = (bf16[128,1280]{1,0:T(8,128)(2,1)S(1)}, bf16[128,1280]{1,0:T(8,128)(2,1)S(1)}, u32[]{:S(2)}, u32[]{:S(2)}) collective-permute-start(bf16[128,1280]{1,0:T(8,128)(2,1)S(1)} %convolution_convert_fusion.2), channel_id=1, source_target_pairs={{0,1},{1,0},{2,3},{3,2},{4,5},{5,4},{6,7},{7,6},{8,9},{9,8},{10,11... | collective-permute-start | bytes 983048 | tf_op jit(solution)/shard_map/ppermute | solution.py:97
  45.3 15.2 %collective-permute-start.5 = (bf16[128,640]{1,0:T(8,128)(2,1)S(1)}, bf16[128,640]{1,0:T(8,128)(2,1)S(1)}, u32[]{:S(2)}, u32[]{:S(2)}) collective-permute-start(bf16[128,640]{1,0:T(8,128)(2,1)S(1)} %fusion.5), channel_id=1, source_target_pairs={{0,12},{4,8},{8,4},{12,0},{1,13},{5,9},{9,5},{13,1},{2,14},{6,10},... | collective-permute-start | bytes 491528 | tf_op jit(solution)/shard_map/ppermute | solution.py:104
  48.0 13.9 %collective-permute-start.11 = (bf16[128,640]{1,0:T(8,128)(2,1)S(1)}, bf16[128,640]{1,0:T(8,128)(2,1)S(1)}, u32[]{:S(2)}, u32[]{:S(2)}) collective-permute-start(bf16[128,640]{1,0:T(8,128)(2,1)S(1)} %fusion.4), channel_id=1, source_target_pairs={{0,8},{4,12},{8,0},{12,4},{1,9},{5,13},{9,1},{13,5},{2,10},{6,14},... | collective-permute-start | bytes 491528 | tf_op jit(solution)/shard_map/ppermute | solution.py:104
  53.2 7.5 %copy-start.5 = (s32[128,1]{0,1:T(1,128)S(1)}, s32[128,1]{0,1:T(1,128)}, u32[]{:S(2)}) copy-start(s32[128,1]{0,1:T(1,128)} %param.8) | copy-start | bytes 1540
  53.6 7.0 %collective-permute-start.16 = (bf16[128,640]{1,0:T(8,128)(2,1)S(1)}, bf16[128,640]{1,0:T(8,128)(2,1)S(1)}, u32[]{:S(2)}, u32[]{:S(2)}) collective-permute-start(bf16[128,640]{1,0:T(8,128)(2,1)S(1)} %slice.66), channel_id=1, source_target_pairs={{0,2},{1,3},{2,0},{3,1},{4,6},{5,7},{6,4},{7,5},{8,10},{9,11},{10,... | collective-permute-start | bytes 491528 | tf_op jit(solution)/shard_map/ppermute | solution.py:99
  54.8 7.4 %collective-permute-start.20 = (bf16[128,640]{1,0:T(8,128)(2,1)S(1)}, bf16[128,640]{1,0:T(8,128)(2,1)S(1)}, u32[]{:S(2)}, u32[]{:S(2)}) collective-permute-start(bf16[128,640]{1,0:T(8,128)(2,1)S(1)} %slice.50), channel_id=1, source_target_pairs={{0,2},{1,3},{2,0},{3,1},{4,6},{5,7},{6,4},{7,5},{8,10},{9,11},{10,... | collective-permute-start | bytes 491528 | tf_op jit(solution)/shard_map/ppermute | solution.py:93
  55.8 6.5 %collective-permute-start.21 = (bf16[128,640]{1,0:T(8,128)(2,1)S(1)}, bf16[128,640]{1,0:T(8,128)(2,1)S(1)}, u32[]{:S(2)}, u32[]{:S(2)}) collective-permute-start(bf16[128,640]{1,0:T(8,128)(2,1)S(1)} %get-tuple-element.23), channel_id=1, source_target_pairs={{0,1},{1,0},{2,3},{3,2},{4,5},{5,4},{6,7},{7,6},{8,9},{9,8},{10,11... | collective-permute-start | bytes 491528 | tf_op jit(solution)/shard_map/ppermute | solution.py:93
  60.5 6.2 %collective-permute-start.22 = (bf16[128,640]{1,0:T(8,128)(2,1)S(1)}, bf16[128,640]{1,0:T(8,128)(2,1)S(1)}, u32[]{:S(2)}, u32[]{:S(2)}) collective-permute-start(bf16[128,640]{1,0:T(8,128)(2,1)S(1)} %get-tuple-element.24), channel_id=1, source_target_pairs={{0,3},{1,2},{2,1},{3,0},{4,7},{5,6},{6,5},{7,4},{8,11},{9,10},{10,... | collective-permute-start | bytes 491528 | tf_op jit(solution)/shard_map/ppermute | solution.py:93
  60.6 6.8 %collective-permute-start.17 = (bf16[128,640]{1,0:T(8,128)(2,1)S(1)}, bf16[128,640]{1,0:T(8,128)(2,1)S(1)}, u32[]{:S(2)}, u32[]{:S(2)}) collective-permute-start(bf16[128,640]{1,0:T(8,128)(2,1)S(1)} %fusion.3), channel_id=1, source_target_pairs={{0,4},{4,0},{8,12},{12,8},{1,5},{5,1},{9,13},{13,9},{2,6},{6,2},{1... | collective-permute-start | bytes 491528 | tf_op jit(solution)/shard_map/ppermute | solution.py:104

commit v25 on v21

--- a/solution.py
+++ b/solution.py
@@ -86,7 +86,7 @@
         hidden = (jax.nn.silu(gate_act) * up_act).astype(jnp.bfloat16)
         keep = jnp.dot(hidden, down_keep, preferred_element_type=jnp.float32).astype(jnp.bfloat16)
         send = jnp.dot(hidden, down_send, preferred_element_type=jnp.float32).astype(jnp.bfloat16)
-        previous = keep
+        previous = send
         over_c = keep.astype(jnp.float32) + lax.ppermute(
             send, "tensor", _xor_pairs(n_tensor, 1)).astype(jnp.float32)
         summed = over_c[:, :width] + lax.ppermute(

time: 62.9 us -> 67.1 us (1.067)
  starting transfers between devices: 21.3 us -> 23.3 us
  waiting for transfers between devices: 17.7 us -> 19.7 us
    ppermute x3, waiting for transfers between devices: 3.72 us -> 7.24 us  [gathered(): lax.ppermute(part.astype(jnp.bfloat16), 'expert', _xor_pairs(n_expert, k))]
    ppermute x3, starting transfers between devices: 5 us -> 7.51 us  [gathered(): lax.ppermute(part.astype(jnp.bfloat16), 'expert', _xor_pairs(n_expert, k))]
    ppermute x4, waiting for transfers between devices: 5.33 us -> 4.06 us  [gathered(): lax.ppermute(over_c[:, width:].astype(jnp.bfloat16), 'tensor', _xor_pairs...]
  transfers between devices with their start and end apart: 22 -> 22, of which waited for: 9 -> 8; matrix products, arithmetic and copies ran while one was open for 31% -> 29% of each run, Pallas kernels for 0% -> 0%
where the time goes in v25:
time: 67.1 us; the launch traced here: 66.7 us
  starting transfers between devices  23.3 us (35%)
  waiting for transfers between devices  19.7 us (29%)
  other arithmetic  9 us (13%)
  matrix products  7.74 us (12%)
  local copies, waits for them, and re-layouts  6.68 us (10%)
    ppermute x3, starting transfers between devices, gathered(): lax.ppermute(part.astype(jnp.bfloat16), 'expert', _xor_pairs(n_expert, k))  7.51 us
    ppermute x3, waiting for transfers between devices, gathered(): lax.ppermute(part.astype(jnp.bfloat16), 'expert', _xor_pairs(n_expert, k))  7.24 us
    ppermute x3, starting transfers between devices, gathered(): lax.ppermute(scaled, 'expert', _xor_pairs(n_expert, k))  5.76 us
    ppermute x3, waiting for transfers between devices, gathered(): lax.ppermute(scaled, 'expert', _xor_pairs(n_expert, k))  4.4 us
    ppermute x4, starting transfers between devices, gathered(): lax.ppermute(over_c[:, width:].astype(jnp.bfloat16), 'tensor', _xor_pairs...  4.31 us
    ppermute x4, starting transfers between devices, gathered(): lax.ppermute(piece, 'tensor', _xor_pairs(n_tensor, 2))  4.13 us
    ppermute x4, waiting for transfers between devices, gathered(): lax.ppermute(over_c[:, width:].astype(jnp.bfloat16), 'tensor', _xor_pairs...  4.06 us
    ppermute x4, waiting for transfers between devices, gathered(): lax.ppermute(piece, 'tensor', _xor_pairs(n_tensor, 2))  3.94 us
  transfers between devices with their start and end apart: 22, of which 8 were waited for; matrix products, arithmetic and copies ran while one was open for 29% of the time, Pallas kernels for 0%

profile of v25, /device:TPU:0, one launch (start us, length us, event | category | flops | bytes accessed | tf_op | source)
XLA Modules:
  0.0 66.7 jit_solution(4499534438307156001)
XLA Ops:
  0.0 1.0 %multiply_convert_fusion = bf16[128,640]{1,0:T(8,128)(2,1)S(1)} fusion(bf16[128,640]{1,0:T(8,128)(2,1)} %param.6, f32[128]{0:T(128)} %param.7), kind=kLoop, calls=%fused_computation.59 | loop fusion | flops 245760 | bytes 328192 | tf_op jit(solution)/shard_map/convert_element_type | solution.py:64
  1.0 5.1 %collective-permute-start = (bf16[128,640]{1,0:T(8,128)(2,1)S(1)}, bf16[128,640]{1,0:T(8,128)(2,1)}, u32[]{:S(2)}, u32[]{:S(2)}) collective-permute-start(bf16[128,640]{1,0:T(8,128)(2,1)S(1)} %multiply_convert_fusion), channel_id=1, source_target_pairs={{0,12},{4,8},{8,4},{12,0},{1,13},{5,9},{9,5},{13,1},{2,14},{6,10},... | collective-permute-start | bytes 491528 | tf_op jit(solution)/shard_map/ppermute | solution.py:66
  6.1 0.6 collective-permute-start.12
  6.8 1.6 %collective-permute-start.18 = (bf16[128,640]{1,0:T(8,128)(2,1)S(1)}, bf16[128,640]{1,0:T(8,128)(2,1)}, u32[]{:S(2)}, u32[]{:S(2)}) collective-permute-start(bf16[128,640]{1,0:T(8,128)(2,1)S(1)} %multiply_convert_fusion), channel_id=1, source_target_pairs={{0,2},{1,3},{2,0},{3,1},{4,6},{5,7},{6,4},{7,5},{8,10},{9,11},{10,... | collective-permute-start | bytes 491528 | tf_op jit(solution)/shard_map/ppermute | solution.py:79
  8.4 2.0 %dynamic-slice_bitcast_fusion.11 = (bf16[640,512]{1,0:T(8,128)(2,1)S(1)}, bf16[640,512]{1,0:T(8,128)(2,1)S(1)}, bf16[640,512]{1,0:T(8,128)(2,1)S(1)}, bf16[640,512]{1,0:T(8,128)(2,1)S(1)}) fusion(bf16[1,2560,512]{2,1,0:T(8,128)(2,1)} %param.9, s32[]{:T(128)S(6)} %select_n.48, s32[]{:T(128)S(6)} %select_n.49, s32[]{:T(128)S(6)} %select_n.51, s32[]{:T(128)S(6)} %select_n.50), kind=kLoop, calls=%fused_computation.40 | loop fusion | bytes 5242896 | tf_op jit(solution)/shard_map/dynamic_slice | solution.py:55
  10.4 0.5 copy-done
  10.9 1.3 %dynamic-slice_bitcast_fusion.7 = (bf16[640,512]{1,0:T(8,128)(2,1)S(1)}, bf16[640,512]{1,0:T(8,128)(2,1)}, bf16[640,512]{1,0:T(8,128)(2,1)}, bf16[640,512]{1,0:T(8,128)(2,1)}) fusion(bf16[1,2560,512]{2,1,0:T(8,128)(2,1)S(1)} %copy-done, s32[]{:T(128)S(6)} %select_n.48, s32[]{:T(128)S(6)} %select_n.49, s32[]{:T(128)S(6)} %select_n.51, s32[]{:T(128)S(6)} %select_n.50), kind=kLoop, calls=%fused_computation.36 | loop fusion | bytes 5242896 | tf_op jit(solution)/shard_map/dynamic_slice | solution.py:55
  12.5 1.5 %copy-done.1 = bf16[1,512,2560]{2,1,0:T(8,128)(2,1)S(1)} copy-done((bf16[1,512,2560]{2,1,0:T(8,128)(2,1)S(1)}, bf16[1,512,2560]{2,1,0:T(8,128)(2,1)}, u32[]{:S(2)}) %copy-start.1) | copy-done | bytes 2621464
  14.2 0.5 collective-permute-start.1
  14.7 0.9 %pad_maximum_fusion.10 = bf16[128,1280]{1,0:T(8,128)(2,1)S(1)} fusion(bf16[128,640]{1,0:T(8,128)(2,1)} %collective-permute-done.18, bf16[128,640]{1,0:T(8,128)(2,1)S(1)} %multiply_convert_fusion), kind=kLoop, calls=%fused_computation.58 | loop fusion | flops 655360 | bytes 655360 | tf_op jit(solution)/shard_map/concatenate | solution.py:78
  15.7 4.4 %collective-permute-done.6 = bf16[128,640]{1,0:T(8,128)(2,1)} collective-permute-done((bf16[128,640]{1,0:T(8,128)(2,1)S(1)}, bf16[128,640]{1,0:T(8,128)(2,1)}, u32[]{:S(2)}, u32[]{:S(2)}) %collective-permute-start.6) | collective-permute-done | bytes 163872 | tf_op jit(solution)/shard_map/ppermute | solution.py:66
  20.1 1.5 %collective-permute-start.7 = (bf16[128,640]{1,0:T(8,128)(2,1)}, bf16[128,640]{1,0:T(8,128)(2,1)S(1)}, u32[]{:S(2)}, u32[]{:S(2)}) collective-permute-start(bf16[128,640]{1,0:T(8,128)(2,1)} %collective-permute-done.6), channel_id=1, source_target_pairs={{0,2},{1,3},{2,0},{3,1},{4,6},{5,7},{6,4},{7,5},{8,10},{9,11},{10,... | collective-permute-start | bytes 491528 | tf_op jit(solution)/shard_map/ppermute | solution.py:79
  21.6 0.5 collective-permute-start.13
  22.2 0.9 %constant_dynamic-update-slice_fusion.2 = bf16[128,2560]{1,0:T(8,128)(2,1)S(1)} fusion(bf16[128,640]{1,0:T(8,128)(2,1)} %collective-permute-done), kind=kLoop, calls=%fused_computation.63 | loop fusion | bytes 327680
  23.1 0.9 %pad_maximum_fusion.7 = bf16[128,1280]{1,0:T(8,128)(2,1)S(1)} fusion(bf16[128,640]{1,0:T(8,128)(2,1)S(1)} %collective-permute-done.1, bf16[128,640]{1,0:T(8,128)(2,1)} %collective-permute-done), kind=kLoop, calls=%fused_computation.55 | loop fusion | flops 655360 | bytes 655360 | tf_op jit(solution)/shard_map/concatenate | solution.py:78
  24.1 3.2 %collective-permute-done.7 = bf16[128,640]{1,0:T(8,128)(2,1)S(1)} collective-permute-done((bf16[128,640]{1,0:T(8,128)(2,1)}, bf16[128,640]{1,0:T(8,128)(2,1)S(1)}, u32[]{:S(2)}, u32[]{:S(2)}) %collective-permute-start.7) | collective-permute-done | bytes 163872 | tf_op jit(solution)/shard_map/ppermute | solution.py:79
  27.3 0.9 %pad_maximum_fusion.8 = bf16[128,1280]{1,0:T(8,128)(2,1)S(1)} fusion(bf16[128,640]{1,0:T(8,128)(2,1)S(1)} %collective-permute-done.7, bf16[128,640]{1,0:T(8,128)(2,1)} %collective-permute-done.6), kind=kLoop, calls=%fused_computation.56 | loop fusion | flops 655360 | bytes 655360 | tf_op jit(solution)/shard_map/concatenate | solution.py:78
  28.4 0.7 %collective-permute-done.13 = bf16[128,640]{1,0:T(8,128)(2,1)S(1)} collective-permute-done((bf16[128,640]{1,0:T(8,128)(2,1)}, bf16[128,640]{1,0:T(8,128)(2,1)S(1)}, u32[]{:S(2)}, u32[]{:S(2)}) %collective-permute-start.13) | collective-permute-done | bytes 163872 | tf_op jit(solution)/shard_map/ppermute | solution.py:79
  29.1 0.9 %pad_maximum_fusion.9 = bf16[128,1280]{1,0:T(8,128)(2,1)S(1)} fusion(bf16[128,640]{1,0:T(8,128)(2,1)S(1)} %collective-permute-done.13, bf16[128,640]{1,0:T(8,128)(2,1)} %collective-permute-done.12), kind=kLoop, calls=%fused_computation.57 | loop fusion | flops 655360 | bytes 655360 | tf_op jit(solution)/shard_map/concatenate | solution.py:78
  30.2 1.1 %pad_maximum_fusion.6 = bf16[128,2560]{1,0:T(8,128)(2,1)S(1)} fusion(bf16[128,1280]{1,0:T(8,128)(2,1)S(1)} %collective-permute-done.19, bf16[128,640]{1,0:T(8,128)(2,1)} %collective-permute-done.18, bf16[128,640]{1,0:T(8,128)(2,1)S(1)} %multiply_convert_fusion), kind=kLoop, calls=%fused_computation.24 | loop fusion | flops 1966080 | bytes 1310720 | tf_op jit(solution)/shard_map/concatenate | solution.py:80
  31.3 0.5 fusion.14
  31.9 0.7 %multiply_convert_fusion.1 = bf16[128,512]{1,0:T(8,128)(2,1)S(1)} fusion(f32[128,512]{1,0:T(8,128)S(1)} %fusion.14, bf16[128,2560]{1,0:T(8,128)(2,1)S(1)} %constant_dynamic-update-slice_fusion, bf16[640,512]{1,0:T(8,128)(2,1)S(1)} %copy-done.3, bf16[640,512]{1,0:T(8,128)(2,1)S(1)} %copy-done.4, bf16[640,512]{1,0:T(8,128)(2,1)S(1)} %copy-done.2, ...), kind=kOutput, calls=%fused_computation.60 | convolution fusion | flops 346423296 | bytes 3670016 | tf_op jit(solution)/shard_map/dot_general | solution.py:85
  32.6 0.3 convolution_convert_fusion.6
  33.0 0.6 collective-permute-start.3
  33.5 1.0 %pad_maximum_fusion.4 = bf16[128,2560]{1,0:T(8,128)(2,1)S(1)} fusion(bf16[128,1280]{1,0:T(8,128)(2,1)S(1)} %collective-permute-done.8, bf16[128,640]{1,0:T(8,128)(2,1)S(1)} %collective-permute-done.7, bf16[128,640]{1,0:T(8,128)(2,1)} %collective-permute-done.6), kind=kLoop, calls=%fused_computation.22 | loop fusion | flops 1966080 | bytes 1310720 | tf_op jit(solution)/shard_map/concatenate | solution.py:80
  34.5 0.5 fusion.15
  35.0 0.7 %fusion.4 = bf16[128,512]{1,0:T(8,128)(2,1)S(1)} fusion(bf16[128,2560]{1,0:T(8,128)(2,1)S(1)} %pad_maximum_fusion.4, f32[128,512]{1,0:T(8,128)S(1)} %fusion.15, bf16[640,512]{1,0:T(8,128)(2,1)S(1)} %copy-done.3, bf16[640,512]{1,0:T(8,128)(2,1)S(1)} %copy-done.4, bf16[640,512]{1,0:T(8,128)(2,1)S(1)} %copy-done.2, bf16[640,512]{1,0:T(8,128)(2,1)S(1)} %get-tuple-element.15), kind=kOutput, calls=%fused_computation.19 | convolution fusion | flops 346423296 | bytes 3670016 | tf_op jit(solution)/shard_map/dot_general | solution.py:85
  36.2 1.0 %pad_maximum_fusion.5 = bf16[128,2560]{1,0:T(8,128)(2,1)S(1)} fusion(bf16[128,1280]{1,0:T(8,128)(2,1)S(1)} %collective-permute-done.14, bf16[128,640]{1,0:T(8,128)(2,1)S(1)} %collective-permute-done.13, bf16[128,640]{1,0:T(8,128)(2,1)} %collective-permute-done.12), kind=kLoop, calls=%fused_computation.23 | loop fusion | flops 1966080 | bytes 1310720 | tf_op jit(solution)/shard_map/concatenate | solution.py:80
  37.2 0.5 fusion.16
  37.7 0.7 %fusion.5 = bf16[128,512]{1,0:T(8,128)(2,1)S(1)} fusion(bf16[128,2560]{1,0:T(8,128)(2,1)S(1)} %pad_maximum_fusion.5, f32[128,512]{1,0:T(8,128)S(1)} %fusion.16, bf16[640,512]{1,0:T(8,128)(2,1)S(1)} %copy-done.3, bf16[640,512]{1,0:T(8,128)(2,1)S(1)} %copy-done.4, bf16[640,512]{1,0:T(8,128)(2,1)S(1)} %copy-done.2, bf16[640,512]{1,0:T(8,128)(2,1)S(1)} %get-tuple-element.15), kind=kOutput, calls=%fused_computation.20 | convolution fusion | flops 346423296 | bytes 3670016 | tf_op jit(solution)/shard_map/dot_general | solution.py:85
  38.4 0.3 convolution_convert_fusion.2
  38.8 0.5 collective-permute-start.15
  39.3 0.5 fusion.17
  39.8 0.7 %fusion.6 = bf16[128,512]{1,0:T(8,128)(2,1)S(1)} fusion(bf16[128,2560]{1,0:T(8,128)(2,1)S(1)} %pad_maximum_fusion.6, f32[128,512]{1,0:T(8,128)S(1)} %fusion.17, bf16[640,512]{1,0:T(8,128)(2,1)S(1)} %copy-done.3, bf16[640,512]{1,0:T(8,128)(2,1)S(1)} %copy-done.4, bf16[640,512]{1,0:T(8,128)(2,1)S(1)} %copy-done.2, bf16[640,512]{1,0:T(8,128)(2,1)S(1)} %get-tuple-element.15), kind=kOutput, calls=%fused_computation.21 | convolution fusion | flops 346423296 | bytes 3670016 | tf_op jit(solution)/shard_map/dot_general | solution.py:85
  40.6 0.3 convolution_convert_fusion
  41.4 1.6 %collective-permute-start.4 = (bf16[128,640]{1,0:T(8,128)(2,1)S(1)}, bf16[128,640]{1,0:T(8,128)(2,1)S(1)}, u32[]{:S(2)}, u32[]{:S(2)}) collective-permute-start(bf16[128,640]{1,0:T(8,128)(2,1)S(1)} %slice.67), channel_id=1, source_target_pairs={{0,2},{1,3},{2,0},{3,1},{4,6},{5,7},{6,4},{7,5},{8,10},{9,11},{10,... | collective-permute-start | bytes 491528 | tf_op jit(solution)/shard_map/ppermute | solution.py:92
  43.4 0.6 collective-permute-start.10
  44.4 1.6 %collective-permute-start.16 = (bf16[128,640]{1,0:T(8,128)(2,1)S(1)}, bf16[128,640]{1,0:T(8,128)(2,1)S(1)}, u32[]{:S(2)}, u32[]{:S(2)}) collective-permute-start(bf16[128,640]{1,0:T(8,128)(2,1)S(1)} %slice.65), channel_id=1, source_target_pairs={{0,2},{1,3},{2,0},{3,1},{4,6},{5,7},{6,4},{7,5},{8,10},{9,11},{10,... | collective-permute-start | bytes 491528 | tf_op jit(solution)/shard_map/ppermute | solution.py:92
  45.9 0.3 convert_add_fusion
  46.3 0.6 collective-permute-start.21
  46.9 1.6 %collective-permute-done.4 = bf16[128,640]{1,0:T(8,128)(2,1)S(1)} collective-permute-done((bf16[128,640]{1,0:T(8,128)(2,1)S(1)}, bf16[128,640]{1,0:T(8,128)(2,1)S(1)}, u32[]{:S(2)}, u32[]{:S(2)}) %collective-permute-start.4) | collective-permute-done | bytes 163872 | tf_op jit(solution)/shard_map/ppermute | solution.py:92
  48.5 2.4 %collective-permute-start.5 = (bf16[128,640]{1,0:T(8,128)(2,1)S(1)}, bf16[128,640]{1,0:T(8,128)(2,1)S(1)}, u32[]{:S(2)}, u32[]{:S(2)}) collective-permute-start(bf16[128,640]{1,0:T(8,128)(2,1)S(1)} %fusion.12), channel_id=1, source_target_pairs={{0,12},{4,8},{8,4},{12,0},{1,13},{5,9},{9,5},{13,1},{2,14},{6,10},... | collective-permute-start | bytes 491528 | tf_op jit(solution)/shard_map/ppermute | solution.py:97
  50.9 1.1 %collective-permute-done.10 = bf16[128,640]{1,0:T(8,128)(2,1)S(1)} collective-permute-done((bf16[128,640]{1,0:T(8,128)(2,1)S(1)}, bf16[128,640]{1,0:T(8,128)(2,1)S(1)}, u32[]{:S(2)}, u32[]{:S(2)}) %collective-permute-start.10) | collective-permute-done | bytes 163872 | tf_op jit(solution)/shard_map/ppermute | solution.py:92
  52.0 3.2 %collective-permute-start.11 = (bf16[128,640]{1,0:T(8,128)(2,1)S(1)}, bf16[128,640]{1,0:T(8,128)(2,1)S(1)}, u32[]{:S(2)}, u32[]{:S(2)}) collective-permute-start(bf16[128,640]{1,0:T(8,128)(2,1)S(1)} %fusion.11), channel_id=1, source_target_pairs={{0,8},{4,12},{8,0},{12,4},{1,9},{5,13},{9,1},{13,5},{2,10},{6,14},... | collective-permute-start | bytes 491528 | tf_op jit(solution)/shard_map/ppermute | solution.py:97
  55.5 2.0 %collective-permute-start.17 = (bf16[128,640]{1,0:T(8,128)(2,1)S(1)}, bf16[128,640]{1,0:T(8,128)(2,1)S(1)}, u32[]{:S(2)}, u32[]{:S(2)}) collective-permute-start(bf16[128,640]{1,0:T(8,128)(2,1)S(1)} %fusion.10), channel_id=1, source_target_pairs={{0,4},{4,0},{8,12},{12,8},{1,5},{5,1},{9,13},{13,9},{2,6},{6,2},{1... | collective-permute-start | bytes 491528 | tf_op jit(solution)/shard_map/ppermute | solution.py:97
  57.5 1.1 %collective-permute-done.21 = bf16[128,640]{1,0:T(8,128)(2,1)S(1)} collective-permute-done((bf16[128,640]{1,0:T(8,128)(2,1)S(1)}, bf16[128,640]{1,0:T(8,128)(2,1)S(1)}, u32[]{:S(2)}, u32[]{:S(2)}) %collective-permute-start.21) | collective-permute-done | bytes 163872 | tf_op jit(solution)/shard_map/ppermute | solution.py:92
  58.6 7.2 %collective-permute-done.11 = bf16[128,640]{1,0:T(8,128)(2,1)S(1)} collective-permute-done((bf16[128,640]{1,0:T(8,128)(2,1)S(1)}, bf16[128,640]{1,0:T(8,128)(2,1)S(1)}, u32[]{:S(2)}, u32[]{:S(2)}) %collective-permute-start.11) | collective-permute-done | bytes 163872 | tf_op jit(solution)/shard_map/ppermute | solution.py:97
  65.8 0.9 %fusion.9 = bf16[128,640]{1,0:T(8,128)(2,1)} fusion(f32[128,1280]{1,0:T(8,128)S(1)} %convert_add_fusion, bf16[128,640]{1,0:T(8,128)(2,1)S(1)} %collective-permute-done.21, bf16[128,640]{1,0:T(8,128)(2,1)S(1)} %collective-permute-done.17, bf16[128,640]{1,0:T(8,128)(2,1)S(1)} %collective-permute-done.11, bf16[128,640]{1,0:T(8,128)(2,1)S(1)} %collective-permute-done.5, ...), kind=kLoop, calls=%fused_computation.45 | loop fusion | flops 1064960 | bytes 1147392 | tf_op jit(solution)/shard_map/convert_element_type | solution.py:101
  (48 shorter events, 2.9 us)
Async XLA Ops:
  1.0 13.2 %collective-permute-start = (bf16[128,640]{1,0:T(8,128)(2,1)S(1)}, bf16[128,640]{1,0:T(8,128)(2,1)}, u32[]{:S(2)}, u32[]{:S(2)}) collective-permute-start(bf16[128,640]{1,0:T(8,128)(2,1)S(1)} %multiply_convert_fusion), channel_id=1, source_target_pairs={{0,12},{4,8},{8,4},{12,0},{1,13},{5,9},{9,5},{13,1},{2,14},{6,10},... | collective-permute-start | bytes 491528 | tf_op jit(solution)/shard_map/ppermute | solution.py:66
  6.1 14.0 %collective-permute-start.6 = (bf16[128,640]{1,0:T(8,128)(2,1)S(1)}, bf16[128,640]{1,0:T(8,128)(2,1)}, u32[]{:S(2)}, u32[]{:S(2)}) collective-permute-start(bf16[128,640]{1,0:T(8,128)(2,1)S(1)} %multiply_convert_fusion), channel_id=1, source_target_pairs={{0,8},{4,12},{8,0},{12,4},{1,9},{5,13},{9,1},{13,5},{2,10},{6,14},... | collective-permute-start | bytes 491528 | tf_op jit(solution)/shard_map/ppermute | solution.py:66
  6.1 15.5 %collective-permute-start.12 = (bf16[128,640]{1,0:T(8,128)(2,1)S(1)}, bf16[128,640]{1,0:T(8,128)(2,1)}, u32[]{:S(2)}, u32[]{:S(2)}) collective-permute-start(bf16[128,640]{1,0:T(8,128)(2,1)S(1)} %multiply_convert_fusion), channel_id=1, source_target_pairs={{0,4},{4,0},{8,12},{12,8},{1,5},{5,1},{9,13},{13,9},{2,6},{6,2},{1... | collective-permute-start | bytes 491528 | tf_op jit(solution)/shard_map/ppermute | solution.py:66
  6.8 7.9 %collective-permute-start.18 = (bf16[128,640]{1,0:T(8,128)(2,1)S(1)}, bf16[128,640]{1,0:T(8,128)(2,1)}, u32[]{:S(2)}, u32[]{:S(2)}) collective-permute-start(bf16[128,640]{1,0:T(8,128)(2,1)S(1)} %multiply_convert_fusion), channel_id=1, source_target_pairs={{0,2},{1,3},{2,0},{3,1},{4,6},{5,7},{6,4},{7,5},{8,10},{9,11},{10,... | collective-permute-start | bytes 491528 | tf_op jit(solution)/shard_map/ppermute | solution.py:79
  8.4 2.5 %copy-start = (bf16[1,2560,512]{2,1,0:T(8,128)(2,1)S(1)}, bf16[1,2560,512]{2,1,0:T(8,128)(2,1)}, u32[]{:S(2)}) copy-start(bf16[1,2560,512]{2,1,0:T(8,128)(2,1)} %param.10) | copy-start | bytes 7864324
  12.3 1.7 %copy-start.1 = (bf16[1,512,2560]{2,1,0:T(8,128)(2,1)S(1)}, bf16[1,512,2560]{2,1,0:T(8,128)(2,1)}, u32[]{:S(2)}) copy-start(bf16[1,512,2560]{2,1,0:T(8,128)(2,1)} %param.11) | copy-start | bytes 7864324
  14.2 8.9 %collective-permute-start.1 = (bf16[128,640]{1,0:T(8,128)(2,1)}, bf16[128,640]{1,0:T(8,128)(2,1)S(1)}, u32[]{:S(2)}, u32[]{:S(2)}) collective-permute-start(bf16[128,640]{1,0:T(8,128)(2,1)} %collective-permute-done), channel_id=1, source_target_pairs={{0,2},{1,3},{2,0},{3,1},{4,6},{5,7},{6,4},{7,5},{8,10},{9,11},{10,... | collective-permute-start | bytes 491528 | tf_op jit(solution)/shard_map/ppermute | solution.py:79
  15.6 14.5 %collective-permute-start.19 = (bf16[128,1280]{1,0:T(8,128)(2,1)S(1)}, bf16[128,1280]{1,0:T(8,128)(2,1)S(1)}, u32[]{:S(2)}, u32[]{:S(2)}) collective-permute-start(bf16[128,1280]{1,0:T(8,128)(2,1)S(1)} %pad_maximum_fusion.10), channel_id=1, source_target_pairs={{0,1},{1,0},{2,3},{3,2},{4,5},{5,4},{6,7},{7,6},{8,9},{9,8},{10,11... | collective-permute-start | bytes 983048 | tf_op jit(solution)/shard_map/ppermute | solution.py:81
  20.1 7.2 %collective-permute-start.7 = (bf16[128,640]{1,0:T(8,128)(2,1)}, bf16[128,640]{1,0:T(8,128)(2,1)S(1)}, u32[]{:S(2)}, u32[]{:S(2)}) collective-permute-start(bf16[128,640]{1,0:T(8,128)(2,1)} %collective-permute-done.6), channel_id=1, source_target_pairs={{0,2},{1,3},{2,0},{3,1},{4,6},{5,7},{6,4},{7,5},{8,10},{9,11},{10,... | collective-permute-start | bytes 491528 | tf_op jit(solution)/shard_map/ppermute | solution.py:79
  21.6 7.5 %collective-permute-start.13 = (bf16[128,640]{1,0:T(8,128)(2,1)}, bf16[128,640]{1,0:T(8,128)(2,1)S(1)}, u32[]{:S(2)}, u32[]{:S(2)}) collective-permute-start(bf16[128,640]{1,0:T(8,128)(2,1)} %collective-permute-done.12), channel_id=1, source_target_pairs={{0,2},{1,3},{2,0},{3,1},{4,6},{5,7},{6,4},{7,5},{8,10},{9,11},{10,... | collective-permute-start | bytes 491528 | tf_op jit(solution)/shard_map/ppermute | solution.py:79
  24.1 7.2 %collective-permute-start.2 = (bf16[128,1280]{1,0:T(8,128)(2,1)S(1)}, bf16[128,1280]{1,0:T(8,128)(2,1)S(1)}, u32[]{:S(2)}, u32[]{:S(2)}) collective-permute-start(bf16[128,1280]{1,0:T(8,128)(2,1)S(1)} %pad_maximum_fusion.7), channel_id=1, source_target_pairs={{0,1},{1,0},{2,3},{3,2},{4,5},{5,4},{6,7},{7,6},{8,9},{9,8},{10,11... | collective-permute-start | bytes 983048 | tf_op jit(solution)/shard_map/ppermute | solution.py:81
  28.3 5.2 %collective-permute-start.8 = (bf16[128,1280]{1,0:T(8,128)(2,1)S(1)}, bf16[128,1280]{1,0:T(8,128)(2,1)S(1)}, u32[]{:S(2)}, u32[]{:S(2)}) collective-permute-start(bf16[128,1280]{1,0:T(8,128)(2,1)S(1)} %pad_maximum_fusion.8), channel_id=1, source_target_pairs={{0,1},{1,0},{2,3},{3,2},{4,5},{5,4},{6,7},{7,6},{8,9},{9,8},{10,11... | collective-permute-start | bytes 983048 | tf_op jit(solution)/shard_map/ppermute | solution.py:81
  30.0 6.2 %collective-permute-start.14 = (bf16[128,1280]{1,0:T(8,128)(2,1)S(1)}, bf16[128,1280]{1,0:T(8,128)(2,1)S(1)}, u32[]{:S(2)}, u32[]{:S(2)}) collective-permute-start(bf16[128,1280]{1,0:T(8,128)(2,1)S(1)} %pad_maximum_fusion.9), channel_id=1, source_target_pairs={{0,1},{1,0},{2,3},{3,2},{4,5},{5,4},{6,7},{7,6},{8,9},{9,8},{10,11... | collective-permute-start | bytes 983048 | tf_op jit(solution)/shard_map/ppermute | solution.py:81
  30.1 1.7 %copy-start.2 = (bf16[640,512]{1,0:T(8,128)(2,1)S(1)}, bf16[640,512]{1,0:T(8,128)(2,1)}, u32[]{:S(2)}) copy-start(bf16[640,512]{1,0:T(8,128)(2,1)} %get-tuple-element.16) | copy-start | bytes 1966084
  30.2 1.7 %copy-start.3 = (bf16[640,512]{1,0:T(8,128)(2,1)S(1)}, bf16[640,512]{1,0:T(8,128)(2,1)}, u32[]{:S(2)}) copy-start(bf16[640,512]{1,0:T(8,128)(2,1)} %get-tuple-element.17) | copy-start | bytes 1966084
  30.2 1.7 %copy-start.4 = (bf16[640,512]{1,0:T(8,128)(2,1)S(1)}, bf16[640,512]{1,0:T(8,128)(2,1)}, u32[]{:S(2)}) copy-start(bf16[640,512]{1,0:T(8,128)(2,1)} %get-tuple-element.18) | copy-start | bytes 1966084
  33.0 8.1 %collective-permute-start.3 = (bf16[128,1280]{1,0:T(8,128)(2,1)S(1)}, bf16[128,1280]{1,0:T(8,128)(2,1)S(1)}, u32[]{:S(2)}, u32[]{:S(2)}) collective-permute-start(bf16[128,1280]{1,0:T(8,128)(2,1)S(1)} %convolution_convert_fusion.6), channel_id=1, source_target_pairs={{0,1},{1,0},{2,3},{3,2},{4,5},{5,4},{6,7},{7,6},{8,9},{9,8},{10,11... | collective-permute-start | bytes 983048 | tf_op jit(solution)/shard_map/ppermute | solution.py:90
  36.1 6.9 %collective-permute-start.9 = (bf16[128,1280]{1,0:T(8,128)(2,1)S(1)}, bf16[128,1280]{1,0:T(8,128)(2,1)S(1)}, u32[]{:S(2)}, u32[]{:S(2)}) collective-permute-start(bf16[128,1280]{1,0:T(8,128)(2,1)S(1)} %convolution_convert_fusion.4), channel_id=1, source_target_pairs={{0,1},{1,0},{2,3},{3,2},{4,5},{5,4},{6,7},{7,6},{8,9},{9,8},{10,11... | collective-permute-start | bytes 983048 | tf_op jit(solution)/shard_map/ppermute | solution.py:90
  38.8 5.2 %collective-permute-start.15 = (bf16[128,1280]{1,0:T(8,128)(2,1)S(1)}, bf16[128,1280]{1,0:T(8,128)(2,1)S(1)}, u32[]{:S(2)}, u32[]{:S(2)}) collective-permute-start(bf16[128,1280]{1,0:T(8,128)(2,1)S(1)} %convolution_convert_fusion.2), channel_id=1, source_target_pairs={{0,1},{1,0},{2,3},{3,2},{4,5},{5,4},{6,7},{7,6},{8,9},{9,8},{10,11... | collective-permute-start | bytes 983048 | tf_op jit(solution)/shard_map/ppermute | solution.py:90
  40.9 5.0 %collective-permute-start.20 = (bf16[128,1280]{1,0:T(8,128)(2,1)S(1)}, bf16[128,1280]{1,0:T(8,128)(2,1)S(1)}, u32[]{:S(2)}, u32[]{:S(2)}) collective-permute-start(bf16[128,1280]{1,0:T(8,128)(2,1)S(1)} %convolution_convert_fusion), channel_id=1, source_target_pairs={{0,1},{1,0},{2,3},{3,2},{4,5},{5,4},{6,7},{7,6},{8,9},{9,8},{10,11... | collective-permute-start | bytes 983048 | tf_op jit(solution)/shard_map/ppermute | solution.py:90
  41.4 7.1 %collective-permute-start.4 = (bf16[128,640]{1,0:T(8,128)(2,1)S(1)}, bf16[128,640]{1,0:T(8,128)(2,1)S(1)}, u32[]{:S(2)}, u32[]{:S(2)}) collective-permute-start(bf16[128,640]{1,0:T(8,128)(2,1)S(1)} %slice.67), channel_id=1, source_target_pairs={{0,2},{1,3},{2,0},{3,1},{4,6},{5,7},{6,4},{7,5},{8,10},{9,11},{10,... | collective-permute-start | bytes 491528 | tf_op jit(solution)/shard_map/ppermute | solution.py:92
  43.4 8.6 %collective-permute-start.10 = (bf16[128,640]{1,0:T(8,128)(2,1)S(1)}, bf16[128,640]{1,0:T(8,128)(2,1)S(1)}, u32[]{:S(2)}, u32[]{:S(2)}) collective-permute-start(bf16[128,640]{1,0:T(8,128)(2,1)S(1)} %slice.66), channel_id=1, source_target_pairs={{0,2},{1,3},{2,0},{3,1},{4,6},{5,7},{6,4},{7,5},{8,10},{9,11},{10,... | collective-permute-start | bytes 491528 | tf_op jit(solution)/shard_map/ppermute | solution.py:92
  44.3 13.2 %copy-start.5 = (s32[128,1]{0,1:T(1,128)S(1)}, s32[128,1]{0,1:T(1,128)}, u32[]{:S(2)}) copy-start(s32[128,1]{0,1:T(1,128)} %param.8) | copy-start | bytes 1540
  44.4 11.1 %collective-permute-start.16 = (bf16[128,640]{1,0:T(8,128)(2,1)S(1)}, bf16[128,640]{1,0:T(8,128)(2,1)S(1)}, u32[]{:S(2)}, u32[]{:S(2)}) collective-permute-start(bf16[128,640]{1,0:T(8,128)(2,1)S(1)} %slice.65), channel_id=1, source_target_pairs={{0,2},{1,3},{2,0},{3,1},{4,6},{5,7},{6,4},{7,5},{8,10},{9,11},{10,... | collective-permute-start | bytes 491528 | tf_op jit(solution)/shard_map/ppermute | solution.py:92
  46.3 12.3 %collective-permute-start.21 = (bf16[128,640]{1,0:T(8,128)(2,1)S(1)}, bf16[128,640]{1,0:T(8,128)(2,1)S(1)}, u32[]{:S(2)}, u32[]{:S(2)}) collective-permute-start(bf16[128,640]{1,0:T(8,128)(2,1)S(1)} %slice.64), channel_id=1, source_target_pairs={{0,2},{1,3},{2,0},{3,1},{4,6},{5,7},{6,4},{7,5},{8,10},{9,11},{10,... | collective-permute-start | bytes 491528 | tf_op jit(solution)/shard_map/ppermute | solution.py:92
  48.5 10.1 %collective-permute-start.5 = (bf16[128,640]{1,0:T(8,128)(2,1)S(1)}, bf16[128,640]{1,0:T(8,128)(2,1)S(1)}, u32[]{:S(2)}, u32[]{:S(2)}) collective-permute-start(bf16[128,640]{1,0:T(8,128)(2,1)S(1)} %fusion.12), channel_id=1, source_target_pairs={{0,12},{4,8},{8,4},{12,0},{1,13},{5,9},{9,5},{13,1},{2,14},{6,10},... | collective-permute-start | bytes 491528 | tf_op jit(solution)/shard_map/ppermute | solution.py:97
  52.0 13.8 %collective-permute-start.11 = (bf16[128,640]{1,0:T(8,128)(2,1)S(1)}, bf16[128,640]{1,0:T(8,128)(2,1)S(1)}, u32[]{:S(2)}, u32[]{:S(2)}) collective-permute-start(bf16[128,640]{1,0:T(8,128)(2,1)S(1)} %fusion.11), channel_id=1, source_target_pairs={{0,8},{4,12},{8,0},{12,4},{1,9},{5,13},{9,1},{13,5},{2,10},{6,14},... | collective-permute-start | bytes 491528 | tf_op jit(solution)/shard_map/ppermute | solution.py:97
  55.5 10.3 %collective-permute-start.17 = (bf16[128,640]{1,0:T(8,128)(2,1)S(1)}, bf16[128,640]{1,0:T(8,128)(2,1)S(1)}, u32[]{:S(2)}, u32[]{:S(2)}) collective-permute-start(bf16[128,640]{1,0:T(8,128)(2,1)S(1)} %fusion.10), channel_id=1, source_target_pairs={{0,4},{4,0},{8,12},{12,8},{1,5},{5,1},{9,13},{13,9},{2,6},{6,2},{1... | collective-permute-start | bytes 491528 | tf_op jit(solution)/shard_map/ppermute | solution.py:97

commit v26 on v21

--- a/solution.py
+++ b/solution.py
@@ -73,10 +73,15 @@
     waves = [[k] for k in list(range(n_expert - 1, 1, -1)) + [1][:n_expert - 1] + [0]]
     total = None
     previous = None
+    own_other = lax.ppermute(tokens, "tensor", _xor_pairs(n_tensor, 2))
+    own_other = (own_other.astype(jnp.float32) * route_scale[:, None]).astype(jnp.bfloat16)
     for wave in waves:
         piece = jnp.concatenate([blocks[k] for k in wave])
-        pair = jnp.concatenate(
-            [piece, lax.ppermute(piece, "tensor", _xor_pairs(n_tensor, 2))], axis=1)
+        if wave == [0]:
+            other = own_other
+        else:
+            other = lax.ppermute(piece, "tensor", _xor_pairs(n_tensor, 2))
+        pair = jnp.concatenate([piece, other], axis=1)
         rows = jnp.concatenate(
             [pair, lax.ppermute(pair, "tensor", _xor_pairs(n_tensor, 1))], axis=1)
         if previous is not None:

time: 62.9 us -> 65.5 us (1.041)
  waiting for transfers between devices: 17.7 us -> 28.2 us
  other arithmetic: 8.86 us -> 1.6 us
  local copies, waits for them, and re-layouts: 6.68 us -> 4.01 us
  starting transfers between devices: 21.3 us -> 23.4 us
    ppermute x3, waiting for transfers between devices: 4.4 us -> 10.3 us  [gathered(): lax.ppermute(scaled, 'expert', _xor_pairs(n_expert, k))]
    concatenate x4, other arithmetic: 3.77 us -> 0.1 us  [gathered(): pair = jnp.concatenate([piece, other], axis=1)]
    ppermute x4, waiting for transfers between devices: 3.91 us -> 7.07 us  [the longest x3 6.44 us: gathered(): other = lax.ppermute(piece, 'tensor', _xor_pairs(n_tensor, 2))]
    concatenate x3, other arithmetic: 2.89 us -> 0.14 us  [gathered(): jnp.concatenate([pair, lax.ppermute(pair, 'tensor', _xor_pairs(n_tensor,...]
    ppermute x4, starting transfers between devices: 4.13 us -> 6.57 us  [the longest x3 3.63 us: gathered(): other = lax.ppermute(piece, 'tensor', _xor_pairs(n_tensor, 2))]
    unnamed x14 -> x12, local copies, waits for them, and re-layouts: 3.03 us -> 1.66 us
    dynamic_slice x3, local copies, waits for them, and re-layouts: 3.54 us -> 2.24 us  [_slots(): lax.dynamic_slice_in_dim(weight, (t ^ k) * width, width, axis=axis)]
    ppermute x4, waiting for transfers between devices: 5.33 us -> 6.56 us  [gathered(): lax.ppermute(over_c[:, width:].astype(jnp.bfloat16), 'tensor', _xor_pairs...]
  transfers between devices with their start and end apart: 22 -> 22, of which waited for: 9 -> 12; matrix products, arithmetic and copies ran while one was open for 31% -> 16% of each run, Pallas kernels for 0% -> 0%
where the time goes in v26:
time: 65.5 us; the launch traced here: 65.3 us
  waiting for transfers between devices  28.2 us (43%)
  starting transfers between devices  23.4 us (36%)
  matrix products  7.75 us (12%)
  local copies, waits for them, and re-layouts  4.01 us (6%)
  other arithmetic  1.6 us (2%)
    ppermute x3, waiting for transfers between devices, gathered(): lax.ppermute(scaled, 'expert', _xor_pairs(n_expert, k))  10.3 us
    ppermute x4, waiting for transfers between devices, gathered(): lax.ppermute(over_c[:, width:].astype(jnp.bfloat16), 'tensor', _xor_pairs...  6.56 us
    ppermute x3, waiting for transfers between devices, gathered(): other = lax.ppermute(piece, 'tensor', _xor_pairs(n_tensor, 2))  6.44 us
    ppermute x3, starting transfers between devices, gathered(): lax.ppermute(part.astype(jnp.bfloat16), 'expert', _xor_pairs(n_expert, k))  5.39 us
    ppermute x3, starting transfers between devices, gathered(): lax.ppermute(scaled, 'expert', _xor_pairs(n_expert, k))  5.02 us
    ppermute x4, starting transfers between devices, gathered(): lax.ppermute(over_c[:, width:].astype(jnp.bfloat16), 'tensor', _xor_pairs...  4.63 us
    ppermute x3, starting transfers between devices, gathered(): other = lax.ppermute(piece, 'tensor', _xor_pairs(n_tensor, 2))  3.63 us
    ppermute x3, waiting for transfers between devices, gathered(): lax.ppermute(part.astype(jnp.bfloat16), 'expert', _xor_pairs(n_expert, k))  3.04 us
  transfers between devices with their start and end apart: 22, of which 12 were waited for; matrix products, arithmetic and copies ran while one was open for 16% of the time, Pallas kernels for 0%

profile of v26, /device:TPU:0, one launch (start us, length us, event | category | flops | bytes accessed | tf_op | source)
XLA Modules:
  0.0 65.3 jit_solution(16478931197931412350)
XLA Ops:
  0.0 2.9 %collective-permute-start.18 = (bf16[128,640]{1,0:T(8,128)(2,1)}, bf16[128,640]{1,0:T(8,128)(2,1)S(1)}, u32[]{:S(2)}, u32[]{:S(2)}) collective-permute-start(bf16[128,640]{1,0:T(8,128)(2,1)} %param.6), channel_id=1, source_target_pairs={{0,2},{1,3},{2,0},{3,1},{4,6},{5,7},{6,4},{7,5},{8,10},{9,11},{10,... | collective-permute-start | bytes 491528 | tf_op jit(solution)/shard_map/ppermute | solution.py:76
  2.9 1.8 %dynamic-slice_bitcast_fusion.11 = (bf16[640,512]{1,0:T(8,128)(2,1)S(1)}, bf16[640,512]{1,0:T(8,128)(2,1)S(1)}, bf16[640,512]{1,0:T(8,128)(2,1)S(1)}, bf16[640,512]{1,0:T(8,128)(2,1)S(1)}) fusion(bf16[1,2560,512]{2,1,0:T(8,128)(2,1)} %param.9, s32[]{:T(128)S(6)} %select_n.48, s32[]{:T(128)S(6)} %select_n.49, s32[]{:T(128)S(6)} %select_n.51, s32[]{:T(128)S(6)} %select_n.50), kind=kLoop, calls=%fused_computation.37 | loop fusion | bytes 5242896 | tf_op jit(solution)/shard_map/dynamic_slice | solution.py:55
  4.8 0.2 pad_maximum_fusion
  5.0 1.5 %copy-done = bf16[1,2560,512]{2,1,0:T(8,128)(2,1)S(1)} copy-done((bf16[1,2560,512]{2,1,0:T(8,128)(2,1)S(1)}, bf16[1,2560,512]{2,1,0:T(8,128)(2,1)}, u32[]{:S(2)}) %copy-start) | copy-done | bytes 2621464
  6.7 0.6 collective-permute-done.18
  7.6 3.8 %collective-permute-start = (bf16[128,640]{1,0:T(8,128)(2,1)S(1)}, bf16[128,640]{1,0:T(8,128)(2,1)S(1)}, u32[]{:S(2)}, u32[]{:S(2)}) collective-permute-start(bf16[128,640]{1,0:T(8,128)(2,1)S(1)} %get-tuple-element.27), channel_id=1, source_target_pairs={{0,12},{4,8},{8,4},{12,0},{1,13},{5,9},{9,5},{13,1},{2,14},{6,10},... | collective-permute-start | bytes 491528 | tf_op jit(solution)/shard_map/ppermute | solution.py:66
  11.4 0.2 dynamic-slice_bitcast_fusion.1
  11.7 1.1 %collective-permute-start.12 = (bf16[128,640]{1,0:T(8,128)(2,1)S(1)}, bf16[128,640]{1,0:T(8,128)(2,1)S(1)}, u32[]{:S(2)}, u32[]{:S(2)}) collective-permute-start(bf16[128,640]{1,0:T(8,128)(2,1)S(1)} %get-tuple-element.27), channel_id=1, source_target_pairs={{0,4},{4,0},{8,12},{12,8},{1,5},{5,1},{9,13},{13,9},{2,6},{6,2},{1... | collective-permute-start | bytes 491528 | tf_op jit(solution)/shard_map/ppermute | solution.py:66
  12.8 3.8 %collective-permute-done = bf16[128,640]{1,0:T(8,128)(2,1)S(1)} collective-permute-done((bf16[128,640]{1,0:T(8,128)(2,1)S(1)}, bf16[128,640]{1,0:T(8,128)(2,1)S(1)}, u32[]{:S(2)}, u32[]{:S(2)}) %collective-permute-start) | collective-permute-done | bytes 163872 | tf_op jit(solution)/shard_map/ppermute | solution.py:66
  16.6 1.6 %collective-permute-start.1 = (bf16[128,640]{1,0:T(8,128)(2,1)S(1)}, bf16[128,640]{1,0:T(8,128)(2,1)S(1)}, u32[]{:S(2)}, u32[]{:S(2)}) collective-permute-start(bf16[128,640]{1,0:T(8,128)(2,1)S(1)} %collective-permute-done), channel_id=1, source_target_pairs={{0,2},{1,3},{2,0},{3,1},{4,6},{5,7},{6,4},{7,5},{8,10},{9,11},{10,... | collective-permute-start | bytes 491528 | tf_op jit(solution)/shard_map/ppermute | solution.py:83
  18.3 6.5 %collective-permute-done.6 = bf16[128,640]{1,0:T(8,128)(2,1)S(1)} collective-permute-done((bf16[128,640]{1,0:T(8,128)(2,1)S(1)}, bf16[128,640]{1,0:T(8,128)(2,1)S(1)}, u32[]{:S(2)}, u32[]{:S(2)}) %collective-permute-start.6) | collective-permute-done | bytes 163872 | tf_op jit(solution)/shard_map/ppermute | solution.py:66
  24.9 1.1 %collective-permute-start.7 = (bf16[128,640]{1,0:T(8,128)(2,1)S(1)}, bf16[128,640]{1,0:T(8,128)(2,1)S(1)}, u32[]{:S(2)}, u32[]{:S(2)}) collective-permute-start(bf16[128,640]{1,0:T(8,128)(2,1)S(1)} %collective-permute-done.6), channel_id=1, source_target_pairs={{0,2},{1,3},{2,0},{3,1},{4,6},{5,7},{6,4},{7,5},{8,10},{9,11},{10,... | collective-permute-start | bytes 491528 | tf_op jit(solution)/shard_map/ppermute | solution.py:83
  25.9 1.0 %collective-permute-start.13 = (bf16[128,640]{1,0:T(8,128)(2,1)S(1)}, bf16[128,640]{1,0:T(8,128)(2,1)S(1)}, u32[]{:S(2)}, u32[]{:S(2)}) collective-permute-start(bf16[128,640]{1,0:T(8,128)(2,1)S(1)} %collective-permute-done.12), channel_id=1, source_target_pairs={{0,2},{1,3},{2,0},{3,1},{4,6},{5,7},{6,4},{7,5},{8,10},{9,11},{10,... | collective-permute-start | bytes 491528 | tf_op jit(solution)/shard_map/ppermute | solution.py:83
  27.0 4.8 %collective-permute-done.7 = bf16[128,640]{1,0:T(8,128)(2,1)S(1)} collective-permute-done((bf16[128,640]{1,0:T(8,128)(2,1)S(1)}, bf16[128,640]{1,0:T(8,128)(2,1)S(1)}, u32[]{:S(2)}, u32[]{:S(2)}) %collective-permute-start.7) | collective-permute-done | bytes 163872 | tf_op jit(solution)/shard_map/ppermute | solution.py:83
  31.9 1.6 %collective-permute-done.13 = bf16[128,640]{1,0:T(8,128)(2,1)S(1)} collective-permute-done((bf16[128,640]{1,0:T(8,128)(2,1)S(1)}, bf16[128,640]{1,0:T(8,128)(2,1)S(1)}, u32[]{:S(2)}, u32[]{:S(2)}) %collective-permute-start.13) | collective-permute-done | bytes 163872 | tf_op jit(solution)/shard_map/ppermute | solution.py:83
  33.8 0.5 fusion.11
  34.3 0.7 %multiply_convert_fusion.2 = bf16[128,512]{1,0:T(8,128)(2,1)S(1)} fusion(f32[128,512]{1,0:T(8,128)S(1)} %fusion.11, bf16[128,2560]{1,0:T(8,128)(2,1)S(1)} %constant_dynamic-update-slice_fusion, bf16[640,512]{1,0:T(8,128)(2,1)S(1)} %get-tuple-element.17, bf16[640,512]{1,0:T(8,128)(2,1)S(1)} %get-tuple-element.18, ...), kind=kOutput, calls=%fused_computation.58 | convolution fusion | flops 346423296 | bytes 3670016 | tf_op jit(solution)/shard_map/dot_general | solution.py:90
  35.0 0.3 convolution_convert_fusion.6
  35.4 0.6 collective-permute-start.3
  36.0 1.2 %collective-permute-done.3 = bf16[128,1280]{1,0:T(8,128)(2,1)S(1)} collective-permute-done((bf16[128,1280]{1,0:T(8,128)(2,1)S(1)}, bf16[128,1280]{1,0:T(8,128)(2,1)S(1)}, u32[]{:S(2)}, u32[]{:S(2)}) %collective-permute-start.3) | collective-permute-done | bytes 327712 | tf_op jit(solution)/shard_map/ppermute | solution.py:95
  37.2 0.3 convert_add_fusion.3
  37.5 0.5 fusion.12
  38.0 0.7 %fusion.1 = bf16[128,512]{1,0:T(8,128)(2,1)S(1)} fusion(bf16[128,2560]{1,0:T(8,128)(2,1)S(1)} %pad_maximum_fusion.4, f32[128,512]{1,0:T(8,128)S(1)} %fusion.12, bf16[640,512]{1,0:T(8,128)(2,1)S(1)} %get-tuple-element.17, bf16[640,512]{1,0:T(8,128)(2,1)S(1)} %get-tuple-element.18, bf16[640,512]{1,0:T(8,128)(2,1)S(1)} %get-tuple-element.16, ...), kind=kOutput, calls=%fused_computation.16 | convolution fusion | flops 346423296 | bytes 3670016 | tf_op jit(solution)/shard_map/dot_general | solution.py:90
  38.8 0.3 convolution_convert_fusion.4
  39.1 0.4 collective-permute-start.9
  39.7 1.1 %collective-permute-start.4 = (bf16[128,640]{1,0:T(8,128)(2,1)S(1)}, bf16[128,640]{1,0:T(8,128)(2,1)S(1)}, u32[]{:S(2)}, u32[]{:S(2)}) collective-permute-start(bf16[128,640]{1,0:T(8,128)(2,1)S(1)} %slice.67), channel_id=1, source_target_pairs={{0,2},{1,3},{2,0},{3,1},{4,6},{5,7},{6,4},{7,5},{8,10},{9,11},{10,... | collective-permute-start | bytes 491528 | tf_op jit(solution)/shard_map/ppermute | solution.py:97
  40.8 0.3 convert_add_fusion.2
  41.2 0.5 fusion.13
  41.7 0.7 %fusion.2 = bf16[128,512]{1,0:T(8,128)(2,1)S(1)} fusion(bf16[128,2560]{1,0:T(8,128)(2,1)S(1)} %pad_maximum_fusion.5, f32[128,512]{1,0:T(8,128)S(1)} %fusion.13, bf16[640,512]{1,0:T(8,128)(2,1)S(1)} %get-tuple-element.17, bf16[640,512]{1,0:T(8,128)(2,1)S(1)} %get-tuple-element.18, bf16[640,512]{1,0:T(8,128)(2,1)S(1)} %get-tuple-element.16, ...), kind=kOutput, calls=%fused_computation.17 | convolution fusion | flops 346423296 | bytes 3670016 | tf_op jit(solution)/shard_map/dot_general | solution.py:90
  42.5 0.3 convolution_convert_fusion.2
  42.8 0.4 collective-permute-start.15
  43.3 2.7 %collective-permute-done.4 = bf16[128,640]{1,0:T(8,128)(2,1)S(1)} collective-permute-done((bf16[128,640]{1,0:T(8,128)(2,1)S(1)}, bf16[128,640]{1,0:T(8,128)(2,1)S(1)}, u32[]{:S(2)}, u32[]{:S(2)}) %collective-permute-start.4) | collective-permute-done | bytes 163872 | tf_op jit(solution)/shard_map/ppermute | solution.py:97
  46.0 2.1 %collective-permute-start.5 = (bf16[128,640]{1,0:T(8,128)(2,1)S(1)}, bf16[128,640]{1,0:T(8,128)(2,1)S(1)}, u32[]{:S(2)}, u32[]{:S(2)}) collective-permute-start(bf16[128,640]{1,0:T(8,128)(2,1)S(1)} %fusion.9), channel_id=1, source_target_pairs={{0,12},{4,8},{8,4},{12,0},{1,13},{5,9},{9,5},{13,1},{2,14},{6,10},... | collective-permute-start | bytes 491528 | tf_op jit(solution)/shard_map/ppermute | solution.py:102
  48.1 0.4 collective-permute-start.10
  48.4 0.3 convert_add_fusion.1
  48.8 1.8 %collective-permute-start.16 = (bf16[128,640]{1,0:T(8,128)(2,1)S(1)}, bf16[128,640]{1,0:T(8,128)(2,1)S(1)}, u32[]{:S(2)}, u32[]{:S(2)}) collective-permute-start(bf16[128,640]{1,0:T(8,128)(2,1)S(1)} %slice.65), channel_id=1, source_target_pairs={{0,2},{1,3},{2,0},{3,1},{4,6},{5,7},{6,4},{7,5},{8,10},{9,11},{10,... | collective-permute-start | bytes 491528 | tf_op jit(solution)/shard_map/ppermute | solution.py:97
  50.6 0.5 fusion.14
  51.2 0.7 %fusion.3 = bf16[128,512]{1,0:T(8,128)(2,1)S(1)} fusion(bf16[128,2560]{1,0:T(8,128)(2,1)S(1)} %pad_maximum_fusion.6, f32[128,512]{1,0:T(8,128)S(1)} %fusion.14, bf16[640,512]{1,0:T(8,128)(2,1)S(1)} %get-tuple-element.17, bf16[640,512]{1,0:T(8,128)(2,1)S(1)} %get-tuple-element.18, bf16[640,512]{1,0:T(8,128)(2,1)S(1)} %get-tuple-element.16, ...), kind=kOutput, calls=%fused_computation.18 | convolution fusion | flops 346423296 | bytes 3670016 | tf_op jit(solution)/shard_map/dot_general | solution.py:90
  51.9 0.4 convolution_convert_fusion
  52.3 2.7 %collective-permute-done.10 = bf16[128,640]{1,0:T(8,128)(2,1)S(1)} collective-permute-done((bf16[128,640]{1,0:T(8,128)(2,1)S(1)}, bf16[128,640]{1,0:T(8,128)(2,1)S(1)}, u32[]{:S(2)}, u32[]{:S(2)}) %collective-permute-start.10) | collective-permute-done | bytes 163872 | tf_op jit(solution)/shard_map/ppermute | solution.py:97
  55.1 1.5 %collective-permute-start.11 = (bf16[128,640]{1,0:T(8,128)(2,1)S(1)}, bf16[128,640]{1,0:T(8,128)(2,1)S(1)}, u32[]{:S(2)}, u32[]{:S(2)}) collective-permute-start(bf16[128,640]{1,0:T(8,128)(2,1)S(1)} %fusion.8), channel_id=1, source_target_pairs={{0,8},{4,12},{8,0},{12,4},{1,9},{5,13},{9,1},{13,5},{2,10},{6,14},... | collective-permute-start | bytes 491528 | tf_op jit(solution)/shard_map/ppermute | solution.py:102
  56.6 0.2 collective-permute-done.16
  56.8 1.8 %collective-permute-start.17 = (bf16[128,640]{1,0:T(8,128)(2,1)S(1)}, bf16[128,640]{1,0:T(8,128)(2,1)S(1)}, u32[]{:S(2)}, u32[]{:S(2)}) collective-permute-start(bf16[128,640]{1,0:T(8,128)(2,1)S(1)} %fusion.7), channel_id=1, source_target_pairs={{0,4},{4,0},{8,12},{12,8},{1,5},{5,1},{9,13},{13,9},{2,6},{6,2},{1... | collective-permute-start | bytes 491528 | tf_op jit(solution)/shard_map/ppermute | solution.py:102
  58.7 0.4 convert_add_fusion
  59.0 1.4 %collective-permute-start.21 = (bf16[128,640]{1,0:T(8,128)(2,1)S(1)}, bf16[128,640]{1,0:T(8,128)(2,1)S(1)}, u32[]{:S(2)}, u32[]{:S(2)}) collective-permute-start(bf16[128,640]{1,0:T(8,128)(2,1)S(1)} %slice.64), channel_id=1, source_target_pairs={{0,2},{1,3},{2,0},{3,1},{4,6},{5,7},{6,4},{7,5},{8,10},{9,11},{10,... | collective-permute-start | bytes 491528 | tf_op jit(solution)/shard_map/ppermute | solution.py:97
  60.4 3.0 %collective-permute-done.11 = bf16[128,640]{1,0:T(8,128)(2,1)S(1)} collective-permute-done((bf16[128,640]{1,0:T(8,128)(2,1)S(1)}, bf16[128,640]{1,0:T(8,128)(2,1)S(1)}, u32[]{:S(2)}, u32[]{:S(2)}) %collective-permute-start.11) | collective-permute-done | bytes 163872 | tf_op jit(solution)/shard_map/ppermute | solution.py:102
  63.5 1.0 %collective-permute-done.21 = bf16[128,640]{1,0:T(8,128)(2,1)S(1)} collective-permute-done((bf16[128,640]{1,0:T(8,128)(2,1)S(1)}, bf16[128,640]{1,0:T(8,128)(2,1)S(1)}, u32[]{:S(2)}, u32[]{:S(2)}) %collective-permute-start.21) | collective-permute-done | bytes 163872 | tf_op jit(solution)/shard_map/ppermute | solution.py:97
  64.4 0.9 %fusion.6 = bf16[128,640]{1,0:T(8,128)(2,1)} fusion(f32[128,1280]{1,0:T(8,128)S(1)} %convert_add_fusion, bf16[128,640]{1,0:T(8,128)(2,1)S(1)} %collective-permute-done.21, bf16[128,640]{1,0:T(8,128)(2,1)S(1)} %collective-permute-done.17, bf16[128,640]{1,0:T(8,128)(2,1)S(1)} %collective-permute-done.11, bf16[128,640]{1,0:T(8,128)(2,1)S(1)} %collective-permute-done.5, ...), kind=kLoop, calls=%fused_computation.42 | loop fusion | flops 1064960 | bytes 1147392 | tf_op jit(solution)/shard_map/convert_element_type | solution.py:106
  (46 shorter events, 1.4 us)
Async XLA Ops:
  0.0 7.3 %collective-permute-start.18 = (bf16[128,640]{1,0:T(8,128)(2,1)}, bf16[128,640]{1,0:T(8,128)(2,1)S(1)}, u32[]{:S(2)}, u32[]{:S(2)}) collective-permute-start(bf16[128,640]{1,0:T(8,128)(2,1)} %param.6), channel_id=1, source_target_pairs={{0,2},{1,3},{2,0},{3,1},{4,6},{5,7},{6,4},{7,5},{8,10},{9,11},{10,... | collective-permute-start | bytes 491528 | tf_op jit(solution)/shard_map/ppermute | solution.py:76
  4.8 1.7 %copy-start = (bf16[1,2560,512]{2,1,0:T(8,128)(2,1)S(1)}, bf16[1,2560,512]{2,1,0:T(8,128)(2,1)}, u32[]{:S(2)}) copy-start(bf16[1,2560,512]{2,1,0:T(8,128)(2,1)} %param.10) | copy-start | bytes 7864324
  6.5 0.9 %copy-start.2 = (bf16[128,640]{1,0:T(8,128)(2,1)S(1)}, bf16[128,640]{1,0:T(8,128)(2,1)}, u32[]{:S(2)}) copy-start(bf16[128,640]{1,0:T(8,128)(2,1)} %param.6) | copy-start | bytes 491524
  6.5 0.9 %copy-start.4 = (f32[128]{0:T(128)S(1)}, f32[128]{0:T(128)}, u32[]{:S(2)}) copy-start(f32[128]{0:T(128)} %param.7) | copy-start | bytes 1540
  6.5 4.9 %copy-start.1 = (bf16[1,512,2560]{2,1,0:T(8,128)(2,1)S(1)}, bf16[1,512,2560]{2,1,0:T(8,128)(2,1)}, u32[]{:S(2)}) copy-start(bf16[1,512,2560]{2,1,0:T(8,128)(2,1)} %param.11) | copy-start | bytes 7864324
  7.6 9.0 %collective-permute-start = (bf16[128,640]{1,0:T(8,128)(2,1)S(1)}, bf16[128,640]{1,0:T(8,128)(2,1)S(1)}, u32[]{:S(2)}, u32[]{:S(2)}) collective-permute-start(bf16[128,640]{1,0:T(8,128)(2,1)S(1)} %get-tuple-element.27), channel_id=1, source_target_pairs={{0,12},{4,8},{8,4},{12,0},{1,13},{5,9},{9,5},{13,1},{2,14},{6,10},... | collective-permute-start | bytes 491528 | tf_op jit(solution)/shard_map/ppermute | solution.py:66
  11.6 13.2 %collective-permute-start.6 = (bf16[128,640]{1,0:T(8,128)(2,1)S(1)}, bf16[128,640]{1,0:T(8,128)(2,1)S(1)}, u32[]{:S(2)}, u32[]{:S(2)}) collective-permute-start(bf16[128,640]{1,0:T(8,128)(2,1)S(1)} %get-tuple-element.27), channel_id=1, source_target_pairs={{0,8},{4,12},{8,0},{12,4},{1,9},{5,13},{9,1},{13,5},{2,10},{6,14},... | collective-permute-start | bytes 491528 | tf_op jit(solution)/shard_map/ppermute | solution.py:66
  11.7 14.2 %collective-permute-start.12 = (bf16[128,640]{1,0:T(8,128)(2,1)S(1)}, bf16[128,640]{1,0:T(8,128)(2,1)S(1)}, u32[]{:S(2)}, u32[]{:S(2)}) collective-permute-start(bf16[128,640]{1,0:T(8,128)(2,1)S(1)} %get-tuple-element.27), channel_id=1, source_target_pairs={{0,4},{4,0},{8,12},{12,8},{1,5},{5,1},{9,13},{13,9},{2,6},{6,2},{1... | collective-permute-start | bytes 491528 | tf_op jit(solution)/shard_map/ppermute | solution.py:66
  16.6 10.3 %collective-permute-start.1 = (bf16[128,640]{1,0:T(8,128)(2,1)S(1)}, bf16[128,640]{1,0:T(8,128)(2,1)S(1)}, u32[]{:S(2)}, u32[]{:S(2)}) collective-permute-start(bf16[128,640]{1,0:T(8,128)(2,1)S(1)} %collective-permute-done), channel_id=1, source_target_pairs={{0,2},{1,3},{2,0},{3,1},{4,6},{5,7},{6,4},{7,5},{8,10},{9,11},{10,... | collective-permute-start | bytes 491528 | tf_op jit(solution)/shard_map/ppermute | solution.py:83
  18.3 25.0 %collective-permute-start.19 = (bf16[128,1280]{1,0:T(8,128)(2,1)S(1)}, bf16[128,1280]{1,0:T(8,128)(2,1)S(1)}, u32[]{:S(2)}, u32[]{:S(2)}) collective-permute-start(bf16[128,1280]{1,0:T(8,128)(2,1)S(1)} %pad_maximum_fusion.10), channel_id=1, source_target_pairs={{0,1},{1,0},{2,3},{3,2},{4,5},{5,4},{6,7},{7,6},{8,9},{9,8},{10,11... | collective-permute-start | bytes 983048 | tf_op jit(solution)/shard_map/ppermute | solution.py:86
  24.9 7.0 %collective-permute-start.7 = (bf16[128,640]{1,0:T(8,128)(2,1)S(1)}, bf16[128,640]{1,0:T(8,128)(2,1)S(1)}, u32[]{:S(2)}, u32[]{:S(2)}) collective-permute-start(bf16[128,640]{1,0:T(8,128)(2,1)S(1)} %collective-permute-done.6), channel_id=1, source_target_pairs={{0,2},{1,3},{2,0},{3,1},{4,6},{5,7},{6,4},{7,5},{8,10},{9,11},{10,... | collective-permute-start | bytes 491528 | tf_op jit(solution)/shard_map/ppermute | solution.py:83
  25.9 7.7 %collective-permute-start.13 = (bf16[128,640]{1,0:T(8,128)(2,1)S(1)}, bf16[128,640]{1,0:T(8,128)(2,1)S(1)}, u32[]{:S(2)}, u32[]{:S(2)}) collective-permute-start(bf16[128,640]{1,0:T(8,128)(2,1)S(1)} %collective-permute-done.12), channel_id=1, source_target_pairs={{0,2},{1,3},{2,0},{3,1},{4,6},{5,7},{6,4},{7,5},{8,10},{9,11},{10,... | collective-permute-start | bytes 491528 | tf_op jit(solution)/shard_map/ppermute | solution.py:83
  27.0 6.8 %collective-permute-start.2 = (bf16[128,1280]{1,0:T(8,128)(2,1)S(1)}, bf16[128,1280]{1,0:T(8,128)(2,1)S(1)}, u32[]{:S(2)}, u32[]{:S(2)}) collective-permute-start(bf16[128,1280]{1,0:T(8,128)(2,1)S(1)} %pad_maximum_fusion.7), channel_id=1, source_target_pairs={{0,1},{1,0},{2,3},{3,2},{4,5},{5,4},{6,7},{7,6},{8,9},{9,8},{10,11... | collective-permute-start | bytes 983048 | tf_op jit(solution)/shard_map/ppermute | solution.py:86
  31.8 4.1 %collective-permute-start.8 = (bf16[128,1280]{1,0:T(8,128)(2,1)S(1)}, bf16[128,1280]{1,0:T(8,128)(2,1)S(1)}, u32[]{:S(2)}, u32[]{:S(2)}) collective-permute-start(bf16[128,1280]{1,0:T(8,128)(2,1)S(1)} %pad_maximum_fusion.8), channel_id=1, source_target_pairs={{0,1},{1,0},{2,3},{3,2},{4,5},{5,4},{6,7},{7,6},{8,9},{9,8},{10,11... | collective-permute-start | bytes 983048 | tf_op jit(solution)/shard_map/ppermute | solution.py:86
  33.6 6.0 %collective-permute-start.14 = (bf16[128,1280]{1,0:T(8,128)(2,1)S(1)}, bf16[128,1280]{1,0:T(8,128)(2,1)S(1)}, u32[]{:S(2)}, u32[]{:S(2)}) collective-permute-start(bf16[128,1280]{1,0:T(8,128)(2,1)S(1)} %pad_maximum_fusion.9), channel_id=1, source_target_pairs={{0,1},{1,0},{2,3},{3,2},{4,5},{5,4},{6,7},{7,6},{8,9},{9,8},{10,11... | collective-permute-start | bytes 983048 | tf_op jit(solution)/shard_map/ppermute | solution.py:86
  35.4 1.8 %collective-permute-start.3 = (bf16[128,1280]{1,0:T(8,128)(2,1)S(1)}, bf16[128,1280]{1,0:T(8,128)(2,1)S(1)}, u32[]{:S(2)}, u32[]{:S(2)}) collective-permute-start(bf16[128,1280]{1,0:T(8,128)(2,1)S(1)} %convolution_convert_fusion.6), channel_id=1, source_target_pairs={{0,1},{1,0},{2,3},{3,2},{4,5},{5,4},{6,7},{7,6},{8,9},{9,8},{10,11... | collective-permute-start | bytes 983048 | tf_op jit(solution)/shard_map/ppermute | solution.py:95
  39.1 1.7 %collective-permute-start.9 = (bf16[128,1280]{1,0:T(8,128)(2,1)S(1)}, bf16[128,1280]{1,0:T(8,128)(2,1)S(1)}, u32[]{:S(2)}, u32[]{:S(2)}) collective-permute-start(bf16[128,1280]{1,0:T(8,128)(2,1)S(1)} %convolution_convert_fusion.4), channel_id=1, source_target_pairs={{0,1},{1,0},{2,3},{3,2},{4,5},{5,4},{6,7},{7,6},{8,9},{9,8},{10,11... | collective-permute-start | bytes 983048 | tf_op jit(solution)/shard_map/ppermute | solution.py:95
  39.7 6.3 %collective-permute-start.4 = (bf16[128,640]{1,0:T(8,128)(2,1)S(1)}, bf16[128,640]{1,0:T(8,128)(2,1)S(1)}, u32[]{:S(2)}, u32[]{:S(2)}) collective-permute-start(bf16[128,640]{1,0:T(8,128)(2,1)S(1)} %slice.67), channel_id=1, source_target_pairs={{0,2},{1,3},{2,0},{3,1},{4,6},{5,7},{6,4},{7,5},{8,10},{9,11},{10,... | collective-permute-start | bytes 491528 | tf_op jit(solution)/shard_map/ppermute | solution.py:97
  42.8 5.6 %collective-permute-start.15 = (bf16[128,1280]{1,0:T(8,128)(2,1)S(1)}, bf16[128,1280]{1,0:T(8,128)(2,1)S(1)}, u32[]{:S(2)}, u32[]{:S(2)}) collective-permute-start(bf16[128,1280]{1,0:T(8,128)(2,1)S(1)} %convolution_convert_fusion.2), channel_id=1, source_target_pairs={{0,1},{1,0},{2,3},{3,2},{4,5},{5,4},{6,7},{7,6},{8,9},{9,8},{10,11... | collective-permute-start | bytes 983048 | tf_op jit(solution)/shard_map/ppermute | solution.py:95
  46.0 14.4 %collective-permute-start.5 = (bf16[128,640]{1,0:T(8,128)(2,1)S(1)}, bf16[128,640]{1,0:T(8,128)(2,1)S(1)}, u32[]{:S(2)}, u32[]{:S(2)}) collective-permute-start(bf16[128,640]{1,0:T(8,128)(2,1)S(1)} %fusion.9), channel_id=1, source_target_pairs={{0,12},{4,8},{8,4},{12,0},{1,13},{5,9},{9,5},{13,1},{2,14},{6,10},... | collective-permute-start | bytes 491528 | tf_op jit(solution)/shard_map/ppermute | solution.py:102
  48.1 7.0 %collective-permute-start.10 = (bf16[128,640]{1,0:T(8,128)(2,1)S(1)}, bf16[128,640]{1,0:T(8,128)(2,1)S(1)}, u32[]{:S(2)}, u32[]{:S(2)}) collective-permute-start(bf16[128,640]{1,0:T(8,128)(2,1)S(1)} %slice.66), channel_id=1, source_target_pairs={{0,2},{1,3},{2,0},{3,1},{4,6},{5,7},{6,4},{7,5},{8,10},{9,11},{10,... | collective-permute-start | bytes 491528 | tf_op jit(solution)/shard_map/ppermute | solution.py:97
  48.8 8.0 %collective-permute-start.16 = (bf16[128,640]{1,0:T(8,128)(2,1)S(1)}, bf16[128,640]{1,0:T(8,128)(2,1)S(1)}, u32[]{:S(2)}, u32[]{:S(2)}) collective-permute-start(bf16[128,640]{1,0:T(8,128)(2,1)S(1)} %slice.65), channel_id=1, source_target_pairs={{0,2},{1,3},{2,0},{3,1},{4,6},{5,7},{6,4},{7,5},{8,10},{9,11},{10,... | collective-permute-start | bytes 491528 | tf_op jit(solution)/shard_map/ppermute | solution.py:97
  52.3 8.2 %copy-start.3 = (s32[128,1]{0,1:T(1,128)S(1)}, s32[128,1]{0,1:T(1,128)}, u32[]{:S(2)}) copy-start(s32[128,1]{0,1:T(1,128)} %param.8) | copy-start | bytes 1540
  52.3 6.4 %collective-permute-start.20 = (bf16[128,1280]{1,0:T(8,128)(2,1)S(1)}, bf16[128,1280]{1,0:T(8,128)(2,1)S(1)}, u32[]{:S(2)}, u32[]{:S(2)}) collective-permute-start(bf16[128,1280]{1,0:T(8,128)(2,1)S(1)} %convolution_convert_fusion), channel_id=1, source_target_pairs={{0,1},{1,0},{2,3},{3,2},{4,5},{5,4},{6,7},{7,6},{8,9},{9,8},{10,11... | collective-permute-start | bytes 983048 | tf_op jit(solution)/shard_map/ppermute | solution.py:95
  55.1 8.4 %collective-permute-start.11 = (bf16[128,640]{1,0:T(8,128)(2,1)S(1)}, bf16[128,640]{1,0:T(8,128)(2,1)S(1)}, u32[]{:S(2)}, u32[]{:S(2)}) collective-permute-start(bf16[128,640]{1,0:T(8,128)(2,1)S(1)} %fusion.8), channel_id=1, source_target_pairs={{0,8},{4,12},{8,0},{12,4},{1,9},{5,13},{9,1},{13,5},{2,10},{6,14},... | collective-permute-start | bytes 491528 | tf_op jit(solution)/shard_map/ppermute | solution.py:102
  56.8 6.6 %collective-permute-start.17 = (bf16[128,640]{1,0:T(8,128)(2,1)S(1)}, bf16[128,640]{1,0:T(8,128)(2,1)S(1)}, u32[]{:S(2)}, u32[]{:S(2)}) collective-permute-start(bf16[128,640]{1,0:T(8,128)(2,1)S(1)} %fusion.7), channel_id=1, source_target_pairs={{0,4},{4,0},{8,12},{12,8},{1,5},{5,1},{9,13},{13,9},{2,6},{6,2},{1... | collective-permute-start | bytes 491528 | tf_op jit(solution)/shard_map/ppermute | solution.py:102
  59.0 5.4 %collective-permute-start.21 = (bf16[128,640]{1,0:T(8,128)(2,1)S(1)}, bf16[128,640]{1,0:T(8,128)(2,1)S(1)}, u32[]{:S(2)}, u32[]{:S(2)}) collective-permute-start(bf16[128,640]{1,0:T(8,128)(2,1)S(1)} %slice.64), channel_id=1, source_target_pairs={{0,2},{1,3},{2,0},{3,1},{4,6},{5,7},{6,4},{7,5},{8,10},{9,11},{10,... | collective-permute-start | bytes 491528 | tf_op jit(solution)/shard_map/ppermute | solution.py:97

commit v27 on v21

--- a/solution.py
+++ b/solution.py
@@ -89,15 +89,14 @@
         previous = keep
         over_c = keep.astype(jnp.float32) + lax.ppermute(
             send, "tensor", _xor_pairs(n_tensor, 1)).astype(jnp.float32)
-        summed = over_c[:, :width] + lax.ppermute(
-            over_c[:, width:].astype(jnp.bfloat16), "tensor", _xor_pairs(n_tensor, 2)).astype(jnp.float32)
-        for i, k in enumerate(wave):
-            part = summed[i * tok_rows:(i + 1) * tok_rows]
-            if k:
-                part = lax.ppermute(
-                    part.astype(jnp.bfloat16), "expert", _xor_pairs(n_expert, k)).astype(jnp.float32)
-            part = jnp.where(routed == (me ^ k) // SPAN, part, 0.0)
-            total = part if total is None else total + part
+        k = wave[0]
+        if k:
+            over_c = lax.ppermute(
+                over_c.astype(jnp.bfloat16), "expert", _xor_pairs(n_expert, k)).astype(jnp.float32)
+        over_c = jnp.where(routed == (me ^ k) // SPAN, over_c, 0.0)
+        total = over_c if total is None else total + over_c
+    total = total[:, :width] + lax.ppermute(
+        total[:, width:].astype(jnp.bfloat16), "tensor", _xor_pairs(n_tensor, 2)).astype(jnp.float32)
     return total.astype(jnp.bfloat16)
 
 

time: 62.9 us -> 80.1 us (1.27)
  waiting for transfers between devices: 17.7 us -> 38.7 us
  starting transfers between devices: 21.3 us -> 17.4 us
    ppermute x7 -> x4, waiting for transfers between devices: 9.05 us -> 29.9 us  [the longest x3 25.3 us: gathered(): lax.ppermute(over_c.astype(jnp.bfloat16), 'expert', _xor_pairs(n_expert, k))]
    ppermute x7 -> x4, starting transfers between devices: 9.96 us -> 5.74 us  [the longest x3 4.52 us: gathered(): lax.ppermute(over_c.astype(jnp.bfloat16), 'expert', _xor_pairs(n_expert, k))]
  transfers between devices with their start and end apart: 22 -> 19, of which waited for: 9 -> 8; matrix products, arithmetic and copies ran while one was open for 31% -> 24% of each run, Pallas kernels for 0% -> 0%
where the time goes in v27:
time: 80.1 us; the launch traced here: 79.8 us
  waiting for transfers between devices  38.7 us (48%)
  starting transfers between devices  17.4 us (22%)
  other arithmetic  8.91 us (11%)
  matrix products  7.74 us (10%)
  local copies, waits for them, and re-layouts  6.65 us (8%)
    ppermute x3, waiting for transfers between devices, gathered(): lax.ppermute(over_c.astype(jnp.bfloat16), 'expert', _xor_pairs(n_expert, k))  25.3 us
    ppermute x3, starting transfers between devices, gathered(): lax.ppermute(scaled, 'expert', _xor_pairs(n_expert, k))  5.76 us
    ppermute x1, waiting for transfers between devices, gathered(): lax.ppermute(total[:, width:].astype(jnp.bfloat16), 'tensor', _xor_pairs(...  4.55 us
    ppermute x3, starting transfers between devices, gathered(): lax.ppermute(over_c.astype(jnp.bfloat16), 'expert', _xor_pairs(n_expert, k))  4.52 us
    ppermute x3, waiting for transfers between devices, gathered(): lax.ppermute(scaled, 'expert', _xor_pairs(n_expert, k))  4.37 us
    ppermute x4, starting transfers between devices, gathered(): lax.ppermute(piece, 'tensor', _xor_pairs(n_tensor, 2))  4.13 us
    ppermute x4, waiting for transfers between devices, gathered(): lax.ppermute(piece, 'tensor', _xor_pairs(n_tensor, 2))  3.91 us
    concatenate x4, other arithmetic, gathered(): jnp.concatenate([piece, lax.ppermute(piece, 'tensor', _xor_pairs(n_tensor...  3.77 us
  transfers between devices with their start and end apart: 19, of which 8 were waited for; matrix products, arithmetic and copies ran while one was open for 24% of the time, Pallas kernels for 0%

profile of v27, /device:TPU:0, one launch (start us, length us, event | category | flops | bytes accessed | tf_op | source)
XLA Modules:
  0.0 79.8 jit_solution(16297571741366790241)
XLA Ops:
  0.0 1.0 %multiply_convert_fusion = bf16[128,640]{1,0:T(8,128)(2,1)S(1)} fusion(bf16[128,640]{1,0:T(8,128)(2,1)} %param.6, f32[128]{0:T(128)} %param.7), kind=kLoop, calls=%fused_computation.45 | loop fusion | flops 245760 | bytes 328192 | tf_op jit(solution)/shard_map/convert_element_type | solution.py:64
  1.0 5.1 %collective-permute-start = (bf16[128,640]{1,0:T(8,128)(2,1)S(1)}, bf16[128,640]{1,0:T(8,128)(2,1)}, u32[]{:S(2)}, u32[]{:S(2)}) collective-permute-start(bf16[128,640]{1,0:T(8,128)(2,1)S(1)} %multiply_convert_fusion), channel_id=1, source_target_pairs={{0,12},{4,8},{8,4},{12,0},{1,13},{5,9},{9,5},{13,1},{2,14},{6,10},... | collective-permute-start | bytes 491528 | tf_op jit(solution)/shard_map/ppermute | solution.py:66
  6.1 0.6 collective-permute-start.10
  6.8 1.6 %collective-permute-start.15 = (bf16[128,640]{1,0:T(8,128)(2,1)S(1)}, bf16[128,640]{1,0:T(8,128)(2,1)}, u32[]{:S(2)}, u32[]{:S(2)}) collective-permute-start(bf16[128,640]{1,0:T(8,128)(2,1)S(1)} %multiply_convert_fusion), channel_id=1, source_target_pairs={{0,2},{1,3},{2,0},{3,1},{4,6},{5,7},{6,4},{7,5},{8,10},{9,11},{10,... | collective-permute-start | bytes 491528 | tf_op jit(solution)/shard_map/ppermute | solution.py:79
  8.4 2.0 %dynamic-slice_bitcast_fusion.11 = (bf16[640,512]{1,0:T(8,128)(2,1)S(1)}, bf16[640,512]{1,0:T(8,128)(2,1)S(1)}, bf16[640,512]{1,0:T(8,128)(2,1)S(1)}, bf16[640,512]{1,0:T(8,128)(2,1)S(1)}) fusion(bf16[1,2560,512]{2,1,0:T(8,128)(2,1)} %param.9, s32[]{:T(128)S(6)} %select_n.48, s32[]{:T(128)S(6)} %select_n.49, s32[]{:T(128)S(6)} %select_n.51, s32[]{:T(128)S(6)} %select_n.50), kind=kLoop, calls=%fused_computation.37 | loop fusion | bytes 5242896 | tf_op jit(solution)/shard_map/dynamic_slice | solution.py:55
  10.4 0.5 copy-done
  10.9 1.4 %dynamic-slice_bitcast_fusion.7 = (bf16[640,512]{1,0:T(8,128)(2,1)S(1)}, bf16[640,512]{1,0:T(8,128)(2,1)}, bf16[640,512]{1,0:T(8,128)(2,1)}, bf16[640,512]{1,0:T(8,128)(2,1)}) fusion(bf16[1,2560,512]{2,1,0:T(8,128)(2,1)S(1)} %copy-done, s32[]{:T(128)S(6)} %select_n.48, s32[]{:T(128)S(6)} %select_n.49, s32[]{:T(128)S(6)} %select_n.51, s32[]{:T(128)S(6)} %select_n.50), kind=kLoop, calls=%fused_computation.33 | loop fusion | bytes 5242896 | tf_op jit(solution)/shard_map/dynamic_slice | solution.py:55
  12.5 1.5 %copy-done.1 = bf16[1,512,2560]{2,1,0:T(8,128)(2,1)S(1)} copy-done((bf16[1,512,2560]{2,1,0:T(8,128)(2,1)S(1)}, bf16[1,512,2560]{2,1,0:T(8,128)(2,1)}, u32[]{:S(2)}) %copy-start.1) | copy-done | bytes 2621464
  14.3 0.5 collective-permute-start.1
  14.7 0.9 %pad_maximum_fusion.10 = bf16[128,1280]{1,0:T(8,128)(2,1)S(1)} fusion(bf16[128,640]{1,0:T(8,128)(2,1)} %collective-permute-done.15, bf16[128,640]{1,0:T(8,128)(2,1)S(1)} %multiply_convert_fusion), kind=kLoop, calls=%fused_computation.44 | loop fusion | flops 655360 | bytes 655360 | tf_op jit(solution)/shard_map/concatenate | solution.py:78
  15.8 4.4 %collective-permute-done.5 = bf16[128,640]{1,0:T(8,128)(2,1)} collective-permute-done((bf16[128,640]{1,0:T(8,128)(2,1)S(1)}, bf16[128,640]{1,0:T(8,128)(2,1)}, u32[]{:S(2)}, u32[]{:S(2)}) %collective-permute-start.5) | collective-permute-done | bytes 163872 | tf_op jit(solution)/shard_map/ppermute | solution.py:66
  20.1 1.5 %collective-permute-start.6 = (bf16[128,640]{1,0:T(8,128)(2,1)}, bf16[128,640]{1,0:T(8,128)(2,1)S(1)}, u32[]{:S(2)}, u32[]{:S(2)}) collective-permute-start(bf16[128,640]{1,0:T(8,128)(2,1)} %collective-permute-done.5), channel_id=1, source_target_pairs={{0,2},{1,3},{2,0},{3,1},{4,6},{5,7},{6,4},{7,5},{8,10},{9,11},{10,... | collective-permute-start | bytes 491528 | tf_op jit(solution)/shard_map/ppermute | solution.py:79
  21.6 0.5 collective-permute-start.11
  22.2 0.9 %constant_dynamic-update-slice_fusion.2 = bf16[128,2560]{1,0:T(8,128)(2,1)S(1)} fusion(bf16[128,640]{1,0:T(8,128)(2,1)} %collective-permute-done), kind=kLoop, calls=%fused_computation.49 | loop fusion | bytes 327680
  23.1 0.9 %pad_maximum_fusion.7 = bf16[128,1280]{1,0:T(8,128)(2,1)S(1)} fusion(bf16[128,640]{1,0:T(8,128)(2,1)S(1)} %collective-permute-done.1, bf16[128,640]{1,0:T(8,128)(2,1)} %collective-permute-done), kind=kLoop, calls=%fused_computation.41 | loop fusion | flops 655360 | bytes 655360 | tf_op jit(solution)/shard_map/concatenate | solution.py:78
  24.1 3.2 %collective-permute-done.6 = bf16[128,640]{1,0:T(8,128)(2,1)S(1)} collective-permute-done((bf16[128,640]{1,0:T(8,128)(2,1)}, bf16[128,640]{1,0:T(8,128)(2,1)S(1)}, u32[]{:S(2)}, u32[]{:S(2)}) %collective-permute-start.6) | collective-permute-done | bytes 163872 | tf_op jit(solution)/shard_map/ppermute | solution.py:79
  27.3 0.9 %pad_maximum_fusion.8 = bf16[128,1280]{1,0:T(8,128)(2,1)S(1)} fusion(bf16[128,640]{1,0:T(8,128)(2,1)S(1)} %collective-permute-done.6, bf16[128,640]{1,0:T(8,128)(2,1)} %collective-permute-done.5), kind=kLoop, calls=%fused_computation.42 | loop fusion | flops 655360 | bytes 655360 | tf_op jit(solution)/shard_map/concatenate | solution.py:78
  28.4 0.7 collective-permute-done.11
  29.1 0.9 %pad_maximum_fusion.9 = bf16[128,1280]{1,0:T(8,128)(2,1)S(1)} fusion(bf16[128,640]{1,0:T(8,128)(2,1)S(1)} %collective-permute-done.11, bf16[128,640]{1,0:T(8,128)(2,1)} %collective-permute-done.10), kind=kLoop, calls=%fused_computation.43 | loop fusion | flops 655360 | bytes 655360 | tf_op jit(solution)/shard_map/concatenate | solution.py:78
  30.2 0.5 fusion.6
  30.7 0.7 multiply_convert_fusion.1
  31.5 0.3 convolution_convert_fusion.6
  31.8 0.6 collective-permute-start.3
  32.4 1.0 %pad_maximum_fusion.4 = bf16[128,2560]{1,0:T(8,128)(2,1)S(1)} fusion(bf16[128,1280]{1,0:T(8,128)(2,1)S(1)} %collective-permute-done.7, bf16[128,640]{1,0:T(8,128)(2,1)S(1)} %collective-permute-done.6, bf16[128,640]{1,0:T(8,128)(2,1)} %collective-permute-done.5), kind=kLoop, calls=%fused_computation.19 | loop fusion | flops 1966080 | bytes 1310720 | tf_op jit(solution)/shard_map/concatenate | solution.py:80
  33.6 0.4 add_convert_fusion.2
  34.0 0.5 fusion.7
  34.5 0.7 fusion.1
  35.2 0.3 convolution_convert_fusion.4
  35.6 0.4 collective-permute-start.8
  36.1 1.0 %pad_maximum_fusion.5 = bf16[128,2560]{1,0:T(8,128)(2,1)S(1)} fusion(bf16[128,1280]{1,0:T(8,128)(2,1)S(1)} %collective-permute-done.12, bf16[128,640]{1,0:T(8,128)(2,1)S(1)} %collective-permute-done.11, bf16[128,640]{1,0:T(8,128)(2,1)} %collective-permute-done.10), kind=kLoop, calls=%fused_computation.20 | loop fusion | flops 1966080 | bytes 1310720 | tf_op jit(solution)/shard_map/concatenate | solution.py:80
  37.3 0.3 add_convert_fusion.1
  37.7 0.5 fusion.8
  38.2 0.7 fusion.2
  38.9 0.3 convolution_convert_fusion.2
  39.3 0.4 collective-permute-start.13
  39.7 1.0 %pad_maximum_fusion.6 = bf16[128,2560]{1,0:T(8,128)(2,1)S(1)} fusion(bf16[128,1280]{1,0:T(8,128)(2,1)S(1)} %collective-permute-done.16, bf16[128,640]{1,0:T(8,128)(2,1)} %collective-permute-done.15, bf16[128,640]{1,0:T(8,128)(2,1)S(1)} %multiply_convert_fusion), kind=kLoop, calls=%fused_computation.21 | loop fusion | flops 1966080 | bytes 1310720 | tf_op jit(solution)/shard_map/concatenate | solution.py:80
  40.7 2.4 %collective-permute-start.4 = (bf16[128,1280]{1,0:T(8,128)(2,1)S(1)}, bf16[128,1280]{1,0:T(8,128)(2,1)S(1)}, u32[]{:S(2)}, u32[]{:S(2)}) collective-permute-start(bf16[128,1280]{1,0:T(8,128)(2,1)S(1)} %add_convert_fusion.2), channel_id=1, source_target_pairs={{0,12},{4,8},{8,4},{12,0},{1,13},{5,9},{9,5},{13,1},{2,14},{6,10},... | collective-permute-start | bytes 983048 | tf_op jit(solution)/shard_map/ppermute | solution.py:94
  43.0 1.1 %collective-permute-start.9 = (bf16[128,1280]{1,0:T(8,128)(2,1)S(1)}, bf16[128,1280]{1,0:T(8,128)(2,1)S(1)}, u32[]{:S(2)}, u32[]{:S(2)}) collective-permute-start(bf16[128,1280]{1,0:T(8,128)(2,1)S(1)} %add_convert_fusion.1), channel_id=1, source_target_pairs={{0,8},{4,12},{8,0},{12,4},{1,9},{5,13},{9,1},{13,5},{2,10},{6,14},... | collective-permute-start | bytes 983048 | tf_op jit(solution)/shard_map/ppermute | solution.py:94
  44.1 0.3 add_convert_fusion
  44.5 0.5 fusion.9
  45.0 0.7 fusion.3
  45.7 0.3 convolution_convert_fusion
  46.2 1.1 %collective-permute-start.14 = (bf16[128,1280]{1,0:T(8,128)(2,1)S(1)}, bf16[128,1280]{1,0:T(8,128)(2,1)S(1)}, u32[]{:S(2)}, u32[]{:S(2)}) collective-permute-start(bf16[128,1280]{1,0:T(8,128)(2,1)S(1)} %add_convert_fusion), channel_id=1, source_target_pairs={{0,4},{4,0},{8,12},{12,8},{1,5},{5,1},{9,13},{13,9},{2,6},{6,2},{1... | collective-permute-start | bytes 983048 | tf_op jit(solution)/shard_map/ppermute | solution.py:94
  47.6 5.6 %collective-permute-done.4 = bf16[128,1280]{1,0:T(8,128)(2,1)S(1)} collective-permute-done((bf16[128,1280]{1,0:T(8,128)(2,1)S(1)}, bf16[128,1280]{1,0:T(8,128)(2,1)S(1)}, u32[]{:S(2)}, u32[]{:S(2)}) %collective-permute-start.4) | collective-permute-done | bytes 327712 | tf_op jit(solution)/shard_map/ppermute | solution.py:94
  53.2 19.7 %collective-permute-done.9 = bf16[128,1280]{1,0:T(8,128)(2,1)S(1)} collective-permute-done((bf16[128,1280]{1,0:T(8,128)(2,1)S(1)}, bf16[128,1280]{1,0:T(8,128)(2,1)S(1)}, u32[]{:S(2)}, u32[]{:S(2)}) %collective-permute-start.9) | collective-permute-done | bytes 327712 | tf_op jit(solution)/shard_map/ppermute | solution.py:94
  73.3 1.2 %collective-permute-start.18 = (bf16[128,640]{1,0:T(8,128)(2,1)S(1)}, bf16[128,640]{1,0:T(8,128)(2,1)S(1)}, u32[]{:S(2)}, u32[]{:S(2)}) collective-permute-start(bf16[128,640]{1,0:T(8,128)(2,1)S(1)} %slice.15), channel_id=1, source_target_pairs={{0,2},{1,3},{2,0},{3,1},{4,6},{5,7},{6,4},{7,5},{8,10},{9,11},{10,... | collective-permute-start | bytes 491528 | tf_op jit(solution)/shard_map/ppermute | solution.py:98
  74.5 4.6 %collective-permute-done.18 = bf16[128,640]{1,0:T(8,128)(2,1)S(1)} collective-permute-done((bf16[128,640]{1,0:T(8,128)(2,1)S(1)}, bf16[128,640]{1,0:T(8,128)(2,1)S(1)}, u32[]{:S(2)}, u32[]{:S(2)}) %collective-permute-start.18) | collective-permute-done | bytes 163872 | tf_op jit(solution)/shard_map/ppermute | solution.py:98
  79.1 0.7 fusion.4
  (37 shorter events, 2.2 us)
Async XLA Ops:
  1.0 13.2 %collective-permute-start = (bf16[128,640]{1,0:T(8,128)(2,1)S(1)}, bf16[128,640]{1,0:T(8,128)(2,1)}, u32[]{:S(2)}, u32[]{:S(2)}) collective-permute-start(bf16[128,640]{1,0:T(8,128)(2,1)S(1)} %multiply_convert_fusion), channel_id=1, source_target_pairs={{0,12},{4,8},{8,4},{12,0},{1,13},{5,9},{9,5},{13,1},{2,14},{6,10},... | collective-permute-start | bytes 491528 | tf_op jit(solution)/shard_map/ppermute | solution.py:66
  6.1 14.0 %collective-permute-start.5 = (bf16[128,640]{1,0:T(8,128)(2,1)S(1)}, bf16[128,640]{1,0:T(8,128)(2,1)}, u32[]{:S(2)}, u32[]{:S(2)}) collective-permute-start(bf16[128,640]{1,0:T(8,128)(2,1)S(1)} %multiply_convert_fusion), channel_id=1, source_target_pairs={{0,8},{4,12},{8,0},{12,4},{1,9},{5,13},{9,1},{13,5},{2,10},{6,14},... | collective-permute-start | bytes 491528 | tf_op jit(solution)/shard_map/ppermute | solution.py:66
  6.1 15.5 %collective-permute-start.10 = (bf16[128,640]{1,0:T(8,128)(2,1)S(1)}, bf16[128,640]{1,0:T(8,128)(2,1)}, u32[]{:S(2)}, u32[]{:S(2)}) collective-permute-start(bf16[128,640]{1,0:T(8,128)(2,1)S(1)} %multiply_convert_fusion), channel_id=1, source_target_pairs={{0,4},{4,0},{8,12},{12,8},{1,5},{5,1},{9,13},{13,9},{2,6},{6,2},{1... | collective-permute-start | bytes 491528 | tf_op jit(solution)/shard_map/ppermute | solution.py:66
  6.8 8.0 %collective-permute-start.15 = (bf16[128,640]{1,0:T(8,128)(2,1)S(1)}, bf16[128,640]{1,0:T(8,128)(2,1)}, u32[]{:S(2)}, u32[]{:S(2)}) collective-permute-start(bf16[128,640]{1,0:T(8,128)(2,1)S(1)} %multiply_convert_fusion), channel_id=1, source_target_pairs={{0,2},{1,3},{2,0},{3,1},{4,6},{5,7},{6,4},{7,5},{8,10},{9,11},{10,... | collective-permute-start | bytes 491528 | tf_op jit(solution)/shard_map/ppermute | solution.py:79
  8.4 2.5 %copy-start = (bf16[1,2560,512]{2,1,0:T(8,128)(2,1)S(1)}, bf16[1,2560,512]{2,1,0:T(8,128)(2,1)}, u32[]{:S(2)}) copy-start(bf16[1,2560,512]{2,1,0:T(8,128)(2,1)} %param.10) | copy-start | bytes 7864324
  12.3 1.7 %copy-start.1 = (bf16[1,512,2560]{2,1,0:T(8,128)(2,1)S(1)}, bf16[1,512,2560]{2,1,0:T(8,128)(2,1)}, u32[]{:S(2)}) copy-start(bf16[1,512,2560]{2,1,0:T(8,128)(2,1)} %param.11) | copy-start | bytes 7864324
  14.3 8.8 %collective-permute-start.1 = (bf16[128,640]{1,0:T(8,128)(2,1)}, bf16[128,640]{1,0:T(8,128)(2,1)S(1)}, u32[]{:S(2)}, u32[]{:S(2)}) collective-permute-start(bf16[128,640]{1,0:T(8,128)(2,1)} %collective-permute-done), channel_id=1, source_target_pairs={{0,2},{1,3},{2,0},{3,1},{4,6},{5,7},{6,4},{7,5},{8,10},{9,11},{10,... | collective-permute-start | bytes 491528 | tf_op jit(solution)/shard_map/ppermute | solution.py:79
  15.7 24.0 %collective-permute-start.16 = (bf16[128,1280]{1,0:T(8,128)(2,1)S(1)}, bf16[128,1280]{1,0:T(8,128)(2,1)S(1)}, u32[]{:S(2)}, u32[]{:S(2)}) collective-permute-start(bf16[128,1280]{1,0:T(8,128)(2,1)S(1)} %pad_maximum_fusion.10), channel_id=1, source_target_pairs={{0,1},{1,0},{2,3},{3,2},{4,5},{5,4},{6,7},{7,6},{8,9},{9,8},{10,11... | collective-permute-start | bytes 983048 | tf_op jit(solution)/shard_map/ppermute | solution.py:81
  20.1 7.2 %collective-permute-start.6 = (bf16[128,640]{1,0:T(8,128)(2,1)}, bf16[128,640]{1,0:T(8,128)(2,1)S(1)}, u32[]{:S(2)}, u32[]{:S(2)}) collective-permute-start(bf16[128,640]{1,0:T(8,128)(2,1)} %collective-permute-done.5), channel_id=1, source_target_pairs={{0,2},{1,3},{2,0},{3,1},{4,6},{5,7},{6,4},{7,5},{8,10},{9,11},{10,... | collective-permute-start | bytes 491528 | tf_op jit(solution)/shard_map/ppermute | solution.py:79
  21.6 7.5 %collective-permute-start.11 = (bf16[128,640]{1,0:T(8,128)(2,1)}, bf16[128,640]{1,0:T(8,128)(2,1)S(1)}, u32[]{:S(2)}, u32[]{:S(2)}) collective-permute-start(bf16[128,640]{1,0:T(8,128)(2,1)} %collective-permute-done.10), channel_id=1, source_target_pairs={{0,2},{1,3},{2,0},{3,1},{4,6},{5,7},{6,4},{7,5},{8,10},{9,11},{10,... | collective-permute-start | bytes 491528 | tf_op jit(solution)/shard_map/ppermute | solution.py:79
  24.1 6.1 %collective-permute-start.2 = (bf16[128,1280]{1,0:T(8,128)(2,1)S(1)}, bf16[128,1280]{1,0:T(8,128)(2,1)S(1)}, u32[]{:S(2)}, u32[]{:S(2)}) collective-permute-start(bf16[128,1280]{1,0:T(8,128)(2,1)S(1)} %pad_maximum_fusion.7), channel_id=1, source_target_pairs={{0,1},{1,0},{2,3},{3,2},{4,5},{5,4},{6,7},{7,6},{8,9},{9,8},{10,11... | collective-permute-start | bytes 983048 | tf_op jit(solution)/shard_map/ppermute | solution.py:81
  28.3 2.4 %copy-start.2 = (bf16[640,512]{1,0:T(8,128)(2,1)S(1)}, bf16[640,512]{1,0:T(8,128)(2,1)}, u32[]{:S(2)}) copy-start(bf16[640,512]{1,0:T(8,128)(2,1)} %get-tuple-element.16) | copy-start | bytes 1966084
  28.3 2.4 %copy-start.3 = (bf16[640,512]{1,0:T(8,128)(2,1)S(1)}, bf16[640,512]{1,0:T(8,128)(2,1)}, u32[]{:S(2)}) copy-start(bf16[640,512]{1,0:T(8,128)(2,1)} %get-tuple-element.17) | copy-start | bytes 1966084
  28.3 2.4 %copy-start.4 = (bf16[640,512]{1,0:T(8,128)(2,1)S(1)}, bf16[640,512]{1,0:T(8,128)(2,1)}, u32[]{:S(2)}) copy-start(bf16[640,512]{1,0:T(8,128)(2,1)} %get-tuple-element.18) | copy-start | bytes 1966084
  28.3 4.1 %collective-permute-start.7 = (bf16[128,1280]{1,0:T(8,128)(2,1)S(1)}, bf16[128,1280]{1,0:T(8,128)(2,1)S(1)}, u32[]{:S(2)}, u32[]{:S(2)}) collective-permute-start(bf16[128,1280]{1,0:T(8,128)(2,1)S(1)} %pad_maximum_fusion.8), channel_id=1, source_target_pairs={{0,1},{1,0},{2,3},{3,2},{4,5},{5,4},{6,7},{7,6},{8,9},{9,8},{10,11... | collective-permute-start | bytes 983048 | tf_op jit(solution)/shard_map/ppermute | solution.py:81
  30.0 6.0 %collective-permute-start.12 = (bf16[128,1280]{1,0:T(8,128)(2,1)S(1)}, bf16[128,1280]{1,0:T(8,128)(2,1)S(1)}, u32[]{:S(2)}, u32[]{:S(2)}) collective-permute-start(bf16[128,1280]{1,0:T(8,128)(2,1)S(1)} %pad_maximum_fusion.9), channel_id=1, source_target_pairs={{0,1},{1,0},{2,3},{3,2},{4,5},{5,4},{6,7},{7,6},{8,9},{9,8},{10,11... | collective-permute-start | bytes 983048 | tf_op jit(solution)/shard_map/ppermute | solution.py:81
  31.8 1.8 %collective-permute-start.3 = (bf16[128,1280]{1,0:T(8,128)(2,1)S(1)}, bf16[128,1280]{1,0:T(8,128)(2,1)S(1)}, u32[]{:S(2)}, u32[]{:S(2)}) collective-permute-start(bf16[128,1280]{1,0:T(8,128)(2,1)S(1)} %convolution_convert_fusion.6), channel_id=1, source_target_pairs={{0,1},{1,0},{2,3},{3,2},{4,5},{5,4},{6,7},{7,6},{8,9},{9,8},{10,11... | collective-permute-start | bytes 983048 | tf_op jit(solution)/shard_map/ppermute | solution.py:90
  35.6 1.7 %collective-permute-start.8 = (bf16[128,1280]{1,0:T(8,128)(2,1)S(1)}, bf16[128,1280]{1,0:T(8,128)(2,1)S(1)}, u32[]{:S(2)}, u32[]{:S(2)}) collective-permute-start(bf16[128,1280]{1,0:T(8,128)(2,1)S(1)} %convolution_convert_fusion.4), channel_id=1, source_target_pairs={{0,1},{1,0},{2,3},{3,2},{4,5},{5,4},{6,7},{7,6},{8,9},{9,8},{10,11... | collective-permute-start | bytes 983048 | tf_op jit(solution)/shard_map/ppermute | solution.py:90
  39.3 4.8 %collective-permute-start.13 = (bf16[128,1280]{1,0:T(8,128)(2,1)S(1)}, bf16[128,1280]{1,0:T(8,128)(2,1)S(1)}, u32[]{:S(2)}, u32[]{:S(2)}) collective-permute-start(bf16[128,1280]{1,0:T(8,128)(2,1)S(1)} %convolution_convert_fusion.2), channel_id=1, source_target_pairs={{0,1},{1,0},{2,3},{3,2},{4,5},{5,4},{6,7},{7,6},{8,9},{9,8},{10,11... | collective-permute-start | bytes 983048 | tf_op jit(solution)/shard_map/ppermute | solution.py:90
  40.7 12.6 %collective-permute-start.4 = (bf16[128,1280]{1,0:T(8,128)(2,1)S(1)}, bf16[128,1280]{1,0:T(8,128)(2,1)S(1)}, u32[]{:S(2)}, u32[]{:S(2)}) collective-permute-start(bf16[128,1280]{1,0:T(8,128)(2,1)S(1)} %add_convert_fusion.2), channel_id=1, source_target_pairs={{0,12},{4,8},{8,4},{12,0},{1,13},{5,9},{9,5},{13,1},{2,14},{6,10},... | collective-permute-start | bytes 983048 | tf_op jit(solution)/shard_map/ppermute | solution.py:94
  43.0 29.9 %collective-permute-start.9 = (bf16[128,1280]{1,0:T(8,128)(2,1)S(1)}, bf16[128,1280]{1,0:T(8,128)(2,1)S(1)}, u32[]{:S(2)}, u32[]{:S(2)}) collective-permute-start(bf16[128,1280]{1,0:T(8,128)(2,1)S(1)} %add_convert_fusion.1), channel_id=1, source_target_pairs={{0,8},{4,12},{8,0},{12,4},{1,9},{5,13},{9,1},{13,5},{2,10},{6,14},... | collective-permute-start | bytes 983048 | tf_op jit(solution)/shard_map/ppermute | solution.py:94
  45.0 2.3 %copy-start.5 = (s32[128,1]{0,1:T(1,128)S(1)}, s32[128,1]{0,1:T(1,128)}, u32[]{:S(2)}) copy-start(s32[128,1]{0,1:T(1,128)} %param.8) | copy-start | bytes 1540
  46.1 26.8 %collective-permute-start.17 = (bf16[128,1280]{1,0:T(8,128)(2,1)S(1)}, bf16[128,1280]{1,0:T(8,128)(2,1)S(1)}, u32[]{:S(2)}, u32[]{:S(2)}) collective-permute-start(bf16[128,1280]{1,0:T(8,128)(2,1)S(1)} %convolution_convert_fusion), channel_id=1, source_target_pairs={{0,1},{1,0},{2,3},{3,2},{4,5},{5,4},{6,7},{7,6},{8,9},{9,8},{10,11... | collective-permute-start | bytes 983048 | tf_op jit(solution)/shard_map/ppermute | solution.py:90
  46.2 26.8 %collective-permute-start.14 = (bf16[128,1280]{1,0:T(8,128)(2,1)S(1)}, bf16[128,1280]{1,0:T(8,128)(2,1)S(1)}, u32[]{:S(2)}, u32[]{:S(2)}) collective-permute-start(bf16[128,1280]{1,0:T(8,128)(2,1)S(1)} %add_convert_fusion), channel_id=1, source_target_pairs={{0,4},{4,0},{8,12},{12,8},{1,5},{5,1},{9,13},{13,9},{2,6},{6,2},{1... | collective-permute-start | bytes 983048 | tf_op jit(solution)/shard_map/ppermute | solution.py:94
  73.3 5.8 %collective-permute-start.18 = (bf16[128,640]{1,0:T(8,128)(2,1)S(1)}, bf16[128,640]{1,0:T(8,128)(2,1)S(1)}, u32[]{:S(2)}, u32[]{:S(2)}) collective-permute-start(bf16[128,640]{1,0:T(8,128)(2,1)S(1)} %slice.15), channel_id=1, source_target_pairs={{0,2},{1,3},{2,0},{3,1},{4,6},{5,7},{6,4},{7,5},{8,10},{9,11},{10,... | collective-permute-start | bytes 491528 | tf_op jit(solution)/shard_map/ppermute | solution.py:98

commit v28 on v23

--- a/solution.py
+++ b/solution.py
@@ -70,7 +70,7 @@
     up_w = _slots(up_weight[0], t, width, 0)
     down_keep = _slots(down_weight[0], t, width, 1, _ORDER[:2])
     down_send = _slots(down_weight[0], t, width, 1, _ORDER[2:])
-    waves = [[k] for k in (n_expert - 1,) + tuple(range(1, n_expert - 1)) + (0,)] if n_expert > 1 else [[0]]
+    waves = [[k] for k in [1][:n_expert - 1] + list(range(n_expert - 1, 1, -1)) + [0]]
     total = None
     previous = None
     for wave in waves:

time: 63.1 us -> 65.6 us (1.040)
  starting transfers between devices: 20.3 us -> 23.1 us
    ppermute x3, waiting for transfers between devices: 6.87 us -> 9.18 us  [gathered(): lax.ppermute(part.astype(jnp.bfloat16), 'expert', _xor_pairs(n_expert, k))]
    ppermute x4, waiting for transfers between devices: 6.69 us -> 4.43 us  [gathered(): lax.ppermute(over_c[:, width:].astype(jnp.bfloat16), 'tensor', _xor_pairs...]
    ppermute x4, waiting for transfers between devices: 2.22 us -> 0.54 us  [gathered(): lax.ppermute(piece, 'tensor', _xor_pairs(n_tensor, 2))]
    ppermute x3, starting transfers between devices: 3.81 us -> 5.17 us  [gathered(): lax.ppermute(part.astype(jnp.bfloat16), 'expert', _xor_pairs(n_expert, k))]
    ppermute x3, waiting for transfers between devices: 2.69 us -> 4.04 us  [gathered(): lax.ppermute(scaled, 'expert', _xor_pairs(n_expert, k))]
    ppermute x4, starting transfers between devices: 4.01 us -> 5.15 us  [gathered(): lax.ppermute(over_c[:, width:].astype(jnp.bfloat16), 'tensor', _xor_pairs...]
  transfers between devices with their start and end apart: 22 -> 22, of which waited for: 9 -> 7; matrix products, arithmetic and copies ran while one was open for 31% -> 30% of each run, Pallas kernels for 0% -> 0%
where the time goes in v28:
time: 65.6 us; the launch traced here: 65.2 us
  starting transfers between devices  23.1 us (35%)
  waiting for transfers between devices  18.5 us (28%)
  other arithmetic  8.86 us (14%)
  matrix products  7.74 us (12%)
  local copies, waits for them, and re-layouts  6.68 us (10%)
    ppermute x3, waiting for transfers between devices, gathered(): lax.ppermute(part.astype(jnp.bfloat16), 'expert', _xor_pairs(n_expert, k))  9.18 us
    ppermute x3, starting transfers between devices, gathered(): lax.ppermute(scaled, 'expert', _xor_pairs(n_expert, k))  5.68 us
    ppermute x3, starting transfers between devices, gathered(): lax.ppermute(part.astype(jnp.bfloat16), 'expert', _xor_pairs(n_expert, k))  5.17 us
    ppermute x4, starting transfers between devices, gathered(): lax.ppermute(over_c[:, width:].astype(jnp.bfloat16), 'tensor', _xor_pairs...  5.15 us
    ppermute x4, starting transfers between devices, gathered(): lax.ppermute(piece, 'tensor', _xor_pairs(n_tensor, 2))  5.14 us
    ppermute x4, waiting for transfers between devices, gathered(): lax.ppermute(over_c[:, width:].astype(jnp.bfloat16), 'tensor', _xor_pairs...  4.43 us
    ppermute x3, waiting for transfers between devices, gathered(): lax.ppermute(scaled, 'expert', _xor_pairs(n_expert, k))  4.04 us
    concatenate x4, other arithmetic, gathered(): jnp.concatenate([piece, lax.ppermute(piece, 'tensor', _xor_pairs(n_tensor...  3.77 us
  transfers between devices with their start and end apart: 22, of which 7 were waited for; matrix products, arithmetic and copies ran while one was open for 30% of the time, Pallas kernels for 0%

profile of v28, /device:TPU:0, one launch (start us, length us, event | category | flops | bytes accessed | tf_op | source)
XLA Modules:
  0.0 65.2 jit_solution(15546433370240678203)
XLA Ops:
  0.0 1.0 %multiply_convert_fusion = bf16[128,640]{1,0:T(8,128)(2,1)S(1)} fusion(bf16[128,640]{1,0:T(8,128)(2,1)} %param.6, f32[128]{0:T(128)} %param.7), kind=kLoop, calls=%fused_computation.56 | loop fusion | flops 245760 | bytes 328192 | tf_op jit(solution)/shard_map/convert_element_type | solution.py:64
  1.0 3.1 %collective-permute-start = (bf16[128,640]{1,0:T(8,128)(2,1)S(1)}, bf16[128,640]{1,0:T(8,128)(2,1)}, u32[]{:S(2)}, u32[]{:S(2)}) collective-permute-start(bf16[128,640]{1,0:T(8,128)(2,1)S(1)} %multiply_convert_fusion), channel_id=1, source_target_pairs={{0,4},{4,0},{8,12},{12,8},{1,5},{5,1},{9,13},{13,9},{2,6},{6,2},{1... | collective-permute-start | bytes 491528 | tf_op jit(solution)/shard_map/ppermute | solution.py:66
  4.1 2.5 %collective-permute-start.6 = (bf16[128,640]{1,0:T(8,128)(2,1)S(1)}, bf16[128,640]{1,0:T(8,128)(2,1)}, u32[]{:S(2)}, u32[]{:S(2)}) collective-permute-start(bf16[128,640]{1,0:T(8,128)(2,1)S(1)} %multiply_convert_fusion), channel_id=1, source_target_pairs={{0,12},{4,8},{8,4},{12,0},{1,13},{5,9},{9,5},{13,1},{2,14},{6,10},... | collective-permute-start | bytes 491528 | tf_op jit(solution)/shard_map/ppermute | solution.py:66
  6.7 1.5 %collective-permute-start.18 = (bf16[128,640]{1,0:T(8,128)(2,1)S(1)}, bf16[128,640]{1,0:T(8,128)(2,1)}, u32[]{:S(2)}, u32[]{:S(2)}) collective-permute-start(bf16[128,640]{1,0:T(8,128)(2,1)S(1)} %multiply_convert_fusion), channel_id=1, source_target_pairs={{0,2},{1,3},{2,0},{3,1},{4,6},{5,7},{6,4},{7,5},{8,10},{9,11},{10,... | collective-permute-start | bytes 491528 | tf_op jit(solution)/shard_map/ppermute | solution.py:79
  8.2 2.0 %dynamic-slice_bitcast_fusion.11 = (bf16[640,512]{1,0:T(8,128)(2,1)S(1)}, bf16[640,512]{1,0:T(8,128)(2,1)S(1)}, bf16[640,512]{1,0:T(8,128)(2,1)S(1)}, bf16[640,512]{1,0:T(8,128)(2,1)S(1)}) fusion(bf16[1,2560,512]{2,1,0:T(8,128)(2,1)} %param.9, s32[]{:T(128)S(6)} %select_n.48, s32[]{:T(128)S(6)} %select_n.49, s32[]{:T(128)S(6)} %select_n.51, s32[]{:T(128)S(6)} %select_n.50), kind=kLoop, calls=%fused_computation.37 | loop fusion | bytes 5242896 | tf_op jit(solution)/shard_map/dynamic_slice | solution.py:55
  10.2 0.5 copy-done
  10.7 1.3 %dynamic-slice_bitcast_fusion.7 = (bf16[640,512]{1,0:T(8,128)(2,1)S(1)}, bf16[640,512]{1,0:T(8,128)(2,1)}, bf16[640,512]{1,0:T(8,128)(2,1)}, bf16[640,512]{1,0:T(8,128)(2,1)}) fusion(bf16[1,2560,512]{2,1,0:T(8,128)(2,1)S(1)} %copy-done, s32[]{:T(128)S(6)} %select_n.48, s32[]{:T(128)S(6)} %select_n.49, s32[]{:T(128)S(6)} %select_n.51, s32[]{:T(128)S(6)} %select_n.50), kind=kLoop, calls=%fused_computation.33 | loop fusion | bytes 5242896 | tf_op jit(solution)/shard_map/dynamic_slice | solution.py:55
  12.2 1.5 %copy-done.1 = bf16[1,512,2560]{2,1,0:T(8,128)(2,1)S(1)} copy-done((bf16[1,512,2560]{2,1,0:T(8,128)(2,1)S(1)}, bf16[1,512,2560]{2,1,0:T(8,128)(2,1)}, u32[]{:S(2)}) %copy-start.1) | copy-done | bytes 2621464
  14.0 0.6 collective-permute-start.1
  14.6 0.9 %pad_maximum_fusion.10 = bf16[128,1280]{1,0:T(8,128)(2,1)S(1)} fusion(bf16[128,640]{1,0:T(8,128)(2,1)} %collective-permute-done.18, bf16[128,640]{1,0:T(8,128)(2,1)S(1)} %multiply_convert_fusion), kind=kLoop, calls=%fused_computation.55 | loop fusion | flops 655360 | bytes 655360 | tf_op jit(solution)/shard_map/concatenate | solution.py:78
  15.7 1.6 %collective-permute-start.7 = (bf16[128,640]{1,0:T(8,128)(2,1)}, bf16[128,640]{1,0:T(8,128)(2,1)S(1)}, u32[]{:S(2)}, u32[]{:S(2)}) collective-permute-start(bf16[128,640]{1,0:T(8,128)(2,1)} %collective-permute-done.6), channel_id=1, source_target_pairs={{0,2},{1,3},{2,0},{3,1},{4,6},{5,7},{6,4},{7,5},{8,10},{9,11},{10,... | collective-permute-start | bytes 491528 | tf_op jit(solution)/shard_map/ppermute | solution.py:79
  17.2 4.0 %collective-permute-done.12 = bf16[128,640]{1,0:T(8,128)(2,1)} collective-permute-done((bf16[128,640]{1,0:T(8,128)(2,1)S(1)}, bf16[128,640]{1,0:T(8,128)(2,1)}, u32[]{:S(2)}, u32[]{:S(2)}) %collective-permute-start.12) | collective-permute-done | bytes 163872 | tf_op jit(solution)/shard_map/ppermute | solution.py:66
  21.2 1.5 %collective-permute-start.13 = (bf16[128,640]{1,0:T(8,128)(2,1)}, bf16[128,640]{1,0:T(8,128)(2,1)S(1)}, u32[]{:S(2)}, u32[]{:S(2)}) collective-permute-start(bf16[128,640]{1,0:T(8,128)(2,1)} %collective-permute-done.12), channel_id=1, source_target_pairs={{0,2},{1,3},{2,0},{3,1},{4,6},{5,7},{6,4},{7,5},{8,10},{9,11},{10,... | collective-permute-start | bytes 491528 | tf_op jit(solution)/shard_map/ppermute | solution.py:79
  22.7 0.9 %constant_dynamic-update-slice_fusion.2 = bf16[128,2560]{1,0:T(8,128)(2,1)S(1)} fusion(bf16[128,640]{1,0:T(8,128)(2,1)} %collective-permute-done), kind=kLoop, calls=%fused_computation.60 | loop fusion | bytes 327680
  23.7 0.9 %pad_maximum_fusion.7 = bf16[128,1280]{1,0:T(8,128)(2,1)S(1)} fusion(bf16[128,640]{1,0:T(8,128)(2,1)S(1)} %collective-permute-done.1, bf16[128,640]{1,0:T(8,128)(2,1)} %collective-permute-done), kind=kLoop, calls=%fused_computation.52 | loop fusion | flops 655360 | bytes 655360 | tf_op jit(solution)/shard_map/concatenate | solution.py:78
  24.7 0.9 %pad_maximum_fusion.8 = bf16[128,1280]{1,0:T(8,128)(2,1)S(1)} fusion(bf16[128,640]{1,0:T(8,128)(2,1)S(1)} %collective-permute-done.7, bf16[128,640]{1,0:T(8,128)(2,1)} %collective-permute-done.6), kind=kLoop, calls=%fused_computation.53 | loop fusion | flops 655360 | bytes 655360 | tf_op jit(solution)/shard_map/concatenate | solution.py:78
  25.7 0.6 collective-permute-start.8
  26.2 0.5 collective-permute-done.13
  26.8 0.9 %pad_maximum_fusion.9 = bf16[128,1280]{1,0:T(8,128)(2,1)S(1)} fusion(bf16[128,640]{1,0:T(8,128)(2,1)S(1)} %collective-permute-done.13, bf16[128,640]{1,0:T(8,128)(2,1)} %collective-permute-done.12), kind=kLoop, calls=%fused_computation.54 | loop fusion | flops 655360 | bytes 655360 | tf_op jit(solution)/shard_map/concatenate | solution.py:78
  27.9 0.5 fusion.11
  28.4 0.7 %multiply_convert_fusion.1 = bf16[128,512]{1,0:T(8,128)(2,1)S(1)} fusion(f32[128,512]{1,0:T(8,128)S(1)} %fusion.11, bf16[128,2560]{1,0:T(8,128)(2,1)S(1)} %constant_dynamic-update-slice_fusion, bf16[640,512]{1,0:T(8,128)(2,1)S(1)} %copy-done.3, bf16[640,512]{1,0:T(8,128)(2,1)S(1)} %copy-done.4, bf16[640,512]{1,0:T(8,128)(2,1)S(1)} %copy-done.2, ...), kind=kOutput, calls=%fused_computation.57 | convolution fusion | flops 346423296 | bytes 3670016 | tf_op jit(solution)/shard_map/dot_general | solution.py:85
  29.2 0.3 convolution_convert_fusion.6
  29.5 0.6 collective-permute-start.3
  30.1 1.0 %pad_maximum_fusion.4 = bf16[128,2560]{1,0:T(8,128)(2,1)S(1)} fusion(bf16[128,1280]{1,0:T(8,128)(2,1)S(1)} %collective-permute-done.8, bf16[128,640]{1,0:T(8,128)(2,1)S(1)} %collective-permute-done.7, bf16[128,640]{1,0:T(8,128)(2,1)} %collective-permute-done.6), kind=kLoop, calls=%fused_computation.19 | loop fusion | flops 1966080 | bytes 1310720 | tf_op jit(solution)/shard_map/concatenate | solution.py:80
  31.3 0.3 convert_add_fusion.3
  31.7 0.5 fusion.12
  32.2 0.7 %fusion.1 = bf16[128,512]{1,0:T(8,128)(2,1)S(1)} fusion(bf16[128,2560]{1,0:T(8,128)(2,1)S(1)} %pad_maximum_fusion.4, f32[128,512]{1,0:T(8,128)S(1)} %fusion.12, bf16[640,512]{1,0:T(8,128)(2,1)S(1)} %copy-done.3, bf16[640,512]{1,0:T(8,128)(2,1)S(1)} %copy-done.4, bf16[640,512]{1,0:T(8,128)(2,1)S(1)} %copy-done.2, bf16[640,512]{1,0:T(8,128)(2,1)S(1)} %get-tuple-element.15), kind=kOutput, calls=%fused_computation.16 | convolution fusion | flops 346423296 | bytes 3670016 | tf_op jit(solution)/shard_map/dot_general | solution.py:85
  33.3 0.4 collective-permute-start.9
  33.8 1.0 %pad_maximum_fusion.5 = bf16[128,2560]{1,0:T(8,128)(2,1)S(1)} fusion(bf16[128,1280]{1,0:T(8,128)(2,1)S(1)} %collective-permute-done.14, bf16[128,640]{1,0:T(8,128)(2,1)S(1)} %collective-permute-done.13, bf16[128,640]{1,0:T(8,128)(2,1)} %collective-permute-done.12), kind=kLoop, calls=%fused_computation.20 | loop fusion | flops 1966080 | bytes 1310720 | tf_op jit(solution)/shard_map/concatenate | solution.py:80
  34.7 1.6 %collective-permute-start.4 = (bf16[128,640]{1,0:T(8,128)(2,1)S(1)}, bf16[128,640]{1,0:T(8,128)(2,1)S(1)}, u32[]{:S(2)}, u32[]{:S(2)}) collective-permute-start(bf16[128,640]{1,0:T(8,128)(2,1)S(1)} %slice.67), channel_id=1, source_target_pairs={{0,2},{1,3},{2,0},{3,1},{4,6},{5,7},{6,4},{7,5},{8,10},{9,11},{10,... | collective-permute-start | bytes 491528 | tf_op jit(solution)/shard_map/ppermute | solution.py:92
  36.7 0.5 fusion.13
  37.2 0.7 %fusion.2 = bf16[128,512]{1,0:T(8,128)(2,1)S(1)} fusion(bf16[128,2560]{1,0:T(8,128)(2,1)S(1)} %pad_maximum_fusion.5, f32[128,512]{1,0:T(8,128)S(1)} %fusion.13, bf16[640,512]{1,0:T(8,128)(2,1)S(1)} %copy-done.3, bf16[640,512]{1,0:T(8,128)(2,1)S(1)} %copy-done.4, bf16[640,512]{1,0:T(8,128)(2,1)S(1)} %copy-done.2, bf16[640,512]{1,0:T(8,128)(2,1)S(1)} %get-tuple-element.15), kind=kOutput, calls=%fused_computation.17 | convolution fusion | flops 346423296 | bytes 3670016 | tf_op jit(solution)/shard_map/dot_general | solution.py:85
  37.9 0.3 convolution_convert_fusion.2
  38.4 1.0 %pad_maximum_fusion.6 = bf16[128,2560]{1,0:T(8,128)(2,1)S(1)} fusion(bf16[128,1280]{1,0:T(8,128)(2,1)S(1)} %collective-permute-done.19, bf16[128,640]{1,0:T(8,128)(2,1)} %collective-permute-done.18, bf16[128,640]{1,0:T(8,128)(2,1)S(1)} %multiply_convert_fusion), kind=kLoop, calls=%fused_computation.21 | loop fusion | flops 1966080 | bytes 1310720 | tf_op jit(solution)/shard_map/concatenate | solution.py:80
  39.3 1.7 %collective-permute-done.4 = bf16[128,640]{1,0:T(8,128)(2,1)S(1)} collective-permute-done((bf16[128,640]{1,0:T(8,128)(2,1)S(1)}, bf16[128,640]{1,0:T(8,128)(2,1)S(1)}, u32[]{:S(2)}, u32[]{:S(2)}) %collective-permute-start.4) | collective-permute-done | bytes 163872 | tf_op jit(solution)/shard_map/ppermute | solution.py:92
  41.1 1.7 %collective-permute-start.5 = (bf16[128,640]{1,0:T(8,128)(2,1)S(1)}, bf16[128,640]{1,0:T(8,128)(2,1)S(1)}, u32[]{:S(2)}, u32[]{:S(2)}) collective-permute-start(bf16[128,640]{1,0:T(8,128)(2,1)S(1)} %fusion.9), channel_id=1, source_target_pairs={{0,4},{4,0},{8,12},{12,8},{1,5},{5,1},{9,13},{13,9},{2,6},{6,2},{1... | collective-permute-start | bytes 491528 | tf_op jit(solution)/shard_map/ppermute | solution.py:97
  42.8 1.1 %collective-permute-start.10 = (bf16[128,640]{1,0:T(8,128)(2,1)S(1)}, bf16[128,640]{1,0:T(8,128)(2,1)S(1)}, u32[]{:S(2)}, u32[]{:S(2)}) collective-permute-start(bf16[128,640]{1,0:T(8,128)(2,1)S(1)} %slice.66), channel_id=1, source_target_pairs={{0,2},{1,3},{2,0},{3,1},{4,6},{5,7},{6,4},{7,5},{8,10},{9,11},{10,... | collective-permute-start | bytes 491528 | tf_op jit(solution)/shard_map/ppermute | solution.py:92
  43.9 0.3 convert_add_fusion.1
  44.3 1.1 %collective-permute-start.16 = (bf16[128,640]{1,0:T(8,128)(2,1)S(1)}, bf16[128,640]{1,0:T(8,128)(2,1)S(1)}, u32[]{:S(2)}, u32[]{:S(2)}) collective-permute-start(bf16[128,640]{1,0:T(8,128)(2,1)S(1)} %slice.65), channel_id=1, source_target_pairs={{0,2},{1,3},{2,0},{3,1},{4,6},{5,7},{6,4},{7,5},{8,10},{9,11},{10,... | collective-permute-start | bytes 491528 | tf_op jit(solution)/shard_map/ppermute | solution.py:92
  45.3 0.5 fusion.14
  45.9 0.7 %fusion.3 = bf16[128,512]{1,0:T(8,128)(2,1)S(1)} fusion(bf16[128,2560]{1,0:T(8,128)(2,1)S(1)} %pad_maximum_fusion.6, f32[128,512]{1,0:T(8,128)S(1)} %fusion.14, bf16[640,512]{1,0:T(8,128)(2,1)S(1)} %copy-done.3, bf16[640,512]{1,0:T(8,128)(2,1)S(1)} %copy-done.4, bf16[640,512]{1,0:T(8,128)(2,1)S(1)} %copy-done.2, bf16[640,512]{1,0:T(8,128)(2,1)S(1)} %get-tuple-element.15), kind=kOutput, calls=%fused_computation.18 | convolution fusion | flops 346423296 | bytes 3670016 | tf_op jit(solution)/shard_map/dot_general | solution.py:85
  47.0 2.7 %collective-permute-done.10 = bf16[128,640]{1,0:T(8,128)(2,1)S(1)} collective-permute-done((bf16[128,640]{1,0:T(8,128)(2,1)S(1)}, bf16[128,640]{1,0:T(8,128)(2,1)S(1)}, u32[]{:S(2)}, u32[]{:S(2)}) %collective-permute-start.10) | collective-permute-done | bytes 163872 | tf_op jit(solution)/shard_map/ppermute | solution.py:92
  49.8 2.6 %collective-permute-start.11 = (bf16[128,640]{1,0:T(8,128)(2,1)S(1)}, bf16[128,640]{1,0:T(8,128)(2,1)S(1)}, u32[]{:S(2)}, u32[]{:S(2)}) collective-permute-start(bf16[128,640]{1,0:T(8,128)(2,1)S(1)} %fusion.8), channel_id=1, source_target_pairs={{0,12},{4,8},{8,4},{12,0},{1,13},{5,9},{9,5},{13,1},{2,14},{6,10},... | collective-permute-start | bytes 491528 | tf_op jit(solution)/shard_map/ppermute | solution.py:97
  52.4 0.9 %collective-permute-start.17 = (bf16[128,640]{1,0:T(8,128)(2,1)S(1)}, bf16[128,640]{1,0:T(8,128)(2,1)S(1)}, u32[]{:S(2)}, u32[]{:S(2)}) collective-permute-start(bf16[128,640]{1,0:T(8,128)(2,1)S(1)} %fusion.7), channel_id=1, source_target_pairs={{0,8},{4,12},{8,0},{12,4},{1,9},{5,13},{9,1},{13,5},{2,10},{6,14},... | collective-permute-start | bytes 491528 | tf_op jit(solution)/shard_map/ppermute | solution.py:97
  53.7 1.4 %collective-permute-start.21 = (bf16[128,640]{1,0:T(8,128)(2,1)S(1)}, bf16[128,640]{1,0:T(8,128)(2,1)S(1)}, u32[]{:S(2)}, u32[]{:S(2)}) collective-permute-start(bf16[128,640]{1,0:T(8,128)(2,1)S(1)} %slice.64), channel_id=1, source_target_pairs={{0,2},{1,3},{2,0},{3,1},{4,6},{5,7},{6,4},{7,5},{8,10},{9,11},{10,... | collective-permute-start | bytes 491528 | tf_op jit(solution)/shard_map/ppermute | solution.py:92
  55.1 2.3 %collective-permute-done.11 = bf16[128,640]{1,0:T(8,128)(2,1)S(1)} collective-permute-done((bf16[128,640]{1,0:T(8,128)(2,1)S(1)}, bf16[128,640]{1,0:T(8,128)(2,1)S(1)}, u32[]{:S(2)}, u32[]{:S(2)}) %collective-permute-start.11) | collective-permute-done | bytes 163872 | tf_op jit(solution)/shard_map/ppermute | solution.py:97
  57.4 6.9 %collective-permute-done.17 = bf16[128,640]{1,0:T(8,128)(2,1)S(1)} collective-permute-done((bf16[128,640]{1,0:T(8,128)(2,1)S(1)}, bf16[128,640]{1,0:T(8,128)(2,1)S(1)}, u32[]{:S(2)}, u32[]{:S(2)}) %collective-permute-start.17) | collective-permute-done | bytes 163872 | tf_op jit(solution)/shard_map/ppermute | solution.py:97
  64.3 0.9 %fusion.6 = bf16[128,640]{1,0:T(8,128)(2,1)} fusion(f32[128,1280]{1,0:T(8,128)S(1)} %convert_add_fusion, bf16[128,640]{1,0:T(8,128)(2,1)S(1)} %collective-permute-done.21, bf16[128,640]{1,0:T(8,128)(2,1)S(1)} %collective-permute-done.17, bf16[128,640]{1,0:T(8,128)(2,1)S(1)} %collective-permute-done.11, bf16[128,640]{1,0:T(8,128)(2,1)S(1)} %collective-permute-done.5, ...), kind=kLoop, calls=%fused_computation.42 | loop fusion | flops 1064960 | bytes 1147392 | tf_op jit(solution)/shard_map/convert_element_type | solution.py:101
  (48 shorter events, 2.9 us)
Async XLA Ops:
  1.0 13.0 %collective-permute-start = (bf16[128,640]{1,0:T(8,128)(2,1)S(1)}, bf16[128,640]{1,0:T(8,128)(2,1)}, u32[]{:S(2)}, u32[]{:S(2)}) collective-permute-start(bf16[128,640]{1,0:T(8,128)(2,1)S(1)} %multiply_convert_fusion), channel_id=1, source_target_pairs={{0,4},{4,0},{8,12},{12,8},{1,5},{5,1},{9,13},{13,9},{2,6},{6,2},{1... | collective-permute-start | bytes 491528 | tf_op jit(solution)/shard_map/ppermute | solution.py:66
  4.1 11.5 %collective-permute-start.6 = (bf16[128,640]{1,0:T(8,128)(2,1)S(1)}, bf16[128,640]{1,0:T(8,128)(2,1)}, u32[]{:S(2)}, u32[]{:S(2)}) collective-permute-start(bf16[128,640]{1,0:T(8,128)(2,1)S(1)} %multiply_convert_fusion), channel_id=1, source_target_pairs={{0,12},{4,8},{8,4},{12,0},{1,13},{5,9},{9,5},{13,1},{2,14},{6,10},... | collective-permute-start | bytes 491528 | tf_op jit(solution)/shard_map/ppermute | solution.py:66
  6.6 14.7 %collective-permute-start.12 = (bf16[128,640]{1,0:T(8,128)(2,1)S(1)}, bf16[128,640]{1,0:T(8,128)(2,1)}, u32[]{:S(2)}, u32[]{:S(2)}) collective-permute-start(bf16[128,640]{1,0:T(8,128)(2,1)S(1)} %multiply_convert_fusion), channel_id=1, source_target_pairs={{0,8},{4,12},{8,0},{12,4},{1,9},{5,13},{9,1},{13,5},{2,10},{6,14},... | collective-permute-start | bytes 491528 | tf_op jit(solution)/shard_map/ppermute | solution.py:66
  6.7 7.9 %collective-permute-start.18 = (bf16[128,640]{1,0:T(8,128)(2,1)S(1)}, bf16[128,640]{1,0:T(8,128)(2,1)}, u32[]{:S(2)}, u32[]{:S(2)}) collective-permute-start(bf16[128,640]{1,0:T(8,128)(2,1)S(1)} %multiply_convert_fusion), channel_id=1, source_target_pairs={{0,2},{1,3},{2,0},{3,1},{4,6},{5,7},{6,4},{7,5},{8,10},{9,11},{10,... | collective-permute-start | bytes 491528 | tf_op jit(solution)/shard_map/ppermute | solution.py:79
  8.2 2.5 %copy-start = (bf16[1,2560,512]{2,1,0:T(8,128)(2,1)S(1)}, bf16[1,2560,512]{2,1,0:T(8,128)(2,1)}, u32[]{:S(2)}) copy-start(bf16[1,2560,512]{2,1,0:T(8,128)(2,1)} %param.10) | copy-start | bytes 7864324
  12.0 1.7 %copy-start.1 = (bf16[1,512,2560]{2,1,0:T(8,128)(2,1)S(1)}, bf16[1,512,2560]{2,1,0:T(8,128)(2,1)}, u32[]{:S(2)}) copy-start(bf16[1,512,2560]{2,1,0:T(8,128)(2,1)} %param.11) | copy-start | bytes 7864324
  14.0 9.7 %collective-permute-start.1 = (bf16[128,640]{1,0:T(8,128)(2,1)}, bf16[128,640]{1,0:T(8,128)(2,1)S(1)}, u32[]{:S(2)}, u32[]{:S(2)}) collective-permute-start(bf16[128,640]{1,0:T(8,128)(2,1)} %collective-permute-done), channel_id=1, source_target_pairs={{0,2},{1,3},{2,0},{3,1},{4,6},{5,7},{6,4},{7,5},{8,10},{9,11},{10,... | collective-permute-start | bytes 491528 | tf_op jit(solution)/shard_map/ppermute | solution.py:79
  15.6 22.8 %collective-permute-start.19 = (bf16[128,1280]{1,0:T(8,128)(2,1)S(1)}, bf16[128,1280]{1,0:T(8,128)(2,1)S(1)}, u32[]{:S(2)}, u32[]{:S(2)}) collective-permute-start(bf16[128,1280]{1,0:T(8,128)(2,1)S(1)} %pad_maximum_fusion.10), channel_id=1, source_target_pairs={{0,1},{1,0},{2,3},{3,2},{4,5},{5,4},{6,7},{7,6},{8,9},{9,8},{10,11... | collective-permute-start | bytes 983048 | tf_op jit(solution)/shard_map/ppermute | solution.py:81
  15.7 9.1 %collective-permute-start.7 = (bf16[128,640]{1,0:T(8,128)(2,1)}, bf16[128,640]{1,0:T(8,128)(2,1)S(1)}, u32[]{:S(2)}, u32[]{:S(2)}) collective-permute-start(bf16[128,640]{1,0:T(8,128)(2,1)} %collective-permute-done.6), channel_id=1, source_target_pairs={{0,2},{1,3},{2,0},{3,1},{4,6},{5,7},{6,4},{7,5},{8,10},{9,11},{10,... | collective-permute-start | bytes 491528 | tf_op jit(solution)/shard_map/ppermute | solution.py:79
  21.2 5.5 %collective-permute-start.13 = (bf16[128,640]{1,0:T(8,128)(2,1)}, bf16[128,640]{1,0:T(8,128)(2,1)S(1)}, u32[]{:S(2)}, u32[]{:S(2)}) collective-permute-start(bf16[128,640]{1,0:T(8,128)(2,1)} %collective-permute-done.12), channel_id=1, source_target_pairs={{0,2},{1,3},{2,0},{3,1},{4,6},{5,7},{6,4},{7,5},{8,10},{9,11},{10,... | collective-permute-start | bytes 491528 | tf_op jit(solution)/shard_map/ppermute | solution.py:79
  24.6 3.2 %collective-permute-start.2 = (bf16[128,1280]{1,0:T(8,128)(2,1)S(1)}, bf16[128,1280]{1,0:T(8,128)(2,1)S(1)}, u32[]{:S(2)}, u32[]{:S(2)}) collective-permute-start(bf16[128,1280]{1,0:T(8,128)(2,1)S(1)} %pad_maximum_fusion.7), channel_id=1, source_target_pairs={{0,1},{1,0},{2,3},{3,2},{4,5},{5,4},{6,7},{7,6},{8,9},{9,8},{10,11... | collective-permute-start | bytes 983048 | tf_op jit(solution)/shard_map/ppermute | solution.py:81
  25.7 2.7 %copy-start.2 = (bf16[640,512]{1,0:T(8,128)(2,1)S(1)}, bf16[640,512]{1,0:T(8,128)(2,1)}, u32[]{:S(2)}) copy-start(bf16[640,512]{1,0:T(8,128)(2,1)} %get-tuple-element.16) | copy-start | bytes 1966084
  25.7 2.7 %copy-start.3 = (bf16[640,512]{1,0:T(8,128)(2,1)S(1)}, bf16[640,512]{1,0:T(8,128)(2,1)}, u32[]{:S(2)}) copy-start(bf16[640,512]{1,0:T(8,128)(2,1)} %get-tuple-element.17) | copy-start | bytes 1966084
  25.7 2.7 %copy-start.4 = (bf16[640,512]{1,0:T(8,128)(2,1)S(1)}, bf16[640,512]{1,0:T(8,128)(2,1)}, u32[]{:S(2)}) copy-start(bf16[640,512]{1,0:T(8,128)(2,1)} %get-tuple-element.18) | copy-start | bytes 1966084
  25.7 4.4 %collective-permute-start.8 = (bf16[128,1280]{1,0:T(8,128)(2,1)S(1)}, bf16[128,1280]{1,0:T(8,128)(2,1)S(1)}, u32[]{:S(2)}, u32[]{:S(2)}) collective-permute-start(bf16[128,1280]{1,0:T(8,128)(2,1)S(1)} %pad_maximum_fusion.8), channel_id=1, source_target_pairs={{0,1},{1,0},{2,3},{3,2},{4,5},{5,4},{6,7},{7,6},{8,9},{9,8},{10,11... | collective-permute-start | bytes 983048 | tf_op jit(solution)/shard_map/ppermute | solution.py:81
  27.7 6.0 %collective-permute-start.14 = (bf16[128,1280]{1,0:T(8,128)(2,1)S(1)}, bf16[128,1280]{1,0:T(8,128)(2,1)S(1)}, u32[]{:S(2)}, u32[]{:S(2)}) collective-permute-start(bf16[128,1280]{1,0:T(8,128)(2,1)S(1)} %pad_maximum_fusion.9), channel_id=1, source_target_pairs={{0,1},{1,0},{2,3},{3,2},{4,5},{5,4},{6,7},{7,6},{8,9},{9,8},{10,11... | collective-permute-start | bytes 983048 | tf_op jit(solution)/shard_map/ppermute | solution.py:81
  29.5 1.8 %collective-permute-start.3 = (bf16[128,1280]{1,0:T(8,128)(2,1)S(1)}, bf16[128,1280]{1,0:T(8,128)(2,1)S(1)}, u32[]{:S(2)}, u32[]{:S(2)}) collective-permute-start(bf16[128,1280]{1,0:T(8,128)(2,1)S(1)} %convolution_convert_fusion.6), channel_id=1, source_target_pairs={{0,1},{1,0},{2,3},{3,2},{4,5},{5,4},{6,7},{7,6},{8,9},{9,8},{10,11... | collective-permute-start | bytes 983048 | tf_op jit(solution)/shard_map/ppermute | solution.py:90
  33.3 3.0 %collective-permute-start.9 = (bf16[128,1280]{1,0:T(8,128)(2,1)S(1)}, bf16[128,1280]{1,0:T(8,128)(2,1)S(1)}, u32[]{:S(2)}, u32[]{:S(2)}) collective-permute-start(bf16[128,1280]{1,0:T(8,128)(2,1)S(1)} %convolution_convert_fusion.4), channel_id=1, source_target_pairs={{0,1},{1,0},{2,3},{3,2},{4,5},{5,4},{6,7},{7,6},{8,9},{9,8},{10,11... | collective-permute-start | bytes 983048 | tf_op jit(solution)/shard_map/ppermute | solution.py:90
  34.7 6.3 %collective-permute-start.4 = (bf16[128,640]{1,0:T(8,128)(2,1)S(1)}, bf16[128,640]{1,0:T(8,128)(2,1)S(1)}, u32[]{:S(2)}, u32[]{:S(2)}) collective-permute-start(bf16[128,640]{1,0:T(8,128)(2,1)S(1)} %slice.67), channel_id=1, source_target_pairs={{0,2},{1,3},{2,0},{3,1},{4,6},{5,7},{6,4},{7,5},{8,10},{9,11},{10,... | collective-permute-start | bytes 491528 | tf_op jit(solution)/shard_map/ppermute | solution.py:92
  38.3 5.6 %collective-permute-start.15 = (bf16[128,1280]{1,0:T(8,128)(2,1)S(1)}, bf16[128,1280]{1,0:T(8,128)(2,1)S(1)}, u32[]{:S(2)}, u32[]{:S(2)}) collective-permute-start(bf16[128,1280]{1,0:T(8,128)(2,1)S(1)} %convolution_convert_fusion.2), channel_id=1, source_target_pairs={{0,1},{1,0},{2,3},{3,2},{4,5},{5,4},{6,7},{7,6},{8,9},{9,8},{10,11... | collective-permute-start | bytes 983048 | tf_op jit(solution)/shard_map/ppermute | solution.py:90
  41.1 14.1 %collective-permute-start.5 = (bf16[128,640]{1,0:T(8,128)(2,1)S(1)}, bf16[128,640]{1,0:T(8,128)(2,1)S(1)}, u32[]{:S(2)}, u32[]{:S(2)}) collective-permute-start(bf16[128,640]{1,0:T(8,128)(2,1)S(1)} %fusion.9), channel_id=1, source_target_pairs={{0,4},{4,0},{8,12},{12,8},{1,5},{5,1},{9,13},{13,9},{2,6},{6,2},{1... | collective-permute-start | bytes 491528 | tf_op jit(solution)/shard_map/ppermute | solution.py:97
  42.8 6.9 %collective-permute-start.10 = (bf16[128,640]{1,0:T(8,128)(2,1)S(1)}, bf16[128,640]{1,0:T(8,128)(2,1)S(1)}, u32[]{:S(2)}, u32[]{:S(2)}) collective-permute-start(bf16[128,640]{1,0:T(8,128)(2,1)S(1)} %slice.66), channel_id=1, source_target_pairs={{0,2},{1,3},{2,0},{3,1},{4,6},{5,7},{6,4},{7,5},{8,10},{9,11},{10,... | collective-permute-start | bytes 491528 | tf_op jit(solution)/shard_map/ppermute | solution.py:92
  44.3 8.1 %collective-permute-start.16 = (bf16[128,640]{1,0:T(8,128)(2,1)S(1)}, bf16[128,640]{1,0:T(8,128)(2,1)S(1)}, u32[]{:S(2)}, u32[]{:S(2)}) collective-permute-start(bf16[128,640]{1,0:T(8,128)(2,1)S(1)} %slice.65), channel_id=1, source_target_pairs={{0,2},{1,3},{2,0},{3,1},{4,6},{5,7},{6,4},{7,5},{8,10},{9,11},{10,... | collective-permute-start | bytes 491528 | tf_op jit(solution)/shard_map/ppermute | solution.py:92
  47.0 8.2 %copy-start.5 = (s32[128,1]{0,1:T(1,128)S(1)}, s32[128,1]{0,1:T(1,128)}, u32[]{:S(2)}) copy-start(s32[128,1]{0,1:T(1,128)} %param.8) | copy-start | bytes 1540
  47.0 6.3 %collective-permute-start.20 = (bf16[128,1280]{1,0:T(8,128)(2,1)S(1)}, bf16[128,1280]{1,0:T(8,128)(2,1)S(1)}, u32[]{:S(2)}, u32[]{:S(2)}) collective-permute-start(bf16[128,1280]{1,0:T(8,128)(2,1)S(1)} %convolution_convert_fusion), channel_id=1, source_target_pairs={{0,1},{1,0},{2,3},{3,2},{4,5},{5,4},{6,7},{7,6},{8,9},{9,8},{10,11... | collective-permute-start | bytes 983048 | tf_op jit(solution)/shard_map/ppermute | solution.py:90
  49.8 7.6 %collective-permute-start.11 = (bf16[128,640]{1,0:T(8,128)(2,1)S(1)}, bf16[128,640]{1,0:T(8,128)(2,1)S(1)}, u32[]{:S(2)}, u32[]{:S(2)}) collective-permute-start(bf16[128,640]{1,0:T(8,128)(2,1)S(1)} %fusion.8), channel_id=1, source_target_pairs={{0,12},{4,8},{8,4},{12,0},{1,13},{5,9},{9,5},{13,1},{2,14},{6,10},... | collective-permute-start | bytes 491528 | tf_op jit(solution)/shard_map/ppermute | solution.py:97
  52.4 11.9 %collective-permute-start.17 = (bf16[128,640]{1,0:T(8,128)(2,1)S(1)}, bf16[128,640]{1,0:T(8,128)(2,1)S(1)}, u32[]{:S(2)}, u32[]{:S(2)}) collective-permute-start(bf16[128,640]{1,0:T(8,128)(2,1)S(1)} %fusion.7), channel_id=1, source_target_pairs={{0,8},{4,12},{8,0},{12,4},{1,9},{5,13},{9,1},{13,5},{2,10},{6,14},... | collective-permute-start | bytes 491528 | tf_op jit(solution)/shard_map/ppermute | solution.py:97
  53.7 10.6 %collective-permute-start.21 = (bf16[128,640]{1,0:T(8,128)(2,1)S(1)}, bf16[128,640]{1,0:T(8,128)(2,1)S(1)}, u32[]{:S(2)}, u32[]{:S(2)}) collective-permute-start(bf16[128,640]{1,0:T(8,128)(2,1)S(1)} %slice.64), channel_id=1, source_target_pairs={{0,2},{1,3},{2,0},{3,1},{4,6},{5,7},{6,4},{7,5},{8,10},{9,11},{10,... | collective-permute-start | bytes 491528 | tf_op jit(solution)/shard_map/ppermute | solution.py:92

commit v29 on v28

--- a/solution.py
+++ b/solution.py
@@ -70,11 +70,14 @@
     up_w = _slots(up_weight[0], t, width, 0)
     down_keep = _slots(down_weight[0], t, width, 1, _ORDER[:2])
     down_send = _slots(down_weight[0], t, width, 1, _ORDER[2:])
-    waves = [[k] for k in [1][:n_expert - 1] + list(range(n_expert - 1, 1, -1)) + [0]]
+    half = tok_rows // 2 if tok_rows % 32 == 0 else tok_rows
+    waves = [(k, 0, tok_rows) for k in list(range(n_expert - 1, 1, -1)) + [1][:n_expert - 1]]
+    waves += [(0, lo, min(lo + half, tok_rows)) for lo in range(0, tok_rows, half)]
     total = None
     previous = None
-    for wave in waves:
-        piece = jnp.concatenate([blocks[k] for k in wave])
+    parts = [None] * len(waves)
+    for index, (k, lo, hi) in enumerate(waves):
+        piece = blocks[k][lo:hi]
         pair = jnp.concatenate(
             [piece, lax.ppermute(piece, "tensor", _xor_pairs(n_tensor, 2))], axis=1)
         rows = jnp.concatenate(
@@ -91,13 +94,16 @@
             send, "tensor", _xor_pairs(n_tensor, 1)).astype(jnp.float32)
         summed = over_c[:, :width] + lax.ppermute(
             over_c[:, width:].astype(jnp.bfloat16), "tensor", _xor_pairs(n_tensor, 2)).astype(jnp.float32)
-        for i, k in enumerate(wave):
-            part = summed[i * tok_rows:(i + 1) * tok_rows]
-            if k:
-                part = lax.ppermute(
-                    part.astype(jnp.bfloat16), "expert", _xor_pairs(n_expert, k)).astype(jnp.float32)
-            part = jnp.where(routed == (me ^ k) // SPAN, part, 0.0)
-            total = part if total is None else total + part
+        if k:
+            summed = lax.ppermute(
+                summed.astype(jnp.bfloat16), "expert", _xor_pairs(n_expert, k)).astype(jnp.float32)
+        summed = jnp.where(routed[lo:hi] == (me ^ k) // SPAN, summed, 0.0)
+        parts[index] = summed
+    full = [p for (k, lo, hi), p in zip(waves, parts) if hi - lo == tok_rows]
+    own = jnp.concatenate([p for (k, lo, hi), p in zip(waves, parts) if hi - lo < tok_rows] or [0.0 * full[0]])
+    total = own
+    for p in full:
+        total = total + p
     return total.astype(jnp.bfloat16)
 
 

time: 65.6 us -> 64.8 us (0.988)
  other arithmetic: 8.86 us -> 4.31 us
  waiting for transfers between devices: 18.5 us -> 21 us
  starting transfers between devices: 23.1 us -> 25.1 us
  local copies, waits for them, and re-layouts: 6.68 us -> 4.93 us
  matrix products: 7.74 us -> 8.8 us
    ppermute x3, waiting for transfers between devices: 9.18 us -> 0.01 us  [gathered(): lax.ppermute(summed.astype(jnp.bfloat16), 'expert', _xor_pairs(n_expert, k))]
    ppermute x4 -> x5, waiting for transfers between devices: 0.54 us -> 7.18 us  [gathered(): lax.ppermute(piece, 'tensor', _xor_pairs(n_tensor, 2))]
    ppermute x4 -> x5, waiting for transfers between devices: 4.43 us -> 10.5 us  [gathered(): lax.ppermute(over_c[:, width:].astype(jnp.bfloat16), 'tensor', _xor_pairs...]
    concatenate x4 -> x5, other arithmetic: 3.77 us -> 0.11 us  [gathered(): jnp.concatenate([piece, lax.ppermute(piece, 'tensor', _xor_pairs(n_tensor...]
    concatenate x3 -> x4, other arithmetic: 2.89 us -> 0.15 us  [gathered(): jnp.concatenate([pair, lax.ppermute(pair, 'tensor', _xor_pairs(n_tensor,...]
    ppermute x3, waiting for transfers between devices: 4.04 us -> 2.08 us  [gathered(): lax.ppermute(scaled, 'expert', _xor_pairs(n_expert, k))]
    ppermute x4 -> x5, starting transfers between devices: 5.15 us -> 6.98 us  [gathered(): lax.ppermute(over_c[:, width:].astype(jnp.bfloat16), 'tensor', _xor_pairs...]
    unnamed x14 -> x4, local copies, waits for them, and re-layouts: 3.03 us -> 1.54 us
  transfers between devices with their start and end apart: 22 -> 26, of which waited for: 7 -> 10; matrix products, arithmetic and copies ran while one was open for 30% -> 23% of each run, Pallas kernels for 0% -> 0%
where the time goes in v29:
time: 64.8 us; the launch traced here: 64.6 us
  starting transfers between devices  25.1 us (39%)
  waiting for transfers between devices  21 us (32%)
  matrix products  8.8 us (14%)
  local copies, waits for them, and re-layouts  4.93 us (8%)
  other arithmetic  4.31 us (7%)
    ppermute x5, waiting for transfers between devices, gathered(): lax.ppermute(over_c[:, width:].astype(jnp.bfloat16), 'tensor', _xor_pairs...  10.5 us
    ppermute x5, waiting for transfers between devices, gathered(): lax.ppermute(piece, 'tensor', _xor_pairs(n_tensor, 2))  7.18 us
    ppermute x5, starting transfers between devices, gathered(): lax.ppermute(over_c[:, width:].astype(jnp.bfloat16), 'tensor', _xor_pairs...  6.98 us
    ppermute x5, starting transfers between devices, gathered(): lax.ppermute(piece, 'tensor', _xor_pairs(n_tensor, 2))  5.77 us
    ppermute x3, starting transfers between devices, gathered(): lax.ppermute(scaled, 'expert', _xor_pairs(n_expert, k))  5.76 us
    ppermute x3, starting transfers between devices, gathered(): lax.ppermute(summed.astype(jnp.bfloat16), 'expert', _xor_pairs(n_expert, k))  4.6 us
    dynamic_slice x2, local copies, waits for them, and re-layouts, _slots(): lax.dynamic_slice_in_dim(weight, (t ^ k) * width, width, axis=axis)  3.27 us
    dot_general x5, matrix products, gathered(): up_act = jnp.dot(rows, up_w, preferred_element_type=jnp.float32)  2.68 us
  transfers between devices with their start and end apart: 26, of which 10 were waited for; matrix products, arithmetic and copies ran while one was open for 23% of the time, Pallas kernels for 0%

profile of v29, /device:TPU:0, one launch (start us, length us, event | category | flops | bytes accessed | tf_op | source)
XLA Modules:
  0.0 64.6 jit_solution(9308644167821763074)
XLA Ops:
  0.0 1.0 %multiply_convert_fusion = bf16[128,640]{1,0:T(8,128)(2,1)S(1)} fusion(bf16[128,640]{1,0:T(8,128)(2,1)} %param.6, f32[128]{0:T(128)} %param.7), kind=kLoop, calls=%fused_computation.60 | loop fusion | flops 245760 | bytes 328192 | tf_op jit(solution)/shard_map/convert_element_type | solution.py:64
  1.0 5.1 %collective-permute-start.8 = (bf16[128,640]{1,0:T(8,128)(2,1)S(1)}, bf16[128,640]{1,0:T(8,128)(2,1)S(1)}, u32[]{:S(2)}, u32[]{:S(2)}) collective-permute-start(bf16[128,640]{1,0:T(8,128)(2,1)S(1)} %multiply_convert_fusion), channel_id=1, source_target_pairs={{0,12},{4,8},{8,4},{12,0},{1,13},{5,9},{9,5},{13,1},{2,14},{6,10},... | collective-permute-start | bytes 491528 | tf_op jit(solution)/shard_map/ppermute | solution.py:66
  6.1 0.6 collective-permute-start.2
  6.8 1.7 %collective-permute-start = (bf16[64,640]{1,0:T(8,128)(2,1)S(1)}, bf16[64,640]{1,0:T(8,128)(2,1)S(1)}, u32[]{:S(2)}, u32[]{:S(2)}) collective-permute-start(bf16[64,640]{1,0:T(8,128)(2,1)S(1)} %get-tuple-element.25), channel_id=1, source_target_pairs={{0,2},{1,3},{2,0},{3,1},{4,6},{5,7},{6,4},{7,5},{8,10},{9,11},{10,... | collective-permute-start | bytes 245768 | tf_op jit(solution)/shard_map/ppermute | solution.py:82
  8.5 0.4 collective-permute-start.13
  8.9 0.8 %compare_bitcast_fusion.4 = (pred[64]{0:T(512)(128)(4,1)S(1)}, pred[64]{0:T(512)(128)(4,1)S(1)}) fusion(s32[128,1]{0,1:T(1,128)} %param.8, s32[]{:T(128)S(6)} %select_n.52), kind=kLoop, calls=%fused_computation.77 | loop fusion | flops 128 | bytes 644 | tf_op jit(solution)/shard_map/jit(_where)/broadcast_in_dim | solution.py:100
  9.7 0.7 %compare_bitcast_fusion.2 = (pred[128]{0:T(512)(128)(4,1)S(1)}, pred[128]{0:T(512)(128)(4,1)S(1)}, pred[128]{0:T(512)(128)(4,1)S(1)}) fusion(s32[128,1]{0,1:T(1,128)} %param.8, s32[]{:T(128)S(6)} %select_n.59, s32[]{:T(128)S(6)} %select_n.63, s32[]{:T(128)S(6)} %select_n.61), kind=kLoop, calls=%fused_computation.75 | loop fusion | flops 384 | bytes 908 | tf_op jit(solution)/shard_map/jit(_where)/broadcast_in_dim | solution.py:100
  10.3 3.0 %dynamic-slice_bitcast_fusion.7 = (bf16[640,512]{1,0:T(8,128)(2,1)S(1)}, bf16[640,512]{1,0:T(8,128)(2,1)S(1)}, bf16[640,512]{1,0:T(8,128)(2,1)S(1)}, bf16[640,51...) fusion(bf16[1,2560,512]{2,1,0:T(8,128)(2,1)} %param.10, ...), kind=kLoop, calls=%fused_computation.35 | loop fusion | bytes 10485776 | tf_op jit(solution)/shard_map/dynamic_slice | solution.py:55
  13.9 1.5 %copy-done = bf16[1,512,2560]{2,1,0:T(8,128)(2,1)S(1)} copy-done((bf16[1,512,2560]{2,1,0:T(8,128)(2,1)S(1)}, bf16[1,512,2560]{2,1,0:T(8,128)(2,1)}, u32[]{:S(2)}) %copy-start) | copy-done | bytes 2621464
  15.8 0.5 collective-permute-start.14
  16.3 1.6 %collective-permute-start.9 = (bf16[128,640]{1,0:T(8,128)(2,1)S(1)}, bf16[128,640]{1,0:T(8,128)(2,1)S(1)}, u32[]{:S(2)}, u32[]{:S(2)}) collective-permute-start(bf16[128,640]{1,0:T(8,128)(2,1)S(1)} %collective-permute-done.8), channel_id=1, source_target_pairs={{0,2},{1,3},{2,0},{3,1},{4,6},{5,7},{6,4},{7,5},{8,10},{9,11},{10,... | collective-permute-start | bytes 491528 | tf_op jit(solution)/shard_map/ppermute | solution.py:82
  17.9 2.1 %collective-permute-done.5 = bf16[128,640]{1,0:T(8,128)(2,1)S(1)} collective-permute-done((bf16[128,640]{1,0:T(8,128)(2,1)S(1)}, bf16[128,640]{1,0:T(8,128)(2,1)S(1)}, u32[]{:S(2)}, u32[]{:S(2)}) %collective-permute-start.5) | collective-permute-done | bytes 163872 | tf_op jit(solution)/shard_map/ppermute | solution.py:66
  20.0 1.5 %collective-permute-start.6 = (bf16[128,640]{1,0:T(8,128)(2,1)S(1)}, bf16[128,640]{1,0:T(8,128)(2,1)S(1)}, u32[]{:S(2)}, u32[]{:S(2)}) collective-permute-start(bf16[128,640]{1,0:T(8,128)(2,1)S(1)} %collective-permute-done.5), channel_id=1, source_target_pairs={{0,2},{1,3},{2,0},{3,1},{4,6},{5,7},{6,4},{7,5},{8,10},{9,11},{10,... | collective-permute-start | bytes 491528 | tf_op jit(solution)/shard_map/ppermute | solution.py:82
  21.5 0.5 collective-permute-start.3
  22.1 1.0 %collective-permute-done.9 = bf16[128,640]{1,0:T(8,128)(2,1)S(1)} collective-permute-done((bf16[128,640]{1,0:T(8,128)(2,1)S(1)}, bf16[128,640]{1,0:T(8,128)(2,1)S(1)}, u32[]{:S(2)}, u32[]{:S(2)}) %collective-permute-start.9) | collective-permute-done | bytes 163872 | tf_op jit(solution)/shard_map/ppermute | solution.py:82
  23.3 3.9 %collective-permute-done.6 = bf16[128,640]{1,0:T(8,128)(2,1)S(1)} collective-permute-done((bf16[128,640]{1,0:T(8,128)(2,1)S(1)}, bf16[128,640]{1,0:T(8,128)(2,1)S(1)}, u32[]{:S(2)}, u32[]{:S(2)}) %collective-permute-start.6) | collective-permute-done | bytes 163872 | tf_op jit(solution)/shard_map/ppermute | solution.py:82
  27.3 2.2 %collective-permute-done.3 = bf16[128,640]{1,0:T(8,128)(2,1)S(1)} collective-permute-done((bf16[128,640]{1,0:T(8,128)(2,1)S(1)}, bf16[128,640]{1,0:T(8,128)(2,1)S(1)}, u32[]{:S(2)}, u32[]{:S(2)}) %collective-permute-start.3) | collective-permute-done | bytes 163872 | tf_op jit(solution)/shard_map/ppermute | solution.py:82
  29.7 0.5 fusion.14
  30.2 0.5 multiply_convert_fusion.1
  31.1 0.6 collective-permute-start.17
  31.7 1.2 %collective-permute-done.17 = bf16[128,1280]{1,0:T(8,128)(2,1)S(1)} collective-permute-done((bf16[128,1280]{1,0:T(8,128)(2,1)S(1)}, bf16[128,1280]{1,0:T(8,128)(2,1)S(1)}, u32[]{:S(2)}, u32[]{:S(2)}) %collective-permute-start.17) | collective-permute-done | bytes 327712 | tf_op jit(solution)/shard_map/ppermute | solution.py:93
  33.2 0.5 fusion.15
  33.8 0.5 fusion.1
  34.3 0.4 convolution_convert_fusion.1
  34.6 0.4 collective-permute-start.20
  35.2 1.7 %collective-permute-start.18 = (bf16[128,640]{1,0:T(8,128)(2,1)S(1)}, bf16[128,640]{1,0:T(8,128)(2,1)S(1)}, u32[]{:S(2)}, u32[]{:S(2)}) collective-permute-start(bf16[128,640]{1,0:T(8,128)(2,1)S(1)} %slice.97), channel_id=1, source_target_pairs={{0,2},{1,3},{2,0},{3,1},{4,6},{5,7},{6,4},{7,5},{8,10},{9,11},{10,... | collective-permute-start | bytes 491528 | tf_op jit(solution)/shard_map/ppermute | solution.py:95
  37.2 0.5 fusion.16
  37.7 0.5 fusion.2
  38.7 2.7 %collective-permute-done.18 = bf16[128,640]{1,0:T(8,128)(2,1)S(1)} collective-permute-done((bf16[128,640]{1,0:T(8,128)(2,1)S(1)}, bf16[128,640]{1,0:T(8,128)(2,1)S(1)}, u32[]{:S(2)}, u32[]{:S(2)}) %collective-permute-start.18) | collective-permute-done | bytes 163872 | tf_op jit(solution)/shard_map/ppermute | solution.py:95
  41.5 3.8 %collective-permute-start.19 = (bf16[128,640]{1,0:T(8,128)(2,1)S(1)}, bf16[128,640]{1,0:T(8,128)(2,1)S(1)}, u32[]{:S(2)}, u32[]{:S(2)}) collective-permute-start(bf16[128,640]{1,0:T(8,128)(2,1)S(1)} %fusion.7), channel_id=1, source_target_pairs={{0,12},{4,8},{8,4},{12,0},{1,13},{5,9},{9,5},{13,1},{2,14},{6,10},... | collective-permute-start | bytes 491528 | tf_op jit(solution)/shard_map/ppermute | solution.py:98
  45.3 1.6 %collective-permute-start.21 = (bf16[128,640]{1,0:T(8,128)(2,1)S(1)}, bf16[128,640]{1,0:T(8,128)(2,1)S(1)}, u32[]{:S(2)}, u32[]{:S(2)}) collective-permute-start(bf16[128,640]{1,0:T(8,128)(2,1)S(1)} %slice.96), channel_id=1, source_target_pairs={{0,2},{1,3},{2,0},{3,1},{4,6},{5,7},{6,4},{7,5},{8,10},{9,11},{10,... | collective-permute-start | bytes 491528 | tf_op jit(solution)/shard_map/ppermute | solution.py:95
  47.3 0.6 fusion.17
  47.8 0.6 fusion.3
  48.4 0.4 convolution_convert_fusion.8
  48.8 1.9 %collective-permute-done.21 = bf16[128,640]{1,0:T(8,128)(2,1)S(1)} collective-permute-done((bf16[128,640]{1,0:T(8,128)(2,1)S(1)}, bf16[128,640]{1,0:T(8,128)(2,1)S(1)}, u32[]{:S(2)}, u32[]{:S(2)}) %collective-permute-start.21) | collective-permute-done | bytes 163872 | tf_op jit(solution)/shard_map/ppermute | solution.py:95
  50.9 1.6 %collective-permute-start.24 = (bf16[128,640]{1,0:T(8,128)(2,1)S(1)}, bf16[128,640]{1,0:T(8,128)(2,1)S(1)}, u32[]{:S(2)}, u32[]{:S(2)}) collective-permute-start(bf16[128,640]{1,0:T(8,128)(2,1)S(1)} %slice.95), channel_id=1, source_target_pairs={{0,2},{1,3},{2,0},{3,1},{4,6},{5,7},{6,4},{7,5},{8,10},{9,11},{10,... | collective-permute-start | bytes 491528 | tf_op jit(solution)/shard_map/ppermute | solution.py:95
  52.4 0.4 convert_add_fusion.4
  52.8 0.6 fusion.18
  53.4 0.6 fusion.4
  53.9 0.4 convolution_convert_fusion.6
  54.4 1.9 %collective-permute-done.24 = bf16[128,640]{1,0:T(8,128)(2,1)S(1)} collective-permute-done((bf16[128,640]{1,0:T(8,128)(2,1)S(1)}, bf16[128,640]{1,0:T(8,128)(2,1)S(1)}, u32[]{:S(2)}, u32[]{:S(2)}) %collective-permute-start.24) | collective-permute-done | bytes 163872 | tf_op jit(solution)/shard_map/ppermute | solution.py:95
  56.3 0.7 %collective-permute-start.25 = (bf16[128,640]{1,0:T(8,128)(2,1)S(1)}, bf16[128,640]{1,0:T(8,128)(2,1)S(1)}, u32[]{:S(2)}, u32[]{:S(2)}) collective-permute-start(bf16[128,640]{1,0:T(8,128)(2,1)S(1)} %fusion.5), channel_id=1, source_target_pairs={{0,4},{4,0},{8,12},{12,8},{1,5},{5,1},{9,13},{13,9},{2,6},{6,2},{1... | collective-permute-start | bytes 491528 | tf_op jit(solution)/shard_map/ppermute | solution.py:98
  57.0 1.7 %collective-permute-start.12 = (bf16[64,640]{1,0:T(8,128)(2,1)S(1)}, bf16[64,640]{1,0:T(8,128)(2,1)S(1)}, u32[]{:S(2)}, u32[]{:S(2)}) collective-permute-start(bf16[64,640]{1,0:T(8,128)(2,1)S(1)} %slice.99), channel_id=1, source_target_pairs={{0,2},{1,3},{2,0},{3,1},{4,6},{5,7},{6,4},{7,5},{8,10},{9,11},{10,... | collective-permute-start | bytes 245768 | tf_op jit(solution)/shard_map/ppermute | solution.py:95
  58.7 0.4 convert_add_fusion.3
  59.1 0.5 collective-permute-start.16
  59.6 2.0 %collective-permute-done.12 = bf16[64,640]{1,0:T(8,128)(2,1)S(1)} collective-permute-done((bf16[64,640]{1,0:T(8,128)(2,1)S(1)}, bf16[64,640]{1,0:T(8,128)(2,1)S(1)}, u32[]{:S(2)}, u32[]{:S(2)}) %collective-permute-start.12) | collective-permute-done | bytes 81952 | tf_op jit(solution)/shard_map/ppermute | solution.py:95
  61.6 2.0 %collective-permute-done.16 = bf16[64,640]{1,0:T(8,128)(2,1)S(1)} collective-permute-done((bf16[64,640]{1,0:T(8,128)(2,1)S(1)}, bf16[64,640]{1,0:T(8,128)(2,1)S(1)}, u32[]{:S(2)}, u32[]{:S(2)}) %collective-permute-start.16) | collective-permute-done | bytes 81952 | tf_op jit(solution)/shard_map/ppermute | solution.py:95
  63.7 0.9 %fusion.10 = bf16[128,640]{1,0:T(8,128)(2,1)} fusion(f32[64,640]{1,0:T(8,128)S(1)} %fusion.11, f32[64,640]{1,0:T(8,128)S(1)} %fusion.12, bf16[128,640]{1,0:T(8,128)(2,1)S(1)} %collective-permute-done.25, bf16[128,640]{1,0:T(8,128)(2,1)S(1)} %collective-permute-done.22, bf16[128,640]{1,0:T(8,128)(2,1)S(1)} %collective-permute-done.19, ...), kind=kLoop, calls=%fused_computation.57 | loop fusion | flops 901120 | bytes 983424 | tf_op jit(solution)/shard_map/convert_element_type | solution.py:107
  (57 shorter events, 3.7 us)
Async XLA Ops:
  1.0 15.3 %collective-permute-start.8 = (bf16[128,640]{1,0:T(8,128)(2,1)S(1)}, bf16[128,640]{1,0:T(8,128)(2,1)S(1)}, u32[]{:S(2)}, u32[]{:S(2)}) collective-permute-start(bf16[128,640]{1,0:T(8,128)(2,1)S(1)} %multiply_convert_fusion), channel_id=1, source_target_pairs={{0,12},{4,8},{8,4},{12,0},{1,13},{5,9},{9,5},{13,1},{2,14},{6,10},... | collective-permute-start | bytes 491528 | tf_op jit(solution)/shard_map/ppermute | solution.py:66
  6.1 13.9 %collective-permute-start.5 = (bf16[128,640]{1,0:T(8,128)(2,1)S(1)}, bf16[128,640]{1,0:T(8,128)(2,1)S(1)}, u32[]{:S(2)}, u32[]{:S(2)}) collective-permute-start(bf16[128,640]{1,0:T(8,128)(2,1)S(1)} %multiply_convert_fusion), channel_id=1, source_target_pairs={{0,8},{4,12},{8,0},{12,4},{1,9},{5,13},{9,1},{13,5},{2,10},{6,14},... | collective-permute-start | bytes 491528 | tf_op jit(solution)/shard_map/ppermute | solution.py:66
  6.1 15.4 %collective-permute-start.2 = (bf16[128,640]{1,0:T(8,128)(2,1)S(1)}, bf16[128,640]{1,0:T(8,128)(2,1)S(1)}, u32[]{:S(2)}, u32[]{:S(2)}) collective-permute-start(bf16[128,640]{1,0:T(8,128)(2,1)S(1)} %multiply_convert_fusion), channel_id=1, source_target_pairs={{0,4},{4,0},{8,12},{12,8},{1,5},{5,1},{9,13},{13,9},{2,6},{6,2},{1... | collective-permute-start | bytes 491528 | tf_op jit(solution)/shard_map/ppermute | solution.py:66
  6.8 8.8 %collective-permute-start = (bf16[64,640]{1,0:T(8,128)(2,1)S(1)}, bf16[64,640]{1,0:T(8,128)(2,1)S(1)}, u32[]{:S(2)}, u32[]{:S(2)}) collective-permute-start(bf16[64,640]{1,0:T(8,128)(2,1)S(1)} %get-tuple-element.25), channel_id=1, source_target_pairs={{0,2},{1,3},{2,0},{3,1},{4,6},{5,7},{6,4},{7,5},{8,10},{9,11},{10,... | collective-permute-start | bytes 245768 | tf_op jit(solution)/shard_map/ppermute | solution.py:82
  8.5 7.2 %collective-permute-start.13 = (bf16[64,640]{1,0:T(8,128)(2,1)S(1)}, bf16[64,640]{1,0:T(8,128)(2,1)S(1)}, u32[]{:S(2)}, u32[]{:S(2)}) collective-permute-start(bf16[64,640]{1,0:T(8,128)(2,1)S(1)} %get-tuple-element.26), channel_id=1, source_target_pairs={{0,2},{1,3},{2,0},{3,1},{4,6},{5,7},{6,4},{7,5},{8,10},{9,11},{10,... | collective-permute-start | bytes 245768 | tf_op jit(solution)/shard_map/ppermute | solution.py:82
  13.6 1.7 %copy-start = (bf16[1,512,2560]{2,1,0:T(8,128)(2,1)S(1)}, bf16[1,512,2560]{2,1,0:T(8,128)(2,1)}, u32[]{:S(2)}) copy-start(bf16[1,512,2560]{2,1,0:T(8,128)(2,1)} %param.11) | copy-start | bytes 7864324
  15.6 6.4 %collective-permute-start.1 = (bf16[64,1280]{1,0:T(8,128)(2,1)S(1)}, bf16[64,1280]{1,0:T(8,128)(2,1)S(1)}, u32[]{:S(2)}, u32[]{:S(2)}) collective-permute-start(bf16[64,1280]{1,0:T(8,128)(2,1)S(1)} %pad_maximum_fusion.11), channel_id=1, source_target_pairs={{0,1},{1,0},{2,3},{3,2},{4,5},{5,4},{6,7},{7,6},{8,9},{9,8},{10,11... | collective-permute-start | bytes 491528 | tf_op jit(solution)/shard_map/ppermute | solution.py:84
  15.8 22.9 %collective-permute-start.14 = (bf16[64,1280]{1,0:T(8,128)(2,1)S(1)}, bf16[64,1280]{1,0:T(8,128)(2,1)S(1)}, u32[]{:S(2)}, u32[]{:S(2)}) collective-permute-start(bf16[64,1280]{1,0:T(8,128)(2,1)S(1)} %pad_maximum_fusion.12), channel_id=1, source_target_pairs={{0,1},{1,0},{2,3},{3,2},{4,5},{5,4},{6,7},{7,6},{8,9},{9,8},{10,11... | collective-permute-start | bytes 491528 | tf_op jit(solution)/shard_map/ppermute | solution.py:84
  16.3 6.9 %collective-permute-start.9 = (bf16[128,640]{1,0:T(8,128)(2,1)S(1)}, bf16[128,640]{1,0:T(8,128)(2,1)S(1)}, u32[]{:S(2)}, u32[]{:S(2)}) collective-permute-start(bf16[128,640]{1,0:T(8,128)(2,1)S(1)} %collective-permute-done.8), channel_id=1, source_target_pairs={{0,2},{1,3},{2,0},{3,1},{4,6},{5,7},{6,4},{7,5},{8,10},{9,11},{10,... | collective-permute-start | bytes 491528 | tf_op jit(solution)/shard_map/ppermute | solution.py:82
  20.0 7.1 %collective-permute-start.6 = (bf16[128,640]{1,0:T(8,128)(2,1)S(1)}, bf16[128,640]{1,0:T(8,128)(2,1)S(1)}, u32[]{:S(2)}, u32[]{:S(2)}) collective-permute-start(bf16[128,640]{1,0:T(8,128)(2,1)S(1)} %collective-permute-done.5), channel_id=1, source_target_pairs={{0,2},{1,3},{2,0},{3,1},{4,6},{5,7},{6,4},{7,5},{8,10},{9,11},{10,... | collective-permute-start | bytes 491528 | tf_op jit(solution)/shard_map/ppermute | solution.py:82
  21.5 8.0 %collective-permute-start.3 = (bf16[128,640]{1,0:T(8,128)(2,1)S(1)}, bf16[128,640]{1,0:T(8,128)(2,1)S(1)}, u32[]{:S(2)}, u32[]{:S(2)}) collective-permute-start(bf16[128,640]{1,0:T(8,128)(2,1)S(1)} %collective-permute-done.2), channel_id=1, source_target_pairs={{0,2},{1,3},{2,0},{3,1},{4,6},{5,7},{6,4},{7,5},{8,10},{9,11},{10,... | collective-permute-start | bytes 491528 | tf_op jit(solution)/shard_map/ppermute | solution.py:82
  23.2 6.5 %collective-permute-start.10 = (bf16[128,1280]{1,0:T(8,128)(2,1)S(1)}, bf16[128,1280]{1,0:T(8,128)(2,1)S(1)}, u32[]{:S(2)}, u32[]{:S(2)}) collective-permute-start(bf16[128,1280]{1,0:T(8,128)(2,1)S(1)} %pad_maximum_fusion.9), channel_id=1, source_target_pairs={{0,1},{1,0},{2,3},{3,2},{4,5},{5,4},{6,7},{7,6},{8,9},{9,8},{10,11... | collective-permute-start | bytes 983048 | tf_op jit(solution)/shard_map/ppermute | solution.py:84
  27.2 4.4 %collective-permute-start.7 = (bf16[128,1280]{1,0:T(8,128)(2,1)S(1)}, bf16[128,1280]{1,0:T(8,128)(2,1)S(1)}, u32[]{:S(2)}, u32[]{:S(2)}) collective-permute-start(bf16[128,1280]{1,0:T(8,128)(2,1)S(1)} %pad_maximum_fusion.8), channel_id=1, source_target_pairs={{0,1},{1,0},{2,3},{3,2},{4,5},{5,4},{6,7},{7,6},{8,9},{9,8},{10,11... | collective-permute-start | bytes 983048 | tf_op jit(solution)/shard_map/ppermute | solution.py:84
  29.5 5.5 %collective-permute-start.4 = (bf16[128,1280]{1,0:T(8,128)(2,1)S(1)}, bf16[128,1280]{1,0:T(8,128)(2,1)S(1)}, u32[]{:S(2)}, u32[]{:S(2)}) collective-permute-start(bf16[128,1280]{1,0:T(8,128)(2,1)S(1)} %pad_maximum_fusion.7), channel_id=1, source_target_pairs={{0,1},{1,0},{2,3},{3,2},{4,5},{5,4},{6,7},{7,6},{8,9},{9,8},{10,11... | collective-permute-start | bytes 983048 | tf_op jit(solution)/shard_map/ppermute | solution.py:84
  31.1 1.8 %collective-permute-start.17 = (bf16[128,1280]{1,0:T(8,128)(2,1)S(1)}, bf16[128,1280]{1,0:T(8,128)(2,1)S(1)}, u32[]{:S(2)}, u32[]{:S(2)}) collective-permute-start(bf16[128,1280]{1,0:T(8,128)(2,1)S(1)} %convolution_convert_fusion.2), channel_id=1, source_target_pairs={{0,1},{1,0},{2,3},{3,2},{4,5},{5,4},{6,7},{7,6},{8,9},{9,8},{10,11... | collective-permute-start | bytes 983048 | tf_op jit(solution)/shard_map/ppermute | solution.py:93
  34.6 2.2 %collective-permute-start.20 = (bf16[128,1280]{1,0:T(8,128)(2,1)S(1)}, bf16[128,1280]{1,0:T(8,128)(2,1)S(1)}, u32[]{:S(2)}, u32[]{:S(2)}) collective-permute-start(bf16[128,1280]{1,0:T(8,128)(2,1)S(1)} %convolution_convert_fusion.1), channel_id=1, source_target_pairs={{0,1},{1,0},{2,3},{3,2},{4,5},{5,4},{6,7},{7,6},{8,9},{9,8},{10,11... | collective-permute-start | bytes 983048 | tf_op jit(solution)/shard_map/ppermute | solution.py:93
  35.2 6.3 %collective-permute-start.18 = (bf16[128,640]{1,0:T(8,128)(2,1)S(1)}, bf16[128,640]{1,0:T(8,128)(2,1)S(1)}, u32[]{:S(2)}, u32[]{:S(2)}) collective-permute-start(bf16[128,640]{1,0:T(8,128)(2,1)S(1)} %slice.97), channel_id=1, source_target_pairs={{0,2},{1,3},{2,0},{3,1},{4,6},{5,7},{6,4},{7,5},{8,10},{9,11},{10,... | collective-permute-start | bytes 491528 | tf_op jit(solution)/shard_map/ppermute | solution.py:95
  38.6 8.3 %collective-permute-start.23 = (bf16[128,1280]{1,0:T(8,128)(2,1)S(1)}, bf16[128,1280]{1,0:T(8,128)(2,1)S(1)}, u32[]{:S(2)}, u32[]{:S(2)}) collective-permute-start(bf16[128,1280]{1,0:T(8,128)(2,1)S(1)} %convolution_convert_fusion), channel_id=1, source_target_pairs={{0,1},{1,0},{2,3},{3,2},{4,5},{5,4},{6,7},{7,6},{8,9},{9,8},{10,11... | collective-permute-start | bytes 983048 | tf_op jit(solution)/shard_map/ppermute | solution.py:93
  41.5 22.2 %collective-permute-start.19 = (bf16[128,640]{1,0:T(8,128)(2,1)S(1)}, bf16[128,640]{1,0:T(8,128)(2,1)S(1)}, u32[]{:S(2)}, u32[]{:S(2)}) collective-permute-start(bf16[128,640]{1,0:T(8,128)(2,1)S(1)} %fusion.7), channel_id=1, source_target_pairs={{0,12},{4,8},{8,4},{12,0},{1,13},{5,9},{9,5},{13,1},{2,14},{6,10},... | collective-permute-start | bytes 491528 | tf_op jit(solution)/shard_map/ppermute | solution.py:98
  45.3 5.4 %collective-permute-start.21 = (bf16[128,640]{1,0:T(8,128)(2,1)S(1)}, bf16[128,640]{1,0:T(8,128)(2,1)S(1)}, u32[]{:S(2)}, u32[]{:S(2)}) collective-permute-start(bf16[128,640]{1,0:T(8,128)(2,1)S(1)} %slice.96), channel_id=1, source_target_pairs={{0,2},{1,3},{2,0},{3,1},{4,6},{5,7},{6,4},{7,5},{8,10},{9,11},{10,... | collective-permute-start | bytes 491528 | tf_op jit(solution)/shard_map/ppermute | solution.py:95
  48.8 3.7 %collective-permute-start.11 = (bf16[64,1280]{1,0:T(8,128)(2,1)S(1)}, bf16[64,1280]{1,0:T(8,128)(2,1)S(1)}, u32[]{:S(2)}, u32[]{:S(2)}) collective-permute-start(bf16[64,1280]{1,0:T(8,128)(2,1)S(1)} %convolution_convert_fusion.8), channel_id=1, source_target_pairs={{0,1},{1,0},{2,3},{3,2},{4,5},{5,4},{6,7},{7,6},{8,9},{9,8},{10,11... | collective-permute-start | bytes 491528 | tf_op jit(solution)/shard_map/ppermute | solution.py:93
  50.8 12.9 %collective-permute-start.22 = (bf16[128,640]{1,0:T(8,128)(2,1)S(1)}, bf16[128,640]{1,0:T(8,128)(2,1)S(1)}, u32[]{:S(2)}, u32[]{:S(2)}) collective-permute-start(bf16[128,640]{1,0:T(8,128)(2,1)S(1)} %fusion.6), channel_id=1, source_target_pairs={{0,8},{4,12},{8,0},{12,4},{1,9},{5,13},{9,1},{13,5},{2,10},{6,14},... | collective-permute-start | bytes 491528 | tf_op jit(solution)/shard_map/ppermute | solution.py:98
  50.9 5.4 %collective-permute-start.24 = (bf16[128,640]{1,0:T(8,128)(2,1)S(1)}, bf16[128,640]{1,0:T(8,128)(2,1)S(1)}, u32[]{:S(2)}, u32[]{:S(2)}) collective-permute-start(bf16[128,640]{1,0:T(8,128)(2,1)S(1)} %slice.95), channel_id=1, source_target_pairs={{0,2},{1,3},{2,0},{3,1},{4,6},{5,7},{6,4},{7,5},{8,10},{9,11},{10,... | collective-permute-start | bytes 491528 | tf_op jit(solution)/shard_map/ppermute | solution.py:95
  54.3 4.4 %collective-permute-start.15 = (bf16[64,1280]{1,0:T(8,128)(2,1)S(1)}, bf16[64,1280]{1,0:T(8,128)(2,1)S(1)}, u32[]{:S(2)}, u32[]{:S(2)}) collective-permute-start(bf16[64,1280]{1,0:T(8,128)(2,1)S(1)} %convolution_convert_fusion.6), channel_id=1, source_target_pairs={{0,1},{1,0},{2,3},{3,2},{4,5},{5,4},{6,7},{7,6},{8,9},{9,8},{10,11... | collective-permute-start | bytes 491528 | tf_op jit(solution)/shard_map/ppermute | solution.py:93
  56.3 7.4 %collective-permute-start.25 = (bf16[128,640]{1,0:T(8,128)(2,1)S(1)}, bf16[128,640]{1,0:T(8,128)(2,1)S(1)}, u32[]{:S(2)}, u32[]{:S(2)}) collective-permute-start(bf16[128,640]{1,0:T(8,128)(2,1)S(1)} %fusion.5), channel_id=1, source_target_pairs={{0,4},{4,0},{8,12},{12,8},{1,5},{5,1},{9,13},{13,9},{2,6},{6,2},{1... | collective-permute-start | bytes 491528 | tf_op jit(solution)/shard_map/ppermute | solution.py:98
  57.0 4.5 %collective-permute-start.12 = (bf16[64,640]{1,0:T(8,128)(2,1)S(1)}, bf16[64,640]{1,0:T(8,128)(2,1)S(1)}, u32[]{:S(2)}, u32[]{:S(2)}) collective-permute-start(bf16[64,640]{1,0:T(8,128)(2,1)S(1)} %slice.99), channel_id=1, source_target_pairs={{0,2},{1,3},{2,0},{3,1},{4,6},{5,7},{6,4},{7,5},{8,10},{9,11},{10,... | collective-permute-start | bytes 245768 | tf_op jit(solution)/shard_map/ppermute | solution.py:95
  59.1 4.5 %collective-permute-start.16 = (bf16[64,640]{1,0:T(8,128)(2,1)S(1)}, bf16[64,640]{1,0:T(8,128)(2,1)S(1)}, u32[]{:S(2)}, u32[]{:S(2)}) collective-permute-start(bf16[64,640]{1,0:T(8,128)(2,1)S(1)} %slice.98), channel_id=1, source_target_pairs={{0,2},{1,3},{2,0},{3,1},{4,6},{5,7},{6,4},{7,5},{8,10},{9,11},{10,... | collective-permute-start | bytes 245768 | tf_op jit(solution)/shard_map/ppermute | solution.py:95

commit v30 on v25

--- a/solution.py
+++ b/solution.py
@@ -86,7 +86,7 @@
         hidden = (jax.nn.silu(gate_act) * up_act).astype(jnp.bfloat16)
         keep = jnp.dot(hidden, down_keep, preferred_element_type=jnp.float32).astype(jnp.bfloat16)
         send = jnp.dot(hidden, down_send, preferred_element_type=jnp.float32).astype(jnp.bfloat16)
-        previous = send
+        previous = hidden
         over_c = keep.astype(jnp.float32) + lax.ppermute(
             send, "tensor", _xor_pairs(n_tensor, 1)).astype(jnp.float32)
         summed = over_c[:, :width] + lax.ppermute(

time: 67.1 us -> 69.8 us (1.040)
  waiting for transfers between devices: 19.7 us -> 24.8 us
  starting transfers between devices: 23.3 us -> 20.8 us
    ppermute x4, waiting for transfers between devices: 4.06 us -> 8.58 us  [gathered(): lax.ppermute(over_c[:, width:].astype(jnp.bfloat16), 'tensor', _xor_pairs...]
    ppermute x3, starting transfers between devices: 7.51 us -> 5.16 us  [gathered(): lax.ppermute(part.astype(jnp.bfloat16), 'expert', _xor_pairs(n_expert, k))]
    ppermute x4, waiting for transfers between devices: 3.94 us -> 2.23 us  [gathered(): lax.ppermute(piece, 'tensor', _xor_pairs(n_tensor, 2))]
    ppermute x3, starting transfers between devices: 5.76 us -> 4.39 us  [gathered(): lax.ppermute(scaled, 'expert', _xor_pairs(n_expert, k))]
    ppermute x4, starting transfers between devices: 4.13 us -> 5.41 us  [gathered(): lax.ppermute(piece, 'tensor', _xor_pairs(n_tensor, 2))]
    ppermute x3, waiting for transfers between devices: 7.24 us -> 8.42 us  [gathered(): lax.ppermute(part.astype(jnp.bfloat16), 'expert', _xor_pairs(n_expert, k))]
    ppermute x3, waiting for transfers between devices: 4.4 us -> 5.12 us  [gathered(): lax.ppermute(scaled, 'expert', _xor_pairs(n_expert, k))]
  transfers between devices with their start and end apart: 22 -> 22, of which waited for: 8 -> 8; matrix products, arithmetic and copies ran while one was open for 29% -> 22% of each run, Pallas kernels for 0% -> 0%
where the time goes in v30:
time: 69.8 us; the launch traced here: 69.4 us
  waiting for transfers between devices  24.8 us (36%)
  starting transfers between devices  20.8 us (30%)
  other arithmetic  9 us (13%)
  matrix products  7.74 us (11%)
  local copies, waits for them, and re-layouts  6.71 us (10%)
    ppermute x4, waiting for transfers between devices, gathered(): lax.ppermute(over_c[:, width:].astype(jnp.bfloat16), 'tensor', _xor_pairs...  8.58 us
    ppermute x3, waiting for transfers between devices, gathered(): lax.ppermute(part.astype(jnp.bfloat16), 'expert', _xor_pairs(n_expert, k))  8.42 us
    ppermute x4, starting transfers between devices, gathered(): lax.ppermute(piece, 'tensor', _xor_pairs(n_tensor, 2))  5.41 us
    ppermute x3, starting transfers between devices, gathered(): lax.ppermute(part.astype(jnp.bfloat16), 'expert', _xor_pairs(n_expert, k))  5.16 us
    ppermute x3, waiting for transfers between devices, gathered(): lax.ppermute(scaled, 'expert', _xor_pairs(n_expert, k))  5.12 us
    ppermute x3, starting transfers between devices, gathered(): lax.ppermute(scaled, 'expert', _xor_pairs(n_expert, k))  4.39 us
    ppermute x4, starting transfers between devices, gathered(): lax.ppermute(over_c[:, width:].astype(jnp.bfloat16), 'tensor', _xor_pairs...  4.31 us
    concatenate x4, other arithmetic, gathered(): jnp.concatenate([piece, lax.ppermute(piece, 'tensor', _xor_pairs(n_tensor...  3.77 us
  transfers between devices with their start and end apart: 22, of which 8 were waited for; matrix products, arithmetic and copies ran while one was open for 22% of the time, Pallas kernels for 0%

profile of v30, /device:TPU:0, one launch (start us, length us, event | category | flops | bytes accessed | tf_op | source)
XLA Modules:
  0.0 69.4 jit_solution(4424205922042345238)
XLA Ops:
  0.0 1.0 %multiply_convert_fusion = bf16[128,640]{1,0:T(8,128)(2,1)S(1)} fusion(bf16[128,640]{1,0:T(8,128)(2,1)} %param.6, f32[128]{0:T(128)} %param.7), kind=kLoop, calls=%fused_computation.59 | loop fusion | flops 245760 | bytes 328192 | tf_op jit(solution)/shard_map/convert_element_type | solution.py:64
  1.0 3.0 %collective-permute-start.18 = (bf16[128,640]{1,0:T(8,128)(2,1)S(1)}, bf16[128,640]{1,0:T(8,128)(2,1)}, u32[]{:S(2)}, u32[]{:S(2)}) collective-permute-start(bf16[128,640]{1,0:T(8,128)(2,1)S(1)} %multiply_convert_fusion), channel_id=1, source_target_pairs={{0,2},{1,3},{2,0},{3,1},{4,6},{5,7},{6,4},{7,5},{8,10},{9,11},{10,... | collective-permute-start | bytes 491528 | tf_op jit(solution)/shard_map/ppermute | solution.py:79
  4.0 1.6 %collective-permute-start.12 = (bf16[128,640]{1,0:T(8,128)(2,1)S(1)}, bf16[128,640]{1,0:T(8,128)(2,1)}, u32[]{:S(2)}, u32[]{:S(2)}) collective-permute-start(bf16[128,640]{1,0:T(8,128)(2,1)S(1)} %multiply_convert_fusion), channel_id=1, source_target_pairs={{0,4},{4,0},{8,12},{12,8},{1,5},{5,1},{9,13},{13,9},{2,6},{6,2},{1... | collective-permute-start | bytes 491528 | tf_op jit(solution)/shard_map/ppermute | solution.py:66
  5.6 2.6 %collective-permute-start.6 = (bf16[128,640]{1,0:T(8,128)(2,1)S(1)}, bf16[128,640]{1,0:T(8,128)(2,1)}, u32[]{:S(2)}, u32[]{:S(2)}) collective-permute-start(bf16[128,640]{1,0:T(8,128)(2,1)S(1)} %multiply_convert_fusion), channel_id=1, source_target_pairs={{0,8},{4,12},{8,0},{12,4},{1,9},{5,13},{9,1},{13,5},{2,10},{6,14},... | collective-permute-start | bytes 491528 | tf_op jit(solution)/shard_map/ppermute | solution.py:66
  8.4 2.0 %dynamic-slice_bitcast_fusion.11 = (bf16[640,512]{1,0:T(8,128)(2,1)S(1)}, bf16[640,512]{1,0:T(8,128)(2,1)S(1)}, bf16[640,512]{1,0:T(8,128)(2,1)S(1)}, bf16[640,512]{1,0:T(8,128)(2,1)S(1)}) fusion(bf16[1,2560,512]{2,1,0:T(8,128)(2,1)} %param.9, s32[]{:T(128)S(6)} %select_n.48, s32[]{:T(128)S(6)} %select_n.49, s32[]{:T(128)S(6)} %select_n.51, s32[]{:T(128)S(6)} %select_n.50), kind=kLoop, calls=%fused_computation.40 | loop fusion | bytes 5242896 | tf_op jit(solution)/shard_map/dynamic_slice | solution.py:55
  10.4 0.5 copy-done
  10.9 1.3 %dynamic-slice_bitcast_fusion.7 = (bf16[640,512]{1,0:T(8,128)(2,1)S(1)}, bf16[640,512]{1,0:T(8,128)(2,1)}, bf16[640,512]{1,0:T(8,128)(2,1)}, bf16[640,512]{1,0:T(8,128)(2,1)}) fusion(bf16[1,2560,512]{2,1,0:T(8,128)(2,1)S(1)} %copy-done, s32[]{:T(128)S(6)} %select_n.48, s32[]{:T(128)S(6)} %select_n.49, s32[]{:T(128)S(6)} %select_n.51, s32[]{:T(128)S(6)} %select_n.50), kind=kLoop, calls=%fused_computation.36 | loop fusion | bytes 5242896 | tf_op jit(solution)/shard_map/dynamic_slice | solution.py:55
  12.5 1.5 %copy-done.1 = bf16[1,512,2560]{2,1,0:T(8,128)(2,1)S(1)} copy-done((bf16[1,512,2560]{2,1,0:T(8,128)(2,1)S(1)}, bf16[1,512,2560]{2,1,0:T(8,128)(2,1)}, u32[]{:S(2)}) %copy-start.1) | copy-done | bytes 2621464
  14.2 0.4 collective-permute-start.13
  14.6 0.9 %pad_maximum_fusion.10 = bf16[128,1280]{1,0:T(8,128)(2,1)S(1)} fusion(bf16[128,640]{1,0:T(8,128)(2,1)} %collective-permute-done.18, bf16[128,640]{1,0:T(8,128)(2,1)S(1)} %multiply_convert_fusion), kind=kLoop, calls=%fused_computation.58 | loop fusion | flops 655360 | bytes 655360 | tf_op jit(solution)/shard_map/concatenate | solution.py:78
  15.6 5.1 %collective-permute-done.6 = bf16[128,640]{1,0:T(8,128)(2,1)} collective-permute-done((bf16[128,640]{1,0:T(8,128)(2,1)S(1)}, bf16[128,640]{1,0:T(8,128)(2,1)}, u32[]{:S(2)}, u32[]{:S(2)}) %collective-permute-start.6) | collective-permute-done | bytes 163872 | tf_op jit(solution)/shard_map/ppermute | solution.py:66
  20.8 0.5 collective-permute-start.7
  21.3 1.5 %collective-permute-start.1 = (bf16[128,640]{1,0:T(8,128)(2,1)}, bf16[128,640]{1,0:T(8,128)(2,1)S(1)}, u32[]{:S(2)}, u32[]{:S(2)}) collective-permute-start(bf16[128,640]{1,0:T(8,128)(2,1)} %collective-permute-done), channel_id=1, source_target_pairs={{0,2},{1,3},{2,0},{3,1},{4,6},{5,7},{6,4},{7,5},{8,10},{9,11},{10,... | collective-permute-start | bytes 491528 | tf_op jit(solution)/shard_map/ppermute | solution.py:79
  22.8 1.0 %constant_dynamic-update-slice_fusion.2 = bf16[128,2560]{1,0:T(8,128)(2,1)S(1)} fusion(bf16[128,640]{1,0:T(8,128)(2,1)} %collective-permute-done), kind=kLoop, calls=%fused_computation.63 | loop fusion | bytes 327680
  23.8 0.9 %pad_maximum_fusion.9 = bf16[128,1280]{1,0:T(8,128)(2,1)S(1)} fusion(bf16[128,640]{1,0:T(8,128)(2,1)S(1)} %collective-permute-done.13, bf16[128,640]{1,0:T(8,128)(2,1)} %collective-permute-done.12), kind=kLoop, calls=%fused_computation.57 | loop fusion | flops 655360 | bytes 655360 | tf_op jit(solution)/shard_map/concatenate | solution.py:78
  24.8 1.5 %collective-permute-done.7 = bf16[128,640]{1,0:T(8,128)(2,1)S(1)} collective-permute-done((bf16[128,640]{1,0:T(8,128)(2,1)}, bf16[128,640]{1,0:T(8,128)(2,1)S(1)}, u32[]{:S(2)}, u32[]{:S(2)}) %collective-permute-start.7) | collective-permute-done | bytes 163872 | tf_op jit(solution)/shard_map/ppermute | solution.py:79
  26.3 0.9 %pad_maximum_fusion.8 = bf16[128,1280]{1,0:T(8,128)(2,1)S(1)} fusion(bf16[128,640]{1,0:T(8,128)(2,1)S(1)} %collective-permute-done.7, bf16[128,640]{1,0:T(8,128)(2,1)} %collective-permute-done.6), kind=kLoop, calls=%fused_computation.56 | loop fusion | flops 655360 | bytes 655360 | tf_op jit(solution)/shard_map/concatenate | solution.py:78
  27.3 0.7 %collective-permute-done.1 = bf16[128,640]{1,0:T(8,128)(2,1)S(1)} collective-permute-done((bf16[128,640]{1,0:T(8,128)(2,1)}, bf16[128,640]{1,0:T(8,128)(2,1)S(1)}, u32[]{:S(2)}, u32[]{:S(2)}) %collective-permute-start.1) | collective-permute-done | bytes 163872 | tf_op jit(solution)/shard_map/ppermute | solution.py:79
  28.0 0.9 %pad_maximum_fusion.7 = bf16[128,1280]{1,0:T(8,128)(2,1)S(1)} fusion(bf16[128,640]{1,0:T(8,128)(2,1)S(1)} %collective-permute-done.1, bf16[128,640]{1,0:T(8,128)(2,1)} %collective-permute-done), kind=kLoop, calls=%fused_computation.55 | loop fusion | flops 655360 | bytes 655360 | tf_op jit(solution)/shard_map/concatenate | solution.py:78
  29.1 1.1 %pad_maximum_fusion.6 = bf16[128,2560]{1,0:T(8,128)(2,1)S(1)} fusion(bf16[128,1280]{1,0:T(8,128)(2,1)S(1)} %collective-permute-done.19, bf16[128,640]{1,0:T(8,128)(2,1)} %collective-permute-done.18, bf16[128,640]{1,0:T(8,128)(2,1)S(1)} %multiply_convert_fusion), kind=kLoop, calls=%fused_computation.24 | loop fusion | flops 1966080 | bytes 1310720 | tf_op jit(solution)/shard_map/concatenate | solution.py:80
  30.2 0.4 collective-permute-done.2
  30.7 0.5 fusion.14
  31.3 0.7 %multiply_convert_fusion.1 = bf16[128,512]{1,0:T(8,128)(2,1)S(1)} fusion(f32[128,512]{1,0:T(8,128)S(1)} %fusion.14, bf16[128,2560]{1,0:T(8,128)(2,1)S(1)} %constant_dynamic-update-slice_fusion, bf16[640,512]{1,0:T(8,128)(2,1)S(1)} %copy-done.3, bf16[640,512]{1,0:T(8,128)(2,1)S(1)} %copy-done.4, bf16[640,512]{1,0:T(8,128)(2,1)S(1)} %copy-done.2, ...), kind=kOutput, calls=%fused_computation.60 | convolution fusion | flops 346423296 | bytes 3670016 | tf_op jit(solution)/shard_map/dot_general | solution.py:85
  32.0 1.0 %pad_maximum_fusion.4 = bf16[128,2560]{1,0:T(8,128)(2,1)S(1)} fusion(bf16[128,1280]{1,0:T(8,128)(2,1)S(1)} %collective-permute-done.8, bf16[128,640]{1,0:T(8,128)(2,1)S(1)} %collective-permute-done.7, bf16[128,640]{1,0:T(8,128)(2,1)} %collective-permute-done.6), kind=kLoop, calls=%fused_computation.22 | loop fusion | flops 1966080 | bytes 1310720 | tf_op jit(solution)/shard_map/concatenate | solution.py:80
  33.0 0.5 fusion.15
  33.5 0.7 %fusion.4 = bf16[128,512]{1,0:T(8,128)(2,1)S(1)} fusion(bf16[128,2560]{1,0:T(8,128)(2,1)S(1)} %pad_maximum_fusion.4, f32[128,512]{1,0:T(8,128)S(1)} %fusion.15, bf16[640,512]{1,0:T(8,128)(2,1)S(1)} %copy-done.3, bf16[640,512]{1,0:T(8,128)(2,1)S(1)} %copy-done.4, bf16[640,512]{1,0:T(8,128)(2,1)S(1)} %copy-done.2, bf16[640,512]{1,0:T(8,128)(2,1)S(1)} %get-tuple-element.15), kind=kOutput, calls=%fused_computation.19 | convolution fusion | flops 346423296 | bytes 3670016 | tf_op jit(solution)/shard_map/dot_general | solution.py:85
  34.2 1.0 %pad_maximum_fusion.5 = bf16[128,2560]{1,0:T(8,128)(2,1)S(1)} fusion(bf16[128,1280]{1,0:T(8,128)(2,1)S(1)} %collective-permute-done.14, bf16[128,640]{1,0:T(8,128)(2,1)S(1)} %collective-permute-done.13, bf16[128,640]{1,0:T(8,128)(2,1)} %collective-permute-done.12), kind=kLoop, calls=%fused_computation.23 | loop fusion | flops 1966080 | bytes 1310720 | tf_op jit(solution)/shard_map/concatenate | solution.py:80
  35.2 0.5 fusion.16
  35.7 0.7 %fusion.5 = bf16[128,512]{1,0:T(8,128)(2,1)S(1)} fusion(bf16[128,2560]{1,0:T(8,128)(2,1)S(1)} %pad_maximum_fusion.5, f32[128,512]{1,0:T(8,128)S(1)} %fusion.16, bf16[640,512]{1,0:T(8,128)(2,1)S(1)} %copy-done.3, bf16[640,512]{1,0:T(8,128)(2,1)S(1)} %copy-done.4, bf16[640,512]{1,0:T(8,128)(2,1)S(1)} %copy-done.2, bf16[640,512]{1,0:T(8,128)(2,1)S(1)} %get-tuple-element.15), kind=kOutput, calls=%fused_computation.20 | convolution fusion | flops 346423296 | bytes 3670016 | tf_op jit(solution)/shard_map/dot_general | solution.py:85
  36.5 0.5 fusion.17
  37.0 0.7 %fusion.6 = bf16[128,512]{1,0:T(8,128)(2,1)S(1)} fusion(bf16[128,2560]{1,0:T(8,128)(2,1)S(1)} %pad_maximum_fusion.6, f32[128,512]{1,0:T(8,128)S(1)} %fusion.17, bf16[640,512]{1,0:T(8,128)(2,1)S(1)} %copy-done.3, bf16[640,512]{1,0:T(8,128)(2,1)S(1)} %copy-done.4, bf16[640,512]{1,0:T(8,128)(2,1)S(1)} %copy-done.2, bf16[640,512]{1,0:T(8,128)(2,1)S(1)} %get-tuple-element.15), kind=kOutput, calls=%fused_computation.21 | convolution fusion | flops 346423296 | bytes 3670016 | tf_op jit(solution)/shard_map/dot_general | solution.py:85
  39.0 0.4 collective-permute-start.15
  40.0 0.4 collective-permute-start.3
  40.7 0.6 collective-permute-start.21
  41.3 0.3 convert_add_fusion.1
  41.7 1.6 %collective-permute-start.16 = (bf16[128,640]{1,0:T(8,128)(2,1)S(1)}, bf16[128,640]{1,0:T(8,128)(2,1)S(1)}, u32[]{:S(2)}, u32[]{:S(2)}) collective-permute-start(bf16[128,640]{1,0:T(8,128)(2,1)S(1)} %slice.65), channel_id=1, source_target_pairs={{0,2},{1,3},{2,0},{3,1},{4,6},{5,7},{6,4},{7,5},{8,10},{9,11},{10,... | collective-permute-start | bytes 491528 | tf_op jit(solution)/shard_map/ppermute | solution.py:92
  43.3 0.3 convert_add_fusion.2
  43.7 0.6 collective-permute-start.10
  44.3 0.4 convert_add_fusion.3
  44.7 1.6 %collective-permute-start.4 = (bf16[128,640]{1,0:T(8,128)(2,1)S(1)}, bf16[128,640]{1,0:T(8,128)(2,1)S(1)}, u32[]{:S(2)}, u32[]{:S(2)}) collective-permute-start(bf16[128,640]{1,0:T(8,128)(2,1)S(1)} %slice.67), channel_id=1, source_target_pairs={{0,2},{1,3},{2,0},{3,1},{4,6},{5,7},{6,4},{7,5},{8,10},{9,11},{10,... | collective-permute-start | bytes 491528 | tf_op jit(solution)/shard_map/ppermute | solution.py:92
  46.2 5.1 %collective-permute-done.16 = bf16[128,640]{1,0:T(8,128)(2,1)S(1)} collective-permute-done((bf16[128,640]{1,0:T(8,128)(2,1)S(1)}, bf16[128,640]{1,0:T(8,128)(2,1)S(1)}, u32[]{:S(2)}, u32[]{:S(2)}) %collective-permute-start.16) | collective-permute-done | bytes 163872 | tf_op jit(solution)/shard_map/ppermute | solution.py:92
  51.4 1.0 %collective-permute-start.17 = (bf16[128,640]{1,0:T(8,128)(2,1)S(1)}, bf16[128,640]{1,0:T(8,128)(2,1)S(1)}, u32[]{:S(2)}, u32[]{:S(2)}) collective-permute-start(bf16[128,640]{1,0:T(8,128)(2,1)S(1)} %fusion.10), channel_id=1, source_target_pairs={{0,4},{4,0},{8,12},{12,8},{1,5},{5,1},{9,13},{13,9},{2,6},{6,2},{1... | collective-permute-start | bytes 491528 | tf_op jit(solution)/shard_map/ppermute | solution.py:97
  52.4 2.5 %collective-permute-done.10 = bf16[128,640]{1,0:T(8,128)(2,1)S(1)} collective-permute-done((bf16[128,640]{1,0:T(8,128)(2,1)S(1)}, bf16[128,640]{1,0:T(8,128)(2,1)S(1)}, u32[]{:S(2)}, u32[]{:S(2)}) %collective-permute-start.10) | collective-permute-done | bytes 163872 | tf_op jit(solution)/shard_map/ppermute | solution.py:92
  54.9 1.7 %collective-permute-start.11 = (bf16[128,640]{1,0:T(8,128)(2,1)S(1)}, bf16[128,640]{1,0:T(8,128)(2,1)S(1)}, u32[]{:S(2)}, u32[]{:S(2)}) collective-permute-start(bf16[128,640]{1,0:T(8,128)(2,1)S(1)} %fusion.11), channel_id=1, source_target_pairs={{0,8},{4,12},{8,0},{12,4},{1,9},{5,13},{9,1},{13,5},{2,10},{6,14},... | collective-permute-start | bytes 491528 | tf_op jit(solution)/shard_map/ppermute | solution.py:97
  56.6 1.0 %collective-permute-done.4 = bf16[128,640]{1,0:T(8,128)(2,1)S(1)} collective-permute-done((bf16[128,640]{1,0:T(8,128)(2,1)S(1)}, bf16[128,640]{1,0:T(8,128)(2,1)S(1)}, u32[]{:S(2)}, u32[]{:S(2)}) %collective-permute-start.4) | collective-permute-done | bytes 163872 | tf_op jit(solution)/shard_map/ppermute | solution.py:92
  57.6 2.5 %collective-permute-start.5 = (bf16[128,640]{1,0:T(8,128)(2,1)S(1)}, bf16[128,640]{1,0:T(8,128)(2,1)S(1)}, u32[]{:S(2)}, u32[]{:S(2)}) collective-permute-start(bf16[128,640]{1,0:T(8,128)(2,1)S(1)} %fusion.12), channel_id=1, source_target_pairs={{0,12},{4,8},{8,4},{12,0},{1,13},{5,9},{9,5},{13,1},{2,14},{6,10},... | collective-permute-start | bytes 491528 | tf_op jit(solution)/shard_map/ppermute | solution.py:97
  60.1 8.4 %collective-permute-done.11 = bf16[128,640]{1,0:T(8,128)(2,1)S(1)} collective-permute-done((bf16[128,640]{1,0:T(8,128)(2,1)S(1)}, bf16[128,640]{1,0:T(8,128)(2,1)S(1)}, u32[]{:S(2)}, u32[]{:S(2)}) %collective-permute-start.11) | collective-permute-done | bytes 163872 | tf_op jit(solution)/shard_map/ppermute | solution.py:97
  68.5 0.9 %fusion.9 = bf16[128,640]{1,0:T(8,128)(2,1)} fusion(f32[128,1280]{1,0:T(8,128)S(1)} %convert_add_fusion, bf16[128,640]{1,0:T(8,128)(2,1)S(1)} %collective-permute-done.21, bf16[128,640]{1,0:T(8,128)(2,1)S(1)} %collective-permute-done.17, bf16[128,640]{1,0:T(8,128)(2,1)S(1)} %collective-permute-done.11, bf16[128,640]{1,0:T(8,128)(2,1)S(1)} %collective-permute-done.5, ...), kind=kLoop, calls=%fused_computation.45 | loop fusion | flops 1064960 | bytes 1147392 | tf_op jit(solution)/shard_map/convert_element_type | solution.py:101
  (48 shorter events, 3.4 us)
Async XLA Ops:
  1.0 13.6 %collective-permute-start.18 = (bf16[128,640]{1,0:T(8,128)(2,1)S(1)}, bf16[128,640]{1,0:T(8,128)(2,1)}, u32[]{:S(2)}, u32[]{:S(2)}) collective-permute-start(bf16[128,640]{1,0:T(8,128)(2,1)S(1)} %multiply_convert_fusion), channel_id=1, source_target_pairs={{0,2},{1,3},{2,0},{3,1},{4,6},{5,7},{6,4},{7,5},{8,10},{9,11},{10,... | collective-permute-start | bytes 491528 | tf_op jit(solution)/shard_map/ppermute | solution.py:79
  4.0 10.2 %collective-permute-start.12 = (bf16[128,640]{1,0:T(8,128)(2,1)S(1)}, bf16[128,640]{1,0:T(8,128)(2,1)}, u32[]{:S(2)}, u32[]{:S(2)}) collective-permute-start(bf16[128,640]{1,0:T(8,128)(2,1)S(1)} %multiply_convert_fusion), channel_id=1, source_target_pairs={{0,4},{4,0},{8,12},{12,8},{1,5},{5,1},{9,13},{13,9},{2,6},{6,2},{1... | collective-permute-start | bytes 491528 | tf_op jit(solution)/shard_map/ppermute | solution.py:66
  5.6 15.2 %collective-permute-start.6 = (bf16[128,640]{1,0:T(8,128)(2,1)S(1)}, bf16[128,640]{1,0:T(8,128)(2,1)}, u32[]{:S(2)}, u32[]{:S(2)}) collective-permute-start(bf16[128,640]{1,0:T(8,128)(2,1)S(1)} %multiply_convert_fusion), channel_id=1, source_target_pairs={{0,8},{4,12},{8,0},{12,4},{1,9},{5,13},{9,1},{13,5},{2,10},{6,14},... | collective-permute-start | bytes 491528 | tf_op jit(solution)/shard_map/ppermute | solution.py:66
  8.2 13.1 %collective-permute-start = (bf16[128,640]{1,0:T(8,128)(2,1)S(1)}, bf16[128,640]{1,0:T(8,128)(2,1)}, u32[]{:S(2)}, u32[]{:S(2)}) collective-permute-start(bf16[128,640]{1,0:T(8,128)(2,1)S(1)} %multiply_convert_fusion), channel_id=1, source_target_pairs={{0,12},{4,8},{8,4},{12,0},{1,13},{5,9},{9,5},{13,1},{2,14},{6,10},... | collective-permute-start | bytes 491528 | tf_op jit(solution)/shard_map/ppermute | solution.py:66
  8.4 2.5 %copy-start = (bf16[1,2560,512]{2,1,0:T(8,128)(2,1)S(1)}, bf16[1,2560,512]{2,1,0:T(8,128)(2,1)}, u32[]{:S(2)}) copy-start(bf16[1,2560,512]{2,1,0:T(8,128)(2,1)} %param.10) | copy-start | bytes 7864324
  12.3 1.7 %copy-start.1 = (bf16[1,512,2560]{2,1,0:T(8,128)(2,1)S(1)}, bf16[1,512,2560]{2,1,0:T(8,128)(2,1)}, u32[]{:S(2)}) copy-start(bf16[1,512,2560]{2,1,0:T(8,128)(2,1)} %param.11) | copy-start | bytes 7864324
  14.2 9.5 %collective-permute-start.13 = (bf16[128,640]{1,0:T(8,128)(2,1)}, bf16[128,640]{1,0:T(8,128)(2,1)S(1)}, u32[]{:S(2)}, u32[]{:S(2)}) collective-permute-start(bf16[128,640]{1,0:T(8,128)(2,1)} %collective-permute-done.12), channel_id=1, source_target_pairs={{0,2},{1,3},{2,0},{3,1},{4,6},{5,7},{6,4},{7,5},{8,10},{9,11},{10,... | collective-permute-start | bytes 491528 | tf_op jit(solution)/shard_map/ppermute | solution.py:79
  15.6 13.6 %collective-permute-start.19 = (bf16[128,1280]{1,0:T(8,128)(2,1)S(1)}, bf16[128,1280]{1,0:T(8,128)(2,1)S(1)}, u32[]{:S(2)}, u32[]{:S(2)}) collective-permute-start(bf16[128,1280]{1,0:T(8,128)(2,1)S(1)} %pad_maximum_fusion.10), channel_id=1, source_target_pairs={{0,1},{1,0},{2,3},{3,2},{4,5},{5,4},{6,7},{7,6},{8,9},{9,8},{10,11... | collective-permute-start | bytes 983048 | tf_op jit(solution)/shard_map/ppermute | solution.py:81
  20.8 5.5 %collective-permute-start.7 = (bf16[128,640]{1,0:T(8,128)(2,1)}, bf16[128,640]{1,0:T(8,128)(2,1)S(1)}, u32[]{:S(2)}, u32[]{:S(2)}) collective-permute-start(bf16[128,640]{1,0:T(8,128)(2,1)} %collective-permute-done.6), channel_id=1, source_target_pairs={{0,2},{1,3},{2,0},{3,1},{4,6},{5,7},{6,4},{7,5},{8,10},{9,11},{10,... | collective-permute-start | bytes 491528 | tf_op jit(solution)/shard_map/ppermute | solution.py:79
  21.3 6.7 %collective-permute-start.1 = (bf16[128,640]{1,0:T(8,128)(2,1)}, bf16[128,640]{1,0:T(8,128)(2,1)S(1)}, u32[]{:S(2)}, u32[]{:S(2)}) collective-permute-start(bf16[128,640]{1,0:T(8,128)(2,1)} %collective-permute-done), channel_id=1, source_target_pairs={{0,2},{1,3},{2,0},{3,1},{4,6},{5,7},{6,4},{7,5},{8,10},{9,11},{10,... | collective-permute-start | bytes 491528 | tf_op jit(solution)/shard_map/ppermute | solution.py:79
  24.7 9.5 %collective-permute-start.14 = (bf16[128,1280]{1,0:T(8,128)(2,1)S(1)}, bf16[128,1280]{1,0:T(8,128)(2,1)S(1)}, u32[]{:S(2)}, u32[]{:S(2)}) collective-permute-start(bf16[128,1280]{1,0:T(8,128)(2,1)S(1)} %pad_maximum_fusion.9), channel_id=1, source_target_pairs={{0,1},{1,0},{2,3},{3,2},{4,5},{5,4},{6,7},{7,6},{8,9},{9,8},{10,11... | collective-permute-start | bytes 983048 | tf_op jit(solution)/shard_map/ppermute | solution.py:81
  27.2 4.8 %collective-permute-start.8 = (bf16[128,1280]{1,0:T(8,128)(2,1)S(1)}, bf16[128,1280]{1,0:T(8,128)(2,1)S(1)}, u32[]{:S(2)}, u32[]{:S(2)}) collective-permute-start(bf16[128,1280]{1,0:T(8,128)(2,1)S(1)} %pad_maximum_fusion.8), channel_id=1, source_target_pairs={{0,1},{1,0},{2,3},{3,2},{4,5},{5,4},{6,7},{7,6},{8,9},{9,8},{10,11... | collective-permute-start | bytes 983048 | tf_op jit(solution)/shard_map/ppermute | solution.py:81
  29.0 1.7 %collective-permute-start.2 = (bf16[128,1280]{1,0:T(8,128)(2,1)S(1)}, bf16[128,1280]{1,0:T(8,128)(2,1)S(1)}, u32[]{:S(2)}, u32[]{:S(2)}) collective-permute-start(bf16[128,1280]{1,0:T(8,128)(2,1)S(1)} %pad_maximum_fusion.7), channel_id=1, source_target_pairs={{0,1},{1,0},{2,3},{3,2},{4,5},{5,4},{6,7},{7,6},{8,9},{9,8},{10,11... | collective-permute-start | bytes 983048 | tf_op jit(solution)/shard_map/ppermute | solution.py:81
  29.1 2.1 %copy-start.2 = (bf16[640,512]{1,0:T(8,128)(2,1)S(1)}, bf16[640,512]{1,0:T(8,128)(2,1)}, u32[]{:S(2)}) copy-start(bf16[640,512]{1,0:T(8,128)(2,1)} %get-tuple-element.16) | copy-start | bytes 1966084
  29.1 2.1 %copy-start.3 = (bf16[640,512]{1,0:T(8,128)(2,1)S(1)}, bf16[640,512]{1,0:T(8,128)(2,1)}, u32[]{:S(2)}) copy-start(bf16[640,512]{1,0:T(8,128)(2,1)} %get-tuple-element.17) | copy-start | bytes 1966084
  29.1 2.1 %copy-start.4 = (bf16[640,512]{1,0:T(8,128)(2,1)S(1)}, bf16[640,512]{1,0:T(8,128)(2,1)}, u32[]{:S(2)}) copy-start(bf16[640,512]{1,0:T(8,128)(2,1)} %get-tuple-element.18) | copy-start | bytes 1966084
  38.4 1.9 %collective-permute-start.20 = (bf16[128,1280]{1,0:T(8,128)(2,1)S(1)}, bf16[128,1280]{1,0:T(8,128)(2,1)S(1)}, u32[]{:S(2)}, u32[]{:S(2)}) collective-permute-start(bf16[128,1280]{1,0:T(8,128)(2,1)S(1)} %convolution_convert_fusion), channel_id=1, source_target_pairs={{0,1},{1,0},{2,3},{3,2},{4,5},{5,4},{6,7},{7,6},{8,9},{9,8},{10,11... | collective-permute-start | bytes 983048 | tf_op jit(solution)/shard_map/ppermute | solution.py:90
  39.0 2.3 %collective-permute-start.15 = (bf16[128,1280]{1,0:T(8,128)(2,1)S(1)}, bf16[128,1280]{1,0:T(8,128)(2,1)S(1)}, u32[]{:S(2)}, u32[]{:S(2)}) collective-permute-start(bf16[128,1280]{1,0:T(8,128)(2,1)S(1)} %convolution_convert_fusion.2), channel_id=1, source_target_pairs={{0,1},{1,0},{2,3},{3,2},{4,5},{5,4},{6,7},{7,6},{8,9},{9,8},{10,11... | collective-permute-start | bytes 983048 | tf_op jit(solution)/shard_map/ppermute | solution.py:90
  39.8 3.5 %collective-permute-start.9 = (bf16[128,1280]{1,0:T(8,128)(2,1)S(1)}, bf16[128,1280]{1,0:T(8,128)(2,1)S(1)}, u32[]{:S(2)}, u32[]{:S(2)}) collective-permute-start(bf16[128,1280]{1,0:T(8,128)(2,1)S(1)} %convolution_convert_fusion.4), channel_id=1, source_target_pairs={{0,1},{1,0},{2,3},{3,2},{4,5},{5,4},{6,7},{7,6},{8,9},{9,8},{10,11... | collective-permute-start | bytes 983048 | tf_op jit(solution)/shard_map/ppermute | solution.py:90
  40.0 4.3 %collective-permute-start.3 = (bf16[128,1280]{1,0:T(8,128)(2,1)S(1)}, bf16[128,1280]{1,0:T(8,128)(2,1)S(1)}, u32[]{:S(2)}, u32[]{:S(2)}) collective-permute-start(bf16[128,1280]{1,0:T(8,128)(2,1)S(1)} %convolution_convert_fusion.6), channel_id=1, source_target_pairs={{0,1},{1,0},{2,3},{3,2},{4,5},{5,4},{6,7},{7,6},{8,9},{9,8},{10,11... | collective-permute-start | bytes 983048 | tf_op jit(solution)/shard_map/ppermute | solution.py:90
  40.7 19.4 %collective-permute-start.21 = (bf16[128,640]{1,0:T(8,128)(2,1)S(1)}, bf16[128,640]{1,0:T(8,128)(2,1)S(1)}, u32[]{:S(2)}, u32[]{:S(2)}) collective-permute-start(bf16[128,640]{1,0:T(8,128)(2,1)S(1)} %slice.64), channel_id=1, source_target_pairs={{0,2},{1,3},{2,0},{3,1},{4,6},{5,7},{6,4},{7,5},{8,10},{9,11},{10,... | collective-permute-start | bytes 491528 | tf_op jit(solution)/shard_map/ppermute | solution.py:92
  41.7 9.6 %collective-permute-start.16 = (bf16[128,640]{1,0:T(8,128)(2,1)S(1)}, bf16[128,640]{1,0:T(8,128)(2,1)S(1)}, u32[]{:S(2)}, u32[]{:S(2)}) collective-permute-start(bf16[128,640]{1,0:T(8,128)(2,1)S(1)} %slice.65), channel_id=1, source_target_pairs={{0,2},{1,3},{2,0},{3,1},{4,6},{5,7},{6,4},{7,5},{8,10},{9,11},{10,... | collective-permute-start | bytes 491528 | tf_op jit(solution)/shard_map/ppermute | solution.py:92
  43.6 16.4 %copy-start.5 = (s32[128,1]{0,1:T(1,128)S(1)}, s32[128,1]{0,1:T(1,128)}, u32[]{:S(2)}) copy-start(s32[128,1]{0,1:T(1,128)} %param.8) | copy-start | bytes 1540
  43.7 11.2 %collective-permute-start.10 = (bf16[128,640]{1,0:T(8,128)(2,1)S(1)}, bf16[128,640]{1,0:T(8,128)(2,1)S(1)}, u32[]{:S(2)}, u32[]{:S(2)}) collective-permute-start(bf16[128,640]{1,0:T(8,128)(2,1)S(1)} %slice.66), channel_id=1, source_target_pairs={{0,2},{1,3},{2,0},{3,1},{4,6},{5,7},{6,4},{7,5},{8,10},{9,11},{10,... | collective-permute-start | bytes 491528 | tf_op jit(solution)/shard_map/ppermute | solution.py:92
  44.7 12.9 %collective-permute-start.4 = (bf16[128,640]{1,0:T(8,128)(2,1)S(1)}, bf16[128,640]{1,0:T(8,128)(2,1)S(1)}, u32[]{:S(2)}, u32[]{:S(2)}) collective-permute-start(bf16[128,640]{1,0:T(8,128)(2,1)S(1)} %slice.67), channel_id=1, source_target_pairs={{0,2},{1,3},{2,0},{3,1},{4,6},{5,7},{6,4},{7,5},{8,10},{9,11},{10,... | collective-permute-start | bytes 491528 | tf_op jit(solution)/shard_map/ppermute | solution.py:92
  51.4 8.7 %collective-permute-start.17 = (bf16[128,640]{1,0:T(8,128)(2,1)S(1)}, bf16[128,640]{1,0:T(8,128)(2,1)S(1)}, u32[]{:S(2)}, u32[]{:S(2)}) collective-permute-start(bf16[128,640]{1,0:T(8,128)(2,1)S(1)} %fusion.10), channel_id=1, source_target_pairs={{0,4},{4,0},{8,12},{12,8},{1,5},{5,1},{9,13},{13,9},{2,6},{6,2},{1... | collective-permute-start | bytes 491528 | tf_op jit(solution)/shard_map/ppermute | solution.py:97
  54.9 13.6 %collective-permute-start.11 = (bf16[128,640]{1,0:T(8,128)(2,1)S(1)}, bf16[128,640]{1,0:T(8,128)(2,1)S(1)}, u32[]{:S(2)}, u32[]{:S(2)}) collective-permute-start(bf16[128,640]{1,0:T(8,128)(2,1)S(1)} %fusion.11), channel_id=1, source_target_pairs={{0,8},{4,12},{8,0},{12,4},{1,9},{5,13},{9,1},{13,5},{2,10},{6,14},... | collective-permute-start | bytes 491528 | tf_op jit(solution)/shard_map/ppermute | solution.py:97
  57.6 10.9 %collective-permute-start.5 = (bf16[128,640]{1,0:T(8,128)(2,1)S(1)}, bf16[128,640]{1,0:T(8,128)(2,1)S(1)}, u32[]{:S(2)}, u32[]{:S(2)}) collective-permute-start(bf16[128,640]{1,0:T(8,128)(2,1)S(1)} %fusion.12), channel_id=1, source_target_pairs={{0,12},{4,8},{8,4},{12,0},{1,13},{5,9},{9,5},{13,1},{2,14},{6,10},... | collective-permute-start | bytes 491528 | tf_op jit(solution)/shard_map/ppermute | solution.py:97

commit v31 on v28

--- a/solution.py
+++ b/solution.py
@@ -70,7 +70,7 @@
     up_w = _slots(up_weight[0], t, width, 0)
     down_keep = _slots(down_weight[0], t, width, 1, _ORDER[:2])
     down_send = _slots(down_weight[0], t, width, 1, _ORDER[2:])
-    waves = [[k] for k in [1][:n_expert - 1] + list(range(n_expert - 1, 1, -1)) + [0]]
+    waves = [[k] for k in ([2, 1, 3] if n_expert == 4 else list(range(n_expert - 1, 0, -1))) + [0]]
     total = None
     previous = None
     for wave in waves:

time: 65.6 us -> 61.4 us (0.936)
  waiting for transfers between devices: 18.5 us -> 14.6 us
    ppermute x3, waiting for transfers between devices: 9.18 us -> 3.96 us  [gathered(): lax.ppermute(part.astype(jnp.bfloat16), 'expert', _xor_pairs(n_expert, k))]
    ppermute x4, waiting for transfers between devices: 0.54 us -> 5.23 us  [gathered(): lax.ppermute(piece, 'tensor', _xor_pairs(n_tensor, 2))]
    ppermute x3, waiting for transfers between devices: 4.04 us -> 0.37 us  [gathered(): lax.ppermute(scaled, 'expert', _xor_pairs(n_expert, k))]
    ppermute x4, starting transfers between devices: 5.14 us -> 5.91 us  [gathered(): lax.ppermute(piece, 'tensor', _xor_pairs(n_tensor, 2))]
  transfers between devices with their start and end apart: 22 -> 22, of which waited for: 7 -> 8; matrix products, arithmetic and copies ran while one was open for 30% -> 32% of each run, Pallas kernels for 0% -> 0%
where the time goes in v31:
time: 61.4 us; the launch traced here: 61.1 us
  starting transfers between devices  22.9 us (37%)
  waiting for transfers between devices  14.6 us (24%)
  other arithmetic  8.86 us (14%)
  matrix products  7.75 us (13%)
  local copies, waits for them, and re-layouts  6.68 us (11%)
    ppermute x4, starting transfers between devices, gathered(): lax.ppermute(piece, 'tensor', _xor_pairs(n_tensor, 2))  5.91 us
    ppermute x3, starting transfers between devices, gathered(): lax.ppermute(scaled, 'expert', _xor_pairs(n_expert, k))  5.68 us
    ppermute x4, waiting for transfers between devices, gathered(): lax.ppermute(piece, 'tensor', _xor_pairs(n_tensor, 2))  5.23 us
    ppermute x4, starting transfers between devices, gathered(): lax.ppermute(over_c[:, width:].astype(jnp.bfloat16), 'tensor', _xor_pairs...  4.94 us
    ppermute x3, starting transfers between devices, gathered(): lax.ppermute(part.astype(jnp.bfloat16), 'expert', _xor_pairs(n_expert, k))  4.93 us
    ppermute x4, waiting for transfers between devices, gathered(): lax.ppermute(over_c[:, width:].astype(jnp.bfloat16), 'tensor', _xor_pairs...  4.69 us
    ppermute x3, waiting for transfers between devices, gathered(): lax.ppermute(part.astype(jnp.bfloat16), 'expert', _xor_pairs(n_expert, k))  3.96 us
    concatenate x4, other arithmetic, gathered(): jnp.concatenate([piece, lax.ppermute(piece, 'tensor', _xor_pairs(n_tensor...  3.76 us
  transfers between devices with their start and end apart: 22, of which 8 were waited for; matrix products, arithmetic and copies ran while one was open for 32% of the time, Pallas kernels for 0%

profile of v31, /device:TPU:0, one launch (start us, length us, event | category | flops | bytes accessed | tf_op | source)
XLA Modules:
  0.0 61.1 jit_solution(7766797947514275304)
XLA Ops:
  0.0 1.0 %multiply_convert_fusion = bf16[128,640]{1,0:T(8,128)(2,1)S(1)} fusion(bf16[128,640]{1,0:T(8,128)(2,1)} %param.6, f32[128]{0:T(128)} %param.7), kind=kLoop, calls=%fused_computation.56 | loop fusion | flops 245760 | bytes 328192 | tf_op jit(solution)/shard_map/convert_element_type | solution.py:64
  1.0 4.1 %collective-permute-start = (bf16[128,640]{1,0:T(8,128)(2,1)S(1)}, bf16[128,640]{1,0:T(8,128)(2,1)}, u32[]{:S(2)}, u32[]{:S(2)}) collective-permute-start(bf16[128,640]{1,0:T(8,128)(2,1)S(1)} %multiply_convert_fusion), channel_id=1, source_target_pairs={{0,8},{4,12},{8,0},{12,4},{1,9},{5,13},{9,1},{13,5},{2,10},{6,14},... | collective-permute-start | bytes 491528 | tf_op jit(solution)/shard_map/ppermute | solution.py:66
  5.1 1.6 %collective-permute-start.6 = (bf16[128,640]{1,0:T(8,128)(2,1)S(1)}, bf16[128,640]{1,0:T(8,128)(2,1)}, u32[]{:S(2)}, u32[]{:S(2)}) collective-permute-start(bf16[128,640]{1,0:T(8,128)(2,1)S(1)} %multiply_convert_fusion), channel_id=1, source_target_pairs={{0,4},{4,0},{8,12},{12,8},{1,5},{5,1},{9,13},{13,9},{2,6},{6,2},{1... | collective-permute-start | bytes 491528 | tf_op jit(solution)/shard_map/ppermute | solution.py:66
  6.7 1.7 %collective-permute-start.18 = (bf16[128,640]{1,0:T(8,128)(2,1)S(1)}, bf16[128,640]{1,0:T(8,128)(2,1)}, u32[]{:S(2)}, u32[]{:S(2)}) collective-permute-start(bf16[128,640]{1,0:T(8,128)(2,1)S(1)} %multiply_convert_fusion), channel_id=1, source_target_pairs={{0,2},{1,3},{2,0},{3,1},{4,6},{5,7},{6,4},{7,5},{8,10},{9,11},{10,... | collective-permute-start | bytes 491528 | tf_op jit(solution)/shard_map/ppermute | solution.py:79
  8.4 2.0 %dynamic-slice_bitcast_fusion.11 = (bf16[640,512]{1,0:T(8,128)(2,1)S(1)}, bf16[640,512]{1,0:T(8,128)(2,1)S(1)}, bf16[640,512]{1,0:T(8,128)(2,1)S(1)}, bf16[640,512]{1,0:T(8,128)(2,1)S(1)}) fusion(bf16[1,2560,512]{2,1,0:T(8,128)(2,1)} %param.9, s32[]{:T(128)S(6)} %select_n.48, s32[]{:T(128)S(6)} %select_n.49, s32[]{:T(128)S(6)} %select_n.51, s32[]{:T(128)S(6)} %select_n.50), kind=kLoop, calls=%fused_computation.37 | loop fusion | bytes 5242896 | tf_op jit(solution)/shard_map/dynamic_slice | solution.py:55
  10.4 0.5 copy-done
  10.9 1.3 %dynamic-slice_bitcast_fusion.7 = (bf16[640,512]{1,0:T(8,128)(2,1)S(1)}, bf16[640,512]{1,0:T(8,128)(2,1)}, bf16[640,512]{1,0:T(8,128)(2,1)}, bf16[640,512]{1,0:T(8,128)(2,1)}) fusion(bf16[1,2560,512]{2,1,0:T(8,128)(2,1)S(1)} %copy-done, s32[]{:T(128)S(6)} %select_n.48, s32[]{:T(128)S(6)} %select_n.49, s32[]{:T(128)S(6)} %select_n.51, s32[]{:T(128)S(6)} %select_n.50), kind=kLoop, calls=%fused_computation.33 | loop fusion | bytes 5242896 | tf_op jit(solution)/shard_map/dynamic_slice | solution.py:55
  12.5 1.5 %copy-done.1 = bf16[1,512,2560]{2,1,0:T(8,128)(2,1)S(1)} copy-done((bf16[1,512,2560]{2,1,0:T(8,128)(2,1)S(1)}, bf16[1,512,2560]{2,1,0:T(8,128)(2,1)}, u32[]{:S(2)}) %copy-start.1) | copy-done | bytes 2621464
  14.2 0.4 collective-permute-done
  14.6 2.1 %collective-permute-start.1 = (bf16[128,640]{1,0:T(8,128)(2,1)}, bf16[128,640]{1,0:T(8,128)(2,1)S(1)}, u32[]{:S(2)}, u32[]{:S(2)}) collective-permute-start(bf16[128,640]{1,0:T(8,128)(2,1)} %collective-permute-done), channel_id=1, source_target_pairs={{0,2},{1,3},{2,0},{3,1},{4,6},{5,7},{6,4},{7,5},{8,10},{9,11},{10,... | collective-permute-start | bytes 491528 | tf_op jit(solution)/shard_map/ppermute | solution.py:79
  16.7 0.9 %pad_maximum_fusion.10 = bf16[128,1280]{1,0:T(8,128)(2,1)S(1)} fusion(bf16[128,640]{1,0:T(8,128)(2,1)} %collective-permute-done.18, bf16[128,640]{1,0:T(8,128)(2,1)S(1)} %multiply_convert_fusion), kind=kLoop, calls=%fused_computation.55 | loop fusion | flops 655360 | bytes 655360 | tf_op jit(solution)/shard_map/concatenate | solution.py:78
  17.8 2.0 %collective-permute-start.13 = (bf16[128,640]{1,0:T(8,128)(2,1)}, bf16[128,640]{1,0:T(8,128)(2,1)S(1)}, u32[]{:S(2)}, u32[]{:S(2)}) collective-permute-start(bf16[128,640]{1,0:T(8,128)(2,1)} %collective-permute-done.12), channel_id=1, source_target_pairs={{0,2},{1,3},{2,0},{3,1},{4,6},{5,7},{6,4},{7,5},{8,10},{9,11},{10,... | collective-permute-start | bytes 491528 | tf_op jit(solution)/shard_map/ppermute | solution.py:79
  19.8 0.9 %constant_dynamic-update-slice_fusion.2 = bf16[128,2560]{1,0:T(8,128)(2,1)S(1)} fusion(bf16[128,640]{1,0:T(8,128)(2,1)} %collective-permute-done), kind=kLoop, calls=%fused_computation.60 | loop fusion | bytes 327680
  20.8 0.9 %pad_maximum_fusion.7 = bf16[128,1280]{1,0:T(8,128)(2,1)S(1)} fusion(bf16[128,640]{1,0:T(8,128)(2,1)S(1)} %collective-permute-done.1, bf16[128,640]{1,0:T(8,128)(2,1)} %collective-permute-done), kind=kLoop, calls=%fused_computation.52 | loop fusion | flops 655360 | bytes 655360 | tf_op jit(solution)/shard_map/concatenate | solution.py:78
  21.8 3.2 %collective-permute-done.7 = bf16[128,640]{1,0:T(8,128)(2,1)S(1)} collective-permute-done((bf16[128,640]{1,0:T(8,128)(2,1)}, bf16[128,640]{1,0:T(8,128)(2,1)S(1)}, u32[]{:S(2)}, u32[]{:S(2)}) %collective-permute-start.7) | collective-permute-done | bytes 163872 | tf_op jit(solution)/shard_map/ppermute | solution.py:79
  25.0 0.9 %pad_maximum_fusion.8 = bf16[128,1280]{1,0:T(8,128)(2,1)S(1)} fusion(bf16[128,640]{1,0:T(8,128)(2,1)S(1)} %collective-permute-done.7, bf16[128,640]{1,0:T(8,128)(2,1)} %collective-permute-done.6), kind=kLoop, calls=%fused_computation.53 | loop fusion | flops 655360 | bytes 655360 | tf_op jit(solution)/shard_map/concatenate | solution.py:78
  26.1 2.0 %collective-permute-done.13 = bf16[128,640]{1,0:T(8,128)(2,1)S(1)} collective-permute-done((bf16[128,640]{1,0:T(8,128)(2,1)}, bf16[128,640]{1,0:T(8,128)(2,1)S(1)}, u32[]{:S(2)}, u32[]{:S(2)}) %collective-permute-start.13) | collective-permute-done | bytes 163872 | tf_op jit(solution)/shard_map/ppermute | solution.py:79
  28.1 0.9 %pad_maximum_fusion.9 = bf16[128,1280]{1,0:T(8,128)(2,1)S(1)} fusion(bf16[128,640]{1,0:T(8,128)(2,1)S(1)} %collective-permute-done.13, bf16[128,640]{1,0:T(8,128)(2,1)} %collective-permute-done.12), kind=kLoop, calls=%fused_computation.54 | loop fusion | flops 655360 | bytes 655360 | tf_op jit(solution)/shard_map/concatenate | solution.py:78
  29.2 0.5 fusion.11
  29.7 0.7 %multiply_convert_fusion.1 = bf16[128,512]{1,0:T(8,128)(2,1)S(1)} fusion(f32[128,512]{1,0:T(8,128)S(1)} %fusion.11, bf16[128,2560]{1,0:T(8,128)(2,1)S(1)} %constant_dynamic-update-slice_fusion, bf16[640,512]{1,0:T(8,128)(2,1)S(1)} %copy-done.3, bf16[640,512]{1,0:T(8,128)(2,1)S(1)} %copy-done.4, bf16[640,512]{1,0:T(8,128)(2,1)S(1)} %copy-done.2, ...), kind=kOutput, calls=%fused_computation.57 | convolution fusion | flops 346423296 | bytes 3670016 | tf_op jit(solution)/shard_map/dot_general | solution.py:85
  30.5 0.3 convolution_convert_fusion.6
  30.8 0.5 collective-permute-start.3
  31.4 1.0 %pad_maximum_fusion.4 = bf16[128,2560]{1,0:T(8,128)(2,1)S(1)} fusion(bf16[128,1280]{1,0:T(8,128)(2,1)S(1)} %collective-permute-done.8, bf16[128,640]{1,0:T(8,128)(2,1)S(1)} %collective-permute-done.7, bf16[128,640]{1,0:T(8,128)(2,1)} %collective-permute-done.6), kind=kLoop, calls=%fused_computation.19 | loop fusion | flops 1966080 | bytes 1310720 | tf_op jit(solution)/shard_map/concatenate | solution.py:80
  33.0 0.5 fusion.12
  33.5 0.7 %fusion.1 = bf16[128,512]{1,0:T(8,128)(2,1)S(1)} fusion(bf16[128,2560]{1,0:T(8,128)(2,1)S(1)} %pad_maximum_fusion.4, f32[128,512]{1,0:T(8,128)S(1)} %fusion.12, bf16[640,512]{1,0:T(8,128)(2,1)S(1)} %copy-done.3, bf16[640,512]{1,0:T(8,128)(2,1)S(1)} %copy-done.4, bf16[640,512]{1,0:T(8,128)(2,1)S(1)} %copy-done.2, bf16[640,512]{1,0:T(8,128)(2,1)S(1)} %get-tuple-element.15), kind=kOutput, calls=%fused_computation.16 | convolution fusion | flops 346423296 | bytes 3670016 | tf_op jit(solution)/shard_map/dot_general | solution.py:85
  34.2 0.3 convolution_convert_fusion.4
  34.6 0.4 collective-permute-start.9
  35.0 1.0 %pad_maximum_fusion.5 = bf16[128,2560]{1,0:T(8,128)(2,1)S(1)} fusion(bf16[128,1280]{1,0:T(8,128)(2,1)S(1)} %collective-permute-done.14, bf16[128,640]{1,0:T(8,128)(2,1)S(1)} %collective-permute-done.13, bf16[128,640]{1,0:T(8,128)(2,1)} %collective-permute-done.12), kind=kLoop, calls=%fused_computation.20 | loop fusion | flops 1966080 | bytes 1310720 | tf_op jit(solution)/shard_map/concatenate | solution.py:80
  36.0 1.3 %collective-permute-start.4 = (bf16[128,640]{1,0:T(8,128)(2,1)S(1)}, bf16[128,640]{1,0:T(8,128)(2,1)S(1)}, u32[]{:S(2)}, u32[]{:S(2)}) collective-permute-start(bf16[128,640]{1,0:T(8,128)(2,1)S(1)} %slice.67), channel_id=1, source_target_pairs={{0,2},{1,3},{2,0},{3,1},{4,6},{5,7},{6,4},{7,5},{8,10},{9,11},{10,... | collective-permute-start | bytes 491528 | tf_op jit(solution)/shard_map/ppermute | solution.py:92
  37.3 0.3 convert_add_fusion.2
  37.7 0.5 fusion.13
  38.2 0.7 %fusion.2 = bf16[128,512]{1,0:T(8,128)(2,1)S(1)} fusion(bf16[128,2560]{1,0:T(8,128)(2,1)S(1)} %pad_maximum_fusion.5, f32[128,512]{1,0:T(8,128)S(1)} %fusion.13, bf16[640,512]{1,0:T(8,128)(2,1)S(1)} %copy-done.3, bf16[640,512]{1,0:T(8,128)(2,1)S(1)} %copy-done.4, bf16[640,512]{1,0:T(8,128)(2,1)S(1)} %copy-done.2, bf16[640,512]{1,0:T(8,128)(2,1)S(1)} %get-tuple-element.15), kind=kOutput, calls=%fused_computation.17 | convolution fusion | flops 346423296 | bytes 3670016 | tf_op jit(solution)/shard_map/dot_general | solution.py:85
  38.9 0.3 convolution_convert_fusion.2
  39.4 1.0 %pad_maximum_fusion.6 = bf16[128,2560]{1,0:T(8,128)(2,1)S(1)} fusion(bf16[128,1280]{1,0:T(8,128)(2,1)S(1)} %collective-permute-done.19, bf16[128,640]{1,0:T(8,128)(2,1)} %collective-permute-done.18, bf16[128,640]{1,0:T(8,128)(2,1)S(1)} %multiply_convert_fusion), kind=kLoop, calls=%fused_computation.21 | loop fusion | flops 1966080 | bytes 1310720 | tf_op jit(solution)/shard_map/concatenate | solution.py:80
  40.3 2.0 %collective-permute-done.4 = bf16[128,640]{1,0:T(8,128)(2,1)S(1)} collective-permute-done((bf16[128,640]{1,0:T(8,128)(2,1)S(1)}, bf16[128,640]{1,0:T(8,128)(2,1)S(1)}, u32[]{:S(2)}, u32[]{:S(2)}) %collective-permute-start.4) | collective-permute-done | bytes 163872 | tf_op jit(solution)/shard_map/ppermute | solution.py:92
  42.4 0.9 %collective-permute-start.5 = (bf16[128,640]{1,0:T(8,128)(2,1)S(1)}, bf16[128,640]{1,0:T(8,128)(2,1)S(1)}, u32[]{:S(2)}, u32[]{:S(2)}) collective-permute-start(bf16[128,640]{1,0:T(8,128)(2,1)S(1)} %fusion.9), channel_id=1, source_target_pairs={{0,8},{4,12},{8,0},{12,4},{1,9},{5,13},{9,1},{13,5},{2,10},{6,14},... | collective-permute-start | bytes 491528 | tf_op jit(solution)/shard_map/ppermute | solution.py:97
  43.3 1.6 %collective-permute-start.10 = (bf16[128,640]{1,0:T(8,128)(2,1)S(1)}, bf16[128,640]{1,0:T(8,128)(2,1)S(1)}, u32[]{:S(2)}, u32[]{:S(2)}) collective-permute-start(bf16[128,640]{1,0:T(8,128)(2,1)S(1)} %slice.66), channel_id=1, source_target_pairs={{0,2},{1,3},{2,0},{3,1},{4,6},{5,7},{6,4},{7,5},{8,10},{9,11},{10,... | collective-permute-start | bytes 491528 | tf_op jit(solution)/shard_map/ppermute | solution.py:92
  45.2 0.6 collective-permute-start.16
  45.8 0.5 fusion.14
  46.4 0.7 %fusion.3 = bf16[128,512]{1,0:T(8,128)(2,1)S(1)} fusion(bf16[128,2560]{1,0:T(8,128)(2,1)S(1)} %pad_maximum_fusion.6, f32[128,512]{1,0:T(8,128)S(1)} %fusion.14, bf16[640,512]{1,0:T(8,128)(2,1)S(1)} %copy-done.3, bf16[640,512]{1,0:T(8,128)(2,1)S(1)} %copy-done.4, bf16[640,512]{1,0:T(8,128)(2,1)S(1)} %copy-done.2, bf16[640,512]{1,0:T(8,128)(2,1)S(1)} %get-tuple-element.15), kind=kOutput, calls=%fused_computation.18 | convolution fusion | flops 346423296 | bytes 3670016 | tf_op jit(solution)/shard_map/dot_general | solution.py:85
  47.5 2.7 %collective-permute-done.10 = bf16[128,640]{1,0:T(8,128)(2,1)S(1)} collective-permute-done((bf16[128,640]{1,0:T(8,128)(2,1)S(1)}, bf16[128,640]{1,0:T(8,128)(2,1)S(1)}, u32[]{:S(2)}, u32[]{:S(2)}) %collective-permute-start.10) | collective-permute-done | bytes 163872 | tf_op jit(solution)/shard_map/ppermute | solution.py:92
  50.3 2.6 %collective-permute-start.11 = (bf16[128,640]{1,0:T(8,128)(2,1)S(1)}, bf16[128,640]{1,0:T(8,128)(2,1)S(1)}, u32[]{:S(2)}, u32[]{:S(2)}) collective-permute-start(bf16[128,640]{1,0:T(8,128)(2,1)S(1)} %fusion.8), channel_id=1, source_target_pairs={{0,4},{4,0},{8,12},{12,8},{1,5},{5,1},{9,13},{13,9},{2,6},{6,2},{1... | collective-permute-start | bytes 491528 | tf_op jit(solution)/shard_map/ppermute | solution.py:97
  52.9 1.5 %collective-permute-start.17 = (bf16[128,640]{1,0:T(8,128)(2,1)S(1)}, bf16[128,640]{1,0:T(8,128)(2,1)S(1)}, u32[]{:S(2)}, u32[]{:S(2)}) collective-permute-start(bf16[128,640]{1,0:T(8,128)(2,1)S(1)} %fusion.7), channel_id=1, source_target_pairs={{0,12},{4,8},{8,4},{12,0},{1,13},{5,9},{9,5},{13,1},{2,14},{6,10},... | collective-permute-start | bytes 491528 | tf_op jit(solution)/shard_map/ppermute | solution.py:97
  54.3 0.3 convert_add_fusion
  54.7 1.5 %collective-permute-start.21 = (bf16[128,640]{1,0:T(8,128)(2,1)S(1)}, bf16[128,640]{1,0:T(8,128)(2,1)S(1)}, u32[]{:S(2)}, u32[]{:S(2)}) collective-permute-start(bf16[128,640]{1,0:T(8,128)(2,1)S(1)} %slice.64), channel_id=1, source_target_pairs={{0,2},{1,3},{2,0},{3,1},{4,6},{5,7},{6,4},{7,5},{8,10},{9,11},{10,... | collective-permute-start | bytes 491528 | tf_op jit(solution)/shard_map/ppermute | solution.py:92
  56.2 1.6 %collective-permute-done.11 = bf16[128,640]{1,0:T(8,128)(2,1)S(1)} collective-permute-done((bf16[128,640]{1,0:T(8,128)(2,1)S(1)}, bf16[128,640]{1,0:T(8,128)(2,1)S(1)}, u32[]{:S(2)}, u32[]{:S(2)}) %collective-permute-start.11) | collective-permute-done | bytes 163872 | tf_op jit(solution)/shard_map/ppermute | solution.py:97
  57.9 2.3 %collective-permute-done.17 = bf16[128,640]{1,0:T(8,128)(2,1)S(1)} collective-permute-done((bf16[128,640]{1,0:T(8,128)(2,1)S(1)}, bf16[128,640]{1,0:T(8,128)(2,1)S(1)}, u32[]{:S(2)}, u32[]{:S(2)}) %collective-permute-start.17) | collective-permute-done | bytes 163872 | tf_op jit(solution)/shard_map/ppermute | solution.py:97
  60.2 0.9 %fusion.6 = bf16[128,640]{1,0:T(8,128)(2,1)} fusion(f32[128,1280]{1,0:T(8,128)S(1)} %convert_add_fusion, bf16[128,640]{1,0:T(8,128)(2,1)S(1)} %collective-permute-done.21, bf16[128,640]{1,0:T(8,128)(2,1)S(1)} %collective-permute-done.17, bf16[128,640]{1,0:T(8,128)(2,1)S(1)} %collective-permute-done.11, bf16[128,640]{1,0:T(8,128)(2,1)S(1)} %collective-permute-done.5, ...), kind=kLoop, calls=%fused_computation.42 | loop fusion | flops 1064960 | bytes 1147392 | tf_op jit(solution)/shard_map/convert_element_type | solution.py:101
  (48 shorter events, 2.6 us)
Async XLA Ops:
  1.0 13.6 %collective-permute-start = (bf16[128,640]{1,0:T(8,128)(2,1)S(1)}, bf16[128,640]{1,0:T(8,128)(2,1)}, u32[]{:S(2)}, u32[]{:S(2)}) collective-permute-start(bf16[128,640]{1,0:T(8,128)(2,1)S(1)} %multiply_convert_fusion), channel_id=1, source_target_pairs={{0,8},{4,12},{8,0},{12,4},{1,9},{5,13},{9,1},{13,5},{2,10},{6,14},... | collective-permute-start | bytes 491528 | tf_op jit(solution)/shard_map/ppermute | solution.py:66
  5.1 12.6 %collective-permute-start.6 = (bf16[128,640]{1,0:T(8,128)(2,1)S(1)}, bf16[128,640]{1,0:T(8,128)(2,1)}, u32[]{:S(2)}, u32[]{:S(2)}) collective-permute-start(bf16[128,640]{1,0:T(8,128)(2,1)S(1)} %multiply_convert_fusion), channel_id=1, source_target_pairs={{0,4},{4,0},{8,12},{12,8},{1,5},{5,1},{9,13},{13,9},{2,6},{6,2},{1... | collective-permute-start | bytes 491528 | tf_op jit(solution)/shard_map/ppermute | solution.py:66
  6.7 11.1 %collective-permute-start.12 = (bf16[128,640]{1,0:T(8,128)(2,1)S(1)}, bf16[128,640]{1,0:T(8,128)(2,1)}, u32[]{:S(2)}, u32[]{:S(2)}) collective-permute-start(bf16[128,640]{1,0:T(8,128)(2,1)S(1)} %multiply_convert_fusion), channel_id=1, source_target_pairs={{0,12},{4,8},{8,4},{12,0},{1,13},{5,9},{9,5},{13,1},{2,14},{6,10},... | collective-permute-start | bytes 491528 | tf_op jit(solution)/shard_map/ppermute | solution.py:66
  6.7 10.0 %collective-permute-start.18 = (bf16[128,640]{1,0:T(8,128)(2,1)S(1)}, bf16[128,640]{1,0:T(8,128)(2,1)}, u32[]{:S(2)}, u32[]{:S(2)}) collective-permute-start(bf16[128,640]{1,0:T(8,128)(2,1)S(1)} %multiply_convert_fusion), channel_id=1, source_target_pairs={{0,2},{1,3},{2,0},{3,1},{4,6},{5,7},{6,4},{7,5},{8,10},{9,11},{10,... | collective-permute-start | bytes 491528 | tf_op jit(solution)/shard_map/ppermute | solution.py:79
  8.4 2.5 %copy-start = (bf16[1,2560,512]{2,1,0:T(8,128)(2,1)S(1)}, bf16[1,2560,512]{2,1,0:T(8,128)(2,1)}, u32[]{:S(2)}) copy-start(bf16[1,2560,512]{2,1,0:T(8,128)(2,1)} %param.10) | copy-start | bytes 7864324
  12.3 1.7 %copy-start.1 = (bf16[1,512,2560]{2,1,0:T(8,128)(2,1)S(1)}, bf16[1,512,2560]{2,1,0:T(8,128)(2,1)}, u32[]{:S(2)}) copy-start(bf16[1,512,2560]{2,1,0:T(8,128)(2,1)} %param.11) | copy-start | bytes 7864324
  14.6 6.2 %collective-permute-start.1 = (bf16[128,640]{1,0:T(8,128)(2,1)}, bf16[128,640]{1,0:T(8,128)(2,1)S(1)}, u32[]{:S(2)}, u32[]{:S(2)}) collective-permute-start(bf16[128,640]{1,0:T(8,128)(2,1)} %collective-permute-done), channel_id=1, source_target_pairs={{0,2},{1,3},{2,0},{3,1},{4,6},{5,7},{6,4},{7,5},{8,10},{9,11},{10,... | collective-permute-start | bytes 491528 | tf_op jit(solution)/shard_map/ppermute | solution.py:79
  17.7 21.7 %collective-permute-start.19 = (bf16[128,1280]{1,0:T(8,128)(2,1)S(1)}, bf16[128,1280]{1,0:T(8,128)(2,1)S(1)}, u32[]{:S(2)}, u32[]{:S(2)}) collective-permute-start(bf16[128,1280]{1,0:T(8,128)(2,1)S(1)} %pad_maximum_fusion.10), channel_id=1, source_target_pairs={{0,1},{1,0},{2,3},{3,2},{4,5},{5,4},{6,7},{7,6},{8,9},{9,8},{10,11... | collective-permute-start | bytes 983048 | tf_op jit(solution)/shard_map/ppermute | solution.py:81
  17.8 7.3 %collective-permute-start.7 = (bf16[128,640]{1,0:T(8,128)(2,1)}, bf16[128,640]{1,0:T(8,128)(2,1)S(1)}, u32[]{:S(2)}, u32[]{:S(2)}) collective-permute-start(bf16[128,640]{1,0:T(8,128)(2,1)} %collective-permute-done.6), channel_id=1, source_target_pairs={{0,2},{1,3},{2,0},{3,1},{4,6},{5,7},{6,4},{7,5},{8,10},{9,11},{10,... | collective-permute-start | bytes 491528 | tf_op jit(solution)/shard_map/ppermute | solution.py:79
  17.8 10.2 %collective-permute-start.13 = (bf16[128,640]{1,0:T(8,128)(2,1)}, bf16[128,640]{1,0:T(8,128)(2,1)S(1)}, u32[]{:S(2)}, u32[]{:S(2)}) collective-permute-start(bf16[128,640]{1,0:T(8,128)(2,1)} %collective-permute-done.12), channel_id=1, source_target_pairs={{0,2},{1,3},{2,0},{3,1},{4,6},{5,7},{6,4},{7,5},{8,10},{9,11},{10,... | collective-permute-start | bytes 491528 | tf_op jit(solution)/shard_map/ppermute | solution.py:79
  21.7 7.4 %collective-permute-start.2 = (bf16[128,1280]{1,0:T(8,128)(2,1)S(1)}, bf16[128,1280]{1,0:T(8,128)(2,1)S(1)}, u32[]{:S(2)}, u32[]{:S(2)}) collective-permute-start(bf16[128,1280]{1,0:T(8,128)(2,1)S(1)} %pad_maximum_fusion.7), channel_id=1, source_target_pairs={{0,1},{1,0},{2,3},{3,2},{4,5},{5,4},{6,7},{7,6},{8,9},{9,8},{10,11... | collective-permute-start | bytes 983048 | tf_op jit(solution)/shard_map/ppermute | solution.py:81
  26.0 3.7 %copy-start.2 = (bf16[640,512]{1,0:T(8,128)(2,1)S(1)}, bf16[640,512]{1,0:T(8,128)(2,1)}, u32[]{:S(2)}) copy-start(bf16[640,512]{1,0:T(8,128)(2,1)} %get-tuple-element.16) | copy-start | bytes 1966084
  26.0 3.7 %copy-start.3 = (bf16[640,512]{1,0:T(8,128)(2,1)S(1)}, bf16[640,512]{1,0:T(8,128)(2,1)}, u32[]{:S(2)}) copy-start(bf16[640,512]{1,0:T(8,128)(2,1)} %get-tuple-element.17) | copy-start | bytes 1966084
  26.0 3.7 %copy-start.4 = (bf16[640,512]{1,0:T(8,128)(2,1)S(1)}, bf16[640,512]{1,0:T(8,128)(2,1)}, u32[]{:S(2)}) copy-start(bf16[640,512]{1,0:T(8,128)(2,1)} %get-tuple-element.18) | copy-start | bytes 1966084
  26.0 5.4 %collective-permute-start.8 = (bf16[128,1280]{1,0:T(8,128)(2,1)S(1)}, bf16[128,1280]{1,0:T(8,128)(2,1)S(1)}, u32[]{:S(2)}, u32[]{:S(2)}) collective-permute-start(bf16[128,1280]{1,0:T(8,128)(2,1)S(1)} %pad_maximum_fusion.8), channel_id=1, source_target_pairs={{0,1},{1,0},{2,3},{3,2},{4,5},{5,4},{6,7},{7,6},{8,9},{9,8},{10,11... | collective-permute-start | bytes 983048 | tf_op jit(solution)/shard_map/ppermute | solution.py:81
  29.0 6.0 %collective-permute-start.14 = (bf16[128,1280]{1,0:T(8,128)(2,1)S(1)}, bf16[128,1280]{1,0:T(8,128)(2,1)S(1)}, u32[]{:S(2)}, u32[]{:S(2)}) collective-permute-start(bf16[128,1280]{1,0:T(8,128)(2,1)S(1)} %pad_maximum_fusion.9), channel_id=1, source_target_pairs={{0,1},{1,0},{2,3},{3,2},{4,5},{5,4},{6,7},{7,6},{8,9},{9,8},{10,11... | collective-permute-start | bytes 983048 | tf_op jit(solution)/shard_map/ppermute | solution.py:81
  30.8 1.8 %collective-permute-start.3 = (bf16[128,1280]{1,0:T(8,128)(2,1)S(1)}, bf16[128,1280]{1,0:T(8,128)(2,1)S(1)}, u32[]{:S(2)}, u32[]{:S(2)}) collective-permute-start(bf16[128,1280]{1,0:T(8,128)(2,1)S(1)} %convolution_convert_fusion.6), channel_id=1, source_target_pairs={{0,1},{1,0},{2,3},{3,2},{4,5},{5,4},{6,7},{7,6},{8,9},{9,8},{10,11... | collective-permute-start | bytes 983048 | tf_op jit(solution)/shard_map/ppermute | solution.py:90
  34.6 2.7 %collective-permute-start.9 = (bf16[128,1280]{1,0:T(8,128)(2,1)S(1)}, bf16[128,1280]{1,0:T(8,128)(2,1)S(1)}, u32[]{:S(2)}, u32[]{:S(2)}) collective-permute-start(bf16[128,1280]{1,0:T(8,128)(2,1)S(1)} %convolution_convert_fusion.4), channel_id=1, source_target_pairs={{0,1},{1,0},{2,3},{3,2},{4,5},{5,4},{6,7},{7,6},{8,9},{9,8},{10,11... | collective-permute-start | bytes 983048 | tf_op jit(solution)/shard_map/ppermute | solution.py:90
  36.0 6.3 %collective-permute-start.4 = (bf16[128,640]{1,0:T(8,128)(2,1)S(1)}, bf16[128,640]{1,0:T(8,128)(2,1)S(1)}, u32[]{:S(2)}, u32[]{:S(2)}) collective-permute-start(bf16[128,640]{1,0:T(8,128)(2,1)S(1)} %slice.67), channel_id=1, source_target_pairs={{0,2},{1,3},{2,0},{3,1},{4,6},{5,7},{6,4},{7,5},{8,10},{9,11},{10,... | collective-permute-start | bytes 491528 | tf_op jit(solution)/shard_map/ppermute | solution.py:92
  39.3 5.6 %collective-permute-start.15 = (bf16[128,1280]{1,0:T(8,128)(2,1)S(1)}, bf16[128,1280]{1,0:T(8,128)(2,1)S(1)}, u32[]{:S(2)}, u32[]{:S(2)}) collective-permute-start(bf16[128,1280]{1,0:T(8,128)(2,1)S(1)} %convolution_convert_fusion.2), channel_id=1, source_target_pairs={{0,1},{1,0},{2,3},{3,2},{4,5},{5,4},{6,7},{7,6},{8,9},{9,8},{10,11... | collective-permute-start | bytes 983048 | tf_op jit(solution)/shard_map/ppermute | solution.py:90
  42.4 13.9 %collective-permute-start.5 = (bf16[128,640]{1,0:T(8,128)(2,1)S(1)}, bf16[128,640]{1,0:T(8,128)(2,1)S(1)}, u32[]{:S(2)}, u32[]{:S(2)}) collective-permute-start(bf16[128,640]{1,0:T(8,128)(2,1)S(1)} %fusion.9), channel_id=1, source_target_pairs={{0,8},{4,12},{8,0},{12,4},{1,9},{5,13},{9,1},{13,5},{2,10},{6,14},... | collective-permute-start | bytes 491528 | tf_op jit(solution)/shard_map/ppermute | solution.py:97
  43.3 6.9 %collective-permute-start.10 = (bf16[128,640]{1,0:T(8,128)(2,1)S(1)}, bf16[128,640]{1,0:T(8,128)(2,1)S(1)}, u32[]{:S(2)}, u32[]{:S(2)}) collective-permute-start(bf16[128,640]{1,0:T(8,128)(2,1)S(1)} %slice.66), channel_id=1, source_target_pairs={{0,2},{1,3},{2,0},{3,1},{4,6},{5,7},{6,4},{7,5},{8,10},{9,11},{10,... | collective-permute-start | bytes 491528 | tf_op jit(solution)/shard_map/ppermute | solution.py:92
  45.2 7.6 %collective-permute-start.16 = (bf16[128,640]{1,0:T(8,128)(2,1)S(1)}, bf16[128,640]{1,0:T(8,128)(2,1)S(1)}, u32[]{:S(2)}, u32[]{:S(2)}) collective-permute-start(bf16[128,640]{1,0:T(8,128)(2,1)S(1)} %slice.65), channel_id=1, source_target_pairs={{0,2},{1,3},{2,0},{3,1},{4,6},{5,7},{6,4},{7,5},{8,10},{9,11},{10,... | collective-permute-start | bytes 491528 | tf_op jit(solution)/shard_map/ppermute | solution.py:92
  47.5 8.8 %copy-start.5 = (s32[128,1]{0,1:T(1,128)S(1)}, s32[128,1]{0,1:T(1,128)}, u32[]{:S(2)}) copy-start(s32[128,1]{0,1:T(1,128)} %param.8) | copy-start | bytes 1540
  47.5 6.9 %collective-permute-start.20 = (bf16[128,1280]{1,0:T(8,128)(2,1)S(1)}, bf16[128,1280]{1,0:T(8,128)(2,1)S(1)}, u32[]{:S(2)}, u32[]{:S(2)}) collective-permute-start(bf16[128,1280]{1,0:T(8,128)(2,1)S(1)} %convolution_convert_fusion), channel_id=1, source_target_pairs={{0,1},{1,0},{2,3},{3,2},{4,5},{5,4},{6,7},{7,6},{8,9},{9,8},{10,11... | collective-permute-start | bytes 983048 | tf_op jit(solution)/shard_map/ppermute | solution.py:90
  50.3 7.6 %collective-permute-start.11 = (bf16[128,640]{1,0:T(8,128)(2,1)S(1)}, bf16[128,640]{1,0:T(8,128)(2,1)S(1)}, u32[]{:S(2)}, u32[]{:S(2)}) collective-permute-start(bf16[128,640]{1,0:T(8,128)(2,1)S(1)} %fusion.8), channel_id=1, source_target_pairs={{0,4},{4,0},{8,12},{12,8},{1,5},{5,1},{9,13},{13,9},{2,6},{6,2},{1... | collective-permute-start | bytes 491528 | tf_op jit(solution)/shard_map/ppermute | solution.py:97
  52.9 7.3 %collective-permute-start.17 = (bf16[128,640]{1,0:T(8,128)(2,1)S(1)}, bf16[128,640]{1,0:T(8,128)(2,1)S(1)}, u32[]{:S(2)}, u32[]{:S(2)}) collective-permute-start(bf16[128,640]{1,0:T(8,128)(2,1)S(1)} %fusion.7), channel_id=1, source_target_pairs={{0,12},{4,8},{8,4},{12,0},{1,13},{5,9},{9,5},{13,1},{2,14},{6,10},... | collective-permute-start | bytes 491528 | tf_op jit(solution)/shard_map/ppermute | solution.py:97
  54.7 5.5 %collective-permute-start.21 = (bf16[128,640]{1,0:T(8,128)(2,1)S(1)}, bf16[128,640]{1,0:T(8,128)(2,1)S(1)}, u32[]{:S(2)}, u32[]{:S(2)}) collective-permute-start(bf16[128,640]{1,0:T(8,128)(2,1)S(1)} %slice.64), channel_id=1, source_target_pairs={{0,2},{1,3},{2,0},{3,1},{4,6},{5,7},{6,4},{7,5},{8,10},{9,11},{10,... | collective-permute-start | bytes 491528 | tf_op jit(solution)/shard_map/ppermute | solution.py:92
